TPU v7x, 32 devices: a whole 2x2x4 slice. The times are simulated.
32 devices in a mesh: seq: 8 (over z, x), head: 4 (over y, core).
Axes of the slice: x: 2, y: 2, z: 4, core: 2. Of those that a mesh axis runs over, the one named last changes fastest.
Arguments:
- features: float32 [1024, 5120], P('seq', 'head'), may hold values from -20 to 20
- gate_pre: float32 [1024, 5120], P('seq', 'head'), may hold values from -6 to 6
- write_keys: float32 [1024, 128], P('seq'), may hold values from -6 to 6
- read_queries: float32 [1024, 128], P('seq'), may hold values from -0.5 to 0.5
- step_sizes: float32 [80, 1024], P('head', 'seq'), may hold values from 0.02 to 0.2
- log_decay: float32 [80, 1024], P('head', 'seq'), may hold values from -2 to 0
- skip_scale: float32 [80], P('head'), may hold values from 0.5 to 1.5
- norm_gain: float32 [5120], P('head'), may hold values from 0.1 to 1.9
- out_grad: float32 [1024, 5120], P('seq', 'head'), may hold values from -6 to 6
Outputs:
- grad_features: float32 [1024, 5120], P('seq', 'head')
- grad_gate: float32 [1024, 5120], P('seq', 'head')
- grad_write: float32 [1024, 128], P('seq')
- grad_read: float32 [1024, 128], P('seq')
- grad_steps: float32 [80, 1024], P('head', 'seq')
- grad_decay: float32 [80, 1024], P('head', 'seq')
All inputs are finite; a program needn't handle non-finite values.
Results may differ from a plain program's by a relative error of at most 0.00022.
Values sent between devices are 32-bit elements; how exact they have to be, the bound alone decides.
No kernel may reach another device: no remote copies, remote signals or barrier semaphores. Data moves between devices by JAX's collectives and lax.ppermute only.
A program may use at most 128 MiB of HBM per device.

v0:
```python
import jax
import jax.numpy as jnp
from jax import lax
from jax.sharding import PartitionSpec as P

BLOCK = 128


eps = 1e-05
highest = lax.Precision.HIGHEST


def entering(part, axis, combine, identity, reverse):
    count = lax.axis_size(axis)
    place = lax.axis_index(axis)
    ahead = count - 1 - place if reverse else place
    gathered = jax.tree.map(lambda a: lax.all_gather(a, axis), part)
    state = jax.tree.map(lambda a, e: jnp.zeros_like(a) + jnp.asarray(e, a.dtype), part, identity)

    def one(step, state):
        source = count - 1 - step if reverse else step
        return combine(
            state, jax.tree.map(lambda a: lax.dynamic_index_in_dim(a, source, 0, False), gathered)
        )

    return lax.fori_loop(0, ahead, one, state)


def block_step(carry_state, inputs, skip_scale):
    feat_block, step_block, decay_block, write_block, read_block = inputs
    length = decay_block.shape[1]
    cumul = jnp.cumsum(decay_block, axis=1)
    row_index = lax.broadcasted_iota(jnp.int32, (length, length), 0)
    col_index = lax.broadcasted_iota(jnp.int32, (length, length), 1)
    causal = row_index >= col_index
    gaps = jnp.where(causal[None], cumul[:, :, None] - cumul[:, None, :], 0.0)
    weights = jnp.where(causal[None], jnp.exp(gaps), 0.0)
    scores = jnp.dot(read_block, jnp.transpose(write_block), precision=highest)
    scaled = feat_block * jnp.transpose(step_block)[:, :, None]
    masked = weights * scores[None]
    within = jnp.einsum("hij,jhp->ihp", masked, scaled, precision=highest)
    carried = jnp.einsum("in,hpn->ihp", read_block, carry_state, precision=highest)
    carried = carried * jnp.transpose(jnp.exp(cumul))[:, :, None]
    output = within + carried + skip_scale[None, :, None] * feat_block
    to_end = jnp.exp(cumul[:, -1:] - cumul)
    weighted_in = scaled * jnp.transpose(to_end)[:, :, None]
    update = jnp.einsum("jhp,jn->hpn", weighted_in, write_block, precision=highest)
    new_state = jnp.exp(cumul[:, -1])[:, None, None] * carry_state + update
    return (new_state, output)


def run_mixer(
    features, step_sizes, log_decay, write_keys, read_queries, carry_state, skip_scale, block
):
    length = features.shape[0]
    head_count = step_sizes.shape[0]
    head_width = features.shape[1] // head_count
    block_total = length // block
    feat_blocks = features.reshape(block_total, block, head_count, head_width)
    step_blocks = jnp.transpose(step_sizes.reshape(head_count, block_total, block), (1, 0, 2))
    decay_blocks = jnp.transpose(log_decay.reshape(head_count, block_total, block), (1, 0, 2))
    write_blocks = write_keys.reshape(block_total, block, write_keys.shape[1])
    read_blocks = read_queries.reshape(block_total, block, read_queries.shape[1])

    def advance(carried_in, inputs):
        return block_step(carried_in, inputs, skip_scale)

    last_state, outputs = lax.scan(
        advance, carry_state, (feat_blocks, step_blocks, decay_blocks, write_blocks, read_blocks)
    )
    return (last_state, outputs.reshape(length, head_count * head_width))


def merge_pairs(earlier, later):
    return (earlier[0] * later[0], later[0][:, None, None] * earlier[1] + later[1])


def carry_forward(decay_pair):
    identity = (jnp.ones_like(decay_pair[0]), jnp.zeros_like(decay_pair[1]))
    return entering(decay_pair, "seq", merge_pairs, identity, False)[1]


def carry_backward(decay_pair):
    identity = (jnp.ones_like(decay_pair[0]), jnp.zeros_like(decay_pair[1]))
    return entering(decay_pair, "seq", merge_pairs, identity, True)[1]


def local(
    features,
    gate_pre,
    write_keys,
    read_queries,
    step_sizes,
    log_decay,
    skip_scale,
    norm_gain,
    out_grad,
):
    head_count, length = step_sizes.shape
    head_width = features.shape[1] // head_count
    channels = features.shape[1] * lax.axis_size("head")
    cumul = jnp.cumsum(log_decay, axis=1)
    decay_total = jnp.exp(cumul[:, -1])
    scaled = (
        features.reshape(length, head_count, head_width) * jnp.transpose(step_sizes)[:, :, None]
    )
    to_end = jnp.exp(cumul[:, -1:] - cumul)
    weighted_in = scaled * jnp.transpose(to_end)[:, :, None]
    local_state = jnp.einsum("jhp,jn->hpn", weighted_in, write_keys, precision=highest)
    state_in = carry_forward((decay_total, local_state))

    def local_mixer(feat_in, step_in, decay_factors, writes, read_in):
        return run_mixer(
            feat_in, step_in, decay_factors, writes, read_in, state_in, skip_scale, BLOCK
        )

    primal, pullback = jax.vjp(
        local_mixer, features, step_sizes, log_decay, write_keys, read_queries
    )
    mixed_out = primal[1]
    sigmoid_gate = jax.nn.sigmoid(gate_pre)
    active = gate_pre * sigmoid_gate
    gated_out = mixed_out * active
    weighted = out_grad * norm_gain[None, :]
    square_sum, cross_sum = lax.psum(
        (jnp.sum(gated_out * gated_out, axis=1), jnp.sum(weighted * gated_out, axis=1)), "head"
    )
    inverse = lax.rsqrt(square_sum / channels + eps)
    grad_gated = (
        inverse[:, None] * weighted
        - (inverse * inverse * inverse * cross_sum / channels)[:, None] * gated_out
    )
    grad_mixed = grad_gated * active
    grad_gate = grad_gated * mixed_out * sigmoid_gate * (1.0 + gate_pre * (1.0 - sigmoid_gate))
    from_start = jnp.transpose(jnp.exp(cumul))
    weighted_grad = grad_mixed.reshape(length, head_count, head_width) * from_start[:, :, None]
    local_grad = jnp.einsum("jhp,jn->hpn", weighted_grad, read_queries, precision=highest)
    state_grad = carry_backward((decay_total, local_grad))
    grad_features, grad_steps, grad_decay, grad_write, grad_read = pullback(
        (state_grad, grad_mixed)
    )
    grad_write, grad_read = lax.psum((grad_write, grad_read), "head")
    return (grad_features, grad_gate, grad_write, grad_read, grad_steps, grad_decay)


def solution(mesh):
    placed = (
        P("seq", "head"),
        P("seq", "head"),
        P("seq", None),
        P("seq", None),
        P("head", "seq"),
        P("head", "seq"),
        P("head"),
        P("head"),
        P("seq", "head"),
    )
    return jax.shard_map(
        local,
        mesh=mesh,
        in_specs=placed,
        out_specs=(
            P("seq", "head"),
            P("seq", "head"),
            P("seq", None),
            P("seq", None),
            P("head", "seq"),
            P("head", "seq"),
        ),
        check_vma=False,
    )
```

profile of v0, /device:TPU:0, one launch (start us, length us, event | category | flops | bytes accessed | tf_op | source)
XLA Modules:
  0.0 269.0 jit_solution(2018952893159528250)
XLA Ops:
  7.2 1.0 reduce_window_sum.30
  8.5 1.3 copy.33
  9.9 1.5 fusion.39
  13.0 23.4 %all-reduce.2 = f32[160]{0:T(256)S(1)} all-reduce(f32[160]{0:T(256)S(1)} %dynamic-update-slice), channel_id=2, replica_groups=mesh['seq'=8,'head'=4] {'seq'}, use_global_device_ids=true, to_apply=%add.2 | all-reduce | flops 160 | bytes 1280
  37.6 63.0 %all-gather.6.cloned.1.call-done = f32[160,64,128]{2,1,0:T(8,128)} async-done(((f32[20,64,128]{2,1,0:T(8,128)}), f32[160,64,128]{2,1,0:T(8,128)}) %all-gather.6.cloned.1.call-update) | async-done | bytes 5242896 | tf_op jit(solution)/shard_map/all_gather | solution.py:17
  101.5 2.7 %fusion.12 = f32[128,20,64]{0,2,1:T(8,128)S(1)} fusion(f32[128,20,64]{0,2,1:T(8,128)S(1)} %bitcast.107, f32[128,20,64]{0,2,1:T(8,128)S(1)} %convolution_bitcast_fusion.1, f32[128,128]{1,0:T(8,128)S(1)} %fusion.70, f32[20,128]{1,0:T(8,128)S(1)} %reduce_window_sum.30, pred[128,128]{1,0:T(8,128)(4,1)S(1)} %iota_compare_fusion, ...), kind=kOutput, calls=%fused_computation.15 | convolution fusion | flops 253788160 | bytes 2078800 | tf_op jit(solution)/shard_map/jvp()/while/body/eval_jaxpr/hij,jhp->ihp/dot_general | solution.py:41
  104.6 5.7 %all-reduce.3 = (f32[128]{0:T(128)S(1)}, f32[128]{0:T(128)S(1)}) all-reduce(f32[128]{0:T(128)S(1)} %get-tuple-element.515, f32[128]{0:T(128)S(1)} %get-tuple-element.514), channel_id=1, replica_groups=mesh['seq'=8,'head'=4] {'head'}, use_global_device_ids=true, to_apply=%region_6.7 | all-reduce | flops 256 | bytes 2048 | tf_op jit(solution)/shard_map/psum | solution.py:125
  110.3 1.5 bitcast_multiply_fusion
  111.8 0.8 copy-done.1
  112.6 1.5 fusion.25
  114.2 1.1 copy.41
  115.3 1.2 convolution_bitcast_fusion.2
  116.5 3.5 %fusion.22 = (f32[20,128]{1,0:T(8,128)}, f32[20,128]{1,0:T(8,128)}, f32[128,128]{1,0:T(8,128)S(1)}) fusion(f32[128,128]{1,0:T(8,128)S(1)} %copy-done.13, f32[20,128]{1,0:T(8,128)S(1)} %reduce_window_sum.30, pred[128,128]{1,0:T(8,128)(4,1)S(1)} %copy-done.19, f32[20,64,128]{2,1,0:T(8,128)S(1)} %bitcast.112, f32[128,20,64]{0,2,1:T(8,128)S(1)} %bitcast.108, ...), kind=kOutput, calls=%fused_computation.23 | convolution fusion | flops 255405056 | bytes 1499136 | tf_op jit(solution)/shard_map/transpose(jvp())/while/body/eval_jaxpr/hij,jhp->ihp/dot_general | solution.py:41
  120.1 0.8 convolution_add_fusion
  120.9 87.1 %all-gather.8.cloned.1.call-done = f32[160,64,128]{2,1,0:T(8,128)} async-done(((f32[20,64,128]{2,1,0:T(8,128)}), f32[160,64,128]{2,1,0:T(8,128)}) %all-gather.8.cloned.1.call-update) | async-done | bytes 5242896 | tf_op jit(solution)/shard_map/all_gather | solution.py:17
  208.0 14.0 %while.21 = (s32[]{:T(128)}, f32[20,64,128]{2,1,0:T(8,128)S(1)}, s32[]{:T(128)}, f32[8,20]{1,0:T(8,128)}, f32[8,20,64,128]{3,2,1,0:T(8,128)}, /*index=5*/s32[]{:T(128)}, s32[]{:T(128)}, s32[]{:T(128)}, s32[]{:T(128)}) while((s32[]{:T(128)}, f32[20,64,128]{2,1,0:T(8,128)S(1)}, s32[]{:T(128)}, f32[8,20]{1,0:T(8,128)}, ...), condition=%wide.region_8.9_spmd, body=%wide.region_7.8_spmd.sunk | while | flops 327686 | bytes 1966475 | solution.py:26
  208.7 1.2 bitcast_add_fusion.5
  210.7 1.2 bitcast_add_fusion.5
  212.7 1.2 bitcast_add_fusion.5
  214.7 1.2 bitcast_add_fusion.5
  216.6 1.2 bitcast_add_fusion.5
  218.6 1.2 bitcast_add_fusion.5
  220.6 1.2 bitcast_add_fusion.5
  222.0 0.7 multiply_reduce_fusion.3
  222.8 1.2 convolution_bitcast_fusion.3
  226.1 0.9 convolution_add_fusion.1
  227.0 3.2 %multiply_reduce_fusion.2 = (f32[128,20]{0,1:T(8,128)S(1)}, f32[128,20]{0,1:T(8,128)}, f32[128,20,64]{0,2,1:T(8,128)S(1)}, f32[128,20]{0,1:T(8,128)S(1)}) fusion(f32[128,20,64]{0,2,1:T(8,128)S(1)} %convolution_bitcast_fusion, f32[128,20,64]{0,2,1:T(8,128)S(1)} %bitcast.110, f32[128,20]{0,1:T(8,128)} %bitcast.119, f32[128,20,64]{0,2,1:T(8,128)S(1)} %bitcast.113, ...), kind=kOutput, calls=%fused_computation.30 | convolution fusion | flops 254927360 | bytes 4075600 | tf_op jit(solution)/shard_map/transpose(jvp())/while/body/eval_jaxpr/hij,jhp->ihp/dot_general | solution.py:41
  230.7 1.1 copy.40
  231.8 1.8 reduce_window_sum.31
  233.6 25.9 %all-reduce.7.cloned.1.call-done = (f32[128,128]{1,0:T(8,128)}, f32[128,128]{1,0:T(8,128)}) async-done(((f32[128,128]{1,0:T(8,128)}, f32[128,128]{1,0:T(8,128)}), (f32[128,128]{1,0:T(8,128)}, f32[128,128]{1,0:T(8,128)})) %all-reduce.7.cloned.1.call-update) | async-done | bytes 131088 | tf_op jit(solution)/shard_map/psum | solution.py:142
  259.5 1.5 copy.59
  261.0 1.5 copy.60
  (84 shorter events, 11.0 us)
Async XLA Ops:
  7.2 2.7 %copy-start = (f32[128,128]{1,0:T(8,128)S(1)}, f32[128,128]{1,0:T(8,128)}, u32[]{:S(2)}) copy-start(f32[128,128]{1,0:T(8,128)} %param.15) | copy-start | bytes 196612
  7.2 2.7 copy-start.14
  7.2 93.5 %all-gather.6.cloned.1.call-start = ((), (), s32[]{:S(2)}) async-start(), calls=%async_computation | async-start | bytes 5898240 | tf_op jit(solution)/shard_map/all_gather | solution.py:17
  8.5 27.9 %copy-start.10 = (f32[128,20]{0,1:T(8,128)}, f32[128,20]{0,1:T(8,128)S(1)}, u32[]{:S(2)}) copy-start(f32[128,20]{0,1:T(8,128)S(1)} %get-tuple-element.549) | copy-start | bytes 30724
  9.8 1.6 copy-start.24
  9.8 26.6 %copy-start.6 = (f32[128,1280]{1,0:T(8,128)S(1)}, f32[128,1280]{1,0:T(8,128)}, u32[]{:S(2)}) copy-start(f32[128,1280]{1,0:T(8,128)} %param.14) | copy-start | bytes 1966084
  11.4 25.3 %copy-start.7 = (f32[128,1280]{1,0:T(8,128)S(1)}, f32[128,1280]{1,0:T(8,128)}, u32[]{:S(2)}) copy-start(f32[128,1280]{1,0:T(8,128)} %param.21) | copy-start | bytes 1966084
  11.4 196.5 %all-gather.8.cloned.1.call-start = ((), (), s32[]{:S(2)}) async-start(), calls=%async_computation.1 | async-start | bytes 5898240 | tf_op jit(solution)/shard_map/all_gather | solution.py:17
  36.5 0.8 copy-start.5
  37.3 64.1 %copy-start.18 = (pred[128,128]{1,0:T(8,128)(4,1)}, pred[128,128]{1,0:T(8,128)(4,1)S(1)}, u32[]{:S(2)}) copy-start(pred[128,128]{1,0:T(8,128)(4,1)S(1)} %iota_compare_fusion) | copy-start | bytes 49156
  37.6 63.9 %copy-start.12 = (f32[128,128]{1,0:T(8,128)}, f32[128,128]{1,0:T(8,128)S(1)}, u32[]{:S(2)}) copy-start(f32[128,128]{1,0:T(8,128)S(1)} %fusion.70) | copy-start | bytes 196612
  100.7 0.7 copy-start.22
  100.8 0.7 copy-start.23
  101.5 2.8 %copy-start.8 = (f32[128,20,64]{0,2,1:T(8,128)}, f32[128,20,64]{0,2,1:T(8,128)S(1)}, u32[]{:S(2)}) copy-start(f32[128,20,64]{0,2,1:T(8,128)S(1)} %convolution_bitcast_fusion.1) | copy-start | bytes 1966084
  101.5 2.8 %copy-start.17 = (f32[1280]{0:T(1024)S(1)}, f32[1280]{0:T(1024)}, u32[]{:S(2)}) copy-start(f32[1280]{0:T(1024)} %param.20) | copy-start | bytes 15364
  111.8 0.8 copy-start.1
  111.8 2.4 copy-start.4
  114.1 1.2 copy-start.3
  114.1 145.4 %all-reduce.7.cloned.1.call-start = ((), (), s32[]{:S(2)}) async-start(), calls=%async_computation.2 | async-start | bytes 262144 | tf_op jit(solution)/shard_map/psum | solution.py:142
  114.2 2.3 copy-start.2
  115.3 1.2 copy-start.13
  115.3 1.2 copy-start.15
  115.3 1.2 copy-start.19
  222.0 0.8 copy-start.11
  222.8 4.2 %copy-start.9 = (f32[128,20,64]{0,2,1:T(8,128)S(1)}, f32[128,20,64]{0,2,1:T(8,128)}, u32[]{:S(2)}) copy-start(f32[128,20,64]{0,2,1:T(8,128)} %copy-done.8) | copy-start | bytes 1966084
  227.0 3.6 %copy-start.16 = (f32[20,1]{1,0:T(8,128)S(1)}, f32[20,1]{1,0:T(8,128)}, u32[]{:S(2)}) copy-start(f32[20,1]{1,0:T(8,128)} %fusion.61) | copy-start | bytes 244
  227.0 3.6 %copy-start.20 = (f32[20,128]{1,0:T(8,128)S(1)}, f32[20,128]{1,0:T(8,128)}, u32[]{:S(2)}) copy-start(f32[20,128]{1,0:T(8,128)} %get-tuple-element.511) | copy-start | bytes 30724
  227.0 3.6 %copy-start.21 = (f32[20,128]{1,0:T(8,128)S(1)}, f32[20,128]{1,0:T(8,128)}, u32[]{:S(2)}) copy-start(f32[20,128]{1,0:T(8,128)} %get-tuple-element.512) | copy-start | bytes 30724
Sparse Core Ops, SparseCore 0:
  11.5 89.0 all-gather.5
  114.3 93.6 all-gather.7
  230.7 28.7 all-reduce.6
where the time goes:
time: 270 us; the launch traced here: 269 us
  waiting for transfers between devices  176 us (65%)
  blocking collectives  29.1 us (11%)
  matrix products  18.3 us (7%)
  local copies, waits for them, and re-layouts  15.1 us (6%)
  other arithmetic  15.1 us (6%)
  between operations  14.8 us (5%)
    all_gather x2, waiting for transfers between devices, entering(): gathered = jax.tree.map(lambda a: lax.all_gather(a, axis), part)  150 us
    psum x1, waiting for transfers between devices, local(): grad_write, grad_read = lax.psum((grad_write, grad_read), 'head')  25.9 us
    unnamed x1, blocking collectives  23.4 us
    dot_general x3, matrix products, block_step(): within = jnp.einsum('hij,jhp->ihp', masked, scaled, precision=highest)  9.52 us
    unnamed x60, local copies, waits for them, and re-layouts  8.98 us
    add x7, other arithmetic, merge_pairs(): later[0][:, None, None] * earlier[1] + later[1]  8.71 us
    psum x1, blocking collectives, local(): lax.psum((jnp.sum(gated_out * gated_out, axis=1), jnp.sum(weighted * gate...  5.7 us
  transfers between devices with their start and end apart: 3, of which 3 were waited for; matrix products, arithmetic and copies ran while one was open for 4% of the time, Pallas kernels for 0%

commit v1 on v0

--- a/solution.py
+++ b/solution.py
@@ -10,20 +10,91 @@
 highest = lax.Precision.HIGHEST
 
 
-def entering(part, axis, combine, identity, reverse):
+def combine(earlier, later):
+    return (earlier[0] * later[0], later[0][:, None, None] * earlier[1] + later[1])
+
+
+def pair_scan(decay, state, axis, reverse):
     count = lax.axis_size(axis)
+    if count == 1:
+        return jnp.zeros_like(state)
+    assert count % 2 == 0 and decay.shape[0] % 2 == 0
     place = lax.axis_index(axis)
-    ahead = count - 1 - place if reverse else place
-    gathered = jax.tree.map(lambda a: lax.all_gather(a, axis), part)
-    state = jax.tree.map(lambda a, e: jnp.zeros_like(a) + jnp.asarray(e, a.dtype), part, identity)
-
-    def one(step, state):
-        source = count - 1 - step if reverse else step
-        return combine(
-            state, jax.tree.map(lambda a: lax.dynamic_index_in_dim(a, source, 0, False), gathered)
-        )
-
-    return lax.fori_loop(0, ahead, one, state)
+    virt = count - 1 - place if reverse else place
+
+    def phys(u):
+        return count - 1 - u if reverse else u
+
+    half = decay.shape[0] // 2
+    groups = count // 2
+    side = virt % 2
+    group = virt // 2
+    first = side == 0
+    own_start = (1 - side) * half
+    send_start = side * half
+
+    def part(x, start):
+        return lax.dynamic_slice_in_dim(x, start, half, 0)
+
+    a_own, s_own = part(decay, own_start), part(state, own_start)
+    a_snd, s_snd = part(decay, send_start), part(state, send_start)
+    swap = [(phys(u), phys(u ^ 1)) for u in range(count)]
+    a_rcv, s_rcv = lax.ppermute((a_snd, s_snd), axis, swap)
+    lead = (jnp.where(first, a_own, a_rcv), jnp.where(first, s_own, s_rcv))
+    trail = (jnp.where(first, a_rcv, a_own), jnp.where(first, s_rcv, s_own))
+    a_tot, s_tot = combine(lead, trail)
+
+    def shift_pairs(k):
+        return [
+            (phys(2 * g + x), phys(2 * (g + k) + x)) for g in range(groups - k) for x in (0, 1)
+        ]
+
+    if groups <= 4:
+        a_g = jnp.ones_like(a_tot)
+        s_g = jnp.zeros_like(s_tot)
+        for r in range(groups - 1):
+            out = combine((a_g, s_g), (a_tot, s_tot))
+            pairs = [(phys(2 * r + x), phys(2 * (r + 1) + x)) for x in (0, 1)]
+            if r == groups - 2:
+                s_in = lax.ppermute(out[1], axis, pairs)
+                a_in = a_g
+            else:
+                a_in, s_in = lax.ppermute(out, axis, pairs)
+            dst = group == r + 1
+            a_g = jnp.where(dst, a_in, a_g)
+            s_g = jnp.where(dst, s_in, s_g)
+    else:
+        a_g, s_g = lax.ppermute((a_tot, s_tot), axis, shift_pairs(1))
+        a_g = jnp.where(group == 0, 1.0, a_g)
+        s_g = jnp.where(group == 0, 0.0, s_g)
+        k = 1
+        while k < groups:
+            got = lax.ppermute((a_g, s_g), axis, shift_pairs(k))
+            a_c, s_c = combine(got, (a_g, s_g))
+            a_g = jnp.where(group >= k, a_c, a_g)
+            s_g = jnp.where(group >= k, s_c, s_g)
+            k *= 2
+
+    with_lead_own = a_own[:, None, None] * s_g + s_own
+    with_lead_rcv = a_rcv[:, None, None] * s_g + s_rcv
+    send = jnp.where(first, with_lead_own, s_g)
+    keep = jnp.where(first, s_g, with_lead_rcv)
+    other = lax.ppermute(send, axis, swap)
+    return jnp.where(
+        first, jnp.concatenate([other, keep], 0), jnp.concatenate([keep, other], 0)
+    )
+
+
+def butterfly_psum(parts, axis):
+    count = lax.axis_size(axis)
+    if count & (count - 1):
+        return lax.psum(parts, axis)
+    k = 1
+    while k < count:
+        got = lax.ppermute(parts, axis, [(i, i ^ k) for i in range(count)])
+        parts = jax.tree.map(jnp.add, parts, got)
+        k *= 2
+    return parts
 
 
 def block_step(carry_state, inputs, skip_scale):
@@ -71,20 +142,6 @@
     return (last_state, outputs.reshape(length, head_count * head_width))
 
 
-def merge_pairs(earlier, later):
-    return (earlier[0] * later[0], later[0][:, None, None] * earlier[1] + later[1])
-
-
-def carry_forward(decay_pair):
-    identity = (jnp.ones_like(decay_pair[0]), jnp.zeros_like(decay_pair[1]))
-    return entering(decay_pair, "seq", merge_pairs, identity, False)[1]
-
-
-def carry_backward(decay_pair):
-    identity = (jnp.ones_like(decay_pair[0]), jnp.zeros_like(decay_pair[1]))
-    return entering(decay_pair, "seq", merge_pairs, identity, True)[1]
-
-
 def local(
     features,
     gate_pre,
@@ -107,7 +164,7 @@
     to_end = jnp.exp(cumul[:, -1:] - cumul)
     weighted_in = scaled * jnp.transpose(to_end)[:, :, None]
     local_state = jnp.einsum("jhp,jn->hpn", weighted_in, write_keys, precision=highest)
-    state_in = carry_forward((decay_total, local_state))
+    state_in = pair_scan(decay_total, local_state, "seq", False)
 
     def local_mixer(feat_in, step_in, decay_factors, writes, read_in):
         return run_mixer(
@@ -122,7 +179,7 @@
     active = gate_pre * sigmoid_gate
     gated_out = mixed_out * active
     weighted = out_grad * norm_gain[None, :]
-    square_sum, cross_sum = lax.psum(
+    square_sum, cross_sum = butterfly_psum(
         (jnp.sum(gated_out * gated_out, axis=1), jnp.sum(weighted * gated_out, axis=1)), "head"
     )
     inverse = lax.rsqrt(square_sum / channels + eps)
@@ -135,11 +192,11 @@
     from_start = jnp.transpose(jnp.exp(cumul))
     weighted_grad = grad_mixed.reshape(length, head_count, head_width) * from_start[:, :, None]
     local_grad = jnp.einsum("jhp,jn->hpn", weighted_grad, read_queries, precision=highest)
-    state_grad = carry_backward((decay_total, local_grad))
+    state_grad = pair_scan(decay_total, local_grad, "seq", True)
     grad_features, grad_steps, grad_decay, grad_write, grad_read = pullback(
         (state_grad, grad_mixed)
     )
-    grad_write, grad_read = lax.psum((grad_write, grad_read), "head")
+    grad_write, grad_read = butterfly_psum((grad_write, grad_read), "head")
     return (grad_features, grad_gate, grad_write, grad_read, grad_steps, grad_decay)
 
 

time: 270 us -> 123 us (0.46)
  waiting for transfers between devices: 176 us -> 65.2 us
  blocking collectives: 29.1 us -> 0 us
  starting transfers between devices: 0.12 us -> 20.2 us
  between operations: 14.8 us -> 1.17 us
  local copies, waits for them, and re-layouts: 15.1 us -> 7.17 us
  other arithmetic: 15.1 us -> 12.3 us
    all_gather x2 -> x0, waiting for transfers between devices: 150 us -> none  [entering(): gathered = jax.tree.map(lambda a: lax.all_gather(a, axis), part)]
    ppermute x0 -> x20, waiting for transfers between devices: none -> 65.2 us  [the longest x2 30.4 us: pair_scan(): s_in = lax.ppermute(out[1], axis, pairs)]
    psum x1 -> x0, waiting for transfers between devices: 25.9 us -> none  [local(): grad_write, grad_read = lax.psum((grad_write, grad_read), 'head')]
    unnamed x1 -> x0, blocking collectives: 23.4 us -> none
    ppermute x0 -> x20, starting transfers between devices: none -> 20.2 us  [the longest x4 6.97 us: pair_scan(): a_in, s_in = lax.ppermute(out, axis, pairs)]
    psum x1 -> x0, blocking collectives: 5.7 us -> none  [local(): lax.psum((jnp.sum(gated_out * gated_out, axis=1), jnp.sum(weighted * gate...]
    mul x7 -> x0, local copies, waits for them, and re-layouts: 4.87 us -> none  [merge_pairs(): later[0][:, None, None] * earlier[1] + later[1]]
    add x7 -> x12, other arithmetic: 8.71 us -> 4.31 us  [the longest x6 2.16 us: combine(): later[0][:, None, None] * earlier[1] + later[1]]
  transfers between devices with their start and end apart: 3 -> 20, of which waited for: 3 -> 12; matrix products, arithmetic and copies ran while one was open for 4% -> 13% of each run, Pallas kernels for 0% -> 0%
where the time goes in v1:
time: 123 us; the launch traced here: 122 us
  waiting for transfers between devices  65.2 us (53%)
  starting transfers between devices  20.2 us (16%)
  matrix products  16.1 us (13%)
  other arithmetic  12.3 us (10%)
  local copies, waits for them, and re-layouts  7.17 us (6%)
    ppermute x2, waiting for transfers between devices, pair_scan(): s_in = lax.ppermute(out[1], axis, pairs)  30.4 us
    ppermute x4, waiting for transfers between devices, pair_scan(): a_rcv, s_rcv = lax.ppermute((a_snd, s_snd), axis, swap)  14.5 us
    dot_general x3, matrix products, block_step(): within = jnp.einsum('hij,jhp->ihp', masked, scaled, precision=highest)  9.58 us
    ppermute x8, waiting for transfers between devices, butterfly_psum(): got = lax.ppermute(parts, axis, [(i, i ^ k) for i in range(count)])  8.19 us
    ppermute x4, starting transfers between devices, pair_scan(): a_in, s_in = lax.ppermute(out, axis, pairs)  6.97 us
    unnamed x59, local copies, waits for them, and re-layouts  6.65 us
    ppermute x2, waiting for transfers between devices, pair_scan(): other = lax.ppermute(send, axis, swap)  6.42 us
    ppermute x4, waiting for transfers between devices, pair_scan(): a_in, s_in = lax.ppermute(out, axis, pairs)  5.66 us
  transfers between devices with their start and end apart: 20, of which 12 were waited for; matrix products, arithmetic and copies ran while one was open for 13% of the time, Pallas kernels for 0%

profile of v1, /device:TPU:0, one launch (start us, length us, event | category | flops | bytes accessed | tf_op | source)
XLA Modules:
  0.0 122.1 jit_solution(16084576789941205583)
XLA Ops:
  0.7 1.0 reduce_window_sum.30
  1.9 2.9 %collective-permute-start.10 = (f32[10]{0:T(128)S(1)}, f32[10]{0:T(128)S(1)}, u32[]{:S(2)}, u32[]{:S(2)}) collective-permute-start(f32[10]{0:T(128)S(1)} %dynamic_slice.88), channel_id=1, source_target_pairs={{28,24},{24,28},{20,16},{16,20},{12,8},{8,12},{4,0},{0,4},{29,25},... | collective-permute-start | bytes 128 | tf_op jit(solution)/shard_map/ppermute | solution.py:42
  5.0 1.3 %copy.24 = f32[128,1280]{0,1:T(8,128)S(1)} copy(f32[128,1280]{1,0:T(8,128)} %param.9) | data formatting | bytes 1310720 | tf_op args[0]
  7.8 2.0 %collective-permute-start = (f32[10]{0:T(128)S(1)}, f32[10]{0:T(128)S(1)}, u32[]{:S(2)}, u32[]{:S(2)}) collective-permute-start(f32[10]{0:T(128)S(1)} %get-tuple-element.411), channel_id=1, source_target_pairs={{0,4},{4,0},{8,12},{12,8},{16,20},{20,16},{24,28},{28,24},{1,5},{5... | collective-permute-start | bytes 128 | tf_op jit(solution)/shard_map/ppermute | solution.py:42
  9.8 6.6 %collective-permute-done = f32[10]{0:T(128)S(1)} collective-permute-done((f32[10]{0:T(128)S(1)}, f32[10]{0:T(128)S(1)}, u32[]{:S(2)}, u32[]{:S(2)}) %collective-permute-start) | collective-permute-done | bytes 72 | tf_op jit(solution)/shard_map/ppermute | solution.py:42
  16.6 3.5 %collective-permute-start.2 = (f32[10,64,128]{2,1,0:T(8,128)S(1)}, f32[10,64,128]{2,1,0:T(8,128)S(1)}, u32[]{:S(2)}, u32[]{:S(2)}) collective-permute-start(f32[10,64,128]{2,1,0:T(8,128)S(1)} %get-tuple-element.396), channel_id=1, source_target_pairs={{0,8},{4,12},{1,9},{5,13},{2,10},{6,14},{3,11},{7,15}} | collective-permute-start | bytes 983048 | tf_op jit(solution)/shard_map/ppermute | solution.py:62
  20.1 5.7 %collective-permute-done.2 = f32[10,64,128]{2,1,0:T(8,128)S(1)} collective-permute-done((f32[10,64,128]{2,1,0:T(8,128)S(1)}, f32[10,64,128]{2,1,0:T(8,128)S(1)}, u32[]{:S(2)}, u32[]{:S(2)}) %collective-permute-start.2) | collective-permute-done | bytes 327712 | tf_op jit(solution)/shard_map/ppermute | solution.py:62
  25.9 1.4 %collective-permute-start.3 = (f32[10,64,128]{2,1,0:T(8,128)S(1)}, f32[10,64,128]{2,1,0:T(8,128)}, u32[]{:S(2)}, u32[]{:S(2)}) collective-permute-start(f32[10,64,128]{2,1,0:T(8,128)S(1)} %multiply_add_fusion.6), channel_id=1, source_target_pairs={{8,16},{12,20},{9,17},{13,21},{10,18},{14,22},{11,19},{15,23}} | collective-permute-start | bytes 983048 | tf_op jit(solution)/shard_map/ppermute | solution.py:62
  29.1 1.3 %copy.27 = f32[128,1280]{0,1:T(8,128)S(1)} copy(f32[128,1280]{1,0:T(8,128)} %param.17) | data formatting | bytes 1310720 | tf_op args[8]
  31.2 1.1 add_select_fusion.3
  33.2 6.4 %collective-permute-done.5 = f32[10,64,128]{2,1,0:T(8,128)S(1)} collective-permute-done((f32[10,64,128]{2,1,0:T(8,128)S(1)}, f32[10,64,128]{2,1,0:T(8,128)S(1)}, u32[]{:S(2)}, u32[]{:S(2)}) %collective-permute-start.5) | collective-permute-done | bytes 327712 | tf_op jit(solution)/shard_map/ppermute | solution.py:82
  40.3 2.7 %multiply_add_fusion.2 = f32[128,20,64]{0,2,1:T(8,128)S(1)} fusion(f32[128,20,64]{0,2,1:T(8,128)S(1)} %bitcast.90, f32[128,20,64]{0,2,1:T(8,128)S(1)} %convolution_bitcast_fusion.1, f32[128,128]{1,0:T(8,128)S(1)} %fusion.73, f32[20,128]{1,0:T(8,128)S(1)} %reduce_window_sum.30, pred[128,128]{1,0:T(8,128)(4,1)S(1)} %iota_compare_fusion, ...), kind=kOutput, calls=%fused_computation.37 | convolution fusion | flops 253788160 | bytes 2078800 | tf_op jit(solution)/shard_map/jvp()/while/body/eval_jaxpr/hij,jhp->ihp/dot_general | solution.py:112
  44.6 1.5 %collective-permute-start.7 = (f32[128]{0:T(128)S(1)}, f32[128]{0:T(128)S(1)}, u32[]{:S(2)}, u32[]{:S(2)}) collective-permute-start(f32[128]{0:T(128)S(1)} %add.145), channel_id=1, source_target_pairs={{0,2},{1,3},{2,0},{3,1},{4,6},{5,7},{6,4},{7,5},{8,10},{9,11},{10,... | collective-permute-start | bytes 1544 | tf_op jit(solution)/shard_map/ppermute | solution.py:94
  46.6 1.5 %collective-permute-done.7 = f32[128]{0:T(128)S(1)} collective-permute-done((f32[128]{0:T(128)S(1)}, f32[128]{0:T(128)S(1)}, u32[]{:S(2)}, u32[]{:S(2)}) %collective-permute-start.7) | collective-permute-done | bytes 544 | tf_op jit(solution)/shard_map/ppermute | solution.py:94
  48.1 1.5 %collective-permute-done.9 = f32[128]{0:T(128)S(1)} collective-permute-done((f32[128]{0:T(128)S(1)}, f32[128]{0:T(128)S(1)}, u32[]{:S(2)}, u32[]{:S(2)}) %collective-permute-start.9) | collective-permute-done | bytes 544 | tf_op jit(solution)/shard_map/ppermute | solution.py:94
  49.6 1.5 %bitcast_multiply_fusion = (f32[128,1280]{0,1:T(8,128)}, f32[128,1280]{0,1:T(8,128)S(1)}, f32[128,1280]{0,1:T(8,128)}) fusion(f32[128,20]{0,1:T(8,128)S(1)} %get-tuple-element.410, f32[128,1280]{0,1:T(8,128)S(1)} %copy.26, f32[128,20,64]{0,2,1:T(8,128)S(1)} %multiply_add_fusion.2, f32[128]{0:T(128)S(1)} %get-tuple-element.392, f32[128,1280]{0,1:T(8,128)S(1)} %copy.27, ...), kind=kLoop, calls=%fused_computation.19 | loop fusion | flops 2785280 | bytes 3948544 | tf_op jit(solution)/shard_map/transpose(jvp())/while/body/eval_jaxpr/mul | solution.py:114
  52.5 7.9 %collective-permute-done.11 = f32[10,64,128]{2,1,0:T(8,128)S(1)} collective-permute-done((f32[10,64,128]{2,1,0:T(8,128)S(1)}, f32[10,64,128]{2,1,0:T(8,128)S(1)}, u32[]{:S(2)}, u32[]{:S(2)}) %collective-permute-start.11) | collective-permute-done | bytes 327712 | tf_op jit(solution)/shard_map/ppermute | solution.py:42
  62.0 1.4 %collective-permute-start.13 = (f32[10,64,128]{2,1,0:T(8,128)}, f32[10,64,128]{2,1,0:T(8,128)}, u32[]{:S(2)}, u32[]{:S(2)}) collective-permute-start(f32[10,64,128]{2,1,0:T(8,128)} %multiply_add_fusion.4), channel_id=1, source_target_pairs={{20,12},{16,8},{21,13},{17,9},{22,14},{18,10},{23,15},{19,11}} | collective-permute-start | bytes 983048 | tf_op jit(solution)/shard_map/ppermute | solution.py:62
  63.5 1.6 %collective-permute-start.14 = (f32[10,64,128]{2,1,0:T(8,128)S(1)}, f32[10,64,128]{2,1,0:T(8,128)S(1)}, u32[]{:S(2)}, u32[]{:S(2)}) collective-permute-start(f32[10,64,128]{2,1,0:T(8,128)S(1)} %get-tuple-element.384), channel_id=1, source_target_pairs={{12,4},{8,0},{13,5},{9,1},{14,6},{10,2},{15,7},{11,3}} | collective-permute-start | bytes 983048 | tf_op jit(solution)/shard_map/ppermute | solution.py:59
  65.2 3.6 %fusion.15 = (f32[20,128]{1,0:T(8,128)}, f32[20,128]{1,0:T(8,128)}, f32[128,128]{1,0:T(8,128)S(1)}) fusion(f32[128,128]{1,0:T(8,128)S(1)} %fusion.73, f32[20,128]{1,0:T(8,128)S(1)} %reduce_window_sum.30, pred[128,128]{1,0:T(8,128)(4,1)S(1)} %iota_compare_fusion, f32[20,64,128]{2,1,0:T(8,128)S(1)} %bitcast.86, f32[128,20,64]{0,2,1:T(8,128)S(1)} %bitcast.91, ...), kind=kOutput, calls=%fused_computation.16 | convolution fusion | flops 255405056 | bytes 1499136 | tf_op jit(solution)/shard_map/transpose(jvp())/while/body/eval_jaxpr/hij,jhp->ihp/dot_general | solution.py:112
  69.0 30.4 %collective-permute-done.14 = f32[10,64,128]{2,1,0:T(8,128)S(1)} collective-permute-done((f32[10,64,128]{2,1,0:T(8,128)S(1)}, f32[10,64,128]{2,1,0:T(8,128)S(1)}, u32[]{:S(2)}, u32[]{:S(2)}) %collective-permute-start.14) | collective-permute-done | bytes 327712 | tf_op jit(solution)/shard_map/ppermute | solution.py:59
  100.9 1.2 %fusion.13 = f32[128,128]{1,0:T(8,128)S(1)} fusion(f32[128,128]{1,0:T(8,128)S(1)} %fusion.75, f32[128,20,64]{0,2,1:T(8,128)S(1)} %bitcast.94, f32[10,64,128]{2,1,0:T(8,128)S(1)} %get-tuple-element.408, f32[10,64,128]{2,1,0:T(8,128)S(1)} %collective-permute-done.5, pred[]{:T(512)S(6)} %eq.27), kind=kOutput, calls=%fused_computation.14 | convolution fusion | flops 252166144 | bytes 1441793 | tf_op jit(solution)/shard_map/transpose(jvp())/while/body/eval_jaxpr/in,hpn->ihp/dot_general | solution.py:113
  102.2 1.2 %collective-permute-done.18 = f32[128,128]{1,0:T(8,128)S(1)} collective-permute-done((f32[128,128]{1,0:T(8,128)S(1)}, f32[128,128]{1,0:T(8,128)S(1)}, u32[]{:S(2)}, u32[]{:S(2)}) %collective-permute-start.18) | collective-permute-done | bytes 65568 | tf_op jit(solution)/shard_map/ppermute | solution.py:94
  104.1 0.9 fusion.74
  105.1 1.1 copy.32
  106.1 1.7 %collective-permute-done.19 = f32[128,128]{1,0:T(8,128)} collective-permute-done((f32[128,128]{1,0:T(8,128)S(1)}, f32[128,128]{1,0:T(8,128)}, u32[]{:S(2)}, u32[]{:S(2)}) %collective-permute-start.19) | collective-permute-done | bytes 65568 | tf_op jit(solution)/shard_map/ppermute | solution.py:94
  107.9 1.5 %add.164 = f32[128,128]{1,0:T(8,128)} add(f32[128,128]{1,0:T(8,128)S(1)} %add.163, f32[128,128]{1,0:T(8,128)} %collective-permute-done.19) | non-fusion elementwise | flops 16384 | bytes 196608 | tf_op jit(solution)/shard_map/add | solution.py:95
  110.5 3.2 %multiply_reduce_fusion.2 = (f32[128,20]{0,1:T(8,128)S(1)}, f32[128,20]{0,1:T(8,128)}, f32[128,20,64]{0,2,1:T(8,128)}, f32[128,20]{0,1:T(8,128)S(1)}) fusion(f32[128,20,64]{0,2,1:T(8,128)S(1)} %convolution_bitcast_fusion, f32[128,20,64]{0,2,1:T(8,128)S(1)} %bitcast.92, f32[128,20]{0,1:T(8,128)S(1)} %bitcast.99, f32[128,20,64]{0,2,1:T(8,128)S(1)} %bitcast.87, ...), kind=kOutput, calls=%fused_computation.25 | convolution fusion | flops 254927360 | bytes 4075600 | tf_op jit(solution)/shard_map/transpose(jvp())/while/body/eval_jaxpr/hij,jhp->ihp/dot_general | solution.py:112
  114.5 1.2 %fusion.12 = f32[128,128]{1,0:T(8,128)S(1)} fusion(f32[128,128]{1,0:T(8,128)S(1)} %copy-done.12, f32[128,20,64]{0,2,1:T(8,128)S(1)} %bitcast.93, f32[128,20]{0,1:T(8,128)S(1)} %copy-done.14, f32[128,20]{0,1:T(8,128)S(1)} %bitcast.100, f32[10,64,128]{2,1,0:T(8,128)S(1)} %get-tuple-element.406, f32[10,64,128]{2,1,0:T(8,128)S(1)} %collective-permute-done.15, ...), kind=kOutput, calls=%fused_computation.13 | convolution fusion | flops 252493824 | bytes 1462273 | tf_op jit(solution)/shard_map/transpose(jvp())/while/body/eval_jaxpr/jhp,jn->hpn/dot_general | solution.py:118
  116.1 1.0 collective-permute-done.16
  117.9 1.1 copy.31
  119.0 1.8 %reduce_window_sum.31 = f32[20,128]{1,0:T(8,128)} reduce-window(f32[20,128]{1,0:T(8,128)S(1)} %fusion.57, f32[]{:T(128)} %constant.158.clone.1), window={size=1x128 pad=0_0x0_127}, to_apply=%region_11.12 | reduce-window | flops 325120 | bytes 20484 | tf_op jit(solution)/shard_map/transpose(jvp())/while/body/eval_jaxpr/jit(cumsum)/reduce_window_sum | solution.py:103
  (113 shorter events, 18.0 us)
Async XLA Ops:
  0.6 32.3 %copy-start = (f32[128,128]{1,0:T(8,128)S(1)}, f32[128,128]{1,0:T(8,128)}, u32[]{:S(2)}) copy-start(f32[128,128]{1,0:T(8,128)} %param.12) | copy-start | bytes 196612
  1.9 5.3 %collective-permute-start.10 = (f32[10]{0:T(128)S(1)}, f32[10]{0:T(128)S(1)}, u32[]{:S(2)}, u32[]{:S(2)}) collective-permute-start(f32[10]{0:T(128)S(1)} %dynamic_slice.88), channel_id=1, source_target_pairs={{28,24},{24,28},{20,16},{16,20},{12,8},{8,12},{4,0},{0,4},{29,25},... | collective-permute-start | bytes 128 | tf_op jit(solution)/shard_map/ppermute | solution.py:42
  6.3 34.0 %copy-start.2 = (f32[128,1280]{0,1:T(8,128)}, f32[128,1280]{0,1:T(8,128)S(1)}, u32[]{:S(2)}) copy-start(f32[128,1280]{0,1:T(8,128)S(1)} %copy.24) | copy-start | bytes 1966084
  7.1 9.4 %collective-permute-start.1 = (f32[10,64,128]{2,1,0:T(8,128)S(1)}, f32[10,64,128]{2,1,0:T(8,128)S(1)}, u32[]{:S(2)}, u32[]{:S(2)}) collective-permute-start(f32[10,64,128]{2,1,0:T(8,128)S(1)} %constant_dynamic-slice_fusion.1), channel_id=1, source_target_pairs={{0,4},{4,0},{8,12},{12,8},{16,20},{20,16},{24,28},{28,24},{1,5},{5... | collective-permute-start | bytes 983048 | tf_op jit(solution)/shard_map/ppermute | solution.py:42
  7.2 2.6 %copy-start.22 = (f32[10]{0:T(128)}, f32[10]{0:T(128)S(1)}, u32[]{:S(2)}) copy-start(f32[10]{0:T(128)S(1)} %collective-permute-done.10) | copy-start | bytes 124
  7.8 8.6 %collective-permute-start = (f32[10]{0:T(128)S(1)}, f32[10]{0:T(128)S(1)}, u32[]{:S(2)}, u32[]{:S(2)}) collective-permute-start(f32[10]{0:T(128)S(1)} %get-tuple-element.411), channel_id=1, source_target_pairs={{0,4},{4,0},{8,12},{12,8},{16,20},{20,16},{24,28},{28,24},{1,5},{5... | collective-permute-start | bytes 128 | tf_op jit(solution)/shard_map/ppermute | solution.py:42
  16.6 9.2 %collective-permute-start.2 = (f32[10,64,128]{2,1,0:T(8,128)S(1)}, f32[10,64,128]{2,1,0:T(8,128)S(1)}, u32[]{:S(2)}, u32[]{:S(2)}) collective-permute-start(f32[10,64,128]{2,1,0:T(8,128)S(1)} %get-tuple-element.396), channel_id=1, source_target_pairs={{0,8},{4,12},{1,9},{5,13},{2,10},{6,14},{3,11},{7,15}} | collective-permute-start | bytes 983048 | tf_op jit(solution)/shard_map/ppermute | solution.py:62
  25.9 1.4 %collective-permute-start.3 = (f32[10,64,128]{2,1,0:T(8,128)S(1)}, f32[10,64,128]{2,1,0:T(8,128)}, u32[]{:S(2)}, u32[]{:S(2)}) collective-permute-start(f32[10,64,128]{2,1,0:T(8,128)S(1)} %multiply_add_fusion.6), channel_id=1, source_target_pairs={{8,16},{12,20},{9,17},{13,21},{10,18},{14,22},{11,19},{15,23}} | collective-permute-start | bytes 983048 | tf_op jit(solution)/shard_map/ppermute | solution.py:62
  28.2 2.2 %collective-permute-start.4 = (f32[10,64,128]{2,1,0:T(8,128)}, f32[10,64,128]{2,1,0:T(8,128)S(1)}, u32[]{:S(2)}, u32[]{:S(2)}) collective-permute-start(f32[10,64,128]{2,1,0:T(8,128)} %get-tuple-element.394), channel_id=1, source_target_pairs={{16,24},{20,28},{17,25},{21,29},{18,26},{22,30},{19,27},{23,31}} | collective-permute-start | bytes 983048 | tf_op jit(solution)/shard_map/ppermute | solution.py:59
  32.3 7.3 %collective-permute-start.5 = (f32[10,64,128]{2,1,0:T(8,128)S(1)}, f32[10,64,128]{2,1,0:T(8,128)S(1)}, u32[]{:S(2)}, u32[]{:S(2)}) collective-permute-start(f32[10,64,128]{2,1,0:T(8,128)S(1)} %get-tuple-element.407), channel_id=1, source_target_pairs={{0,4},{4,0},{8,12},{12,8},{16,20},{20,16},{24,28},{28,24},{1,5},{5... | collective-permute-start | bytes 983048 | tf_op jit(solution)/shard_map/ppermute | solution.py:82
  32.9 32.2 %copy-start.16 = (pred[128,128]{1,0:T(8,128)(4,1)}, pred[128,128]{1,0:T(8,128)(4,1)S(1)}, u32[]{:S(2)}) copy-start(pred[128,128]{1,0:T(8,128)(4,1)S(1)} %iota_compare_fusion) | copy-start | bytes 49156
  40.3 2.8 %copy-start.8 = (f32[128,20,64]{0,2,1:T(8,128)}, f32[128,20,64]{0,2,1:T(8,128)S(1)}, u32[]{:S(2)}) copy-start(f32[128,20,64]{0,2,1:T(8,128)S(1)} %convolution_bitcast_fusion.1) | copy-start | bytes 1966084
  40.3 2.8 %copy-start.15 = (f32[1280]{0:T(1024)S(1)}, f32[1280]{0:T(1024)}, u32[]{:S(2)}) copy-start(f32[1280]{0:T(1024)} %param.16) | copy-start | bytes 15364
  43.4 1.2 collective-permute-start.6
  43.5 2.6 %collective-permute-start.8 = (f32[128]{0:T(128)S(1)}, f32[128]{0:T(128)S(1)}, u32[]{:S(2)}, u32[]{:S(2)}) collective-permute-start(f32[128]{0:T(128)S(1)} %get-tuple-element.379), channel_id=1, source_target_pairs={{0,1},{1,0},{2,3},{3,2},{4,5},{5,4},{6,7},{7,6},{8,9},{9,8},{10,11... | collective-permute-start | bytes 1544 | tf_op jit(solution)/shard_map/ppermute | solution.py:94
  44.6 3.5 %collective-permute-start.7 = (f32[128]{0:T(128)S(1)}, f32[128]{0:T(128)S(1)}, u32[]{:S(2)}, u32[]{:S(2)}) collective-permute-start(f32[128]{0:T(128)S(1)} %add.145), channel_id=1, source_target_pairs={{0,2},{1,3},{2,0},{3,1},{4,6},{5,7},{6,4},{7,5},{8,10},{9,11},{10,... | collective-permute-start | bytes 1544 | tf_op jit(solution)/shard_map/ppermute | solution.py:94
  46.1 3.5 %collective-permute-start.9 = (f32[128]{0:T(128)S(1)}, f32[128]{0:T(128)S(1)}, u32[]{:S(2)}, u32[]{:S(2)}) collective-permute-start(f32[128]{0:T(128)S(1)} %add.149), channel_id=1, source_target_pairs={{0,2},{1,3},{2,0},{3,1},{4,6},{5,7},{6,4},{7,5},{8,10},{9,11},{10,... | collective-permute-start | bytes 1544 | tf_op jit(solution)/shard_map/ppermute | solution.py:94
  51.9 8.5 %collective-permute-start.11 = (f32[10,64,128]{2,1,0:T(8,128)S(1)}, f32[10,64,128]{2,1,0:T(8,128)S(1)}, u32[]{:S(2)}, u32[]{:S(2)}) collective-permute-start(f32[10,64,128]{2,1,0:T(8,128)S(1)} %constant_dynamic-slice_fusion), channel_id=1, source_target_pairs={{28,24},{24,28},{20,16},{16,20},{12,8},{8,12},{4,0},{0,4},{29,25},... | collective-permute-start | bytes 983048 | tf_op jit(solution)/shard_map/ppermute | solution.py:42
  60.4 0.7 collective-permute-start.12
  62.0 1.4 %collective-permute-start.13 = (f32[10,64,128]{2,1,0:T(8,128)}, f32[10,64,128]{2,1,0:T(8,128)}, u32[]{:S(2)}, u32[]{:S(2)}) collective-permute-start(f32[10,64,128]{2,1,0:T(8,128)} %multiply_add_fusion.4), channel_id=1, source_target_pairs={{20,12},{16,8},{21,13},{17,9},{22,14},{18,10},{23,15},{19,11}} | collective-permute-start | bytes 983048 | tf_op jit(solution)/shard_map/ppermute | solution.py:62
  63.5 35.9 %collective-permute-start.14 = (f32[10,64,128]{2,1,0:T(8,128)S(1)}, f32[10,64,128]{2,1,0:T(8,128)S(1)}, u32[]{:S(2)}, u32[]{:S(2)}) collective-permute-start(f32[10,64,128]{2,1,0:T(8,128)S(1)} %get-tuple-element.384), channel_id=1, source_target_pairs={{12,4},{8,0},{13,5},{9,1},{14,6},{10,2},{15,7},{11,3}} | collective-permute-start | bytes 983048 | tf_op jit(solution)/shard_map/ppermute | solution.py:59
  65.2 34.3 %copy-start.23 = (f32[10]{0:T(128)S(1)}, f32[10]{0:T(128)}, u32[]{:S(2)}) copy-start(f32[10]{0:T(128)} %copy-done.22) | copy-start | bytes 124
  65.2 34.3 %copy-start.24 = (f32[10]{0:T(128)S(1)}, f32[10]{0:T(128)}, u32[]{:S(2)}) copy-start(f32[10]{0:T(128)} %get-tuple-element.391) | copy-start | bytes 124
  100.3 9.0 %collective-permute-start.15 = (f32[10,64,128]{2,1,0:T(8,128)}, f32[10,64,128]{2,1,0:T(8,128)S(1)}, u32[]{:S(2)}, u32[]{:S(2)}) collective-permute-start(f32[10,64,128]{2,1,0:T(8,128)} %get-tuple-element.405), channel_id=1, source_target_pairs={{28,24},{24,28},{20,16},{16,20},{12,8},{8,12},{4,0},{0,4},{29,25},... | collective-permute-start | bytes 983048 | tf_op jit(solution)/shard_map/ppermute | solution.py:82
  100.9 4.2 %copy-start.1 = (f32[128,1280]{0,1:T(8,128)S(1)}, f32[128,1280]{0,1:T(8,128)}, u32[]{:S(2)}) copy-start(f32[128,1280]{0,1:T(8,128)} %get-tuple-element.402) | copy-start | bytes 1966084
  102.1 1.3 %collective-permute-start.18 = (f32[128,128]{1,0:T(8,128)S(1)}, f32[128,128]{1,0:T(8,128)S(1)}, u32[]{:S(2)}, u32[]{:S(2)}) collective-permute-start(f32[128,128]{1,0:T(8,128)S(1)} %fusion.13), channel_id=1, source_target_pairs={{0,1},{1,0},{2,3},{3,2},{4,5},{5,4},{6,7},{7,6},{8,9},{9,8},{10,11... | collective-permute-start | bytes 196616 | tf_op jit(solution)/shard_map/ppermute | solution.py:94
  103.4 4.4 %collective-permute-start.19 = (f32[128,128]{1,0:T(8,128)S(1)}, f32[128,128]{1,0:T(8,128)}, u32[]{:S(2)}, u32[]{:S(2)}) collective-permute-start(f32[128,128]{1,0:T(8,128)S(1)} %add.163), channel_id=1, source_target_pairs={{0,2},{1,3},{2,0},{3,1},{4,6},{5,7},{6,4},{7,5},{8,10},{9,11},{10,... | collective-permute-start | bytes 196616 | tf_op jit(solution)/shard_map/ppermute | solution.py:94
  114.5 3.3 %copy-start.20 = (f32[20,128]{1,0:T(8,128)S(1)}, f32[20,128]{1,0:T(8,128)}, u32[]{:S(2)}) copy-start(f32[20,128]{1,0:T(8,128)} %get-tuple-element.375) | copy-start | bytes 30724
  114.5 3.3 %copy-start.21 = (f32[20,128]{1,0:T(8,128)S(1)}, f32[20,128]{1,0:T(8,128)}, u32[]{:S(2)}) copy-start(f32[20,128]{1,0:T(8,128)} %get-tuple-element.376) | copy-start | bytes 30724
  114.5 3.4 %copy-start.10 = (f32[128,20,64]{0,2,1:T(8,128)S(1)}, f32[128,20,64]{0,2,1:T(8,128)}, u32[]{:S(2)}) copy-start(f32[128,20,64]{0,2,1:T(8,128)} %get-tuple-element.403) | copy-start | bytes 1966084
  115.8 1.3 %collective-permute-start.16 = (f32[128,128]{1,0:T(8,128)S(1)}, f32[128,128]{1,0:T(8,128)S(1)}, u32[]{:S(2)}, u32[]{:S(2)}) collective-permute-start(f32[128,128]{1,0:T(8,128)S(1)} %fusion.12), channel_id=1, source_target_pairs={{0,1},{1,0},{2,3},{3,2},{4,5},{5,4},{6,7},{7,6},{8,9},{9,8},{10,11... | collective-permute-start | bytes 196616 | tf_op jit(solution)/shard_map/ppermute | solution.py:94
  117.1 4.3 %collective-permute-start.17 = (f32[128,128]{1,0:T(8,128)S(1)}, f32[128,128]{1,0:T(8,128)S(1)}, u32[]{:S(2)}, u32[]{:S(2)}) collective-permute-start(f32[128,128]{1,0:T(8,128)S(1)} %add.161), channel_id=1, source_target_pairs={{0,2},{1,3},{2,0},{3,1},{4,6},{5,7},{6,4},{7,5},{8,10},{9,11},{10,... | collective-permute-start | bytes 196616 | tf_op jit(solution)/shard_map/ppermute | solution.py:94
  (15 other events, 18.9 us)

commit v2 on v1

--- a/solution.py
+++ b/solution.py
@@ -142,6 +142,46 @@
     return (last_state, outputs.reshape(length, head_count * head_width))
 
 
+def within_part(feat_in, step_in, decay_in, writes, read_in, skip_scale):
+    head_count, length = step_in.shape
+    head_width = feat_in.shape[1] // head_count
+    cumul = jnp.cumsum(decay_in, axis=1)
+    row_index = lax.broadcasted_iota(jnp.int32, (length, length), 0)
+    col_index = lax.broadcasted_iota(jnp.int32, (length, length), 1)
+    causal = row_index >= col_index
+    gaps = jnp.where(causal[None], cumul[:, :, None] - cumul[:, None, :], 0.0)
+    weights = jnp.where(causal[None], jnp.exp(gaps), 0.0)
+    scores = jnp.dot(read_in, jnp.transpose(writes), precision=highest)
+    feat3 = feat_in.reshape(length, head_count, head_width)
+    scaled = feat3 * jnp.transpose(step_in)[:, :, None]
+    masked = weights * scores[None]
+    within = jnp.einsum("hij,jhp->ihp", masked, scaled, precision=highest)
+    return (within + skip_scale[None, :, None] * feat3).reshape(length, -1)
+
+
+def carried_part(decay_in, read_in, state_in):
+    length = decay_in.shape[1]
+    cumul = jnp.cumsum(decay_in, axis=1)
+    carried = jnp.einsum("in,hpn->ihp", read_in, state_in, precision=highest)
+    carried = carried * jnp.transpose(jnp.exp(cumul))[:, :, None]
+    return carried.reshape(length, -1)
+
+
+def state_update(feat_in, step_in, decay_in, writes):
+    head_count, length = step_in.shape
+    head_width = feat_in.shape[1] // head_count
+    cumul = jnp.cumsum(decay_in, axis=1)
+    scaled = feat_in.reshape(length, head_count, head_width) * jnp.transpose(step_in)[:, :, None]
+    to_end = jnp.exp(cumul[:, -1:] - cumul)
+    weighted_in = scaled * jnp.transpose(to_end)[:, :, None]
+    return jnp.einsum("jhp,jn->hpn", weighted_in, writes, precision=highest)
+
+
+def end_part(feat_in, step_in, decay_in, writes, state_in):
+    total = jnp.exp(jnp.cumsum(decay_in, axis=1)[:, -1])
+    return total[:, None, None] * state_in + state_update(feat_in, step_in, decay_in, writes)
+
+
 def local(
     features,
     gate_pre,
@@ -165,16 +205,27 @@
     weighted_in = scaled * jnp.transpose(to_end)[:, :, None]
     local_state = jnp.einsum("jhp,jn->hpn", weighted_in, write_keys, precision=highest)
     state_in = pair_scan(decay_total, local_state, "seq", False)
-
-    def local_mixer(feat_in, step_in, decay_factors, writes, read_in):
-        return run_mixer(
-            feat_in, step_in, decay_factors, writes, read_in, state_in, skip_scale, BLOCK
-        )
-
-    primal, pullback = jax.vjp(
-        local_mixer, features, step_sizes, log_decay, write_keys, read_queries
-    )
-    mixed_out = primal[1]
+    single = length == BLOCK
+    if single:
+        mixed_w, pull_w = jax.vjp(
+            lambda f, s, d, w, r: within_part(f, s, d, w, r, skip_scale),
+            features, step_sizes, log_decay, write_keys, read_queries,
+        )
+        mixed_c, pull_c = jax.vjp(
+            lambda d, r: carried_part(d, r, state_in), log_decay, read_queries
+        )
+        mixed_out = mixed_w + mixed_c
+    else:
+
+        def local_mixer(feat_in, step_in, decay_factors, writes, read_in):
+            return run_mixer(
+                feat_in, step_in, decay_factors, writes, read_in, state_in, skip_scale, BLOCK
+            )
+
+        primal, pullback = jax.vjp(
+            local_mixer, features, step_sizes, log_decay, write_keys, read_queries
+        )
+        mixed_out = primal[1]
     sigmoid_gate = jax.nn.sigmoid(gate_pre)
     active = gate_pre * sigmoid_gate
     gated_out = mixed_out * active
@@ -193,10 +244,24 @@
     weighted_grad = grad_mixed.reshape(length, head_count, head_width) * from_start[:, :, None]
     local_grad = jnp.einsum("jhp,jn->hpn", weighted_grad, read_queries, precision=highest)
     state_grad = pair_scan(decay_total, local_grad, "seq", True)
-    grad_features, grad_steps, grad_decay, grad_write, grad_read = pullback(
-        (state_grad, grad_mixed)
-    )
-    grad_write, grad_read = butterfly_psum((grad_write, grad_read), "head")
+    if single:
+        gf_w, gs_w, gd_w, gw_w, gr_w = pull_w(grad_mixed)
+        gd_c, gr_c = pull_c(grad_mixed)
+        grad_read = butterfly_psum(gr_w + gr_c, "head")
+        _, pull_e = jax.vjp(
+            lambda f, s, d, w: end_part(f, s, d, w, state_in),
+            features, step_sizes, log_decay, write_keys,
+        )
+        gf_e, gs_e, gd_e, gw_e = pull_e(state_grad)
+        grad_features = gf_w + gf_e
+        grad_steps = gs_w + gs_e
+        grad_decay = gd_w + gd_c + gd_e
+        grad_write = butterfly_psum(gw_w + gw_e, "head")
+    else:
+        grad_features, grad_steps, grad_decay, grad_write, grad_read = pullback(
+            (state_grad, grad_mixed)
+        )
+        grad_write, grad_read = butterfly_psum((grad_write, grad_read), "head")
     return (grad_features, grad_gate, grad_write, grad_read, grad_steps, grad_decay)
 
 

time: 123 us -> 125 us (1.016)
  other arithmetic: 12.3 us -> 14.9 us
  starting transfers between devices: 20.2 us -> 22.2 us
  waiting for transfers between devices: 65.2 us -> 63.3 us
    unnamed x59 -> x38, local copies, waits for them, and re-layouts: 6.65 us -> 2.98 us
    ppermute x2, waiting for transfers between devices: 30.4 us -> 28.2 us  [pair_scan(): s_in = lax.ppermute(out[1], axis, pairs)]
    another operation x2 -> x5, other arithmetic: 2.83 us -> 4.87 us  [the longest x2 2.26 us: within_part(): cumul = jnp.cumsum(decay_in, axis=1)]
    ppermute x2, starting transfers between devices: 1.15 us -> 3.05 us  [pair_scan(): other = lax.ppermute(send, axis, swap)]
    ppermute x4, waiting for transfers between devices: 14.5 us -> 16.3 us  [pair_scan(): a_rcv, s_rcv = lax.ppermute((a_snd, s_snd), axis, swap)]
    add x0 -> x1, local copies, waits for them, and re-layouts: none -> 1.38 us  [local(): mixed_out = mixed_w + mixed_c]
    mul x0 -> x1, local copies, waits for them, and re-layouts: none -> 1.31 us  [local(): grad_mixed = grad_gated * active]
  transfers between devices with their start and end apart: 20 -> 20, of which waited for: 12 -> 12; matrix products, arithmetic and copies ran while one was open for 13% -> 11% of each run, Pallas kernels for 0% -> 0%
where the time goes in v2:
time: 125 us; the launch traced here: 124 us
  waiting for transfers between devices  63.3 us (51%)
  starting transfers between devices  22.2 us (18%)
  matrix products  16.4 us (13%)
  other arithmetic  14.9 us (12%)
  local copies, waits for them, and re-layouts  6.19 us (5%)
    ppermute x2, waiting for transfers between devices, pair_scan(): s_in = lax.ppermute(out[1], axis, pairs)  28.2 us
    ppermute x4, waiting for transfers between devices, pair_scan(): a_rcv, s_rcv = lax.ppermute((a_snd, s_snd), axis, swap)  16.3 us
    dot_general x3, matrix products, within_part(): within = jnp.einsum('hij,jhp->ihp', masked, scaled, precision=highest)  8.92 us
    ppermute x8, waiting for transfers between devices, butterfly_psum(): got = lax.ppermute(parts, axis, [(i, i ^ k) for i in range(count)])  8.68 us
    ppermute x4, starting transfers between devices, pair_scan(): a_in, s_in = lax.ppermute(out, axis, pairs)  6.51 us
    ppermute x4, starting transfers between devices, pair_scan(): a_rcv, s_rcv = lax.ppermute((a_snd, s_snd), axis, swap)  6.37 us
    ppermute x2, waiting for transfers between devices, pair_scan(): other = lax.ppermute(send, axis, swap)  5.31 us
    ppermute x4, waiting for transfers between devices, pair_scan(): a_in, s_in = lax.ppermute(out, axis, pairs)  4.84 us
  transfers between devices with their start and end apart: 20, of which 12 were waited for; matrix products, arithmetic and copies ran while one was open for 11% of the time, Pallas kernels for 0%

profile of v2, /device:TPU:0, one launch (start us, length us, event | category | flops | bytes accessed | tf_op | source)
XLA Modules:
  0.0 124.2 jit_solution(17420674461100275618)
XLA Ops:
  1.9 1.3 %copy.22 = f32[128,1280]{0,1:T(8,128)S(1)} copy(f32[128,1280]{1,0:T(8,128)} %param.9) | data formatting | bytes 1310720 | tf_op args[0]
  4.0 3.0 %collective-permute-start.1 = (f32[10,64,128]{2,1,0:T(8,128)S(1)}, f32[10,64,128]{2,1,0:T(8,128)S(1)}, u32[]{:S(2)}, u32[]{:S(2)}) collective-permute-start(f32[10,64,128]{2,1,0:T(8,128)S(1)} %constant_dynamic-slice_fusion.1), channel_id=1, source_target_pairs={{0,4},{4,0},{8,12},{12,8},{16,20},{20,16},{24,28},{28,24},{1,5},{5... | collective-permute-start | bytes 983048 | tf_op jit(solution)/shard_map/ppermute | solution.py:42
  7.2 7.6 %collective-permute-done.10 = f32[10]{0:T(128)S(1)} collective-permute-done((f32[10]{0:T(128)S(1)}, f32[10]{0:T(128)S(1)}, u32[]{:S(2)}, u32[]{:S(2)}) %collective-permute-start.10) | collective-permute-done | bytes 72 | tf_op jit(solution)/shard_map/ppermute | solution.py:42
  15.4 1.7 %collective-permute-start = (f32[10]{0:T(128)S(1)}, f32[10]{0:T(128)S(1)}, u32[]{:S(2)}, u32[]{:S(2)}) collective-permute-start(f32[10]{0:T(128)S(1)} %get-tuple-element.56), channel_id=1, source_target_pairs={{0,4},{4,0},{8,12},{12,8},{16,20},{20,16},{24,28},{28,24},{1,5},{5... | collective-permute-start | bytes 128 | tf_op jit(solution)/shard_map/ppermute | solution.py:42
  17.1 1.8 %collective-permute-done = f32[10]{0:T(128)S(1)} collective-permute-done((f32[10]{0:T(128)S(1)}, f32[10]{0:T(128)S(1)}, u32[]{:S(2)}, u32[]{:S(2)}) %collective-permute-start) | collective-permute-done | bytes 72 | tf_op jit(solution)/shard_map/ppermute | solution.py:42
  19.1 3.7 %collective-permute-start.2 = (f32[10,64,128]{2,1,0:T(8,128)S(1)}, f32[10,64,128]{2,1,0:T(8,128)S(1)}, u32[]{:S(2)}, u32[]{:S(2)}) collective-permute-start(f32[10,64,128]{2,1,0:T(8,128)S(1)} %get-tuple-element.38), channel_id=1, source_target_pairs={{0,8},{4,12},{1,9},{5,13},{2,10},{6,14},{3,11},{7,15}} | collective-permute-start | bytes 983048 | tf_op jit(solution)/shard_map/ppermute | solution.py:62
  22.9 4.8 %collective-permute-done.2 = f32[10,64,128]{2,1,0:T(8,128)S(1)} collective-permute-done((f32[10,64,128]{2,1,0:T(8,128)S(1)}, f32[10,64,128]{2,1,0:T(8,128)S(1)}, u32[]{:S(2)}, u32[]{:S(2)}) %collective-permute-start.2) | collective-permute-done | bytes 327712 | tf_op jit(solution)/shard_map/ppermute | solution.py:62
  29.5 1.5 %collective-permute-start.5 = (f32[10,64,128]{2,1,0:T(8,128)S(1)}, f32[10,64,128]{2,1,0:T(8,128)S(1)}, u32[]{:S(2)}, u32[]{:S(2)}) collective-permute-start(f32[10,64,128]{2,1,0:T(8,128)S(1)} %get-tuple-element.50), channel_id=1, source_target_pairs={{0,4},{4,0},{8,12},{12,8},{16,20},{20,16},{24,28},{28,24},{1,5},{5... | collective-permute-start | bytes 983048 | tf_op jit(solution)/shard_map/ppermute | solution.py:82
  31.4 5.3 %collective-permute-done.5 = f32[10,64,128]{2,1,0:T(8,128)S(1)} collective-permute-done((f32[10,64,128]{2,1,0:T(8,128)S(1)}, f32[10,64,128]{2,1,0:T(8,128)S(1)}, u32[]{:S(2)}, u32[]{:S(2)}) %collective-permute-start.5) | collective-permute-done | bytes 327712 | tf_op jit(solution)/shard_map/ppermute | solution.py:82
  37.4 3.5 %multiply_add_fusion.1 = f32[128,20,64]{0,2,1:T(8,128)} fusion(f32[128,20,64]{0,2,1:T(8,128)S(1)} %convolution_bitcast_fusion.1, f32[128,20,64]{0,2,1:T(8,128)S(1)} %bitcast.64, f32[128,128]{1,0:T(8,128)S(1)} %fusion.71, f32[20,128]{1,0:T(8,128)S(1)} %reduce_window_sum.45, pred[128,128]{1,0:T(8,128)(4,1)S(1)} %iota_compare_fusion, ...), kind=kOutput, calls=%fused_computation.32 | convolution fusion | flops 253788160 | bytes 2078800 | tf_op jit(solution)/shard_map/jvp(hij,jhp->ihp)/dot_general | solution.py:158
  40.9 1.4 %copy.23 = f32[128,1280]{1,0:T(8,128)S(1)} copy(f32[128,1280]{0,1:T(8,128)} %bitcast.74) | data formatting | bytes 1310720 | tf_op jit(solution)/shard_map/add | solution.py:217
  42.4 1.5 %multiply_reduce_fusion.7 = (f32[128]{0:T(128)S(1)}, f32[128]{0:T(128)S(1)}) fusion(f32[128,1280]{1,0:T(8,128)S(1)} %copy.23, f32[128,1280]{1,0:T(8,128)S(1)} %copy-done.1, f32[128,1280]{1,0:T(8,128)} %param.17, f32[1280]{0:T(1024)S(1)} %copy-done.12), kind=kLoop, calls=%fused_computation.29 | loop fusion | flops 1638144 | bytes 1972224 | tf_op jit(solution)/shard_map/reduce_sum | solution.py:234
  45.0 1.5 %collective-permute-start.7 = (f32[128]{0:T(128)S(1)}, f32[128]{0:T(128)S(1)}, u32[]{:S(2)}, u32[]{:S(2)}) collective-permute-start(f32[128]{0:T(128)S(1)} %add.145), channel_id=1, source_target_pairs={{0,2},{1,3},{2,0},{3,1},{4,6},{5,7},{6,4},{7,5},{8,10},{9,11},{10,... | collective-permute-start | bytes 1544 | tf_op jit(solution)/shard_map/ppermute | solution.py:94
  47.1 1.5 %collective-permute-done.7 = f32[128]{0:T(128)S(1)} collective-permute-done((f32[128]{0:T(128)S(1)}, f32[128]{0:T(128)S(1)}, u32[]{:S(2)}, u32[]{:S(2)}) %collective-permute-start.7) | collective-permute-done | bytes 544 | tf_op jit(solution)/shard_map/ppermute | solution.py:94
  48.6 1.5 %collective-permute-done.9 = f32[128]{0:T(128)S(1)} collective-permute-done((f32[128]{0:T(128)S(1)}, f32[128]{0:T(128)S(1)}, u32[]{:S(2)}, u32[]{:S(2)}) %collective-permute-start.9) | collective-permute-done | bytes 544 | tf_op jit(solution)/shard_map/ppermute | solution.py:94
  50.1 1.5 %add_multiply_fusion = (f32[128,1280]{1,0:T(8,128)}, f32[128,1280]{1,0:T(8,128)}) fusion(f32[128,1280]{1,0:T(8,128)S(1)} %copy-done.1, f32[128,1280]{1,0:T(8,128)S(1)} %copy.23, f32[128]{0:T(128)S(1)} %get-tuple-element.34, f32[128,1280]{1,0:T(8,128)S(1)} %copy-done.2, f32[1280]{0:T(1024)S(1)} %copy-done.12, f32[128]{0:T(128)S(1)} %get-tuple-element.35), kind=kLoop, calls=%fused_computation.25 | loop fusion | flops 2621440 | bytes 3282944 | tf_op jit(solution)/shard_map/mul | solution.py:242
  51.6 1.3 %copy.24 = f32[128,1280]{0,1:T(8,128)S(1)} copy(f32[128,1280]{1,0:T(8,128)} %get-tuple-element.45) | data formatting | bytes 1310720 | tf_op jit(solution)/shard_map/mul | solution.py:241
  53.6 1.6 %collective-permute-start.11 = (f32[10,64,128]{2,1,0:T(8,128)S(1)}, f32[10,64,128]{2,1,0:T(8,128)S(1)}, u32[]{:S(2)}, u32[]{:S(2)}) collective-permute-start(f32[10,64,128]{2,1,0:T(8,128)S(1)} %constant_dynamic-slice_fusion), channel_id=1, source_target_pairs={{28,24},{24,28},{20,16},{16,20},{12,8},{8,12},{4,0},{0,4},{29,25},... | collective-permute-start | bytes 983048 | tf_op jit(solution)/shard_map/ppermute | solution.py:42
  55.2 6.9 %collective-permute-done.11 = f32[10,64,128]{2,1,0:T(8,128)S(1)} collective-permute-done((f32[10,64,128]{2,1,0:T(8,128)S(1)}, f32[10,64,128]{2,1,0:T(8,128)S(1)}, u32[]{:S(2)}, u32[]{:S(2)}) %collective-permute-start.11) | collective-permute-done | bytes 327712 | tf_op jit(solution)/shard_map/ppermute | solution.py:42
  62.9 1.4 %collective-permute-start.12 = (f32[10,64,128]{2,1,0:T(8,128)}, f32[10,64,128]{2,1,0:T(8,128)}, u32[]{:S(2)}, u32[]{:S(2)}) collective-permute-start(f32[10,64,128]{2,1,0:T(8,128)} %get-tuple-element.28), channel_id=1, source_target_pairs={{28,20},{24,16},{29,21},{25,17},{30,22},{26,18},{31,23},{27,19}} | collective-permute-start | bytes 983048 | tf_op jit(solution)/shard_map/ppermute | solution.py:62
  65.1 3.0 %fusion.18 = (f32[20,128]{1,0:T(8,128)S(1)}, f32[20,128]{1,0:T(8,128)S(1)}, f32[128,128]{1,0:T(8,128)S(1)}) fusion(f32[128,128]{1,0:T(8,128)S(1)} %fusion.71, f32[20,128]{1,0:T(8,128)S(1)} %reduce_window_sum.45, pred[128,128]{1,0:T(8,128)(4,1)S(1)} %iota_compare_fusion, f32[20,64,128]{2,1,0:T(8,128)S(1)} %bitcast.69, f32[128,20,64]{0,2,1:T(8,128)S(1)} %bitcast.65, ...), kind=kOutput, calls=%fused_computation.17 | convolution fusion | flops 255405056 | bytes 1499136 | tf_op jit(solution)/shard_map/transpose(jvp(hij,jhp->ihp))/dot_general | solution.py:158
  68.4 1.5 %collective-permute-start.14 = (f32[10,64,128]{2,1,0:T(8,128)S(1)}, f32[10,64,128]{2,1,0:T(8,128)S(1)}, u32[]{:S(2)}, u32[]{:S(2)}) collective-permute-start(f32[10,64,128]{2,1,0:T(8,128)S(1)} %get-tuple-element.26), channel_id=1, source_target_pairs={{12,4},{8,0},{13,5},{9,1},{14,6},{10,2},{15,7},{11,3}} | collective-permute-start | bytes 983048 | tf_op jit(solution)/shard_map/ppermute | solution.py:59
  71.3 2.4 %fusion.12 = f32[128,20,64]{0,2,1:T(8,128)} fusion(f32[20,64,128]{2,1,0:T(8,128)S(1)} %bitcast.71, f32[128,128]{1,0:T(8,128)S(1)} %fusion.71, f32[20,128]{1,0:T(8,128)S(1)} %reduce_window_sum.45, pred[128,128]{1,0:T(8,128)(4,1)S(1)} %iota_compare_fusion), kind=kOutput, calls=%fused_computation.11 | convolution fusion | flops 252968960 | bytes 1402880 | tf_op jit(solution)/shard_map/transpose(jvp(hij,jhp->ihp))/dot_general | solution.py:158
  73.7 28.2 %collective-permute-done.14 = f32[10,64,128]{2,1,0:T(8,128)S(1)} collective-permute-done((f32[10,64,128]{2,1,0:T(8,128)S(1)}, f32[10,64,128]{2,1,0:T(8,128)S(1)}, u32[]{:S(2)}, u32[]{:S(2)}) %collective-permute-start.14) | collective-permute-done | bytes 327712 | tf_op jit(solution)/shard_map/ppermute | solution.py:59
  102.7 1.5 %collective-permute-start.15 = (f32[10,64,128]{2,1,0:T(8,128)}, f32[10,64,128]{2,1,0:T(8,128)S(1)}, u32[]{:S(2)}, u32[]{:S(2)}) collective-permute-start(f32[10,64,128]{2,1,0:T(8,128)} %get-tuple-element.48), channel_id=1, source_target_pairs={{28,24},{24,28},{20,16},{16,20},{12,8},{8,12},{4,0},{0,4},{29,25},... | collective-permute-start | bytes 983048 | tf_op jit(solution)/shard_map/ppermute | solution.py:82
  105.3 1.2 reduce_window_sum.46
  106.5 2.5 %collective-permute-done.19 = f32[128,128]{1,0:T(8,128)} collective-permute-done((f32[128,128]{1,0:T(8,128)S(1)}, f32[128,128]{1,0:T(8,128)}, u32[]{:S(2)}, u32[]{:S(2)}) %collective-permute-start.19) | collective-permute-done | bytes 65568 | tf_op jit(solution)/shard_map/ppermute | solution.py:94
  109.0 1.5 %add.168 = f32[128,128]{1,0:T(8,128)} add(f32[128,128]{1,0:T(8,128)S(1)} %add.167, f32[128,128]{1,0:T(8,128)} %collective-permute-done.19) | non-fusion elementwise | flops 16384 | bytes 196608 | tf_op jit(solution)/shard_map/add | solution.py:95
  111.5 2.3 %multiply_reduce_fusion.2 = (f32[128,20]{0,1:T(8,128)S(1)}, f32[128,20]{0,1:T(8,128)S(1)}, f32[128,20]{0,1:T(8,128)S(1)}, f32[128,20,64]{0,2,1:T(8,128)S(1)}, f32[128,20]{0,1:T(8,128)S(1)}) fusion(f32[128,20,64]{0,2,1:T(8,128)S(1)} %bitcast.66, f32[128,20]{0,1:T(8,128)S(1)} %bitcast.78, f32[128,20]{0,1:T(8,128)S(1)} %get-tuple-element.55, ...), kind=kOutput, calls=%fused_computation.21 | convolution fusion | flops 254597120 | bytes 4059217 | tf_op jit(solution)/shard_map/transpose(jvp(jhp,jn->hpn))/dot_general | solution.py:177
  114.2 1.2 reduce_window_sum.47
  115.4 1.2 reduce_window_sum.48
  121.6 1.9 %collective-permute-done.17 = f32[128,128]{1,0:T(8,128)S(1)} collective-permute-done((f32[128,128]{1,0:T(8,128)S(1)}, f32[128,128]{1,0:T(8,128)S(1)}, u32[]{:S(2)}, u32[]{:S(2)}) %collective-permute-start.17) | collective-permute-done | bytes 65568 | tf_op jit(solution)/shard_map/ppermute | solution.py:94
  (100 shorter events, 20.2 us)
Async XLA Ops:
  0.6 2.7 %copy-start = (f32[128,128]{1,0:T(8,128)S(1)}, f32[128,128]{1,0:T(8,128)}, u32[]{:S(2)}) copy-start(f32[128,128]{1,0:T(8,128)} %param.11) | copy-start | bytes 196612
  4.0 15.0 %collective-permute-start.1 = (f32[10,64,128]{2,1,0:T(8,128)S(1)}, f32[10,64,128]{2,1,0:T(8,128)S(1)}, u32[]{:S(2)}, u32[]{:S(2)}) collective-permute-start(f32[10,64,128]{2,1,0:T(8,128)S(1)} %constant_dynamic-slice_fusion.1), channel_id=1, source_target_pairs={{0,4},{4,0},{8,12},{12,8},{16,20},{20,16},{24,28},{28,24},{1,5},{5... | collective-permute-start | bytes 983048 | tf_op jit(solution)/shard_map/ppermute | solution.py:42
  7.1 7.7 %collective-permute-start.10 = (f32[10]{0:T(128)S(1)}, f32[10]{0:T(128)S(1)}, u32[]{:S(2)}, u32[]{:S(2)}) collective-permute-start(f32[10]{0:T(128)S(1)} %dynamic_slice.29), channel_id=1, source_target_pairs={{28,24},{24,28},{20,16},{16,20},{12,8},{8,12},{4,0},{0,4},{29,25},... | collective-permute-start | bytes 128 | tf_op jit(solution)/shard_map/ppermute | solution.py:42
  14.8 2.3 %copy-start.13 = (f32[10]{0:T(128)}, f32[10]{0:T(128)S(1)}, u32[]{:S(2)}) copy-start(f32[10]{0:T(128)S(1)} %collective-permute-done.10) | copy-start | bytes 124
  15.4 3.5 %collective-permute-start = (f32[10]{0:T(128)S(1)}, f32[10]{0:T(128)S(1)}, u32[]{:S(2)}, u32[]{:S(2)}) collective-permute-start(f32[10]{0:T(128)S(1)} %get-tuple-element.56), channel_id=1, source_target_pairs={{0,4},{4,0},{8,12},{12,8},{16,20},{20,16},{24,28},{28,24},{1,5},{5... | collective-permute-start | bytes 128 | tf_op jit(solution)/shard_map/ppermute | solution.py:42
  19.1 8.6 %collective-permute-start.2 = (f32[10,64,128]{2,1,0:T(8,128)S(1)}, f32[10,64,128]{2,1,0:T(8,128)S(1)}, u32[]{:S(2)}, u32[]{:S(2)}) collective-permute-start(f32[10,64,128]{2,1,0:T(8,128)S(1)} %get-tuple-element.38), channel_id=1, source_target_pairs={{0,8},{4,12},{1,9},{5,13},{2,10},{6,14},{3,11},{7,15}} | collective-permute-start | bytes 983048 | tf_op jit(solution)/shard_map/ppermute | solution.py:62
  27.9 0.7 collective-permute-start.3
  28.7 0.7 collective-permute-start.4
  29.4 1.7 %copy-start.10 = (f32[128,128]{1,0:T(8,128)S(1)}, f32[128,128]{1,0:T(8,128)}, u32[]{:S(2)}) copy-start(f32[128,128]{1,0:T(8,128)} %param.12) | copy-start | bytes 196612
  29.5 7.1 %collective-permute-start.5 = (f32[10,64,128]{2,1,0:T(8,128)S(1)}, f32[10,64,128]{2,1,0:T(8,128)S(1)}, u32[]{:S(2)}, u32[]{:S(2)}) collective-permute-start(f32[10,64,128]{2,1,0:T(8,128)S(1)} %get-tuple-element.50), channel_id=1, source_target_pairs={{0,4},{4,0},{8,12},{12,8},{16,20},{20,16},{24,28},{28,24},{1,5},{5... | collective-permute-start | bytes 983048 | tf_op jit(solution)/shard_map/ppermute | solution.py:82
  40.9 1.4 %copy-start.1 = (f32[128,1280]{1,0:T(8,128)S(1)}, f32[128,1280]{1,0:T(8,128)}, u32[]{:S(2)}) copy-start(f32[128,1280]{1,0:T(8,128)} %param.10) | copy-start | bytes 1966084
  40.9 1.4 %copy-start.12 = (f32[1280]{0:T(1024)S(1)}, f32[1280]{0:T(1024)}, u32[]{:S(2)}) copy-start(f32[1280]{0:T(1024)} %param.16) | copy-start | bytes 15364
  42.4 7.8 %copy-start.2 = (f32[128,1280]{1,0:T(8,128)S(1)}, f32[128,1280]{1,0:T(8,128)}, u32[]{:S(2)}) copy-start(f32[128,1280]{1,0:T(8,128)} %param.17) | copy-start | bytes 1966084
  43.9 1.2 collective-permute-start.6
  43.9 2.6 %collective-permute-start.8 = (f32[128]{0:T(128)S(1)}, f32[128]{0:T(128)S(1)}, u32[]{:S(2)}, u32[]{:S(2)}) collective-permute-start(f32[128]{0:T(128)S(1)} %get-tuple-element.24), channel_id=1, source_target_pairs={{0,1},{1,0},{2,3},{3,2},{4,5},{5,4},{6,7},{7,6},{8,9},{9,8},{10,11... | collective-permute-start | bytes 1544 | tf_op jit(solution)/shard_map/ppermute | solution.py:94
  45.0 3.5 %collective-permute-start.7 = (f32[128]{0:T(128)S(1)}, f32[128]{0:T(128)S(1)}, u32[]{:S(2)}, u32[]{:S(2)}) collective-permute-start(f32[128]{0:T(128)S(1)} %add.145), channel_id=1, source_target_pairs={{0,2},{1,3},{2,0},{3,1},{4,6},{5,7},{6,4},{7,5},{8,10},{9,11},{10,... | collective-permute-start | bytes 1544 | tf_op jit(solution)/shard_map/ppermute | solution.py:94
  46.5 3.5 %collective-permute-start.9 = (f32[128]{0:T(128)S(1)}, f32[128]{0:T(128)S(1)}, u32[]{:S(2)}, u32[]{:S(2)}) collective-permute-start(f32[128]{0:T(128)S(1)} %add.149), channel_id=1, source_target_pairs={{0,2},{1,3},{2,0},{3,1},{4,6},{5,7},{6,4},{7,5},{8,10},{9,11},{10,... | collective-permute-start | bytes 1544 | tf_op jit(solution)/shard_map/ppermute | solution.py:94
  53.6 8.5 %collective-permute-start.11 = (f32[10,64,128]{2,1,0:T(8,128)S(1)}, f32[10,64,128]{2,1,0:T(8,128)S(1)}, u32[]{:S(2)}, u32[]{:S(2)}) collective-permute-start(f32[10,64,128]{2,1,0:T(8,128)S(1)} %constant_dynamic-slice_fusion), channel_id=1, source_target_pairs={{28,24},{24,28},{20,16},{16,20},{12,8},{8,12},{4,0},{0,4},{29,25},... | collective-permute-start | bytes 983048 | tf_op jit(solution)/shard_map/ppermute | solution.py:42
  62.9 1.4 %collective-permute-start.12 = (f32[10,64,128]{2,1,0:T(8,128)}, f32[10,64,128]{2,1,0:T(8,128)}, u32[]{:S(2)}, u32[]{:S(2)}) collective-permute-start(f32[10,64,128]{2,1,0:T(8,128)} %get-tuple-element.28), channel_id=1, source_target_pairs={{28,20},{24,16},{29,21},{25,17},{30,22},{26,18},{31,23},{27,19}} | collective-permute-start | bytes 983048 | tf_op jit(solution)/shard_map/ppermute | solution.py:62
  64.4 3.9 %collective-permute-start.13 = (f32[10,64,128]{2,1,0:T(8,128)S(1)}, f32[10,64,128]{2,1,0:T(8,128)S(1)}, u32[]{:S(2)}, u32[]{:S(2)}) collective-permute-start(f32[10,64,128]{2,1,0:T(8,128)S(1)} %multiply_add_fusion.3), channel_id=1, source_target_pairs={{20,12},{16,8},{21,13},{17,9},{22,14},{18,10},{23,15},{19,11}} | collective-permute-start | bytes 983048 | tf_op jit(solution)/shard_map/ppermute | solution.py:62
  68.3 1.6 %copy-start.8 = (f32[10,64,128]{2,1,0:T(8,128)S(1)}, f32[10,64,128]{2,1,0:T(8,128)}, u32[]{:S(2)}) copy-start(f32[10,64,128]{2,1,0:T(8,128)} %copy-done.7) | copy-start | bytes 983044
  68.4 33.4 %collective-permute-start.14 = (f32[10,64,128]{2,1,0:T(8,128)S(1)}, f32[10,64,128]{2,1,0:T(8,128)S(1)}, u32[]{:S(2)}, u32[]{:S(2)}) collective-permute-start(f32[10,64,128]{2,1,0:T(8,128)S(1)} %get-tuple-element.26), channel_id=1, source_target_pairs={{12,4},{8,0},{13,5},{9,1},{14,6},{10,2},{15,7},{11,3}} | collective-permute-start | bytes 983048 | tf_op jit(solution)/shard_map/ppermute | solution.py:59
  71.2 30.7 %copy-start.6 = (f32[10,64,128]{2,1,0:T(8,128)S(1)}, f32[10,64,128]{2,1,0:T(8,128)}, u32[]{:S(2)}) copy-start(f32[10,64,128]{2,1,0:T(8,128)} %copy-done.5) | copy-start | bytes 983044
  71.2 30.7 %copy-start.14 = (f32[10]{0:T(128)S(1)}, f32[10]{0:T(128)}, u32[]{:S(2)}) copy-start(f32[10]{0:T(128)} %copy-done.13) | copy-start | bytes 124
  71.2 30.7 %copy-start.15 = (f32[10]{0:T(128)S(1)}, f32[10]{0:T(128)}, u32[]{:S(2)}) copy-start(f32[10]{0:T(128)} %get-tuple-element.33) | copy-start | bytes 124
  71.2 33.3 %collective-permute-start.18 = (f32[128,128]{1,0:T(8,128)S(1)}, f32[128,128]{1,0:T(8,128)S(1)}, u32[]{:S(2)}, u32[]{:S(2)}) collective-permute-start(f32[128,128]{1,0:T(8,128)S(1)} %fusion.16), channel_id=1, source_target_pairs={{0,1},{1,0},{2,3},{3,2},{4,5},{5,4},{6,7},{7,6},{8,9},{9,8},{10,11... | collective-permute-start | bytes 196616 | tf_op jit(solution)/shard_map/ppermute | solution.py:94
  102.7 7.7 %copy-start.9 = (f32[10,64,128]{2,1,0:T(8,128)S(1)}, f32[10,64,128]{2,1,0:T(8,128)}, u32[]{:S(2)}) copy-start(f32[10,64,128]{2,1,0:T(8,128)} %copy-done.7) | copy-start | bytes 983044
  102.7 7.7 %collective-permute-start.15 = (f32[10,64,128]{2,1,0:T(8,128)}, f32[10,64,128]{2,1,0:T(8,128)S(1)}, u32[]{:S(2)}, u32[]{:S(2)}) collective-permute-start(f32[10,64,128]{2,1,0:T(8,128)} %get-tuple-element.48), channel_id=1, source_target_pairs={{28,24},{24,28},{20,16},{16,20},{12,8},{8,12},{4,0},{0,4},{29,25},... | collective-permute-start | bytes 983048 | tf_op jit(solution)/shard_map/ppermute | solution.py:82
  104.6 4.4 %collective-permute-start.19 = (f32[128,128]{1,0:T(8,128)S(1)}, f32[128,128]{1,0:T(8,128)}, u32[]{:S(2)}, u32[]{:S(2)}) collective-permute-start(f32[128,128]{1,0:T(8,128)S(1)} %add.167), channel_id=1, source_target_pairs={{0,2},{1,3},{2,0},{3,1},{4,6},{5,7},{6,4},{7,5},{8,10},{9,11},{10,... | collective-permute-start | bytes 196616 | tf_op jit(solution)/shard_map/ppermute | solution.py:94
  111.5 5.2 %copy-start.4 = (f32[10,64,128]{2,1,0:T(8,128)S(1)}, f32[10,64,128]{2,1,0:T(8,128)}, u32[]{:S(2)}) copy-start(f32[10,64,128]{2,1,0:T(8,128)} %copy-done.3) | copy-start | bytes 983044
  117.9 1.3 %collective-permute-start.16 = (f32[128,128]{1,0:T(8,128)S(1)}, f32[128,128]{1,0:T(8,128)S(1)}, u32[]{:S(2)}, u32[]{:S(2)}) collective-permute-start(f32[128,128]{1,0:T(8,128)S(1)} %fusion.15), channel_id=1, source_target_pairs={{0,1},{1,0},{2,3},{3,2},{4,5},{5,4},{6,7},{7,6},{8,9},{9,8},{10,11... | collective-permute-start | bytes 196616 | tf_op jit(solution)/shard_map/ppermute | solution.py:94
  119.2 4.3 %collective-permute-start.17 = (f32[128,128]{1,0:T(8,128)S(1)}, f32[128,128]{1,0:T(8,128)S(1)}, u32[]{:S(2)}, u32[]{:S(2)}) collective-permute-start(f32[128,128]{1,0:T(8,128)S(1)} %add.164), channel_id=1, source_target_pairs={{0,2},{1,3},{2,0},{3,1},{4,6},{5,7},{6,4},{7,5},{8,10},{9,11},{10,... | collective-permute-start | bytes 196616 | tf_op jit(solution)/shard_map/ppermute | solution.py:94
  (6 other events, 5.4 us)

commit v3 on v2

--- a/solution.py
+++ b/solution.py
@@ -39,47 +39,110 @@
     a_own, s_own = part(decay, own_start), part(state, own_start)
     a_snd, s_snd = part(decay, send_start), part(state, send_start)
     swap = [(phys(u), phys(u ^ 1)) for u in range(count)]
+
+    def shift_pairs(k):
+        return [
+            (phys(2 * g + x), phys(2 * (g + k) + x)) for g in range(groups - k) for x in (0, 1)
+        ]
+
+    if groups <= 4:
+        return wavefront(
+            a_own, s_own, a_snd, s_snd, first, group, groups, axis, swap, shift_pairs(1)
+        )
+
     a_rcv, s_rcv = lax.ppermute((a_snd, s_snd), axis, swap)
     lead = (jnp.where(first, a_own, a_rcv), jnp.where(first, s_own, s_rcv))
     trail = (jnp.where(first, a_rcv, a_own), jnp.where(first, s_rcv, s_own))
     a_tot, s_tot = combine(lead, trail)
-
-    def shift_pairs(k):
-        return [
-            (phys(2 * g + x), phys(2 * (g + k) + x)) for g in range(groups - k) for x in (0, 1)
-        ]
-
-    if groups <= 4:
-        a_g = jnp.ones_like(a_tot)
-        s_g = jnp.zeros_like(s_tot)
-        for r in range(groups - 1):
-            out = combine((a_g, s_g), (a_tot, s_tot))
-            pairs = [(phys(2 * r + x), phys(2 * (r + 1) + x)) for x in (0, 1)]
-            if r == groups - 2:
-                s_in = lax.ppermute(out[1], axis, pairs)
-                a_in = a_g
-            else:
-                a_in, s_in = lax.ppermute(out, axis, pairs)
-            dst = group == r + 1
-            a_g = jnp.where(dst, a_in, a_g)
-            s_g = jnp.where(dst, s_in, s_g)
-    else:
-        a_g, s_g = lax.ppermute((a_tot, s_tot), axis, shift_pairs(1))
-        a_g = jnp.where(group == 0, 1.0, a_g)
-        s_g = jnp.where(group == 0, 0.0, s_g)
-        k = 1
-        while k < groups:
-            got = lax.ppermute((a_g, s_g), axis, shift_pairs(k))
-            a_c, s_c = combine(got, (a_g, s_g))
-            a_g = jnp.where(group >= k, a_c, a_g)
-            s_g = jnp.where(group >= k, s_c, s_g)
-            k *= 2
+    a_g, s_g = lax.ppermute((a_tot, s_tot), axis, shift_pairs(1))
+    a_g = jnp.where(group == 0, 1.0, a_g)
+    s_g = jnp.where(group == 0, 0.0, s_g)
+    k = 1
+    while k < groups:
+        got = lax.ppermute((a_g, s_g), axis, shift_pairs(k))
+        a_c, s_c = combine(got, (a_g, s_g))
+        a_g = jnp.where(group >= k, a_c, a_g)
+        s_g = jnp.where(group >= k, s_c, s_g)
+        k *= 2
 
     with_lead_own = a_own[:, None, None] * s_g + s_own
     with_lead_rcv = a_rcv[:, None, None] * s_g + s_rcv
     send = jnp.where(first, with_lead_own, s_g)
     keep = jnp.where(first, s_g, with_lead_rcv)
     other = lax.ppermute(send, axis, swap)
+    return jnp.where(
+        first, jnp.concatenate([other, keep], 0), jnp.concatenate([keep, other], 0)
+    )
+
+
+def wavefront(a_own, s_own, a_snd, s_snd, first, group, groups, axis, swap, chain):
+    half = a_own.shape[0]
+    chunks = 2 if half % 2 == 0 else 1
+    width = half // chunks
+
+    def split(x):
+        return x.reshape((chunks, width) + x.shape[1:])
+
+    a_own, s_own, a_snd, s_snd = split(a_own), split(s_own), split(a_snd), split(s_snd)
+    a_rcv = jnp.zeros_like(a_own)
+    s_rcv = jnp.zeros_like(s_own)
+    a_tot = jnp.ones_like(a_own)
+    s_tot = jnp.zeros_like(s_own)
+    a_g = jnp.ones_like(a_own)
+    s_g = jnp.zeros_like(s_own)
+    other = jnp.zeros_like(s_own)
+    keep = jnp.zeros_like(s_own)
+
+    def pick(x, i):
+        return lax.dynamic_index_in_dim(x, jnp.clip(i, 0, chunks - 1), 0, False)
+
+    def put(x, v, i, ok):
+        i = jnp.clip(i, 0, chunks - 1)
+        old = lax.dynamic_index_in_dim(x, i, 0, False)
+        return lax.dynamic_update_index_in_dim(x, jnp.where(ok, v, old), i, 0)
+
+    for t in range(chunks + groups):
+        late = t - 1 - group
+        late_ok = (late >= 0) & (late < chunks)
+        do_first = t < chunks
+        do_last = t >= 1
+        do_chain = 1 <= t <= chunks + groups - 2
+        if do_last or do_chain:
+            ag, sg = pick(a_g, late), pick(s_g, late)
+            at, st = pick(a_tot, late), pick(s_tot, late)
+        if do_last:
+            ao, so = pick(a_own, late), pick(s_own, late)
+            ar, sr = pick(a_rcv, late), pick(s_rcv, late)
+            last_send = jnp.where(first, ao[:, None, None] * sg + so, sg)
+            last_keep = jnp.where(first, sg, ar[:, None, None] * sg + sr)
+            keep = put(keep, last_keep, late, late_ok)
+        payload = {}
+        if do_first:
+            payload["a"] = a_snd[t]
+            payload["s"] = s_snd[t]
+        if do_last:
+            payload["e"] = last_send
+        got = lax.ppermute(payload, axis, swap)
+        if do_chain:
+            out = combine((ag, sg), (at, st))
+            a_in, s_in = lax.ppermute(out, axis, chain)
+            early = t - group
+            early_ok = (group >= 1) & (early >= 0) & (early < chunks)
+            a_g = put(a_g, a_in, early, early_ok)
+            s_g = put(s_g, s_in, early, early_ok)
+        if do_first:
+            a_rcv = a_rcv.at[t].set(got["a"])
+            s_rcv = s_rcv.at[t].set(got["s"])
+            lead = (jnp.where(first, a_own[t], got["a"]), jnp.where(first, s_own[t], got["s"]))
+            trail = (jnp.where(first, got["a"], a_own[t]), jnp.where(first, got["s"], s_own[t]))
+            a_c, s_c = combine(lead, trail)
+            a_tot = a_tot.at[t].set(a_c)
+            s_tot = s_tot.at[t].set(s_c)
+        if do_last:
+            other = put(other, got["e"], late, late_ok)
+
+    other = other.reshape((-1,) + other.shape[2:])
+    keep = keep.reshape((-1,) + keep.shape[2:])
     return jnp.where(
         first, jnp.concatenate([other, keep], 0), jnp.concatenate([keep, other], 0)
     )

time: 125 us -> 158 us (1.26)
  starting transfers between devices: 22.2 us -> 50.7 us
  waiting for transfers between devices: 63.3 us -> 57.6 us
  other arithmetic: 14.9 us -> 19.1 us
  local copies, waits for them, and re-layouts: 6.19 us -> 9.74 us
  matrix products: 16.4 us -> 18.3 us
    ppermute x12 -> x26, starting transfers between devices: 18.1 us -> 47 us  [the longest x18 24.4 us: wavefront(): got = lax.ppermute(payload, axis, swap)]
    ppermute x8, waiting for transfers between devices: 8.68 us -> 5.01 us  [butterfly_psum(): got = lax.ppermute(parts, axis, [(i, i ^ k) for i in range(count)])]
    dynamic_update_slice x0 -> x22, other arithmetic: none -> 2.16 us  [put(): return lax.dynamic_update_index_in_dim(x, jnp.where(ok, v, old), i, 0)]
    ppermute x12 -> x26, waiting for transfers between devices: 54.7 us -> 52.6 us  [the longest x8 30 us: wavefront(): a_in, s_in = lax.ppermute(out, axis, chain)]
    unnamed x38 -> x96, local copies, waits for them, and re-layouts: 2.98 us -> 3.72 us
  transfers between devices with their start and end apart: 20 -> 34, of which waited for: 12 -> 24; matrix products, arithmetic and copies ran while one was open for 11% -> 14% of each run, Pallas kernels for 0% -> 0%
where the time goes in v3:
time: 158 us; the launch traced here: 157 us
  waiting for transfers between devices  57.6 us (36%)
  starting transfers between devices  50.7 us (32%)
  other arithmetic  19.1 us (12%)
  matrix products  18.3 us (12%)
  local copies, waits for them, and re-layouts  9.74 us (6%)
  between operations  1.96 us (1%)
    ppermute x8, waiting for transfers between devices, wavefront(): a_in, s_in = lax.ppermute(out, axis, chain)  30 us
    ppermute x18, starting transfers between devices, wavefront(): got = lax.ppermute(payload, axis, swap)  24.4 us
    ppermute x18, waiting for transfers between devices, wavefront(): got = lax.ppermute(payload, axis, swap)  22.6 us
    ppermute x8, starting transfers between devices, wavefront(): a_in, s_in = lax.ppermute(out, axis, chain)  22.6 us
    dot_general x3, matrix products, within_part(): within = jnp.einsum('hij,jhp->ihp', masked, scaled, precision=highest)  8.91 us
    ppermute x8, waiting for transfers between devices, butterfly_psum(): got = lax.ppermute(parts, axis, [(i, i ^ k) for i in range(count)])  5.01 us
    dot_general x2, matrix products, state_update(): return jnp.einsum('jhp,jn->hpn', weighted_in, writes, precision=highest)  4.53 us
    ppermute x8, starting transfers between devices, butterfly_psum(): got = lax.ppermute(parts, axis, [(i, i ^ k) for i in range(count)])  3.74 us
  transfers between devices with their start and end apart: 34, of which 24 were waited for; matrix products, arithmetic and copies ran while one was open for 14% of the time, Pallas kernels for 0%

profile of v3, /device:TPU:0, one launch (start us, length us, event | category | flops | bytes accessed | tf_op | source)
XLA Modules:
  0.0 157.4 jit_solution(6124959048526907157)
XLA Ops:
  2.1 2.9 %collective-permute-start.1 = (f32[5]{0:T(128)S(1)}, f32[5]{0:T(128)S(1)}, u32[]{:S(2)}, u32[]{:S(2)}) collective-permute-start(f32[5]{0:T(128)S(1)} %get-tuple-element.297), channel_id=1, source_target_pairs={{0,4},{4,0},{8,12},{12,8},{16,20},{20,16},{24,28},{28,24},{1,5},{5... | collective-permute-start | bytes 68 | tf_op jit(solution)/shard_map/ppermute | solution.py:125
  7.2 2.0 %collective-permute-start.6 = (f32[5,64,128]{2,1,0:T(8,128)S(1)}, f32[5,64,128]{2,1,0:T(8,128)S(1)}, u32[]{:S(2)}, u32[]{:S(2)}) collective-permute-start(f32[5,64,128]{2,1,0:T(8,128)S(1)} %constant_dynamic-slice_fusion.43), channel_id=1, source_target_pairs={{0,4},{4,0},{8,12},{12,8},{16,20},{20,16},{24,28},{28,24},{1,5},{5... | collective-permute-start | bytes 491528 | tf_op jit(solution)/shard_map/ppermute | solution.py:125
  9.4 1.9 %collective-permute-start.22 = (f32[5]{0:T(128)S(1)}, f32[5]{0:T(128)S(1)}, u32[]{:S(2)}, u32[]{:S(2)}) collective-permute-start(f32[5]{0:T(128)S(1)} %get-tuple-element.288), channel_id=1, source_target_pairs={{28,24},{24,28},{20,16},{16,20},{12,8},{8,12},{4,0},{0,4},{29,25},... | collective-permute-start | bytes 68 | tf_op jit(solution)/shard_map/ppermute | solution.py:125
  13.8 1.9 %collective-permute-start.2 = (f32[5,64,128]{2,1,0:T(8,128)S(1)}, f32[5,64,128]{2,1,0:T(8,128)S(1)}, u32[]{:S(2)}, u32[]{:S(2)}) collective-permute-start(f32[5,64,128]{2,1,0:T(8,128)S(1)} %get-tuple-element.227), channel_id=1, source_target_pairs={{0,4},{4,0},{8,12},{12,8},{16,20},{20,16},{24,28},{28,24},{1,5},{5... | collective-permute-start | bytes 491528 | tf_op jit(solution)/shard_map/ppermute | solution.py:125
  15.7 3.4 %collective-permute-done.2 = f32[5,64,128]{2,1,0:T(8,128)S(1)} collective-permute-done((f32[5,64,128]{2,1,0:T(8,128)S(1)}, f32[5,64,128]{2,1,0:T(8,128)S(1)}, u32[]{:S(2)}, u32[]{:S(2)}) %collective-permute-start.2) | collective-permute-done | bytes 163872 | tf_op jit(solution)/shard_map/ppermute | solution.py:125
  19.3 3.8 %collective-permute-start.3 = (f32[5,64,128]{2,1,0:T(8,128)S(1)}, f32[5,64,128]{2,1,0:T(8,128)S(1)}, u32[]{:S(2)}, u32[]{:S(2)}) collective-permute-start(f32[5,64,128]{2,1,0:T(8,128)S(1)} %fusion.52), channel_id=1, source_target_pairs={{0,8},{4,12},{8,16},{12,20},{16,24},{20,28},{1,9},{5,13},{9,17},{1... | collective-permute-start | bytes 491528 | tf_op jit(solution)/shard_map/ppermute | solution.py:128
  23.8 2.2 %collective-permute-done.3 = f32[5,64,128]{2,1,0:T(8,128)S(1)} collective-permute-done((f32[5,64,128]{2,1,0:T(8,128)S(1)}, f32[5,64,128]{2,1,0:T(8,128)S(1)}, u32[]{:S(2)}, u32[]{:S(2)}) %collective-permute-start.3) | collective-permute-done | bytes 163872 | tf_op jit(solution)/shard_map/ppermute | solution.py:128
  26.1 4.4 %collective-permute-start.7 = (f32[5,64,128]{2,1,0:T(8,128)S(1)}, f32[5,64,128]{2,1,0:T(8,128)S(1)}, u32[]{:S(2)}, u32[]{:S(2)}) collective-permute-start(f32[5,64,128]{2,1,0:T(8,128)S(1)} %fusion.77), channel_id=1, source_target_pairs={{0,8},{4,12},{8,16},{12,20},{16,24},{20,28},{1,9},{5,13},{9,17},{1... | collective-permute-start | bytes 491528 | tf_op jit(solution)/shard_map/ppermute | solution.py:128
  30.7 3.5 %collective-permute-done.7 = f32[5,64,128]{2,1,0:T(8,128)S(1)} collective-permute-done((f32[5,64,128]{2,1,0:T(8,128)S(1)}, f32[5,64,128]{2,1,0:T(8,128)S(1)}, u32[]{:S(2)}, u32[]{:S(2)}) %collective-permute-start.7) | collective-permute-done | bytes 163872 | tf_op jit(solution)/shard_map/ppermute | solution.py:128
  34.4 4.4 %collective-permute-start.9 = (f32[5,64,128]{2,1,0:T(8,128)S(1)}, f32[5,64,128]{2,1,0:T(8,128)S(1)}, u32[]{:S(2)}, u32[]{:S(2)}) collective-permute-start(f32[5,64,128]{2,1,0:T(8,128)S(1)} %fusion.80), channel_id=1, source_target_pairs={{0,8},{4,12},{8,16},{12,20},{16,24},{20,28},{1,9},{5,13},{9,17},{1... | collective-permute-start | bytes 491528 | tf_op jit(solution)/shard_map/ppermute | solution.py:128
  38.9 4.2 %collective-permute-done.9 = f32[5,64,128]{2,1,0:T(8,128)S(1)} collective-permute-done((f32[5,64,128]{2,1,0:T(8,128)S(1)}, f32[5,64,128]{2,1,0:T(8,128)S(1)}, u32[]{:S(2)}, u32[]{:S(2)}) %collective-permute-start.9) | collective-permute-done | bytes 163872 | tf_op jit(solution)/shard_map/ppermute | solution.py:128
  43.3 4.6 %collective-permute-start.11 = (f32[5,64,128]{2,1,0:T(8,128)S(1)}, f32[5,64,128]{2,1,0:T(8,128)S(1)}, u32[]{:S(2)}, u32[]{:S(2)}) collective-permute-start(f32[5,64,128]{2,1,0:T(8,128)S(1)} %fusion.74), channel_id=1, source_target_pairs={{0,8},{4,12},{8,16},{12,20},{16,24},{20,28},{1,9},{5,13},{9,17},{1... | collective-permute-start | bytes 491528 | tf_op jit(solution)/shard_map/ppermute | solution.py:128
  48.5 2.0 %collective-permute-done.11 = f32[5,64,128]{2,1,0:T(8,128)S(1)} collective-permute-done((f32[5,64,128]{2,1,0:T(8,128)S(1)}, f32[5,64,128]{2,1,0:T(8,128)S(1)}, u32[]{:S(2)}, u32[]{:S(2)}) %collective-permute-start.11) | collective-permute-done | bytes 163872 | tf_op jit(solution)/shard_map/ppermute | solution.py:128
  58.2 1.7 %collective-permute-done.8 = f32[5,64,128]{2,1,0:T(8,128)S(1)} collective-permute-done((f32[5,64,128]{2,1,0:T(8,128)S(1)}, f32[5,64,128]{2,1,0:T(8,128)S(1)}, u32[]{:S(2)}, u32[]{:S(2)}) %collective-permute-start.8) | collective-permute-done | bytes 163872 | tf_op jit(solution)/shard_map/ppermute | solution.py:125
  61.7 1.7 %collective-permute-done.12 = f32[5,64,128]{2,1,0:T(8,128)S(1)} collective-permute-done((f32[5,64,128]{2,1,0:T(8,128)S(1)}, f32[5,64,128]{2,1,0:T(8,128)S(1)}, u32[]{:S(2)}, u32[]{:S(2)}) %collective-permute-start.12) | collective-permute-done | bytes 163872 | tf_op jit(solution)/shard_map/ppermute | solution.py:125
  64.2 3.6 %fusion.12 = f32[128,20,64]{0,2,1:T(8,128)} fusion(f32[128,20,64]{0,2,1:T(8,128)S(1)} %convolution_bitcast_fusion.1, f32[128,20,64]{0,2,1:T(8,128)S(1)} %bitcast.380, f32[128,128]{1,0:T(8,128)S(1)} %fusion.191, f32[20,128]{1,0:T(8,128)S(1)} %reduce_window_sum.45, pred[128,128]{1,0:T(8,128)(4,1)S(1)} %iota_compare_fusion, ...), kind=kOutput, calls=%fused_computation.11 | convolution fusion | flops 253788160 | bytes 2078800 | tf_op jit(solution)/shard_map/jvp(hij,jhp->ihp)/dot_general | solution.py:221
  78.7 2.9 %fusion.19 = (f32[20,128]{1,0:T(8,128)S(1)}, f32[20,128]{1,0:T(8,128)S(1)}, f32[128,128]{1,0:T(8,128)S(1)}) fusion(f32[128,128]{1,0:T(8,128)S(1)} %copy-done.14, f32[20,128]{1,0:T(8,128)S(1)} %reduce_window_sum.45, pred[128,128]{1,0:T(8,128)(4,1)S(1)} %copy-done.19, f32[20,64,128]{2,1,0:T(8,128)S(1)} %bitcast.384, f32[128,20,64]{0,2,1:T(8,128)S(1)} %bitcast.381, ...), kind=kOutput, calls=%fused_computation.18 | convolution fusion | flops 255405056 | bytes 1499136 | tf_op jit(solution)/shard_map/transpose(jvp(hij,jhp->ihp))/dot_general | solution.py:221
  85.1 2.6 %collective-permute-done.23 = f32[5,64,128]{2,1,0:T(8,128)S(1)} collective-permute-done((f32[5,64,128]{2,1,0:T(8,128)S(1)}, f32[5,64,128]{2,1,0:T(8,128)S(1)}, u32[]{:S(2)}, u32[]{:S(2)}) %collective-permute-start.23) | collective-permute-done | bytes 163872 | tf_op jit(solution)/shard_map/ppermute | solution.py:125
  89.7 3.5 %collective-permute-done.19 = f32[5,64,128]{2,1,0:T(8,128)S(1)} collective-permute-done((f32[5,64,128]{2,1,0:T(8,128)S(1)}, f32[5,64,128]{2,1,0:T(8,128)S(1)}, u32[]{:S(2)}, u32[]{:S(2)}) %collective-permute-start.19) | collective-permute-done | bytes 163872 | tf_op jit(solution)/shard_map/ppermute | solution.py:125
  94.9 2.4 %fusion.15 = f32[128,20,64]{0,2,1:T(8,128)} fusion(f32[20,64,128]{2,1,0:T(8,128)S(1)} %bitcast.387, f32[128,128]{1,0:T(8,128)S(1)} %copy-done.14, f32[20,128]{1,0:T(8,128)S(1)} %reduce_window_sum.45, pred[128,128]{1,0:T(8,128)(4,1)S(1)} %copy-done.19), kind=kOutput, calls=%fused_computation.12 | convolution fusion | flops 252968960 | bytes 1402880 | tf_op jit(solution)/shard_map/transpose(jvp(hij,jhp->ihp))/dot_general | solution.py:221
  97.3 3.8 %collective-permute-done.20 = f32[5,64,128]{2,1,0:T(8,128)S(1)} collective-permute-done((f32[5,64,128]{2,1,0:T(8,128)S(1)}, f32[5,64,128]{2,1,0:T(8,128)S(1)}, u32[]{:S(2)}, u32[]{:S(2)}) %collective-permute-start.20) | collective-permute-done | bytes 163872 | tf_op jit(solution)/shard_map/ppermute | solution.py:128
  102.8 5.7 %collective-permute-done.24 = f32[5,64,128]{2,1,0:T(8,128)S(1)} collective-permute-done((f32[5,64,128]{2,1,0:T(8,128)S(1)}, f32[5,64,128]{2,1,0:T(8,128)S(1)}, u32[]{:S(2)}, u32[]{:S(2)}) %collective-permute-start.24) | collective-permute-done | bytes 163872 | tf_op jit(solution)/shard_map/ppermute | solution.py:128
  111.1 5.4 %collective-permute-done.26 = f32[5,64,128]{2,1,0:T(8,128)S(1)} collective-permute-done((f32[5,64,128]{2,1,0:T(8,128)S(1)}, f32[5,64,128]{2,1,0:T(8,128)S(1)}, u32[]{:S(2)}, u32[]{:S(2)}) %collective-permute-start.26) | collective-permute-done | bytes 163872 | tf_op jit(solution)/shard_map/ppermute | solution.py:128
  119.9 1.8 %reduce_window_sum.46 = f32[20,128]{1,0:T(8,128)} reduce-window(f32[20,128]{1,0:T(8,128)S(1)} %negate_add_fusion, f32[]{:T(128)} %constant.666.clone.1), window={size=1x128 pad=0_0x0_127}, to_apply=%region_8.9 | reduce-window | flops 325120 | bytes 20484 | tf_op jit(solution)/shard_map/transpose(jvp(jit(cumsum)))/reduce_window_sum | solution.py:211
  122.4 3.2 %collective-permute-done.28 = f32[5,64,128]{2,1,0:T(8,128)} collective-permute-done((f32[5,64,128]{2,1,0:T(8,128)}, f32[5,64,128]{2,1,0:T(8,128)}, u32[]{:S(2)}, u32[]{:S(2)}) %collective-permute-start.28) | collective-permute-done | bytes 163872 | tf_op jit(solution)/shard_map/ppermute | solution.py:128
  127.1 2.7 %collective-permute-start.17 = (f32[5,64,128]{2,1,0:T(8,128)S(1)}, f32[5,64,128]{2,1,0:T(8,128)S(1)}, u32[]{:S(2)}, u32[]{:S(2)}) collective-permute-start(f32[5,64,128]{2,1,0:T(8,128)S(1)} %get-tuple-element.232), channel_id=1, source_target_pairs={{28,24},{24,28},{20,16},{16,20},{12,8},{8,12},{4,0},{0,4},{29,25},... | collective-permute-start | bytes 491528 | tf_op jit(solution)/shard_map/ppermute | solution.py:125
  129.8 1.9 %collective-permute-start.25 = (f32[5,64,128]{2,1,0:T(8,128)S(1)}, f32[5,64,128]{2,1,0:T(8,128)S(1)}, u32[]{:S(2)}, u32[]{:S(2)}) collective-permute-start(f32[5,64,128]{2,1,0:T(8,128)S(1)} %get-tuple-element.230), channel_id=1, source_target_pairs={{28,24},{24,28},{20,16},{16,20},{12,8},{8,12},{4,0},{0,4},{29,25},... | collective-permute-start | bytes 491528 | tf_op jit(solution)/shard_map/ppermute | solution.py:125
  131.8 1.9 %collective-permute-start.29 = (f32[5,64,128]{2,1,0:T(8,128)S(1)}, f32[5,64,128]{2,1,0:T(8,128)S(1)}, u32[]{:S(2)}, u32[]{:S(2)}) collective-permute-start(f32[5,64,128]{2,1,0:T(8,128)S(1)} %get-tuple-element.228), channel_id=1, source_target_pairs={{28,24},{24,28},{20,16},{16,20},{12,8},{8,12},{4,0},{0,4},{29,25},... | collective-permute-start | bytes 491528 | tf_op jit(solution)/shard_map/ppermute | solution.py:125
  135.1 1.7 %collective-permute-done.25 = f32[5,64,128]{2,1,0:T(8,128)S(1)} collective-permute-done((f32[5,64,128]{2,1,0:T(8,128)S(1)}, f32[5,64,128]{2,1,0:T(8,128)S(1)}, u32[]{:S(2)}, u32[]{:S(2)}) %collective-permute-start.25) | collective-permute-done | bytes 163872 | tf_op jit(solution)/shard_map/ppermute | solution.py:125
  140.6 1.9 %convolution_bitcast_fusion.3 = f32[128,128]{1,0:T(8,128)} fusion(f32[128,20,64]{0,2,1:T(8,128)S(1)} %bitcast.382, f32[128,20]{0,1:T(8,128)S(1)} %get-tuple-element.253, f32[128,20]{0,1:T(8,128)S(1)} %bitcast.414, f32[10,64,128]{2,1,0:T(8,128)S(1)} %bitcast.371, f32[10,64,128]{2,1,0:T(8,128)S(1)} %bitcast.368, pred[]{:T(512)S(6)} %eq.10), kind=kOutput, calls=%fused_computation.15 | convolution fusion | flops 252477440 | bytes 1396737 | tf_op jit(solution)/shard_map/transpose(jvp(jhp,jn->hpn))/dot_general | solution.py:240
  143.2 2.7 %multiply_reduce_fusion.2 = (f32[128,20]{0,1:T(8,128)S(1)}, f32[128,20]{0,1:T(8,128)S(1)}, f32[128,20]{0,1:T(8,128)}, f32[128,20,64]{0,2,1:T(8,128)S(1)}, f32[128,20]{0,1:T(8,128)S(1)}) fusion(f32[128,20,64]{0,2,1:T(8,128)S(1)} %bitcast.383, f32[128,20]{0,1:T(8,128)S(1)} %bitcast.415, f32[128,20]{0,1:T(8,128)S(1)} %get-tuple-element.253, ...), kind=kOutput, calls=%fused_computation.22 | convolution fusion | flops 254597120 | bytes 4059217 | tf_op jit(solution)/shard_map/transpose(jvp(jhp,jn->hpn))/dot_general | solution.py:240
  154.3 2.5 %collective-permute-done.31 = f32[128,128]{1,0:T(8,128)S(1)} collective-permute-done((f32[128,128]{1,0:T(8,128)S(1)}, f32[128,128]{1,0:T(8,128)S(1)}, u32[]{:S(2)}, u32[]{:S(2)}) %collective-permute-start.31) | collective-permute-done | bytes 65568 | tf_op jit(solution)/shard_map/ppermute | solution.py:157
  (254 shorter events, 60.5 us)
Async XLA Ops:
  2.1 10.6 %collective-permute-start.1 = (f32[5]{0:T(128)S(1)}, f32[5]{0:T(128)S(1)}, u32[]{:S(2)}, u32[]{:S(2)}) collective-permute-start(f32[5]{0:T(128)S(1)} %get-tuple-element.297), channel_id=1, source_target_pairs={{0,4},{4,0},{8,12},{12,8},{16,20},{20,16},{24,28},{28,24},{1,5},{5... | collective-permute-start | bytes 68 | tf_op jit(solution)/shard_map/ppermute | solution.py:125
  5.0 7.7 %collective-permute-start.5 = (f32[5]{0:T(128)S(1)}, f32[5]{0:T(128)S(1)}, u32[]{:S(2)}, u32[]{:S(2)}) collective-permute-start(f32[5]{0:T(128)S(1)} %get-tuple-element.296), channel_id=1, source_target_pairs={{0,4},{4,0},{8,12},{12,8},{16,20},{20,16},{24,28},{28,24},{1,5},{5... | collective-permute-start | bytes 68 | tf_op jit(solution)/shard_map/ppermute | solution.py:125
  7.2 6.4 %collective-permute-start.6 = (f32[5,64,128]{2,1,0:T(8,128)S(1)}, f32[5,64,128]{2,1,0:T(8,128)S(1)}, u32[]{:S(2)}, u32[]{:S(2)}) collective-permute-start(f32[5,64,128]{2,1,0:T(8,128)S(1)} %constant_dynamic-slice_fusion.43), channel_id=1, source_target_pairs={{0,4},{4,0},{8,12},{12,8},{16,20},{20,16},{24,28},{28,24},{1,5},{5... | collective-permute-start | bytes 491528 | tf_op jit(solution)/shard_map/ppermute | solution.py:125
  9.3 3.7 %collective-permute-start.18 = (f32[5]{0:T(128)S(1)}, f32[5]{0:T(128)S(1)}, u32[]{:S(2)}, u32[]{:S(2)}) collective-permute-start(f32[5]{0:T(128)S(1)} %get-tuple-element.289), channel_id=1, source_target_pairs={{28,24},{24,28},{20,16},{16,20},{12,8},{8,12},{4,0},{0,4},{29,25},... | collective-permute-start | bytes 68 | tf_op jit(solution)/shard_map/ppermute | solution.py:125
  9.4 3.6 %collective-permute-start.22 = (f32[5]{0:T(128)S(1)}, f32[5]{0:T(128)S(1)}, u32[]{:S(2)}, u32[]{:S(2)}) collective-permute-start(f32[5]{0:T(128)S(1)} %get-tuple-element.288), channel_id=1, source_target_pairs={{28,24},{24,28},{20,16},{16,20},{12,8},{8,12},{4,0},{0,4},{29,25},... | collective-permute-start | bytes 68 | tf_op jit(solution)/shard_map/ppermute | solution.py:125
  13.8 5.4 %collective-permute-start.2 = (f32[5,64,128]{2,1,0:T(8,128)S(1)}, f32[5,64,128]{2,1,0:T(8,128)S(1)}, u32[]{:S(2)}, u32[]{:S(2)}) collective-permute-start(f32[5,64,128]{2,1,0:T(8,128)S(1)} %get-tuple-element.227), channel_id=1, source_target_pairs={{0,4},{4,0},{8,12},{12,8},{16,20},{20,16},{24,28},{28,24},{1,5},{5... | collective-permute-start | bytes 491528 | tf_op jit(solution)/shard_map/ppermute | solution.py:125
  19.3 6.7 %collective-permute-start.3 = (f32[5,64,128]{2,1,0:T(8,128)S(1)}, f32[5,64,128]{2,1,0:T(8,128)S(1)}, u32[]{:S(2)}, u32[]{:S(2)}) collective-permute-start(f32[5,64,128]{2,1,0:T(8,128)S(1)} %fusion.52), channel_id=1, source_target_pairs={{0,8},{4,12},{8,16},{12,20},{16,24},{20,28},{1,9},{5,13},{9,17},{1... | collective-permute-start | bytes 491528 | tf_op jit(solution)/shard_map/ppermute | solution.py:128
  26.1 8.1 %collective-permute-start.7 = (f32[5,64,128]{2,1,0:T(8,128)S(1)}, f32[5,64,128]{2,1,0:T(8,128)S(1)}, u32[]{:S(2)}, u32[]{:S(2)}) collective-permute-start(f32[5,64,128]{2,1,0:T(8,128)S(1)} %fusion.77), channel_id=1, source_target_pairs={{0,8},{4,12},{8,16},{12,20},{16,24},{20,28},{1,9},{5,13},{9,17},{1... | collective-permute-start | bytes 491528 | tf_op jit(solution)/shard_map/ppermute | solution.py:128
  34.4 8.7 %collective-permute-start.9 = (f32[5,64,128]{2,1,0:T(8,128)S(1)}, f32[5,64,128]{2,1,0:T(8,128)S(1)}, u32[]{:S(2)}, u32[]{:S(2)}) collective-permute-start(f32[5,64,128]{2,1,0:T(8,128)S(1)} %fusion.80), channel_id=1, source_target_pairs={{0,8},{4,12},{8,16},{12,20},{16,24},{20,28},{1,9},{5,13},{9,17},{1... | collective-permute-start | bytes 491528 | tf_op jit(solution)/shard_map/ppermute | solution.py:128
  43.3 7.2 %collective-permute-start.11 = (f32[5,64,128]{2,1,0:T(8,128)S(1)}, f32[5,64,128]{2,1,0:T(8,128)S(1)}, u32[]{:S(2)}, u32[]{:S(2)}) collective-permute-start(f32[5,64,128]{2,1,0:T(8,128)S(1)} %fusion.74), channel_id=1, source_target_pairs={{0,8},{4,12},{8,16},{12,20},{16,24},{20,28},{1,9},{5,13},{9,17},{1... | collective-permute-start | bytes 491528 | tf_op jit(solution)/shard_map/ppermute | solution.py:128
  50.8 5.7 %collective-permute-start = (f32[5,64,128]{2,1,0:T(8,128)S(1)}, f32[5,64,128]{2,1,0:T(8,128)S(1)}, u32[]{:S(2)}, u32[]{:S(2)}) collective-permute-start(f32[5,64,128]{2,1,0:T(8,128)S(1)} %get-tuple-element.243), channel_id=1, source_target_pairs={{0,4},{4,0},{8,12},{12,8},{16,20},{20,16},{24,28},{28,24},{1,5},{5... | collective-permute-start | bytes 491528 | tf_op jit(solution)/shard_map/ppermute | solution.py:125
  52.3 5.8 %collective-permute-start.4 = (f32[5,64,128]{2,1,0:T(8,128)S(1)}, f32[5,64,128]{2,1,0:T(8,128)S(1)}, u32[]{:S(2)}, u32[]{:S(2)}) collective-permute-start(f32[5,64,128]{2,1,0:T(8,128)S(1)} %get-tuple-element.242), channel_id=1, source_target_pairs={{0,4},{4,0},{8,12},{12,8},{16,20},{20,16},{24,28},{28,24},{1,5},{5... | collective-permute-start | bytes 491528 | tf_op jit(solution)/shard_map/ppermute | solution.py:125
  52.9 7.0 %collective-permute-start.8 = (f32[5,64,128]{2,1,0:T(8,128)S(1)}, f32[5,64,128]{2,1,0:T(8,128)S(1)}, u32[]{:S(2)}, u32[]{:S(2)}) collective-permute-start(f32[5,64,128]{2,1,0:T(8,128)S(1)} %get-tuple-element.241), channel_id=1, source_target_pairs={{0,4},{4,0},{8,12},{12,8},{16,20},{20,16},{24,28},{28,24},{1,5},{5... | collective-permute-start | bytes 491528 | tf_op jit(solution)/shard_map/ppermute | solution.py:125
  54.4 7.3 %collective-permute-start.10 = (f32[5,64,128]{2,1,0:T(8,128)S(1)}, f32[5,64,128]{2,1,0:T(8,128)S(1)}, u32[]{:S(2)}, u32[]{:S(2)}) collective-permute-start(f32[5,64,128]{2,1,0:T(8,128)S(1)} %get-tuple-element.240), channel_id=1, source_target_pairs={{0,4},{4,0},{8,12},{12,8},{16,20},{20,16},{24,28},{28,24},{1,5},{5... | collective-permute-start | bytes 491528 | tf_op jit(solution)/shard_map/ppermute | solution.py:125
  54.9 8.5 %collective-permute-start.12 = (f32[5,64,128]{2,1,0:T(8,128)S(1)}, f32[5,64,128]{2,1,0:T(8,128)S(1)}, u32[]{:S(2)}, u32[]{:S(2)}) collective-permute-start(f32[5,64,128]{2,1,0:T(8,128)S(1)} %get-tuple-element.239), channel_id=1, source_target_pairs={{0,4},{4,0},{8,12},{12,8},{16,20},{20,16},{24,28},{28,24},{1,5},{5... | collective-permute-start | bytes 491528 | tf_op jit(solution)/shard_map/ppermute | solution.py:125
  70.8 3.5 %collective-permute-start.14 = (f32[128]{0:T(128)S(1)}, f32[128]{0:T(128)S(1)}, u32[]{:S(2)}, u32[]{:S(2)}) collective-permute-start(f32[128]{0:T(128)S(1)} %add.398), channel_id=1, source_target_pairs={{0,2},{1,3},{2,0},{3,1},{4,6},{5,7},{6,4},{7,5},{8,10},{9,11},{10,... | collective-permute-start | bytes 1544 | tf_op jit(solution)/shard_map/ppermute | solution.py:157
  72.3 3.5 %collective-permute-start.16 = (f32[128]{0:T(128)S(1)}, f32[128]{0:T(128)S(1)}, u32[]{:S(2)}, u32[]{:S(2)}) collective-permute-start(f32[128]{0:T(128)S(1)} %add.402), channel_id=1, source_target_pairs={{0,2},{1,3},{2,0},{3,1},{4,6},{5,7},{6,4},{7,5},{8,10},{9,11},{10,... | collective-permute-start | bytes 1544 | tf_op jit(solution)/shard_map/ppermute | solution.py:157
  82.3 5.4 %collective-permute-start.23 = (f32[5,64,128]{2,1,0:T(8,128)S(1)}, f32[5,64,128]{2,1,0:T(8,128)S(1)}, u32[]{:S(2)}, u32[]{:S(2)}) collective-permute-start(f32[5,64,128]{2,1,0:T(8,128)S(1)} %constant_dynamic-slice_fusion.14), channel_id=1, source_target_pairs={{28,24},{24,28},{20,16},{16,20},{12,8},{8,12},{4,0},{0,4},{29,25},... | collective-permute-start | bytes 491528 | tf_op jit(solution)/shard_map/ppermute | solution.py:125
  87.8 5.4 %collective-permute-start.19 = (f32[5,64,128]{2,1,0:T(8,128)S(1)}, f32[5,64,128]{2,1,0:T(8,128)S(1)}, u32[]{:S(2)}, u32[]{:S(2)}) collective-permute-start(f32[5,64,128]{2,1,0:T(8,128)S(1)} %get-tuple-element.225), channel_id=1, source_target_pairs={{28,24},{24,28},{20,16},{16,20},{12,8},{8,12},{4,0},{0,4},{29,25},... | collective-permute-start | bytes 491528 | tf_op jit(solution)/shard_map/ppermute | solution.py:125
  89.6 20.9 %collective-permute-start.32 = (f32[128,128]{1,0:T(8,128)S(1)}, f32[128,128]{1,0:T(8,128)S(1)}, u32[]{:S(2)}, u32[]{:S(2)}) collective-permute-start(f32[128,128]{1,0:T(8,128)S(1)} %convolution_add_fusion), channel_id=1, source_target_pairs={{0,1},{1,0},{2,3},{3,2},{4,5},{5,4},{6,7},{7,6},{8,9},{9,8},{10,11... | collective-permute-start | bytes 196616 | tf_op jit(solution)/shard_map/ppermute | solution.py:157
  93.4 7.7 %collective-permute-start.20 = (f32[5,64,128]{2,1,0:T(8,128)S(1)}, f32[5,64,128]{2,1,0:T(8,128)S(1)}, u32[]{:S(2)}, u32[]{:S(2)}) collective-permute-start(f32[5,64,128]{2,1,0:T(8,128)S(1)} %fusion.58), channel_id=1, source_target_pairs={{28,20},{24,16},{20,12},{16,8},{12,4},{8,0},{29,21},{25,17},{21,13... | collective-permute-start | bytes 491528 | tf_op jit(solution)/shard_map/ppermute | solution.py:128
  101.3 7.2 %collective-permute-start.24 = (f32[5,64,128]{2,1,0:T(8,128)S(1)}, f32[5,64,128]{2,1,0:T(8,128)S(1)}, u32[]{:S(2)}, u32[]{:S(2)}) collective-permute-start(f32[5,64,128]{2,1,0:T(8,128)S(1)} %fusion.68), channel_id=1, source_target_pairs={{28,20},{24,16},{20,12},{16,8},{12,4},{8,0},{29,21},{25,17},{21,13... | collective-permute-start | bytes 491528 | tf_op jit(solution)/shard_map/ppermute | solution.py:128
  109.2 7.4 %collective-permute-start.26 = (f32[5,64,128]{2,1,0:T(8,128)S(1)}, f32[5,64,128]{2,1,0:T(8,128)S(1)}, u32[]{:S(2)}, u32[]{:S(2)}) collective-permute-start(f32[5,64,128]{2,1,0:T(8,128)S(1)} %fusion.71), channel_id=1, source_target_pairs={{28,20},{24,16},{20,12},{16,8},{12,4},{8,0},{29,21},{25,17},{21,13... | collective-permute-start | bytes 491528 | tf_op jit(solution)/shard_map/ppermute | solution.py:128
  110.5 11.2 %collective-permute-start.33 = (f32[128,128]{1,0:T(8,128)S(1)}, f32[128,128]{1,0:T(8,128)S(1)}, u32[]{:S(2)}, u32[]{:S(2)}) collective-permute-start(f32[128,128]{1,0:T(8,128)S(1)} %add.430), channel_id=1, source_target_pairs={{0,2},{1,3},{2,0},{3,1},{4,6},{5,7},{6,4},{7,5},{8,10},{9,11},{10,... | collective-permute-start | bytes 196616 | tf_op jit(solution)/shard_map/ppermute | solution.py:157
  117.9 7.8 %collective-permute-start.28 = (f32[5,64,128]{2,1,0:T(8,128)}, f32[5,64,128]{2,1,0:T(8,128)}, u32[]{:S(2)}, u32[]{:S(2)}) collective-permute-start(f32[5,64,128]{2,1,0:T(8,128)} %fusion.65), channel_id=1, source_target_pairs={{28,20},{24,16},{20,12},{16,8},{12,4},{8,0},{29,21},{25,17},{21,13... | collective-permute-start | bytes 491528 | tf_op jit(solution)/shard_map/ppermute | solution.py:128
  127.1 6.8 %collective-permute-start.17 = (f32[5,64,128]{2,1,0:T(8,128)S(1)}, f32[5,64,128]{2,1,0:T(8,128)S(1)}, u32[]{:S(2)}, u32[]{:S(2)}) collective-permute-start(f32[5,64,128]{2,1,0:T(8,128)S(1)} %get-tuple-element.232), channel_id=1, source_target_pairs={{28,24},{24,28},{20,16},{16,20},{12,8},{8,12},{4,0},{0,4},{29,25},... | collective-permute-start | bytes 491528 | tf_op jit(solution)/shard_map/ppermute | solution.py:125
  129.7 5.3 %collective-permute-start.21 = (f32[5,64,128]{2,1,0:T(8,128)S(1)}, f32[5,64,128]{2,1,0:T(8,128)S(1)}, u32[]{:S(2)}, u32[]{:S(2)}) collective-permute-start(f32[5,64,128]{2,1,0:T(8,128)S(1)} %get-tuple-element.231), channel_id=1, source_target_pairs={{28,24},{24,28},{20,16},{16,20},{12,8},{8,12},{4,0},{0,4},{29,25},... | collective-permute-start | bytes 491528 | tf_op jit(solution)/shard_map/ppermute | solution.py:125
  129.8 7.0 %collective-permute-start.25 = (f32[5,64,128]{2,1,0:T(8,128)S(1)}, f32[5,64,128]{2,1,0:T(8,128)S(1)}, u32[]{:S(2)}, u32[]{:S(2)}) collective-permute-start(f32[5,64,128]{2,1,0:T(8,128)S(1)} %get-tuple-element.230), channel_id=1, source_target_pairs={{28,24},{24,28},{20,16},{16,20},{12,8},{8,12},{4,0},{0,4},{29,25},... | collective-permute-start | bytes 491528 | tf_op jit(solution)/shard_map/ppermute | solution.py:125
  131.7 6.8 %collective-permute-start.27 = (f32[5,64,128]{2,1,0:T(8,128)S(1)}, f32[5,64,128]{2,1,0:T(8,128)S(1)}, u32[]{:S(2)}, u32[]{:S(2)}) collective-permute-start(f32[5,64,128]{2,1,0:T(8,128)S(1)} %get-tuple-element.229), channel_id=1, source_target_pairs={{28,24},{24,28},{20,16},{16,20},{12,8},{8,12},{4,0},{0,4},{29,25},... | collective-permute-start | bytes 491528 | tf_op jit(solution)/shard_map/ppermute | solution.py:125
  131.8 8.5 %collective-permute-start.29 = (f32[5,64,128]{2,1,0:T(8,128)S(1)}, f32[5,64,128]{2,1,0:T(8,128)S(1)}, u32[]{:S(2)}, u32[]{:S(2)}) collective-permute-start(f32[5,64,128]{2,1,0:T(8,128)S(1)} %get-tuple-element.228), channel_id=1, source_target_pairs={{28,24},{24,28},{20,16},{16,20},{12,8},{8,12},{4,0},{0,4},{29,25},... | collective-permute-start | bytes 491528 | tf_op jit(solution)/shard_map/ppermute | solution.py:125
  147.3 4.8 %collective-permute-start.30 = (f32[128,128]{1,0:T(8,128)S(1)}, f32[128,128]{1,0:T(8,128)S(1)}, u32[]{:S(2)}, u32[]{:S(2)}) collective-permute-start(f32[128,128]{1,0:T(8,128)S(1)} %convolution_add_fusion.1), channel_id=1, source_target_pairs={{0,1},{1,0},{2,3},{3,2},{4,5},{5,4},{6,7},{7,6},{8,9},{9,8},{10,11... | collective-permute-start | bytes 196616 | tf_op jit(solution)/shard_map/ppermute | solution.py:157
  152.2 4.6 %collective-permute-start.31 = (f32[128,128]{1,0:T(8,128)S(1)}, f32[128,128]{1,0:T(8,128)S(1)}, u32[]{:S(2)}, u32[]{:S(2)}) collective-permute-start(f32[128,128]{1,0:T(8,128)S(1)} %add.427), channel_id=1, source_target_pairs={{0,2},{1,3},{2,0},{3,1},{4,6},{5,7},{6,4},{7,5},{8,10},{9,11},{10,... | collective-permute-start | bytes 196616 | tf_op jit(solution)/shard_map/ppermute | solution.py:157
  (46 other events, 263.6 us)

commit v4 on v2

--- a/solution.py
+++ b/solution.py
@@ -142,10 +142,19 @@
     return (last_state, outputs.reshape(length, head_count * head_width))
 
 
+def prefix_sum(decay_in):
+    length = decay_in.shape[1]
+    upper = (
+        lax.broadcasted_iota(jnp.int32, (length, length), 0)
+        <= lax.broadcasted_iota(jnp.int32, (length, length), 1)
+    ).astype(decay_in.dtype)
+    return jnp.dot(decay_in, upper, precision=highest)
+
+
 def within_part(feat_in, step_in, decay_in, writes, read_in, skip_scale):
     head_count, length = step_in.shape
     head_width = feat_in.shape[1] // head_count
-    cumul = jnp.cumsum(decay_in, axis=1)
+    cumul = prefix_sum(decay_in)
     row_index = lax.broadcasted_iota(jnp.int32, (length, length), 0)
     col_index = lax.broadcasted_iota(jnp.int32, (length, length), 1)
     causal = row_index >= col_index
@@ -161,7 +170,7 @@
 
 def carried_part(decay_in, read_in, state_in):
     length = decay_in.shape[1]
-    cumul = jnp.cumsum(decay_in, axis=1)
+    cumul = prefix_sum(decay_in)
     carried = jnp.einsum("in,hpn->ihp", read_in, state_in, precision=highest)
     carried = carried * jnp.transpose(jnp.exp(cumul))[:, :, None]
     return carried.reshape(length, -1)
@@ -170,7 +179,7 @@
 def state_update(feat_in, step_in, decay_in, writes):
     head_count, length = step_in.shape
     head_width = feat_in.shape[1] // head_count
-    cumul = jnp.cumsum(decay_in, axis=1)
+    cumul = prefix_sum(decay_in)
     scaled = feat_in.reshape(length, head_count, head_width) * jnp.transpose(step_in)[:, :, None]
     to_end = jnp.exp(cumul[:, -1:] - cumul)
     weighted_in = scaled * jnp.transpose(to_end)[:, :, None]
@@ -178,7 +187,7 @@
 
 
 def end_part(feat_in, step_in, decay_in, writes, state_in):
-    total = jnp.exp(jnp.cumsum(decay_in, axis=1)[:, -1])
+    total = jnp.exp(prefix_sum(decay_in)[:, -1])
     return total[:, None, None] * state_in + state_update(feat_in, step_in, decay_in, writes)
 
 
@@ -196,7 +205,7 @@
     head_count, length = step_sizes.shape
     head_width = features.shape[1] // head_count
     channels = features.shape[1] * lax.axis_size("head")
-    cumul = jnp.cumsum(log_decay, axis=1)
+    cumul = prefix_sum(log_decay)
     decay_total = jnp.exp(cumul[:, -1])
     scaled = (
         features.reshape(length, head_count, head_width) * jnp.transpose(step_sizes)[:, :, None]

time: 125 us -> 121 us (0.968)
  other arithmetic: 14.9 us -> 7.83 us
  matrix products: 16.4 us -> 18.7 us
    another operation x5 -> x0, other arithmetic: 4.87 us -> none  [the longest x2 2.26 us: within_part(): cumul = jnp.cumsum(decay_in, axis=1)]
    dot_general x0 -> x5, matrix products: none -> 2.23 us  [prefix_sum(): return jnp.dot(decay_in, upper, precision=highest)]
    unnamed x38 -> x36, local copies, waits for them, and re-layouts: 2.98 us -> 2.98 us
  transfers between devices with their start and end apart: 20 -> 20, of which waited for: 12 -> 13; matrix products, arithmetic and copies ran while one was open for 11% -> 10% of each run, Pallas kernels for 0% -> 0%
where the time goes in v4:
time: 121 us; the launch traced here: 120 us
  waiting for transfers between devices  64.2 us (53%)
  starting transfers between devices  22.3 us (18%)
  matrix products  18.7 us (15%)
  other arithmetic  7.83 us (6%)
  local copies, waits for them, and re-layouts  6.19 us (5%)
    ppermute x2, waiting for transfers between devices, pair_scan(): s_in = lax.ppermute(out[1], axis, pairs)  28.2 us
    ppermute x4, waiting for transfers between devices, pair_scan(): a_rcv, s_rcv = lax.ppermute((a_snd, s_snd), axis, swap)  16.4 us
    ppermute x8, waiting for transfers between devices, butterfly_psum(): got = lax.ppermute(parts, axis, [(i, i ^ k) for i in range(count)])  9.27 us
    dot_general x3, matrix products, within_part(): within = jnp.einsum('hij,jhp->ihp', masked, scaled, precision=highest)  8.92 us
    ppermute x4, starting transfers between devices, pair_scan(): a_in, s_in = lax.ppermute(out, axis, pairs)  6.49 us
    ppermute x4, starting transfers between devices, pair_scan(): a_rcv, s_rcv = lax.ppermute((a_snd, s_snd), axis, swap)  6.35 us
    ppermute x2, waiting for transfers between devices, pair_scan(): other = lax.ppermute(send, axis, swap)  5.56 us
    ppermute x4, waiting for transfers between devices, pair_scan(): a_in, s_in = lax.ppermute(out, axis, pairs)  4.82 us
  transfers between devices with their start and end apart: 20, of which 13 were waited for; matrix products, arithmetic and copies ran while one was open for 10% of the time, Pallas kernels for 0%

profile of v4, /device:TPU:0, one launch (start us, length us, event | category | flops | bytes accessed | tf_op | source)
XLA Modules:
  0.0 120.3 jit_solution(11759581658569980509)
XLA Ops:
  0.7 0.9 fusion.60
  1.8 1.3 %copy.22 = f32[128,1280]{0,1:T(8,128)S(1)} copy(f32[128,1280]{1,0:T(8,128)} %param.9) | data formatting | bytes 1310720 | tf_op args[0]
  3.9 3.0 %collective-permute-start.1 = (f32[10,64,128]{2,1,0:T(8,128)S(1)}, f32[10,64,128]{2,1,0:T(8,128)S(1)}, u32[]{:S(2)}, u32[]{:S(2)}) collective-permute-start(f32[10,64,128]{2,1,0:T(8,128)S(1)} %constant_dynamic-slice_fusion.1), channel_id=1, source_target_pairs={{0,4},{4,0},{8,12},{12,8},{16,20},{20,16},{24,28},{28,24},{1,5},{5... | collective-permute-start | bytes 983048 | tf_op jit(solution)/shard_map/ppermute | solution.py:42
  7.0 7.6 %collective-permute-done.10 = f32[10]{0:T(128)S(1)} collective-permute-done((f32[10]{0:T(128)S(1)}, f32[10]{0:T(128)S(1)}, u32[]{:S(2)}, u32[]{:S(2)}) %collective-permute-start.10) | collective-permute-done | bytes 72 | tf_op jit(solution)/shard_map/ppermute | solution.py:42
  15.3 1.7 %collective-permute-start = (f32[10]{0:T(128)S(1)}, f32[10]{0:T(128)S(1)}, u32[]{:S(2)}, u32[]{:S(2)}) collective-permute-start(f32[10]{0:T(128)S(1)} %get-tuple-element.54), channel_id=1, source_target_pairs={{0,4},{4,0},{8,12},{12,8},{16,20},{20,16},{24,28},{28,24},{1,5},{5... | collective-permute-start | bytes 128 | tf_op jit(solution)/shard_map/ppermute | solution.py:42
  17.0 1.8 %collective-permute-done = f32[10]{0:T(128)S(1)} collective-permute-done((f32[10]{0:T(128)S(1)}, f32[10]{0:T(128)S(1)}, u32[]{:S(2)}, u32[]{:S(2)}) %collective-permute-start) | collective-permute-done | bytes 72 | tf_op jit(solution)/shard_map/ppermute | solution.py:42
  19.0 3.7 %collective-permute-start.2 = (f32[10,64,128]{2,1,0:T(8,128)S(1)}, f32[10,64,128]{2,1,0:T(8,128)S(1)}, u32[]{:S(2)}, u32[]{:S(2)}) collective-permute-start(f32[10,64,128]{2,1,0:T(8,128)S(1)} %get-tuple-element.38), channel_id=1, source_target_pairs={{0,8},{4,12},{1,9},{5,13},{2,10},{6,14},{3,11},{7,15}} | collective-permute-start | bytes 983048 | tf_op jit(solution)/shard_map/ppermute | solution.py:62
  22.8 4.8 %collective-permute-done.2 = f32[10,64,128]{2,1,0:T(8,128)S(1)} collective-permute-done((f32[10,64,128]{2,1,0:T(8,128)S(1)}, f32[10,64,128]{2,1,0:T(8,128)S(1)}, u32[]{:S(2)}, u32[]{:S(2)}) %collective-permute-start.2) | collective-permute-done | bytes 327712 | tf_op jit(solution)/shard_map/ppermute | solution.py:62
  29.4 1.6 %collective-permute-start.5 = (f32[10,64,128]{2,1,0:T(8,128)S(1)}, f32[10,64,128]{2,1,0:T(8,128)S(1)}, u32[]{:S(2)}, u32[]{:S(2)}) collective-permute-start(f32[10,64,128]{2,1,0:T(8,128)S(1)} %get-tuple-element.50), channel_id=1, source_target_pairs={{0,4},{4,0},{8,12},{12,8},{16,20},{20,16},{24,28},{28,24},{1,5},{5... | collective-permute-start | bytes 983048 | tf_op jit(solution)/shard_map/ppermute | solution.py:82
  31.2 5.3 %collective-permute-done.5 = f32[10,64,128]{2,1,0:T(8,128)S(1)} collective-permute-done((f32[10,64,128]{2,1,0:T(8,128)S(1)}, f32[10,64,128]{2,1,0:T(8,128)S(1)}, u32[]{:S(2)}, u32[]{:S(2)}) %collective-permute-start.5) | collective-permute-done | bytes 327712 | tf_op jit(solution)/shard_map/ppermute | solution.py:82
  37.2 3.5 %multiply_add_fusion.1 = f32[128,20,64]{0,2,1:T(8,128)} fusion(f32[128,20,64]{0,2,1:T(8,128)S(1)} %convolution_bitcast_fusion.1, f32[128,20,64]{0,2,1:T(8,128)S(1)} %bitcast.73, f32[128,128]{1,0:T(8,128)S(1)} %fusion.86, f32[20,128]{1,0:T(8,128)S(1)} %bitcast.85, pred[128,128]{1,0:T(8,128)(4,1)S(1)} %iota_compare_fusion.6, ...), kind=kOutput, calls=%fused_computation.35 | convolution fusion | flops 253788160 | bytes 2078800 | tf_op jit(solution)/shard_map/jvp(hij,jhp->ihp)/dot_general | solution.py:167
  40.8 1.4 %copy.23 = f32[128,1280]{1,0:T(8,128)S(1)} copy(f32[128,1280]{0,1:T(8,128)} %bitcast.83) | data formatting | bytes 1310720 | tf_op jit(solution)/shard_map/add | solution.py:226
  42.2 1.5 %multiply_reduce_fusion.7 = (f32[128]{0:T(128)S(1)}, f32[128]{0:T(128)S(1)}) fusion(f32[128,1280]{1,0:T(8,128)S(1)} %copy.23, f32[128,1280]{1,0:T(8,128)S(1)} %copy-done.1, f32[128,1280]{1,0:T(8,128)} %param.17, f32[1280]{0:T(1024)S(1)} %copy-done.11), kind=kLoop, calls=%fused_computation.32 | loop fusion | flops 1638144 | bytes 1972224 | tf_op jit(solution)/shard_map/reduce_sum | solution.py:243
  44.9 1.5 %collective-permute-start.7 = (f32[128]{0:T(128)S(1)}, f32[128]{0:T(128)S(1)}, u32[]{:S(2)}, u32[]{:S(2)}) collective-permute-start(f32[128]{0:T(128)S(1)} %add.147), channel_id=1, source_target_pairs={{0,2},{1,3},{2,0},{3,1},{4,6},{5,7},{6,4},{7,5},{8,10},{9,11},{10,... | collective-permute-start | bytes 1544 | tf_op jit(solution)/shard_map/ppermute | solution.py:94
  46.9 1.5 %collective-permute-done.7 = f32[128]{0:T(128)S(1)} collective-permute-done((f32[128]{0:T(128)S(1)}, f32[128]{0:T(128)S(1)}, u32[]{:S(2)}, u32[]{:S(2)}) %collective-permute-start.7) | collective-permute-done | bytes 544 | tf_op jit(solution)/shard_map/ppermute | solution.py:94
  48.4 1.5 %collective-permute-done.9 = f32[128]{0:T(128)S(1)} collective-permute-done((f32[128]{0:T(128)S(1)}, f32[128]{0:T(128)S(1)}, u32[]{:S(2)}, u32[]{:S(2)}) %collective-permute-start.9) | collective-permute-done | bytes 544 | tf_op jit(solution)/shard_map/ppermute | solution.py:94
  50.0 1.5 %add_multiply_fusion = (f32[128,1280]{1,0:T(8,128)}, f32[128,1280]{1,0:T(8,128)}) fusion(f32[128,1280]{1,0:T(8,128)S(1)} %copy-done.1, f32[128,1280]{1,0:T(8,128)S(1)} %copy.23, f32[128]{0:T(128)S(1)} %get-tuple-element.34, f32[128,1280]{1,0:T(8,128)S(1)} %copy-done.2, f32[1280]{0:T(1024)S(1)} %copy-done.11, f32[128]{0:T(128)S(1)} %get-tuple-element.35), kind=kLoop, calls=%fused_computation.28 | loop fusion | flops 2621440 | bytes 3282944 | tf_op jit(solution)/shard_map/mul | solution.py:251
  51.5 1.3 %copy.24 = f32[128,1280]{0,1:T(8,128)S(1)} copy(f32[128,1280]{1,0:T(8,128)} %get-tuple-element.45) | data formatting | bytes 1310720 | tf_op jit(solution)/shard_map/mul | solution.py:250
  53.5 1.6 %collective-permute-start.11 = (f32[10,64,128]{2,1,0:T(8,128)S(1)}, f32[10,64,128]{2,1,0:T(8,128)S(1)}, u32[]{:S(2)}, u32[]{:S(2)}) collective-permute-start(f32[10,64,128]{2,1,0:T(8,128)S(1)} %constant_dynamic-slice_fusion), channel_id=1, source_target_pairs={{28,24},{24,28},{20,16},{16,20},{12,8},{8,12},{4,0},{0,4},{29,25},... | collective-permute-start | bytes 983048 | tf_op jit(solution)/shard_map/ppermute | solution.py:42
  55.1 6.9 %collective-permute-done.11 = f32[10,64,128]{2,1,0:T(8,128)S(1)} collective-permute-done((f32[10,64,128]{2,1,0:T(8,128)S(1)}, f32[10,64,128]{2,1,0:T(8,128)S(1)}, u32[]{:S(2)}, u32[]{:S(2)}) %collective-permute-start.11) | collective-permute-done | bytes 327712 | tf_op jit(solution)/shard_map/ppermute | solution.py:42
  62.8 1.4 %collective-permute-start.12 = (f32[10,64,128]{2,1,0:T(8,128)}, f32[10,64,128]{2,1,0:T(8,128)}, u32[]{:S(2)}, u32[]{:S(2)}) collective-permute-start(f32[10,64,128]{2,1,0:T(8,128)} %get-tuple-element.28), channel_id=1, source_target_pairs={{28,20},{24,16},{29,21},{25,17},{30,22},{26,18},{31,23},{27,19}} | collective-permute-start | bytes 983048 | tf_op jit(solution)/shard_map/ppermute | solution.py:62
  65.0 3.0 %fusion.19 = (f32[20,128]{1,0:T(8,128)S(1)}, f32[20,128]{1,0:T(8,128)S(1)}, f32[128,128]{1,0:T(8,128)S(1)}) fusion(f32[128,128]{1,0:T(8,128)S(1)} %fusion.86, f32[20,128]{1,0:T(8,128)S(1)} %bitcast.86, pred[128,128]{1,0:T(8,128)(4,1)S(1)} %iota_compare_fusion.6, f32[20,64,128]{2,1,0:T(8,128)S(1)} %bitcast.78, f32[128,20,64]{0,2,1:T(8,128)S(1)} %bitcast.74, ...), kind=kOutput, calls=%fused_computation.20 | convolution fusion | flops 255405056 | bytes 1499136 | tf_op jit(solution)/shard_map/transpose(jvp(hij,jhp->ihp))/dot_general | solution.py:167
  68.3 1.5 %collective-permute-start.14 = (f32[10,64,128]{2,1,0:T(8,128)S(1)}, f32[10,64,128]{2,1,0:T(8,128)S(1)}, u32[]{:S(2)}, u32[]{:S(2)}) collective-permute-start(f32[10,64,128]{2,1,0:T(8,128)S(1)} %get-tuple-element.26), channel_id=1, source_target_pairs={{12,4},{8,0},{13,5},{9,1},{14,6},{10,2},{15,7},{11,3}} | collective-permute-start | bytes 983048 | tf_op jit(solution)/shard_map/ppermute | solution.py:59
  69.8 1.2 %fusion.16 = f32[128,128]{1,0:T(8,128)S(1)} fusion(f32[128,128]{1,0:T(8,128)S(1)} %fusion.88, f32[128,20,64]{0,2,1:T(8,128)S(1)} %bitcast.79, f32[128,20]{0,1:T(8,128)S(1)} %get-tuple-element.52, f32[10,64,128]{2,1,0:T(8,128)S(1)} %get-tuple-element.51, f32[10,64,128]{2,1,0:T(8,128)S(1)} %copy-done.8, pred[]{:T(512)S(6)} %eq.27), kind=kOutput, calls=%fused_computation.15 | convolution fusion | flops 252329984 | bytes 1452033 | tf_op jit(solution)/shard_map/transpose(jvp(in,hpn->ihp))/dot_general | solution.py:174
  71.2 2.4 %fusion.12 = f32[128,20,64]{0,2,1:T(8,128)} fusion(f32[20,64,128]{2,1,0:T(8,128)S(1)} %bitcast.80, f32[128,128]{1,0:T(8,128)S(1)} %fusion.86, f32[20,128]{1,0:T(8,128)S(1)} %bitcast.87, pred[128,128]{1,0:T(8,128)(4,1)S(1)} %iota_compare_fusion.6), kind=kOutput, calls=%fused_computation.11 | convolution fusion | flops 252968960 | bytes 1402880 | tf_op jit(solution)/shard_map/transpose(jvp(hij,jhp->ihp))/dot_general | solution.py:167
  73.6 28.2 %collective-permute-done.14 = f32[10,64,128]{2,1,0:T(8,128)S(1)} collective-permute-done((f32[10,64,128]{2,1,0:T(8,128)S(1)}, f32[10,64,128]{2,1,0:T(8,128)S(1)}, u32[]{:S(2)}, u32[]{:S(2)}) %collective-permute-start.14) | collective-permute-done | bytes 327712 | tf_op jit(solution)/shard_map/ppermute | solution.py:59
  101.9 1.6 %collective-permute-start.15 = (f32[10,64,128]{2,1,0:T(8,128)S(1)}, f32[10,64,128]{2,1,0:T(8,128)S(1)}, u32[]{:S(2)}, u32[]{:S(2)}) collective-permute-start(f32[10,64,128]{2,1,0:T(8,128)S(1)} %get-tuple-element.48), channel_id=1, source_target_pairs={{28,24},{24,28},{20,16},{16,20},{12,8},{8,12},{4,0},{0,4},{29,25},... | collective-permute-start | bytes 983048 | tf_op jit(solution)/shard_map/ppermute | solution.py:82
  104.6 3.5 %collective-permute-done.19 = f32[128,128]{1,0:T(8,128)S(1)} collective-permute-done((f32[128,128]{1,0:T(8,128)S(1)}, f32[128,128]{1,0:T(8,128)S(1)}, u32[]{:S(2)}, u32[]{:S(2)}) %collective-permute-start.19) | collective-permute-done | bytes 65568 | tf_op jit(solution)/shard_map/ppermute | solution.py:94
  109.9 2.3 %multiply_reduce_fusion.2 = (f32[128,20]{0,1:T(8,128)S(1)}, f32[128,20]{0,1:T(8,128)S(1)}, f32[128,20]{0,1:T(8,128)S(1)}, f32[128,20,64]{0,2,1:T(8,128)S(1)}, f32[128,20]{0,1:T(8,128)S(1)}) fusion(f32[128,20,64]{0,2,1:T(8,128)S(1)} %bitcast.75, f32[128,20]{0,1:T(8,128)S(1)} %bitcast.92, f32[128,20]{0,1:T(8,128)S(1)} %get-tuple-element.53, ...), kind=kOutput, calls=%fused_computation.24 | convolution fusion | flops 254597120 | bytes 4059217 | tf_op jit(solution)/shard_map/transpose(jvp(jhp,jn->hpn))/dot_general | solution.py:186
  112.8 1.2 %fusion.15 = f32[128,128]{1,0:T(8,128)S(1)} fusion(f32[128,128]{1,0:T(8,128)S(1)} %fusion.87, f32[128,20,64]{0,2,1:T(8,128)S(1)} %bitcast.76, f32[128,20]{0,1:T(8,128)S(1)} %get-tuple-element.53, f32[128,20]{0,1:T(8,128)S(1)} %bitcast.93, f32[10,64,128]{2,1,0:T(8,128)S(1)} %get-tuple-element.49, f32[10,64,128]{2,1,0:T(8,128)S(1)} %copy-done.4, pred[]{:T(512)S(6)} %eq.31), kind=kOutput, calls=%fused_computation.14 | convolution fusion | flops 252493824 | bytes 1462273 | tf_op jit(solution)/shard_map/transpose(jvp(jhp,jn->hpn))/dot_general | solution.py:186
  116.9 1.1 copy.28
  117.9 1.7 %collective-permute-done.17 = f32[128,128]{1,0:T(8,128)S(1)} collective-permute-done((f32[128,128]{1,0:T(8,128)S(1)}, f32[128,128]{1,0:T(8,128)S(1)}, u32[]{:S(2)}, u32[]{:S(2)}) %collective-permute-start.17) | collective-permute-done | bytes 65568 | tf_op jit(solution)/shard_map/ppermute | solution.py:94
  (95 shorter events, 16.2 us)
Async XLA Ops:
  0.6 2.5 %copy-start = (f32[128,128]{1,0:T(8,128)S(1)}, f32[128,128]{1,0:T(8,128)}, u32[]{:S(2)}) copy-start(f32[128,128]{1,0:T(8,128)} %param.11) | copy-start | bytes 196612
  1.8 1.4 %copy-start.10 = (f32[20,128]{1,0:T(8,128)S(1)}, f32[20,128]{1,0:T(8,128)}, u32[]{:S(2)}) copy-start(f32[20,128]{1,0:T(8,128)} %param.13) | copy-start | bytes 30724
  3.9 15.0 %collective-permute-start.1 = (f32[10,64,128]{2,1,0:T(8,128)S(1)}, f32[10,64,128]{2,1,0:T(8,128)S(1)}, u32[]{:S(2)}, u32[]{:S(2)}) collective-permute-start(f32[10,64,128]{2,1,0:T(8,128)S(1)} %constant_dynamic-slice_fusion.1), channel_id=1, source_target_pairs={{0,4},{4,0},{8,12},{12,8},{16,20},{20,16},{24,28},{28,24},{1,5},{5... | collective-permute-start | bytes 983048 | tf_op jit(solution)/shard_map/ppermute | solution.py:42
  7.0 7.7 %collective-permute-start.10 = (f32[10]{0:T(128)S(1)}, f32[10]{0:T(128)S(1)}, u32[]{:S(2)}, u32[]{:S(2)}) collective-permute-start(f32[10]{0:T(128)S(1)} %dynamic_slice.29), channel_id=1, source_target_pairs={{28,24},{24,28},{20,16},{16,20},{12,8},{8,12},{4,0},{0,4},{29,25},... | collective-permute-start | bytes 128 | tf_op jit(solution)/shard_map/ppermute | solution.py:42
  14.7 2.3 %copy-start.12 = (f32[10]{0:T(128)}, f32[10]{0:T(128)S(1)}, u32[]{:S(2)}) copy-start(f32[10]{0:T(128)S(1)} %collective-permute-done.10) | copy-start | bytes 124
  15.3 3.5 %collective-permute-start = (f32[10]{0:T(128)S(1)}, f32[10]{0:T(128)S(1)}, u32[]{:S(2)}, u32[]{:S(2)}) collective-permute-start(f32[10]{0:T(128)S(1)} %get-tuple-element.54), channel_id=1, source_target_pairs={{0,4},{4,0},{8,12},{12,8},{16,20},{20,16},{24,28},{28,24},{1,5},{5... | collective-permute-start | bytes 128 | tf_op jit(solution)/shard_map/ppermute | solution.py:42
  19.0 8.6 %collective-permute-start.2 = (f32[10,64,128]{2,1,0:T(8,128)S(1)}, f32[10,64,128]{2,1,0:T(8,128)S(1)}, u32[]{:S(2)}, u32[]{:S(2)}) collective-permute-start(f32[10,64,128]{2,1,0:T(8,128)S(1)} %get-tuple-element.38), channel_id=1, source_target_pairs={{0,8},{4,12},{1,9},{5,13},{2,10},{6,14},{3,11},{7,15}} | collective-permute-start | bytes 983048 | tf_op jit(solution)/shard_map/ppermute | solution.py:62
  27.7 0.7 collective-permute-start.3
  28.5 0.7 collective-permute-start.4
  29.2 1.8 %copy-start.9 = (f32[128,128]{1,0:T(8,128)S(1)}, f32[128,128]{1,0:T(8,128)}, u32[]{:S(2)}) copy-start(f32[128,128]{1,0:T(8,128)} %param.12) | copy-start | bytes 196612
  29.4 7.1 %collective-permute-start.5 = (f32[10,64,128]{2,1,0:T(8,128)S(1)}, f32[10,64,128]{2,1,0:T(8,128)S(1)}, u32[]{:S(2)}, u32[]{:S(2)}) collective-permute-start(f32[10,64,128]{2,1,0:T(8,128)S(1)} %get-tuple-element.50), channel_id=1, source_target_pairs={{0,4},{4,0},{8,12},{12,8},{16,20},{20,16},{24,28},{28,24},{1,5},{5... | collective-permute-start | bytes 983048 | tf_op jit(solution)/shard_map/ppermute | solution.py:82
  40.8 1.4 %copy-start.1 = (f32[128,1280]{1,0:T(8,128)S(1)}, f32[128,1280]{1,0:T(8,128)}, u32[]{:S(2)}) copy-start(f32[128,1280]{1,0:T(8,128)} %param.10) | copy-start | bytes 1966084
  40.8 1.4 %copy-start.11 = (f32[1280]{0:T(1024)S(1)}, f32[1280]{0:T(1024)}, u32[]{:S(2)}) copy-start(f32[1280]{0:T(1024)} %param.16) | copy-start | bytes 15364
  42.2 7.8 %copy-start.2 = (f32[128,1280]{1,0:T(8,128)S(1)}, f32[128,1280]{1,0:T(8,128)}, u32[]{:S(2)}) copy-start(f32[128,1280]{1,0:T(8,128)} %param.17) | copy-start | bytes 1966084
  43.7 1.2 collective-permute-start.6
  43.8 2.6 %collective-permute-start.8 = (f32[128]{0:T(128)S(1)}, f32[128]{0:T(128)S(1)}, u32[]{:S(2)}, u32[]{:S(2)}) collective-permute-start(f32[128]{0:T(128)S(1)} %get-tuple-element.24), channel_id=1, source_target_pairs={{0,1},{1,0},{2,3},{3,2},{4,5},{5,4},{6,7},{7,6},{8,9},{9,8},{10,11... | collective-permute-start | bytes 1544 | tf_op jit(solution)/shard_map/ppermute | solution.py:94
  44.9 3.5 %collective-permute-start.7 = (f32[128]{0:T(128)S(1)}, f32[128]{0:T(128)S(1)}, u32[]{:S(2)}, u32[]{:S(2)}) collective-permute-start(f32[128]{0:T(128)S(1)} %add.147), channel_id=1, source_target_pairs={{0,2},{1,3},{2,0},{3,1},{4,6},{5,7},{6,4},{7,5},{8,10},{9,11},{10,... | collective-permute-start | bytes 1544 | tf_op jit(solution)/shard_map/ppermute | solution.py:94
  46.4 3.5 %collective-permute-start.9 = (f32[128]{0:T(128)S(1)}, f32[128]{0:T(128)S(1)}, u32[]{:S(2)}, u32[]{:S(2)}) collective-permute-start(f32[128]{0:T(128)S(1)} %add.151), channel_id=1, source_target_pairs={{0,2},{1,3},{2,0},{3,1},{4,6},{5,7},{6,4},{7,5},{8,10},{9,11},{10,... | collective-permute-start | bytes 1544 | tf_op jit(solution)/shard_map/ppermute | solution.py:94
  53.5 8.5 %collective-permute-start.11 = (f32[10,64,128]{2,1,0:T(8,128)S(1)}, f32[10,64,128]{2,1,0:T(8,128)S(1)}, u32[]{:S(2)}, u32[]{:S(2)}) collective-permute-start(f32[10,64,128]{2,1,0:T(8,128)S(1)} %constant_dynamic-slice_fusion), channel_id=1, source_target_pairs={{28,24},{24,28},{20,16},{16,20},{12,8},{8,12},{4,0},{0,4},{29,25},... | collective-permute-start | bytes 983048 | tf_op jit(solution)/shard_map/ppermute | solution.py:42
  62.8 1.4 %collective-permute-start.12 = (f32[10,64,128]{2,1,0:T(8,128)}, f32[10,64,128]{2,1,0:T(8,128)}, u32[]{:S(2)}, u32[]{:S(2)}) collective-permute-start(f32[10,64,128]{2,1,0:T(8,128)} %get-tuple-element.28), channel_id=1, source_target_pairs={{28,20},{24,16},{29,21},{25,17},{30,22},{26,18},{31,23},{27,19}} | collective-permute-start | bytes 983048 | tf_op jit(solution)/shard_map/ppermute | solution.py:62
  64.3 3.9 %collective-permute-start.13 = (f32[10,64,128]{2,1,0:T(8,128)S(1)}, f32[10,64,128]{2,1,0:T(8,128)S(1)}, u32[]{:S(2)}, u32[]{:S(2)}) collective-permute-start(f32[10,64,128]{2,1,0:T(8,128)S(1)} %multiply_add_fusion.3), channel_id=1, source_target_pairs={{20,12},{16,8},{21,13},{17,9},{22,14},{18,10},{23,15},{19,11}} | collective-permute-start | bytes 983048 | tf_op jit(solution)/shard_map/ppermute | solution.py:62
  68.2 1.6 %copy-start.8 = (f32[10,64,128]{2,1,0:T(8,128)S(1)}, f32[10,64,128]{2,1,0:T(8,128)}, u32[]{:S(2)}) copy-start(f32[10,64,128]{2,1,0:T(8,128)} %copy-done.7) | copy-start | bytes 983044
  68.3 33.4 %collective-permute-start.14 = (f32[10,64,128]{2,1,0:T(8,128)S(1)}, f32[10,64,128]{2,1,0:T(8,128)S(1)}, u32[]{:S(2)}, u32[]{:S(2)}) collective-permute-start(f32[10,64,128]{2,1,0:T(8,128)S(1)} %get-tuple-element.26), channel_id=1, source_target_pairs={{12,4},{8,0},{13,5},{9,1},{14,6},{10,2},{15,7},{11,3}} | collective-permute-start | bytes 983048 | tf_op jit(solution)/shard_map/ppermute | solution.py:59
  71.0 30.7 %copy-start.6 = (f32[10,64,128]{2,1,0:T(8,128)S(1)}, f32[10,64,128]{2,1,0:T(8,128)}, u32[]{:S(2)}) copy-start(f32[10,64,128]{2,1,0:T(8,128)} %copy-done.5) | copy-start | bytes 983044
  71.1 30.7 %copy-start.13 = (f32[10]{0:T(128)S(1)}, f32[10]{0:T(128)}, u32[]{:S(2)}) copy-start(f32[10]{0:T(128)} %copy-done.12) | copy-start | bytes 124
  71.1 30.7 %copy-start.14 = (f32[10]{0:T(128)S(1)}, f32[10]{0:T(128)}, u32[]{:S(2)}) copy-start(f32[10]{0:T(128)} %get-tuple-element.33) | copy-start | bytes 124
  71.1 32.7 %collective-permute-start.18 = (f32[128,128]{1,0:T(8,128)S(1)}, f32[128,128]{1,0:T(8,128)S(1)}, u32[]{:S(2)}, u32[]{:S(2)}) collective-permute-start(f32[128,128]{1,0:T(8,128)S(1)} %fusion.16), channel_id=1, source_target_pairs={{0,1},{1,0},{2,3},{3,2},{4,5},{5,4},{6,7},{7,6},{8,9},{9,8},{10,11... | collective-permute-start | bytes 196616 | tf_op jit(solution)/shard_map/ppermute | solution.py:94
  101.9 7.1 %collective-permute-start.15 = (f32[10,64,128]{2,1,0:T(8,128)S(1)}, f32[10,64,128]{2,1,0:T(8,128)S(1)}, u32[]{:S(2)}, u32[]{:S(2)}) collective-permute-start(f32[10,64,128]{2,1,0:T(8,128)S(1)} %get-tuple-element.48), channel_id=1, source_target_pairs={{28,24},{24,28},{20,16},{16,20},{12,8},{8,12},{4,0},{0,4},{29,25},... | collective-permute-start | bytes 983048 | tf_op jit(solution)/shard_map/ppermute | solution.py:82
  103.8 4.3 %collective-permute-start.19 = (f32[128,128]{1,0:T(8,128)S(1)}, f32[128,128]{1,0:T(8,128)S(1)}, u32[]{:S(2)}, u32[]{:S(2)}) collective-permute-start(f32[128,128]{1,0:T(8,128)S(1)} %add.169), channel_id=1, source_target_pairs={{0,2},{1,3},{2,0},{3,1},{4,6},{5,7},{6,4},{7,5},{8,10},{9,11},{10,... | collective-permute-start | bytes 196616 | tf_op jit(solution)/shard_map/ppermute | solution.py:94
  109.9 2.8 %copy-start.4 = (f32[10,64,128]{2,1,0:T(8,128)S(1)}, f32[10,64,128]{2,1,0:T(8,128)}, u32[]{:S(2)}) copy-start(f32[10,64,128]{2,1,0:T(8,128)} %copy-done.3) | copy-start | bytes 983044
  114.0 1.3 %collective-permute-start.16 = (f32[128,128]{1,0:T(8,128)S(1)}, f32[128,128]{1,0:T(8,128)S(1)}, u32[]{:S(2)}, u32[]{:S(2)}) collective-permute-start(f32[128,128]{1,0:T(8,128)S(1)} %fusion.15), channel_id=1, source_target_pairs={{0,1},{1,0},{2,3},{3,2},{4,5},{5,4},{6,7},{7,6},{8,9},{9,8},{10,11... | collective-permute-start | bytes 196616 | tf_op jit(solution)/shard_map/ppermute | solution.py:94
  115.3 4.3 %collective-permute-start.17 = (f32[128,128]{1,0:T(8,128)S(1)}, f32[128,128]{1,0:T(8,128)S(1)}, u32[]{:S(2)}, u32[]{:S(2)}) collective-permute-start(f32[128,128]{1,0:T(8,128)S(1)} %add.166), channel_id=1, source_target_pairs={{0,2},{1,3},{2,0},{3,1},{4,6},{5,7},{6,4},{7,5},{8,10},{9,11},{10,... | collective-permute-start | bytes 196616 | tf_op jit(solution)/shard_map/ppermute | solution.py:94
  (5 other events, 3.9 us)

commit v5 on v4

--- a/solution.py
+++ b/solution.py
@@ -14,7 +14,7 @@
     return (earlier[0] * later[0], later[0][:, None, None] * earlier[1] + later[1])
 
 
-def pair_scan(decay, state, axis, reverse):
+def pair_scan(decay, state, axis, reverse, tie=None, during=None):
     count = lax.axis_size(axis)
     if count == 1:
         return jnp.zeros_like(state)
@@ -40,6 +40,11 @@
     a_snd, s_snd = part(decay, send_start), part(state, send_start)
     swap = [(phys(u), phys(u ^ 1)) for u in range(count)]
     a_rcv, s_rcv = lax.ppermute((a_snd, s_snd), axis, swap)
+    tie_at = groups - 3 if groups <= 4 else -1
+    extra = None
+    if tie is not None and tie_at < 0:
+        s_rcv, tie = lax.optimization_barrier((s_rcv, tie))
+        extra = during(tie)
     lead = (jnp.where(first, a_own, a_rcv), jnp.where(first, s_own, s_rcv))
     trail = (jnp.where(first, a_rcv, a_own), jnp.where(first, s_rcv, s_own))
     a_tot, s_tot = combine(lead, trail)
@@ -60,6 +65,9 @@
                 a_in = a_g
             else:
                 a_in, s_in = lax.ppermute(out, axis, pairs)
+            if tie is not None and r == tie_at:
+                s_in, tie = lax.optimization_barrier((s_in, tie))
+                extra = during(tie)
             dst = group == r + 1
             a_g = jnp.where(dst, a_in, a_g)
             s_g = jnp.where(dst, s_in, s_g)
@@ -79,10 +87,15 @@
     with_lead_rcv = a_rcv[:, None, None] * s_g + s_rcv
     send = jnp.where(first, with_lead_own, s_g)
     keep = jnp.where(first, s_g, with_lead_rcv)
+    if tie is not None:
+        if extra is None:
+            extra = during(tie)
+        send, extra = lax.optimization_barrier((send, extra))
     other = lax.ppermute(send, axis, swap)
-    return jnp.where(
+    result = jnp.where(
         first, jnp.concatenate([other, keep], 0), jnp.concatenate([keep, other], 0)
     )
+    return result if tie is None else (result, extra)
 
 
 def butterfly_psum(parts, axis):
@@ -213,18 +226,22 @@
     to_end = jnp.exp(cumul[:, -1:] - cumul)
     weighted_in = scaled * jnp.transpose(to_end)[:, :, None]
     local_state = jnp.einsum("jhp,jn->hpn", weighted_in, write_keys, precision=highest)
-    state_in = pair_scan(decay_total, local_state, "seq", False)
     single = length == BLOCK
     if single:
-        mixed_w, pull_w = jax.vjp(
-            lambda f, s, d, w, r: within_part(f, s, d, w, r, skip_scale),
-            features, step_sizes, log_decay, write_keys, read_queries,
+        def within_vjp(args):
+            return jax.vjp(lambda f, s, d, w, r: within_part(f, s, d, w, r, skip_scale), *args)
+
+        state_in, (mixed_w, pull_w) = pair_scan(
+            decay_total, local_state, "seq", False,
+            tie=(features, step_sizes, log_decay, write_keys, read_queries),
+            during=within_vjp,
         )
         mixed_c, pull_c = jax.vjp(
             lambda d, r: carried_part(d, r, state_in), log_decay, read_queries
         )
         mixed_out = mixed_w + mixed_c
     else:
+        state_in = pair_scan(decay_total, local_state, "seq", False)
 
         def local_mixer(feat_in, step_in, decay_factors, writes, read_in):
             return run_mixer(
@@ -252,10 +269,11 @@
     from_start = jnp.transpose(jnp.exp(cumul))
     weighted_grad = grad_mixed.reshape(length, head_count, head_width) * from_start[:, :, None]
     local_grad = jnp.einsum("jhp,jn->hpn", weighted_grad, read_queries, precision=highest)
-    state_grad = pair_scan(decay_total, local_grad, "seq", True)
     if single:
-        gf_w, gs_w, gd_w, gw_w, gr_w = pull_w(grad_mixed)
-        gd_c, gr_c = pull_c(grad_mixed)
+        state_grad, ((gf_w, gs_w, gd_w, gw_w, gr_w), (gd_c, gr_c)) = pair_scan(
+            decay_total, local_grad, "seq", True, tie=grad_mixed,
+            during=lambda g: (pull_w(g), pull_c(g)),
+        )
         grad_read = butterfly_psum(gr_w + gr_c, "head")
         _, pull_e = jax.vjp(
             lambda f, s, d, w: end_part(f, s, d, w, state_in),
@@ -267,6 +285,7 @@
         grad_decay = gd_w + gd_c + gd_e
         grad_write = butterfly_psum(gw_w + gw_e, "head")
     else:
+        state_grad = pair_scan(decay_total, local_grad, "seq", True)
         grad_features, grad_steps, grad_decay, grad_write, grad_read = pullback(
             (state_grad, grad_mixed)
         )

time: 121 us -> 131 us (1.083)
  the two profiles are of different devices: /device:TPU:0 before, /device:TPU:8 now
where the time goes in v5:
time: 131 us
  waiting for transfers between devices  59.6 us (45%)
  matrix products  22.6 us (17%)
  other arithmetic  21.5 us (16%)
  starting transfers between devices  18.6 us (14%)
  local copies, waits for them, and re-layouts  7.19 us (5%)
  between operations  1.53 us (1%)
    ppermute x4, waiting for transfers between devices, pair_scan(): a_in, s_in = lax.ppermute(out, axis, pairs)  31.1 us
    ppermute x4, waiting for transfers between devices, pair_scan(): a_rcv, s_rcv = lax.ppermute((a_snd, s_snd), axis, swap)  13.8 us
    ppermute x8, waiting for transfers between devices, butterfly_psum(): got = lax.ppermute(parts, axis, [(i, i ^ k) for i in range(count)])  10.6 us
    dot_general x3, matrix products, within_part(): within = jnp.einsum('hij,jhp->ihp', masked, scaled, precision=highest)  8.44 us
    ppermute x4, starting transfers between devices, pair_scan(): a_rcv, s_rcv = lax.ppermute((a_snd, s_snd), axis, swap)  4.76 us
    add x6, other arithmetic, combine(): later[0][:, None, None] * earlier[1] + later[1]  4.7 us
    ppermute x4, starting transfers between devices, pair_scan(): a_in, s_in = lax.ppermute(out, axis, pairs)  4.68 us
    dot_general x2, matrix products, state_update(): return jnp.einsum('jhp,jn->hpn', weighted_in, writes, precision=highest)  4.22 us
  transfers between devices with their start and end apart: 20, of which 13 were waited for; matrix products, arithmetic and copies ran while one was open for 22% of the time, Pallas kernels for 0%

profile of v5, /device:TPU:8, one launch (start us, length us, event | category | flops | bytes accessed | tf_op | source)
XLA Modules:
  0.0 130.9 jit_solution(4371337560320315645)
XLA Ops:
  1.9 1.5 %collective-permute-start = (f32[10]{0:T(128)S(1)}, f32[10]{0:T(128)S(1)}, u32[]{:S(2)}, u32[]{:S(2)}) collective-permute-start(f32[10]{0:T(128)S(1)} %dynamic_slice.25), channel_id=1, source_target_pairs={{28,24},{24,28},{20,16},{16,20},{12,8},{8,12},{4,0},{0,4},{29,25},... | collective-permute-start | bytes 128 | tf_op jit(solution)/shard_map/ppermute | solution.py:42
  4.0 1.3 %copy.25 = f32[128,1280]{0,1:T(8,128)S(1)} copy(f32[128,1280]{1,0:T(8,128)} %param.9) | data formatting | bytes 1310720 | tf_op args[0]
  7.3 1.5 %collective-permute-start.1 = (f32[10]{0:T(128)S(1)}, f32[10]{0:T(128)S(1)}, u32[]{:S(2)}, u32[]{:S(2)}) collective-permute-start(f32[10]{0:T(128)S(1)} %get-tuple-element.109), channel_id=1, source_target_pairs={{0,4},{4,0},{8,12},{12,8},{16,20},{20,16},{24,28},{28,24},{1,5},{5... | collective-permute-start | bytes 128 | tf_op jit(solution)/shard_map/ppermute | solution.py:42
  8.8 6.6 %collective-permute-done.1 = f32[10]{0:T(128)S(1)} collective-permute-done((f32[10]{0:T(128)S(1)}, f32[10]{0:T(128)S(1)}, u32[]{:S(2)}, u32[]{:S(2)}) %collective-permute-start.1) | collective-permute-done | bytes 72 | tf_op jit(solution)/shard_map/ppermute | solution.py:42
  16.2 1.3 collective-permute-start.3
  17.5 8.8 %collective-permute-done.3 = f32[10,64,128]{2,1,0:T(8,128)S(1)} collective-permute-done((f32[10,64,128]{2,1,0:T(8,128)S(1)}, f32[10,64,128]{2,1,0:T(8,128)S(1)}, u32[]{:S(2)}, u32[]{:S(2)}) %collective-permute-start.3) | collective-permute-done | bytes 327712 | tf_op jit(solution)/shard_map/ppermute | solution.py:67
  26.4 1.4 %collective-permute-start.4 = (f32[10,64,128]{2,1,0:T(8,128)S(1)}, f32[10,64,128]{2,1,0:T(8,128)S(1)}, u32[]{:S(2)}, u32[]{:S(2)}) collective-permute-start(f32[10,64,128]{2,1,0:T(8,128)S(1)} %multiply_add_fusion.4), channel_id=1, source_target_pairs={{8,16},{12,20},{9,17},{13,21},{10,18},{14,22},{11,19},{15,23}} | collective-permute-start | bytes 983048 | tf_op jit(solution)/shard_map/ppermute | solution.py:67
  27.9 5.0 %collective-permute-done.4 = f32[10,64,128]{2,1,0:T(8,128)S(1)} collective-permute-done((f32[10,64,128]{2,1,0:T(8,128)S(1)}, f32[10,64,128]{2,1,0:T(8,128)S(1)}, u32[]{:S(2)}, u32[]{:S(2)}) %collective-permute-start.4) | collective-permute-done | bytes 327712 | tf_op jit(solution)/shard_map/ppermute | solution.py:67
  35.2 3.5 %fusion = f32[128,20,64]{0,2,1:T(8,128)} fusion(f32[128,20,64]{0,2,1:T(8,128)S(1)} %bitcast.90, f32[128,128]{1,0:T(8,128)S(1)} %fusion.55, pred[128,128]{1,0:T(8,128)(4,1)S(1)} %iota_compare_fusion, f32[20,128]{1,0:T(8,128)S(1)} %fusion.26, f32[20]{0:T(128)S(1)} %copy-done.49, f32[128,20]{0,1:T(8,128)S(1)} %bitcast.105), kind=kOutput, calls=%fused_computation.7 | convolution fusion | flops 253460480 | bytes 1413200 | tf_op jit(solution)/shard_map/jvp(hij,jhp->ihp)/dot_general | solution.py:180
  39.7 2.1 %broadcast_multiply_fusion = (f32[20,128,128]{2,1,0:T(8,128)}, f32[20,128,128]{2,1,0:T(8,128)S(1)}, f32[20,128,128]{2,1,0:T(8,128)}) fusion(f32[128,128]{1,0:T(8,128)S(1)} %fusion.55, f32[20,128]{1,0:T(8,128)S(1)} %copy-done.30, pred[128,128]{1,0:T(8,128)(4,1)S(1)} %copy-done.25), kind=kLoop, calls=%fused_computation.29 | loop fusion | flops 1310720 | bytes 4024320 | tf_op jit(solution)/shard_map/jvp()/mul | solution.py:179
  45.4 2.2 %copy.27 = f32[128,1280]{1,0:T(8,128)} copy(f32[128,1280]{0,1:T(8,128)} %bitcast.100) | data formatting | bytes 1310720 | tf_op jit(solution)/shard_map/optimization_barrier | solution.py:93
  47.5 4.0 %collective-permute-done.6 = f32[10,64,128]{2,1,0:T(8,128)S(1)} collective-permute-done((f32[10,64,128]{2,1,0:T(8,128)}, f32[10,64,128]{2,1,0:T(8,128)S(1)}, u32[]{:S(2)}, u32[]{:S(2)}) %collective-permute-start.6) | collective-permute-done | bytes 327712 | tf_op jit(solution)/shard_map/ppermute | solution.py:94
  51.6 2.2 %broadcast_multiply_fusion.2 = (f32[128,20,64]{0,2,1:T(8,128)S(1)}, f32[128,20,64]{0,2,1:T(8,128)}) fusion(f32[128,20]{0,1:T(8,128)} %get-tuple-element.107, f32[128,128]{1,0:T(8,128)S(1)} %copy-done, f32[10,64,128]{2,1,0:T(8,128)S(1)} %get-tuple-element.102, f32[10,64,128]{2,1,0:T(8,128)S(1)} %collective-permute-done.6, pred[]{:T(512)S(6)} %eq.31), kind=kOutput, calls=%fused_computation.45 | convolution fusion | flops 252313600 | bytes 2041857 | tf_op jit(solution)/shard_map/jvp(in,hpn->ihp)/dot_general | solution.py:187
  54.1 1.9 %multiply_reduce_fusion.7 = (f32[128]{0:T(128)S(1)}, f32[128]{0:T(128)S(1)}, f32[128,1280]{1,0:T(8,128)S(1)}) fusion(f32[128,1280]{1,0:T(8,128)} %param.10, f32[128,1280]{1,0:T(8,128)} %param.17, f32[1280]{0:T(1024)} %param.16, f32[128,1280]{1,0:T(8,128)} %copy.27, f32[128,1280]{1,0:T(8,128)S(1)} %copy.28), kind=kLoop, calls=%fused_computation.26 | loop fusion | flops 1801984 | bytes 3282944 | tf_op jit(solution)/shard_map/reduce_sum | solution.py:260
  57.2 1.5 %collective-permute-start.8 = (f32[128]{0:T(128)S(1)}, f32[128]{0:T(128)S(1)}, u32[]{:S(2)}, u32[]{:S(2)}) collective-permute-start(f32[128]{0:T(128)S(1)} %add.140), channel_id=1, source_target_pairs={{0,2},{1,3},{2,0},{3,1},{4,6},{5,7},{6,4},{7,5},{8,10},{9,11},{10,... | collective-permute-start | bytes 1544 | tf_op jit(solution)/shard_map/ppermute | solution.py:107
  59.2 1.5 %collective-permute-done.8 = f32[128]{0:T(128)S(1)} collective-permute-done((f32[128]{0:T(128)S(1)}, f32[128]{0:T(128)S(1)}, u32[]{:S(2)}, u32[]{:S(2)}) %collective-permute-start.8) | collective-permute-done | bytes 544 | tf_op jit(solution)/shard_map/ppermute | solution.py:107
  60.7 1.5 %collective-permute-done.10 = f32[128]{0:T(128)S(1)} collective-permute-done((f32[128]{0:T(128)S(1)}, f32[128]{0:T(128)S(1)}, u32[]{:S(2)}, u32[]{:S(2)}) %collective-permute-start.10) | collective-permute-done | bytes 544 | tf_op jit(solution)/shard_map/ppermute | solution.py:107
  63.8 1.4 %fusion.3 = f32[20,64,128]{2,1,0:T(8,128)S(1)} fusion(f32[128,20,64]{0,2,1:T(8,128)S(1)} %bitcast.97, f32[128,20]{0,1:T(8,128)} %get-tuple-element.107, f32[128,128]{1,0:T(8,128)S(1)} %copy-done), kind=kOutput, calls=%fused_computation.22 | convolution fusion | flops 251822080 | bytes 1386496 | tf_op jit(solution)/shard_map/jhp,jn->hpn/dot_general | solution.py:271
  66.4 7.3 %collective-permute-done.11 = f32[10,64,128]{2,1,0:T(8,128)S(1)} collective-permute-done((f32[10,64,128]{2,1,0:T(8,128)S(1)}, f32[10,64,128]{2,1,0:T(8,128)S(1)}, u32[]{:S(2)}, u32[]{:S(2)}) %collective-permute-start.11) | collective-permute-done | bytes 327712 | tf_op jit(solution)/shard_map/ppermute | solution.py:42
  76.1 1.3 collective-permute-start.13
  77.4 17.3 %collective-permute-done.13 = f32[10,64,128]{2,1,0:T(8,128)} collective-permute-done((f32[10,64,128]{2,1,0:T(8,128)}, f32[10,64,128]{2,1,0:T(8,128)}, u32[]{:S(2)}, u32[]{:S(2)}) %collective-permute-start.13) | collective-permute-done | bytes 327712 | tf_op jit(solution)/shard_map/ppermute | solution.py:67
  94.7 1.9 %multiply_add_fusion.1 = (f32[10,64,128]{2,1,0:T(8,128)}, f32[10,64,128]{2,1,0:T(8,128)}) fusion(f32[10,64,128]{2,1,0:T(8,128)S(1)} %get-tuple-element.78, f32[10]{0:T(128)S(1)} %get-tuple-element.80, f32[10,64,128]{2,1,0:T(8,128)} %collective-permute-done.13, f32[10,64,128]{2,1,0:T(8,128)S(1)} %collective-permute-done.12, pred[]{:T(512)S(6)} %eq.30, pred[]{:T(512)S(6)} %eq.29), kind=kLoop, calls=%fused_computation.39 | loop fusion | flops 327680 | bytes 1638442 | tf_op jit(solution)/shard_map/add | solution.py:14
  96.6 2.0 %collective-permute-start.14 = (f32[10,64,128]{2,1,0:T(8,128)}, f32[10,64,128]{2,1,0:T(8,128)}, u32[]{:S(2)}, u32[]{:S(2)}) collective-permute-start(f32[10,64,128]{2,1,0:T(8,128)} %get-tuple-element.75), channel_id=1, source_target_pairs={{12,4},{8,0},{13,5},{9,1},{14,6},{10,2},{15,7},{11,3}} | collective-permute-start | bytes 983048 | tf_op jit(solution)/shard_map/ppermute | solution.py:64
  98.9 2.6 %convolution_bitcast_fusion.2 = f32[128,20,64]{0,2,1:T(8,128)S(1)} fusion(f32[20,64,128]{2,1,0:T(8,128)S(1)} %bitcast.86, f32[20,128,128]{2,1,0:T(8,128)} %get-tuple-element.48), kind=kOutput, calls=%fused_computation.5 | convolution fusion | flops 251658240 | bytes 2621440 | tf_op jit(solution)/shard_map/transpose(jvp(hij,jhp->ihp))/dot_general | solution.py:180
  101.6 1.7 %multiply_reduce_fusion.4 = (f32[128,20]{0,1:T(8,128)S(1)}, f32[128,20,64]{0,2,1:T(8,128)}, f32[128,20]{0,1:T(8,128)}) fusion(f32[128,20,64]{0,2,1:T(8,128)S(1)} %copy-done.10, f32[128,20,64]{0,2,1:T(8,128)S(1)} %bitcast.87, f32[128,20,64]{0,2,1:T(8,128)S(1)} %convolution_bitcast_fusion.2, f32[128,20]{0,1:T(8,128)S(1)} %bitcast.107, f32[20]{0:T(128)S(1)} %copy-done.50, ...), kind=kLoop, calls=%fused_computation.19 | loop fusion | flops 1141760 | bytes 3307600 | tf_op jit(solution)/shard_map/transpose(jvp())/reduce_sum | solution.py:188
  104.1 2.3 %fusion.56 = f32[20,128,128]{2,1,0:T(8,128)S(1)} fusion(f32[20,64,128]{2,1,0:T(8,128)S(1)} %bitcast.88, f32[128,20,64]{0,2,1:T(8,128)S(1)} %copy-done.6), kind=kOutput, calls=%fused_computation.116 | convolution fusion | flops 251658240 | bytes 2621440 | tf_op jit(solution)/shard_map/transpose(jvp(hij,jhp->ihp))/dot_general | solution.py:180
  113.3 3.5 %collective-permute-done.19 = f32[128,128]{1,0:T(8,128)} collective-permute-done((f32[128,128]{1,0:T(8,128)S(1)}, f32[128,128]{1,0:T(8,128)}, u32[]{:S(2)}, u32[]{:S(2)}) %collective-permute-start.19) | collective-permute-done | bytes 65568 | tf_op jit(solution)/shard_map/ppermute | solution.py:107
  116.8 1.5 %add.159 = f32[128,128]{1,0:T(8,128)} add(f32[128,128]{1,0:T(8,128)S(1)} %add.158, f32[128,128]{1,0:T(8,128)} %collective-permute-done.19) | non-fusion elementwise | flops 16384 | bytes 196608 | tf_op jit(solution)/shard_map/add | solution.py:108
  118.3 1.3 %multiply_reduce_fusion.1 = f32[20]{0:T(128)S(1)} fusion(f32[10,64,128]{2,1,0:T(8,128)} %collective-permute-done.15, f32[10,64,128]{2,1,0:T(8,128)S(1)} %get-tuple-element.97, pred[]{:T(512)S(6)} %eq.27, f32[10,64,128]{2,1,0:T(8,128)S(1)} %copy-done.19, f32[10,64,128]{2,1,0:T(8,128)S(1)} %copy-done.5, pred[]{:T(512)S(6)} %eq.31), kind=kLoop, calls=%fused_computation.14 | loop fusion | flops 1310700 | bytes 1310802 | tf_op jit(solution)/shard_map/transpose(jvp())/reduce_sum | solution.py:204
  119.8 1.9 %multiply_reduce_fusion.2 = (f32[128,20]{0,1:T(8,128)S(1)}, f32[128,20]{0,1:T(8,128)S(1)}, f32[128,20,64]{0,2,1:T(8,128)S(1)}) fusion(f32[128,20,64]{0,2,1:T(8,128)S(1)} %bitcast.94, f32[128,20]{0,1:T(8,128)S(1)} %bitcast.108, f32[128,20]{0,1:T(8,128)S(1)} %copy-done.33, f32[128,128]{1,0:T(8,128)S(1)} %copy-done.22, ...), kind=kOutput, calls=%fused_computation.15 | convolution fusion | flops 253291520 | bytes 2072577 | tf_op jit(solution)/shard_map/transpose(jvp(jhp,jn->hpn))/dot_general | solution.py:199
  122.2 2.3 %convolution_bitcast_fusion.4 = f32[128,128]{1,0:T(8,128)S(1)} fusion(f32[128,20,64]{0,2,1:T(8,128)S(1)} %bitcast.95, f32[128,20]{0,1:T(8,128)S(1)} %copy-done.33, f32[128,20]{0,1:T(8,128)S(1)} %bitcast.109, f32[10,64,128]{2,1,0:T(8,128)S(1)} %get-tuple-element.97, f32[10,64,128]{2,1,0:T(8,128)} %collective-permute-done.15, pred[]{:T(512)S(6)} %eq.27), kind=kOutput, calls=%fused_computation.8 | convolution fusion | flops 252477440 | bytes 1396737 | tf_op jit(solution)/shard_map/transpose(jvp(jhp,jn->hpn))/dot_general | solution.py:199
  128.4 1.9 %collective-permute-done.17 = f32[128,128]{1,0:T(8,128)S(1)} collective-permute-done((f32[128,128]{1,0:T(8,128)S(1)}, f32[128,128]{1,0:T(8,128)S(1)}, u32[]{:S(2)}, u32[]{:S(2)}) %collective-permute-start.17) | collective-permute-done | bytes 65568 | tf_op jit(solution)/shard_map/ppermute | solution.py:107
  (177 shorter events, 31.4 us)
Async XLA Ops:
  0.6 34.2 %copy-start = (f32[128,128]{1,0:T(8,128)S(1)}, f32[128,128]{1,0:T(8,128)}, u32[]{:S(2)}) copy-start(f32[128,128]{1,0:T(8,128)} %param.12) | copy-start | bytes 196612
  1.9 4.8 %collective-permute-start = (f32[10]{0:T(128)S(1)}, f32[10]{0:T(128)S(1)}, u32[]{:S(2)}, u32[]{:S(2)}) collective-permute-start(f32[10]{0:T(128)S(1)} %dynamic_slice.25), channel_id=1, source_target_pairs={{28,24},{24,28},{20,16},{16,20},{12,8},{8,12},{4,0},{0,4},{29,25},... | collective-permute-start | bytes 128 | tf_op jit(solution)/shard_map/ppermute | solution.py:42
  5.3 10.8 %copy-start.8 = (f32[128,1280]{0,1:T(8,128)}, f32[128,1280]{0,1:T(8,128)S(1)}, u32[]{:S(2)}) copy-start(f32[128,1280]{0,1:T(8,128)S(1)} %copy.25) | copy-start | bytes 1966084
  6.1 26.8 %copy-start.35 = (f32[20,128]{1,0:T(8,128)S(1)}, f32[20,128]{1,0:T(8,128)}, u32[]{:S(2)}) copy-start(f32[20,128]{1,0:T(8,128)} %param.14) | copy-start | bytes 30724
  6.1 10.0 %collective-permute-start.2 = (f32[10,64,128]{2,1,0:T(8,128)S(1)}, f32[10,64,128]{2,1,0:T(8,128)S(1)}, u32[]{:S(2)}, u32[]{:S(2)}) collective-permute-start(f32[10,64,128]{2,1,0:T(8,128)S(1)} %constant_dynamic-slice_fusion.1), channel_id=1, source_target_pairs={{0,4},{4,0},{8,12},{12,8},{16,20},{20,16},{24,28},{28,24},{1,5},{5... | collective-permute-start | bytes 983048 | tf_op jit(solution)/shard_map/ppermute | solution.py:42
  7.3 8.0 %collective-permute-start.1 = (f32[10]{0:T(128)S(1)}, f32[10]{0:T(128)S(1)}, u32[]{:S(2)}, u32[]{:S(2)}) collective-permute-start(f32[10]{0:T(128)S(1)} %get-tuple-element.109), channel_id=1, source_target_pairs={{0,4},{4,0},{8,12},{12,8},{16,20},{20,16},{24,28},{28,24},{1,5},{5... | collective-permute-start | bytes 128 | tf_op jit(solution)/shard_map/ppermute | solution.py:42
  15.4 18.6 %copy-start.46 = (f32[10]{0:T(128)}, f32[10]{0:T(128)S(1)}, u32[]{:S(2)}) copy-start(f32[10]{0:T(128)S(1)} %collective-permute-done.1) | copy-start | bytes 124
  16.2 10.1 %collective-permute-start.3 = (f32[10,64,128]{2,1,0:T(8,128)S(1)}, f32[10,64,128]{2,1,0:T(8,128)S(1)}, u32[]{:S(2)}, u32[]{:S(2)}) collective-permute-start(f32[10,64,128]{2,1,0:T(8,128)S(1)} %get-tuple-element.88), channel_id=1, source_target_pairs={{0,8},{4,12},{1,9},{5,13},{2,10},{6,14},{3,11},{7,15}} | collective-permute-start | bytes 983048 | tf_op jit(solution)/shard_map/ppermute | solution.py:67
  26.3 8.4 %copy-start.7 = (f32[128,1280]{1,0:T(8,128)S(1)}, f32[128,1280]{1,0:T(8,128)}, u32[]{:S(2)}) copy-start(f32[128,1280]{1,0:T(8,128)} %param.9) | copy-start | bytes 1966084
  26.4 6.5 %collective-permute-start.4 = (f32[10,64,128]{2,1,0:T(8,128)S(1)}, f32[10,64,128]{2,1,0:T(8,128)S(1)}, u32[]{:S(2)}, u32[]{:S(2)}) collective-permute-start(f32[10,64,128]{2,1,0:T(8,128)S(1)} %multiply_add_fusion.4), channel_id=1, source_target_pairs={{8,16},{12,20},{9,17},{13,21},{10,18},{14,22},{11,19},{15,23}} | collective-permute-start | bytes 983048 | tf_op jit(solution)/shard_map/ppermute | solution.py:67
  34.0 7.8 %collective-permute-start.5 = (f32[10,64,128]{2,1,0:T(8,128)}, f32[10,64,128]{2,1,0:T(8,128)S(1)}, u32[]{:S(2)}, u32[]{:S(2)}) collective-permute-start(f32[10,64,128]{2,1,0:T(8,128)} %get-tuple-element.86), channel_id=1, source_target_pairs={{16,24},{20,28},{17,25},{21,29},{18,26},{22,30},{19,27},{23,31}} | collective-permute-start | bytes 983048 | tf_op jit(solution)/shard_map/ppermute | solution.py:64
  43.4 10.4 %copy-start.4 = (f32[10,64,128]{2,1,0:T(8,128)}, f32[10,64,128]{2,1,0:T(8,128)S(1)}, u32[]{:S(2)}) copy-start(f32[10,64,128]{2,1,0:T(8,128)S(1)} %get-tuple-element.102) | copy-start | bytes 983044
  44.3 7.3 %collective-permute-start.6 = (f32[10,64,128]{2,1,0:T(8,128)}, f32[10,64,128]{2,1,0:T(8,128)S(1)}, u32[]{:S(2)}, u32[]{:S(2)}) collective-permute-start(f32[10,64,128]{2,1,0:T(8,128)} %get-tuple-element.44), channel_id=1, source_target_pairs={{0,4},{4,0},{8,12},{12,8},{16,20},{20,16},{24,28},{28,24},{1,5},{5... | collective-permute-start | bytes 983048 | tf_op jit(solution)/shard_map/ppermute | solution.py:94
  54.0 8.2 %copy-start.12 = (f32[128,1280]{1,0:T(8,128)S(1)}, f32[128,1280]{1,0:T(8,128)}, u32[]{:S(2)}) copy-start(f32[128,1280]{1,0:T(8,128)} %param.10) | copy-start | bytes 1966084
  54.0 8.2 %copy-start.13 = (f32[128,1280]{1,0:T(8,128)S(1)}, f32[128,1280]{1,0:T(8,128)}, u32[]{:S(2)}) copy-start(f32[128,1280]{1,0:T(8,128)} %param.17) | copy-start | bytes 1966084
  56.0 1.2 collective-permute-start.7
  56.1 2.6 %collective-permute-start.9 = (f32[128]{0:T(128)S(1)}, f32[128]{0:T(128)S(1)}, u32[]{:S(2)}, u32[]{:S(2)}) collective-permute-start(f32[128]{0:T(128)S(1)} %get-tuple-element.74), channel_id=1, source_target_pairs={{0,1},{1,0},{2,3},{3,2},{4,5},{5,4},{6,7},{7,6},{8,9},{9,8},{10,11... | collective-permute-start | bytes 1544 | tf_op jit(solution)/shard_map/ppermute | solution.py:107
  57.2 3.5 %collective-permute-start.8 = (f32[128]{0:T(128)S(1)}, f32[128]{0:T(128)S(1)}, u32[]{:S(2)}, u32[]{:S(2)}) collective-permute-start(f32[128]{0:T(128)S(1)} %add.140), channel_id=1, source_target_pairs={{0,2},{1,3},{2,0},{3,1},{4,6},{5,7},{6,4},{7,5},{8,10},{9,11},{10,... | collective-permute-start | bytes 1544 | tf_op jit(solution)/shard_map/ppermute | solution.py:107
  58.7 3.5 %collective-permute-start.10 = (f32[128]{0:T(128)S(1)}, f32[128]{0:T(128)S(1)}, u32[]{:S(2)}, u32[]{:S(2)}) collective-permute-start(f32[128]{0:T(128)S(1)} %add.144), channel_id=1, source_target_pairs={{0,2},{1,3},{2,0},{3,1},{4,6},{5,7},{6,4},{7,5},{8,10},{9,11},{10,... | collective-permute-start | bytes 1544 | tf_op jit(solution)/shard_map/ppermute | solution.py:107
  63.8 9.9 %copy-start.41 = (f32[10]{0:T(128)S(1)}, f32[10]{0:T(128)}, u32[]{:S(2)}) copy-start(f32[10]{0:T(128)} %get-tuple-element.79) | copy-start | bytes 124
  63.8 9.9 %copy-start.42 = (f32[10]{0:T(128)S(1)}, f32[10]{0:T(128)}, u32[]{:S(2)}) copy-start(f32[10]{0:T(128)} %get-tuple-element.81) | copy-start | bytes 124
  65.2 8.5 %copy-start.2 = (f32[20,64,128]{2,1,0:T(8,128)}, f32[20,64,128]{2,1,0:T(8,128)S(1)}, u32[]{:S(2)}) copy-start(f32[20,64,128]{2,1,0:T(8,128)S(1)} %fusion.3) | copy-start | bytes 1966084
  65.2 8.5 %collective-permute-start.11 = (f32[10,64,128]{2,1,0:T(8,128)S(1)}, f32[10,64,128]{2,1,0:T(8,128)S(1)}, u32[]{:S(2)}, u32[]{:S(2)}) collective-permute-start(f32[10,64,128]{2,1,0:T(8,128)S(1)} %constant_dynamic-slice_fusion), channel_id=1, source_target_pairs={{28,24},{24,28},{20,16},{16,20},{12,8},{8,12},{4,0},{0,4},{29,25},... | collective-permute-start | bytes 983048 | tf_op jit(solution)/shard_map/ppermute | solution.py:42
  74.6 0.7 collective-permute-start.12
  76.1 18.6 %collective-permute-start.13 = (f32[10,64,128]{2,1,0:T(8,128)}, f32[10,64,128]{2,1,0:T(8,128)}, u32[]{:S(2)}, u32[]{:S(2)}) collective-permute-start(f32[10,64,128]{2,1,0:T(8,128)} %multiply_add_fusion.2), channel_id=1, source_target_pairs={{20,12},{16,8},{21,13},{17,9},{22,14},{18,10},{23,15},{19,11}} | collective-permute-start | bytes 983048 | tf_op jit(solution)/shard_map/ppermute | solution.py:67
  96.6 13.0 %collective-permute-start.14 = (f32[10,64,128]{2,1,0:T(8,128)}, f32[10,64,128]{2,1,0:T(8,128)}, u32[]{:S(2)}, u32[]{:S(2)}) collective-permute-start(f32[10,64,128]{2,1,0:T(8,128)} %get-tuple-element.75), channel_id=1, source_target_pairs={{12,4},{8,0},{13,5},{9,1},{14,6},{10,2},{15,7},{11,3}} | collective-permute-start | bytes 983048 | tf_op jit(solution)/shard_map/ppermute | solution.py:64
  109.8 8.5 %copy-start.19 = (f32[10,64,128]{2,1,0:T(8,128)S(1)}, f32[10,64,128]{2,1,0:T(8,128)}, u32[]{:S(2)}) copy-start(f32[10,64,128]{2,1,0:T(8,128)} %copy-done.17) | copy-start | bytes 983044
  109.8 8.5 %collective-permute-start.15 = (f32[10,64,128]{2,1,0:T(8,128)S(1)}, f32[10,64,128]{2,1,0:T(8,128)}, u32[]{:S(2)}, u32[]{:S(2)}) collective-permute-start(f32[10,64,128]{2,1,0:T(8,128)S(1)} %get-tuple-element.61), channel_id=1, source_target_pairs={{28,24},{24,28},{20,16},{16,20},{12,8},{8,12},{4,0},{0,4},{29,25},... | collective-permute-start | bytes 983048 | tf_op jit(solution)/shard_map/ppermute | solution.py:94
  111.0 1.3 %collective-permute-start.18 = (f32[128,128]{1,0:T(8,128)S(1)}, f32[128,128]{1,0:T(8,128)S(1)}, u32[]{:S(2)}, u32[]{:S(2)}) collective-permute-start(f32[128,128]{1,0:T(8,128)S(1)} %add.157), channel_id=1, source_target_pairs={{0,1},{1,0},{2,3},{3,2},{4,5},{5,4},{6,7},{7,6},{8,9},{9,8},{10,11... | collective-permute-start | bytes 196616 | tf_op jit(solution)/shard_map/ppermute | solution.py:107
  112.3 4.4 %collective-permute-start.19 = (f32[128,128]{1,0:T(8,128)S(1)}, f32[128,128]{1,0:T(8,128)}, u32[]{:S(2)}, u32[]{:S(2)}) collective-permute-start(f32[128,128]{1,0:T(8,128)S(1)} %add.158), channel_id=1, source_target_pairs={{0,2},{1,3},{2,0},{3,1},{4,6},{5,7},{6,4},{7,5},{8,10},{9,11},{10,... | collective-permute-start | bytes 196616 | tf_op jit(solution)/shard_map/ppermute | solution.py:107
  124.6 1.3 %collective-permute-start.16 = (f32[128,128]{1,0:T(8,128)S(1)}, f32[128,128]{1,0:T(8,128)S(1)}, u32[]{:S(2)}, u32[]{:S(2)}) collective-permute-start(f32[128,128]{1,0:T(8,128)S(1)} %add.154), channel_id=1, source_target_pairs={{0,1},{1,0},{2,3},{3,2},{4,5},{5,4},{6,7},{7,6},{8,9},{9,8},{10,11... | collective-permute-start | bytes 196616 | tf_op jit(solution)/shard_map/ppermute | solution.py:107
  125.9 4.3 %collective-permute-start.17 = (f32[128,128]{1,0:T(8,128)S(1)}, f32[128,128]{1,0:T(8,128)S(1)}, u32[]{:S(2)}, u32[]{:S(2)}) collective-permute-start(f32[128,128]{1,0:T(8,128)S(1)} %add.155), channel_id=1, source_target_pairs={{0,2},{1,3},{2,0},{3,1},{4,6},{5,7},{6,4},{7,5},{8,10},{9,11},{10,... | collective-permute-start | bytes 196616 | tf_op jit(solution)/shard_map/ppermute | solution.py:107
  (39 other events, 109.8 us)

commit v6 on v4

--- a/solution.py
+++ b/solution.py
@@ -168,22 +168,27 @@
     return (within + skip_scale[None, :, None] * feat3).reshape(length, -1)
 
 
+def per_channel(factors, head_width):
+    return jnp.repeat(jnp.transpose(factors), head_width, axis=1)
+
+
 def carried_part(decay_in, read_in, state_in):
-    length = decay_in.shape[1]
-    cumul = prefix_sum(decay_in)
-    carried = jnp.einsum("in,hpn->ihp", read_in, state_in, precision=highest)
-    carried = carried * jnp.transpose(jnp.exp(cumul))[:, :, None]
-    return carried.reshape(length, -1)
+    head_width = state_in.shape[1]
+    flat = state_in.reshape(-1, state_in.shape[2])
+    carried = jnp.dot(read_in, jnp.transpose(flat), precision=highest)
+    return carried * per_channel(jnp.exp(prefix_sum(decay_in)), head_width)
 
 
 def state_update(feat_in, step_in, decay_in, writes):
     head_count, length = step_in.shape
     head_width = feat_in.shape[1] // head_count
     cumul = prefix_sum(decay_in)
-    scaled = feat_in.reshape(length, head_count, head_width) * jnp.transpose(step_in)[:, :, None]
     to_end = jnp.exp(cumul[:, -1:] - cumul)
-    weighted_in = scaled * jnp.transpose(to_end)[:, :, None]
-    return jnp.einsum("jhp,jn->hpn", weighted_in, writes, precision=highest)
+    weighted_in = feat_in * per_channel(step_in * to_end, head_width)
+    update = lax.dot_general(
+        weighted_in, writes, (((0,), (0,)), ((), ())), precision=highest
+    )
+    return update.reshape(head_count, head_width, writes.shape[1])
 
 
 def end_part(feat_in, step_in, decay_in, writes, state_in):
@@ -207,12 +212,7 @@
     channels = features.shape[1] * lax.axis_size("head")
     cumul = prefix_sum(log_decay)
     decay_total = jnp.exp(cumul[:, -1])
-    scaled = (
-        features.reshape(length, head_count, head_width) * jnp.transpose(step_sizes)[:, :, None]
-    )
-    to_end = jnp.exp(cumul[:, -1:] - cumul)
-    weighted_in = scaled * jnp.transpose(to_end)[:, :, None]
-    local_state = jnp.einsum("jhp,jn->hpn", weighted_in, write_keys, precision=highest)
+    local_state = state_update(features, step_sizes, log_decay, write_keys)
     state_in = pair_scan(decay_total, local_state, "seq", False)
     single = length == BLOCK
     if single:
@@ -240,7 +240,8 @@
     gated_out = mixed_out * active
     weighted = out_grad * norm_gain[None, :]
     square_sum, cross_sum = butterfly_psum(
-        (jnp.sum(gated_out * gated_out, axis=1), jnp.sum(weighted * gated_out, axis=1)), "head"
+        jnp.stack([jnp.sum(gated_out * gated_out, axis=1), jnp.sum(weighted * gated_out, axis=1)]),
+        "head",
     )
     inverse = lax.rsqrt(square_sum / channels + eps)
     grad_gated = (
@@ -249,9 +250,10 @@
     )
     grad_mixed = grad_gated * active
     grad_gate = grad_gated * mixed_out * sigmoid_gate * (1.0 + gate_pre * (1.0 - sigmoid_gate))
-    from_start = jnp.transpose(jnp.exp(cumul))
-    weighted_grad = grad_mixed.reshape(length, head_count, head_width) * from_start[:, :, None]
-    local_grad = jnp.einsum("jhp,jn->hpn", weighted_grad, read_queries, precision=highest)
+    weighted_grad = grad_mixed * per_channel(jnp.exp(cumul), head_width)
+    local_grad = lax.dot_general(
+        weighted_grad, read_queries, (((0,), (0,)), ((), ())), precision=highest
+    ).reshape(head_count, head_width, read_queries.shape[1])
     state_grad = pair_scan(decay_total, local_grad, "seq", True)
     if single:
         gf_w, gs_w, gd_w, gw_w, gr_w = pull_w(grad_mixed)

time: 121 us -> 121 us (level)
  waiting for transfers between devices: 64.2 us -> 54.4 us
  other arithmetic: 7.83 us -> 16.7 us
  local copies, waits for them, and re-layouts: 6.19 us -> 11 us
  starting transfers between devices: 22.3 us -> 20 us
  matrix products: 18.7 us -> 16.9 us
    unnamed x36 -> x53, local copies, waits for them, and re-layouts: 2.98 us -> 9.72 us
    ppermute x2, waiting for transfers between devices: 28.2 us -> 23.9 us  [pair_scan(): s_in = lax.ppermute(out[1], axis, pairs)]
    ppermute x8 -> x6, waiting for transfers between devices: 9.27 us -> 5.79 us  [butterfly_psum(): got = lax.ppermute(parts, axis, [(i, i ^ k) for i in range(count)])]
    select_n x0 -> x2, other arithmetic: none -> 2.08 us  [the longest x1 2.03 us: pair_scan(): keep = jnp.where(first, s_g, with_lead_rcv)]
    ppermute x2, starting transfers between devices: 3.13 us -> 1.12 us  [pair_scan(): other = lax.ppermute(send, axis, swap)]
    dot_general x3, matrix products: 8.92 us -> 7.27 us  [within_part(): within = jnp.einsum('hij,jhp->ihp', masked, scaled, precision=highest)]
    ppermute x2, waiting for transfers between devices: 5.56 us -> 3.98 us  [pair_scan(): other = lax.ppermute(send, axis, swap)]
    dot_general x6, matrix products: 6.78 us -> 5.32 us  [the longest x3 2.55 us: state_update(): lax.dot_general(weighted_in, writes, (((0,), (0,)), ((), ())), precision=...]
  transfers between devices with their start and end apart: 20 -> 18, of which waited for: 13 -> 10; matrix products, arithmetic and copies ran while one was open for 10% -> 22% of each run, Pallas kernels for 0% -> 0%
where the time goes in v6:
time: 121 us; the launch traced here: 120 us
  waiting for transfers between devices  54.4 us (45%)
  starting transfers between devices  20 us (17%)
  matrix products  16.9 us (14%)
  other arithmetic  16.7 us (14%)
  local copies, waits for them, and re-layouts  11 us (9%)
  between operations  1.23 us (1%)
    ppermute x2, waiting for transfers between devices, pair_scan(): s_in = lax.ppermute(out[1], axis, pairs)  23.9 us
    ppermute x4, waiting for transfers between devices, pair_scan(): a_rcv, s_rcv = lax.ppermute((a_snd, s_snd), axis, swap)  15 us
    unnamed x53, local copies, waits for them, and re-layouts  9.72 us
    dot_general x3, matrix products, within_part(): within = jnp.einsum('hij,jhp->ihp', masked, scaled, precision=highest)  7.27 us
    ppermute x6, waiting for transfers between devices, butterfly_psum(): got = lax.ppermute(parts, axis, [(i, i ^ k) for i in range(count)])  5.79 us
    ppermute x4, starting transfers between devices, pair_scan(): a_in, s_in = lax.ppermute(out, axis, pairs)  5.71 us
    ppermute x4, waiting for transfers between devices, pair_scan(): a_in, s_in = lax.ppermute(out, axis, pairs)  5.67 us
    ppermute x4, starting transfers between devices, pair_scan(): a_rcv, s_rcv = lax.ppermute((a_snd, s_snd), axis, swap)  5.53 us
  transfers between devices with their start and end apart: 18, of which 10 were waited for; matrix products, arithmetic and copies ran while one was open for 22% of the time, Pallas kernels for 0%

profile of v6, /device:TPU:0, one launch (start us, length us, event | category | flops | bytes accessed | tf_op | source)
XLA Modules:
  0.0 120.1 jit_solution(15594444282429943892)
XLA Ops:
  1.8 2.9 %collective-permute-start.8 = (f32[10]{0:T(128)S(1)}, f32[10]{0:T(128)S(1)}, u32[]{:S(2)}, u32[]{:S(2)}) collective-permute-start(f32[10]{0:T(128)S(1)} %dynamic_slice.29), channel_id=1, source_target_pairs={{28,24},{24,28},{20,16},{16,20},{12,8},{8,12},{4,0},{0,4},{29,25},... | collective-permute-start | bytes 128 | tf_op jit(solution)/shard_map/ppermute | solution.py:42
  5.6 1.3 %copy.26 = f32[128,1280]{0,1:T(8,128)S(1)} copy(f32[128,1280]{1,0:T(8,128)} %param.9) | data formatting | bytes 1310720 | tf_op args[0]
  9.2 2.0 %collective-permute-start = (f32[10]{0:T(128)S(1)}, f32[10]{0:T(128)S(1)}, u32[]{:S(2)}, u32[]{:S(2)}) collective-permute-start(f32[10]{0:T(128)S(1)} %get-tuple-element.56), channel_id=1, source_target_pairs={{0,4},{4,0},{8,12},{12,8},{16,20},{20,16},{24,28},{28,24},{1,5},{5... | collective-permute-start | bytes 128 | tf_op jit(solution)/shard_map/ppermute | solution.py:42
  11.1 6.6 %collective-permute-done = f32[10]{0:T(128)S(1)} collective-permute-done((f32[10]{0:T(128)S(1)}, f32[10]{0:T(128)S(1)}, u32[]{:S(2)}, u32[]{:S(2)}) %collective-permute-start) | collective-permute-done | bytes 72 | tf_op jit(solution)/shard_map/ppermute | solution.py:42
  18.6 3.5 %collective-permute-start.2 = (f32[10,64,128]{2,1,0:T(8,128)S(1)}, f32[10,64,128]{2,1,0:T(8,128)S(1)}, u32[]{:S(2)}, u32[]{:S(2)}) collective-permute-start(f32[10,64,128]{2,1,0:T(8,128)S(1)} %get-tuple-element.40), channel_id=1, source_target_pairs={{0,8},{4,12},{1,9},{5,13},{2,10},{6,14},{3,11},{7,15}} | collective-permute-start | bytes 983048 | tf_op jit(solution)/shard_map/ppermute | solution.py:62
  22.1 5.7 %collective-permute-done.2 = f32[10,64,128]{2,1,0:T(8,128)S(1)} collective-permute-done((f32[10,64,128]{2,1,0:T(8,128)S(1)}, f32[10,64,128]{2,1,0:T(8,128)S(1)}, u32[]{:S(2)}, u32[]{:S(2)}) %collective-permute-start.2) | collective-permute-done | bytes 327712 | tf_op jit(solution)/shard_map/ppermute | solution.py:62
  29.4 1.4 %collective-permute-start.4 = (f32[10,64,128]{2,1,0:T(8,128)}, f32[10,64,128]{2,1,0:T(8,128)}, u32[]{:S(2)}, u32[]{:S(2)}) collective-permute-start(f32[10,64,128]{2,1,0:T(8,128)} %get-tuple-element.38), channel_id=1, source_target_pairs={{16,24},{20,28},{17,25},{21,29},{18,26},{22,30},{19,27},{23,31}} | collective-permute-start | bytes 983048 | tf_op jit(solution)/shard_map/ppermute | solution.py:59
  30.8 1.3 %copy.29 = f32[128,1280]{0,1:T(8,128)S(1)} copy(f32[128,1280]{1,0:T(8,128)} %param.10) | data formatting | bytes 1310720 | tf_op args[1]
  32.1 1.3 %copy.30 = f32[128,1280]{0,1:T(8,128)S(1)} copy(f32[128,1280]{1,0:T(8,128)} %param.17) | data formatting | bytes 1310720 | tf_op args[8]
  33.8 1.2 %add_select_fusion.3 = (f32[10,64,128]{2,1,0:T(8,128)S(1)}, f32[10,64,128]{2,1,0:T(8,128)S(1)}) fusion(f32[20,64,128]{2,1,0:T(8,128)S(1)} %bitcast.114, s32[]{:T(128)S(6)} %select_n.171, f32[10]{0:T(128)S(1)} %get-tuple-element.45, pred[]{:T(512)S(6)} %eq.27, f32[10,64,128]{2,1,0:T(8,128)} %collective-permute-done.4, f32[10,64,128]{2,1,0:T(8,128)} %get-tuple-element.39, ...), kind=kLoop, calls=%fused_computation.55 | loop fusion | flops 573440 | bytes 1966166 | tf_op jit(solution)/shard_map/jit(_where)/select_n | solution.py:80
  35.6 2.7 %fusion.9 = f32[128,20,64]{0,2,1:T(8,128)S(1)} fusion(f32[128,20,64]{0,2,1:T(8,128)S(1)} %bitcast.102, f32[128,128]{1,0:T(8,128)S(1)} %fusion.69, f32[20,128]{1,0:T(8,128)S(1)} %bitcast.121, pred[128,128]{1,0:T(8,128)(4,1)S(1)} %iota_compare_fusion.6, f32[128,20]{0,1:T(8,128)S(1)} %bitcast.125, f32[20]{0:T(128)S(1)} %copy-done.22), kind=kOutput, calls=%fused_computation.10 | convolution fusion | flops 253460480 | bytes 1413200 | tf_op jit(solution)/shard_map/jvp(hij,jhp->ihp)/dot_general | solution.py:167
  38.4 4.0 %collective-permute-done.5 = f32[10,64,128]{2,1,0:T(8,128)S(1)} collective-permute-done((f32[10,64,128]{2,1,0:T(8,128)S(1)}, f32[10,64,128]{2,1,0:T(8,128)S(1)}, u32[]{:S(2)}, u32[]{:S(2)}) %collective-permute-start.5) | collective-permute-done | bytes 327712 | tf_op jit(solution)/shard_map/ppermute | solution.py:82
  44.0 1.1 collective-permute-done.6
  45.2 1.6 %collective-permute-start.7 = (f32[2,128]{1,0:T(2,128)S(1)}, f32[2,128]{1,0:T(2,128)S(1)}, u32[]{:S(2)}, u32[]{:S(2)}) collective-permute-start(f32[2,128]{1,0:T(2,128)S(1)} %fusion.59), channel_id=1, source_target_pairs={{0,2},{1,3},{2,0},{3,1},{4,6},{5,7},{6,4},{7,5},{8,10},{9,11},{10,... | collective-permute-start | bytes 3080 | tf_op jit(solution)/shard_map/ppermute | solution.py:94
  46.7 2.0 %collective-permute-done.7 = f32[2,128]{1,0:T(2,128)S(1)} collective-permute-done((f32[2,128]{1,0:T(2,128)S(1)}, f32[2,128]{1,0:T(2,128)S(1)}, u32[]{:S(2)}, u32[]{:S(2)}) %collective-permute-start.7) | collective-permute-done | bytes 1056 | tf_op jit(solution)/shard_map/ppermute | solution.py:94
  48.8 2.6 %fusion.62 = (f32[128,1280]{0,1:T(8,128)}, f32[128,1280]{0,1:T(8,128)S(1)}, f32[128,1280]{0,1:T(8,128)}) fusion(f32[128,1280]{0,1:T(8,128)S(1)} %get-tuple-element.59, f32[128,1280]{0,1:T(8,128)S(1)} %copy.29, f32[128,1280]{0,1:T(8,128)S(1)} %get-tuple-element.37, f32[128]{0:T(128)S(1)} %fusion.53, f32[128,1280]{0,1:T(8,128)} %copy-done.1, ...), kind=kLoop, calls=%fused_computation.112 | loop fusion | flops 2949120 | bytes 5259264 | tf_op jit(solution)/shard_map/transpose(jvp())/mul | solution.py:179
  54.3 8.4 %collective-permute-done.9 = f32[10,64,128]{2,1,0:T(8,128)} collective-permute-done((f32[10,64,128]{2,1,0:T(8,128)}, f32[10,64,128]{2,1,0:T(8,128)}, u32[]{:S(2)}, u32[]{:S(2)}) %collective-permute-start.9) | collective-permute-done | bytes 327712 | tf_op jit(solution)/shard_map/ppermute | solution.py:42
  62.7 1.2 broadcast_add_fusion
  64.6 1.6 %fusion.12 = f32[128,20,64]{0,2,1:T(8,128)S(1)} fusion(f32[20,64,128]{2,1,0:T(8,128)S(1)} %bitcast.109, f32[128,128]{1,0:T(8,128)S(1)} %fusion.69, f32[20,128]{1,0:T(8,128)S(1)} %bitcast.122, pred[128,128]{1,0:T(8,128)(4,1)S(1)} %iota_compare_fusion.6), kind=kOutput, calls=%fused_computation.11 | convolution fusion | flops 252968960 | bytes 1402880 | tf_op jit(solution)/shard_map/transpose(jvp(hij,jhp->ihp))/dot_general | solution.py:167
  66.2 3.0 %fusion.17 = (f32[20,128]{1,0:T(8,128)S(1)}, f32[20,128]{1,0:T(8,128)S(1)}, f32[128,128]{1,0:T(8,128)S(1)}) fusion(f32[128,128]{1,0:T(8,128)S(1)} %fusion.69, f32[20,128]{1,0:T(8,128)S(1)} %bitcast.123, pred[128,128]{1,0:T(8,128)(4,1)S(1)} %iota_compare_fusion.6, f32[20,64,128]{2,1,0:T(8,128)S(1)} %bitcast.110, f32[128,20,64]{0,2,1:T(8,128)S(1)} %bitcast.103, ...), kind=kOutput, calls=%fused_computation.22 | convolution fusion | flops 255405056 | bytes 1499136 | tf_op jit(solution)/shard_map/transpose(jvp(hij,jhp->ihp))/dot_general | solution.py:167
  70.4 1.2 %convolution_add_fusion = f32[128,128]{1,0:T(8,128)S(1)} fusion(f32[128,128]{1,0:T(8,128)S(1)} %fusion.73, f32[128,1280]{0,1:T(8,128)S(1)} %bitcast_multiply_fusion, f32[1280,128]{1,0:T(8,128)S(1)} %bitcast.106), kind=kOutput, calls=%fused_computation.12 | convolution fusion | flops 251674624 | bytes 1441792 | tf_op jit(solution)/shard_map/transpose(jvp())/dot_general | solution.py:178
  71.7 1.3 %collective-permute-start.12 = (f32[10,64,128]{2,1,0:T(8,128)S(1)}, f32[10,64,128]{2,1,0:T(8,128)S(1)}, u32[]{:S(2)}, u32[]{:S(2)}) collective-permute-start(f32[10,64,128]{2,1,0:T(8,128)S(1)} %get-tuple-element.29), channel_id=1, source_target_pairs={{12,4},{8,0},{13,5},{9,1},{14,6},{10,2},{15,7},{11,3}} | collective-permute-start | bytes 983048 | tf_op jit(solution)/shard_map/ppermute | solution.py:59
  73.5 1.6 %multiply_reduce_fusion.2 = (f32[128,20]{0,1:T(8,128)}, f32[128,20,64]{0,2,1:T(8,128)}) fusion(f32[128,20,64]{0,2,1:T(8,128)S(1)} %bitcast.104, f32[128,20,64]{0,2,1:T(8,128)S(1)} %fusion.12, f32[128,20]{0,1:T(8,128)S(1)} %bitcast.127, f32[128,20,64]{0,2,1:T(8,128)S(1)} %bitcast.111, f32[20]{0:T(128)S(1)} %copy-done.23), kind=kLoop, calls=%fused_computation.28 | loop fusion | flops 816640 | bytes 2642000 | tf_op jit(solution)/shard_map/transpose(jvp())/reduce_sum | solution.py:165
  75.1 23.9 %collective-permute-done.12 = f32[10,64,128]{2,1,0:T(8,128)S(1)} collective-permute-done((f32[10,64,128]{2,1,0:T(8,128)S(1)}, f32[10,64,128]{2,1,0:T(8,128)S(1)}, u32[]{:S(2)}, u32[]{:S(2)}) %collective-permute-start.12) | collective-permute-done | bytes 327712 | tf_op jit(solution)/shard_map/ppermute | solution.py:59
  99.0 2.0 %add_select_fusion = (f32[10,64,128]{2,1,0:T(8,128)}, f32[10,64,128]{2,1,0:T(8,128)}) fusion(f32[10,64,128]{2,1,0:T(8,128)} %collective-permute-done.9, f32[10]{0:T(128)S(1)} %copy-done.20, pred[]{:T(512)S(6)} %eq.31, f32[10,64,128]{2,1,0:T(8,128)S(1)} %collective-permute-done.12, f32[10,64,128]{2,1,0:T(8,128)S(1)} %get-tuple-element.30, pred[]{:T(512)S(6)} %eq.32, ...), kind=kLoop, calls=%fused_computation.49 | loop fusion | flops 573440 | bytes 1966166 | tf_op jit(solution)/shard_map/jit(_where)/select_n | solution.py:81
  103.9 1.6 %collective-permute-start.17 = (f32[128,128]{1,0:T(8,128)S(1)}, f32[128,128]{1,0:T(8,128)S(1)}, u32[]{:S(2)}, u32[]{:S(2)}) collective-permute-start(f32[128,128]{1,0:T(8,128)S(1)} %add.158), channel_id=1, source_target_pairs={{0,2},{1,3},{2,0},{3,1},{4,6},{5,7},{6,4},{7,5},{8,10},{9,11},{10,... | collective-permute-start | bytes 196616 | tf_op jit(solution)/shard_map/ppermute | solution.py:94
  106.4 1.1 copy.36
  108.8 1.3 %multiply_reduce_fusion.1 = (f32[20]{0:T(128)S(1)}, f32[20,64,128]{2,1,0:T(8,128)S(1)}) fusion(f32[20,64,128]{2,1,0:T(8,128)S(1)} %maximum_select_fusion, f32[10,64,128]{2,1,0:T(8,128)} %collective-permute-done.13, f32[10,64,128]{2,1,0:T(8,128)S(1)} %copy-done.8, pred[]{:T(512)S(6)} %eq.31), kind=kLoop, calls=%fused_computation.27 | loop fusion | flops 819180 | bytes 1966161 | tf_op jit(solution)/shard_map/transpose(jvp())/reduce_sum | solution.py:196
  110.2 1.2 %convolution_add_fusion.1 = f32[128,128]{1,0:T(8,128)S(1)} fusion(f32[128,128]{1,0:T(8,128)S(1)} %fusion.72, f32[128,1280]{0,1:T(8,128)S(1)} %bitcast_multiply_fusion.3, f32[1280,128]{1,0:T(8,128)S(1)} %bitcast.107), kind=kOutput, calls=%fused_computation.13 | convolution fusion | flops 251674624 | bytes 1441792 | tf_op jit(solution)/shard_map/transpose(jvp())/dot_general | solution.py:188
  114.1 1.0 collective-permute-done.14
  115.2 1.6 %collective-permute-start.15 = (f32[128,128]{1,0:T(8,128)S(1)}, f32[128,128]{1,0:T(8,128)S(1)}, u32[]{:S(2)}, u32[]{:S(2)}) collective-permute-start(f32[128,128]{1,0:T(8,128)S(1)} %add.155), channel_id=1, source_target_pairs={{0,2},{1,3},{2,0},{3,1},{4,6},{5,7},{6,4},{7,5},{8,10},{9,11},{10,... | collective-permute-start | bytes 196616 | tf_op jit(solution)/shard_map/ppermute | solution.py:94
  117.6 1.1 copy.35
  (112 shorter events, 24.5 us)
Async XLA Ops:
  0.6 32.8 %copy-start = (f32[128,128]{1,0:T(8,128)S(1)}, f32[128,128]{1,0:T(8,128)}, u32[]{:S(2)}) copy-start(f32[128,128]{1,0:T(8,128)} %param.12) | copy-start | bytes 196612
  1.8 6.7 %collective-permute-start.8 = (f32[10]{0:T(128)S(1)}, f32[10]{0:T(128)S(1)}, u32[]{:S(2)}, u32[]{:S(2)}) collective-permute-start(f32[10]{0:T(128)S(1)} %dynamic_slice.29), channel_id=1, source_target_pairs={{28,24},{24,28},{20,16},{16,20},{12,8},{8,12},{4,0},{0,4},{29,25},... | collective-permute-start | bytes 128 | tf_op jit(solution)/shard_map/ppermute | solution.py:42
  8.5 9.4 %collective-permute-start.1 = (f32[10,64,128]{2,1,0:T(8,128)S(1)}, f32[10,64,128]{2,1,0:T(8,128)S(1)}, u32[]{:S(2)}, u32[]{:S(2)}) collective-permute-start(f32[10,64,128]{2,1,0:T(8,128)S(1)} %constant_dynamic-slice_fusion.1), channel_id=1, source_target_pairs={{0,4},{4,0},{8,12},{12,8},{16,20},{20,16},{24,28},{28,24},{1,5},{5... | collective-permute-start | bytes 983048 | tf_op jit(solution)/shard_map/ppermute | solution.py:42
  8.6 2.6 %copy-start.19 = (f32[10]{0:T(128)}, f32[10]{0:T(128)S(1)}, u32[]{:S(2)}) copy-start(f32[10]{0:T(128)S(1)} %collective-permute-done.8) | copy-start | bytes 124
  9.2 60.0 %copy-start.17 = (f32[10]{0:T(128)}, f32[10]{0:T(128)S(1)}, u32[]{:S(2)}) copy-start(f32[10]{0:T(128)S(1)} %get-tuple-element.34) | copy-start | bytes 124
  9.2 8.6 %collective-permute-start = (f32[10]{0:T(128)S(1)}, f32[10]{0:T(128)S(1)}, u32[]{:S(2)}, u32[]{:S(2)}) collective-permute-start(f32[10]{0:T(128)S(1)} %get-tuple-element.56), channel_id=1, source_target_pairs={{0,4},{4,0},{8,12},{12,8},{16,20},{20,16},{24,28},{28,24},{1,5},{5... | collective-permute-start | bytes 128 | tf_op jit(solution)/shard_map/ppermute | solution.py:42
  18.6 9.2 %collective-permute-start.2 = (f32[10,64,128]{2,1,0:T(8,128)S(1)}, f32[10,64,128]{2,1,0:T(8,128)S(1)}, u32[]{:S(2)}, u32[]{:S(2)}) collective-permute-start(f32[10,64,128]{2,1,0:T(8,128)S(1)} %get-tuple-element.40), channel_id=1, source_target_pairs={{0,8},{4,12},{1,9},{5,13},{2,10},{6,14},{3,11},{7,15}} | collective-permute-start | bytes 983048 | tf_op jit(solution)/shard_map/ppermute | solution.py:62
  27.8 0.7 collective-permute-start.3
  29.4 4.3 %collective-permute-start.4 = (f32[10,64,128]{2,1,0:T(8,128)}, f32[10,64,128]{2,1,0:T(8,128)}, u32[]{:S(2)}, u32[]{:S(2)}) collective-permute-start(f32[10,64,128]{2,1,0:T(8,128)} %get-tuple-element.38), channel_id=1, source_target_pairs={{16,24},{20,28},{17,25},{21,29},{18,26},{22,30},{19,27},{23,31}} | collective-permute-start | bytes 983048 | tf_op jit(solution)/shard_map/ppermute | solution.py:59
  33.4 8.9 %copy-start.1 = (f32[128,1280]{0,1:T(8,128)}, f32[128,1280]{0,1:T(8,128)S(1)}, u32[]{:S(2)}) copy-start(f32[128,1280]{0,1:T(8,128)S(1)} %copy.30) | copy-start | bytes 1966084
  33.7 1.9 %copy-start.12 = (f32[20,128]{1,0:T(8,128)S(1)}, f32[20,128]{1,0:T(8,128)}, u32[]{:S(2)}) copy-start(f32[20,128]{1,0:T(8,128)} %param.13) | copy-start | bytes 30724
  33.7 1.9 %copy-start.22 = (f32[20]{0:T(128)S(1)}, f32[20]{0:T(128)}, u32[]{:S(2)}) copy-start(f32[20]{0:T(128)} %param.15) | copy-start | bytes 244
  35.0 7.3 %collective-permute-start.5 = (f32[10,64,128]{2,1,0:T(8,128)S(1)}, f32[10,64,128]{2,1,0:T(8,128)S(1)}, u32[]{:S(2)}, u32[]{:S(2)}) collective-permute-start(f32[10,64,128]{2,1,0:T(8,128)S(1)} %get-tuple-element.53), channel_id=1, source_target_pairs={{0,4},{4,0},{8,12},{12,8},{16,20},{20,16},{24,28},{28,24},{1,5},{5... | collective-permute-start | bytes 983048 | tf_op jit(solution)/shard_map/ppermute | solution.py:82
  43.9 1.2 %collective-permute-start.6 = (f32[2,128]{1,0:T(2,128)S(1)}, f32[2,128]{1,0:T(2,128)S(1)}, u32[]{:S(2)}, u32[]{:S(2)}) collective-permute-start(f32[2,128]{1,0:T(2,128)S(1)} %pad_maximum_fusion), channel_id=1, source_target_pairs={{0,1},{1,0},{2,3},{3,2},{4,5},{5,4},{6,7},{7,6},{8,9},{9,8},{10,11... | collective-permute-start | bytes 3080 | tf_op jit(solution)/shard_map/ppermute | solution.py:94
  45.2 3.6 %collective-permute-start.7 = (f32[2,128]{1,0:T(2,128)S(1)}, f32[2,128]{1,0:T(2,128)S(1)}, u32[]{:S(2)}, u32[]{:S(2)}) collective-permute-start(f32[2,128]{1,0:T(2,128)S(1)} %fusion.59), channel_id=1, source_target_pairs={{0,2},{1,3},{2,0},{3,1},{4,6},{5,7},{6,4},{7,5},{8,10},{9,11},{10,... | collective-permute-start | bytes 3080 | tf_op jit(solution)/shard_map/ppermute | solution.py:94
  53.8 8.9 %collective-permute-start.9 = (f32[10,64,128]{2,1,0:T(8,128)}, f32[10,64,128]{2,1,0:T(8,128)}, u32[]{:S(2)}, u32[]{:S(2)}) collective-permute-start(f32[10,64,128]{2,1,0:T(8,128)} %constant_dynamic-slice_fusion), channel_id=1, source_target_pairs={{28,24},{24,28},{20,16},{16,20},{12,8},{8,12},{4,0},{0,4},{29,25},... | collective-permute-start | bytes 983048 | tf_op jit(solution)/shard_map/ppermute | solution.py:42
  63.9 5.2 %collective-permute-start.10 = (f32[10,64,128]{2,1,0:T(8,128)S(1)}, f32[10,64,128]{2,1,0:T(8,128)S(1)}, u32[]{:S(2)}, u32[]{:S(2)}) collective-permute-start(f32[10,64,128]{2,1,0:T(8,128)S(1)} %get-tuple-element.31), channel_id=1, source_target_pairs={{28,20},{24,16},{29,21},{25,17},{30,22},{26,18},{31,23},{27,19}} | collective-permute-start | bytes 983048 | tf_op jit(solution)/shard_map/ppermute | solution.py:62
  69.3 2.3 %collective-permute-start.11 = (f32[10,64,128]{2,1,0:T(8,128)S(1)}, f32[10,64,128]{2,1,0:T(8,128)S(1)}, u32[]{:S(2)}, u32[]{:S(2)}) collective-permute-start(f32[10,64,128]{2,1,0:T(8,128)S(1)} %multiply_add_fusion.2), channel_id=1, source_target_pairs={{20,12},{16,8},{21,13},{17,9},{22,14},{18,10},{23,15},{19,11}} | collective-permute-start | bytes 983048 | tf_op jit(solution)/shard_map/ppermute | solution.py:62
  71.6 1.8 %copy-start.13 = (f32[20,128]{1,0:T(8,128)S(1)}, f32[20,128]{1,0:T(8,128)}, u32[]{:S(2)}) copy-start(f32[20,128]{1,0:T(8,128)} %param.13) | copy-start | bytes 30724
  71.6 1.8 %copy-start.23 = (f32[20]{0:T(128)S(1)}, f32[20]{0:T(128)}, u32[]{:S(2)}) copy-start(f32[20]{0:T(128)} %param.15) | copy-start | bytes 244
  71.7 27.3 %collective-permute-start.12 = (f32[10,64,128]{2,1,0:T(8,128)S(1)}, f32[10,64,128]{2,1,0:T(8,128)S(1)}, u32[]{:S(2)}, u32[]{:S(2)}) collective-permute-start(f32[10,64,128]{2,1,0:T(8,128)S(1)} %get-tuple-element.29), channel_id=1, source_target_pairs={{12,4},{8,0},{13,5},{9,1},{14,6},{10,2},{15,7},{11,3}} | collective-permute-start | bytes 983048 | tf_op jit(solution)/shard_map/ppermute | solution.py:59
  73.3 29.7 %collective-permute-start.16 = (f32[128,128]{1,0:T(8,128)S(1)}, f32[128,128]{1,0:T(8,128)}, u32[]{:S(2)}, u32[]{:S(2)}) collective-permute-start(f32[128,128]{1,0:T(8,128)S(1)} %convolution_add_fusion), channel_id=1, source_target_pairs={{0,1},{1,0},{2,3},{3,2},{4,5},{5,4},{6,7},{7,6},{8,9},{9,8},{10,11... | collective-permute-start | bytes 196616 | tf_op jit(solution)/shard_map/ppermute | solution.py:94
  73.4 25.6 %copy-start.3 = (f32[1280,128]{1,0:T(8,128)S(1)}, f32[1280,128]{1,0:T(8,128)}, u32[]{:S(2)}) copy-start(f32[1280,128]{1,0:T(8,128)} %copy-done.2) | copy-start | bytes 1966084
  73.4 25.6 %copy-start.20 = (f32[10]{0:T(128)S(1)}, f32[10]{0:T(128)}, u32[]{:S(2)}) copy-start(f32[10]{0:T(128)} %copy-done.19) | copy-start | bytes 124
  73.4 25.6 %copy-start.21 = (f32[10]{0:T(128)S(1)}, f32[10]{0:T(128)}, u32[]{:S(2)}) copy-start(f32[10]{0:T(128)} %get-tuple-element.36) | copy-start | bytes 124
  99.0 3.4 %copy-start.5 = (f32[128,1280]{0,1:T(8,128)S(1)}, f32[128,1280]{0,1:T(8,128)}, u32[]{:S(2)}) copy-start(f32[128,1280]{0,1:T(8,128)} %get-tuple-element.27) | copy-start | bytes 1966084
  101.0 5.3 %copy-start.4 = (f32[128,1280]{0,1:T(8,128)S(1)}, f32[128,1280]{0,1:T(8,128)}, u32[]{:S(2)}) copy-start(f32[128,1280]{0,1:T(8,128)} %get-tuple-element.46) | copy-start | bytes 1966084
  101.0 7.8 %collective-permute-start.13 = (f32[10,64,128]{2,1,0:T(8,128)}, f32[10,64,128]{2,1,0:T(8,128)}, u32[]{:S(2)}, u32[]{:S(2)}) collective-permute-start(f32[10,64,128]{2,1,0:T(8,128)} %get-tuple-element.52), channel_id=1, source_target_pairs={{28,24},{24,28},{20,16},{16,20},{12,8},{8,12},{4,0},{0,4},{29,25},... | collective-permute-start | bytes 983048 | tf_op jit(solution)/shard_map/ppermute | solution.py:82
  103.9 4.3 %collective-permute-start.17 = (f32[128,128]{1,0:T(8,128)S(1)}, f32[128,128]{1,0:T(8,128)S(1)}, u32[]{:S(2)}, u32[]{:S(2)}) collective-permute-start(f32[128,128]{1,0:T(8,128)S(1)} %add.158), channel_id=1, source_target_pairs={{0,2},{1,3},{2,0},{3,1},{4,6},{5,7},{6,4},{7,5},{8,10},{9,11},{10,... | collective-permute-start | bytes 196616 | tf_op jit(solution)/shard_map/ppermute | solution.py:94
  106.4 2.5 %copy-start.8 = (f32[10,64,128]{2,1,0:T(8,128)S(1)}, f32[10,64,128]{2,1,0:T(8,128)}, u32[]{:S(2)}) copy-start(f32[10,64,128]{2,1,0:T(8,128)} %get-tuple-element.51) | copy-start | bytes 983044
  113.9 1.3 %collective-permute-start.14 = (f32[128,128]{1,0:T(8,128)S(1)}, f32[128,128]{1,0:T(8,128)S(1)}, u32[]{:S(2)}, u32[]{:S(2)}) collective-permute-start(f32[128,128]{1,0:T(8,128)S(1)} %convolution_add_fusion.1), channel_id=1, source_target_pairs={{0,1},{1,0},{2,3},{3,2},{4,5},{5,4},{6,7},{7,6},{8,9},{9,8},{10,11... | collective-permute-start | bytes 196616 | tf_op jit(solution)/shard_map/ppermute | solution.py:94
  115.2 4.3 %collective-permute-start.15 = (f32[128,128]{1,0:T(8,128)S(1)}, f32[128,128]{1,0:T(8,128)S(1)}, u32[]{:S(2)}, u32[]{:S(2)}) collective-permute-start(f32[128,128]{1,0:T(8,128)S(1)} %add.155), channel_id=1, source_target_pairs={{0,2},{1,3},{2,0},{3,1},{4,6},{5,7},{6,4},{7,5},{8,10},{9,11},{10,... | collective-permute-start | bytes 196616 | tf_op jit(solution)/shard_map/ppermute | solution.py:94
  (10 other events, 9.6 us)

commit v7 on v5

--- a/solution.py
+++ b/solution.py
@@ -87,15 +87,15 @@
     with_lead_rcv = a_rcv[:, None, None] * s_g + s_rcv
     send = jnp.where(first, with_lead_own, s_g)
     keep = jnp.where(first, s_g, with_lead_rcv)
-    if tie is not None:
-        if extra is None:
-            extra = during(tie)
-        send, extra = lax.optimization_barrier((send, extra))
     other = lax.ppermute(send, axis, swap)
     result = jnp.where(
         first, jnp.concatenate([other, keep], 0), jnp.concatenate([keep, other], 0)
     )
-    return result if tie is None else (result, extra)
+    if tie is None:
+        return result
+    if extra is None:
+        extra = during(tie)
+    return lax.optimization_barrier((result, extra))
 
 
 def butterfly_psum(parts, axis):
@@ -228,6 +228,7 @@
     local_state = jnp.einsum("jhp,jn->hpn", weighted_in, write_keys, precision=highest)
     single = length == BLOCK
     if single:
+
         def within_vjp(args):
             return jax.vjp(lambda f, s, d, w, r: within_part(f, s, d, w, r, skip_scale), *args)
 
@@ -269,11 +270,10 @@
     from_start = jnp.transpose(jnp.exp(cumul))
     weighted_grad = grad_mixed.reshape(length, head_count, head_width) * from_start[:, :, None]
     local_grad = jnp.einsum("jhp,jn->hpn", weighted_grad, read_queries, precision=highest)
+    state_grad = pair_scan(decay_total, local_grad, "seq", True)
     if single:
-        state_grad, ((gf_w, gs_w, gd_w, gw_w, gr_w), (gd_c, gr_c)) = pair_scan(
-            decay_total, local_grad, "seq", True, tie=grad_mixed,
-            during=lambda g: (pull_w(g), pull_c(g)),
-        )
+        gf_w, gs_w, gd_w, gw_w, gr_w = pull_w(grad_mixed)
+        gd_c, gr_c = pull_c(grad_mixed)
         grad_read = butterfly_psum(gr_w + gr_c, "head")
         _, pull_e = jax.vjp(
             lambda f, s, d, w: end_part(f, s, d, w, state_in),
@@ -285,7 +285,6 @@
         grad_decay = gd_w + gd_c + gd_e
         grad_write = butterfly_psum(gw_w + gw_e, "head")
     else:
-        state_grad = pair_scan(decay_total, local_grad, "seq", True)
         grad_features, grad_steps, grad_decay, grad_write, grad_read = pullback(
             (state_grad, grad_mixed)
         )

time: 131 us -> 126 us (0.962)
  the two profiles are of different devices: /device:TPU:8 before, /device:TPU:0 now
where the time goes in v7:
time: 126 us; the launch traced here: 125 us
  waiting for transfers between devices  57.5 us (46%)
  matrix products  22 us (17%)
  starting transfers between devices  20.2 us (16%)
  other arithmetic  17.2 us (14%)
  local copies, waits for them, and re-layouts  7.01 us (6%)
  between operations  1.34 us (1%)
    ppermute x2, waiting for transfers between devices, pair_scan(): s_in = lax.ppermute(out[1], axis, pairs)  24.1 us
    ppermute x4, waiting for transfers between devices, pair_scan(): a_rcv, s_rcv = lax.ppermute((a_snd, s_snd), axis, swap)  14.7 us
    ppermute x8, waiting for transfers between devices, butterfly_psum(): got = lax.ppermute(parts, axis, [(i, i ^ k) for i in range(count)])  8.37 us
    dot_general x3, matrix products, within_part(): within = jnp.einsum('hij,jhp->ihp', masked, scaled, precision=highest)  7.86 us
    ppermute x4, starting transfers between devices, pair_scan(): a_in, s_in = lax.ppermute(out, axis, pairs)  6.57 us
    ppermute x4, waiting for transfers between devices, pair_scan(): a_in, s_in = lax.ppermute(out, axis, pairs)  5.67 us
    ppermute x4, starting transfers between devices, pair_scan(): a_rcv, s_rcv = lax.ppermute((a_snd, s_snd), axis, swap)  5.53 us
    dot_general x6, matrix products, prefix_sum(): return jnp.dot(decay_in, upper, precision=highest)  5.09 us
  transfers between devices with their start and end apart: 20, of which 11 were waited for; matrix products, arithmetic and copies ran while one was open for 24% of the time, Pallas kernels for 0%

profile of v7, /device:TPU:0, one launch (start us, length us, event | category | flops | bytes accessed | tf_op | source)
XLA Modules:
  0.0 125.3 jit_solution(18437067324946650501)
XLA Ops:
  1.9 2.9 %collective-permute-start.10 = (f32[10]{0:T(128)S(1)}, f32[10]{0:T(128)S(1)}, u32[]{:S(2)}, u32[]{:S(2)}) collective-permute-start(f32[10]{0:T(128)S(1)} %dynamic_slice.29), channel_id=1, source_target_pairs={{28,24},{24,28},{20,16},{16,20},{12,8},{8,12},{4,0},{0,4},{29,25},... | collective-permute-start | bytes 128 | tf_op jit(solution)/shard_map/ppermute | solution.py:42
  5.4 1.3 %copy.23 = f32[128,1280]{0,1:T(8,128)S(1)} copy(f32[128,1280]{1,0:T(8,128)} %param.9) | data formatting | bytes 1310720 | tf_op args[0]
  8.3 2.0 %collective-permute-start = (f32[10]{0:T(128)S(1)}, f32[10]{0:T(128)S(1)}, u32[]{:S(2)}, u32[]{:S(2)}) collective-permute-start(f32[10]{0:T(128)S(1)} %get-tuple-element.100), channel_id=1, source_target_pairs={{0,4},{4,0},{8,12},{12,8},{16,20},{20,16},{24,28},{28,24},{1,5},{5... | collective-permute-start | bytes 128 | tf_op jit(solution)/shard_map/ppermute | solution.py:42
  10.3 6.6 %collective-permute-done = f32[10]{0:T(128)S(1)} collective-permute-done((f32[10]{0:T(128)S(1)}, f32[10]{0:T(128)S(1)}, u32[]{:S(2)}, u32[]{:S(2)}) %collective-permute-start) | collective-permute-done | bytes 72 | tf_op jit(solution)/shard_map/ppermute | solution.py:42
  17.6 3.5 %collective-permute-start.2 = (f32[10,64,128]{2,1,0:T(8,128)S(1)}, f32[10,64,128]{2,1,0:T(8,128)S(1)}, u32[]{:S(2)}, u32[]{:S(2)}) collective-permute-start(f32[10,64,128]{2,1,0:T(8,128)S(1)} %get-tuple-element.80), channel_id=1, source_target_pairs={{0,8},{4,12},{1,9},{5,13},{2,10},{6,14},{3,11},{7,15}} | collective-permute-start | bytes 983048 | tf_op jit(solution)/shard_map/ppermute | solution.py:67
  21.1 5.7 %collective-permute-done.2 = f32[10,64,128]{2,1,0:T(8,128)S(1)} collective-permute-done((f32[10,64,128]{2,1,0:T(8,128)S(1)}, f32[10,64,128]{2,1,0:T(8,128)S(1)}, u32[]{:S(2)}, u32[]{:S(2)}) %collective-permute-start.2) | collective-permute-done | bytes 327712 | tf_op jit(solution)/shard_map/ppermute | solution.py:67
  26.9 1.5 %collective-permute-start.3 = (f32[10,64,128]{2,1,0:T(8,128)S(1)}, f32[10,64,128]{2,1,0:T(8,128)}, u32[]{:S(2)}, u32[]{:S(2)}) collective-permute-start(f32[10,64,128]{2,1,0:T(8,128)S(1)} %multiply_add_fusion.4), channel_id=1, source_target_pairs={{8,16},{12,20},{9,17},{13,21},{10,18},{14,22},{11,19},{15,23}} | collective-permute-start | bytes 983048 | tf_op jit(solution)/shard_map/ppermute | solution.py:67
  29.9 1.4 %collective-permute-start.4 = (f32[10,64,128]{2,1,0:T(8,128)}, f32[10,64,128]{2,1,0:T(8,128)}, u32[]{:S(2)}, u32[]{:S(2)}) collective-permute-start(f32[10,64,128]{2,1,0:T(8,128)} %get-tuple-element.78), channel_id=1, source_target_pairs={{16,24},{20,28},{17,25},{21,29},{18,26},{22,30},{19,27},{23,31}} | collective-permute-start | bytes 983048 | tf_op jit(solution)/shard_map/ppermute | solution.py:64
  31.5 1.5 %fusion.26 = f32[20,128]{1,0:T(8,128)} fusion(f32[20,128]{1,0:T(8,128)} %param.14), kind=kOutput, calls=%fused_computation.73 | convolution fusion | flops 3948544 | bytes 20480 | tf_op jit(solution)/shard_map/jvp()/dot_general | solution.py:164
  33.3 4.3 %fusion = f32[128,20,64]{0,2,1:T(8,128)} fusion(f32[128,20,64]{0,2,1:T(8,128)S(1)} %bitcast.95, f32[128,128]{1,0:T(8,128)S(1)} %fusion.53, pred[128,128]{1,0:T(8,128)(4,1)} %iota_compare_fusion, f32[20,128]{1,0:T(8,128)} %fusion.26, f32[20]{0:T(128)} %param.15, f32[128,20]{0,1:T(8,128)} %bitcast.104), kind=kOutput, calls=%fused_computation.7 | convolution fusion | flops 253460480 | bytes 1413200 | tf_op jit(solution)/shard_map/jvp(hij,jhp->ihp)/dot_general | solution.py:180
  39.3 2.5 %broadcast_multiply_fusion = (f32[20,128,128]{2,1,0:T(8,128)}, f32[20,128,128]{2,1,0:T(8,128)}, f32[20,128,128]{2,1,0:T(8,128)}) fusion(f32[128,128]{1,0:T(8,128)S(1)} %fusion.53, f32[20,128]{1,0:T(8,128)S(1)} %copy-done.19, pred[128,128]{1,0:T(8,128)(4,1)S(1)} %copy-done.18), kind=kLoop, calls=%fused_computation.29 | loop fusion | flops 1310720 | bytes 4024320 | tf_op jit(solution)/shard_map/jvp()/mul | solution.py:179
  41.8 3.4 %collective-permute-done.5 = f32[10,64,128]{2,1,0:T(8,128)S(1)} collective-permute-done((f32[10,64,128]{2,1,0:T(8,128)S(1)}, f32[10,64,128]{2,1,0:T(8,128)S(1)}, u32[]{:S(2)}, u32[]{:S(2)}) %collective-permute-start.5) | collective-permute-done | bytes 327712 | tf_op jit(solution)/shard_map/ppermute | solution.py:90
  46.3 2.2 %broadcast_multiply_fusion.2 = (f32[128,20,64]{0,2,1:T(8,128)S(1)}, f32[128,20,64]{0,2,1:T(8,128)}) fusion(f32[128,20]{0,1:T(8,128)} %get-tuple-element.98, f32[20,64,128]{2,1,0:T(8,128)S(1)} %maximum_select_fusion, f32[128,128]{1,0:T(8,128)S(1)} %copy-done), kind=kOutput, calls=%fused_computation.47 | convolution fusion | flops 251822080 | bytes 2041856 | tf_op jit(solution)/shard_map/jvp(in,hpn->ihp)/dot_general | solution.py:187
  49.6 1.9 %multiply_reduce_fusion.7 = (f32[128]{0:T(128)S(1)}, f32[128]{0:T(128)S(1)}, f32[128,1280]{1,0:T(8,128)S(1)}) fusion(f32[128,1280]{1,0:T(8,128)} %param.10, f32[128,1280]{1,0:T(8,128)} %param.17, f32[1280]{0:T(1024)} %param.16, f32[128,1280]{1,0:T(8,128)S(1)} %copy.25, f32[128,1280]{1,0:T(8,128)} %copy.26), kind=kLoop, calls=%fused_computation.26 | loop fusion | flops 1801984 | bytes 3282944 | tf_op jit(solution)/shard_map/reduce_sum | solution.py:261
  52.8 1.5 %collective-permute-start.9 = (f32[128]{0:T(128)S(1)}, f32[128]{0:T(128)S(1)}, u32[]{:S(2)}, u32[]{:S(2)}) collective-permute-start(f32[128]{0:T(128)S(1)} %add.147), channel_id=1, source_target_pairs={{0,2},{1,3},{2,0},{3,1},{4,6},{5,7},{6,4},{7,5},{8,10},{9,11},{10,... | collective-permute-start | bytes 1544 | tf_op jit(solution)/shard_map/ppermute | solution.py:107
  54.8 1.5 %collective-permute-done.9 = f32[128]{0:T(128)S(1)} collective-permute-done((f32[128]{0:T(128)S(1)}, f32[128]{0:T(128)S(1)}, u32[]{:S(2)}, u32[]{:S(2)}) %collective-permute-start.9) | collective-permute-done | bytes 544 | tf_op jit(solution)/shard_map/ppermute | solution.py:107
  56.3 1.5 %collective-permute-done.7 = f32[128]{0:T(128)S(1)} collective-permute-done((f32[128]{0:T(128)S(1)}, f32[128]{0:T(128)S(1)}, u32[]{:S(2)}, u32[]{:S(2)}) %collective-permute-start.7) | collective-permute-done | bytes 544 | tf_op jit(solution)/shard_map/ppermute | solution.py:107
  57.9 1.3 %add_multiply_fusion = (f32[128,1280]{1,0:T(8,128)}, f32[128,1280]{1,0:T(8,128)S(1)}) fusion(f32[128,1280]{1,0:T(8,128)S(1)} %copy-done.8, f32[128,1280]{1,0:T(8,128)S(1)} %get-tuple-element.77, f32[128]{0:T(128)S(1)} %get-tuple-element.75, f32[128,1280]{1,0:T(8,128)S(1)} %copy-done.9, f32[1280]{0:T(1024)S(1)} %copy-done.27, f32[128]{0:T(128)S(1)} %get-tuple-element.76), kind=kLoop, calls=%fused_computation.22 | loop fusion | flops 2621440 | bytes 3282944 | tf_op jit(solution)/shard_map/mul | solution.py:269
  59.4 1.4 %fusion.5 = f32[20,64,128]{2,1,0:T(8,128)S(1)} fusion(f32[128,20,64]{0,2,1:T(8,128)S(1)} %bitcast.87, f32[128,20]{0,1:T(8,128)} %get-tuple-element.98, f32[128,128]{1,0:T(8,128)S(1)} %copy-done), kind=kOutput, calls=%fused_computation.32 | convolution fusion | flops 251822080 | bytes 1386496 | tf_op jit(solution)/shard_map/jhp,jn->hpn/dot_general | solution.py:272
  62.0 8.2 %collective-permute-done.11 = f32[10,64,128]{2,1,0:T(8,128)} collective-permute-done((f32[10,64,128]{2,1,0:T(8,128)}, f32[10,64,128]{2,1,0:T(8,128)}, u32[]{:S(2)}, u32[]{:S(2)}) %collective-permute-start.11) | collective-permute-done | bytes 327712 | tf_op jit(solution)/shard_map/ppermute | solution.py:42
  70.2 1.2 broadcast_add_fusion
  72.3 1.2 convolution_bitcast_fusion.4
  73.5 2.2 %fusion.54 = f32[20,128,128]{2,1,0:T(8,128)S(1)} fusion(f32[20,64,128]{2,1,0:T(8,128)S(1)} %bitcast.89, f32[128,20,64]{0,2,1:T(8,128)S(1)} %copy-done.5), kind=kOutput, calls=%fused_computation.115 | convolution fusion | flops 251658240 | bytes 2621440 | tf_op jit(solution)/shard_map/transpose(jvp(hij,jhp->ihp))/dot_general | solution.py:180
  77.2 1.4 %collective-permute-start.14 = (f32[10,64,128]{2,1,0:T(8,128)S(1)}, f32[10,64,128]{2,1,0:T(8,128)S(1)}, u32[]{:S(2)}, u32[]{:S(2)}) collective-permute-start(f32[10,64,128]{2,1,0:T(8,128)S(1)} %get-tuple-element.67), channel_id=1, source_target_pairs={{12,4},{8,0},{13,5},{9,1},{14,6},{10,2},{15,7},{11,3}} | collective-permute-start | bytes 983048 | tf_op jit(solution)/shard_map/ppermute | solution.py:64
  79.0 1.3 %convolution_bitcast_fusion.2 = f32[128,20,64]{0,2,1:T(8,128)S(1)} fusion(f32[20,64,128]{2,1,0:T(8,128)S(1)} %bitcast.90, f32[20,128,128]{2,1,0:T(8,128)S(1)} %copy-done.1), kind=kOutput, calls=%fused_computation.5 | convolution fusion | flops 251658240 | bytes 2621440 | tf_op jit(solution)/shard_map/transpose(jvp(hij,jhp->ihp))/dot_general | solution.py:180
  80.3 24.1 %collective-permute-done.14 = f32[10,64,128]{2,1,0:T(8,128)S(1)} collective-permute-done((f32[10,64,128]{2,1,0:T(8,128)S(1)}, f32[10,64,128]{2,1,0:T(8,128)S(1)}, u32[]{:S(2)}, u32[]{:S(2)}) %collective-permute-start.14) | collective-permute-done | bytes 327712 | tf_op jit(solution)/shard_map/ppermute | solution.py:64
  108.0 2.8 %collective-permute-done.19 = f32[128,128]{1,0:T(8,128)S(1)} collective-permute-done((f32[128,128]{1,0:T(8,128)S(1)}, f32[128,128]{1,0:T(8,128)S(1)}, u32[]{:S(2)}, u32[]{:S(2)}) %collective-permute-start.19) | collective-permute-done | bytes 65568 | tf_op jit(solution)/shard_map/ppermute | solution.py:107
  111.5 1.3 %collective-permute-done.15 = f32[10,64,128]{2,1,0:T(8,128)S(1)} collective-permute-done((f32[10,64,128]{2,1,0:T(8,128)S(1)}, f32[10,64,128]{2,1,0:T(8,128)S(1)}, u32[]{:S(2)}, u32[]{:S(2)}) %collective-permute-start.15) | collective-permute-done | bytes 327712 | tf_op jit(solution)/shard_map/ppermute | solution.py:90
  112.7 1.2 fusion.1
  114.1 1.6 %multiply_reduce_fusion.2 = (f32[128,20]{0,1:T(8,128)S(1)}, f32[128,20]{0,1:T(8,128)}, f32[128,20,64]{0,2,1:T(8,128)S(1)}, f32[128,20]{0,1:T(8,128)}, f32[128,20]{0,1:T(8,128)}) fusion(f32[128,20,64]{0,2,1:T(8,128)S(1)} %bitcast.94, f32[128,20]{0,1:T(8,128)S(1)} %bitcast.108, f32[128,20]{0,1:T(8,128)S(1)} %copy-done.21, ...), kind=kOutput, calls=%fused_computation.18 | convolution fusion | flops 254597120 | bytes 4724817 | tf_op jit(solution)/shard_map/transpose(jvp(jhp,jn->hpn))/dot_general | solution.py:199
  117.5 1.6 %multiply_reduce_fusion.1 = f32[20]{0:T(128)S(1)} fusion(f32[20,64,128]{2,1,0:T(8,128)S(1)} %maximum_select_fusion, f32[10,64,128]{2,1,0:T(8,128)} %copy-done.11, f32[10,64,128]{2,1,0:T(8,128)} %copy-done.4, pred[]{:T(512)S(6)} %eq.31), kind=kLoop, calls=%fused_computation.17 | loop fusion | flops 819180 | bytes 1310801 | tf_op jit(solution)/shard_map/transpose(jvp())/reduce_sum | solution.py:204
  122.8 1.9 %collective-permute-done.17 = f32[128,128]{1,0:T(8,128)S(1)} collective-permute-done((f32[128,128]{1,0:T(8,128)S(1)}, f32[128,128]{1,0:T(8,128)S(1)}, u32[]{:S(2)}, u32[]{:S(2)}) %collective-permute-start.17) | collective-permute-done | bytes 65568 | tf_op jit(solution)/shard_map/ppermute | solution.py:107
  (144 shorter events, 26.1 us)
Async XLA Ops:
  0.6 30.6 %copy-start = (f32[128,128]{1,0:T(8,128)S(1)}, f32[128,128]{1,0:T(8,128)}, u32[]{:S(2)}) copy-start(f32[128,128]{1,0:T(8,128)} %param.12) | copy-start | bytes 196612
  1.9 5.7 %collective-permute-start.10 = (f32[10]{0:T(128)S(1)}, f32[10]{0:T(128)S(1)}, u32[]{:S(2)}, u32[]{:S(2)}) collective-permute-start(f32[10]{0:T(128)S(1)} %dynamic_slice.29), channel_id=1, source_target_pairs={{28,24},{24,28},{20,16},{16,20},{12,8},{8,12},{4,0},{0,4},{29,25},... | collective-permute-start | bytes 128 | tf_op jit(solution)/shard_map/ppermute | solution.py:42
  7.5 10.0 %collective-permute-start.1 = (f32[10,64,128]{2,1,0:T(8,128)S(1)}, f32[10,64,128]{2,1,0:T(8,128)S(1)}, u32[]{:S(2)}, u32[]{:S(2)}) collective-permute-start(f32[10,64,128]{2,1,0:T(8,128)S(1)} %constant_dynamic-slice_fusion.1), channel_id=1, source_target_pairs={{0,4},{4,0},{8,12},{12,8},{16,20},{20,16},{24,28},{28,24},{1,5},{5... | collective-permute-start | bytes 983048 | tf_op jit(solution)/shard_map/ppermute | solution.py:42
  7.6 22.3 %copy-start.30 = (f32[10]{0:T(128)}, f32[10]{0:T(128)S(1)}, u32[]{:S(2)}) copy-start(f32[10]{0:T(128)S(1)} %collective-permute-done.10) | copy-start | bytes 124
  8.3 8.5 %collective-permute-start = (f32[10]{0:T(128)S(1)}, f32[10]{0:T(128)S(1)}, u32[]{:S(2)}, u32[]{:S(2)}) collective-permute-start(f32[10]{0:T(128)S(1)} %get-tuple-element.100), channel_id=1, source_target_pairs={{0,4},{4,0},{8,12},{12,8},{16,20},{20,16},{24,28},{28,24},{1,5},{5... | collective-permute-start | bytes 128 | tf_op jit(solution)/shard_map/ppermute | solution.py:42
  16.8 13.1 %copy-start.33 = (f32[10]{0:T(128)}, f32[10]{0:T(128)S(1)}, u32[]{:S(2)}) copy-start(f32[10]{0:T(128)S(1)} %collective-permute-done) | copy-start | bytes 124
  17.6 9.2 %collective-permute-start.2 = (f32[10,64,128]{2,1,0:T(8,128)S(1)}, f32[10,64,128]{2,1,0:T(8,128)S(1)}, u32[]{:S(2)}, u32[]{:S(2)}) collective-permute-start(f32[10,64,128]{2,1,0:T(8,128)S(1)} %get-tuple-element.80), channel_id=1, source_target_pairs={{0,8},{4,12},{1,9},{5,13},{2,10},{6,14},{3,11},{7,15}} | collective-permute-start | bytes 983048 | tf_op jit(solution)/shard_map/ppermute | solution.py:67
  26.9 2.2 %collective-permute-start.3 = (f32[10,64,128]{2,1,0:T(8,128)S(1)}, f32[10,64,128]{2,1,0:T(8,128)}, u32[]{:S(2)}, u32[]{:S(2)}) collective-permute-start(f32[10,64,128]{2,1,0:T(8,128)S(1)} %multiply_add_fusion.4), channel_id=1, source_target_pairs={{8,16},{12,20},{9,17},{13,21},{10,18},{14,22},{11,19},{15,23}} | collective-permute-start | bytes 983048 | tf_op jit(solution)/shard_map/ppermute | solution.py:67
  29.9 7.7 %collective-permute-start.4 = (f32[10,64,128]{2,1,0:T(8,128)}, f32[10,64,128]{2,1,0:T(8,128)}, u32[]{:S(2)}, u32[]{:S(2)}) collective-permute-start(f32[10,64,128]{2,1,0:T(8,128)} %get-tuple-element.78), channel_id=1, source_target_pairs={{16,24},{20,28},{17,25},{21,29},{18,26},{22,30},{19,27},{23,31}} | collective-permute-start | bytes 983048 | tf_op jit(solution)/shard_map/ppermute | solution.py:64
  37.8 7.3 %collective-permute-start.5 = (f32[10,64,128]{2,1,0:T(8,128)S(1)}, f32[10,64,128]{2,1,0:T(8,128)S(1)}, u32[]{:S(2)}, u32[]{:S(2)}) collective-permute-start(f32[10,64,128]{2,1,0:T(8,128)S(1)} %get-tuple-element.93), channel_id=1, source_target_pairs={{0,4},{4,0},{8,12},{12,8},{16,20},{20,16},{24,28},{28,24},{1,5},{5... | collective-permute-start | bytes 983048 | tf_op jit(solution)/shard_map/ppermute | solution.py:90
  49.6 8.2 %copy-start.27 = (f32[1280]{0:T(1024)S(1)}, f32[1280]{0:T(1024)}, u32[]{:S(2)}) copy-start(f32[1280]{0:T(1024)} %param.16) | copy-start | bytes 15364
  51.6 1.2 collective-permute-start.8
  51.6 2.6 %collective-permute-start.6 = (f32[128]{0:T(128)S(1)}, f32[128]{0:T(128)S(1)}, u32[]{:S(2)}, u32[]{:S(2)}) collective-permute-start(f32[128]{0:T(128)S(1)} %get-tuple-element.65), channel_id=1, source_target_pairs={{0,1},{1,0},{2,3},{3,2},{4,5},{5,4},{6,7},{7,6},{8,9},{9,8},{10,11... | collective-permute-start | bytes 1544 | tf_op jit(solution)/shard_map/ppermute | solution.py:107
  52.8 3.5 %collective-permute-start.9 = (f32[128]{0:T(128)S(1)}, f32[128]{0:T(128)S(1)}, u32[]{:S(2)}, u32[]{:S(2)}) collective-permute-start(f32[128]{0:T(128)S(1)} %add.147), channel_id=1, source_target_pairs={{0,2},{1,3},{2,0},{3,1},{4,6},{5,7},{6,4},{7,5},{8,10},{9,11},{10,... | collective-permute-start | bytes 1544 | tf_op jit(solution)/shard_map/ppermute | solution.py:107
  54.3 3.5 %collective-permute-start.7 = (f32[128]{0:T(128)S(1)}, f32[128]{0:T(128)S(1)}, u32[]{:S(2)}, u32[]{:S(2)}) collective-permute-start(f32[128]{0:T(128)S(1)} %add.143), channel_id=1, source_target_pairs={{0,2},{1,3},{2,0},{3,1},{4,6},{5,7},{6,4},{7,5},{8,10},{9,11},{10,... | collective-permute-start | bytes 1544 | tf_op jit(solution)/shard_map/ppermute | solution.py:107
  61.5 8.7 %collective-permute-start.11 = (f32[10,64,128]{2,1,0:T(8,128)}, f32[10,64,128]{2,1,0:T(8,128)}, u32[]{:S(2)}, u32[]{:S(2)}) collective-permute-start(f32[10,64,128]{2,1,0:T(8,128)} %constant_dynamic-slice_fusion), channel_id=1, source_target_pairs={{28,24},{24,28},{20,16},{16,20},{12,8},{8,12},{4,0},{0,4},{29,25},... | collective-permute-start | bytes 983048 | tf_op jit(solution)/shard_map/ppermute | solution.py:42
  62.0 10.2 %copy-start.17 = (f32[128,20]{0,1:T(8,128)S(1)}, f32[128,20]{0,1:T(8,128)}, u32[]{:S(2)}) copy-start(f32[128,20]{0,1:T(8,128)} %get-tuple-element.98) | copy-start | bytes 30724
  71.4 4.4 %collective-permute-start.12 = (f32[10,64,128]{2,1,0:T(8,128)S(1)}, f32[10,64,128]{2,1,0:T(8,128)S(1)}, u32[]{:S(2)}, u32[]{:S(2)}) collective-permute-start(f32[10,64,128]{2,1,0:T(8,128)S(1)} %get-tuple-element.69), channel_id=1, source_target_pairs={{28,20},{24,16},{29,21},{25,17},{30,22},{26,18},{31,23},{27,19}} | collective-permute-start | bytes 983048 | tf_op jit(solution)/shard_map/ppermute | solution.py:67
  75.9 1.3 %collective-permute-start.13 = (f32[10,64,128]{2,1,0:T(8,128)S(1)}, f32[10,64,128]{2,1,0:T(8,128)S(1)}, u32[]{:S(2)}, u32[]{:S(2)}) collective-permute-start(f32[10,64,128]{2,1,0:T(8,128)S(1)} %multiply_add_fusion.2), channel_id=1, source_target_pairs={{20,12},{16,8},{21,13},{17,9},{22,14},{18,10},{23,15},{19,11}} | collective-permute-start | bytes 983048 | tf_op jit(solution)/shard_map/ppermute | solution.py:67
  77.2 27.1 %collective-permute-start.14 = (f32[10,64,128]{2,1,0:T(8,128)S(1)}, f32[10,64,128]{2,1,0:T(8,128)S(1)}, u32[]{:S(2)}, u32[]{:S(2)}) collective-permute-start(f32[10,64,128]{2,1,0:T(8,128)S(1)} %get-tuple-element.67), channel_id=1, source_target_pairs={{12,4},{8,0},{13,5},{9,1},{14,6},{10,2},{15,7},{11,3}} | collective-permute-start | bytes 983048 | tf_op jit(solution)/shard_map/ppermute | solution.py:64
  78.9 25.5 %copy-start.31 = (f32[10]{0:T(128)S(1)}, f32[10]{0:T(128)}, u32[]{:S(2)}) copy-start(f32[10]{0:T(128)} %copy-done.30) | copy-start | bytes 124
  78.9 25.5 %copy-start.32 = (f32[10]{0:T(128)S(1)}, f32[10]{0:T(128)}, u32[]{:S(2)}) copy-start(f32[10]{0:T(128)} %get-tuple-element.74) | copy-start | bytes 124
  78.9 27.6 %collective-permute-start.18 = (f32[128,128]{1,0:T(8,128)S(1)}, f32[128,128]{1,0:T(8,128)S(1)}, u32[]{:S(2)}, u32[]{:S(2)}) collective-permute-start(f32[128,128]{1,0:T(8,128)S(1)} %convolution_add_fusion), channel_id=1, source_target_pairs={{0,1},{1,0},{2,3},{3,2},{4,5},{5,4},{6,7},{7,6},{8,9},{9,8},{10,11... | collective-permute-start | bytes 196616 | tf_op jit(solution)/shard_map/ppermute | solution.py:107
  104.4 8.3 %copy-start.16 = (f32[20,128]{1,0:T(8,128)S(1)}, f32[20,128]{1,0:T(8,128)}, u32[]{:S(2)}) copy-start(f32[20,128]{1,0:T(8,128)} %param.13) | copy-start | bytes 30724
  104.4 8.3 %copy-start.21 = (f32[128,20]{0,1:T(8,128)S(1)}, f32[128,20]{0,1:T(8,128)}, u32[]{:S(2)}) copy-start(f32[128,20]{0,1:T(8,128)} %copy-done.20) | copy-start | bytes 30724
  105.5 10.1 %copy-start.4 = (f32[10,64,128]{2,1,0:T(8,128)}, f32[10,64,128]{2,1,0:T(8,128)S(1)}, u32[]{:S(2)}) copy-start(f32[10,64,128]{2,1,0:T(8,128)S(1)} %get-tuple-element.92) | copy-start | bytes 983044
  105.5 8.5 %copy-start.6 = (f32[128,20,64]{0,2,1:T(8,128)S(1)}, f32[128,20,64]{0,2,1:T(8,128)}, u32[]{:S(2)}) copy-start(f32[128,20,64]{0,2,1:T(8,128)} %get-tuple-element.102) | copy-start | bytes 1966084
  105.6 8.5 %copy-start.36 = (f32[20]{0:T(128)S(1)}, f32[20]{0:T(128)}, u32[]{:S(2)}) copy-start(f32[20]{0:T(128)} %param.15) | copy-start | bytes 244
  105.6 7.1 %collective-permute-start.15 = (f32[10,64,128]{2,1,0:T(8,128)S(1)}, f32[10,64,128]{2,1,0:T(8,128)S(1)}, u32[]{:S(2)}, u32[]{:S(2)}) collective-permute-start(f32[10,64,128]{2,1,0:T(8,128)S(1)} %get-tuple-element.91), channel_id=1, source_target_pairs={{28,24},{24,28},{20,16},{16,20},{12,8},{8,12},{4,0},{0,4},{29,25},... | collective-permute-start | bytes 983048 | tf_op jit(solution)/shard_map/ppermute | solution.py:90
  106.5 4.3 %collective-permute-start.19 = (f32[128,128]{1,0:T(8,128)S(1)}, f32[128,128]{1,0:T(8,128)S(1)}, u32[]{:S(2)}, u32[]{:S(2)}) collective-permute-start(f32[128,128]{1,0:T(8,128)S(1)} %add.165), channel_id=1, source_target_pairs={{0,2},{1,3},{2,0},{3,1},{4,6},{5,7},{6,4},{7,5},{8,10},{9,11},{10,... | collective-permute-start | bytes 196616 | tf_op jit(solution)/shard_map/ppermute | solution.py:107
  114.0 6.2 %collective-permute-start.16 = (f32[128,128]{1,0:T(8,128)S(1)}, f32[128,128]{1,0:T(8,128)S(1)}, u32[]{:S(2)}, u32[]{:S(2)}) collective-permute-start(f32[128,128]{1,0:T(8,128)S(1)} %fusion.1), channel_id=1, source_target_pairs={{0,1},{1,0},{2,3},{3,2},{4,5},{5,4},{6,7},{7,6},{8,9},{9,8},{10,11... | collective-permute-start | bytes 196616 | tf_op jit(solution)/shard_map/ppermute | solution.py:107
  120.1 4.5 %collective-permute-start.17 = (f32[128,128]{1,0:T(8,128)S(1)}, f32[128,128]{1,0:T(8,128)S(1)}, u32[]{:S(2)}, u32[]{:S(2)}) collective-permute-start(f32[128,128]{1,0:T(8,128)S(1)} %add.162), channel_id=1, source_target_pairs={{0,2},{1,3},{2,0},{3,1},{4,6},{5,7},{6,4},{7,5},{8,10},{9,11},{10,... | collective-permute-start | bytes 196616 | tf_op jit(solution)/shard_map/ppermute | solution.py:107
  (25 other events, 94.9 us)

commit v8 on v4

--- a/solution.py
+++ b/solution.py
@@ -89,12 +89,15 @@
     count = lax.axis_size(axis)
     if count & (count - 1):
         return lax.psum(parts, axis)
+    got = [parts] + [
+        lax.ppermute(parts, axis, [(i, i ^ m) for i in range(count)]) for m in range(1, count)
+    ]
     k = 1
     while k < count:
-        got = lax.ppermute(parts, axis, [(i, i ^ k) for i in range(count)])
-        parts = jax.tree.map(jnp.add, parts, got)
+        got = [jax.tree.map(jnp.add, got[m], got[m ^ k]) if m % (2 * k) == 0 else None
+               for m in range(count)]
         k *= 2
-    return parts
+    return got[0]
 
 
 def block_step(carry_state, inputs, skip_scale):
@@ -240,7 +243,8 @@
     gated_out = mixed_out * active
     weighted = out_grad * norm_gain[None, :]
     square_sum, cross_sum = butterfly_psum(
-        (jnp.sum(gated_out * gated_out, axis=1), jnp.sum(weighted * gated_out, axis=1)), "head"
+        jnp.stack([jnp.sum(gated_out * gated_out, axis=1), jnp.sum(weighted * gated_out, axis=1)]),
+        "head",
     )
     inverse = lax.rsqrt(square_sum / channels + eps)
     grad_gated = (

time: 121 us -> 124 us (1.025)
  starting transfers between devices: 22.3 us -> 23.9 us
    ppermute x8 -> x9, waiting for transfers between devices: 9.27 us -> 2.77 us  [butterfly_psum(): lax.ppermute(parts, axis, [(i, i ^ m) for i in range(count)])]
    ppermute x2, waiting for transfers between devices: 5.56 us -> 10 us  [pair_scan(): other = lax.ppermute(send, axis, swap)]
    ppermute x8 -> x9, starting transfers between devices: 4.15 us -> 5.8 us  [butterfly_psum(): lax.ppermute(parts, axis, [(i, i ^ m) for i in range(count)])]
    ppermute x2, waiting for transfers between devices: 28.2 us -> 29.6 us  [pair_scan(): s_in = lax.ppermute(out[1], axis, pairs)]
    ppermute x4, waiting for transfers between devices: 16.4 us -> 17.7 us  [pair_scan(): a_rcv, s_rcv = lax.ppermute((a_snd, s_snd), axis, swap)]
    unnamed x36 -> x34, local copies, waits for them, and re-layouts: 2.98 us -> 2.53 us
  transfers between devices with their start and end apart: 20 -> 21, of which waited for: 13 -> 9; matrix products, arithmetic and copies ran while one was open for 10% -> 12% of each run, Pallas kernels for 0% -> 0%
where the time goes in v8:
time: 124 us; the launch traced here: 123 us
  waiting for transfers between devices  65 us (52%)
  starting transfers between devices  23.9 us (19%)
  matrix products  18.7 us (15%)
  other arithmetic  8.73 us (7%)
  local copies, waits for them, and re-layouts  5.74 us (5%)
    ppermute x2, waiting for transfers between devices, pair_scan(): s_in = lax.ppermute(out[1], axis, pairs)  29.6 us
    ppermute x4, waiting for transfers between devices, pair_scan(): a_rcv, s_rcv = lax.ppermute((a_snd, s_snd), axis, swap)  17.7 us
    ppermute x2, waiting for transfers between devices, pair_scan(): other = lax.ppermute(send, axis, swap)  10 us
    dot_general x3, matrix products, within_part(): within = jnp.einsum('hij,jhp->ihp', masked, scaled, precision=highest)  8.91 us
    ppermute x4, starting transfers between devices, pair_scan(): a_in, s_in = lax.ppermute(out, axis, pairs)  6.66 us
    ppermute x4, starting transfers between devices, pair_scan(): a_rcv, s_rcv = lax.ppermute((a_snd, s_snd), axis, swap)  6.35 us
    ppermute x9, starting transfers between devices, butterfly_psum(): lax.ppermute(parts, axis, [(i, i ^ m) for i in range(count)])  5.8 us
    ppermute x4, waiting for transfers between devices, pair_scan(): a_in, s_in = lax.ppermute(out, axis, pairs)  4.82 us
  transfers between devices with their start and end apart: 21, of which 9 were waited for; matrix products, arithmetic and copies ran while one was open for 12% of the time, Pallas kernels for 0%

profile of v8, /device:TPU:0, one launch (start us, length us, event | category | flops | bytes accessed | tf_op | source)
XLA Modules:
  0.0 123.1 jit_solution(5757814555940932766)
XLA Ops:
  1.8 1.3 %copy.22 = f32[128,1280]{0,1:T(8,128)S(1)} copy(f32[128,1280]{1,0:T(8,128)} %param.9) | data formatting | bytes 1310720 | tf_op args[0]
  3.9 3.0 %collective-permute-start.1 = (f32[10,64,128]{2,1,0:T(8,128)S(1)}, f32[10,64,128]{2,1,0:T(8,128)S(1)}, u32[]{:S(2)}, u32[]{:S(2)}) collective-permute-start(f32[10,64,128]{2,1,0:T(8,128)S(1)} %constant_dynamic-slice_fusion.1), channel_id=1, source_target_pairs={{0,4},{4,0},{8,12},{12,8},{16,20},{20,16},{24,28},{28,24},{1,5},{5... | collective-permute-start | bytes 983048 | tf_op jit(solution)/shard_map/ppermute | solution.py:42
  7.0 7.6 %collective-permute-done.9 = f32[10]{0:T(128)S(1)} collective-permute-done((f32[10]{0:T(128)S(1)}, f32[10]{0:T(128)S(1)}, u32[]{:S(2)}, u32[]{:S(2)}) %collective-permute-start.9) | collective-permute-done | bytes 72 | tf_op jit(solution)/shard_map/ppermute | solution.py:42
  15.3 1.7 %collective-permute-start = (f32[10]{0:T(128)S(1)}, f32[10]{0:T(128)S(1)}, u32[]{:S(2)}, u32[]{:S(2)}) collective-permute-start(f32[10]{0:T(128)S(1)} %get-tuple-element.52), channel_id=1, source_target_pairs={{0,4},{4,0},{8,12},{12,8},{16,20},{20,16},{24,28},{28,24},{1,5},{5... | collective-permute-start | bytes 128 | tf_op jit(solution)/shard_map/ppermute | solution.py:42
  17.0 1.8 %collective-permute-done = f32[10]{0:T(128)S(1)} collective-permute-done((f32[10]{0:T(128)S(1)}, f32[10]{0:T(128)S(1)}, u32[]{:S(2)}, u32[]{:S(2)}) %collective-permute-start) | collective-permute-done | bytes 72 | tf_op jit(solution)/shard_map/ppermute | solution.py:42
  19.0 3.7 %collective-permute-start.2 = (f32[10,64,128]{2,1,0:T(8,128)S(1)}, f32[10,64,128]{2,1,0:T(8,128)S(1)}, u32[]{:S(2)}, u32[]{:S(2)}) collective-permute-start(f32[10,64,128]{2,1,0:T(8,128)S(1)} %get-tuple-element.36), channel_id=1, source_target_pairs={{0,8},{4,12},{1,9},{5,13},{2,10},{6,14},{3,11},{7,15}} | collective-permute-start | bytes 983048 | tf_op jit(solution)/shard_map/ppermute | solution.py:62
  22.8 4.8 %collective-permute-done.2 = f32[10,64,128]{2,1,0:T(8,128)S(1)} collective-permute-done((f32[10,64,128]{2,1,0:T(8,128)S(1)}, f32[10,64,128]{2,1,0:T(8,128)S(1)}, u32[]{:S(2)}, u32[]{:S(2)}) %collective-permute-start.2) | collective-permute-done | bytes 327712 | tf_op jit(solution)/shard_map/ppermute | solution.py:62
  29.4 1.6 %collective-permute-start.5 = (f32[10,64,128]{2,1,0:T(8,128)S(1)}, f32[10,64,128]{2,1,0:T(8,128)S(1)}, u32[]{:S(2)}, u32[]{:S(2)}) collective-permute-start(f32[10,64,128]{2,1,0:T(8,128)S(1)} %get-tuple-element.48), channel_id=1, source_target_pairs={{0,4},{4,0},{8,12},{12,8},{16,20},{20,16},{24,28},{28,24},{1,5},{5... | collective-permute-start | bytes 983048 | tf_op jit(solution)/shard_map/ppermute | solution.py:82
  31.2 5.3 %collective-permute-done.5 = f32[10,64,128]{2,1,0:T(8,128)S(1)} collective-permute-done((f32[10,64,128]{2,1,0:T(8,128)S(1)}, f32[10,64,128]{2,1,0:T(8,128)S(1)}, u32[]{:S(2)}, u32[]{:S(2)}) %collective-permute-start.5) | collective-permute-done | bytes 327712 | tf_op jit(solution)/shard_map/ppermute | solution.py:82
  37.3 3.5 %multiply_add_fusion.1 = f32[128,20,64]{0,2,1:T(8,128)} fusion(f32[128,20,64]{0,2,1:T(8,128)S(1)} %convolution_bitcast_fusion.1, f32[128,20,64]{0,2,1:T(8,128)S(1)} %bitcast.83, f32[128,128]{1,0:T(8,128)S(1)} %fusion.86, f32[20,128]{1,0:T(8,128)S(1)} %bitcast.95, pred[128,128]{1,0:T(8,128)(4,1)S(1)} %iota_compare_fusion.6, ...), kind=kOutput, calls=%fused_computation.35 | convolution fusion | flops 253788160 | bytes 2078800 | tf_op jit(solution)/shard_map/jvp(hij,jhp->ihp)/dot_general | solution.py:170
  40.8 1.4 %copy.23 = f32[128,1280]{1,0:T(8,128)S(1)} copy(f32[128,1280]{0,1:T(8,128)} %bitcast.93) | data formatting | bytes 1310720 | tf_op jit(solution)/shard_map/add | solution.py:229
  42.2 1.5 %multiply_reduce_fusion.7 = (f32[128]{0:T(128)S(1)}, f32[128]{0:T(128)S(1)}) fusion(f32[128,1280]{1,0:T(8,128)S(1)} %copy.23, f32[128,1280]{1,0:T(8,128)S(1)} %copy-done.1, f32[128,1280]{1,0:T(8,128)} %param.17, f32[1280]{0:T(1024)S(1)} %copy-done.10), kind=kLoop, calls=%fused_computation.32 | loop fusion | flops 1638144 | bytes 1972224 | tf_op jit(solution)/shard_map/reduce_sum | solution.py:246
  43.8 1.6 %collective-permute-start.7 = (f32[2,128]{1,0:T(2,128)S(1)}, f32[2,128]{1,0:T(2,128)S(1)}, u32[]{:S(2)}, u32[]{:S(2)}) collective-permute-start(f32[2,128]{1,0:T(2,128)S(1)} %pad_maximum_fusion), channel_id=1, source_target_pairs={{0,2},{1,3},{2,0},{3,1},{4,6},{5,7},{6,4},{7,5},{8,10},{9,11},{10,... | collective-permute-start | bytes 3080 | tf_op jit(solution)/shard_map/ppermute | solution.py:93
  45.7 1.8 %collective-permute-done.7 = f32[2,128]{1,0:T(2,128)S(1)} collective-permute-done((f32[2,128]{1,0:T(2,128)S(1)}, f32[2,128]{1,0:T(2,128)S(1)}, u32[]{:S(2)}, u32[]{:S(2)}) %collective-permute-start.7) | collective-permute-done | bytes 1056 | tf_op jit(solution)/shard_map/ppermute | solution.py:93
  48.5 1.5 %add_multiply_fusion = (f32[128,1280]{1,0:T(8,128)}, f32[128,1280]{1,0:T(8,128)}) fusion(f32[128,1280]{1,0:T(8,128)S(1)} %copy-done.1, f32[128,1280]{1,0:T(8,128)S(1)} %copy.23, f32[128]{0:T(128)S(1)} %fusion.72, f32[128,1280]{1,0:T(8,128)S(1)} %copy-done.2, f32[128]{0:T(128)S(1)} %rsqrt_bitcast_fusion, f32[1280]{0:T(1024)S(1)} %copy-done.10), kind=kLoop, calls=%fused_computation.28 | loop fusion | flops 2621440 | bytes 3282944 | tf_op jit(solution)/shard_map/mul | solution.py:255
  49.9 1.3 %copy.24 = f32[128,1280]{0,1:T(8,128)S(1)} copy(f32[128,1280]{1,0:T(8,128)} %get-tuple-element.43) | data formatting | bytes 1310720 | tf_op jit(solution)/shard_map/mul | solution.py:254
  52.0 1.6 %collective-permute-start.10 = (f32[10,64,128]{2,1,0:T(8,128)S(1)}, f32[10,64,128]{2,1,0:T(8,128)S(1)}, u32[]{:S(2)}, u32[]{:S(2)}) collective-permute-start(f32[10,64,128]{2,1,0:T(8,128)S(1)} %constant_dynamic-slice_fusion), channel_id=1, source_target_pairs={{28,24},{24,28},{20,16},{16,20},{12,8},{8,12},{4,0},{0,4},{29,25},... | collective-permute-start | bytes 983048 | tf_op jit(solution)/shard_map/ppermute | solution.py:42
  53.5 8.3 %collective-permute-done.10 = f32[10,64,128]{2,1,0:T(8,128)S(1)} collective-permute-done((f32[10,64,128]{2,1,0:T(8,128)S(1)}, f32[10,64,128]{2,1,0:T(8,128)S(1)}, u32[]{:S(2)}, u32[]{:S(2)}) %collective-permute-start.10) | collective-permute-done | bytes 327712 | tf_op jit(solution)/shard_map/ppermute | solution.py:42
  62.6 1.4 %collective-permute-start.11 = (f32[10,64,128]{2,1,0:T(8,128)}, f32[10,64,128]{2,1,0:T(8,128)}, u32[]{:S(2)}, u32[]{:S(2)}) collective-permute-start(f32[10,64,128]{2,1,0:T(8,128)} %get-tuple-element.28), channel_id=1, source_target_pairs={{28,20},{24,16},{29,21},{25,17},{30,22},{26,18},{31,23},{27,19}} | collective-permute-start | bytes 983048 | tf_op jit(solution)/shard_map/ppermute | solution.py:62
  64.0 3.0 %fusion.19 = (f32[20,128]{1,0:T(8,128)S(1)}, f32[20,128]{1,0:T(8,128)S(1)}, f32[128,128]{1,0:T(8,128)S(1)}) fusion(f32[128,128]{1,0:T(8,128)S(1)} %fusion.86, f32[20,128]{1,0:T(8,128)S(1)} %bitcast.96, pred[128,128]{1,0:T(8,128)(4,1)S(1)} %iota_compare_fusion.6, f32[20,64,128]{2,1,0:T(8,128)S(1)} %bitcast.88, f32[128,20,64]{0,2,1:T(8,128)S(1)} %bitcast.84, ...), kind=kOutput, calls=%fused_computation.20 | convolution fusion | flops 255405056 | bytes 1499136 | tf_op jit(solution)/shard_map/transpose(jvp(hij,jhp->ihp))/dot_general | solution.py:170
  68.2 1.2 %fusion.16 = f32[128,128]{1,0:T(8,128)S(1)} fusion(f32[128,128]{1,0:T(8,128)S(1)} %fusion.88, f32[128,20,64]{0,2,1:T(8,128)S(1)} %bitcast.89, f32[128,20]{0,1:T(8,128)S(1)} %get-tuple-element.50, f32[10,64,128]{2,1,0:T(8,128)S(1)} %get-tuple-element.49, f32[10,64,128]{2,1,0:T(8,128)S(1)} %copy-done.7, pred[]{:T(512)S(6)} %eq.27), kind=kOutput, calls=%fused_computation.15 | convolution fusion | flops 252329984 | bytes 1452033 | tf_op jit(solution)/shard_map/transpose(jvp(in,hpn->ihp))/dot_general | solution.py:177
  70.1 1.3 %collective-permute-start.20 = (f32[128,128]{1,0:T(8,128)S(1)}, f32[128,128]{1,0:T(8,128)S(1)}, u32[]{:S(2)}, u32[]{:S(2)}) collective-permute-start(f32[128,128]{1,0:T(8,128)S(1)} %fusion.16), channel_id=1, source_target_pairs={{0,3},{1,2},{2,1},{3,0},{4,7},{5,6},{6,5},{7,4},{8,11},{9,10},{10,... | collective-permute-start | bytes 196616 | tf_op jit(solution)/shard_map/ppermute | solution.py:93
  71.5 1.3 %collective-permute-start.13 = (f32[10,64,128]{2,1,0:T(8,128)S(1)}, f32[10,64,128]{2,1,0:T(8,128)S(1)}, u32[]{:S(2)}, u32[]{:S(2)}) collective-permute-start(f32[10,64,128]{2,1,0:T(8,128)S(1)} %get-tuple-element.26), channel_id=1, source_target_pairs={{12,4},{8,0},{13,5},{9,1},{14,6},{10,2},{15,7},{11,3}} | collective-permute-start | bytes 983048 | tf_op jit(solution)/shard_map/ppermute | solution.py:59
  73.1 2.4 %fusion.12 = f32[128,20,64]{0,2,1:T(8,128)} fusion(f32[20,64,128]{2,1,0:T(8,128)S(1)} %bitcast.90, f32[128,128]{1,0:T(8,128)S(1)} %fusion.86, f32[20,128]{1,0:T(8,128)S(1)} %bitcast.97, pred[128,128]{1,0:T(8,128)(4,1)S(1)} %iota_compare_fusion.6), kind=kOutput, calls=%fused_computation.11 | convolution fusion | flops 252968960 | bytes 1402880 | tf_op jit(solution)/shard_map/transpose(jvp(hij,jhp->ihp))/dot_general | solution.py:170
  75.5 29.6 %collective-permute-done.13 = f32[10,64,128]{2,1,0:T(8,128)S(1)} collective-permute-done((f32[10,64,128]{2,1,0:T(8,128)S(1)}, f32[10,64,128]{2,1,0:T(8,128)S(1)}, u32[]{:S(2)}, u32[]{:S(2)}) %collective-permute-start.13) | collective-permute-done | bytes 327712 | tf_op jit(solution)/shard_map/ppermute | solution.py:59
  105.3 1.5 %collective-permute-start.14 = (f32[10,64,128]{2,1,0:T(8,128)S(1)}, f32[10,64,128]{2,1,0:T(8,128)S(1)}, u32[]{:S(2)}, u32[]{:S(2)}) collective-permute-start(f32[10,64,128]{2,1,0:T(8,128)S(1)} %get-tuple-element.46), channel_id=1, source_target_pairs={{28,24},{24,28},{20,16},{16,20},{12,8},{8,12},{4,0},{0,4},{29,25},... | collective-permute-start | bytes 983048 | tf_op jit(solution)/shard_map/ppermute | solution.py:82
  107.7 4.8 %collective-permute-done.14 = f32[10,64,128]{2,1,0:T(8,128)S(1)} collective-permute-done((f32[10,64,128]{2,1,0:T(8,128)S(1)}, f32[10,64,128]{2,1,0:T(8,128)S(1)}, u32[]{:S(2)}, u32[]{:S(2)}) %collective-permute-start.14) | collective-permute-done | bytes 327712 | tf_op jit(solution)/shard_map/ppermute | solution.py:82
  112.4 1.2 fusion.15
  114.1 1.5 %collective-permute-start.17 = (f32[128,128]{1,0:T(8,128)S(1)}, f32[128,128]{1,0:T(8,128)}, u32[]{:S(2)}, u32[]{:S(2)}) collective-permute-start(f32[128,128]{1,0:T(8,128)S(1)} %fusion.15), channel_id=1, source_target_pairs={{0,3},{1,2},{2,1},{3,0},{4,7},{5,6},{6,5},{7,4},{8,11},{9,10},{10,... | collective-permute-start | bytes 196616 | tf_op jit(solution)/shard_map/ppermute | solution.py:93
  116.1 2.2 %multiply_reduce_fusion.2 = (f32[128,20]{0,1:T(8,128)S(1)}, f32[128,20]{0,1:T(8,128)S(1)}, f32[128,20]{0,1:T(8,128)S(1)}, f32[128,20,64]{0,2,1:T(8,128)S(1)}, f32[128,20]{0,1:T(8,128)S(1)}) fusion(f32[128,20,64]{0,2,1:T(8,128)S(1)} %bitcast.86, f32[128,20]{0,1:T(8,128)S(1)} %bitcast.103, f32[128,20]{0,1:T(8,128)S(1)} %get-tuple-element.51, ...), kind=kOutput, calls=%fused_computation.24 | convolution fusion | flops 254597120 | bytes 4059217 | tf_op jit(solution)/shard_map/transpose(jvp(jhp,jn->hpn))/dot_general | solution.py:189
  120.5 1.1 copy.28
  121.6 1.5 %add_add_fusion.1 = f32[128,128]{1,0:T(8,128)} fusion(f32[128,128]{1,0:T(8,128)} %collective-permute-done.16, f32[128,128]{1,0:T(8,128)} %collective-permute-done.17, f32[128,128]{1,0:T(8,128)S(1)} %fusion.15, f32[128,128]{1,0:T(8,128)S(1)} %collective-permute-done.15), kind=kLoop, calls=%fused_computation.88 | loop fusion | flops 49152 | bytes 327680 | tf_op jit(solution)/shard_map/add | solution.py:97
  (94 shorter events, 14.6 us)
Async XLA Ops:
  0.6 2.5 %copy-start = (f32[128,128]{1,0:T(8,128)S(1)}, f32[128,128]{1,0:T(8,128)}, u32[]{:S(2)}) copy-start(f32[128,128]{1,0:T(8,128)} %param.11) | copy-start | bytes 196612
  3.9 15.0 %collective-permute-start.1 = (f32[10,64,128]{2,1,0:T(8,128)S(1)}, f32[10,64,128]{2,1,0:T(8,128)S(1)}, u32[]{:S(2)}, u32[]{:S(2)}) collective-permute-start(f32[10,64,128]{2,1,0:T(8,128)S(1)} %constant_dynamic-slice_fusion.1), channel_id=1, source_target_pairs={{0,4},{4,0},{8,12},{12,8},{16,20},{20,16},{24,28},{28,24},{1,5},{5... | collective-permute-start | bytes 983048 | tf_op jit(solution)/shard_map/ppermute | solution.py:42
  7.0 7.7 %collective-permute-start.9 = (f32[10]{0:T(128)S(1)}, f32[10]{0:T(128)S(1)}, u32[]{:S(2)}, u32[]{:S(2)}) collective-permute-start(f32[10]{0:T(128)S(1)} %dynamic_slice.29), channel_id=1, source_target_pairs={{28,24},{24,28},{20,16},{16,20},{12,8},{8,12},{4,0},{0,4},{29,25},... | collective-permute-start | bytes 128 | tf_op jit(solution)/shard_map/ppermute | solution.py:42
  14.7 2.3 %copy-start.11 = (f32[10]{0:T(128)}, f32[10]{0:T(128)S(1)}, u32[]{:S(2)}) copy-start(f32[10]{0:T(128)S(1)} %collective-permute-done.9) | copy-start | bytes 124
  15.3 3.5 %collective-permute-start = (f32[10]{0:T(128)S(1)}, f32[10]{0:T(128)S(1)}, u32[]{:S(2)}, u32[]{:S(2)}) collective-permute-start(f32[10]{0:T(128)S(1)} %get-tuple-element.52), channel_id=1, source_target_pairs={{0,4},{4,0},{8,12},{12,8},{16,20},{20,16},{24,28},{28,24},{1,5},{5... | collective-permute-start | bytes 128 | tf_op jit(solution)/shard_map/ppermute | solution.py:42
  19.0 8.6 %collective-permute-start.2 = (f32[10,64,128]{2,1,0:T(8,128)S(1)}, f32[10,64,128]{2,1,0:T(8,128)S(1)}, u32[]{:S(2)}, u32[]{:S(2)}) collective-permute-start(f32[10,64,128]{2,1,0:T(8,128)S(1)} %get-tuple-element.36), channel_id=1, source_target_pairs={{0,8},{4,12},{1,9},{5,13},{2,10},{6,14},{3,11},{7,15}} | collective-permute-start | bytes 983048 | tf_op jit(solution)/shard_map/ppermute | solution.py:62
  27.7 0.7 collective-permute-start.3
  28.5 0.7 collective-permute-start.4
  29.2 1.8 %copy-start.8 = (f32[128,128]{1,0:T(8,128)S(1)}, f32[128,128]{1,0:T(8,128)}, u32[]{:S(2)}) copy-start(f32[128,128]{1,0:T(8,128)} %param.12) | copy-start | bytes 196612
  29.4 7.1 %collective-permute-start.5 = (f32[10,64,128]{2,1,0:T(8,128)S(1)}, f32[10,64,128]{2,1,0:T(8,128)S(1)}, u32[]{:S(2)}, u32[]{:S(2)}) collective-permute-start(f32[10,64,128]{2,1,0:T(8,128)S(1)} %get-tuple-element.48), channel_id=1, source_target_pairs={{0,4},{4,0},{8,12},{12,8},{16,20},{20,16},{24,28},{28,24},{1,5},{5... | collective-permute-start | bytes 983048 | tf_op jit(solution)/shard_map/ppermute | solution.py:82
  40.8 1.4 %copy-start.1 = (f32[128,1280]{1,0:T(8,128)S(1)}, f32[128,1280]{1,0:T(8,128)}, u32[]{:S(2)}) copy-start(f32[128,1280]{1,0:T(8,128)} %param.10) | copy-start | bytes 1966084
  40.8 1.4 %copy-start.10 = (f32[1280]{0:T(1024)S(1)}, f32[1280]{0:T(1024)}, u32[]{:S(2)}) copy-start(f32[1280]{0:T(1024)} %param.16) | copy-start | bytes 15364
  42.2 6.2 %copy-start.2 = (f32[128,1280]{1,0:T(8,128)S(1)}, f32[128,1280]{1,0:T(8,128)}, u32[]{:S(2)}) copy-start(f32[128,1280]{1,0:T(8,128)} %param.17) | copy-start | bytes 1966084
  43.7 1.9 %collective-permute-start.6 = (f32[2,128]{1,0:T(2,128)S(1)}, f32[2,128]{1,0:T(2,128)S(1)}, u32[]{:S(2)}, u32[]{:S(2)}) collective-permute-start(f32[2,128]{1,0:T(2,128)S(1)} %pad_maximum_fusion), channel_id=1, source_target_pairs={{0,1},{1,0},{2,3},{3,2},{4,5},{5,4},{6,7},{7,6},{8,9},{9,8},{10,11... | collective-permute-start | bytes 3080 | tf_op jit(solution)/shard_map/ppermute | solution.py:93
  43.8 3.6 %collective-permute-start.7 = (f32[2,128]{1,0:T(2,128)S(1)}, f32[2,128]{1,0:T(2,128)S(1)}, u32[]{:S(2)}, u32[]{:S(2)}) collective-permute-start(f32[2,128]{1,0:T(2,128)S(1)} %pad_maximum_fusion), channel_id=1, source_target_pairs={{0,2},{1,3},{2,0},{3,1},{4,6},{5,7},{6,4},{7,5},{8,10},{9,11},{10,... | collective-permute-start | bytes 3080 | tf_op jit(solution)/shard_map/ppermute | solution.py:93
  45.4 3.0 %collective-permute-start.8 = (f32[2,128]{1,0:T(2,128)S(1)}, f32[2,128]{1,0:T(2,128)S(1)}, u32[]{:S(2)}, u32[]{:S(2)}) collective-permute-start(f32[2,128]{1,0:T(2,128)S(1)} %pad_maximum_fusion), channel_id=1, source_target_pairs={{0,3},{1,2},{2,1},{3,0},{4,7},{5,6},{6,5},{7,4},{8,11},{9,10},{10,... | collective-permute-start | bytes 3080 | tf_op jit(solution)/shard_map/ppermute | solution.py:93
  52.0 9.8 %collective-permute-start.10 = (f32[10,64,128]{2,1,0:T(8,128)S(1)}, f32[10,64,128]{2,1,0:T(8,128)S(1)}, u32[]{:S(2)}, u32[]{:S(2)}) collective-permute-start(f32[10,64,128]{2,1,0:T(8,128)S(1)} %constant_dynamic-slice_fusion), channel_id=1, source_target_pairs={{28,24},{24,28},{20,16},{16,20},{12,8},{8,12},{4,0},{0,4},{29,25},... | collective-permute-start | bytes 983048 | tf_op jit(solution)/shard_map/ppermute | solution.py:42
  62.6 4.3 %collective-permute-start.11 = (f32[10,64,128]{2,1,0:T(8,128)}, f32[10,64,128]{2,1,0:T(8,128)}, u32[]{:S(2)}, u32[]{:S(2)}) collective-permute-start(f32[10,64,128]{2,1,0:T(8,128)} %get-tuple-element.28), channel_id=1, source_target_pairs={{28,20},{24,16},{29,21},{25,17},{30,22},{26,18},{31,23},{27,19}} | collective-permute-start | bytes 983048 | tf_op jit(solution)/shard_map/ppermute | solution.py:62
  67.1 4.3 %collective-permute-start.12 = (f32[10,64,128]{2,1,0:T(8,128)S(1)}, f32[10,64,128]{2,1,0:T(8,128)S(1)}, u32[]{:S(2)}, u32[]{:S(2)}) collective-permute-start(f32[10,64,128]{2,1,0:T(8,128)S(1)} %multiply_add_fusion.3), channel_id=1, source_target_pairs={{20,12},{16,8},{21,13},{17,9},{22,14},{18,10},{23,15},{19,11}} | collective-permute-start | bytes 983048 | tf_op jit(solution)/shard_map/ppermute | solution.py:62
  69.5 37.5 %collective-permute-start.18 = (f32[128,128]{1,0:T(8,128)S(1)}, f32[128,128]{1,0:T(8,128)S(1)}, u32[]{:S(2)}, u32[]{:S(2)}) collective-permute-start(f32[128,128]{1,0:T(8,128)S(1)} %fusion.16), channel_id=1, source_target_pairs={{0,1},{1,0},{2,3},{3,2},{4,5},{5,4},{6,7},{7,6},{8,9},{9,8},{10,11... | collective-permute-start | bytes 196616 | tf_op jit(solution)/shard_map/ppermute | solution.py:93
  69.5 37.5 %collective-permute-start.19 = (f32[128,128]{1,0:T(8,128)S(1)}, f32[128,128]{1,0:T(8,128)S(1)}, u32[]{:S(2)}, u32[]{:S(2)}) collective-permute-start(f32[128,128]{1,0:T(8,128)S(1)} %fusion.16), channel_id=1, source_target_pairs={{0,2},{1,3},{2,0},{3,1},{4,6},{5,7},{6,4},{7,5},{8,10},{9,11},{10,... | collective-permute-start | bytes 196616 | tf_op jit(solution)/shard_map/ppermute | solution.py:93
  70.1 36.9 %collective-permute-start.20 = (f32[128,128]{1,0:T(8,128)S(1)}, f32[128,128]{1,0:T(8,128)S(1)}, u32[]{:S(2)}, u32[]{:S(2)}) collective-permute-start(f32[128,128]{1,0:T(8,128)S(1)} %fusion.16), channel_id=1, source_target_pairs={{0,3},{1,2},{2,1},{3,0},{4,7},{5,6},{6,5},{7,4},{8,11},{9,10},{10,... | collective-permute-start | bytes 196616 | tf_op jit(solution)/shard_map/ppermute | solution.py:93
  71.5 33.6 %collective-permute-start.13 = (f32[10,64,128]{2,1,0:T(8,128)S(1)}, f32[10,64,128]{2,1,0:T(8,128)S(1)}, u32[]{:S(2)}, u32[]{:S(2)}) collective-permute-start(f32[10,64,128]{2,1,0:T(8,128)S(1)} %get-tuple-element.26), channel_id=1, source_target_pairs={{12,4},{8,0},{13,5},{9,1},{14,6},{10,2},{15,7},{11,3}} | collective-permute-start | bytes 983048 | tf_op jit(solution)/shard_map/ppermute | solution.py:59
  73.1 32.0 %copy-start.5 = (f32[10,64,128]{2,1,0:T(8,128)S(1)}, f32[10,64,128]{2,1,0:T(8,128)}, u32[]{:S(2)}) copy-start(f32[10,64,128]{2,1,0:T(8,128)} %copy-done.4) | copy-start | bytes 983044
  73.1 32.0 %copy-start.12 = (f32[10]{0:T(128)S(1)}, f32[10]{0:T(128)}, u32[]{:S(2)}) copy-start(f32[10]{0:T(128)} %copy-done.11) | copy-start | bytes 124
  73.1 32.0 %copy-start.13 = (f32[10]{0:T(128)S(1)}, f32[10]{0:T(128)}, u32[]{:S(2)}) copy-start(f32[10]{0:T(128)} %get-tuple-element.33) | copy-start | bytes 124
  105.3 7.1 %collective-permute-start.14 = (f32[10,64,128]{2,1,0:T(8,128)S(1)}, f32[10,64,128]{2,1,0:T(8,128)S(1)}, u32[]{:S(2)}, u32[]{:S(2)}) collective-permute-start(f32[10,64,128]{2,1,0:T(8,128)S(1)} %get-tuple-element.46), channel_id=1, source_target_pairs={{28,24},{24,28},{20,16},{16,20},{12,8},{8,12},{4,0},{0,4},{29,25},... | collective-permute-start | bytes 983048 | tf_op jit(solution)/shard_map/ppermute | solution.py:82
  112.4 3.2 %copy-start.3 = (f32[10,64,128]{2,1,0:T(8,128)}, f32[10,64,128]{2,1,0:T(8,128)S(1)}, u32[]{:S(2)}) copy-start(f32[10,64,128]{2,1,0:T(8,128)S(1)} %collective-permute-done.14) | copy-start | bytes 983044
  113.7 2.4 %copy-start.15 = (f32[20]{0:T(128)S(1)}, f32[20]{0:T(128)}, u32[]{:S(2)}) copy-start(f32[20]{0:T(128)} %param.15) | copy-start | bytes 244
  113.7 7.9 %collective-permute-start.15 = (f32[128,128]{1,0:T(8,128)S(1)}, f32[128,128]{1,0:T(8,128)S(1)}, u32[]{:S(2)}, u32[]{:S(2)}) collective-permute-start(f32[128,128]{1,0:T(8,128)S(1)} %fusion.15), channel_id=1, source_target_pairs={{0,1},{1,0},{2,3},{3,2},{4,5},{5,4},{6,7},{7,6},{8,9},{9,8},{10,11... | collective-permute-start | bytes 196616 | tf_op jit(solution)/shard_map/ppermute | solution.py:93
  113.8 7.8 %collective-permute-start.16 = (f32[128,128]{1,0:T(8,128)S(1)}, f32[128,128]{1,0:T(8,128)}, u32[]{:S(2)}, u32[]{:S(2)}) collective-permute-start(f32[128,128]{1,0:T(8,128)S(1)} %fusion.15), channel_id=1, source_target_pairs={{0,2},{1,3},{2,0},{3,1},{4,6},{5,7},{6,4},{7,5},{8,10},{9,11},{10,... | collective-permute-start | bytes 196616 | tf_op jit(solution)/shard_map/ppermute | solution.py:93
  114.1 7.4 %collective-permute-start.17 = (f32[128,128]{1,0:T(8,128)S(1)}, f32[128,128]{1,0:T(8,128)}, u32[]{:S(2)}, u32[]{:S(2)}) collective-permute-start(f32[128,128]{1,0:T(8,128)S(1)} %fusion.15), channel_id=1, source_target_pairs={{0,3},{1,2},{2,1},{3,0},{4,7},{5,6},{6,5},{7,4},{8,11},{9,10},{10,... | collective-permute-start | bytes 196616 | tf_op jit(solution)/shard_map/ppermute | solution.py:93
  (5 other events, 4.9 us)

commit v9 on v4

--- a/solution.py
+++ b/solution.py
@@ -7,7 +7,7 @@
 
 
 eps = 1e-05
-highest = lax.Precision.HIGHEST
+highest = lax.Precision.HIGH
 
 
 def combine(earlier, later):
@@ -148,7 +148,7 @@
         lax.broadcasted_iota(jnp.int32, (length, length), 0)
         <= lax.broadcasted_iota(jnp.int32, (length, length), 1)
     ).astype(decay_in.dtype)
-    return jnp.dot(decay_in, upper, precision=highest)
+    return jnp.dot(decay_in, upper, precision=lax.Precision.HIGHEST)
 
 
 def within_part(feat_in, step_in, decay_in, writes, read_in, skip_scale):

time: 121 us -> 118 us (0.975)
  matrix products: 18.7 us -> 13.6 us
  waiting for transfers between devices: 64.2 us -> 66.5 us
    dot_general x3, matrix products: 8.92 us -> 6.02 us  [within_part(): within = jnp.einsum('hij,jhp->ihp', masked, scaled, precision=highest)]
    ppermute x2, waiting for transfers between devices: 28.2 us -> 30.4 us  [pair_scan(): s_in = lax.ppermute(out[1], axis, pairs)]
  transfers between devices with their start and end apart: 20 -> 20, of which waited for: 13 -> 13; matrix products, arithmetic and copies ran while one was open for 10% -> 8% of each run, Pallas kernels for 0% -> 0%
where the time goes in v9:
time: 118 us
  waiting for transfers between devices  66.5 us (56%)
  starting transfers between devices  22.3 us (19%)
  matrix products  13.6 us (12%)
  other arithmetic  7.83 us (7%)
  local copies, waits for them, and re-layouts  6.44 us (5%)
    ppermute x2, waiting for transfers between devices, pair_scan(): s_in = lax.ppermute(out[1], axis, pairs)  30.4 us
    ppermute x4, waiting for transfers between devices, pair_scan(): a_rcv, s_rcv = lax.ppermute((a_snd, s_snd), axis, swap)  16.3 us
    ppermute x8, waiting for transfers between devices, butterfly_psum(): got = lax.ppermute(parts, axis, [(i, i ^ k) for i in range(count)])  9.28 us
    ppermute x4, starting transfers between devices, pair_scan(): a_in, s_in = lax.ppermute(out, axis, pairs)  6.49 us
    ppermute x4, starting transfers between devices, pair_scan(): a_rcv, s_rcv = lax.ppermute((a_snd, s_snd), axis, swap)  6.36 us
    dot_general x3, matrix products, within_part(): within = jnp.einsum('hij,jhp->ihp', masked, scaled, precision=highest)  6.02 us
    ppermute x2, waiting for transfers between devices, pair_scan(): other = lax.ppermute(send, axis, swap)  5.67 us
    ppermute x4, waiting for transfers between devices, pair_scan(): a_in, s_in = lax.ppermute(out, axis, pairs)  4.83 us
  transfers between devices with their start and end apart: 20, of which 13 were waited for; matrix products, arithmetic and copies ran while one was open for 8% of the time, Pallas kernels for 0%

profile of v9, /device:TPU:0, one launch (start us, length us, event | category | flops | bytes accessed | tf_op | source)
XLA Modules:
  0.0 117.8 jit_solution(14149974543354514381)
XLA Ops:
  0.7 0.9 fusion.60
  1.8 1.3 %copy.22 = f32[128,1280]{0,1:T(8,128)S(1)} copy(f32[128,1280]{1,0:T(8,128)} %param.9) | data formatting | bytes 1310720 | tf_op args[0]
  3.6 3.0 %collective-permute-start.1 = (f32[10,64,128]{2,1,0:T(8,128)S(1)}, f32[10,64,128]{2,1,0:T(8,128)S(1)}, u32[]{:S(2)}, u32[]{:S(2)}) collective-permute-start(f32[10,64,128]{2,1,0:T(8,128)S(1)} %constant_dynamic-slice_fusion.1), channel_id=1, source_target_pairs={{0,4},{4,0},{8,12},{12,8},{16,20},{20,16},{24,28},{28,24},{1,5},{5... | collective-permute-start | bytes 983048 | tf_op jit(solution)/shard_map/ppermute | solution.py:42
  6.8 7.6 %collective-permute-done.10 = f32[10]{0:T(128)S(1)} collective-permute-done((f32[10]{0:T(128)S(1)}, f32[10]{0:T(128)S(1)}, u32[]{:S(2)}, u32[]{:S(2)}) %collective-permute-start.10) | collective-permute-done | bytes 72 | tf_op jit(solution)/shard_map/ppermute | solution.py:42
  15.0 1.7 %collective-permute-start = (f32[10]{0:T(128)S(1)}, f32[10]{0:T(128)S(1)}, u32[]{:S(2)}, u32[]{:S(2)}) collective-permute-start(f32[10]{0:T(128)S(1)} %get-tuple-element.54), channel_id=1, source_target_pairs={{0,4},{4,0},{8,12},{12,8},{16,20},{20,16},{24,28},{28,24},{1,5},{5... | collective-permute-start | bytes 128 | tf_op jit(solution)/shard_map/ppermute | solution.py:42
  16.8 1.8 %collective-permute-done = f32[10]{0:T(128)S(1)} collective-permute-done((f32[10]{0:T(128)S(1)}, f32[10]{0:T(128)S(1)}, u32[]{:S(2)}, u32[]{:S(2)}) %collective-permute-start) | collective-permute-done | bytes 72 | tf_op jit(solution)/shard_map/ppermute | solution.py:42
  18.8 3.7 %collective-permute-start.2 = (f32[10,64,128]{2,1,0:T(8,128)S(1)}, f32[10,64,128]{2,1,0:T(8,128)S(1)}, u32[]{:S(2)}, u32[]{:S(2)}) collective-permute-start(f32[10,64,128]{2,1,0:T(8,128)S(1)} %get-tuple-element.38), channel_id=1, source_target_pairs={{0,8},{4,12},{1,9},{5,13},{2,10},{6,14},{3,11},{7,15}} | collective-permute-start | bytes 983048 | tf_op jit(solution)/shard_map/ppermute | solution.py:62
  22.5 4.8 %collective-permute-done.2 = f32[10,64,128]{2,1,0:T(8,128)S(1)} collective-permute-done((f32[10,64,128]{2,1,0:T(8,128)S(1)}, f32[10,64,128]{2,1,0:T(8,128)S(1)}, u32[]{:S(2)}, u32[]{:S(2)}) %collective-permute-start.2) | collective-permute-done | bytes 327712 | tf_op jit(solution)/shard_map/ppermute | solution.py:62
  29.1 1.6 %collective-permute-start.5 = (f32[10,64,128]{2,1,0:T(8,128)S(1)}, f32[10,64,128]{2,1,0:T(8,128)S(1)}, u32[]{:S(2)}, u32[]{:S(2)}) collective-permute-start(f32[10,64,128]{2,1,0:T(8,128)S(1)} %get-tuple-element.50), channel_id=1, source_target_pairs={{0,4},{4,0},{8,12},{12,8},{16,20},{20,16},{24,28},{28,24},{1,5},{5... | collective-permute-start | bytes 983048 | tf_op jit(solution)/shard_map/ppermute | solution.py:82
  30.9 5.3 %collective-permute-done.5 = f32[10,64,128]{2,1,0:T(8,128)S(1)} collective-permute-done((f32[10,64,128]{2,1,0:T(8,128)S(1)}, f32[10,64,128]{2,1,0:T(8,128)S(1)}, u32[]{:S(2)}, u32[]{:S(2)}) %collective-permute-start.5) | collective-permute-done | bytes 327712 | tf_op jit(solution)/shard_map/ppermute | solution.py:82
  37.0 2.3 %multiply_add_fusion.1 = f32[128,20,64]{0,2,1:T(8,128)} fusion(f32[128,20,64]{0,2,1:T(8,128)S(1)} %convolution_bitcast_fusion.1, f32[128,20,64]{0,2,1:T(8,128)S(1)} %bitcast.73, f32[128,128]{1,0:T(8,128)S(1)} %fusion.86, f32[20,128]{1,0:T(8,128)S(1)} %bitcast.85, pred[128,128]{1,0:T(8,128)(4,1)S(1)} %iota_compare_fusion.6, ...), kind=kOutput, calls=%fused_computation.35 | convolution fusion | flops 127959040 | bytes 2078800 | tf_op jit(solution)/shard_map/jvp(hij,jhp->ihp)/dot_general | solution.py:167
  39.3 1.4 %copy.23 = f32[128,1280]{1,0:T(8,128)S(1)} copy(f32[128,1280]{0,1:T(8,128)} %bitcast.83) | data formatting | bytes 1310720 | tf_op jit(solution)/shard_map/add | solution.py:226
  40.7 1.5 %multiply_reduce_fusion.7 = (f32[128]{0:T(128)S(1)}, f32[128]{0:T(128)S(1)}) fusion(f32[128,1280]{1,0:T(8,128)S(1)} %copy.23, f32[128,1280]{1,0:T(8,128)S(1)} %copy-done.1, f32[128,1280]{1,0:T(8,128)} %param.17, f32[1280]{0:T(1024)S(1)} %copy-done.11), kind=kLoop, calls=%fused_computation.32 | loop fusion | flops 1638144 | bytes 1972224 | tf_op jit(solution)/shard_map/reduce_sum | solution.py:243
  43.4 1.5 %collective-permute-start.7 = (f32[128]{0:T(128)S(1)}, f32[128]{0:T(128)S(1)}, u32[]{:S(2)}, u32[]{:S(2)}) collective-permute-start(f32[128]{0:T(128)S(1)} %add.147), channel_id=1, source_target_pairs={{0,2},{1,3},{2,0},{3,1},{4,6},{5,7},{6,4},{7,5},{8,10},{9,11},{10,... | collective-permute-start | bytes 1544 | tf_op jit(solution)/shard_map/ppermute | solution.py:94
  45.4 1.5 %collective-permute-done.7 = f32[128]{0:T(128)S(1)} collective-permute-done((f32[128]{0:T(128)S(1)}, f32[128]{0:T(128)S(1)}, u32[]{:S(2)}, u32[]{:S(2)}) %collective-permute-start.7) | collective-permute-done | bytes 544 | tf_op jit(solution)/shard_map/ppermute | solution.py:94
  47.0 1.5 %collective-permute-done.9 = f32[128]{0:T(128)S(1)} collective-permute-done((f32[128]{0:T(128)S(1)}, f32[128]{0:T(128)S(1)}, u32[]{:S(2)}, u32[]{:S(2)}) %collective-permute-start.9) | collective-permute-done | bytes 544 | tf_op jit(solution)/shard_map/ppermute | solution.py:94
  48.5 1.5 %add_multiply_fusion = (f32[128,1280]{1,0:T(8,128)}, f32[128,1280]{1,0:T(8,128)}) fusion(f32[128,1280]{1,0:T(8,128)S(1)} %copy-done.1, f32[128,1280]{1,0:T(8,128)S(1)} %copy.23, f32[128]{0:T(128)S(1)} %get-tuple-element.34, f32[128,1280]{1,0:T(8,128)S(1)} %copy-done.2, f32[1280]{0:T(1024)S(1)} %copy-done.11, f32[128]{0:T(128)S(1)} %get-tuple-element.35), kind=kLoop, calls=%fused_computation.28 | loop fusion | flops 2621440 | bytes 3282944 | tf_op jit(solution)/shard_map/mul | solution.py:251
  50.0 1.3 %copy.24 = f32[128,1280]{0,1:T(8,128)S(1)} copy(f32[128,1280]{1,0:T(8,128)} %get-tuple-element.45) | data formatting | bytes 1310720 | tf_op jit(solution)/shard_map/mul | solution.py:250
  51.8 1.6 %collective-permute-start.11 = (f32[10,64,128]{2,1,0:T(8,128)S(1)}, f32[10,64,128]{2,1,0:T(8,128)S(1)}, u32[]{:S(2)}, u32[]{:S(2)}) collective-permute-start(f32[10,64,128]{2,1,0:T(8,128)S(1)} %constant_dynamic-slice_fusion), channel_id=1, source_target_pairs={{28,24},{24,28},{20,16},{16,20},{12,8},{8,12},{4,0},{0,4},{29,25},... | collective-permute-start | bytes 983048 | tf_op jit(solution)/shard_map/ppermute | solution.py:42
  53.3 6.9 %collective-permute-done.11 = f32[10,64,128]{2,1,0:T(8,128)S(1)} collective-permute-done((f32[10,64,128]{2,1,0:T(8,128)S(1)}, f32[10,64,128]{2,1,0:T(8,128)S(1)}, u32[]{:S(2)}, u32[]{:S(2)}) %collective-permute-start.11) | collective-permute-done | bytes 327712 | tf_op jit(solution)/shard_map/ppermute | solution.py:42
  60.2 0.8 broadcast_add_fusion
  61.1 1.4 %collective-permute-start.12 = (f32[10,64,128]{2,1,0:T(8,128)}, f32[10,64,128]{2,1,0:T(8,128)}, u32[]{:S(2)}, u32[]{:S(2)}) collective-permute-start(f32[10,64,128]{2,1,0:T(8,128)} %get-tuple-element.28), channel_id=1, source_target_pairs={{28,20},{24,16},{29,21},{25,17},{30,22},{26,18},{31,23},{27,19}} | collective-permute-start | bytes 983048 | tf_op jit(solution)/shard_map/ppermute | solution.py:62
  63.2 2.0 %fusion.19 = (f32[20,128]{1,0:T(8,128)S(1)}, f32[20,128]{1,0:T(8,128)S(1)}, f32[128,128]{1,0:T(8,128)S(1)}) fusion(f32[128,128]{1,0:T(8,128)S(1)} %fusion.86, f32[20,128]{1,0:T(8,128)S(1)} %bitcast.86, pred[128,128]{1,0:T(8,128)(4,1)S(1)} %iota_compare_fusion.6, f32[20,64,128]{2,1,0:T(8,128)S(1)} %bitcast.78, f32[128,20,64]{0,2,1:T(8,128)S(1)} %bitcast.74, ...), kind=kOutput, calls=%fused_computation.20 | convolution fusion | flops 129575936 | bytes 1499136 | tf_op jit(solution)/shard_map/transpose(jvp(hij,jhp->ihp))/dot_general | solution.py:167
  65.5 1.5 %collective-permute-start.14 = (f32[10,64,128]{2,1,0:T(8,128)S(1)}, f32[10,64,128]{2,1,0:T(8,128)S(1)}, u32[]{:S(2)}, u32[]{:S(2)}) collective-permute-start(f32[10,64,128]{2,1,0:T(8,128)S(1)} %get-tuple-element.26), channel_id=1, source_target_pairs={{12,4},{8,0},{13,5},{9,1},{14,6},{10,2},{15,7},{11,3}} | collective-permute-start | bytes 983048 | tf_op jit(solution)/shard_map/ppermute | solution.py:59
  67.8 1.8 %fusion.12 = f32[128,20,64]{0,2,1:T(8,128)} fusion(f32[20,64,128]{2,1,0:T(8,128)S(1)} %bitcast.80, f32[128,128]{1,0:T(8,128)S(1)} %fusion.86, f32[20,128]{1,0:T(8,128)S(1)} %bitcast.87, pred[128,128]{1,0:T(8,128)(4,1)S(1)} %iota_compare_fusion.6), kind=kOutput, calls=%fused_computation.11 | convolution fusion | flops 127139840 | bytes 1402880 | tf_op jit(solution)/shard_map/transpose(jvp(hij,jhp->ihp))/dot_general | solution.py:167
  69.6 30.4 %collective-permute-done.14 = f32[10,64,128]{2,1,0:T(8,128)S(1)} collective-permute-done((f32[10,64,128]{2,1,0:T(8,128)S(1)}, f32[10,64,128]{2,1,0:T(8,128)S(1)}, u32[]{:S(2)}, u32[]{:S(2)}) %collective-permute-start.14) | collective-permute-done | bytes 327712 | tf_op jit(solution)/shard_map/ppermute | solution.py:59
  100.1 1.6 %collective-permute-start.15 = (f32[10,64,128]{2,1,0:T(8,128)S(1)}, f32[10,64,128]{2,1,0:T(8,128)S(1)}, u32[]{:S(2)}, u32[]{:S(2)}) collective-permute-start(f32[10,64,128]{2,1,0:T(8,128)S(1)} %get-tuple-element.48), channel_id=1, source_target_pairs={{28,24},{24,28},{20,16},{16,20},{12,8},{8,12},{4,0},{0,4},{29,25},... | collective-permute-start | bytes 983048 | tf_op jit(solution)/shard_map/ppermute | solution.py:82
  102.8 3.5 %collective-permute-done.19 = f32[128,128]{1,0:T(8,128)S(1)} collective-permute-done((f32[128,128]{1,0:T(8,128)S(1)}, f32[128,128]{1,0:T(8,128)S(1)}, u32[]{:S(2)}, u32[]{:S(2)}) %collective-permute-start.19) | collective-permute-done | bytes 65568 | tf_op jit(solution)/shard_map/ppermute | solution.py:94
  108.2 2.0 %multiply_reduce_fusion.2 = (f32[128,20]{0,1:T(8,128)S(1)}, f32[128,20]{0,1:T(8,128)S(1)}, f32[128,20]{0,1:T(8,128)S(1)}, f32[128,20,64]{0,2,1:T(8,128)S(1)}, f32[128,20]{0,1:T(8,128)S(1)}) fusion(f32[128,20,64]{0,2,1:T(8,128)S(1)} %bitcast.75, f32[128,20]{0,1:T(8,128)S(1)} %bitcast.92, f32[128,20]{0,1:T(8,128)S(1)} %get-tuple-element.53, ...), kind=kOutput, calls=%fused_computation.24 | convolution fusion | flops 128768000 | bytes 4059217 | tf_op jit(solution)/shard_map/transpose(jvp(jhp,jn->hpn))/dot_general | solution.py:186
  113.5 0.8 fusion.17
  114.3 1.1 copy.28
  115.4 1.7 %collective-permute-done.17 = f32[128,128]{1,0:T(8,128)S(1)} collective-permute-done((f32[128,128]{1,0:T(8,128)S(1)}, f32[128,128]{1,0:T(8,128)S(1)}, u32[]{:S(2)}, u32[]{:S(2)}) %collective-permute-start.17) | collective-permute-done | bytes 65568 | tf_op jit(solution)/shard_map/ppermute | solution.py:94
  (95 shorter events, 15.3 us)
Async XLA Ops:
  0.6 2.5 %copy-start = (f32[128,128]{1,0:T(8,128)S(1)}, f32[128,128]{1,0:T(8,128)}, u32[]{:S(2)}) copy-start(f32[128,128]{1,0:T(8,128)} %param.11) | copy-start | bytes 196612
  1.8 1.4 %copy-start.10 = (f32[20,128]{1,0:T(8,128)S(1)}, f32[20,128]{1,0:T(8,128)}, u32[]{:S(2)}) copy-start(f32[20,128]{1,0:T(8,128)} %param.13) | copy-start | bytes 30724
  3.6 15.0 %collective-permute-start.1 = (f32[10,64,128]{2,1,0:T(8,128)S(1)}, f32[10,64,128]{2,1,0:T(8,128)S(1)}, u32[]{:S(2)}, u32[]{:S(2)}) collective-permute-start(f32[10,64,128]{2,1,0:T(8,128)S(1)} %constant_dynamic-slice_fusion.1), channel_id=1, source_target_pairs={{0,4},{4,0},{8,12},{12,8},{16,20},{20,16},{24,28},{28,24},{1,5},{5... | collective-permute-start | bytes 983048 | tf_op jit(solution)/shard_map/ppermute | solution.py:42
  6.7 7.7 %collective-permute-start.10 = (f32[10]{0:T(128)S(1)}, f32[10]{0:T(128)S(1)}, u32[]{:S(2)}, u32[]{:S(2)}) collective-permute-start(f32[10]{0:T(128)S(1)} %dynamic_slice.29), channel_id=1, source_target_pairs={{28,24},{24,28},{20,16},{16,20},{12,8},{8,12},{4,0},{0,4},{29,25},... | collective-permute-start | bytes 128 | tf_op jit(solution)/shard_map/ppermute | solution.py:42
  14.4 2.3 %copy-start.12 = (f32[10]{0:T(128)}, f32[10]{0:T(128)S(1)}, u32[]{:S(2)}) copy-start(f32[10]{0:T(128)S(1)} %collective-permute-done.10) | copy-start | bytes 124
  15.0 3.5 %collective-permute-start = (f32[10]{0:T(128)S(1)}, f32[10]{0:T(128)S(1)}, u32[]{:S(2)}, u32[]{:S(2)}) collective-permute-start(f32[10]{0:T(128)S(1)} %get-tuple-element.54), channel_id=1, source_target_pairs={{0,4},{4,0},{8,12},{12,8},{16,20},{20,16},{24,28},{28,24},{1,5},{5... | collective-permute-start | bytes 128 | tf_op jit(solution)/shard_map/ppermute | solution.py:42
  18.8 8.6 %collective-permute-start.2 = (f32[10,64,128]{2,1,0:T(8,128)S(1)}, f32[10,64,128]{2,1,0:T(8,128)S(1)}, u32[]{:S(2)}, u32[]{:S(2)}) collective-permute-start(f32[10,64,128]{2,1,0:T(8,128)S(1)} %get-tuple-element.38), channel_id=1, source_target_pairs={{0,8},{4,12},{1,9},{5,13},{2,10},{6,14},{3,11},{7,15}} | collective-permute-start | bytes 983048 | tf_op jit(solution)/shard_map/ppermute | solution.py:62
  27.5 0.7 collective-permute-start.3
  28.3 0.7 collective-permute-start.4
  29.0 1.7 %copy-start.9 = (f32[128,128]{1,0:T(8,128)S(1)}, f32[128,128]{1,0:T(8,128)}, u32[]{:S(2)}) copy-start(f32[128,128]{1,0:T(8,128)} %param.12) | copy-start | bytes 196612
  29.1 7.1 %collective-permute-start.5 = (f32[10,64,128]{2,1,0:T(8,128)S(1)}, f32[10,64,128]{2,1,0:T(8,128)S(1)}, u32[]{:S(2)}, u32[]{:S(2)}) collective-permute-start(f32[10,64,128]{2,1,0:T(8,128)S(1)} %get-tuple-element.50), channel_id=1, source_target_pairs={{0,4},{4,0},{8,12},{12,8},{16,20},{20,16},{24,28},{28,24},{1,5},{5... | collective-permute-start | bytes 983048 | tf_op jit(solution)/shard_map/ppermute | solution.py:82
  39.3 1.4 %copy-start.1 = (f32[128,1280]{1,0:T(8,128)S(1)}, f32[128,1280]{1,0:T(8,128)}, u32[]{:S(2)}) copy-start(f32[128,1280]{1,0:T(8,128)} %param.10) | copy-start | bytes 1966084
  39.3 1.4 %copy-start.11 = (f32[1280]{0:T(1024)S(1)}, f32[1280]{0:T(1024)}, u32[]{:S(2)}) copy-start(f32[1280]{0:T(1024)} %param.16) | copy-start | bytes 15364
  40.7 7.8 %copy-start.2 = (f32[128,1280]{1,0:T(8,128)S(1)}, f32[128,1280]{1,0:T(8,128)}, u32[]{:S(2)}) copy-start(f32[128,1280]{1,0:T(8,128)} %param.17) | copy-start | bytes 1966084
  42.2 1.2 %collective-permute-start.6 = (f32[128]{0:T(128)S(1)}, f32[128]{0:T(128)S(1)}, u32[]{:S(2)}, u32[]{:S(2)}) collective-permute-start(f32[128]{0:T(128)S(1)} %get-tuple-element.23), channel_id=1, source_target_pairs={{0,1},{1,0},{2,3},{3,2},{4,5},{5,4},{6,7},{7,6},{8,9},{9,8},{10,11... | collective-permute-start | bytes 1544 | tf_op jit(solution)/shard_map/ppermute | solution.py:94
  42.3 2.6 %collective-permute-start.8 = (f32[128]{0:T(128)S(1)}, f32[128]{0:T(128)S(1)}, u32[]{:S(2)}, u32[]{:S(2)}) collective-permute-start(f32[128]{0:T(128)S(1)} %get-tuple-element.24), channel_id=1, source_target_pairs={{0,1},{1,0},{2,3},{3,2},{4,5},{5,4},{6,7},{7,6},{8,9},{9,8},{10,11... | collective-permute-start | bytes 1544 | tf_op jit(solution)/shard_map/ppermute | solution.py:94
  43.4 3.5 %collective-permute-start.7 = (f32[128]{0:T(128)S(1)}, f32[128]{0:T(128)S(1)}, u32[]{:S(2)}, u32[]{:S(2)}) collective-permute-start(f32[128]{0:T(128)S(1)} %add.147), channel_id=1, source_target_pairs={{0,2},{1,3},{2,0},{3,1},{4,6},{5,7},{6,4},{7,5},{8,10},{9,11},{10,... | collective-permute-start | bytes 1544 | tf_op jit(solution)/shard_map/ppermute | solution.py:94
  44.9 3.5 %collective-permute-start.9 = (f32[128]{0:T(128)S(1)}, f32[128]{0:T(128)S(1)}, u32[]{:S(2)}, u32[]{:S(2)}) collective-permute-start(f32[128]{0:T(128)S(1)} %add.151), channel_id=1, source_target_pairs={{0,2},{1,3},{2,0},{3,1},{4,6},{5,7},{6,4},{7,5},{8,10},{9,11},{10,... | collective-permute-start | bytes 1544 | tf_op jit(solution)/shard_map/ppermute | solution.py:94
  51.8 8.5 %collective-permute-start.11 = (f32[10,64,128]{2,1,0:T(8,128)S(1)}, f32[10,64,128]{2,1,0:T(8,128)S(1)}, u32[]{:S(2)}, u32[]{:S(2)}) collective-permute-start(f32[10,64,128]{2,1,0:T(8,128)S(1)} %constant_dynamic-slice_fusion), channel_id=1, source_target_pairs={{28,24},{24,28},{20,16},{16,20},{12,8},{8,12},{4,0},{0,4},{29,25},... | collective-permute-start | bytes 983048 | tf_op jit(solution)/shard_map/ppermute | solution.py:42
  61.1 1.4 %collective-permute-start.12 = (f32[10,64,128]{2,1,0:T(8,128)}, f32[10,64,128]{2,1,0:T(8,128)}, u32[]{:S(2)}, u32[]{:S(2)}) collective-permute-start(f32[10,64,128]{2,1,0:T(8,128)} %get-tuple-element.28), channel_id=1, source_target_pairs={{28,20},{24,16},{29,21},{25,17},{30,22},{26,18},{31,23},{27,19}} | collective-permute-start | bytes 983048 | tf_op jit(solution)/shard_map/ppermute | solution.py:62
  62.6 2.8 %collective-permute-start.13 = (f32[10,64,128]{2,1,0:T(8,128)S(1)}, f32[10,64,128]{2,1,0:T(8,128)S(1)}, u32[]{:S(2)}, u32[]{:S(2)}) collective-permute-start(f32[10,64,128]{2,1,0:T(8,128)S(1)} %multiply_add_fusion.3), channel_id=1, source_target_pairs={{20,12},{16,8},{21,13},{17,9},{22,14},{18,10},{23,15},{19,11}} | collective-permute-start | bytes 983048 | tf_op jit(solution)/shard_map/ppermute | solution.py:62
  65.4 1.6 %copy-start.8 = (f32[10,64,128]{2,1,0:T(8,128)S(1)}, f32[10,64,128]{2,1,0:T(8,128)}, u32[]{:S(2)}) copy-start(f32[10,64,128]{2,1,0:T(8,128)} %copy-done.7) | copy-start | bytes 983044
  65.5 34.5 %collective-permute-start.14 = (f32[10,64,128]{2,1,0:T(8,128)S(1)}, f32[10,64,128]{2,1,0:T(8,128)S(1)}, u32[]{:S(2)}, u32[]{:S(2)}) collective-permute-start(f32[10,64,128]{2,1,0:T(8,128)S(1)} %get-tuple-element.26), channel_id=1, source_target_pairs={{12,4},{8,0},{13,5},{9,1},{14,6},{10,2},{15,7},{11,3}} | collective-permute-start | bytes 983048 | tf_op jit(solution)/shard_map/ppermute | solution.py:59
  67.7 32.2 %copy-start.6 = (f32[10,64,128]{2,1,0:T(8,128)S(1)}, f32[10,64,128]{2,1,0:T(8,128)}, u32[]{:S(2)}) copy-start(f32[10,64,128]{2,1,0:T(8,128)} %copy-done.5) | copy-start | bytes 983044
  67.7 32.2 %copy-start.13 = (f32[10]{0:T(128)S(1)}, f32[10]{0:T(128)}, u32[]{:S(2)}) copy-start(f32[10]{0:T(128)} %copy-done.12) | copy-start | bytes 124
  67.8 32.2 %copy-start.14 = (f32[10]{0:T(128)S(1)}, f32[10]{0:T(128)}, u32[]{:S(2)}) copy-start(f32[10]{0:T(128)} %get-tuple-element.33) | copy-start | bytes 124
  67.8 34.2 %collective-permute-start.18 = (f32[128,128]{1,0:T(8,128)S(1)}, f32[128,128]{1,0:T(8,128)S(1)}, u32[]{:S(2)}, u32[]{:S(2)}) collective-permute-start(f32[128,128]{1,0:T(8,128)S(1)} %fusion.16), channel_id=1, source_target_pairs={{0,1},{1,0},{2,3},{3,2},{4,5},{5,4},{6,7},{7,6},{8,9},{9,8},{10,11... | collective-permute-start | bytes 196616 | tf_op jit(solution)/shard_map/ppermute | solution.py:94
  100.1 7.1 %collective-permute-start.15 = (f32[10,64,128]{2,1,0:T(8,128)S(1)}, f32[10,64,128]{2,1,0:T(8,128)S(1)}, u32[]{:S(2)}, u32[]{:S(2)}) collective-permute-start(f32[10,64,128]{2,1,0:T(8,128)S(1)} %get-tuple-element.48), channel_id=1, source_target_pairs={{28,24},{24,28},{20,16},{16,20},{12,8},{8,12},{4,0},{0,4},{29,25},... | collective-permute-start | bytes 983048 | tf_op jit(solution)/shard_map/ppermute | solution.py:82
  102.0 4.3 %collective-permute-start.19 = (f32[128,128]{1,0:T(8,128)S(1)}, f32[128,128]{1,0:T(8,128)S(1)}, u32[]{:S(2)}, u32[]{:S(2)}) collective-permute-start(f32[128,128]{1,0:T(8,128)S(1)} %add.169), channel_id=1, source_target_pairs={{0,2},{1,3},{2,0},{3,1},{4,6},{5,7},{6,4},{7,5},{8,10},{9,11},{10,... | collective-permute-start | bytes 196616 | tf_op jit(solution)/shard_map/ppermute | solution.py:94
  108.2 2.5 %copy-start.4 = (f32[10,64,128]{2,1,0:T(8,128)S(1)}, f32[10,64,128]{2,1,0:T(8,128)}, u32[]{:S(2)}) copy-start(f32[10,64,128]{2,1,0:T(8,128)} %copy-done.3) | copy-start | bytes 983044
  111.5 1.3 %collective-permute-start.16 = (f32[128,128]{1,0:T(8,128)S(1)}, f32[128,128]{1,0:T(8,128)S(1)}, u32[]{:S(2)}, u32[]{:S(2)}) collective-permute-start(f32[128,128]{1,0:T(8,128)S(1)} %fusion.15), channel_id=1, source_target_pairs={{0,1},{1,0},{2,3},{3,2},{4,5},{5,4},{6,7},{7,6},{8,9},{9,8},{10,11... | collective-permute-start | bytes 196616 | tf_op jit(solution)/shard_map/ppermute | solution.py:94
  112.8 4.3 %collective-permute-start.17 = (f32[128,128]{1,0:T(8,128)S(1)}, f32[128,128]{1,0:T(8,128)S(1)}, u32[]{:S(2)}, u32[]{:S(2)}) collective-permute-start(f32[128,128]{1,0:T(8,128)S(1)} %add.166), channel_id=1, source_target_pairs={{0,2},{1,3},{2,0},{3,1},{4,6},{5,7},{6,4},{7,5},{8,10},{9,11},{10,... | collective-permute-start | bytes 196616 | tf_op jit(solution)/shard_map/ppermute | solution.py:94
  (5 other events, 3.9 us)

commit v10 on v6

--- a/solution.py
+++ b/solution.py
@@ -7,18 +7,18 @@
 
 
 eps = 1e-05
-highest = lax.Precision.HIGHEST
+highest = lax.Precision.HIGH
 
 
 def combine(earlier, later):
-    return (earlier[0] * later[0], later[0][:, None, None] * earlier[1] + later[1])
+    return (earlier[0] * later[0], later[0][None, :] * earlier[1] + later[1])
 
 
 def pair_scan(decay, state, axis, reverse):
     count = lax.axis_size(axis)
     if count == 1:
         return jnp.zeros_like(state)
-    assert count % 2 == 0 and decay.shape[0] % 2 == 0
+    assert count % 2 == 0 and decay.shape[0] % 2 == 0 and state.shape[1] == decay.shape[0]
     place = lax.axis_index(axis)
     virt = count - 1 - place if reverse else place
 
@@ -34,7 +34,7 @@
     send_start = side * half
 
     def part(x, start):
-        return lax.dynamic_slice_in_dim(x, start, half, 0)
+        return lax.dynamic_slice_in_dim(x, start, half, x.ndim - 1)
 
     a_own, s_own = part(decay, own_start), part(state, own_start)
     a_snd, s_snd = part(decay, send_start), part(state, send_start)
@@ -75,13 +75,13 @@
             s_g = jnp.where(group >= k, s_c, s_g)
             k *= 2
 
-    with_lead_own = a_own[:, None, None] * s_g + s_own
-    with_lead_rcv = a_rcv[:, None, None] * s_g + s_rcv
+    with_lead_own = a_own[None, :] * s_g + s_own
+    with_lead_rcv = a_rcv[None, :] * s_g + s_rcv
     send = jnp.where(first, with_lead_own, s_g)
     keep = jnp.where(first, s_g, with_lead_rcv)
     other = lax.ppermute(send, axis, swap)
     return jnp.where(
-        first, jnp.concatenate([other, keep], 0), jnp.concatenate([keep, other], 0)
+        first, jnp.concatenate([other, keep], 1), jnp.concatenate([keep, other], 1)
     )
 
 
@@ -148,7 +148,7 @@
         lax.broadcasted_iota(jnp.int32, (length, length), 0)
         <= lax.broadcasted_iota(jnp.int32, (length, length), 1)
     ).astype(decay_in.dtype)
-    return jnp.dot(decay_in, upper, precision=highest)
+    return jnp.dot(decay_in, upper, precision=lax.Precision.HIGHEST)
 
 
 def within_part(feat_in, step_in, decay_in, writes, read_in, skip_scale):
@@ -173,9 +173,8 @@
 
 
 def carried_part(decay_in, read_in, state_in):
-    head_width = state_in.shape[1]
-    flat = state_in.reshape(-1, state_in.shape[2])
-    carried = jnp.dot(read_in, jnp.transpose(flat), precision=highest)
+    head_width = state_in.shape[1] // decay_in.shape[0]
+    carried = jnp.dot(read_in, state_in, precision=highest)
     return carried * per_channel(jnp.exp(prefix_sum(decay_in)), head_width)
 
 
@@ -185,15 +184,17 @@
     cumul = prefix_sum(decay_in)
     to_end = jnp.exp(cumul[:, -1:] - cumul)
     weighted_in = feat_in * per_channel(step_in * to_end, head_width)
-    update = lax.dot_general(
-        weighted_in, writes, (((0,), (0,)), ((), ())), precision=highest
-    )
-    return update.reshape(head_count, head_width, writes.shape[1])
+    return lax.dot_general(writes, weighted_in, (((0,), (0,)), ((), ())), precision=highest)
 
 
 def end_part(feat_in, step_in, decay_in, writes, state_in):
-    total = jnp.exp(prefix_sum(decay_in)[:, -1])
-    return total[:, None, None] * state_in + state_update(feat_in, step_in, decay_in, writes)
+    head_width = feat_in.shape[1] // step_in.shape[0]
+    total = jnp.repeat(jnp.exp(prefix_sum(decay_in)[:, -1]), head_width)
+    return total[None, :] * state_in + state_update(feat_in, step_in, decay_in, writes)
+
+
+def to_heads(state, head_count):
+    return jnp.transpose(state).reshape(head_count, -1, state.shape[0])
 
 
 def local(
@@ -212,8 +213,9 @@
     channels = features.shape[1] * lax.axis_size("head")
     cumul = prefix_sum(log_decay)
     decay_total = jnp.exp(cumul[:, -1])
+    decay_channels = jnp.repeat(decay_total, head_width)
     local_state = state_update(features, step_sizes, log_decay, write_keys)
-    state_in = pair_scan(decay_total, local_state, "seq", False)
+    state_in = pair_scan(decay_channels, local_state, "seq", False)
     single = length == BLOCK
     if single:
         mixed_w, pull_w = jax.vjp(
@@ -228,7 +230,8 @@
 
         def local_mixer(feat_in, step_in, decay_factors, writes, read_in):
             return run_mixer(
-                feat_in, step_in, decay_factors, writes, read_in, state_in, skip_scale, BLOCK
+                feat_in, step_in, decay_factors, writes, read_in,
+                to_heads(state_in, head_count), skip_scale, BLOCK,
             )
 
         primal, pullback = jax.vjp(
@@ -240,8 +243,7 @@
     gated_out = mixed_out * active
     weighted = out_grad * norm_gain[None, :]
     square_sum, cross_sum = butterfly_psum(
-        jnp.stack([jnp.sum(gated_out * gated_out, axis=1), jnp.sum(weighted * gated_out, axis=1)]),
-        "head",
+        (jnp.sum(gated_out * gated_out, axis=1), jnp.sum(weighted * gated_out, axis=1)), "head"
     )
     inverse = lax.rsqrt(square_sum / channels + eps)
     grad_gated = (
@@ -252,9 +254,9 @@
     grad_gate = grad_gated * mixed_out * sigmoid_gate * (1.0 + gate_pre * (1.0 - sigmoid_gate))
     weighted_grad = grad_mixed * per_channel(jnp.exp(cumul), head_width)
     local_grad = lax.dot_general(
-        weighted_grad, read_queries, (((0,), (0,)), ((), ())), precision=highest
-    ).reshape(head_count, head_width, read_queries.shape[1])
-    state_grad = pair_scan(decay_total, local_grad, "seq", True)
+        read_queries, weighted_grad, (((0,), (0,)), ((), ())), precision=highest
+    )
+    state_grad = pair_scan(decay_channels, local_grad, "seq", True)
     if single:
         gf_w, gs_w, gd_w, gw_w, gr_w = pull_w(grad_mixed)
         gd_c, gr_c = pull_c(grad_mixed)
@@ -270,7 +272,7 @@
         grad_write = butterfly_psum(gw_w + gw_e, "head")
     else:
         grad_features, grad_steps, grad_decay, grad_write, grad_read = pullback(
-            (state_grad, grad_mixed)
+            (to_heads(state_grad, head_count), grad_mixed)
         )
         grad_write, grad_read = butterfly_psum((grad_write, grad_read), "head")
     return (grad_features, grad_gate, grad_write, grad_read, grad_steps, grad_decay)

time: 121 us -> 125 us (1.033)
  waiting for transfers between devices: 54.4 us -> 59.3 us
  matrix products: 16.9 us -> 14.5 us
  starting transfers between devices: 20 us -> 22.3 us
  local copies, waits for them, and re-layouts: 11 us -> 8.81 us
  other arithmetic: 16.7 us -> 18.1 us
    ppermute x2, waiting for transfers between devices: 23.9 us -> 27.9 us  [pair_scan(): s_in = lax.ppermute(out[1], axis, pairs)]
    dot_general x3, matrix products: 7.27 us -> 4.36 us  [within_part(): within = jnp.einsum('hij,jhp->ihp', masked, scaled, precision=highest)]
    unnamed x53 -> x69, local copies, waits for them, and re-layouts: 9.72 us -> 7.3 us
    reduce_sum x2, other arithmetic: 0.71 us -> 2.88 us  [per_channel(): return jnp.repeat(jnp.transpose(factors), head_width, axis=1)]
    select_n x2, other arithmetic: 2.08 us -> 0.01 us  [pair_scan(): trail = (jnp.where(first, a_rcv, a_own), jnp.where(first, s_rcv, s_own))]
    select_n x1 -> x2, other arithmetic: 1.23 us -> 3.28 us  [pair_scan(): send = jnp.where(first, with_lead_own, s_g)]
    ppermute x2, starting transfers between devices: 1.12 us -> 3.07 us  [pair_scan(): other = lax.ppermute(send, axis, swap)]
    ppermute x6 -> x8, waiting for transfers between devices: 5.79 us -> 7.57 us  [butterfly_psum(): got = lax.ppermute(parts, axis, [(i, i ^ k) for i in range(count)])]
  transfers between devices with their start and end apart: 18 -> 20, of which waited for: 10 -> 12; matrix products, arithmetic and copies ran while one was open for 22% -> 19% of each run, Pallas kernels for 0% -> 0%
where the time goes in v10:
time: 125 us; the launch traced here: 124 us
  waiting for transfers between devices  59.3 us (47%)
  starting transfers between devices  22.3 us (18%)
  other arithmetic  18.1 us (14%)
  matrix products  14.5 us (12%)
  local copies, waits for them, and re-layouts  8.81 us (7%)
  between operations  1.31 us (1%)
    ppermute x2, waiting for transfers between devices, pair_scan(): s_in = lax.ppermute(out[1], axis, pairs)  27.9 us
    ppermute x4, waiting for transfers between devices, pair_scan(): a_rcv, s_rcv = lax.ppermute((a_snd, s_snd), axis, swap)  14.3 us
    ppermute x8, waiting for transfers between devices, butterfly_psum(): got = lax.ppermute(parts, axis, [(i, i ^ k) for i in range(count)])  7.57 us
    unnamed x69, local copies, waits for them, and re-layouts  7.3 us
    ppermute x4, starting transfers between devices, pair_scan(): a_rcv, s_rcv = lax.ppermute((a_snd, s_snd), axis, swap)  6.56 us
    ppermute x4, starting transfers between devices, pair_scan(): a_in, s_in = lax.ppermute(out, axis, pairs)  6.49 us
    ppermute x4, waiting for transfers between devices, pair_scan(): a_in, s_in = lax.ppermute(out, axis, pairs)  5.48 us
    dot_general x3, matrix products, within_part(): within = jnp.einsum('hij,jhp->ihp', masked, scaled, precision=highest)  4.36 us
  transfers between devices with their start and end apart: 20, of which 12 were waited for; matrix products, arithmetic and copies ran while one was open for 19% of the time, Pallas kernels for 0%

profile of v10, /device:TPU:0, one launch (start us, length us, event | category | flops | bytes accessed | tf_op | source)
XLA Modules:
  0.0 124.4 jit_solution(14640121965015086555)
XLA Ops:
  2.0 2.9 %collective-permute-start.10 = (f32[640]{0:T(1024)S(1)}, f32[640]{0:T(1024)S(1)}, u32[]{:S(2)}, u32[]{:S(2)}) collective-permute-start(f32[640]{0:T(1024)S(1)} %dynamic_slice.29), channel_id=1, source_target_pairs={{28,24},{24,28},{20,16},{16,20},{12,8},{8,12},{4,0},{0,4},{29,25},... | collective-permute-start | bytes 7688 | tf_op jit(solution)/shard_map/ppermute | solution.py:42
  5.7 1.3 %copy.37 = f32[128,1280]{0,1:T(8,128)S(1)} copy(f32[128,1280]{1,0:T(8,128)} %param.9) | data formatting | bytes 1310720 | tf_op args[0]
  8.7 2.0 %collective-permute-start.1 = (f32[128,640]{0,1:T(8,128)S(1)}, f32[128,640]{0,1:T(8,128)S(1)}, u32[]{:S(2)}, u32[]{:S(2)}) collective-permute-start(f32[128,640]{0,1:T(8,128)S(1)} %dynamic-slice_bitcast_fusion.1), channel_id=1, source_target_pairs={{0,4},{4,0},{8,12},{12,8},{16,20},{20,16},{24,28},{28,24},{1,5},{5... | collective-permute-start | bytes 983048 | tf_op jit(solution)/shard_map/ppermute | solution.py:42
  10.6 1.6 %collective-permute-done = f32[640]{0:T(1024)S(1)} collective-permute-done((f32[640]{0:T(1024)S(1)}, f32[640]{0:T(1024)S(1)}, u32[]{:S(2)}, u32[]{:S(2)}) %collective-permute-start) | collective-permute-done | bytes 2592 | tf_op jit(solution)/shard_map/ppermute | solution.py:42
  12.3 5.6 %collective-permute-done.1 = f32[128,640]{0,1:T(8,128)S(1)} collective-permute-done((f32[128,640]{0,1:T(8,128)S(1)}, f32[128,640]{0,1:T(8,128)S(1)}, u32[]{:S(2)}, u32[]{:S(2)}) %collective-permute-start.1) | collective-permute-done | bytes 327712 | tf_op jit(solution)/shard_map/ppermute | solution.py:42
  18.6 3.7 %collective-permute-start.2 = (f32[128,640]{0,1:T(8,128)S(1)}, f32[128,640]{0,1:T(8,128)S(1)}, u32[]{:S(2)}, u32[]{:S(2)}) collective-permute-start(f32[128,640]{0,1:T(8,128)S(1)} %get-tuple-element.45), channel_id=1, source_target_pairs={{0,8},{4,12},{1,9},{5,13},{2,10},{6,14},{3,11},{7,15}} | collective-permute-start | bytes 983048 | tf_op jit(solution)/shard_map/ppermute | solution.py:62
  22.3 5.5 %collective-permute-done.2 = f32[128,640]{0,1:T(8,128)S(1)} collective-permute-done((f32[128,640]{0,1:T(8,128)S(1)}, f32[128,640]{0,1:T(8,128)S(1)}, u32[]{:S(2)}, u32[]{:S(2)}) %collective-permute-start.2) | collective-permute-done | bytes 327712 | tf_op jit(solution)/shard_map/ppermute | solution.py:62
  28.6 1.4 %collective-permute-start.3 = (f32[128,640]{0,1:T(8,128)}, f32[128,640]{0,1:T(8,128)}, u32[]{:S(2)}, u32[]{:S(2)}) collective-permute-start(f32[128,640]{0,1:T(8,128)} %multiply_add_fusion.4), channel_id=1, source_target_pairs={{8,16},{12,20},{9,17},{13,21},{10,18},{14,22},{11,19},{15,23}} | collective-permute-start | bytes 983048 | tf_op jit(solution)/shard_map/ppermute | solution.py:62
  31.9 1.4 %copy.41 = f32[128,1280]{0,1:T(8,128)S(1)} copy(f32[128,1280]{1,0:T(8,128)} %param.17) | data formatting | bytes 1310720 | tf_op args[8]
  34.3 1.3 %fusion.39 = (f32[128,640]{0,1:T(8,128)S(1)}, f32[128,640]{0,1:T(8,128)S(1)}) fusion(f32[1280,128]{1,0:T(8,128)} %copy-done.3, s32[]{:T(128)S(6)} %select_n.163, f32[640]{0:T(1024)S(1)} %get-tuple-element.49, pred[]{:T(512)S(6)} %eq.27, f32[128,640]{0,1:T(8,128)} %copy-done.13, f32[128,640]{0,1:T(8,128)} %get-tuple-element.44, pred[]{:T(512)S(6)} %eq.28, ...), kind=kLoop, calls=%fused_computation.60 | loop fusion | flops 573440 | bytes 1971206 | tf_op jit(solution)/shard_map/jit(_where)/select_n | solution.py:80
  35.6 1.6 %collective-permute-start.5 = (f32[128,640]{0,1:T(8,128)S(1)}, f32[128,640]{0,1:T(8,128)S(1)}, u32[]{:S(2)}, u32[]{:S(2)}) collective-permute-start(f32[128,640]{0,1:T(8,128)S(1)} %get-tuple-element.57), channel_id=1, source_target_pairs={{0,4},{4,0},{8,12},{12,8},{16,20},{20,16},{24,28},{28,24},{1,5},{5... | collective-permute-start | bytes 983048 | tf_op jit(solution)/shard_map/ppermute | solution.py:82
  37.2 1.5 %fusion.9 = f32[128,20,64]{0,2,1:T(8,128)S(1)} fusion(f32[128,20,64]{0,2,1:T(8,128)S(1)} %bitcast.114, f32[128,128]{1,0:T(8,128)S(1)} %fusion.76, f32[20,128]{1,0:T(8,128)S(1)} %bitcast.123, pred[128,128]{1,0:T(8,128)(4,1)S(1)} %iota_compare_fusion.6, f32[128,20]{0,1:T(8,128)S(1)} %bitcast.127, f32[20]{0:T(128)S(1)} %copy-done.30), kind=kOutput, calls=%fused_computation.10 | convolution fusion | flops 127631360 | bytes 1413200 | tf_op jit(solution)/shard_map/jvp(hij,jhp->ihp)/dot_general | solution.py:167
  38.7 4.0 %collective-permute-done.5 = f32[128,640]{0,1:T(8,128)S(1)} collective-permute-done((f32[128,640]{0,1:T(8,128)S(1)}, f32[128,640]{0,1:T(8,128)S(1)}, u32[]{:S(2)}, u32[]{:S(2)}) %collective-permute-start.5) | collective-permute-done | bytes 327712 | tf_op jit(solution)/shard_map/ppermute | solution.py:82
  44.6 1.5 %collective-permute-start.7 = (f32[128]{0:T(128)S(1)}, f32[128]{0:T(128)S(1)}, u32[]{:S(2)}, u32[]{:S(2)}) collective-permute-start(f32[128]{0:T(128)S(1)} %add.137), channel_id=1, source_target_pairs={{0,2},{1,3},{2,0},{3,1},{4,6},{5,7},{6,4},{7,5},{8,10},{9,11},{10,... | collective-permute-start | bytes 1544 | tf_op jit(solution)/shard_map/ppermute | solution.py:94
  46.6 1.5 %collective-permute-done.7 = f32[128]{0:T(128)S(1)} collective-permute-done((f32[128]{0:T(128)S(1)}, f32[128]{0:T(128)S(1)}, u32[]{:S(2)}, u32[]{:S(2)}) %collective-permute-start.7) | collective-permute-done | bytes 544 | tf_op jit(solution)/shard_map/ppermute | solution.py:94
  48.1 1.5 %collective-permute-done.9 = f32[128]{0:T(128)S(1)} collective-permute-done((f32[128]{0:T(128)S(1)}, f32[128]{0:T(128)S(1)}, u32[]{:S(2)}, u32[]{:S(2)}) %collective-permute-start.9) | collective-permute-done | bytes 544 | tf_op jit(solution)/shard_map/ppermute | solution.py:94
  49.7 1.5 %fusion.69 = (f32[128,1280]{0,1:T(8,128)}, f32[128,1280]{0,1:T(8,128)S(1)}, f32[128,1280]{0,1:T(8,128)}) fusion(f32[128,1280]{0,1:T(8,128)S(1)} %get-tuple-element.63, f32[128,1280]{0,1:T(8,128)S(1)} %copy.40, f32[128,1280]{0,1:T(8,128)S(1)} %get-tuple-element.42, f32[128]{0:T(128)S(1)} %get-tuple-element.40, f32[128,1280]{0,1:T(8,128)S(1)} %copy.41, ...), kind=kLoop, calls=%fused_computation.120 | loop fusion | flops 2949120 | bytes 5259264 | tf_op jit(solution)/shard_map/transpose(jvp())/mul | solution.py:178
  52.5 1.5 %collective-permute-start.11 = (f32[128,640]{0,1:T(8,128)}, f32[128,640]{0,1:T(8,128)}, u32[]{:S(2)}, u32[]{:S(2)}) collective-permute-start(f32[128,640]{0,1:T(8,128)} %dynamic-slice_bitcast_fusion), channel_id=1, source_target_pairs={{28,24},{24,28},{20,16},{16,20},{12,8},{8,12},{4,0},{0,4},{29,25},... | collective-permute-start | bytes 983048 | tf_op jit(solution)/shard_map/ppermute | solution.py:42
  54.0 7.2 %collective-permute-done.11 = f32[128,640]{0,1:T(8,128)} collective-permute-done((f32[128,640]{0,1:T(8,128)}, f32[128,640]{0,1:T(8,128)}, u32[]{:S(2)}, u32[]{:S(2)}) %collective-permute-start.11) | collective-permute-done | bytes 327712 | tf_op jit(solution)/shard_map/ppermute | solution.py:42
  61.2 1.2 broadcast_add_fusion
  63.1 2.0 %fusion.17 = (f32[20,128]{1,0:T(8,128)S(1)}, f32[20,128]{1,0:T(8,128)S(1)}, f32[128,128]{1,0:T(8,128)S(1)}) fusion(f32[128,128]{1,0:T(8,128)S(1)} %fusion.76, f32[20,128]{1,0:T(8,128)S(1)} %bitcast.124, pred[128,128]{1,0:T(8,128)(4,1)S(1)} %iota_compare_fusion.6, f32[20,64,128]{2,1,0:T(8,128)S(1)} %bitcast.117, f32[128,20,64]{0,2,1:T(8,128)S(1)} %bitcast.115, ...), kind=kOutput, calls=%fused_computation.22 | convolution fusion | flops 129575936 | bytes 1499136 | tf_op jit(solution)/shard_map/transpose(jvp(hij,jhp->ihp))/dot_general | solution.py:167
  68.0 1.5 %collective-permute-start.14 = (f32[128,640]{0,1:T(8,128)S(1)}, f32[128,640]{0,1:T(8,128)S(1)}, u32[]{:S(2)}, u32[]{:S(2)}) collective-permute-start(f32[128,640]{0,1:T(8,128)S(1)} %get-tuple-element.33), channel_id=1, source_target_pairs={{12,4},{8,0},{13,5},{9,1},{14,6},{10,2},{15,7},{11,3}} | collective-permute-start | bytes 983048 | tf_op jit(solution)/shard_map/ppermute | solution.py:59
  69.9 1.6 %multiply_reduce_fusion.2 = (f32[128,20]{0,1:T(8,128)}, f32[128,20,64]{0,2,1:T(8,128)}) fusion(f32[128,20,64]{0,2,1:T(8,128)S(1)} %bitcast.116, f32[128,20,64]{0,2,1:T(8,128)S(1)} %fusion.12, f32[128,20]{0,1:T(8,128)S(1)} %bitcast.129, f32[128,20,64]{0,2,1:T(8,128)S(1)} %bitcast.119, f32[20]{0:T(128)S(1)} %copy-done.31), kind=kLoop, calls=%fused_computation.28 | loop fusion | flops 816640 | bytes 2642000 | tf_op jit(solution)/shard_map/transpose(jvp())/reduce_sum | solution.py:165
  71.5 27.9 %collective-permute-done.14 = f32[128,640]{0,1:T(8,128)S(1)} collective-permute-done((f32[128,640]{0,1:T(8,128)S(1)}, f32[128,640]{0,1:T(8,128)S(1)}, u32[]{:S(2)}, u32[]{:S(2)}) %collective-permute-start.14) | collective-permute-done | bytes 327712 | tf_op jit(solution)/shard_map/ppermute | solution.py:59
  99.4 2.0 %fusion.36 = (f32[128,640]{0,1:T(8,128)}, f32[128,640]{0,1:T(8,128)S(1)}) fusion(f32[1280,128]{1,0:T(8,128)S(1)} %copy-done.5, s32[]{:T(128)S(6)} %select_n.183, f32[640]{0:T(1024)S(1)} %copy-done.24, pred[]{:T(512)S(6)} %eq.31, f32[128,640]{0,1:T(8,128)S(1)} %collective-permute-done.14, f32[128,640]{0,1:T(8,128)S(1)} %get-tuple-element.34, pred[]{:T(512)S(6)} %eq.32, ...), kind=kLoop, calls=%fused_computation.54 | loop fusion | flops 573440 | bytes 1971206 | tf_op jit(solution)/shard_map/jit(_where)/select_n | solution.py:80
  101.4 1.5 %collective-permute-start.15 = (f32[128,640]{0,1:T(8,128)}, f32[128,640]{0,1:T(8,128)S(1)}, u32[]{:S(2)}, u32[]{:S(2)}) collective-permute-start(f32[128,640]{0,1:T(8,128)} %get-tuple-element.55), channel_id=1, source_target_pairs={{28,24},{24,28},{20,16},{16,20},{12,8},{8,12},{4,0},{0,4},{29,25},... | collective-permute-start | bytes 983048 | tf_op jit(solution)/shard_map/ppermute | solution.py:82
  103.7 1.7 %reduce_sum.128 = f32[128,20]{0,1:T(8,128)} reduce(f32[128,20,64]{0,2,1:T(8,128)} %bitcast.120, f32[]{:T(128)} %constant.51.clone.1), dimensions={2}, to_apply=%region_7.8 | reduce | flops 161280 | bytes 665604 | tf_op jit(solution)/shard_map/transpose(jvp())/reduce_sum | solution.py:172
  107.0 1.5 %convolution_add_fusion.3 = f32[20,128]{1,0:T(8,128)} fusion(f32[20,128]{1,0:T(8,128)} %fusion.45, f32[128,20]{0,1:T(8,128)} %reduce_sum.128, f32[128,20]{0,1:T(8,128)S(1)} %get-tuple-element.62), kind=kOutput, calls=%fused_computation.16 | convolution fusion | flops 3953664 | bytes 40960 | tf_op jit(solution)/shard_map/transpose(jvp())/dot_general | solution.py:151
  109.6 1.1 collective-permute-done.19
  110.7 1.5 %add.159 = f32[128,128]{1,0:T(8,128)} add(f32[128,128]{1,0:T(8,128)S(1)} %add.158, f32[128,128]{1,0:T(8,128)} %collective-permute-done.19) | non-fusion elementwise | flops 16384 | bytes 196608 | tf_op jit(solution)/shard_map/add | solution.py:95
  112.2 2.4 %fusion.74 = (f32[128,1280]{0,1:T(8,128)}, f32[128,1280]{0,1:T(8,128)S(1)}) fusion(f32[128,1280]{0,1:T(8,128)S(1)} %copy.37, f32[128,20]{0,1:T(8,128)} %copy-done.15, f32[128,20,64]{0,2,1:T(8,128)} %get-tuple-element.52, f32[128,128]{1,0:T(8,128)S(1)} %copy-done.11, f32[128,640]{0,1:T(8,128)S(1)} %get-tuple-element.56, ...), kind=kOutput, calls=%fused_computation.121 | convolution fusion | flops 126812160 | bytes 3352577 | tf_op jit(solution)/shard_map/transpose(jvp())/dot_general | solution.py:187
  122.0 1.7 %collective-permute-done.17 = f32[128,128]{1,0:T(8,128)S(1)} collective-permute-done((f32[128,128]{1,0:T(8,128)S(1)}, f32[128,128]{1,0:T(8,128)S(1)}, u32[]{:S(2)}, u32[]{:S(2)}) %collective-permute-start.17) | collective-permute-done | bytes 65568 | tf_op jit(solution)/shard_map/ppermute | solution.py:94
  (135 shorter events, 27.0 us)
Async XLA Ops:
  0.6 32.7 %copy-start = (f32[128,128]{1,0:T(8,128)S(1)}, f32[128,128]{1,0:T(8,128)}, u32[]{:S(2)}) copy-start(f32[128,128]{1,0:T(8,128)} %param.12) | copy-start | bytes 196612
  2.0 6.4 %collective-permute-start.10 = (f32[640]{0:T(1024)S(1)}, f32[640]{0:T(1024)S(1)}, u32[]{:S(2)}, u32[]{:S(2)}) collective-permute-start(f32[640]{0:T(1024)S(1)} %dynamic_slice.29), channel_id=1, source_target_pairs={{28,24},{24,28},{20,16},{16,20},{12,8},{8,12},{4,0},{0,4},{29,25},... | collective-permute-start | bytes 7688 | tf_op jit(solution)/shard_map/ppermute | solution.py:42
  8.3 22.7 %copy-start.3 = (f32[1280,128]{1,0:T(8,128)}, f32[1280,128]{1,0:T(8,128)S(1)}, u32[]{:S(2)}) copy-start(f32[1280,128]{1,0:T(8,128)S(1)} %fusion.77) | copy-start | bytes 1966084
  8.4 45.6 %copy-start.21 = (f32[640]{0:T(1024)}, f32[640]{0:T(1024)S(1)}, u32[]{:S(2)}) copy-start(f32[640]{0:T(1024)S(1)} %collective-permute-done.10) | copy-start | bytes 7684
  8.5 45.5 %copy-start.23 = (f32[640]{0:T(1024)}, f32[640]{0:T(1024)S(1)}, u32[]{:S(2)}) copy-start(f32[640]{0:T(1024)S(1)} %get-tuple-element.39) | copy-start | bytes 7684
  8.5 3.7 %collective-permute-start = (f32[640]{0:T(1024)S(1)}, f32[640]{0:T(1024)S(1)}, u32[]{:S(2)}, u32[]{:S(2)}) collective-permute-start(f32[640]{0:T(1024)S(1)} %get-tuple-element.60), channel_id=1, source_target_pairs={{0,4},{4,0},{8,12},{12,8},{16,20},{20,16},{24,28},{28,24},{1,5},{5... | collective-permute-start | bytes 7688 | tf_op jit(solution)/shard_map/ppermute | solution.py:42
  8.7 9.2 %collective-permute-start.1 = (f32[128,640]{0,1:T(8,128)S(1)}, f32[128,640]{0,1:T(8,128)S(1)}, u32[]{:S(2)}, u32[]{:S(2)}) collective-permute-start(f32[128,640]{0,1:T(8,128)S(1)} %dynamic-slice_bitcast_fusion.1), channel_id=1, source_target_pairs={{0,4},{4,0},{8,12},{12,8},{16,20},{20,16},{24,28},{28,24},{1,5},{5... | collective-permute-start | bytes 983048 | tf_op jit(solution)/shard_map/ppermute | solution.py:42
  18.6 9.2 %collective-permute-start.2 = (f32[128,640]{0,1:T(8,128)S(1)}, f32[128,640]{0,1:T(8,128)S(1)}, u32[]{:S(2)}, u32[]{:S(2)}) collective-permute-start(f32[128,640]{0,1:T(8,128)S(1)} %get-tuple-element.45), channel_id=1, source_target_pairs={{0,8},{4,12},{1,9},{5,13},{2,10},{6,14},{3,11},{7,15}} | collective-permute-start | bytes 983048 | tf_op jit(solution)/shard_map/ppermute | solution.py:62
  28.6 1.4 %collective-permute-start.3 = (f32[128,640]{0,1:T(8,128)}, f32[128,640]{0,1:T(8,128)}, u32[]{:S(2)}, u32[]{:S(2)}) collective-permute-start(f32[128,640]{0,1:T(8,128)} %multiply_add_fusion.4), channel_id=1, source_target_pairs={{8,16},{12,20},{9,17},{13,21},{10,18},{14,22},{11,19},{15,23}} | collective-permute-start | bytes 983048 | tf_op jit(solution)/shard_map/ppermute | solution.py:62
  31.0 2.5 %collective-permute-start.4 = (f32[128,640]{0,1:T(8,128)}, f32[128,640]{0,1:T(8,128)S(1)}, u32[]{:S(2)}, u32[]{:S(2)}) collective-permute-start(f32[128,640]{0,1:T(8,128)} %get-tuple-element.43), channel_id=1, source_target_pairs={{16,24},{20,28},{17,25},{21,29},{18,26},{22,30},{19,27},{23,31}} | collective-permute-start | bytes 983048 | tf_op jit(solution)/shard_map/ppermute | solution.py:59
  35.6 7.2 %copy-start.1 = (f32[128,640]{0,1:T(8,128)}, f32[128,640]{0,1:T(8,128)S(1)}, u32[]{:S(2)}) copy-start(f32[128,640]{0,1:T(8,128)S(1)} %get-tuple-element.58) | copy-start | bytes 983044
  35.6 7.2 %collective-permute-start.5 = (f32[128,640]{0,1:T(8,128)S(1)}, f32[128,640]{0,1:T(8,128)S(1)}, u32[]{:S(2)}, u32[]{:S(2)}) collective-permute-start(f32[128,640]{0,1:T(8,128)S(1)} %get-tuple-element.57), channel_id=1, source_target_pairs={{0,4},{4,0},{8,12},{12,8},{16,20},{20,16},{24,28},{28,24},{1,5},{5... | collective-permute-start | bytes 983048 | tf_op jit(solution)/shard_map/ppermute | solution.py:82
  37.2 26.0 %copy-start.26 = (pred[128,128]{1,0:T(8,128)(4,1)}, pred[128,128]{1,0:T(8,128)(4,1)S(1)}, u32[]{:S(2)}) copy-start(pred[128,128]{1,0:T(8,128)(4,1)S(1)} %iota_compare_fusion.6) | copy-start | bytes 49156
  37.2 5.5 %copy-start.25 = (f32[1280]{0:T(1024)S(1)}, f32[1280]{0:T(1024)}, u32[]{:S(2)}) copy-start(f32[1280]{0:T(1024)} %param.16) | copy-start | bytes 15364
  43.5 1.1 collective-permute-start.6
  43.5 2.6 %collective-permute-start.8 = (f32[128]{0:T(128)S(1)}, f32[128]{0:T(128)S(1)}, u32[]{:S(2)}, u32[]{:S(2)}) collective-permute-start(f32[128]{0:T(128)S(1)} %get-tuple-element.28), channel_id=1, source_target_pairs={{0,1},{1,0},{2,3},{3,2},{4,5},{5,4},{6,7},{7,6},{8,9},{9,8},{10,11... | collective-permute-start | bytes 1544 | tf_op jit(solution)/shard_map/ppermute | solution.py:94
  44.6 3.5 %collective-permute-start.7 = (f32[128]{0:T(128)S(1)}, f32[128]{0:T(128)S(1)}, u32[]{:S(2)}, u32[]{:S(2)}) collective-permute-start(f32[128]{0:T(128)S(1)} %add.137), channel_id=1, source_target_pairs={{0,2},{1,3},{2,0},{3,1},{4,6},{5,7},{6,4},{7,5},{8,10},{9,11},{10,... | collective-permute-start | bytes 1544 | tf_op jit(solution)/shard_map/ppermute | solution.py:94
  46.1 3.5 %collective-permute-start.9 = (f32[128]{0:T(128)S(1)}, f32[128]{0:T(128)S(1)}, u32[]{:S(2)}, u32[]{:S(2)}) collective-permute-start(f32[128]{0:T(128)S(1)} %add.141), channel_id=1, source_target_pairs={{0,2},{1,3},{2,0},{3,1},{4,6},{5,7},{6,4},{7,5},{8,10},{9,11},{10,... | collective-permute-start | bytes 1544 | tf_op jit(solution)/shard_map/ppermute | solution.py:94
  51.7 10.8 %copy-start.4 = (f32[1280,128]{1,0:T(8,128)}, f32[1280,128]{1,0:T(8,128)S(1)}, u32[]{:S(2)}) copy-start(f32[1280,128]{1,0:T(8,128)S(1)} %fusion.78) | copy-start | bytes 1966084
  52.5 8.7 %collective-permute-start.11 = (f32[128,640]{0,1:T(8,128)}, f32[128,640]{0,1:T(8,128)}, u32[]{:S(2)}, u32[]{:S(2)}) collective-permute-start(f32[128,640]{0,1:T(8,128)} %dynamic-slice_bitcast_fusion), channel_id=1, source_target_pairs={{28,24},{24,28},{20,16},{16,20},{12,8},{8,12},{4,0},{0,4},{29,25},... | collective-permute-start | bytes 983048 | tf_op jit(solution)/shard_map/ppermute | solution.py:42
  62.4 2.9 %collective-permute-start.12 = (f32[128,640]{0,1:T(8,128)S(1)}, f32[128,640]{0,1:T(8,128)S(1)}, u32[]{:S(2)}, u32[]{:S(2)}) collective-permute-start(f32[128,640]{0,1:T(8,128)S(1)} %get-tuple-element.35), channel_id=1, source_target_pairs={{28,20},{24,16},{29,21},{25,17},{30,22},{26,18},{31,23},{27,19}} | collective-permute-start | bytes 983048 | tf_op jit(solution)/shard_map/ppermute | solution.py:62
  65.5 2.4 %collective-permute-start.13 = (f32[128,640]{0,1:T(8,128)S(1)}, f32[128,640]{0,1:T(8,128)S(1)}, u32[]{:S(2)}, u32[]{:S(2)}) collective-permute-start(f32[128,640]{0,1:T(8,128)S(1)} %multiply_add_fusion.2), channel_id=1, source_target_pairs={{20,12},{16,8},{21,13},{17,9},{22,14},{18,10},{23,15},{19,11}} | collective-permute-start | bytes 983048 | tf_op jit(solution)/shard_map/ppermute | solution.py:62
  68.0 31.4 %collective-permute-start.14 = (f32[128,640]{0,1:T(8,128)S(1)}, f32[128,640]{0,1:T(8,128)S(1)}, u32[]{:S(2)}, u32[]{:S(2)}) collective-permute-start(f32[128,640]{0,1:T(8,128)S(1)} %get-tuple-element.33), channel_id=1, source_target_pairs={{12,4},{8,0},{13,5},{9,1},{14,6},{10,2},{15,7},{11,3}} | collective-permute-start | bytes 983048 | tf_op jit(solution)/shard_map/ppermute | solution.py:59
  69.8 35.6 %collective-permute-start.18 = (f32[128,128]{1,0:T(8,128)S(1)}, f32[128,128]{1,0:T(8,128)}, u32[]{:S(2)}, u32[]{:S(2)}) collective-permute-start(f32[128,128]{1,0:T(8,128)S(1)} %convolution_add_fusion), channel_id=1, source_target_pairs={{0,1},{1,0},{2,3},{3,2},{4,5},{5,4},{6,7},{7,6},{8,9},{9,8},{10,11... | collective-permute-start | bytes 196616 | tf_op jit(solution)/shard_map/ppermute | solution.py:94
  69.9 29.5 %copy-start.5 = (f32[1280,128]{1,0:T(8,128)S(1)}, f32[1280,128]{1,0:T(8,128)}, u32[]{:S(2)}) copy-start(f32[1280,128]{1,0:T(8,128)} %copy-done.4) | copy-start | bytes 1966084
  69.9 29.5 %copy-start.22 = (f32[640]{0:T(1024)S(1)}, f32[640]{0:T(1024)}, u32[]{:S(2)}) copy-start(f32[640]{0:T(1024)} %copy-done.21) | copy-start | bytes 7684
  69.9 29.5 %copy-start.24 = (f32[640]{0:T(1024)S(1)}, f32[640]{0:T(1024)}, u32[]{:S(2)}) copy-start(f32[640]{0:T(1024)} %copy-done.23) | copy-start | bytes 7684
  101.4 7.1 %copy-start.8 = (f32[128,1280]{0,1:T(8,128)S(1)}, f32[128,1280]{0,1:T(8,128)}, u32[]{:S(2)}) copy-start(f32[128,1280]{0,1:T(8,128)} %get-tuple-element.50) | copy-start | bytes 1966084
  101.4 10.8 %collective-permute-start.15 = (f32[128,640]{0,1:T(8,128)}, f32[128,640]{0,1:T(8,128)S(1)}, u32[]{:S(2)}, u32[]{:S(2)}) collective-permute-start(f32[128,640]{0,1:T(8,128)} %get-tuple-element.55), channel_id=1, source_target_pairs={{28,24},{24,28},{20,16},{16,20},{12,8},{8,12},{4,0},{0,4},{29,25},... | collective-permute-start | bytes 983048 | tf_op jit(solution)/shard_map/ppermute | solution.py:82
  106.3 4.4 %collective-permute-start.19 = (f32[128,128]{1,0:T(8,128)S(1)}, f32[128,128]{1,0:T(8,128)}, u32[]{:S(2)}, u32[]{:S(2)}) collective-permute-start(f32[128,128]{1,0:T(8,128)S(1)} %add.158), channel_id=1, source_target_pairs={{0,2},{1,3},{2,0},{3,1},{4,6},{5,7},{6,4},{7,5},{8,10},{9,11},{10,... | collective-permute-start | bytes 196616 | tf_op jit(solution)/shard_map/ppermute | solution.py:94
  118.1 1.3 %collective-permute-start.16 = (f32[128,128]{1,0:T(8,128)S(1)}, f32[128,128]{1,0:T(8,128)S(1)}, u32[]{:S(2)}, u32[]{:S(2)}) collective-permute-start(f32[128,128]{1,0:T(8,128)S(1)} %convolution_add_fusion.1), channel_id=1, source_target_pairs={{0,1},{1,0},{2,3},{3,2},{4,5},{5,4},{6,7},{7,6},{8,9},{9,8},{10,11... | collective-permute-start | bytes 196616 | tf_op jit(solution)/shard_map/ppermute | solution.py:94
  119.4 4.3 %collective-permute-start.17 = (f32[128,128]{1,0:T(8,128)S(1)}, f32[128,128]{1,0:T(8,128)S(1)}, u32[]{:S(2)}, u32[]{:S(2)}) collective-permute-start(f32[128,128]{1,0:T(8,128)S(1)} %add.155), channel_id=1, source_target_pairs={{0,2},{1,3},{2,0},{3,1},{4,6},{5,7},{6,4},{7,5},{8,10},{9,11},{10,... | collective-permute-start | bytes 196616 | tf_op jit(solution)/shard_map/ppermute | solution.py:94
  (20 other events, 34.9 us)

commit v11 on v9

--- a/solution.py
+++ b/solution.py
@@ -97,6 +97,20 @@
     return parts
 
 
+def fan_psum(parts, axis):
+    count = lax.axis_size(axis)
+    if count & (count - 1):
+        return lax.psum(parts, axis)
+    got = [parts] + [
+        lax.ppermute(parts, axis, [(i, i ^ m) for i in range(count)]) for m in range(1, count)
+    ]
+    k = 1
+    while k < count:
+        got = [got[m] + got[m ^ k] if m % (2 * k) == 0 else None for m in range(count)]
+        k *= 2
+    return got[0]
+
+
 def block_step(carry_state, inputs, skip_scale):
     feat_block, step_block, decay_block, write_block, read_block = inputs
     length = decay_block.shape[1]
@@ -239,8 +253,9 @@
     active = gate_pre * sigmoid_gate
     gated_out = mixed_out * active
     weighted = out_grad * norm_gain[None, :]
-    square_sum, cross_sum = butterfly_psum(
-        (jnp.sum(gated_out * gated_out, axis=1), jnp.sum(weighted * gated_out, axis=1)), "head"
+    square_sum, cross_sum = fan_psum(
+        jnp.stack([jnp.sum(gated_out * gated_out, axis=1), jnp.sum(weighted * gated_out, axis=1)]),
+        "head",
     )
     inverse = lax.rsqrt(square_sum / channels + eps)
     grad_gated = (

time: 118 us -> 122 us (1.034)
  waiting for transfers between devices: 66.5 us -> 71.2 us
  starting transfers between devices: 22.3 us -> 20.9 us
    ppermute x2, waiting for transfers between devices: 30.4 us -> 33.9 us  [pair_scan(): s_in = lax.ppermute(out[1], axis, pairs)]
    ppermute x8 -> x4, starting transfers between devices: 4.14 us -> 0.88 us  [butterfly_psum(): got = lax.ppermute(parts, axis, [(i, i ^ k) for i in range(count)])]
    ppermute x8 -> x4, waiting for transfers between devices: 9.28 us -> 6.3 us  [butterfly_psum(): got = lax.ppermute(parts, axis, [(i, i ^ k) for i in range(count)])]
    ppermute x0 -> x3, waiting for transfers between devices: none -> 2.71 us  [fan_psum(): lax.ppermute(parts, axis, [(i, i ^ m) for i in range(count)])]
    ppermute x0 -> x3, starting transfers between devices: none -> 1.93 us  [fan_psum(): lax.ppermute(parts, axis, [(i, i ^ m) for i in range(count)])]
    ppermute x4, waiting for transfers between devices: 16.3 us -> 17.7 us  [pair_scan(): a_rcv, s_rcv = lax.ppermute((a_snd, s_snd), axis, swap)]
  transfers between devices with their start and end apart: 20 -> 19, of which waited for: 13 -> 12; matrix products, arithmetic and copies ran while one was open for 8% -> 8% of each run, Pallas kernels for 0% -> 0%
where the time goes in v11:
time: 122 us; the launch traced here: 121 us
  waiting for transfers between devices  71.2 us (58%)
  starting transfers between devices  20.9 us (17%)
  matrix products  13.6 us (11%)
  other arithmetic  7.85 us (6%)
  local copies, waits for them, and re-layouts  6.43 us (5%)
    ppermute x2, waiting for transfers between devices, pair_scan(): s_in = lax.ppermute(out[1], axis, pairs)  33.9 us
    ppermute x4, waiting for transfers between devices, pair_scan(): a_rcv, s_rcv = lax.ppermute((a_snd, s_snd), axis, swap)  17.7 us
    ppermute x4, starting transfers between devices, pair_scan(): a_in, s_in = lax.ppermute(out, axis, pairs)  6.48 us
    ppermute x4, starting transfers between devices, pair_scan(): a_rcv, s_rcv = lax.ppermute((a_snd, s_snd), axis, swap)  6.35 us
    ppermute x4, waiting for transfers between devices, butterfly_psum(): got = lax.ppermute(parts, axis, [(i, i ^ k) for i in range(count)])  6.3 us
    dot_general x3, matrix products, within_part(): within = jnp.einsum('hij,jhp->ihp', masked, scaled, precision=highest)  6.03 us
    ppermute x2, waiting for transfers between devices, pair_scan(): other = lax.ppermute(send, axis, swap)  5.67 us
    ppermute x4, waiting for transfers between devices, pair_scan(): a_in, s_in = lax.ppermute(out, axis, pairs)  4.83 us
  transfers between devices with their start and end apart: 19, of which 12 were waited for; matrix products, arithmetic and copies ran while one was open for 8% of the time, Pallas kernels for 0%

profile of v11, /device:TPU:0, one launch (start us, length us, event | category | flops | bytes accessed | tf_op | source)
XLA Modules:
  0.0 121.2 jit_solution(14515011942472873833)
XLA Ops:
  0.7 0.9 fusion.60
  1.8 1.3 %copy.22 = f32[128,1280]{0,1:T(8,128)S(1)} copy(f32[128,1280]{1,0:T(8,128)} %param.9) | data formatting | bytes 1310720 | tf_op args[0]
  3.6 3.0 %collective-permute-start.1 = (f32[10,64,128]{2,1,0:T(8,128)S(1)}, f32[10,64,128]{2,1,0:T(8,128)S(1)}, u32[]{:S(2)}, u32[]{:S(2)}) collective-permute-start(f32[10,64,128]{2,1,0:T(8,128)S(1)} %constant_dynamic-slice_fusion.1), channel_id=1, source_target_pairs={{0,4},{4,0},{8,12},{12,8},{16,20},{20,16},{24,28},{28,24},{1,5},{5... | collective-permute-start | bytes 983048 | tf_op jit(solution)/shard_map/ppermute | solution.py:42
  6.8 7.6 %collective-permute-done.9 = f32[10]{0:T(128)S(1)} collective-permute-done((f32[10]{0:T(128)S(1)}, f32[10]{0:T(128)S(1)}, u32[]{:S(2)}, u32[]{:S(2)}) %collective-permute-start.9) | collective-permute-done | bytes 72 | tf_op jit(solution)/shard_map/ppermute | solution.py:42
  15.0 1.7 %collective-permute-start = (f32[10]{0:T(128)S(1)}, f32[10]{0:T(128)S(1)}, u32[]{:S(2)}, u32[]{:S(2)}) collective-permute-start(f32[10]{0:T(128)S(1)} %get-tuple-element.52), channel_id=1, source_target_pairs={{0,4},{4,0},{8,12},{12,8},{16,20},{20,16},{24,28},{28,24},{1,5},{5... | collective-permute-start | bytes 128 | tf_op jit(solution)/shard_map/ppermute | solution.py:42
  16.8 1.8 %collective-permute-done = f32[10]{0:T(128)S(1)} collective-permute-done((f32[10]{0:T(128)S(1)}, f32[10]{0:T(128)S(1)}, u32[]{:S(2)}, u32[]{:S(2)}) %collective-permute-start) | collective-permute-done | bytes 72 | tf_op jit(solution)/shard_map/ppermute | solution.py:42
  18.8 3.7 %collective-permute-start.2 = (f32[10,64,128]{2,1,0:T(8,128)S(1)}, f32[10,64,128]{2,1,0:T(8,128)S(1)}, u32[]{:S(2)}, u32[]{:S(2)}) collective-permute-start(f32[10,64,128]{2,1,0:T(8,128)S(1)} %get-tuple-element.36), channel_id=1, source_target_pairs={{0,8},{4,12},{1,9},{5,13},{2,10},{6,14},{3,11},{7,15}} | collective-permute-start | bytes 983048 | tf_op jit(solution)/shard_map/ppermute | solution.py:62
  22.5 4.8 %collective-permute-done.2 = f32[10,64,128]{2,1,0:T(8,128)S(1)} collective-permute-done((f32[10,64,128]{2,1,0:T(8,128)S(1)}, f32[10,64,128]{2,1,0:T(8,128)S(1)}, u32[]{:S(2)}, u32[]{:S(2)}) %collective-permute-start.2) | collective-permute-done | bytes 327712 | tf_op jit(solution)/shard_map/ppermute | solution.py:62
  29.1 1.6 %collective-permute-start.5 = (f32[10,64,128]{2,1,0:T(8,128)S(1)}, f32[10,64,128]{2,1,0:T(8,128)S(1)}, u32[]{:S(2)}, u32[]{:S(2)}) collective-permute-start(f32[10,64,128]{2,1,0:T(8,128)S(1)} %get-tuple-element.48), channel_id=1, source_target_pairs={{0,4},{4,0},{8,12},{12,8},{16,20},{20,16},{24,28},{28,24},{1,5},{5... | collective-permute-start | bytes 983048 | tf_op jit(solution)/shard_map/ppermute | solution.py:82
  30.9 5.3 %collective-permute-done.5 = f32[10,64,128]{2,1,0:T(8,128)S(1)} collective-permute-done((f32[10,64,128]{2,1,0:T(8,128)S(1)}, f32[10,64,128]{2,1,0:T(8,128)S(1)}, u32[]{:S(2)}, u32[]{:S(2)}) %collective-permute-start.5) | collective-permute-done | bytes 327712 | tf_op jit(solution)/shard_map/ppermute | solution.py:82
  37.0 2.3 %multiply_add_fusion.1 = f32[128,20,64]{0,2,1:T(8,128)} fusion(f32[128,20,64]{0,2,1:T(8,128)S(1)} %convolution_bitcast_fusion.1, f32[128,20,64]{0,2,1:T(8,128)S(1)} %bitcast.83, f32[128,128]{1,0:T(8,128)S(1)} %fusion.86, f32[20,128]{1,0:T(8,128)S(1)} %bitcast.95, pred[128,128]{1,0:T(8,128)(4,1)S(1)} %iota_compare_fusion.6, ...), kind=kOutput, calls=%fused_computation.35 | convolution fusion | flops 127959040 | bytes 2078800 | tf_op jit(solution)/shard_map/jvp(hij,jhp->ihp)/dot_general | solution.py:181
  39.3 1.4 %copy.23 = f32[128,1280]{1,0:T(8,128)S(1)} copy(f32[128,1280]{0,1:T(8,128)} %bitcast.93) | data formatting | bytes 1310720 | tf_op jit(solution)/shard_map/add | solution.py:240
  40.7 1.5 %multiply_reduce_fusion.7 = (f32[128]{0:T(128)S(1)}, f32[128]{0:T(128)S(1)}) fusion(f32[128,1280]{1,0:T(8,128)S(1)} %copy.23, f32[128,1280]{1,0:T(8,128)S(1)} %copy-done.1, f32[128,1280]{1,0:T(8,128)} %param.17, f32[1280]{0:T(1024)S(1)} %copy-done.11), kind=kLoop, calls=%fused_computation.32 | loop fusion | flops 1638144 | bytes 1972224 | tf_op jit(solution)/shard_map/reduce_sum | solution.py:257
  42.3 1.6 %collective-permute-start.7 = (f32[2,128]{1,0:T(2,128)S(1)}, f32[2,128]{1,0:T(2,128)S(1)}, u32[]{:S(2)}, u32[]{:S(2)}) collective-permute-start(f32[2,128]{1,0:T(2,128)S(1)} %pad_maximum_fusion), channel_id=1, source_target_pairs={{0,2},{1,3},{2,0},{3,1},{4,6},{5,7},{6,4},{7,5},{8,10},{9,11},{10,... | collective-permute-start | bytes 3080 | tf_op jit(solution)/shard_map/ppermute | solution.py:105
  44.2 1.8 %collective-permute-done.7 = f32[2,128]{1,0:T(2,128)S(1)} collective-permute-done((f32[2,128]{1,0:T(2,128)S(1)}, f32[2,128]{1,0:T(2,128)S(1)}, u32[]{:S(2)}, u32[]{:S(2)}) %collective-permute-start.7) | collective-permute-done | bytes 1056 | tf_op jit(solution)/shard_map/ppermute | solution.py:105
  46.0 0.9 collective-permute-done.8
  46.9 1.5 %add_multiply_fusion = (f32[128,1280]{1,0:T(8,128)}, f32[128,1280]{1,0:T(8,128)}) fusion(f32[128,1280]{1,0:T(8,128)S(1)} %copy-done.1, f32[128,1280]{1,0:T(8,128)S(1)} %copy.23, f32[128]{0:T(128)S(1)} %fusion.72, f32[128,1280]{1,0:T(8,128)S(1)} %copy-done.2, f32[128]{0:T(128)S(1)} %rsqrt_bitcast_fusion, f32[1280]{0:T(1024)S(1)} %copy-done.11), kind=kLoop, calls=%fused_computation.28 | loop fusion | flops 2621440 | bytes 3282944 | tf_op jit(solution)/shard_map/mul | solution.py:266
  48.4 1.3 %copy.24 = f32[128,1280]{0,1:T(8,128)S(1)} copy(f32[128,1280]{1,0:T(8,128)} %get-tuple-element.43) | data formatting | bytes 1310720 | tf_op jit(solution)/shard_map/mul | solution.py:265
  50.2 1.6 %collective-permute-start.10 = (f32[10,64,128]{2,1,0:T(8,128)S(1)}, f32[10,64,128]{2,1,0:T(8,128)S(1)}, u32[]{:S(2)}, u32[]{:S(2)}) collective-permute-start(f32[10,64,128]{2,1,0:T(8,128)S(1)} %constant_dynamic-slice_fusion), channel_id=1, source_target_pairs={{28,24},{24,28},{20,16},{16,20},{12,8},{8,12},{4,0},{0,4},{29,25},... | collective-permute-start | bytes 983048 | tf_op jit(solution)/shard_map/ppermute | solution.py:42
  51.7 8.3 %collective-permute-done.10 = f32[10,64,128]{2,1,0:T(8,128)S(1)} collective-permute-done((f32[10,64,128]{2,1,0:T(8,128)S(1)}, f32[10,64,128]{2,1,0:T(8,128)S(1)}, u32[]{:S(2)}, u32[]{:S(2)}) %collective-permute-start.10) | collective-permute-done | bytes 327712 | tf_op jit(solution)/shard_map/ppermute | solution.py:42
  60.0 0.8 broadcast_add_fusion
  60.9 1.4 %collective-permute-start.11 = (f32[10,64,128]{2,1,0:T(8,128)}, f32[10,64,128]{2,1,0:T(8,128)}, u32[]{:S(2)}, u32[]{:S(2)}) collective-permute-start(f32[10,64,128]{2,1,0:T(8,128)} %get-tuple-element.28), channel_id=1, source_target_pairs={{28,20},{24,16},{29,21},{25,17},{30,22},{26,18},{31,23},{27,19}} | collective-permute-start | bytes 983048 | tf_op jit(solution)/shard_map/ppermute | solution.py:62
  63.1 2.0 %fusion.19 = (f32[20,128]{1,0:T(8,128)S(1)}, f32[20,128]{1,0:T(8,128)S(1)}, f32[128,128]{1,0:T(8,128)S(1)}) fusion(f32[128,128]{1,0:T(8,128)S(1)} %fusion.86, f32[20,128]{1,0:T(8,128)S(1)} %bitcast.96, pred[128,128]{1,0:T(8,128)(4,1)S(1)} %iota_compare_fusion.6, f32[20,64,128]{2,1,0:T(8,128)S(1)} %bitcast.88, f32[128,20,64]{0,2,1:T(8,128)S(1)} %bitcast.84, ...), kind=kOutput, calls=%fused_computation.20 | convolution fusion | flops 129575936 | bytes 1499136 | tf_op jit(solution)/shard_map/transpose(jvp(hij,jhp->ihp))/dot_general | solution.py:181
  65.3 1.5 %collective-permute-start.13 = (f32[10,64,128]{2,1,0:T(8,128)S(1)}, f32[10,64,128]{2,1,0:T(8,128)S(1)}, u32[]{:S(2)}, u32[]{:S(2)}) collective-permute-start(f32[10,64,128]{2,1,0:T(8,128)S(1)} %get-tuple-element.26), channel_id=1, source_target_pairs={{12,4},{8,0},{13,5},{9,1},{14,6},{10,2},{15,7},{11,3}} | collective-permute-start | bytes 983048 | tf_op jit(solution)/shard_map/ppermute | solution.py:59
  67.7 1.8 %fusion.12 = f32[128,20,64]{0,2,1:T(8,128)} fusion(f32[20,64,128]{2,1,0:T(8,128)S(1)} %bitcast.90, f32[128,128]{1,0:T(8,128)S(1)} %fusion.86, f32[20,128]{1,0:T(8,128)S(1)} %bitcast.97, pred[128,128]{1,0:T(8,128)(4,1)S(1)} %iota_compare_fusion.6), kind=kOutput, calls=%fused_computation.11 | convolution fusion | flops 127139840 | bytes 1402880 | tf_op jit(solution)/shard_map/transpose(jvp(hij,jhp->ihp))/dot_general | solution.py:181
  69.4 33.9 %collective-permute-done.13 = f32[10,64,128]{2,1,0:T(8,128)S(1)} collective-permute-done((f32[10,64,128]{2,1,0:T(8,128)S(1)}, f32[10,64,128]{2,1,0:T(8,128)S(1)}, u32[]{:S(2)}, u32[]{:S(2)}) %collective-permute-start.13) | collective-permute-done | bytes 327712 | tf_op jit(solution)/shard_map/ppermute | solution.py:59
  103.5 1.6 %collective-permute-start.14 = (f32[10,64,128]{2,1,0:T(8,128)S(1)}, f32[10,64,128]{2,1,0:T(8,128)S(1)}, u32[]{:S(2)}, u32[]{:S(2)}) collective-permute-start(f32[10,64,128]{2,1,0:T(8,128)S(1)} %get-tuple-element.46), channel_id=1, source_target_pairs={{28,24},{24,28},{20,16},{16,20},{12,8},{8,12},{4,0},{0,4},{29,25},... | collective-permute-start | bytes 983048 | tf_op jit(solution)/shard_map/ppermute | solution.py:82
  105.9 3.8 %collective-permute-done.18 = f32[128,128]{1,0:T(8,128)S(1)} collective-permute-done((f32[128,128]{1,0:T(8,128)S(1)}, f32[128,128]{1,0:T(8,128)S(1)}, u32[]{:S(2)}, u32[]{:S(2)}) %collective-permute-start.18) | collective-permute-done | bytes 65568 | tf_op jit(solution)/shard_map/ppermute | solution.py:94
  111.6 2.0 %multiply_reduce_fusion.2 = (f32[128,20]{0,1:T(8,128)S(1)}, f32[128,20]{0,1:T(8,128)S(1)}, f32[128,20]{0,1:T(8,128)S(1)}, f32[128,20,64]{0,2,1:T(8,128)S(1)}, f32[128,20]{0,1:T(8,128)S(1)}) fusion(f32[128,20,64]{0,2,1:T(8,128)S(1)} %bitcast.85, f32[128,20]{0,1:T(8,128)S(1)} %bitcast.102, f32[128,20]{0,1:T(8,128)S(1)} %get-tuple-element.51, ...), kind=kOutput, calls=%fused_computation.24 | convolution fusion | flops 128768000 | bytes 4059217 | tf_op jit(solution)/shard_map/transpose(jvp(jhp,jn->hpn))/dot_general | solution.py:200
  116.6 0.8 fusion.17
  117.4 1.1 copy.28
  118.5 2.1 %collective-permute-done.16 = f32[128,128]{1,0:T(8,128)S(1)} collective-permute-done((f32[128,128]{1,0:T(8,128)S(1)}, f32[128,128]{1,0:T(8,128)S(1)}, u32[]{:S(2)}, u32[]{:S(2)}) %collective-permute-start.16) | collective-permute-done | bytes 65568 | tf_op jit(solution)/shard_map/ppermute | solution.py:94
  (94 shorter events, 13.4 us)
Async XLA Ops:
  0.6 2.5 %copy-start = (f32[128,128]{1,0:T(8,128)S(1)}, f32[128,128]{1,0:T(8,128)}, u32[]{:S(2)}) copy-start(f32[128,128]{1,0:T(8,128)} %param.11) | copy-start | bytes 196612
  1.8 1.4 %copy-start.10 = (f32[20,128]{1,0:T(8,128)S(1)}, f32[20,128]{1,0:T(8,128)}, u32[]{:S(2)}) copy-start(f32[20,128]{1,0:T(8,128)} %param.13) | copy-start | bytes 30724
  3.6 15.0 %collective-permute-start.1 = (f32[10,64,128]{2,1,0:T(8,128)S(1)}, f32[10,64,128]{2,1,0:T(8,128)S(1)}, u32[]{:S(2)}, u32[]{:S(2)}) collective-permute-start(f32[10,64,128]{2,1,0:T(8,128)S(1)} %constant_dynamic-slice_fusion.1), channel_id=1, source_target_pairs={{0,4},{4,0},{8,12},{12,8},{16,20},{20,16},{24,28},{28,24},{1,5},{5... | collective-permute-start | bytes 983048 | tf_op jit(solution)/shard_map/ppermute | solution.py:42
  6.7 7.7 %collective-permute-start.9 = (f32[10]{0:T(128)S(1)}, f32[10]{0:T(128)S(1)}, u32[]{:S(2)}, u32[]{:S(2)}) collective-permute-start(f32[10]{0:T(128)S(1)} %dynamic_slice.29), channel_id=1, source_target_pairs={{28,24},{24,28},{20,16},{16,20},{12,8},{8,12},{4,0},{0,4},{29,25},... | collective-permute-start | bytes 128 | tf_op jit(solution)/shard_map/ppermute | solution.py:42
  14.4 2.3 %copy-start.12 = (f32[10]{0:T(128)}, f32[10]{0:T(128)S(1)}, u32[]{:S(2)}) copy-start(f32[10]{0:T(128)S(1)} %collective-permute-done.9) | copy-start | bytes 124
  15.0 3.5 %collective-permute-start = (f32[10]{0:T(128)S(1)}, f32[10]{0:T(128)S(1)}, u32[]{:S(2)}, u32[]{:S(2)}) collective-permute-start(f32[10]{0:T(128)S(1)} %get-tuple-element.52), channel_id=1, source_target_pairs={{0,4},{4,0},{8,12},{12,8},{16,20},{20,16},{24,28},{28,24},{1,5},{5... | collective-permute-start | bytes 128 | tf_op jit(solution)/shard_map/ppermute | solution.py:42
  18.8 8.6 %collective-permute-start.2 = (f32[10,64,128]{2,1,0:T(8,128)S(1)}, f32[10,64,128]{2,1,0:T(8,128)S(1)}, u32[]{:S(2)}, u32[]{:S(2)}) collective-permute-start(f32[10,64,128]{2,1,0:T(8,128)S(1)} %get-tuple-element.36), channel_id=1, source_target_pairs={{0,8},{4,12},{1,9},{5,13},{2,10},{6,14},{3,11},{7,15}} | collective-permute-start | bytes 983048 | tf_op jit(solution)/shard_map/ppermute | solution.py:62
  27.5 0.7 collective-permute-start.3
  28.3 0.7 collective-permute-start.4
  29.0 1.7 %copy-start.9 = (f32[128,128]{1,0:T(8,128)S(1)}, f32[128,128]{1,0:T(8,128)}, u32[]{:S(2)}) copy-start(f32[128,128]{1,0:T(8,128)} %param.12) | copy-start | bytes 196612
  29.1 7.1 %collective-permute-start.5 = (f32[10,64,128]{2,1,0:T(8,128)S(1)}, f32[10,64,128]{2,1,0:T(8,128)S(1)}, u32[]{:S(2)}, u32[]{:S(2)}) collective-permute-start(f32[10,64,128]{2,1,0:T(8,128)S(1)} %get-tuple-element.48), channel_id=1, source_target_pairs={{0,4},{4,0},{8,12},{12,8},{16,20},{20,16},{24,28},{28,24},{1,5},{5... | collective-permute-start | bytes 983048 | tf_op jit(solution)/shard_map/ppermute | solution.py:82
  39.3 1.4 %copy-start.1 = (f32[128,1280]{1,0:T(8,128)S(1)}, f32[128,1280]{1,0:T(8,128)}, u32[]{:S(2)}) copy-start(f32[128,1280]{1,0:T(8,128)} %param.10) | copy-start | bytes 1966084
  39.3 1.4 %copy-start.11 = (f32[1280]{0:T(1024)S(1)}, f32[1280]{0:T(1024)}, u32[]{:S(2)}) copy-start(f32[1280]{0:T(1024)} %param.16) | copy-start | bytes 15364
  40.7 6.2 %copy-start.2 = (f32[128,1280]{1,0:T(8,128)S(1)}, f32[128,1280]{1,0:T(8,128)}, u32[]{:S(2)}) copy-start(f32[128,1280]{1,0:T(8,128)} %param.17) | copy-start | bytes 1966084
  42.2 1.9 %collective-permute-start.6 = (f32[2,128]{1,0:T(2,128)S(1)}, f32[2,128]{1,0:T(2,128)S(1)}, u32[]{:S(2)}, u32[]{:S(2)}) collective-permute-start(f32[2,128]{1,0:T(2,128)S(1)} %pad_maximum_fusion), channel_id=1, source_target_pairs={{0,1},{1,0},{2,3},{3,2},{4,5},{5,4},{6,7},{7,6},{8,9},{9,8},{10,11... | collective-permute-start | bytes 3080 | tf_op jit(solution)/shard_map/ppermute | solution.py:105
  42.3 3.6 %collective-permute-start.7 = (f32[2,128]{1,0:T(2,128)S(1)}, f32[2,128]{1,0:T(2,128)S(1)}, u32[]{:S(2)}, u32[]{:S(2)}) collective-permute-start(f32[2,128]{1,0:T(2,128)S(1)} %pad_maximum_fusion), channel_id=1, source_target_pairs={{0,2},{1,3},{2,0},{3,1},{4,6},{5,7},{6,4},{7,5},{8,10},{9,11},{10,... | collective-permute-start | bytes 3080 | tf_op jit(solution)/shard_map/ppermute | solution.py:105
  43.9 3.0 %collective-permute-start.8 = (f32[2,128]{1,0:T(2,128)S(1)}, f32[2,128]{1,0:T(2,128)S(1)}, u32[]{:S(2)}, u32[]{:S(2)}) collective-permute-start(f32[2,128]{1,0:T(2,128)S(1)} %pad_maximum_fusion), channel_id=1, source_target_pairs={{0,3},{1,2},{2,1},{3,0},{4,7},{5,6},{6,5},{7,4},{8,11},{9,10},{10,... | collective-permute-start | bytes 3080 | tf_op jit(solution)/shard_map/ppermute | solution.py:105
  50.2 9.9 %collective-permute-start.10 = (f32[10,64,128]{2,1,0:T(8,128)S(1)}, f32[10,64,128]{2,1,0:T(8,128)S(1)}, u32[]{:S(2)}, u32[]{:S(2)}) collective-permute-start(f32[10,64,128]{2,1,0:T(8,128)S(1)} %constant_dynamic-slice_fusion), channel_id=1, source_target_pairs={{28,24},{24,28},{20,16},{16,20},{12,8},{8,12},{4,0},{0,4},{29,25},... | collective-permute-start | bytes 983048 | tf_op jit(solution)/shard_map/ppermute | solution.py:42
  60.9 1.4 %collective-permute-start.11 = (f32[10,64,128]{2,1,0:T(8,128)}, f32[10,64,128]{2,1,0:T(8,128)}, u32[]{:S(2)}, u32[]{:S(2)}) collective-permute-start(f32[10,64,128]{2,1,0:T(8,128)} %get-tuple-element.28), channel_id=1, source_target_pairs={{28,20},{24,16},{29,21},{25,17},{30,22},{26,18},{31,23},{27,19}} | collective-permute-start | bytes 983048 | tf_op jit(solution)/shard_map/ppermute | solution.py:62
  62.4 2.8 %collective-permute-start.12 = (f32[10,64,128]{2,1,0:T(8,128)S(1)}, f32[10,64,128]{2,1,0:T(8,128)S(1)}, u32[]{:S(2)}, u32[]{:S(2)}) collective-permute-start(f32[10,64,128]{2,1,0:T(8,128)S(1)} %multiply_add_fusion.3), channel_id=1, source_target_pairs={{20,12},{16,8},{21,13},{17,9},{22,14},{18,10},{23,15},{19,11}} | collective-permute-start | bytes 983048 | tf_op jit(solution)/shard_map/ppermute | solution.py:62
  65.2 1.6 %copy-start.8 = (f32[10,64,128]{2,1,0:T(8,128)S(1)}, f32[10,64,128]{2,1,0:T(8,128)}, u32[]{:S(2)}) copy-start(f32[10,64,128]{2,1,0:T(8,128)} %copy-done.7) | copy-start | bytes 983044
  65.3 38.0 %collective-permute-start.13 = (f32[10,64,128]{2,1,0:T(8,128)S(1)}, f32[10,64,128]{2,1,0:T(8,128)S(1)}, u32[]{:S(2)}, u32[]{:S(2)}) collective-permute-start(f32[10,64,128]{2,1,0:T(8,128)S(1)} %get-tuple-element.26), channel_id=1, source_target_pairs={{12,4},{8,0},{13,5},{9,1},{14,6},{10,2},{15,7},{11,3}} | collective-permute-start | bytes 983048 | tf_op jit(solution)/shard_map/ppermute | solution.py:59
  67.6 35.8 %copy-start.6 = (f32[10,64,128]{2,1,0:T(8,128)S(1)}, f32[10,64,128]{2,1,0:T(8,128)}, u32[]{:S(2)}) copy-start(f32[10,64,128]{2,1,0:T(8,128)} %copy-done.5) | copy-start | bytes 983044
  67.6 35.8 %copy-start.13 = (f32[10]{0:T(128)S(1)}, f32[10]{0:T(128)}, u32[]{:S(2)}) copy-start(f32[10]{0:T(128)} %copy-done.12) | copy-start | bytes 124
  67.6 35.8 %copy-start.14 = (f32[10]{0:T(128)S(1)}, f32[10]{0:T(128)}, u32[]{:S(2)}) copy-start(f32[10]{0:T(128)} %get-tuple-element.33) | copy-start | bytes 124
  67.6 37.8 %collective-permute-start.17 = (f32[128,128]{1,0:T(8,128)S(1)}, f32[128,128]{1,0:T(8,128)S(1)}, u32[]{:S(2)}, u32[]{:S(2)}) collective-permute-start(f32[128,128]{1,0:T(8,128)S(1)} %fusion.16), channel_id=1, source_target_pairs={{0,1},{1,0},{2,3},{3,2},{4,5},{5,4},{6,7},{7,6},{8,9},{9,8},{10,11... | collective-permute-start | bytes 196616 | tf_op jit(solution)/shard_map/ppermute | solution.py:94
  103.5 7.1 %collective-permute-start.14 = (f32[10,64,128]{2,1,0:T(8,128)S(1)}, f32[10,64,128]{2,1,0:T(8,128)S(1)}, u32[]{:S(2)}, u32[]{:S(2)}) collective-permute-start(f32[10,64,128]{2,1,0:T(8,128)S(1)} %get-tuple-element.46), channel_id=1, source_target_pairs={{28,24},{24,28},{20,16},{16,20},{12,8},{8,12},{4,0},{0,4},{29,25},... | collective-permute-start | bytes 983048 | tf_op jit(solution)/shard_map/ppermute | solution.py:82
  105.4 4.3 %collective-permute-start.18 = (f32[128,128]{1,0:T(8,128)S(1)}, f32[128,128]{1,0:T(8,128)S(1)}, u32[]{:S(2)}, u32[]{:S(2)}) collective-permute-start(f32[128,128]{1,0:T(8,128)S(1)} %add.173), channel_id=1, source_target_pairs={{0,2},{1,3},{2,0},{3,1},{4,6},{5,7},{6,4},{7,5},{8,10},{9,11},{10,... | collective-permute-start | bytes 196616 | tf_op jit(solution)/shard_map/ppermute | solution.py:94
  110.7 0.9 copy-start.16
  111.6 2.5 %copy-start.4 = (f32[10,64,128]{2,1,0:T(8,128)S(1)}, f32[10,64,128]{2,1,0:T(8,128)}, u32[]{:S(2)}) copy-start(f32[10,64,128]{2,1,0:T(8,128)} %copy-done.3) | copy-start | bytes 983044
  114.9 1.3 %collective-permute-start.15 = (f32[128,128]{1,0:T(8,128)S(1)}, f32[128,128]{1,0:T(8,128)S(1)}, u32[]{:S(2)}, u32[]{:S(2)}) collective-permute-start(f32[128,128]{1,0:T(8,128)S(1)} %fusion.15), channel_id=1, source_target_pairs={{0,1},{1,0},{2,3},{3,2},{4,5},{5,4},{6,7},{7,6},{8,9},{9,8},{10,11... | collective-permute-start | bytes 196616 | tf_op jit(solution)/shard_map/ppermute | solution.py:94
  116.2 4.3 %collective-permute-start.16 = (f32[128,128]{1,0:T(8,128)S(1)}, f32[128,128]{1,0:T(8,128)S(1)}, u32[]{:S(2)}, u32[]{:S(2)}) collective-permute-start(f32[128,128]{1,0:T(8,128)S(1)} %add.170), channel_id=1, source_target_pairs={{0,2},{1,3},{2,0},{3,1},{4,6},{5,7},{6,4},{7,5},{8,10},{9,11},{10,... | collective-permute-start | bytes 196616 | tf_op jit(solution)/shard_map/ppermute | solution.py:94
  (4 other events, 3.0 us)

commit v12 on v9

--- a/solution.py
+++ b/solution.py
@@ -223,6 +223,7 @@
         mixed_c, pull_c = jax.vjp(
             lambda d, r: carried_part(d, r, state_in), log_decay, read_queries
         )
+        mixed_w = lax.optimization_barrier(mixed_w)
         mixed_out = mixed_w + mixed_c
     else:
 

time: 118 us -> 116 us (0.983)
  waiting for transfers between devices: 66.5 us -> 64.1 us
  other arithmetic: 7.83 us -> 9.2 us
    ppermute x2, waiting for transfers between devices: 5.67 us -> 4.18 us  [pair_scan(): other = lax.ppermute(send, axis, swap)]
    add x1 -> x0, local copies, waits for them, and re-layouts: 1.38 us -> none  [local(): mixed_out = mixed_w + mixed_c]
    unnamed x36 -> x46, local copies, waits for them, and re-layouts: 3.23 us -> 3.29 us
  transfers between devices with their start and end apart: 20 -> 20, of which waited for: 13 -> 13; matrix products, arithmetic and copies ran while one was open for 8% -> 11% of each run, Pallas kernels for 0% -> 0%
where the time goes in v12:
time: 116 us
  waiting for transfers between devices  64.1 us (55%)
  starting transfers between devices  22.3 us (19%)
  matrix products  14 us (12%)
  other arithmetic  9.2 us (8%)
  local copies, waits for them, and re-layouts  5.33 us (5%)
  between operations  1.18 us (1%)
    ppermute x2, waiting for transfers between devices, pair_scan(): s_in = lax.ppermute(out[1], axis, pairs)  30.1 us
    ppermute x4, waiting for transfers between devices, pair_scan(): a_rcv, s_rcv = lax.ppermute((a_snd, s_snd), axis, swap)  16.3 us
    ppermute x8, waiting for transfers between devices, butterfly_psum(): got = lax.ppermute(parts, axis, [(i, i ^ k) for i in range(count)])  8.62 us
    ppermute x4, starting transfers between devices, pair_scan(): a_in, s_in = lax.ppermute(out, axis, pairs)  6.52 us
    ppermute x4, starting transfers between devices, pair_scan(): a_rcv, s_rcv = lax.ppermute((a_snd, s_snd), axis, swap)  6.35 us
    dot_general x3, matrix products, within_part(): within = jnp.einsum('hij,jhp->ihp', masked, scaled, precision=highest)  5.17 us
    ppermute x4, waiting for transfers between devices, pair_scan(): a_in, s_in = lax.ppermute(out, axis, pairs)  4.83 us
    ppermute x2, waiting for transfers between devices, pair_scan(): other = lax.ppermute(send, axis, swap)  4.18 us
  transfers between devices with their start and end apart: 20, of which 13 were waited for; matrix products, arithmetic and copies ran while one was open for 11% of the time, Pallas kernels for 0%

profile of v12, /device:TPU:0, one launch (start us, length us, event | category | flops | bytes accessed | tf_op | source)
XLA Modules:
  0.0 116.1 jit_solution(8530932540227722840)
XLA Ops:
  0.7 0.9 fusion.58
  1.8 1.3 %copy.22 = f32[128,1280]{0,1:T(8,128)S(1)} copy(f32[128,1280]{1,0:T(8,128)} %param.9) | data formatting | bytes 1310720 | tf_op args[0]
  3.7 3.0 %collective-permute-start.1 = (f32[10,64,128]{2,1,0:T(8,128)S(1)}, f32[10,64,128]{2,1,0:T(8,128)S(1)}, u32[]{:S(2)}, u32[]{:S(2)}) collective-permute-start(f32[10,64,128]{2,1,0:T(8,128)S(1)} %constant_dynamic-slice_fusion.1), channel_id=1, source_target_pairs={{0,4},{4,0},{8,12},{12,8},{16,20},{20,16},{24,28},{28,24},{1,5},{5... | collective-permute-start | bytes 983048 | tf_op jit(solution)/shard_map/ppermute | solution.py:42
  6.8 7.6 %collective-permute-done.10 = f32[10]{0:T(128)S(1)} collective-permute-done((f32[10]{0:T(128)S(1)}, f32[10]{0:T(128)S(1)}, u32[]{:S(2)}, u32[]{:S(2)}) %collective-permute-start.10) | collective-permute-done | bytes 72 | tf_op jit(solution)/shard_map/ppermute | solution.py:42
  15.0 1.7 %collective-permute-start = (f32[10]{0:T(128)S(1)}, f32[10]{0:T(128)S(1)}, u32[]{:S(2)}, u32[]{:S(2)}) collective-permute-start(f32[10]{0:T(128)S(1)} %get-tuple-element.55), channel_id=1, source_target_pairs={{0,4},{4,0},{8,12},{12,8},{16,20},{20,16},{24,28},{28,24},{1,5},{5... | collective-permute-start | bytes 128 | tf_op jit(solution)/shard_map/ppermute | solution.py:42
  16.8 1.8 %collective-permute-done = f32[10]{0:T(128)S(1)} collective-permute-done((f32[10]{0:T(128)S(1)}, f32[10]{0:T(128)S(1)}, u32[]{:S(2)}, u32[]{:S(2)}) %collective-permute-start) | collective-permute-done | bytes 72 | tf_op jit(solution)/shard_map/ppermute | solution.py:42
  19.3 3.7 %collective-permute-start.2 = (f32[10,64,128]{2,1,0:T(8,128)S(1)}, f32[10,64,128]{2,1,0:T(8,128)S(1)}, u32[]{:S(2)}, u32[]{:S(2)}) collective-permute-start(f32[10,64,128]{2,1,0:T(8,128)S(1)} %get-tuple-element.39), channel_id=1, source_target_pairs={{0,8},{4,12},{1,9},{5,13},{2,10},{6,14},{3,11},{7,15}} | collective-permute-start | bytes 983048 | tf_op jit(solution)/shard_map/ppermute | solution.py:62
  23.1 4.8 %collective-permute-done.2 = f32[10,64,128]{2,1,0:T(8,128)S(1)} collective-permute-done((f32[10,64,128]{2,1,0:T(8,128)S(1)}, f32[10,64,128]{2,1,0:T(8,128)S(1)}, u32[]{:S(2)}, u32[]{:S(2)}) %collective-permute-start.2) | collective-permute-done | bytes 327712 | tf_op jit(solution)/shard_map/ppermute | solution.py:62
  29.9 1.6 %collective-permute-start.5 = (f32[10,64,128]{2,1,0:T(8,128)S(1)}, f32[10,64,128]{2,1,0:T(8,128)S(1)}, u32[]{:S(2)}, u32[]{:S(2)}) collective-permute-start(f32[10,64,128]{2,1,0:T(8,128)S(1)} %get-tuple-element.51), channel_id=1, source_target_pairs={{0,4},{4,0},{8,12},{12,8},{16,20},{20,16},{24,28},{28,24},{1,5},{5... | collective-permute-start | bytes 983048 | tf_op jit(solution)/shard_map/ppermute | solution.py:82
  31.5 1.5 %fusion.9 = f32[128,20,64]{0,2,1:T(8,128)S(1)} fusion(f32[128,20,64]{0,2,1:T(8,128)S(1)} %bitcast.74, f32[128,128]{1,0:T(8,128)S(1)} %fusion.84, f32[20,128]{1,0:T(8,128)S(1)} %bitcast.87, pred[128,128]{1,0:T(8,128)(4,1)S(1)} %iota_compare_fusion.6, f32[128,20]{0,1:T(8,128)S(1)} %bitcast.92, f32[20]{0:T(128)S(1)} %copy-done.20), kind=kOutput, calls=%fused_computation.10 | convolution fusion | flops 127631360 | bytes 1413200 | tf_op jit(solution)/shard_map/jvp(hij,jhp->ihp)/dot_general | solution.py:167
  33.2 3.8 %collective-permute-done.5 = f32[10,64,128]{2,1,0:T(8,128)S(1)} collective-permute-done((f32[10,64,128]{2,1,0:T(8,128)S(1)}, f32[10,64,128]{2,1,0:T(8,128)S(1)}, u32[]{:S(2)}, u32[]{:S(2)}) %collective-permute-start.5) | collective-permute-done | bytes 327712 | tf_op jit(solution)/shard_map/ppermute | solution.py:82
  37.8 1.1 copy.24
  38.9 1.9 %multiply_reduce_fusion.7 = (f32[128]{0:T(128)S(1)}, f32[128]{0:T(128)S(1)}, f32[128,1280]{1,0:T(8,128)S(1)}) fusion(f32[128,1280]{1,0:T(8,128)} %param.10, f32[128,1280]{1,0:T(8,128)} %param.17, f32[1280]{0:T(1024)S(1)} %copy-done.14, f32[128,1280]{1,0:T(8,128)S(1)} %copy.23, f32[128,1280]{1,0:T(8,128)} %copy.24), kind=kLoop, calls=%fused_computation.32 | loop fusion | flops 1801984 | bytes 3282944 | tf_op jit(solution)/shard_map/reduce_sum | solution.py:244
  42.0 1.5 %collective-permute-start.7 = (f32[128]{0:T(128)S(1)}, f32[128]{0:T(128)S(1)}, u32[]{:S(2)}, u32[]{:S(2)}) collective-permute-start(f32[128]{0:T(128)S(1)} %add.143), channel_id=1, source_target_pairs={{0,2},{1,3},{2,0},{3,1},{4,6},{5,7},{6,4},{7,5},{8,10},{9,11},{10,... | collective-permute-start | bytes 1544 | tf_op jit(solution)/shard_map/ppermute | solution.py:94
  44.0 1.5 %collective-permute-done.7 = f32[128]{0:T(128)S(1)} collective-permute-done((f32[128]{0:T(128)S(1)}, f32[128]{0:T(128)S(1)}, u32[]{:S(2)}, u32[]{:S(2)}) %collective-permute-start.7) | collective-permute-done | bytes 544 | tf_op jit(solution)/shard_map/ppermute | solution.py:94
  45.5 1.5 %collective-permute-done.9 = f32[128]{0:T(128)S(1)} collective-permute-done((f32[128]{0:T(128)S(1)}, f32[128]{0:T(128)S(1)}, u32[]{:S(2)}, u32[]{:S(2)}) %collective-permute-start.9) | collective-permute-done | bytes 544 | tf_op jit(solution)/shard_map/ppermute | solution.py:94
  47.1 1.3 %add_multiply_fusion = (f32[128,1280]{1,0:T(8,128)}, f32[128,1280]{1,0:T(8,128)S(1)}) fusion(f32[128,1280]{1,0:T(8,128)S(1)} %copy-done.1, f32[128,1280]{1,0:T(8,128)S(1)} %get-tuple-element.36, f32[128]{0:T(128)S(1)} %get-tuple-element.34, f32[128,1280]{1,0:T(8,128)S(1)} %copy-done.2, f32[1280]{0:T(1024)S(1)} %copy-done.14, f32[128]{0:T(128)S(1)} %get-tuple-element.35), kind=kLoop, calls=%fused_computation.28 | loop fusion | flops 2621440 | bytes 3282944 | tf_op jit(solution)/shard_map/mul | solution.py:252
  49.1 1.6 %collective-permute-start.11 = (f32[10,64,128]{2,1,0:T(8,128)S(1)}, f32[10,64,128]{2,1,0:T(8,128)S(1)}, u32[]{:S(2)}, u32[]{:S(2)}) collective-permute-start(f32[10,64,128]{2,1,0:T(8,128)S(1)} %constant_dynamic-slice_fusion), channel_id=1, source_target_pairs={{28,24},{24,28},{20,16},{16,20},{12,8},{8,12},{4,0},{0,4},{29,25},... | collective-permute-start | bytes 983048 | tf_op jit(solution)/shard_map/ppermute | solution.py:42
  50.6 6.9 %collective-permute-done.11 = f32[10,64,128]{2,1,0:T(8,128)S(1)} collective-permute-done((f32[10,64,128]{2,1,0:T(8,128)S(1)}, f32[10,64,128]{2,1,0:T(8,128)S(1)}, u32[]{:S(2)}, u32[]{:S(2)}) %collective-permute-start.11) | collective-permute-done | bytes 327712 | tf_op jit(solution)/shard_map/ppermute | solution.py:42
  57.5 0.8 broadcast_add_fusion
  58.4 1.4 %collective-permute-start.12 = (f32[10,64,128]{2,1,0:T(8,128)}, f32[10,64,128]{2,1,0:T(8,128)}, u32[]{:S(2)}, u32[]{:S(2)}) collective-permute-start(f32[10,64,128]{2,1,0:T(8,128)} %get-tuple-element.28), channel_id=1, source_target_pairs={{28,20},{24,16},{29,21},{25,17},{30,22},{26,18},{31,23},{27,19}} | collective-permute-start | bytes 983048 | tf_op jit(solution)/shard_map/ppermute | solution.py:62
  60.6 1.9 %fusion.19 = (f32[20,128]{1,0:T(8,128)S(1)}, f32[20,128]{1,0:T(8,128)S(1)}, f32[128,128]{1,0:T(8,128)S(1)}) fusion(f32[128,128]{1,0:T(8,128)S(1)} %fusion.84, f32[20,128]{1,0:T(8,128)S(1)} %bitcast.88, pred[128,128]{1,0:T(8,128)(4,1)S(1)} %iota_compare_fusion.6, f32[20,64,128]{2,1,0:T(8,128)S(1)} %bitcast.79, f32[128,20,64]{0,2,1:T(8,128)S(1)} %bitcast.75, ...), kind=kOutput, calls=%fused_computation.20 | convolution fusion | flops 129575936 | bytes 1499136 | tf_op jit(solution)/shard_map/transpose(jvp(hij,jhp->ihp))/dot_general | solution.py:167
  62.9 1.5 %collective-permute-start.14 = (f32[10,64,128]{2,1,0:T(8,128)S(1)}, f32[10,64,128]{2,1,0:T(8,128)S(1)}, u32[]{:S(2)}, u32[]{:S(2)}) collective-permute-start(f32[10,64,128]{2,1,0:T(8,128)S(1)} %get-tuple-element.26), channel_id=1, source_target_pairs={{12,4},{8,0},{13,5},{9,1},{14,6},{10,2},{15,7},{11,3}} | collective-permute-start | bytes 983048 | tf_op jit(solution)/shard_map/ppermute | solution.py:59
  65.2 1.8 %fusion.12 = f32[128,20,64]{0,2,1:T(8,128)} fusion(f32[20,64,128]{2,1,0:T(8,128)S(1)} %bitcast.81, f32[128,128]{1,0:T(8,128)S(1)} %fusion.84, f32[20,128]{1,0:T(8,128)S(1)} %bitcast.89, pred[128,128]{1,0:T(8,128)(4,1)S(1)} %iota_compare_fusion.6), kind=kOutput, calls=%fused_computation.11 | convolution fusion | flops 127139840 | bytes 1402880 | tf_op jit(solution)/shard_map/transpose(jvp(hij,jhp->ihp))/dot_general | solution.py:167
  67.0 30.1 %collective-permute-done.14 = f32[10,64,128]{2,1,0:T(8,128)S(1)} collective-permute-done((f32[10,64,128]{2,1,0:T(8,128)S(1)}, f32[10,64,128]{2,1,0:T(8,128)S(1)}, u32[]{:S(2)}, u32[]{:S(2)}) %collective-permute-start.14) | collective-permute-done | bytes 327712 | tf_op jit(solution)/shard_map/ppermute | solution.py:59
  97.2 1.6 %collective-permute-start.15 = (f32[10,64,128]{2,1,0:T(8,128)S(1)}, f32[10,64,128]{2,1,0:T(8,128)S(1)}, u32[]{:S(2)}, u32[]{:S(2)}) collective-permute-start(f32[10,64,128]{2,1,0:T(8,128)S(1)} %get-tuple-element.49), channel_id=1, source_target_pairs={{28,24},{24,28},{20,16},{16,20},{12,8},{8,12},{4,0},{0,4},{29,25},... | collective-permute-start | bytes 983048 | tf_op jit(solution)/shard_map/ppermute | solution.py:82
  99.7 0.8 fusion.57
  100.5 2.8 %collective-permute-done.19 = f32[128,128]{1,0:T(8,128)S(1)} collective-permute-done((f32[128,128]{1,0:T(8,128)S(1)}, f32[128,128]{1,0:T(8,128)S(1)}, u32[]{:S(2)}, u32[]{:S(2)}) %collective-permute-start.19) | collective-permute-done | bytes 65568 | tf_op jit(solution)/shard_map/ppermute | solution.py:94
  105.9 2.6 %multiply_reduce_fusion.2 = (f32[128,20]{0,1:T(8,128)S(1)}, f32[128,20]{0,1:T(8,128)S(1)}, f32[128,20]{0,1:T(8,128)S(1)}, f32[128,20,64]{0,2,1:T(8,128)S(1)}, f32[128,20]{0,1:T(8,128)}) fusion(f32[128,20,64]{0,2,1:T(8,128)S(1)} %bitcast.76, f32[128,20]{0,1:T(8,128)S(1)} %bitcast.94, f32[128,20]{0,1:T(8,128)S(1)} %get-tuple-element.54, ...), kind=kOutput, calls=%fused_computation.24 | convolution fusion | flops 128768000 | bytes 4059217 | tf_op jit(solution)/shard_map/transpose(jvp(jhp,jn->hpn))/dot_general | solution.py:186
  111.8 0.8 fusion.17
  112.7 1.1 copy.28
  113.7 1.7 %collective-permute-done.17 = f32[128,128]{1,0:T(8,128)S(1)} collective-permute-done((f32[128,128]{1,0:T(8,128)S(1)}, f32[128,128]{1,0:T(8,128)S(1)}, u32[]{:S(2)}, u32[]{:S(2)}) %collective-permute-start.17) | collective-permute-done | bytes 65568 | tf_op jit(solution)/shard_map/ppermute | solution.py:94
  (106 shorter events, 16.8 us)
Async XLA Ops:
  0.6 28.9 %copy-start = (f32[128,128]{1,0:T(8,128)S(1)}, f32[128,128]{1,0:T(8,128)}, u32[]{:S(2)}) copy-start(f32[128,128]{1,0:T(8,128)} %param.12) | copy-start | bytes 196612
  3.7 15.5 %collective-permute-start.1 = (f32[10,64,128]{2,1,0:T(8,128)S(1)}, f32[10,64,128]{2,1,0:T(8,128)S(1)}, u32[]{:S(2)}, u32[]{:S(2)}) collective-permute-start(f32[10,64,128]{2,1,0:T(8,128)S(1)} %constant_dynamic-slice_fusion.1), channel_id=1, source_target_pairs={{0,4},{4,0},{8,12},{12,8},{16,20},{20,16},{24,28},{28,24},{1,5},{5... | collective-permute-start | bytes 983048 | tf_op jit(solution)/shard_map/ppermute | solution.py:42
  6.8 7.7 %collective-permute-start.10 = (f32[10]{0:T(128)S(1)}, f32[10]{0:T(128)S(1)}, u32[]{:S(2)}, u32[]{:S(2)}) collective-permute-start(f32[10]{0:T(128)S(1)} %dynamic_slice.29), channel_id=1, source_target_pairs={{28,24},{24,28},{20,16},{16,20},{12,8},{8,12},{4,0},{0,4},{29,25},... | collective-permute-start | bytes 128 | tf_op jit(solution)/shard_map/ppermute | solution.py:42
  14.5 2.3 %copy-start.16 = (f32[10]{0:T(128)}, f32[10]{0:T(128)S(1)}, u32[]{:S(2)}) copy-start(f32[10]{0:T(128)S(1)} %collective-permute-done.10) | copy-start | bytes 124
  15.0 3.5 %collective-permute-start = (f32[10]{0:T(128)S(1)}, f32[10]{0:T(128)S(1)}, u32[]{:S(2)}, u32[]{:S(2)}) collective-permute-start(f32[10]{0:T(128)S(1)} %get-tuple-element.55), channel_id=1, source_target_pairs={{0,4},{4,0},{8,12},{12,8},{16,20},{20,16},{24,28},{28,24},{1,5},{5... | collective-permute-start | bytes 128 | tf_op jit(solution)/shard_map/ppermute | solution.py:42
  19.3 8.6 %collective-permute-start.2 = (f32[10,64,128]{2,1,0:T(8,128)S(1)}, f32[10,64,128]{2,1,0:T(8,128)S(1)}, u32[]{:S(2)}, u32[]{:S(2)}) collective-permute-start(f32[10,64,128]{2,1,0:T(8,128)S(1)} %get-tuple-element.39), channel_id=1, source_target_pairs={{0,8},{4,12},{1,9},{5,13},{2,10},{6,14},{3,11},{7,15}} | collective-permute-start | bytes 983048 | tf_op jit(solution)/shard_map/ppermute | solution.py:62
  28.0 0.7 collective-permute-start.3
  28.8 0.9 collective-permute-start.4
  29.7 1.8 %copy-start.20 = (f32[20]{0:T(128)S(1)}, f32[20]{0:T(128)}, u32[]{:S(2)}) copy-start(f32[20]{0:T(128)} %param.15) | copy-start | bytes 244
  29.9 7.1 %collective-permute-start.5 = (f32[10,64,128]{2,1,0:T(8,128)S(1)}, f32[10,64,128]{2,1,0:T(8,128)S(1)}, u32[]{:S(2)}, u32[]{:S(2)}) collective-permute-start(f32[10,64,128]{2,1,0:T(8,128)S(1)} %get-tuple-element.51), channel_id=1, source_target_pairs={{0,4},{4,0},{8,12},{12,8},{16,20},{20,16},{24,28},{28,24},{1,5},{5... | collective-permute-start | bytes 983048 | tf_op jit(solution)/shard_map/ppermute | solution.py:82
  38.9 8.2 %copy-start.1 = (f32[128,1280]{1,0:T(8,128)S(1)}, f32[128,1280]{1,0:T(8,128)}, u32[]{:S(2)}) copy-start(f32[128,1280]{1,0:T(8,128)} %param.10) | copy-start | bytes 1966084
  38.9 8.2 %copy-start.2 = (f32[128,1280]{1,0:T(8,128)S(1)}, f32[128,1280]{1,0:T(8,128)}, u32[]{:S(2)}) copy-start(f32[128,1280]{1,0:T(8,128)} %param.17) | copy-start | bytes 1966084
  40.8 1.2 %collective-permute-start.6 = (f32[128]{0:T(128)S(1)}, f32[128]{0:T(128)S(1)}, u32[]{:S(2)}, u32[]{:S(2)}) collective-permute-start(f32[128]{0:T(128)S(1)} %get-tuple-element.23), channel_id=1, source_target_pairs={{0,1},{1,0},{2,3},{3,2},{4,5},{5,4},{6,7},{7,6},{8,9},{9,8},{10,11... | collective-permute-start | bytes 1544 | tf_op jit(solution)/shard_map/ppermute | solution.py:94
  40.9 2.6 %collective-permute-start.8 = (f32[128]{0:T(128)S(1)}, f32[128]{0:T(128)S(1)}, u32[]{:S(2)}, u32[]{:S(2)}) collective-permute-start(f32[128]{0:T(128)S(1)} %get-tuple-element.24), channel_id=1, source_target_pairs={{0,1},{1,0},{2,3},{3,2},{4,5},{5,4},{6,7},{7,6},{8,9},{9,8},{10,11... | collective-permute-start | bytes 1544 | tf_op jit(solution)/shard_map/ppermute | solution.py:94
  42.0 3.5 %collective-permute-start.7 = (f32[128]{0:T(128)S(1)}, f32[128]{0:T(128)S(1)}, u32[]{:S(2)}, u32[]{:S(2)}) collective-permute-start(f32[128]{0:T(128)S(1)} %add.143), channel_id=1, source_target_pairs={{0,2},{1,3},{2,0},{3,1},{4,6},{5,7},{6,4},{7,5},{8,10},{9,11},{10,... | collective-permute-start | bytes 1544 | tf_op jit(solution)/shard_map/ppermute | solution.py:94
  43.5 3.5 %collective-permute-start.9 = (f32[128]{0:T(128)S(1)}, f32[128]{0:T(128)S(1)}, u32[]{:S(2)}, u32[]{:S(2)}) collective-permute-start(f32[128]{0:T(128)S(1)} %add.147), channel_id=1, source_target_pairs={{0,2},{1,3},{2,0},{3,1},{4,6},{5,7},{6,4},{7,5},{8,10},{9,11},{10,... | collective-permute-start | bytes 1544 | tf_op jit(solution)/shard_map/ppermute | solution.py:94
  49.0 8.5 %copy-start.15 = (f32[10]{0:T(128)S(1)}, f32[10]{0:T(128)}, u32[]{:S(2)}) copy-start(f32[10]{0:T(128)} %get-tuple-element.32) | copy-start | bytes 124
  49.1 8.5 %collective-permute-start.11 = (f32[10,64,128]{2,1,0:T(8,128)S(1)}, f32[10,64,128]{2,1,0:T(8,128)S(1)}, u32[]{:S(2)}, u32[]{:S(2)}) collective-permute-start(f32[10,64,128]{2,1,0:T(8,128)S(1)} %constant_dynamic-slice_fusion), channel_id=1, source_target_pairs={{28,24},{24,28},{20,16},{16,20},{12,8},{8,12},{4,0},{0,4},{29,25},... | collective-permute-start | bytes 983048 | tf_op jit(solution)/shard_map/ppermute | solution.py:42
  58.4 1.4 %collective-permute-start.12 = (f32[10,64,128]{2,1,0:T(8,128)}, f32[10,64,128]{2,1,0:T(8,128)}, u32[]{:S(2)}, u32[]{:S(2)}) collective-permute-start(f32[10,64,128]{2,1,0:T(8,128)} %get-tuple-element.28), channel_id=1, source_target_pairs={{28,20},{24,16},{29,21},{25,17},{30,22},{26,18},{31,23},{27,19}} | collective-permute-start | bytes 983048 | tf_op jit(solution)/shard_map/ppermute | solution.py:62
  59.9 2.8 %collective-permute-start.13 = (f32[10,64,128]{2,1,0:T(8,128)S(1)}, f32[10,64,128]{2,1,0:T(8,128)S(1)}, u32[]{:S(2)}, u32[]{:S(2)}) collective-permute-start(f32[10,64,128]{2,1,0:T(8,128)S(1)} %multiply_add_fusion.2), channel_id=1, source_target_pairs={{20,12},{16,8},{21,13},{17,9},{22,14},{18,10},{23,15},{19,11}} | collective-permute-start | bytes 983048 | tf_op jit(solution)/shard_map/ppermute | solution.py:62
  62.7 1.6 %copy-start.8 = (f32[10,64,128]{2,1,0:T(8,128)S(1)}, f32[10,64,128]{2,1,0:T(8,128)}, u32[]{:S(2)}) copy-start(f32[10,64,128]{2,1,0:T(8,128)} %copy-done.7) | copy-start | bytes 983044
  62.9 34.2 %collective-permute-start.14 = (f32[10,64,128]{2,1,0:T(8,128)S(1)}, f32[10,64,128]{2,1,0:T(8,128)S(1)}, u32[]{:S(2)}, u32[]{:S(2)}) collective-permute-start(f32[10,64,128]{2,1,0:T(8,128)S(1)} %get-tuple-element.26), channel_id=1, source_target_pairs={{12,4},{8,0},{13,5},{9,1},{14,6},{10,2},{15,7},{11,3}} | collective-permute-start | bytes 983048 | tf_op jit(solution)/shard_map/ppermute | solution.py:59
  65.1 32.0 %copy-start.6 = (f32[10,64,128]{2,1,0:T(8,128)S(1)}, f32[10,64,128]{2,1,0:T(8,128)}, u32[]{:S(2)}) copy-start(f32[10,64,128]{2,1,0:T(8,128)} %copy-done.5) | copy-start | bytes 983044
  65.1 32.0 %copy-start.17 = (f32[10]{0:T(128)S(1)}, f32[10]{0:T(128)}, u32[]{:S(2)}) copy-start(f32[10]{0:T(128)} %copy-done.16) | copy-start | bytes 124
  65.1 32.0 %copy-start.18 = (f32[10]{0:T(128)S(1)}, f32[10]{0:T(128)}, u32[]{:S(2)}) copy-start(f32[10]{0:T(128)} %get-tuple-element.33) | copy-start | bytes 124
  65.1 33.9 %collective-permute-start.18 = (f32[128,128]{1,0:T(8,128)S(1)}, f32[128,128]{1,0:T(8,128)S(1)}, u32[]{:S(2)}, u32[]{:S(2)}) collective-permute-start(f32[128,128]{1,0:T(8,128)S(1)} %fusion.16), channel_id=1, source_target_pairs={{0,1},{1,0},{2,3},{3,2},{4,5},{5,4},{6,7},{7,6},{8,9},{9,8},{10,11... | collective-permute-start | bytes 196616 | tf_op jit(solution)/shard_map/ppermute | solution.py:94
  97.2 7.1 %collective-permute-start.15 = (f32[10,64,128]{2,1,0:T(8,128)S(1)}, f32[10,64,128]{2,1,0:T(8,128)S(1)}, u32[]{:S(2)}, u32[]{:S(2)}) collective-permute-start(f32[10,64,128]{2,1,0:T(8,128)S(1)} %get-tuple-element.49), channel_id=1, source_target_pairs={{28,24},{24,28},{20,16},{16,20},{12,8},{8,12},{4,0},{0,4},{29,25},... | collective-permute-start | bytes 983048 | tf_op jit(solution)/shard_map/ppermute | solution.py:82
  99.0 4.3 %collective-permute-start.19 = (f32[128,128]{1,0:T(8,128)S(1)}, f32[128,128]{1,0:T(8,128)S(1)}, u32[]{:S(2)}, u32[]{:S(2)}) collective-permute-start(f32[128,128]{1,0:T(8,128)S(1)} %add.165), channel_id=1, source_target_pairs={{0,2},{1,3},{2,0},{3,1},{4,6},{5,7},{6,4},{7,5},{8,10},{9,11},{10,... | collective-permute-start | bytes 196616 | tf_op jit(solution)/shard_map/ppermute | solution.py:94
  105.9 3.1 %copy-start.4 = (f32[10,64,128]{2,1,0:T(8,128)S(1)}, f32[10,64,128]{2,1,0:T(8,128)}, u32[]{:S(2)}) copy-start(f32[10,64,128]{2,1,0:T(8,128)} %copy-done.3) | copy-start | bytes 983044
  109.0 2.8 %copy-start.13 = (f32[20,1]{1,0:T(8,128)S(1)}, f32[20,1]{1,0:T(8,128)}, u32[]{:S(2)}) copy-start(f32[20,1]{1,0:T(8,128)} %exponential_multiply_fusion) | copy-start | bytes 244
  109.8 1.3 %collective-permute-start.16 = (f32[128,128]{1,0:T(8,128)S(1)}, f32[128,128]{1,0:T(8,128)S(1)}, u32[]{:S(2)}, u32[]{:S(2)}) collective-permute-start(f32[128,128]{1,0:T(8,128)S(1)} %fusion.15), channel_id=1, source_target_pairs={{0,1},{1,0},{2,3},{3,2},{4,5},{5,4},{6,7},{7,6},{8,9},{9,8},{10,11... | collective-permute-start | bytes 196616 | tf_op jit(solution)/shard_map/ppermute | solution.py:94
  111.1 4.3 %collective-permute-start.17 = (f32[128,128]{1,0:T(8,128)S(1)}, f32[128,128]{1,0:T(8,128)S(1)}, u32[]{:S(2)}, u32[]{:S(2)}) collective-permute-start(f32[128,128]{1,0:T(8,128)S(1)} %add.162), channel_id=1, source_target_pairs={{0,2},{1,3},{2,0},{3,1},{4,6},{5,7},{6,4},{7,5},{8,10},{9,11},{10,... | collective-permute-start | bytes 196616 | tf_op jit(solution)/shard_map/ppermute | solution.py:94
  (10 other events, 10.4 us)

commit v13 on v12

--- a/solution.py
+++ b/solution.py
@@ -255,8 +255,9 @@
     local_grad = jnp.einsum("jhp,jn->hpn", weighted_grad, read_queries, precision=highest)
     state_grad = pair_scan(decay_total, local_grad, "seq", True)
     if single:
-        gf_w, gs_w, gd_w, gw_w, gr_w = pull_w(grad_mixed)
-        gd_c, gr_c = pull_c(grad_mixed)
+        (gf_w, gs_w, gd_w, gw_w, gr_w), (gd_c, gr_c) = lax.optimization_barrier(
+            (pull_w(grad_mixed), pull_c(grad_mixed))
+        )
         grad_read = butterfly_psum(gr_w + gr_c, "head")
         _, pull_e = jax.vjp(
             lambda f, s, d, w: end_part(f, s, d, w, state_in),

time: 116 us -> 119 us (1.026)
  matrix products: 14 us -> 16.8 us
    ppermute x8, waiting for transfers between devices: 8.62 us -> 4.35 us  [butterfly_psum(): got = lax.ppermute(parts, axis, [(i, i ^ k) for i in range(count)])]
    ppermute x2, waiting for transfers between devices: 4.18 us -> 6.34 us  [pair_scan(): other = lax.ppermute(send, axis, swap)]
    add x0 -> x2, other arithmetic: none -> 1.78 us  [the longest x1 0.91 us: local(): grad_features = gf_w + gf_e]
    ppermute x2, waiting for transfers between devices: 30.1 us -> 31.7 us  [pair_scan(): s_in = lax.ppermute(out[1], axis, pairs)]
    dot_general x2, matrix products: 1.17 us -> 2.61 us  [carried_part(): carried = jnp.einsum('in,hpn->ihp', read_in, state_in, precision=highest)]
    ppermute x8, starting transfers between devices: 4.15 us -> 5.36 us  [butterfly_psum(): got = lax.ppermute(parts, axis, [(i, i ^ k) for i in range(count)])]
    unnamed x46 -> x39, local copies, waits for them, and re-layouts: 3.29 us -> 2.57 us
  transfers between devices with their start and end apart: 20 -> 20, of which waited for: 13 -> 12; matrix products, arithmetic and copies ran while one was open for 11% -> 11% of each run, Pallas kernels for 0% -> 0%
where the time goes in v13:
time: 119 us
  waiting for transfers between devices  63.5 us (53%)
  starting transfers between devices  23.4 us (20%)
  matrix products  16.8 us (14%)
  other arithmetic  9.63 us (8%)
  local copies, waits for them, and re-layouts  4.24 us (4%)
    ppermute x2, waiting for transfers between devices, pair_scan(): s_in = lax.ppermute(out[1], axis, pairs)  31.7 us
    ppermute x4, waiting for transfers between devices, pair_scan(): a_rcv, s_rcv = lax.ppermute((a_snd, s_snd), axis, swap)  16.3 us
    ppermute x4, starting transfers between devices, pair_scan(): a_in, s_in = lax.ppermute(out, axis, pairs)  6.49 us
    ppermute x4, starting transfers between devices, pair_scan(): a_rcv, s_rcv = lax.ppermute((a_snd, s_snd), axis, swap)  6.35 us
    ppermute x2, waiting for transfers between devices, pair_scan(): other = lax.ppermute(send, axis, swap)  6.34 us
    ppermute x8, starting transfers between devices, butterfly_psum(): got = lax.ppermute(parts, axis, [(i, i ^ k) for i in range(count)])  5.36 us
    dot_general x3, matrix products, within_part(): within = jnp.einsum('hij,jhp->ihp', masked, scaled, precision=highest)  5.18 us
    ppermute x4, waiting for transfers between devices, pair_scan(): a_in, s_in = lax.ppermute(out, axis, pairs)  4.83 us
  transfers between devices with their start and end apart: 20, of which 12 were waited for; matrix products, arithmetic and copies ran while one was open for 11% of the time, Pallas kernels for 0%

profile of v13, /device:TPU:0, one launch (start us, length us, event | category | flops | bytes accessed | tf_op | source)
XLA Modules:
  0.0 118.8 jit_solution(11622487115770221875)
XLA Ops:
  0.7 0.9 fusion.58
  1.8 1.3 %copy.23 = f32[128,1280]{0,1:T(8,128)S(1)} copy(f32[128,1280]{1,0:T(8,128)} %param.9) | data formatting | bytes 1310720 | tf_op args[0]
  3.6 3.0 %collective-permute-start.1 = (f32[10,64,128]{2,1,0:T(8,128)S(1)}, f32[10,64,128]{2,1,0:T(8,128)S(1)}, u32[]{:S(2)}, u32[]{:S(2)}) collective-permute-start(f32[10,64,128]{2,1,0:T(8,128)S(1)} %constant_dynamic-slice_fusion.1), channel_id=1, source_target_pairs={{0,4},{4,0},{8,12},{12,8},{16,20},{20,16},{24,28},{28,24},{1,5},{5... | collective-permute-start | bytes 983048 | tf_op jit(solution)/shard_map/ppermute | solution.py:42
  6.8 7.6 %collective-permute-done.10 = f32[10]{0:T(128)S(1)} collective-permute-done((f32[10]{0:T(128)S(1)}, f32[10]{0:T(128)S(1)}, u32[]{:S(2)}, u32[]{:S(2)}) %collective-permute-start.10) | collective-permute-done | bytes 72 | tf_op jit(solution)/shard_map/ppermute | solution.py:42
  15.0 1.7 %collective-permute-start = (f32[10]{0:T(128)S(1)}, f32[10]{0:T(128)S(1)}, u32[]{:S(2)}, u32[]{:S(2)}) collective-permute-start(f32[10]{0:T(128)S(1)} %get-tuple-element.58), channel_id=1, source_target_pairs={{0,4},{4,0},{8,12},{12,8},{16,20},{20,16},{24,28},{28,24},{1,5},{5... | collective-permute-start | bytes 128 | tf_op jit(solution)/shard_map/ppermute | solution.py:42
  16.8 1.8 %collective-permute-done = f32[10]{0:T(128)S(1)} collective-permute-done((f32[10]{0:T(128)S(1)}, f32[10]{0:T(128)S(1)}, u32[]{:S(2)}, u32[]{:S(2)}) %collective-permute-start) | collective-permute-done | bytes 72 | tf_op jit(solution)/shard_map/ppermute | solution.py:42
  18.8 3.8 %collective-permute-start.2 = (f32[10,64,128]{2,1,0:T(8,128)S(1)}, f32[10,64,128]{2,1,0:T(8,128)S(1)}, u32[]{:S(2)}, u32[]{:S(2)}) collective-permute-start(f32[10,64,128]{2,1,0:T(8,128)S(1)} %get-tuple-element.41), channel_id=1, source_target_pairs={{0,8},{4,12},{1,9},{5,13},{2,10},{6,14},{3,11},{7,15}} | collective-permute-start | bytes 983048 | tf_op jit(solution)/shard_map/ppermute | solution.py:62
  22.5 4.8 %collective-permute-done.2 = f32[10,64,128]{2,1,0:T(8,128)S(1)} collective-permute-done((f32[10,64,128]{2,1,0:T(8,128)S(1)}, f32[10,64,128]{2,1,0:T(8,128)S(1)}, u32[]{:S(2)}, u32[]{:S(2)}) %collective-permute-start.2) | collective-permute-done | bytes 327712 | tf_op jit(solution)/shard_map/ppermute | solution.py:62
  29.4 1.6 %collective-permute-start.5 = (f32[10,64,128]{2,1,0:T(8,128)S(1)}, f32[10,64,128]{2,1,0:T(8,128)S(1)}, u32[]{:S(2)}, u32[]{:S(2)}) collective-permute-start(f32[10,64,128]{2,1,0:T(8,128)S(1)} %get-tuple-element.54), channel_id=1, source_target_pairs={{0,4},{4,0},{8,12},{12,8},{16,20},{20,16},{24,28},{28,24},{1,5},{5... | collective-permute-start | bytes 983048 | tf_op jit(solution)/shard_map/ppermute | solution.py:82
  31.0 1.5 %fusion.9 = f32[128,20,64]{0,2,1:T(8,128)S(1)} fusion(f32[128,20,64]{0,2,1:T(8,128)S(1)} %bitcast.74, f32[128,128]{1,0:T(8,128)S(1)} %fusion.84, f32[20,128]{1,0:T(8,128)S(1)} %bitcast.88, pred[128,128]{1,0:T(8,128)(4,1)S(1)} %iota_compare_fusion.6, f32[128,20]{0,1:T(8,128)S(1)} %bitcast.93, f32[20]{0:T(128)S(1)} %copy-done.18), kind=kOutput, calls=%fused_computation.10 | convolution fusion | flops 127631360 | bytes 1413200 | tf_op jit(solution)/shard_map/jvp(hij,jhp->ihp)/dot_general | solution.py:167
  32.7 3.8 %collective-permute-done.5 = f32[10,64,128]{2,1,0:T(8,128)S(1)} collective-permute-done((f32[10,64,128]{2,1,0:T(8,128)S(1)}, f32[10,64,128]{2,1,0:T(8,128)S(1)}, u32[]{:S(2)}, u32[]{:S(2)}) %collective-permute-start.5) | collective-permute-done | bytes 327712 | tf_op jit(solution)/shard_map/ppermute | solution.py:82
  36.5 1.3 %broadcast_multiply_fusion = (f32[128,20,64]{0,2,1:T(8,128)S(1)}, f32[128,20,64]{0,2,1:T(8,128)}) fusion(f32[128,20]{0,1:T(8,128)S(1)} %get-tuple-element.56, f32[128,128]{1,0:T(8,128)S(1)} %copy-done.5, f32[10,64,128]{2,1,0:T(8,128)S(1)} %get-tuple-element.55, f32[10,64,128]{2,1,0:T(8,128)S(1)} %collective-permute-done.5, pred[]{:T(512)S(6)} %eq.27), kind=kOutput, calls=%fused_computation.63 | convolution fusion | flops 126484480 | bytes 2041857 | tf_op jit(solution)/shard_map/jvp(in,hpn->ihp)/dot_general | solution.py:174
  38.5 1.7 %multiply_reduce_fusion.7 = (f32[128]{0:T(128)S(1)}, f32[128]{0:T(128)S(1)}, f32[128,1280]{1,0:T(8,128)S(1)}) fusion(f32[128,1280]{1,0:T(8,128)} %param.10, f32[128,1280]{1,0:T(8,128)} %param.17, f32[1280]{0:T(1024)S(1)} %copy-done.10, f32[128,1280]{1,0:T(8,128)S(1)} %copy.24, f32[128,1280]{1,0:T(8,128)S(1)} %copy.25), kind=kLoop, calls=%fused_computation.30 | loop fusion | flops 1801984 | bytes 3282944 | tf_op jit(solution)/shard_map/reduce_sum | solution.py:244
  41.4 1.5 %collective-permute-start.7 = (f32[128]{0:T(128)S(1)}, f32[128]{0:T(128)S(1)}, u32[]{:S(2)}, u32[]{:S(2)}) collective-permute-start(f32[128]{0:T(128)S(1)} %add.137), channel_id=1, source_target_pairs={{0,2},{1,3},{2,0},{3,1},{4,6},{5,7},{6,4},{7,5},{8,10},{9,11},{10,... | collective-permute-start | bytes 1544 | tf_op jit(solution)/shard_map/ppermute | solution.py:94
  43.5 1.5 %collective-permute-done.7 = f32[128]{0:T(128)S(1)} collective-permute-done((f32[128]{0:T(128)S(1)}, f32[128]{0:T(128)S(1)}, u32[]{:S(2)}, u32[]{:S(2)}) %collective-permute-start.7) | collective-permute-done | bytes 544 | tf_op jit(solution)/shard_map/ppermute | solution.py:94
  45.0 1.5 %collective-permute-done.9 = f32[128]{0:T(128)S(1)} collective-permute-done((f32[128]{0:T(128)S(1)}, f32[128]{0:T(128)S(1)}, u32[]{:S(2)}, u32[]{:S(2)}) %collective-permute-start.9) | collective-permute-done | bytes 544 | tf_op jit(solution)/shard_map/ppermute | solution.py:94
  46.5 1.3 %add_multiply_fusion = (f32[128,1280]{1,0:T(8,128)}, f32[128,1280]{1,0:T(8,128)S(1)}) fusion(f32[128,1280]{1,0:T(8,128)S(1)} %copy-done.1, f32[128,1280]{1,0:T(8,128)S(1)} %get-tuple-element.38, f32[128]{0:T(128)S(1)} %get-tuple-element.36, f32[128,1280]{1,0:T(8,128)S(1)} %copy-done.2, f32[1280]{0:T(1024)S(1)} %copy-done.10, f32[128]{0:T(128)S(1)} %get-tuple-element.37), kind=kLoop, calls=%fused_computation.24 | loop fusion | flops 2621440 | bytes 3282944 | tf_op jit(solution)/shard_map/mul | solution.py:252
  48.5 1.6 %collective-permute-start.11 = (f32[10,64,128]{2,1,0:T(8,128)S(1)}, f32[10,64,128]{2,1,0:T(8,128)S(1)}, u32[]{:S(2)}, u32[]{:S(2)}) collective-permute-start(f32[10,64,128]{2,1,0:T(8,128)S(1)} %constant_dynamic-slice_fusion), channel_id=1, source_target_pairs={{28,24},{24,28},{20,16},{16,20},{12,8},{8,12},{4,0},{0,4},{29,25},... | collective-permute-start | bytes 983048 | tf_op jit(solution)/shard_map/ppermute | solution.py:42
  50.1 6.9 %collective-permute-done.11 = f32[10,64,128]{2,1,0:T(8,128)S(1)} collective-permute-done((f32[10,64,128]{2,1,0:T(8,128)S(1)}, f32[10,64,128]{2,1,0:T(8,128)S(1)}, u32[]{:S(2)}, u32[]{:S(2)}) %collective-permute-start.11) | collective-permute-done | bytes 327712 | tf_op jit(solution)/shard_map/ppermute | solution.py:42
  57.9 1.4 %collective-permute-start.12 = (f32[10,64,128]{2,1,0:T(8,128)}, f32[10,64,128]{2,1,0:T(8,128)}, u32[]{:S(2)}, u32[]{:S(2)}) collective-permute-start(f32[10,64,128]{2,1,0:T(8,128)} %get-tuple-element.30), channel_id=1, source_target_pairs={{28,20},{24,16},{29,21},{25,17},{30,22},{26,18},{31,23},{27,19}} | collective-permute-start | bytes 983048 | tf_op jit(solution)/shard_map/ppermute | solution.py:62
  60.0 2.0 %fusion.18 = (f32[20,128]{1,0:T(8,128)S(1)}, f32[20,128]{1,0:T(8,128)S(1)}, f32[128,128]{1,0:T(8,128)S(1)}) fusion(f32[128,128]{1,0:T(8,128)S(1)} %fusion.84, f32[20,128]{1,0:T(8,128)S(1)} %bitcast.89, pred[128,128]{1,0:T(8,128)(4,1)S(1)} %iota_compare_fusion.6, f32[20,64,128]{2,1,0:T(8,128)S(1)} %bitcast.79, f32[128,20,64]{0,2,1:T(8,128)S(1)} %bitcast.75, ...), kind=kOutput, calls=%fused_computation.18 | convolution fusion | flops 129575936 | bytes 1499136 | tf_op jit(solution)/shard_map/transpose(jvp(hij,jhp->ihp))/dot_general | solution.py:167
  62.0 0.9 fusion.85
  63.0 1.5 %collective-permute-start.14 = (f32[10,64,128]{2,1,0:T(8,128)S(1)}, f32[10,64,128]{2,1,0:T(8,128)S(1)}, u32[]{:S(2)}, u32[]{:S(2)}) collective-permute-start(f32[10,64,128]{2,1,0:T(8,128)S(1)} %get-tuple-element.28), channel_id=1, source_target_pairs={{12,4},{8,0},{13,5},{9,1},{14,6},{10,2},{15,7},{11,3}} | collective-permute-start | bytes 983048 | tf_op jit(solution)/shard_map/ppermute | solution.py:59
  64.8 31.7 %collective-permute-done.14 = f32[10,64,128]{2,1,0:T(8,128)S(1)} collective-permute-done((f32[10,64,128]{2,1,0:T(8,128)S(1)}, f32[10,64,128]{2,1,0:T(8,128)S(1)}, u32[]{:S(2)}, u32[]{:S(2)}) %collective-permute-start.14) | collective-permute-done | bytes 327712 | tf_op jit(solution)/shard_map/ppermute | solution.py:59
  96.7 1.5 %collective-permute-start.15 = (f32[10,64,128]{2,1,0:T(8,128)S(1)}, f32[10,64,128]{2,1,0:T(8,128)S(1)}, u32[]{:S(2)}, u32[]{:S(2)}) collective-permute-start(f32[10,64,128]{2,1,0:T(8,128)S(1)} %get-tuple-element.52), channel_id=1, source_target_pairs={{28,24},{24,28},{20,16},{16,20},{12,8},{8,12},{4,0},{0,4},{29,25},... | collective-permute-start | bytes 983048 | tf_op jit(solution)/shard_map/ppermute | solution.py:82
  98.2 1.3 %convolution_bitcast_fusion.3 = f32[128,128]{1,0:T(8,128)} fusion(f32[128,20,64]{0,2,1:T(8,128)S(1)} %bitcast.80, f32[128,20]{0,1:T(8,128)S(1)} %get-tuple-element.56, f32[10,64,128]{2,1,0:T(8,128)S(1)} %get-tuple-element.55, f32[10,64,128]{2,1,0:T(8,128)S(1)} %collective-permute-done.5, pred[]{:T(512)S(6)} %eq.27), kind=kOutput, calls=%fused_computation.13 | convolution fusion | flops 126484480 | bytes 1386497 | tf_op jit(solution)/shard_map/transpose(jvp(in,hpn->ihp))/dot_general | solution.py:174
  99.6 1.8 %fusion.12 = f32[128,20,64]{0,2,1:T(8,128)} fusion(f32[20,64,128]{2,1,0:T(8,128)S(1)} %bitcast.81, f32[128,128]{1,0:T(8,128)S(1)} %fusion.84, f32[20,128]{1,0:T(8,128)S(1)} %bitcast.90, pred[128,128]{1,0:T(8,128)(4,1)S(1)} %copy-done.12), kind=kOutput, calls=%fused_computation.11 | convolution fusion | flops 127139840 | bytes 1402880 | tf_op jit(solution)/shard_map/transpose(jvp(hij,jhp->ihp))/dot_general | solution.py:167
  101.3 2.5 %collective-permute-done.15 = f32[10,64,128]{2,1,0:T(8,128)S(1)} collective-permute-done((f32[10,64,128]{2,1,0:T(8,128)S(1)}, f32[10,64,128]{2,1,0:T(8,128)S(1)}, u32[]{:S(2)}, u32[]{:S(2)}) %collective-permute-start.15) | collective-permute-done | bytes 327712 | tf_op jit(solution)/shard_map/ppermute | solution.py:82
  104.9 3.3 %multiply_reduce_fusion.2 = (f32[128,20]{0,1:T(8,128)S(1)}, f32[128,20]{0,1:T(8,128)}, f32[128,20]{0,1:T(8,128)}, f32[128,20,64]{0,2,1:T(8,128)S(1)}, f32[128,20,64]{0,2,1:T(8,128)}, /*index=5*/f32[128,20]{0,1:T(8,128)}) fusion(f32[128,20,64]{0,2,1:T(8,128)S(1)} %bitcast.76, f32[128,20]{0,1:T(8,128)S(1)} %bitcast.95, f32[128,20]{0,1:T(8,128)S(1)} %get-tuple-element.57, ...), kind=kOutput, calls=%fused_computation.22 | convolution fusion | flops 128604160 | bytes 4714577 | tf_op jit(solution)/shard_map/transpose(jvp(jhp,jn->hpn))/dot_general | solution.py:186
  108.7 0.9 fusion.56
  113.4 1.5 %collective-permute-start.17 = (f32[128,128]{1,0:T(8,128)S(1)}, f32[128,128]{1,0:T(8,128)S(1)}, u32[]{:S(2)}, u32[]{:S(2)}) collective-permute-start(f32[128,128]{1,0:T(8,128)S(1)} %add.155), channel_id=1, source_target_pairs={{0,2},{1,3},{2,0},{3,1},{4,6},{5,7},{6,4},{7,5},{8,10},{9,11},{10,... | collective-permute-start | bytes 196616 | tf_op jit(solution)/shard_map/ppermute | solution.py:94
  115.9 0.9 add.152
  (103 shorter events, 17.5 us)
Async XLA Ops:
  3.6 15.0 %collective-permute-start.1 = (f32[10,64,128]{2,1,0:T(8,128)S(1)}, f32[10,64,128]{2,1,0:T(8,128)S(1)}, u32[]{:S(2)}, u32[]{:S(2)}) collective-permute-start(f32[10,64,128]{2,1,0:T(8,128)S(1)} %constant_dynamic-slice_fusion.1), channel_id=1, source_target_pairs={{0,4},{4,0},{8,12},{12,8},{16,20},{20,16},{24,28},{28,24},{1,5},{5... | collective-permute-start | bytes 983048 | tf_op jit(solution)/shard_map/ppermute | solution.py:42
  6.7 7.7 %collective-permute-start.10 = (f32[10]{0:T(128)S(1)}, f32[10]{0:T(128)S(1)}, u32[]{:S(2)}, u32[]{:S(2)}) collective-permute-start(f32[10]{0:T(128)S(1)} %dynamic_slice.29), channel_id=1, source_target_pairs={{28,24},{24,28},{20,16},{16,20},{12,8},{8,12},{4,0},{0,4},{29,25},... | collective-permute-start | bytes 128 | tf_op jit(solution)/shard_map/ppermute | solution.py:42
  15.0 3.5 %collective-permute-start = (f32[10]{0:T(128)S(1)}, f32[10]{0:T(128)S(1)}, u32[]{:S(2)}, u32[]{:S(2)}) collective-permute-start(f32[10]{0:T(128)S(1)} %get-tuple-element.58), channel_id=1, source_target_pairs={{0,4},{4,0},{8,12},{12,8},{16,20},{20,16},{24,28},{28,24},{1,5},{5... | collective-permute-start | bytes 128 | tf_op jit(solution)/shard_map/ppermute | solution.py:42
  18.8 8.6 %collective-permute-start.2 = (f32[10,64,128]{2,1,0:T(8,128)S(1)}, f32[10,64,128]{2,1,0:T(8,128)S(1)}, u32[]{:S(2)}, u32[]{:S(2)}) collective-permute-start(f32[10,64,128]{2,1,0:T(8,128)S(1)} %get-tuple-element.41), channel_id=1, source_target_pairs={{0,8},{4,12},{1,9},{5,13},{2,10},{6,14},{3,11},{7,15}} | collective-permute-start | bytes 983048 | tf_op jit(solution)/shard_map/ppermute | solution.py:62
  27.5 0.7 collective-permute-start.3
  28.3 0.9 collective-permute-start.4
  29.4 7.1 %collective-permute-start.5 = (f32[10,64,128]{2,1,0:T(8,128)S(1)}, f32[10,64,128]{2,1,0:T(8,128)S(1)}, u32[]{:S(2)}, u32[]{:S(2)}) collective-permute-start(f32[10,64,128]{2,1,0:T(8,128)S(1)} %get-tuple-element.54), channel_id=1, source_target_pairs={{0,4},{4,0},{8,12},{12,8},{16,20},{20,16},{24,28},{28,24},{1,5},{5... | collective-permute-start | bytes 983048 | tf_op jit(solution)/shard_map/ppermute | solution.py:82
  31.0 29.0 %copy-start.11 = (pred[128,128]{1,0:T(8,128)(4,1)}, pred[128,128]{1,0:T(8,128)(4,1)S(1)}, u32[]{:S(2)}) copy-start(pred[128,128]{1,0:T(8,128)(4,1)S(1)} %iota_compare_fusion.6) | copy-start | bytes 49156
  38.5 8.0 %copy-start.1 = (f32[128,1280]{1,0:T(8,128)S(1)}, f32[128,1280]{1,0:T(8,128)}, u32[]{:S(2)}) copy-start(f32[128,1280]{1,0:T(8,128)} %param.10) | copy-start | bytes 1966084
  38.5 8.0 %copy-start.2 = (f32[128,1280]{1,0:T(8,128)S(1)}, f32[128,1280]{1,0:T(8,128)}, u32[]{:S(2)}) copy-start(f32[128,1280]{1,0:T(8,128)} %param.17) | copy-start | bytes 1966084
  40.3 1.2 collective-permute-start.6
  40.3 2.6 %collective-permute-start.8 = (f32[128]{0:T(128)S(1)}, f32[128]{0:T(128)S(1)}, u32[]{:S(2)}, u32[]{:S(2)}) collective-permute-start(f32[128]{0:T(128)S(1)} %get-tuple-element.26), channel_id=1, source_target_pairs={{0,1},{1,0},{2,3},{3,2},{4,5},{5,4},{6,7},{7,6},{8,9},{9,8},{10,11... | collective-permute-start | bytes 1544 | tf_op jit(solution)/shard_map/ppermute | solution.py:94
  41.4 3.5 %collective-permute-start.7 = (f32[128]{0:T(128)S(1)}, f32[128]{0:T(128)S(1)}, u32[]{:S(2)}, u32[]{:S(2)}) collective-permute-start(f32[128]{0:T(128)S(1)} %add.137), channel_id=1, source_target_pairs={{0,2},{1,3},{2,0},{3,1},{4,6},{5,7},{6,4},{7,5},{8,10},{9,11},{10,... | collective-permute-start | bytes 1544 | tf_op jit(solution)/shard_map/ppermute | solution.py:94
  43.0 3.5 %collective-permute-start.9 = (f32[128]{0:T(128)S(1)}, f32[128]{0:T(128)S(1)}, u32[]{:S(2)}, u32[]{:S(2)}) collective-permute-start(f32[128]{0:T(128)S(1)} %add.141), channel_id=1, source_target_pairs={{0,2},{1,3},{2,0},{3,1},{4,6},{5,7},{6,4},{7,5},{8,10},{9,11},{10,... | collective-permute-start | bytes 1544 | tf_op jit(solution)/shard_map/ppermute | solution.py:94
  48.5 8.5 %copy-start.13 = (f32[10]{0:T(128)S(1)}, f32[10]{0:T(128)}, u32[]{:S(2)}) copy-start(f32[10]{0:T(128)} %get-tuple-element.32) | copy-start | bytes 124
  48.5 8.5 %copy-start.14 = (f32[10]{0:T(128)S(1)}, f32[10]{0:T(128)}, u32[]{:S(2)}) copy-start(f32[10]{0:T(128)} %get-tuple-element.34) | copy-start | bytes 124
  48.5 8.5 %collective-permute-start.11 = (f32[10,64,128]{2,1,0:T(8,128)S(1)}, f32[10,64,128]{2,1,0:T(8,128)S(1)}, u32[]{:S(2)}, u32[]{:S(2)}) collective-permute-start(f32[10,64,128]{2,1,0:T(8,128)S(1)} %constant_dynamic-slice_fusion), channel_id=1, source_target_pairs={{28,24},{24,28},{20,16},{16,20},{12,8},{8,12},{4,0},{0,4},{29,25},... | collective-permute-start | bytes 983048 | tf_op jit(solution)/shard_map/ppermute | solution.py:42
  57.9 1.4 %collective-permute-start.12 = (f32[10,64,128]{2,1,0:T(8,128)}, f32[10,64,128]{2,1,0:T(8,128)}, u32[]{:S(2)}, u32[]{:S(2)}) collective-permute-start(f32[10,64,128]{2,1,0:T(8,128)} %get-tuple-element.30), channel_id=1, source_target_pairs={{28,20},{24,16},{29,21},{25,17},{30,22},{26,18},{31,23},{27,19}} | collective-permute-start | bytes 983048 | tf_op jit(solution)/shard_map/ppermute | solution.py:62
  59.3 3.5 %collective-permute-start.13 = (f32[10,64,128]{2,1,0:T(8,128)S(1)}, f32[10,64,128]{2,1,0:T(8,128)S(1)}, u32[]{:S(2)}, u32[]{:S(2)}) collective-permute-start(f32[10,64,128]{2,1,0:T(8,128)S(1)} %multiply_add_fusion.2), channel_id=1, source_target_pairs={{20,12},{16,8},{21,13},{17,9},{22,14},{18,10},{23,15},{19,11}} | collective-permute-start | bytes 983048 | tf_op jit(solution)/shard_map/ppermute | solution.py:62
  62.9 33.6 %copy-start.16 = (f32[10]{0:T(128)S(1)}, f32[10]{0:T(128)}, u32[]{:S(2)}) copy-start(f32[10]{0:T(128)} %copy-done.15) | copy-start | bytes 124
  62.9 33.6 %copy-start.17 = (f32[10]{0:T(128)S(1)}, f32[10]{0:T(128)}, u32[]{:S(2)}) copy-start(f32[10]{0:T(128)} %get-tuple-element.35) | copy-start | bytes 124
  63.0 33.5 %collective-permute-start.14 = (f32[10,64,128]{2,1,0:T(8,128)S(1)}, f32[10,64,128]{2,1,0:T(8,128)S(1)}, u32[]{:S(2)}, u32[]{:S(2)}) collective-permute-start(f32[10,64,128]{2,1,0:T(8,128)S(1)} %get-tuple-element.28), channel_id=1, source_target_pairs={{12,4},{8,0},{13,5},{9,1},{14,6},{10,2},{15,7},{11,3}} | collective-permute-start | bytes 983048 | tf_op jit(solution)/shard_map/ppermute | solution.py:59
  96.7 2.9 %copy-start.12 = (pred[128,128]{1,0:T(8,128)(4,1)S(1)}, pred[128,128]{1,0:T(8,128)(4,1)}, u32[]{:S(2)}) copy-start(pred[128,128]{1,0:T(8,128)(4,1)} %copy-done.11) | copy-start | bytes 49156
  96.7 7.1 %collective-permute-start.15 = (f32[10,64,128]{2,1,0:T(8,128)S(1)}, f32[10,64,128]{2,1,0:T(8,128)S(1)}, u32[]{:S(2)}, u32[]{:S(2)}) collective-permute-start(f32[10,64,128]{2,1,0:T(8,128)S(1)} %get-tuple-element.52), channel_id=1, source_target_pairs={{28,24},{24,28},{20,16},{16,20},{12,8},{8,12},{4,0},{0,4},{29,25},... | collective-permute-start | bytes 983048 | tf_op jit(solution)/shard_map/ppermute | solution.py:82
  104.9 5.6 %copy-start.6 = (f32[128,128]{1,0:T(8,128)S(1)}, f32[128,128]{1,0:T(8,128)}, u32[]{:S(2)}) copy-start(f32[128,128]{1,0:T(8,128)} %fusion.85) | copy-start | bytes 196612
  110.5 4.4 %copy-start.8 = (f32[128,20]{0,1:T(8,128)S(1)}, f32[128,20]{0,1:T(8,128)}, u32[]{:S(2)}) copy-start(f32[128,20]{0,1:T(8,128)} %get-tuple-element.24) | copy-start | bytes 30724
  110.5 4.4 %copy-start.9 = (f32[128,20]{0,1:T(8,128)S(1)}, f32[128,20]{0,1:T(8,128)}, u32[]{:S(2)}) copy-start(f32[128,20]{0,1:T(8,128)} %get-tuple-element.27) | copy-start | bytes 30724
  110.5 2.2 %collective-permute-start.18 = (f32[128,128]{1,0:T(8,128)S(1)}, f32[128,128]{1,0:T(8,128)S(1)}, u32[]{:S(2)}, u32[]{:S(2)}) collective-permute-start(f32[128,128]{1,0:T(8,128)S(1)} %add.157), channel_id=1, source_target_pairs={{0,1},{1,0},{2,3},{3,2},{4,5},{5,4},{6,7},{7,6},{8,9},{9,8},{10,11... | collective-permute-start | bytes 196616 | tf_op jit(solution)/shard_map/ppermute | solution.py:94
  110.6 4.9 %copy-start.4 = (f32[128,20,64]{0,2,1:T(8,128)S(1)}, f32[128,20,64]{0,2,1:T(8,128)}, u32[]{:S(2)}) copy-start(f32[128,20,64]{0,2,1:T(8,128)} %get-tuple-element.50) | copy-start | bytes 1966084
  111.3 2.1 %collective-permute-start.16 = (f32[128,128]{1,0:T(8,128)S(1)}, f32[128,128]{1,0:T(8,128)S(1)}, u32[]{:S(2)}, u32[]{:S(2)}) collective-permute-start(f32[128,128]{1,0:T(8,128)S(1)} %fusion.15), channel_id=1, source_target_pairs={{0,1},{1,0},{2,3},{3,2},{4,5},{5,4},{6,7},{7,6},{8,9},{9,8},{10,11... | collective-permute-start | bytes 196616 | tf_op jit(solution)/shard_map/ppermute | solution.py:94
  112.7 4.8 %collective-permute-start.19 = (f32[128,128]{1,0:T(8,128)S(1)}, f32[128,128]{1,0:T(8,128)S(1)}, u32[]{:S(2)}, u32[]{:S(2)}) collective-permute-start(f32[128,128]{1,0:T(8,128)S(1)} %add.158), channel_id=1, source_target_pairs={{0,2},{1,3},{2,0},{3,1},{4,6},{5,7},{6,4},{7,5},{8,10},{9,11},{10,... | collective-permute-start | bytes 196616 | tf_op jit(solution)/shard_map/ppermute | solution.py:94
  113.4 4.8 %collective-permute-start.17 = (f32[128,128]{1,0:T(8,128)S(1)}, f32[128,128]{1,0:T(8,128)S(1)}, u32[]{:S(2)}, u32[]{:S(2)}) collective-permute-start(f32[128,128]{1,0:T(8,128)S(1)} %add.155), channel_id=1, source_target_pairs={{0,2},{1,3},{2,0},{3,1},{4,6},{5,7},{6,4},{7,5},{8,10},{9,11},{10,... | collective-permute-start | bytes 196616 | tf_op jit(solution)/shard_map/ppermute | solution.py:94
  (7 other events, 10.6 us)

commit v14 on v12

--- a/solution.py
+++ b/solution.py
@@ -241,7 +241,8 @@
     gated_out = mixed_out * active
     weighted = out_grad * norm_gain[None, :]
     square_sum, cross_sum = butterfly_psum(
-        (jnp.sum(gated_out * gated_out, axis=1), jnp.sum(weighted * gated_out, axis=1)), "head"
+        jnp.stack([jnp.sum(gated_out * gated_out, axis=1), jnp.sum(weighted * gated_out, axis=1)]),
+        "head",
     )
     inverse = lax.rsqrt(square_sum / channels + eps)
     grad_gated = (

time: 116 us -> 116 us (level)
  waiting for transfers between devices: 64.1 us -> 62.3 us
    ppermute x8 -> x6, waiting for transfers between devices: 8.62 us -> 6.38 us  [butterfly_psum(): got = lax.ppermute(parts, axis, [(i, i ^ k) for i in range(count)])]
    ppermute x8 -> x6, starting transfers between devices: 4.15 us -> 4.98 us  [butterfly_psum(): got = lax.ppermute(parts, axis, [(i, i ^ k) for i in range(count)])]
  transfers between devices with their start and end apart: 20 -> 18, of which waited for: 13 -> 12; matrix products, arithmetic and copies ran while one was open for 11% -> 11% of each run, Pallas kernels for 0% -> 0%
where the time goes in v14:
time: 116 us; the launch traced here: 115 us
  waiting for transfers between devices  62.3 us (54%)
  starting transfers between devices  23.1 us (20%)
  matrix products  14 us (12%)
  other arithmetic  9.22 us (8%)
  local copies, waits for them, and re-layouts  5.32 us (5%)
  between operations  1.19 us (1%)
    ppermute x2, waiting for transfers between devices, pair_scan(): s_in = lax.ppermute(out[1], axis, pairs)  30.4 us
    ppermute x4, waiting for transfers between devices, pair_scan(): a_rcv, s_rcv = lax.ppermute((a_snd, s_snd), axis, swap)  16.5 us
    ppermute x4, starting transfers between devices, pair_scan(): a_in, s_in = lax.ppermute(out, axis, pairs)  6.51 us
    ppermute x6, waiting for transfers between devices, butterfly_psum(): got = lax.ppermute(parts, axis, [(i, i ^ k) for i in range(count)])  6.38 us
    ppermute x4, starting transfers between devices, pair_scan(): a_rcv, s_rcv = lax.ppermute((a_snd, s_snd), axis, swap)  6.36 us
    dot_general x3, matrix products, within_part(): within = jnp.einsum('hij,jhp->ihp', masked, scaled, precision=highest)  5.17 us
    ppermute x6, starting transfers between devices, butterfly_psum(): got = lax.ppermute(parts, axis, [(i, i ^ k) for i in range(count)])  4.98 us
    ppermute x4, waiting for transfers between devices, pair_scan(): a_in, s_in = lax.ppermute(out, axis, pairs)  4.83 us
  transfers between devices with their start and end apart: 18, of which 12 were waited for; matrix products, arithmetic and copies ran while one was open for 11% of the time, Pallas kernels for 0%

profile of v14, /device:TPU:0, one launch (start us, length us, event | category | flops | bytes accessed | tf_op | source)
XLA Modules:
  0.0 115.2 jit_solution(17298846808373385419)
XLA Ops:
  0.7 0.9 fusion.58
  1.8 1.3 %copy.22 = f32[128,1280]{0,1:T(8,128)S(1)} copy(f32[128,1280]{1,0:T(8,128)} %param.9) | data formatting | bytes 1310720 | tf_op args[0]
  3.7 3.0 %collective-permute-start.1 = (f32[10,64,128]{2,1,0:T(8,128)S(1)}, f32[10,64,128]{2,1,0:T(8,128)S(1)}, u32[]{:S(2)}, u32[]{:S(2)}) collective-permute-start(f32[10,64,128]{2,1,0:T(8,128)S(1)} %constant_dynamic-slice_fusion.1), channel_id=1, source_target_pairs={{0,4},{4,0},{8,12},{12,8},{16,20},{20,16},{24,28},{28,24},{1,5},{5... | collective-permute-start | bytes 983048 | tf_op jit(solution)/shard_map/ppermute | solution.py:42
  6.8 7.6 %collective-permute-done.8 = f32[10]{0:T(128)S(1)} collective-permute-done((f32[10]{0:T(128)S(1)}, f32[10]{0:T(128)S(1)}, u32[]{:S(2)}, u32[]{:S(2)}) %collective-permute-start.8) | collective-permute-done | bytes 72 | tf_op jit(solution)/shard_map/ppermute | solution.py:42
  15.0 1.7 %collective-permute-start = (f32[10]{0:T(128)S(1)}, f32[10]{0:T(128)S(1)}, u32[]{:S(2)}, u32[]{:S(2)}) collective-permute-start(f32[10]{0:T(128)S(1)} %get-tuple-element.53), channel_id=1, source_target_pairs={{0,4},{4,0},{8,12},{12,8},{16,20},{20,16},{24,28},{28,24},{1,5},{5... | collective-permute-start | bytes 128 | tf_op jit(solution)/shard_map/ppermute | solution.py:42
  16.8 1.8 %collective-permute-done = f32[10]{0:T(128)S(1)} collective-permute-done((f32[10]{0:T(128)S(1)}, f32[10]{0:T(128)S(1)}, u32[]{:S(2)}, u32[]{:S(2)}) %collective-permute-start) | collective-permute-done | bytes 72 | tf_op jit(solution)/shard_map/ppermute | solution.py:42
  19.3 3.7 %collective-permute-start.2 = (f32[10,64,128]{2,1,0:T(8,128)S(1)}, f32[10,64,128]{2,1,0:T(8,128)S(1)}, u32[]{:S(2)}, u32[]{:S(2)}) collective-permute-start(f32[10,64,128]{2,1,0:T(8,128)S(1)} %get-tuple-element.37), channel_id=1, source_target_pairs={{0,8},{4,12},{1,9},{5,13},{2,10},{6,14},{3,11},{7,15}} | collective-permute-start | bytes 983048 | tf_op jit(solution)/shard_map/ppermute | solution.py:62
  23.1 4.8 %collective-permute-done.2 = f32[10,64,128]{2,1,0:T(8,128)S(1)} collective-permute-done((f32[10,64,128]{2,1,0:T(8,128)S(1)}, f32[10,64,128]{2,1,0:T(8,128)S(1)}, u32[]{:S(2)}, u32[]{:S(2)}) %collective-permute-start.2) | collective-permute-done | bytes 327712 | tf_op jit(solution)/shard_map/ppermute | solution.py:62
  29.9 1.6 %collective-permute-start.5 = (f32[10,64,128]{2,1,0:T(8,128)S(1)}, f32[10,64,128]{2,1,0:T(8,128)S(1)}, u32[]{:S(2)}, u32[]{:S(2)}) collective-permute-start(f32[10,64,128]{2,1,0:T(8,128)S(1)} %get-tuple-element.49), channel_id=1, source_target_pairs={{0,4},{4,0},{8,12},{12,8},{16,20},{20,16},{24,28},{28,24},{1,5},{5... | collective-permute-start | bytes 983048 | tf_op jit(solution)/shard_map/ppermute | solution.py:82
  31.5 1.5 %fusion.9 = f32[128,20,64]{0,2,1:T(8,128)S(1)} fusion(f32[128,20,64]{0,2,1:T(8,128)S(1)} %bitcast.84, f32[128,128]{1,0:T(8,128)S(1)} %fusion.85, f32[20,128]{1,0:T(8,128)S(1)} %bitcast.97, pred[128,128]{1,0:T(8,128)(4,1)S(1)} %iota_compare_fusion.6, f32[128,20]{0,1:T(8,128)S(1)} %bitcast.102, f32[20]{0:T(128)S(1)} %copy-done.20), kind=kOutput, calls=%fused_computation.10 | convolution fusion | flops 127631360 | bytes 1413200 | tf_op jit(solution)/shard_map/jvp(hij,jhp->ihp)/dot_general | solution.py:167
  33.2 3.8 %collective-permute-done.5 = f32[10,64,128]{2,1,0:T(8,128)S(1)} collective-permute-done((f32[10,64,128]{2,1,0:T(8,128)S(1)}, f32[10,64,128]{2,1,0:T(8,128)S(1)}, u32[]{:S(2)}, u32[]{:S(2)}) %collective-permute-start.5) | collective-permute-done | bytes 327712 | tf_op jit(solution)/shard_map/ppermute | solution.py:82
  37.8 1.1 copy.24
  38.9 1.9 %multiply_reduce_fusion.7 = (f32[128]{0:T(128)S(1)}, f32[128]{0:T(128)S(1)}, f32[128,1280]{1,0:T(8,128)S(1)}) fusion(f32[128,1280]{1,0:T(8,128)} %param.10, f32[128,1280]{1,0:T(8,128)} %param.17, f32[1280]{0:T(1024)S(1)} %copy-done.14, f32[128,1280]{1,0:T(8,128)S(1)} %copy.23, f32[128,1280]{1,0:T(8,128)} %copy.24), kind=kLoop, calls=%fused_computation.32 | loop fusion | flops 1801984 | bytes 3282944 | tf_op jit(solution)/shard_map/reduce_sum | solution.py:244
  40.9 1.1 collective-permute-done.6
  42.0 1.6 %collective-permute-start.7 = (f32[2,128]{1,0:T(2,128)S(1)}, f32[2,128]{1,0:T(2,128)S(1)}, u32[]{:S(2)}, u32[]{:S(2)}) collective-permute-start(f32[2,128]{1,0:T(2,128)S(1)} %fusion.81), channel_id=1, source_target_pairs={{0,2},{1,3},{2,0},{3,1},{4,6},{5,7},{6,4},{7,5},{8,10},{9,11},{10,... | collective-permute-start | bytes 3080 | tf_op jit(solution)/shard_map/ppermute | solution.py:94
  43.6 2.0 %collective-permute-done.7 = f32[2,128]{1,0:T(2,128)S(1)} collective-permute-done((f32[2,128]{1,0:T(2,128)S(1)}, f32[2,128]{1,0:T(2,128)S(1)}, u32[]{:S(2)}, u32[]{:S(2)}) %collective-permute-start.7) | collective-permute-done | bytes 1056 | tf_op jit(solution)/shard_map/ppermute | solution.py:94
  45.7 1.3 %add_multiply_fusion = (f32[128,1280]{1,0:T(8,128)}, f32[128,1280]{1,0:T(8,128)S(1)}) fusion(f32[128,1280]{1,0:T(8,128)S(1)} %copy-done.1, f32[128,1280]{1,0:T(8,128)S(1)} %get-tuple-element.34, f32[128]{0:T(128)S(1)} %fusion.70, f32[128,1280]{1,0:T(8,128)S(1)} %copy-done.2, f32[128]{0:T(128)S(1)} %rsqrt_bitcast_fusion, f32[1280]{0:T(1024)S(1)} %copy-done.14), kind=kLoop, calls=%fused_computation.28 | loop fusion | flops 2621440 | bytes 3282944 | tf_op jit(solution)/shard_map/mul | solution.py:253
  47.7 1.6 %collective-permute-start.9 = (f32[10,64,128]{2,1,0:T(8,128)S(1)}, f32[10,64,128]{2,1,0:T(8,128)S(1)}, u32[]{:S(2)}, u32[]{:S(2)}) collective-permute-start(f32[10,64,128]{2,1,0:T(8,128)S(1)} %constant_dynamic-slice_fusion), channel_id=1, source_target_pairs={{28,24},{24,28},{20,16},{16,20},{12,8},{8,12},{4,0},{0,4},{29,25},... | collective-permute-start | bytes 983048 | tf_op jit(solution)/shard_map/ppermute | solution.py:42
  49.2 7.1 %collective-permute-done.9 = f32[10,64,128]{2,1,0:T(8,128)S(1)} collective-permute-done((f32[10,64,128]{2,1,0:T(8,128)S(1)}, f32[10,64,128]{2,1,0:T(8,128)S(1)}, u32[]{:S(2)}, u32[]{:S(2)}) %collective-permute-start.9) | collective-permute-done | bytes 327712 | tf_op jit(solution)/shard_map/ppermute | solution.py:42
  56.4 0.8 broadcast_add_fusion
  57.2 1.4 %collective-permute-start.10 = (f32[10,64,128]{2,1,0:T(8,128)}, f32[10,64,128]{2,1,0:T(8,128)}, u32[]{:S(2)}, u32[]{:S(2)}) collective-permute-start(f32[10,64,128]{2,1,0:T(8,128)} %get-tuple-element.28), channel_id=1, source_target_pairs={{28,20},{24,16},{29,21},{25,17},{30,22},{26,18},{31,23},{27,19}} | collective-permute-start | bytes 983048 | tf_op jit(solution)/shard_map/ppermute | solution.py:62
  59.4 1.9 %fusion.19 = (f32[20,128]{1,0:T(8,128)S(1)}, f32[20,128]{1,0:T(8,128)S(1)}, f32[128,128]{1,0:T(8,128)S(1)}) fusion(f32[128,128]{1,0:T(8,128)S(1)} %fusion.85, f32[20,128]{1,0:T(8,128)S(1)} %bitcast.98, pred[128,128]{1,0:T(8,128)(4,1)S(1)} %iota_compare_fusion.6, f32[20,64,128]{2,1,0:T(8,128)S(1)} %bitcast.89, f32[128,20,64]{0,2,1:T(8,128)S(1)} %bitcast.85, ...), kind=kOutput, calls=%fused_computation.20 | convolution fusion | flops 129575936 | bytes 1499136 | tf_op jit(solution)/shard_map/transpose(jvp(hij,jhp->ihp))/dot_general | solution.py:167
  61.7 1.5 %collective-permute-start.12 = (f32[10,64,128]{2,1,0:T(8,128)S(1)}, f32[10,64,128]{2,1,0:T(8,128)S(1)}, u32[]{:S(2)}, u32[]{:S(2)}) collective-permute-start(f32[10,64,128]{2,1,0:T(8,128)S(1)} %get-tuple-element.26), channel_id=1, source_target_pairs={{12,4},{8,0},{13,5},{9,1},{14,6},{10,2},{15,7},{11,3}} | collective-permute-start | bytes 983048 | tf_op jit(solution)/shard_map/ppermute | solution.py:59
  64.0 1.8 %fusion.12 = f32[128,20,64]{0,2,1:T(8,128)} fusion(f32[20,64,128]{2,1,0:T(8,128)S(1)} %bitcast.91, f32[128,128]{1,0:T(8,128)S(1)} %fusion.85, f32[20,128]{1,0:T(8,128)S(1)} %bitcast.99, pred[128,128]{1,0:T(8,128)(4,1)S(1)} %iota_compare_fusion.6), kind=kOutput, calls=%fused_computation.11 | convolution fusion | flops 127139840 | bytes 1402880 | tf_op jit(solution)/shard_map/transpose(jvp(hij,jhp->ihp))/dot_general | solution.py:167
  65.8 30.4 %collective-permute-done.12 = f32[10,64,128]{2,1,0:T(8,128)S(1)} collective-permute-done((f32[10,64,128]{2,1,0:T(8,128)S(1)}, f32[10,64,128]{2,1,0:T(8,128)S(1)}, u32[]{:S(2)}, u32[]{:S(2)}) %collective-permute-start.12) | collective-permute-done | bytes 327712 | tf_op jit(solution)/shard_map/ppermute | solution.py:59
  96.3 1.6 %collective-permute-start.13 = (f32[10,64,128]{2,1,0:T(8,128)S(1)}, f32[10,64,128]{2,1,0:T(8,128)S(1)}, u32[]{:S(2)}, u32[]{:S(2)}) collective-permute-start(f32[10,64,128]{2,1,0:T(8,128)S(1)} %get-tuple-element.47), channel_id=1, source_target_pairs={{28,24},{24,28},{20,16},{16,20},{12,8},{8,12},{4,0},{0,4},{29,25},... | collective-permute-start | bytes 983048 | tf_op jit(solution)/shard_map/ppermute | solution.py:82
  98.2 1.6 %collective-permute-start.17 = (f32[128,128]{1,0:T(8,128)S(1)}, f32[128,128]{1,0:T(8,128)S(1)}, u32[]{:S(2)}, u32[]{:S(2)}) collective-permute-start(f32[128,128]{1,0:T(8,128)S(1)} %add.165), channel_id=1, source_target_pairs={{0,2},{1,3},{2,0},{3,1},{4,6},{5,7},{6,4},{7,5},{8,10},{9,11},{10,... | collective-permute-start | bytes 196616 | tf_op jit(solution)/shard_map/ppermute | solution.py:94
  100.5 2.0 %collective-permute-done.17 = f32[128,128]{1,0:T(8,128)S(1)} collective-permute-done((f32[128,128]{1,0:T(8,128)S(1)}, f32[128,128]{1,0:T(8,128)S(1)}, u32[]{:S(2)}, u32[]{:S(2)}) %collective-permute-start.17) | collective-permute-done | bytes 65568 | tf_op jit(solution)/shard_map/ppermute | solution.py:94
  105.0 2.6 %multiply_reduce_fusion.2 = (f32[128,20]{0,1:T(8,128)S(1)}, f32[128,20]{0,1:T(8,128)S(1)}, f32[128,20]{0,1:T(8,128)S(1)}, f32[128,20,64]{0,2,1:T(8,128)S(1)}, f32[128,20]{0,1:T(8,128)}) fusion(f32[128,20,64]{0,2,1:T(8,128)S(1)} %bitcast.86, f32[128,20]{0,1:T(8,128)S(1)} %bitcast.104, f32[128,20]{0,1:T(8,128)S(1)} %get-tuple-element.52, ...), kind=kOutput, calls=%fused_computation.24 | convolution fusion | flops 128768000 | bytes 4059217 | tf_op jit(solution)/shard_map/transpose(jvp(jhp,jn->hpn))/dot_general | solution.py:186
  110.2 1.6 %collective-permute-start.15 = (f32[128,128]{1,0:T(8,128)S(1)}, f32[128,128]{1,0:T(8,128)S(1)}, u32[]{:S(2)}, u32[]{:S(2)}) collective-permute-start(f32[128,128]{1,0:T(8,128)S(1)} %add.162), channel_id=1, source_target_pairs={{0,2},{1,3},{2,0},{3,1},{4,6},{5,7},{6,4},{7,5},{8,10},{9,11},{10,... | collective-permute-start | bytes 196616 | tf_op jit(solution)/shard_map/ppermute | solution.py:94
  112.6 1.1 copy.28
  113.7 0.8 collective-permute-done.15
  (104 shorter events, 15.4 us)
Async XLA Ops:
  0.6 28.9 %copy-start = (f32[128,128]{1,0:T(8,128)S(1)}, f32[128,128]{1,0:T(8,128)}, u32[]{:S(2)}) copy-start(f32[128,128]{1,0:T(8,128)} %param.12) | copy-start | bytes 196612
  1.8 1.4 %copy-start.10 = (f32[20,128]{1,0:T(8,128)S(1)}, f32[20,128]{1,0:T(8,128)}, u32[]{:S(2)}) copy-start(f32[20,128]{1,0:T(8,128)} %param.13) | copy-start | bytes 30724
  3.7 15.5 %collective-permute-start.1 = (f32[10,64,128]{2,1,0:T(8,128)S(1)}, f32[10,64,128]{2,1,0:T(8,128)S(1)}, u32[]{:S(2)}, u32[]{:S(2)}) collective-permute-start(f32[10,64,128]{2,1,0:T(8,128)S(1)} %constant_dynamic-slice_fusion.1), channel_id=1, source_target_pairs={{0,4},{4,0},{8,12},{12,8},{16,20},{20,16},{24,28},{28,24},{1,5},{5... | collective-permute-start | bytes 983048 | tf_op jit(solution)/shard_map/ppermute | solution.py:42
  6.8 7.7 %collective-permute-start.8 = (f32[10]{0:T(128)S(1)}, f32[10]{0:T(128)S(1)}, u32[]{:S(2)}, u32[]{:S(2)}) collective-permute-start(f32[10]{0:T(128)S(1)} %dynamic_slice.29), channel_id=1, source_target_pairs={{28,24},{24,28},{20,16},{16,20},{12,8},{8,12},{4,0},{0,4},{29,25},... | collective-permute-start | bytes 128 | tf_op jit(solution)/shard_map/ppermute | solution.py:42
  14.5 2.3 %copy-start.16 = (f32[10]{0:T(128)}, f32[10]{0:T(128)S(1)}, u32[]{:S(2)}) copy-start(f32[10]{0:T(128)S(1)} %collective-permute-done.8) | copy-start | bytes 124
  15.0 3.5 %collective-permute-start = (f32[10]{0:T(128)S(1)}, f32[10]{0:T(128)S(1)}, u32[]{:S(2)}, u32[]{:S(2)}) collective-permute-start(f32[10]{0:T(128)S(1)} %get-tuple-element.53), channel_id=1, source_target_pairs={{0,4},{4,0},{8,12},{12,8},{16,20},{20,16},{24,28},{28,24},{1,5},{5... | collective-permute-start | bytes 128 | tf_op jit(solution)/shard_map/ppermute | solution.py:42
  19.3 8.6 %collective-permute-start.2 = (f32[10,64,128]{2,1,0:T(8,128)S(1)}, f32[10,64,128]{2,1,0:T(8,128)S(1)}, u32[]{:S(2)}, u32[]{:S(2)}) collective-permute-start(f32[10,64,128]{2,1,0:T(8,128)S(1)} %get-tuple-element.37), channel_id=1, source_target_pairs={{0,8},{4,12},{1,9},{5,13},{2,10},{6,14},{3,11},{7,15}} | collective-permute-start | bytes 983048 | tf_op jit(solution)/shard_map/ppermute | solution.py:62
  28.0 0.7 collective-permute-start.3
  28.8 0.9 collective-permute-start.4
  29.7 1.8 %copy-start.20 = (f32[20]{0:T(128)S(1)}, f32[20]{0:T(128)}, u32[]{:S(2)}) copy-start(f32[20]{0:T(128)} %param.15) | copy-start | bytes 244
  29.9 7.1 %collective-permute-start.5 = (f32[10,64,128]{2,1,0:T(8,128)S(1)}, f32[10,64,128]{2,1,0:T(8,128)S(1)}, u32[]{:S(2)}, u32[]{:S(2)}) collective-permute-start(f32[10,64,128]{2,1,0:T(8,128)S(1)} %get-tuple-element.49), channel_id=1, source_target_pairs={{0,4},{4,0},{8,12},{12,8},{16,20},{20,16},{24,28},{28,24},{1,5},{5... | collective-permute-start | bytes 983048 | tf_op jit(solution)/shard_map/ppermute | solution.py:82
  38.9 6.8 %copy-start.1 = (f32[128,1280]{1,0:T(8,128)S(1)}, f32[128,1280]{1,0:T(8,128)}, u32[]{:S(2)}) copy-start(f32[128,1280]{1,0:T(8,128)} %param.10) | copy-start | bytes 1966084
  38.9 6.8 %copy-start.2 = (f32[128,1280]{1,0:T(8,128)S(1)}, f32[128,1280]{1,0:T(8,128)}, u32[]{:S(2)}) copy-start(f32[128,1280]{1,0:T(8,128)} %param.17) | copy-start | bytes 1966084
  40.8 1.2 %collective-permute-start.6 = (f32[2,128]{1,0:T(2,128)S(1)}, f32[2,128]{1,0:T(2,128)S(1)}, u32[]{:S(2)}, u32[]{:S(2)}) collective-permute-start(f32[2,128]{1,0:T(2,128)S(1)} %pad_maximum_fusion), channel_id=1, source_target_pairs={{0,1},{1,0},{2,3},{3,2},{4,5},{5,4},{6,7},{7,6},{8,9},{9,8},{10,11... | collective-permute-start | bytes 3080 | tf_op jit(solution)/shard_map/ppermute | solution.py:94
  42.0 3.6 %collective-permute-start.7 = (f32[2,128]{1,0:T(2,128)S(1)}, f32[2,128]{1,0:T(2,128)S(1)}, u32[]{:S(2)}, u32[]{:S(2)}) collective-permute-start(f32[2,128]{1,0:T(2,128)S(1)} %fusion.81), channel_id=1, source_target_pairs={{0,2},{1,3},{2,0},{3,1},{4,6},{5,7},{6,4},{7,5},{8,10},{9,11},{10,... | collective-permute-start | bytes 3080 | tf_op jit(solution)/shard_map/ppermute | solution.py:94
  47.6 8.7 %copy-start.15 = (f32[10]{0:T(128)S(1)}, f32[10]{0:T(128)}, u32[]{:S(2)}) copy-start(f32[10]{0:T(128)} %get-tuple-element.32) | copy-start | bytes 124
  47.7 8.7 %collective-permute-start.9 = (f32[10,64,128]{2,1,0:T(8,128)S(1)}, f32[10,64,128]{2,1,0:T(8,128)S(1)}, u32[]{:S(2)}, u32[]{:S(2)}) collective-permute-start(f32[10,64,128]{2,1,0:T(8,128)S(1)} %constant_dynamic-slice_fusion), channel_id=1, source_target_pairs={{28,24},{24,28},{20,16},{16,20},{12,8},{8,12},{4,0},{0,4},{29,25},... | collective-permute-start | bytes 983048 | tf_op jit(solution)/shard_map/ppermute | solution.py:42
  57.2 1.4 %collective-permute-start.10 = (f32[10,64,128]{2,1,0:T(8,128)}, f32[10,64,128]{2,1,0:T(8,128)}, u32[]{:S(2)}, u32[]{:S(2)}) collective-permute-start(f32[10,64,128]{2,1,0:T(8,128)} %get-tuple-element.28), channel_id=1, source_target_pairs={{28,20},{24,16},{29,21},{25,17},{30,22},{26,18},{31,23},{27,19}} | collective-permute-start | bytes 983048 | tf_op jit(solution)/shard_map/ppermute | solution.py:62
  58.7 2.8 %collective-permute-start.11 = (f32[10,64,128]{2,1,0:T(8,128)S(1)}, f32[10,64,128]{2,1,0:T(8,128)S(1)}, u32[]{:S(2)}, u32[]{:S(2)}) collective-permute-start(f32[10,64,128]{2,1,0:T(8,128)S(1)} %multiply_add_fusion.2), channel_id=1, source_target_pairs={{20,12},{16,8},{21,13},{17,9},{22,14},{18,10},{23,15},{19,11}} | collective-permute-start | bytes 983048 | tf_op jit(solution)/shard_map/ppermute | solution.py:62
  61.5 1.6 %copy-start.8 = (f32[10,64,128]{2,1,0:T(8,128)S(1)}, f32[10,64,128]{2,1,0:T(8,128)}, u32[]{:S(2)}) copy-start(f32[10,64,128]{2,1,0:T(8,128)} %copy-done.7) | copy-start | bytes 983044
  61.7 34.5 %collective-permute-start.12 = (f32[10,64,128]{2,1,0:T(8,128)S(1)}, f32[10,64,128]{2,1,0:T(8,128)S(1)}, u32[]{:S(2)}, u32[]{:S(2)}) collective-permute-start(f32[10,64,128]{2,1,0:T(8,128)S(1)} %get-tuple-element.26), channel_id=1, source_target_pairs={{12,4},{8,0},{13,5},{9,1},{14,6},{10,2},{15,7},{11,3}} | collective-permute-start | bytes 983048 | tf_op jit(solution)/shard_map/ppermute | solution.py:59
  63.9 32.3 %copy-start.6 = (f32[10,64,128]{2,1,0:T(8,128)S(1)}, f32[10,64,128]{2,1,0:T(8,128)}, u32[]{:S(2)}) copy-start(f32[10,64,128]{2,1,0:T(8,128)} %copy-done.5) | copy-start | bytes 983044
  63.9 32.3 %copy-start.17 = (f32[10]{0:T(128)S(1)}, f32[10]{0:T(128)}, u32[]{:S(2)}) copy-start(f32[10]{0:T(128)} %copy-done.16) | copy-start | bytes 124
  63.9 32.3 %copy-start.18 = (f32[10]{0:T(128)S(1)}, f32[10]{0:T(128)}, u32[]{:S(2)}) copy-start(f32[10]{0:T(128)} %get-tuple-element.33) | copy-start | bytes 124
  63.9 34.2 %collective-permute-start.16 = (f32[128,128]{1,0:T(8,128)S(1)}, f32[128,128]{1,0:T(8,128)S(1)}, u32[]{:S(2)}, u32[]{:S(2)}) collective-permute-start(f32[128,128]{1,0:T(8,128)S(1)} %fusion.16), channel_id=1, source_target_pairs={{0,1},{1,0},{2,3},{3,2},{4,5},{5,4},{6,7},{7,6},{8,9},{9,8},{10,11... | collective-permute-start | bytes 196616 | tf_op jit(solution)/shard_map/ppermute | solution.py:94
  96.3 7.1 %collective-permute-start.13 = (f32[10,64,128]{2,1,0:T(8,128)S(1)}, f32[10,64,128]{2,1,0:T(8,128)S(1)}, u32[]{:S(2)}, u32[]{:S(2)}) collective-permute-start(f32[10,64,128]{2,1,0:T(8,128)S(1)} %get-tuple-element.47), channel_id=1, source_target_pairs={{28,24},{24,28},{20,16},{16,20},{12,8},{8,12},{4,0},{0,4},{29,25},... | collective-permute-start | bytes 983048 | tf_op jit(solution)/shard_map/ppermute | solution.py:82
  98.2 4.3 %collective-permute-start.17 = (f32[128,128]{1,0:T(8,128)S(1)}, f32[128,128]{1,0:T(8,128)S(1)}, u32[]{:S(2)}, u32[]{:S(2)}) collective-permute-start(f32[128,128]{1,0:T(8,128)S(1)} %add.165), channel_id=1, source_target_pairs={{0,2},{1,3},{2,0},{3,1},{4,6},{5,7},{6,4},{7,5},{8,10},{9,11},{10,... | collective-permute-start | bytes 196616 | tf_op jit(solution)/shard_map/ppermute | solution.py:94
  103.5 1.5 %copy-start.21 = (f32[20]{0:T(128)S(1)}, f32[20]{0:T(128)}, u32[]{:S(2)}) copy-start(f32[20]{0:T(128)} %param.15) | copy-start | bytes 244
  105.0 3.1 %copy-start.4 = (f32[10,64,128]{2,1,0:T(8,128)S(1)}, f32[10,64,128]{2,1,0:T(8,128)}, u32[]{:S(2)}) copy-start(f32[10,64,128]{2,1,0:T(8,128)} %copy-done.3) | copy-start | bytes 983044
  108.2 3.6 %copy-start.13 = (f32[20,1]{1,0:T(8,128)S(1)}, f32[20,1]{1,0:T(8,128)}, u32[]{:S(2)}) copy-start(f32[20,1]{1,0:T(8,128)} %exponential_multiply_fusion) | copy-start | bytes 244
  108.9 1.3 %collective-permute-start.14 = (f32[128,128]{1,0:T(8,128)S(1)}, f32[128,128]{1,0:T(8,128)S(1)}, u32[]{:S(2)}, u32[]{:S(2)}) collective-permute-start(f32[128,128]{1,0:T(8,128)S(1)} %fusion.15), channel_id=1, source_target_pairs={{0,1},{1,0},{2,3},{3,2},{4,5},{5,4},{6,7},{7,6},{8,9},{9,8},{10,11... | collective-permute-start | bytes 196616 | tf_op jit(solution)/shard_map/ppermute | solution.py:94
  110.2 4.3 %collective-permute-start.15 = (f32[128,128]{1,0:T(8,128)S(1)}, f32[128,128]{1,0:T(8,128)S(1)}, u32[]{:S(2)}, u32[]{:S(2)}) collective-permute-start(f32[128,128]{1,0:T(8,128)S(1)} %add.162), channel_id=1, source_target_pairs={{0,2},{1,3},{2,0},{3,1},{4,6},{5,7},{6,4},{7,5},{8,10},{9,11},{10,... | collective-permute-start | bytes 196616 | tf_op jit(solution)/shard_map/ppermute | solution.py:94
  (8 other events, 7.5 us)

commit v15 on v14

--- a/solution.py
+++ b/solution.py
@@ -14,10 +14,10 @@
     return (earlier[0] * later[0], later[0][:, None, None] * earlier[1] + later[1])
 
 
-def pair_scan(decay, state, axis, reverse):
+def pair_scan(decay, state_of, axis, reverse):
     count = lax.axis_size(axis)
     if count == 1:
-        return jnp.zeros_like(state)
+        return jnp.zeros_like(state_of(0, decay.shape[0]))
     assert count % 2 == 0 and decay.shape[0] % 2 == 0
     place = lax.axis_index(axis)
     virt = count - 1 - place if reverse else place
@@ -36,10 +36,12 @@
     def part(x, start):
         return lax.dynamic_slice_in_dim(x, start, half, 0)
 
-    a_own, s_own = part(decay, own_start), part(state, own_start)
-    a_snd, s_snd = part(decay, send_start), part(state, send_start)
+    a_snd, s_snd = part(decay, send_start), state_of(send_start, half)
+    row = jnp.broadcast_to(a_snd[:, None, None], (half, 1, s_snd.shape[2]))
     swap = [(phys(u), phys(u ^ 1)) for u in range(count)]
-    a_rcv, s_rcv = lax.ppermute((a_snd, s_snd), axis, swap)
+    got = lax.ppermute(jnp.concatenate([s_snd, row], 1), axis, swap)
+    s_rcv, a_rcv = got[:, : s_snd.shape[1]], got[:, s_snd.shape[1], 0]
+    a_own, s_own = part(decay, own_start), state_of(own_start, half)
     lead = (jnp.where(first, a_own, a_rcv), jnp.where(first, s_own, s_rcv))
     trail = (jnp.where(first, a_rcv, a_own), jnp.where(first, s_rcv, s_own))
     a_tot, s_tot = combine(lead, trail)
@@ -212,7 +214,11 @@
     )
     to_end = jnp.exp(cumul[:, -1:] - cumul)
     weighted_in = scaled * jnp.transpose(to_end)[:, :, None]
-    local_state = jnp.einsum("jhp,jn->hpn", weighted_in, write_keys, precision=highest)
+
+    def local_state(start, size):
+        part = lax.dynamic_slice_in_dim(weighted_in, start, size, 1)
+        return jnp.einsum("jhp,jn->hpn", part, write_keys, precision=highest)
+
     state_in = pair_scan(decay_total, local_state, "seq", False)
     single = length == BLOCK
     if single:
@@ -253,7 +259,11 @@
     grad_gate = grad_gated * mixed_out * sigmoid_gate * (1.0 + gate_pre * (1.0 - sigmoid_gate))
     from_start = jnp.transpose(jnp.exp(cumul))
     weighted_grad = grad_mixed.reshape(length, head_count, head_width) * from_start[:, :, None]
-    local_grad = jnp.einsum("jhp,jn->hpn", weighted_grad, read_queries, precision=highest)
+
+    def local_grad(start, size):
+        part = lax.dynamic_slice_in_dim(weighted_grad, start, size, 1)
+        return jnp.einsum("jhp,jn->hpn", part, read_queries, precision=highest)
+
     state_grad = pair_scan(decay_total, local_grad, "seq", True)
     if single:
         gf_w, gs_w, gd_w, gw_w, gr_w = pull_w(grad_mixed)

time: 116 us -> 122 us (1.052)
  waiting for transfers between devices: 62.3 us -> 65.2 us
  matrix products: 14 us -> 16.6 us
  starting transfers between devices: 23.1 us -> 21.1 us
  local copies, waits for them, and re-layouts: 5.32 us -> 7.19 us
    dot_general x2 -> x4, matrix products: 0.83 us -> 2.95 us  [the longest x2 2.38 us: local_grad(): return jnp.einsum('jhp,jn->hpn', part, read_queries, precision=highest)]
    ppermute x4 -> x2, starting transfers between devices: 6.36 us -> 4.48 us  [pair_scan(): got = lax.ppermute(jnp.concatenate([s_snd, row], 1), axis, swap)]
    ppermute x4, waiting for transfers between devices: 4.83 us -> 6.06 us  [pair_scan(): a_in, s_in = lax.ppermute(out, axis, pairs)]
    unnamed x46 -> x36, local copies, waits for them, and re-layouts: 3.27 us -> 3.95 us
    ppermute x4 -> x2, waiting for transfers between devices: 16.5 us -> 16.9 us  [pair_scan(): got = lax.ppermute(jnp.concatenate([s_snd, row], 1), axis, swap)]
  transfers between devices with their start and end apart: 18 -> 16, of which waited for: 12 -> 11; matrix products, arithmetic and copies ran while one was open for 11% -> 10% of each run, Pallas kernels for 0% -> 0%
where the time goes in v15:
time: 122 us; the launch traced here: 121 us
  waiting for transfers between devices  65.2 us (53%)
  starting transfers between devices  21.1 us (17%)
  matrix products  16.6 us (14%)
  other arithmetic  9.69 us (8%)
  local copies, waits for them, and re-layouts  7.19 us (6%)
    ppermute x2, waiting for transfers between devices, pair_scan(): s_in = lax.ppermute(out[1], axis, pairs)  31 us
    ppermute x2, waiting for transfers between devices, pair_scan(): got = lax.ppermute(jnp.concatenate([s_snd, row], 1), axis, swap)  16.9 us
    ppermute x4, starting transfers between devices, pair_scan(): a_in, s_in = lax.ppermute(out, axis, pairs)  6.5 us
    ppermute x6, waiting for transfers between devices, butterfly_psum(): got = lax.ppermute(parts, axis, [(i, i ^ k) for i in range(count)])  6.43 us
    ppermute x4, waiting for transfers between devices, pair_scan(): a_in, s_in = lax.ppermute(out, axis, pairs)  6.06 us
    dot_general x3, matrix products, within_part(): within = jnp.einsum('hij,jhp->ihp', masked, scaled, precision=highest)  5.17 us
    ppermute x6, starting transfers between devices, butterfly_psum(): got = lax.ppermute(parts, axis, [(i, i ^ k) for i in range(count)])  4.94 us
    ppermute x2, waiting for transfers between devices, pair_scan(): other = lax.ppermute(send, axis, swap)  4.88 us
  transfers between devices with their start and end apart: 16, of which 11 were waited for; matrix products, arithmetic and copies ran while one was open for 10% of the time, Pallas kernels for 0%

profile of v15, /device:TPU:0, one launch (start us, length us, event | category | flops | bytes accessed | tf_op | source)
XLA Modules:
  0.0 121.0 jit_solution(12109768790046672693)
XLA Ops:
  1.8 1.3 %copy.22 = f32[128,1280]{0,1:T(8,128)S(1)} copy(f32[128,1280]{1,0:T(8,128)} %param.9) | data formatting | bytes 1310720 | tf_op args[0]
  4.5 3.0 %collective-permute-start = (f32[10,65,128]{2,1,0:T(8,128)S(1)}, f32[10,65,128]{2,1,0:T(8,128)S(1)}, u32[]{:S(2)}, u32[]{:S(2)}) collective-permute-start(f32[10,65,128]{2,1,0:T(8,128)S(1)} %pad_maximum_fusion), channel_id=1, source_target_pairs={{0,4},{4,0},{8,12},{12,8},{16,20},{20,16},{24,28},{28,24},{1,5},{5... | collective-permute-start | bytes 998408 | tf_op jit(solution)/shard_map/ppermute | solution.py:42
  7.5 8.6 %collective-permute-done = f32[10,65,128]{2,1,0:T(8,128)S(1)} collective-permute-done((f32[10,65,128]{2,1,0:T(8,128)S(1)}, f32[10,65,128]{2,1,0:T(8,128)S(1)}, u32[]{:S(2)}, u32[]{:S(2)}) %collective-permute-start) | collective-permute-done | bytes 332832 | tf_op jit(solution)/shard_map/ppermute | solution.py:42
  16.6 3.8 %collective-permute-start.1 = (f32[10,64,128]{2,1,0:T(8,128)S(1)}, f32[10,64,128]{2,1,0:T(8,128)S(1)}, u32[]{:S(2)}, u32[]{:S(2)}) collective-permute-start(f32[10,64,128]{2,1,0:T(8,128)S(1)} %get-tuple-element.37), channel_id=1, source_target_pairs={{0,8},{4,12},{1,9},{5,13},{2,10},{6,14},{3,11},{7,15}} | collective-permute-start | bytes 983048 | tf_op jit(solution)/shard_map/ppermute | solution.py:64
  20.4 6.0 %collective-permute-done.1 = f32[10,64,128]{2,1,0:T(8,128)S(1)} collective-permute-done((f32[10,64,128]{2,1,0:T(8,128)S(1)}, f32[10,64,128]{2,1,0:T(8,128)S(1)}, u32[]{:S(2)}, u32[]{:S(2)}) %collective-permute-start.1) | collective-permute-done | bytes 327712 | tf_op jit(solution)/shard_map/ppermute | solution.py:64
  28.5 1.5 %collective-permute-start.4 = (f32[10,64,128]{2,1,0:T(8,128)S(1)}, f32[10,64,128]{2,1,0:T(8,128)S(1)}, u32[]{:S(2)}, u32[]{:S(2)}) collective-permute-start(f32[10,64,128]{2,1,0:T(8,128)S(1)} %get-tuple-element.49), channel_id=1, source_target_pairs={{0,4},{4,0},{8,12},{12,8},{16,20},{20,16},{24,28},{28,24},{1,5},{5... | collective-permute-start | bytes 983048 | tf_op jit(solution)/shard_map/ppermute | solution.py:84
  30.1 1.5 %fusion.9 = f32[128,20,64]{0,2,1:T(8,128)S(1)} fusion(f32[128,20,64]{0,2,1:T(8,128)S(1)} %bitcast.94, f32[128,128]{1,0:T(8,128)S(1)} %fusion.86, f32[20,128]{1,0:T(8,128)S(1)} %bitcast.105, pred[128,128]{1,0:T(8,128)(4,1)S(1)} %iota_compare_fusion.6, f32[128,20]{0,1:T(8,128)S(1)} %bitcast.111, f32[20]{0:T(128)S(1)} %copy-done.15), kind=kOutput, calls=%fused_computation.10 | convolution fusion | flops 127631360 | bytes 1413200 | tf_op jit(solution)/shard_map/jvp(hij,jhp->ihp)/dot_general | solution.py:169
  31.8 4.5 %collective-permute-done.4 = f32[10,64,128]{2,1,0:T(8,128)S(1)} collective-permute-done((f32[10,64,128]{2,1,0:T(8,128)S(1)}, f32[10,64,128]{2,1,0:T(8,128)S(1)}, u32[]{:S(2)}, u32[]{:S(2)}) %collective-permute-start.4) | collective-permute-done | bytes 327712 | tf_op jit(solution)/shard_map/ppermute | solution.py:84
  36.9 1.1 copy.24
  38.0 1.9 %multiply_reduce_fusion.7 = (f32[128]{0:T(128)S(1)}, f32[128]{0:T(128)S(1)}, f32[128,1280]{1,0:T(8,128)S(1)}) fusion(f32[128,1280]{1,0:T(8,128)} %param.10, f32[128,1280]{1,0:T(8,128)} %param.17, f32[1280]{0:T(1024)S(1)} %copy-done.13, f32[128,1280]{1,0:T(8,128)S(1)} %copy.23, f32[128,1280]{1,0:T(8,128)} %copy.24), kind=kLoop, calls=%fused_computation.32 | loop fusion | flops 1801984 | bytes 3282944 | tf_op jit(solution)/shard_map/reduce_sum | solution.py:250
  40.0 1.1 collective-permute-done.5
  41.2 1.6 %collective-permute-start.6 = (f32[2,128]{1,0:T(2,128)S(1)}, f32[2,128]{1,0:T(2,128)S(1)}, u32[]{:S(2)}, u32[]{:S(2)}) collective-permute-start(f32[2,128]{1,0:T(2,128)S(1)} %fusion.81), channel_id=1, source_target_pairs={{0,2},{1,3},{2,0},{3,1},{4,6},{5,7},{6,4},{7,5},{8,10},{9,11},{10,... | collective-permute-start | bytes 3080 | tf_op jit(solution)/shard_map/ppermute | solution.py:96
  42.7 2.1 %collective-permute-done.6 = f32[2,128]{1,0:T(2,128)S(1)} collective-permute-done((f32[2,128]{1,0:T(2,128)S(1)}, f32[2,128]{1,0:T(2,128)S(1)}, u32[]{:S(2)}, u32[]{:S(2)}) %collective-permute-start.6) | collective-permute-done | bytes 1056 | tf_op jit(solution)/shard_map/ppermute | solution.py:96
  44.9 1.3 %add_multiply_fusion = (f32[128,1280]{1,0:T(8,128)}, f32[128,1280]{1,0:T(8,128)S(1)}) fusion(f32[128,1280]{1,0:T(8,128)S(1)} %copy-done.2, f32[128,1280]{1,0:T(8,128)S(1)} %get-tuple-element.34, f32[128]{0:T(128)S(1)} %fusion.70, f32[128,1280]{1,0:T(8,128)S(1)} %copy-done.3, f32[128]{0:T(128)S(1)} %rsqrt_bitcast_fusion, f32[1280]{0:T(1024)S(1)} %copy-done.13), kind=kLoop, calls=%fused_computation.28 | loop fusion | flops 2621440 | bytes 3282944 | tf_op jit(solution)/shard_map/mul | solution.py:259
  47.6 1.5 %collective-permute-start.7 = (f32[10,65,128]{2,1,0:T(8,128)}, f32[10,65,128]{2,1,0:T(8,128)}, u32[]{:S(2)}, u32[]{:S(2)}) collective-permute-start(f32[10,65,128]{2,1,0:T(8,128)} %pad_maximum_fusion.1), channel_id=1, source_target_pairs={{28,24},{24,28},{20,16},{16,20},{12,8},{8,12},{4,0},{0,4},{29,25},... | collective-permute-start | bytes 998408 | tf_op jit(solution)/shard_map/ppermute | solution.py:42
  49.0 8.3 %collective-permute-done.7 = f32[10,65,128]{2,1,0:T(8,128)} collective-permute-done((f32[10,65,128]{2,1,0:T(8,128)}, f32[10,65,128]{2,1,0:T(8,128)}, u32[]{:S(2)}, u32[]{:S(2)}) %collective-permute-start.7) | collective-permute-done | bytes 332832 | tf_op jit(solution)/shard_map/ppermute | solution.py:42
  57.4 0.9 slice_reduce_fusion.1
  58.9 2.1 %broadcast_add_fusion = (f32[10,64,128]{2,1,0:T(8,128)}, f32[10,64,128]{2,1,0:T(8,128)S(1)}, f32[10,64,128]{2,1,0:T(8,128)}) fusion(f32[10]{0:T(128)S(1)} %get-tuple-element.30, f32[10,65,128]{2,1,0:T(8,128)} %collective-permute-done.7, pred[]{:T(512)S(6)} %eq.31, f32[10]{0:T(128)S(1)} %get-tuple-element.32, f32[128,128]{1,0:T(8,128)S(1)} %copy-done, ...), kind=kOutput, calls=%fused_computation.76 | convolution fusion | flops 63324160 | bytes 1704965 | tf_op jit(solution)/shard_map/jhp,jn->hpn/dot_general | solution.py:265
  61.0 1.4 %collective-permute-start.8 = (f32[10,64,128]{2,1,0:T(8,128)}, f32[10,64,128]{2,1,0:T(8,128)}, u32[]{:S(2)}, u32[]{:S(2)}) collective-permute-start(f32[10,64,128]{2,1,0:T(8,128)} %get-tuple-element.28), channel_id=1, source_target_pairs={{28,20},{24,16},{29,21},{25,17},{30,22},{26,18},{31,23},{27,19}} | collective-permute-start | bytes 983048 | tf_op jit(solution)/shard_map/ppermute | solution.py:64
  63.2 1.9 %fusion.19 = (f32[20,128]{1,0:T(8,128)S(1)}, f32[20,128]{1,0:T(8,128)S(1)}, f32[128,128]{1,0:T(8,128)S(1)}) fusion(f32[128,128]{1,0:T(8,128)S(1)} %fusion.86, f32[20,128]{1,0:T(8,128)S(1)} %bitcast.106, pred[128,128]{1,0:T(8,128)(4,1)S(1)} %iota_compare_fusion.6, f32[20,64,128]{2,1,0:T(8,128)S(1)} %bitcast.98, f32[128,20,64]{0,2,1:T(8,128)S(1)} %bitcast.95, ...), kind=kOutput, calls=%fused_computation.20 | convolution fusion | flops 129575936 | bytes 1499136 | tf_op jit(solution)/shard_map/transpose(jvp(hij,jhp->ihp))/dot_general | solution.py:169
  65.5 1.5 %collective-permute-start.10 = (f32[10,64,128]{2,1,0:T(8,128)S(1)}, f32[10,64,128]{2,1,0:T(8,128)S(1)}, u32[]{:S(2)}, u32[]{:S(2)}) collective-permute-start(f32[10,64,128]{2,1,0:T(8,128)S(1)} %get-tuple-element.26), channel_id=1, source_target_pairs={{12,4},{8,0},{13,5},{9,1},{14,6},{10,2},{15,7},{11,3}} | collective-permute-start | bytes 983048 | tf_op jit(solution)/shard_map/ppermute | solution.py:61
  67.8 1.8 %fusion.12 = f32[128,20,64]{0,2,1:T(8,128)} fusion(f32[20,64,128]{2,1,0:T(8,128)S(1)} %bitcast.99, f32[128,128]{1,0:T(8,128)S(1)} %fusion.86, f32[20,128]{1,0:T(8,128)S(1)} %bitcast.107, pred[128,128]{1,0:T(8,128)(4,1)S(1)} %iota_compare_fusion.6), kind=kOutput, calls=%fused_computation.11 | convolution fusion | flops 127139840 | bytes 1402880 | tf_op jit(solution)/shard_map/transpose(jvp(hij,jhp->ihp))/dot_general | solution.py:169
  69.5 31.0 %collective-permute-done.10 = f32[10,64,128]{2,1,0:T(8,128)S(1)} collective-permute-done((f32[10,64,128]{2,1,0:T(8,128)S(1)}, f32[10,64,128]{2,1,0:T(8,128)S(1)}, u32[]{:S(2)}, u32[]{:S(2)}) %collective-permute-start.10) | collective-permute-done | bytes 327712 | tf_op jit(solution)/shard_map/ppermute | solution.py:61
  100.5 1.1 add_select_fusion.1
  101.6 1.5 %collective-permute-start.11 = (f32[10,64,128]{2,1,0:T(8,128)S(1)}, f32[10,64,128]{2,1,0:T(8,128)S(1)}, u32[]{:S(2)}, u32[]{:S(2)}) collective-permute-start(f32[10,64,128]{2,1,0:T(8,128)S(1)} %get-tuple-element.47), channel_id=1, source_target_pairs={{28,24},{24,28},{20,16},{16,20},{12,8},{8,12},{4,0},{0,4},{29,25},... | collective-permute-start | bytes 983048 | tf_op jit(solution)/shard_map/ppermute | solution.py:84
  103.4 1.6 %collective-permute-start.15 = (f32[128,128]{1,0:T(8,128)S(1)}, f32[128,128]{1,0:T(8,128)S(1)}, u32[]{:S(2)}, u32[]{:S(2)}) collective-permute-start(f32[128,128]{1,0:T(8,128)S(1)} %add.165), channel_id=1, source_target_pairs={{0,2},{1,3},{2,0},{3,1},{4,6},{5,7},{6,4},{7,5},{8,10},{9,11},{10,... | collective-permute-start | bytes 196616 | tf_op jit(solution)/shard_map/ppermute | solution.py:96
  105.8 1.9 %collective-permute-done.15 = f32[128,128]{1,0:T(8,128)S(1)} collective-permute-done((f32[128,128]{1,0:T(8,128)S(1)}, f32[128,128]{1,0:T(8,128)S(1)}, u32[]{:S(2)}, u32[]{:S(2)}) %collective-permute-start.15) | collective-permute-done | bytes 65568 | tf_op jit(solution)/shard_map/ppermute | solution.py:96
  110.3 2.0 %multiply_reduce_fusion.2 = (f32[128,20]{0,1:T(8,128)S(1)}, f32[128,20]{0,1:T(8,128)S(1)}, f32[128,20]{0,1:T(8,128)S(1)}, f32[128,20,64]{0,2,1:T(8,128)S(1)}, f32[128,20]{0,1:T(8,128)S(1)}) fusion(f32[128,20,64]{0,2,1:T(8,128)S(1)} %bitcast.96, f32[128,20]{0,1:T(8,128)} %bitcast.109, f32[128,20]{0,1:T(8,128)S(1)} %get-tuple-element.52, ...), kind=kOutput, calls=%fused_computation.24 | convolution fusion | flops 128768000 | bytes 4059217 | tf_op jit(solution)/shard_map/transpose(jvp(jhp,jn->hpn))/dot_general | solution.py:188
  112.9 1.8 %fusion.15 = f32[128,128]{1,0:T(8,128)S(1)} fusion(f32[128,128]{1,0:T(8,128)S(1)} %fusion.87, f32[128,20,64]{0,2,1:T(8,128)} %copy-done.1, f32[10,64,128]{2,1,0:T(8,128)S(1)} %get-tuple-element.48, f32[10,64,128]{2,1,0:T(8,128)S(1)} %copy-done.6, pred[]{:T(512)S(6)} %eq.31), kind=kOutput, calls=%fused_computation.14 | convolution fusion | flops 126337024 | bytes 1441793 | tf_op jit(solution)/shard_map/transpose(jvp(jhp,jn->hpn))/dot_general | solution.py:188
  116.0 1.6 %collective-permute-start.13 = (f32[128,128]{1,0:T(8,128)S(1)}, f32[128,128]{1,0:T(8,128)S(1)}, u32[]{:S(2)}, u32[]{:S(2)}) collective-permute-start(f32[128,128]{1,0:T(8,128)S(1)} %add.162), channel_id=1, source_target_pairs={{0,2},{1,3},{2,0},{3,1},{4,6},{5,7},{6,4},{7,5},{8,10},{9,11},{10,... | collective-permute-start | bytes 196616 | tf_op jit(solution)/shard_map/ppermute | solution.py:96
  118.4 1.1 copy.28
  119.5 0.9 collective-permute-done.13
  (96 shorter events, 16.7 us)
Async XLA Ops:
  0.6 27.5 %copy-start = (f32[128,128]{1,0:T(8,128)S(1)}, f32[128,128]{1,0:T(8,128)}, u32[]{:S(2)}) copy-start(f32[128,128]{1,0:T(8,128)} %param.12) | copy-start | bytes 196612
  1.8 1.4 %copy-start.12 = (f32[20,128]{1,0:T(8,128)S(1)}, f32[20,128]{1,0:T(8,128)}, u32[]{:S(2)}) copy-start(f32[20,128]{1,0:T(8,128)} %param.13) | copy-start | bytes 30724
  3.2 0.8 copy-start.4
  4.0 12.3 %copy-start.1 = (f32[128,20,64]{0,2,1:T(8,128)}, f32[128,20,64]{0,2,1:T(8,128)S(1)}, u32[]{:S(2)}) copy-start(f32[128,20,64]{0,2,1:T(8,128)S(1)} %multiply_multiply_fusion) | copy-start | bytes 1966084
  4.5 11.6 %collective-permute-start = (f32[10,65,128]{2,1,0:T(8,128)S(1)}, f32[10,65,128]{2,1,0:T(8,128)S(1)}, u32[]{:S(2)}, u32[]{:S(2)}) collective-permute-start(f32[10,65,128]{2,1,0:T(8,128)S(1)} %pad_maximum_fusion), channel_id=1, source_target_pairs={{0,4},{4,0},{8,12},{12,8},{16,20},{20,16},{24,28},{28,24},{1,5},{5... | collective-permute-start | bytes 998408 | tf_op jit(solution)/shard_map/ppermute | solution.py:42
  16.6 9.8 %collective-permute-start.1 = (f32[10,64,128]{2,1,0:T(8,128)S(1)}, f32[10,64,128]{2,1,0:T(8,128)S(1)}, u32[]{:S(2)}, u32[]{:S(2)}) collective-permute-start(f32[10,64,128]{2,1,0:T(8,128)S(1)} %get-tuple-element.37), channel_id=1, source_target_pairs={{0,8},{4,12},{1,9},{5,13},{2,10},{6,14},{3,11},{7,15}} | collective-permute-start | bytes 983048 | tf_op jit(solution)/shard_map/ppermute | solution.py:64
  26.6 0.7 collective-permute-start.2
  27.4 0.9 collective-permute-start.3
  28.3 1.7 %copy-start.15 = (f32[20]{0:T(128)S(1)}, f32[20]{0:T(128)}, u32[]{:S(2)}) copy-start(f32[20]{0:T(128)} %param.15) | copy-start | bytes 244
  28.5 7.7 %collective-permute-start.4 = (f32[10,64,128]{2,1,0:T(8,128)S(1)}, f32[10,64,128]{2,1,0:T(8,128)S(1)}, u32[]{:S(2)}, u32[]{:S(2)}) collective-permute-start(f32[10,64,128]{2,1,0:T(8,128)S(1)} %get-tuple-element.49), channel_id=1, source_target_pairs={{0,4},{4,0},{8,12},{12,8},{16,20},{20,16},{24,28},{28,24},{1,5},{5... | collective-permute-start | bytes 983048 | tf_op jit(solution)/shard_map/ppermute | solution.py:84
  36.2 0.7 copy-start.7
  36.9 1.1 copy-start.13
  38.0 6.8 %copy-start.2 = (f32[128,1280]{1,0:T(8,128)S(1)}, f32[128,1280]{1,0:T(8,128)}, u32[]{:S(2)}) copy-start(f32[128,1280]{1,0:T(8,128)} %param.10) | copy-start | bytes 1966084
  38.0 6.8 %copy-start.3 = (f32[128,1280]{1,0:T(8,128)S(1)}, f32[128,1280]{1,0:T(8,128)}, u32[]{:S(2)}) copy-start(f32[128,1280]{1,0:T(8,128)} %param.17) | copy-start | bytes 1966084
  40.0 1.2 collective-permute-start.5
  41.2 3.6 %collective-permute-start.6 = (f32[2,128]{1,0:T(2,128)S(1)}, f32[2,128]{1,0:T(2,128)S(1)}, u32[]{:S(2)}, u32[]{:S(2)}) collective-permute-start(f32[2,128]{1,0:T(2,128)S(1)} %fusion.81), channel_id=1, source_target_pairs={{0,2},{1,3},{2,0},{3,1},{4,6},{5,7},{6,4},{7,5},{8,10},{9,11},{10,... | collective-permute-start | bytes 3080 | tf_op jit(solution)/shard_map/ppermute | solution.py:96
  47.6 9.8 %collective-permute-start.7 = (f32[10,65,128]{2,1,0:T(8,128)}, f32[10,65,128]{2,1,0:T(8,128)}, u32[]{:S(2)}, u32[]{:S(2)}) collective-permute-start(f32[10,65,128]{2,1,0:T(8,128)} %pad_maximum_fusion.1), channel_id=1, source_target_pairs={{28,24},{24,28},{20,16},{16,20},{12,8},{8,12},{4,0},{0,4},{29,25},... | collective-permute-start | bytes 998408 | tf_op jit(solution)/shard_map/ppermute | solution.py:42
  61.0 1.4 %collective-permute-start.8 = (f32[10,64,128]{2,1,0:T(8,128)}, f32[10,64,128]{2,1,0:T(8,128)}, u32[]{:S(2)}, u32[]{:S(2)}) collective-permute-start(f32[10,64,128]{2,1,0:T(8,128)} %get-tuple-element.28), channel_id=1, source_target_pairs={{28,20},{24,16},{29,21},{25,17},{30,22},{26,18},{31,23},{27,19}} | collective-permute-start | bytes 983048 | tf_op jit(solution)/shard_map/ppermute | solution.py:64
  62.5 2.8 %collective-permute-start.9 = (f32[10,64,128]{2,1,0:T(8,128)S(1)}, f32[10,64,128]{2,1,0:T(8,128)S(1)}, u32[]{:S(2)}, u32[]{:S(2)}) collective-permute-start(f32[10,64,128]{2,1,0:T(8,128)S(1)} %multiply_add_fusion.2), channel_id=1, source_target_pairs={{20,12},{16,8},{21,13},{17,9},{22,14},{18,10},{23,15},{19,11}} | collective-permute-start | bytes 983048 | tf_op jit(solution)/shard_map/ppermute | solution.py:64
  65.3 1.6 %copy-start.8 = (f32[10,64,128]{2,1,0:T(8,128)S(1)}, f32[10,64,128]{2,1,0:T(8,128)}, u32[]{:S(2)}) copy-start(f32[10,64,128]{2,1,0:T(8,128)} %copy-done.7) | copy-start | bytes 983044
  65.5 35.0 %collective-permute-start.10 = (f32[10,64,128]{2,1,0:T(8,128)S(1)}, f32[10,64,128]{2,1,0:T(8,128)S(1)}, u32[]{:S(2)}, u32[]{:S(2)}) collective-permute-start(f32[10,64,128]{2,1,0:T(8,128)S(1)} %get-tuple-element.26), channel_id=1, source_target_pairs={{12,4},{8,0},{13,5},{9,1},{14,6},{10,2},{15,7},{11,3}} | collective-permute-start | bytes 983048 | tf_op jit(solution)/shard_map/ppermute | solution.py:61
  67.7 32.8 %copy-start.9 = (f32[10,64,128]{2,1,0:T(8,128)S(1)}, f32[10,64,128]{2,1,0:T(8,128)}, u32[]{:S(2)}) copy-start(f32[10,64,128]{2,1,0:T(8,128)} %get-tuple-element.58) | copy-start | bytes 983044
  67.7 32.8 %copy-start.14 = (f32[10]{0:T(128)S(1)}, f32[10]{0:T(128)}, u32[]{:S(2)}) copy-start(f32[10]{0:T(128)} %get-tuple-element.33) | copy-start | bytes 124
  67.7 35.7 %collective-permute-start.14 = (f32[128,128]{1,0:T(8,128)S(1)}, f32[128,128]{1,0:T(8,128)S(1)}, u32[]{:S(2)}, u32[]{:S(2)}) collective-permute-start(f32[128,128]{1,0:T(8,128)S(1)} %fusion.16), channel_id=1, source_target_pairs={{0,1},{1,0},{2,3},{3,2},{4,5},{5,4},{6,7},{7,6},{8,9},{9,8},{10,11... | collective-permute-start | bytes 196616 | tf_op jit(solution)/shard_map/ppermute | solution.py:96
  101.6 7.1 %collective-permute-start.11 = (f32[10,64,128]{2,1,0:T(8,128)S(1)}, f32[10,64,128]{2,1,0:T(8,128)S(1)}, u32[]{:S(2)}, u32[]{:S(2)}) collective-permute-start(f32[10,64,128]{2,1,0:T(8,128)S(1)} %get-tuple-element.47), channel_id=1, source_target_pairs={{28,24},{24,28},{20,16},{16,20},{12,8},{8,12},{4,0},{0,4},{29,25},... | collective-permute-start | bytes 983048 | tf_op jit(solution)/shard_map/ppermute | solution.py:84
  103.4 4.3 %collective-permute-start.15 = (f32[128,128]{1,0:T(8,128)S(1)}, f32[128,128]{1,0:T(8,128)S(1)}, u32[]{:S(2)}, u32[]{:S(2)}) collective-permute-start(f32[128,128]{1,0:T(8,128)S(1)} %add.165), channel_id=1, source_target_pairs={{0,2},{1,3},{2,0},{3,1},{4,6},{5,7},{6,4},{7,5},{8,10},{9,11},{10,... | collective-permute-start | bytes 196616 | tf_op jit(solution)/shard_map/ppermute | solution.py:96
  108.8 1.5 %copy-start.16 = (f32[20]{0:T(128)S(1)}, f32[20]{0:T(128)}, u32[]{:S(2)}) copy-start(f32[20]{0:T(128)} %param.15) | copy-start | bytes 244
  110.3 2.6 %copy-start.6 = (f32[10,64,128]{2,1,0:T(8,128)S(1)}, f32[10,64,128]{2,1,0:T(8,128)}, u32[]{:S(2)}) copy-start(f32[10,64,128]{2,1,0:T(8,128)} %copy-done.5) | copy-start | bytes 983044
  112.8 1.9 %copy-start.10 = (f32[20,128]{1,0:T(8,128)S(1)}, f32[20,128]{1,0:T(8,128)}, u32[]{:S(2)}) copy-start(f32[20,128]{1,0:T(8,128)} %fusion.53) | copy-start | bytes 30724
  112.9 4.7 %copy-start.11 = (f32[20,1]{1,0:T(8,128)S(1)}, f32[20,1]{1,0:T(8,128)}, u32[]{:S(2)}) copy-start(f32[20,1]{1,0:T(8,128)} %exponential_multiply_fusion) | copy-start | bytes 244
  114.7 1.3 %collective-permute-start.12 = (f32[128,128]{1,0:T(8,128)S(1)}, f32[128,128]{1,0:T(8,128)S(1)}, u32[]{:S(2)}, u32[]{:S(2)}) collective-permute-start(f32[128,128]{1,0:T(8,128)S(1)} %fusion.15), channel_id=1, source_target_pairs={{0,1},{1,0},{2,3},{3,2},{4,5},{5,4},{6,7},{7,6},{8,9},{9,8},{10,11... | collective-permute-start | bytes 196616 | tf_op jit(solution)/shard_map/ppermute | solution.py:96
  116.0 4.3 %collective-permute-start.13 = (f32[128,128]{1,0:T(8,128)S(1)}, f32[128,128]{1,0:T(8,128)S(1)}, u32[]{:S(2)}, u32[]{:S(2)}) collective-permute-start(f32[128,128]{1,0:T(8,128)S(1)} %add.162), channel_id=1, source_target_pairs={{0,2},{1,3},{2,0},{3,1},{4,6},{5,7},{6,4},{7,5},{8,10},{9,11},{10,... | collective-permute-start | bytes 196616 | tf_op jit(solution)/shard_map/ppermute | solution.py:96
  (1 other events, 0.7 us)

commit v16 on v14

--- a/solution.py
+++ b/solution.py
@@ -259,15 +259,22 @@
         gf_w, gs_w, gd_w, gw_w, gr_w = pull_w(grad_mixed)
         gd_c, gr_c = pull_c(grad_mixed)
         grad_read = butterfly_psum(gr_w + gr_c, "head")
+        gw_e = jnp.dot(
+            weighted_in.reshape(length, -1),
+            state_grad.reshape(-1, state_grad.shape[2]),
+            precision=highest,
+        )
+        write_part = gw_w + gw_e
+        grad_write = butterfly_psum(write_part, "head")
+        state_grad, write_part = lax.optimization_barrier((state_grad, write_part))
         _, pull_e = jax.vjp(
-            lambda f, s, d, w: end_part(f, s, d, w, state_in),
-            features, step_sizes, log_decay, write_keys,
-        )
-        gf_e, gs_e, gd_e, gw_e = pull_e(state_grad)
+            lambda f, s, d: end_part(f, s, d, write_keys, state_in),
+            features, step_sizes, log_decay,
+        )
+        gf_e, gs_e, gd_e = pull_e(state_grad)
         grad_features = gf_w + gf_e
         grad_steps = gs_w + gs_e
         grad_decay = gd_w + gd_c + gd_e
-        grad_write = butterfly_psum(gw_w + gw_e, "head")
     else:
         grad_features, grad_steps, grad_decay, grad_write, grad_read = pullback(
             (state_grad, grad_mixed)

time: 116 us -> 116 us (level)
    dot_general x2 -> x1, matrix products: 3.33 us -> 2.39 us  [state_update(): return jnp.einsum('jhp,jn->hpn', weighted_in, writes, precision=highest)]
    unnamed x46 -> x28, local copies, waits for them, and re-layouts: 3.27 us -> 2.76 us
  transfers between devices with their start and end apart: 18 -> 18, of which waited for: 12 -> 11; matrix products, arithmetic and copies ran while one was open for 11% -> 14% of each run, Pallas kernels for 0% -> 0%
where the time goes in v16:
time: 116 us; the launch traced here: 115 us
  waiting for transfers between devices  62 us (53%)
  starting transfers between devices  23.2 us (20%)
  matrix products  14.7 us (13%)
  other arithmetic  9.21 us (8%)
  local copies, waits for them, and re-layouts  4.81 us (4%)
    ppermute x2, waiting for transfers between devices, pair_scan(): s_in = lax.ppermute(out[1], axis, pairs)  29.6 us
    ppermute x4, waiting for transfers between devices, pair_scan(): a_rcv, s_rcv = lax.ppermute((a_snd, s_snd), axis, swap)  16.6 us
    ppermute x6, waiting for transfers between devices, butterfly_psum(): got = lax.ppermute(parts, axis, [(i, i ^ k) for i in range(count)])  6.84 us
    ppermute x4, starting transfers between devices, pair_scan(): a_in, s_in = lax.ppermute(out, axis, pairs)  6.49 us
    ppermute x4, starting transfers between devices, pair_scan(): a_rcv, s_rcv = lax.ppermute((a_snd, s_snd), axis, swap)  6.34 us
    dot_general x3, matrix products, within_part(): within = jnp.einsum('hij,jhp->ihp', masked, scaled, precision=highest)  6.02 us
    ppermute x6, starting transfers between devices, butterfly_psum(): got = lax.ppermute(parts, axis, [(i, i ^ k) for i in range(count)])  4.95 us
    ppermute x4, waiting for transfers between devices, pair_scan(): a_in, s_in = lax.ppermute(out, axis, pairs)  4.83 us
  transfers between devices with their start and end apart: 18, of which 11 were waited for; matrix products, arithmetic and copies ran while one was open for 14% of the time, Pallas kernels for 0%

profile of v16, /device:TPU:0, one launch (start us, length us, event | category | flops | bytes accessed | tf_op | source)
XLA Modules:
  0.0 115.0 jit_solution(3535442043793028561)
XLA Ops:
  1.8 1.3 %copy.22 = f32[128,1280]{0,1:T(8,128)S(1)} copy(f32[128,1280]{1,0:T(8,128)} %param.9) | data formatting | bytes 1310720 | tf_op args[0]
  3.7 3.0 %collective-permute-start.1 = (f32[10,64,128]{2,1,0:T(8,128)S(1)}, f32[10,64,128]{2,1,0:T(8,128)S(1)}, u32[]{:S(2)}, u32[]{:S(2)}) collective-permute-start(f32[10,64,128]{2,1,0:T(8,128)S(1)} %constant_dynamic-slice_fusion.1), channel_id=1, source_target_pairs={{0,4},{4,0},{8,12},{12,8},{16,20},{20,16},{24,28},{28,24},{1,5},{5... | collective-permute-start | bytes 983048 | tf_op jit(solution)/shard_map/ppermute | solution.py:42
  6.8 7.6 %collective-permute-done.8 = f32[10]{0:T(128)S(1)} collective-permute-done((f32[10]{0:T(128)S(1)}, f32[10]{0:T(128)S(1)}, u32[]{:S(2)}, u32[]{:S(2)}) %collective-permute-start.8) | collective-permute-done | bytes 72 | tf_op jit(solution)/shard_map/ppermute | solution.py:42
  14.5 1.7 %collective-permute-start = (f32[10]{0:T(128)S(1)}, f32[10]{0:T(128)S(1)}, u32[]{:S(2)}, u32[]{:S(2)}) collective-permute-start(f32[10]{0:T(128)S(1)} %get-tuple-element.55), channel_id=1, source_target_pairs={{0,4},{4,0},{8,12},{12,8},{16,20},{20,16},{24,28},{28,24},{1,5},{5... | collective-permute-start | bytes 128 | tf_op jit(solution)/shard_map/ppermute | solution.py:42
  16.3 1.8 %collective-permute-done = f32[10]{0:T(128)S(1)} collective-permute-done((f32[10]{0:T(128)S(1)}, f32[10]{0:T(128)S(1)}, u32[]{:S(2)}, u32[]{:S(2)}) %collective-permute-start) | collective-permute-done | bytes 72 | tf_op jit(solution)/shard_map/ppermute | solution.py:42
  18.3 3.7 %collective-permute-start.2 = (f32[10,64,128]{2,1,0:T(8,128)S(1)}, f32[10,64,128]{2,1,0:T(8,128)S(1)}, u32[]{:S(2)}, u32[]{:S(2)}) collective-permute-start(f32[10,64,128]{2,1,0:T(8,128)S(1)} %get-tuple-element.39), channel_id=1, source_target_pairs={{0,8},{4,12},{1,9},{5,13},{2,10},{6,14},{3,11},{7,15}} | collective-permute-start | bytes 983048 | tf_op jit(solution)/shard_map/ppermute | solution.py:62
  22.1 4.8 %collective-permute-done.2 = f32[10,64,128]{2,1,0:T(8,128)S(1)} collective-permute-done((f32[10,64,128]{2,1,0:T(8,128)S(1)}, f32[10,64,128]{2,1,0:T(8,128)S(1)}, u32[]{:S(2)}, u32[]{:S(2)}) %collective-permute-start.2) | collective-permute-done | bytes 327712 | tf_op jit(solution)/shard_map/ppermute | solution.py:62
  28.9 1.6 %collective-permute-start.5 = (f32[10,64,128]{2,1,0:T(8,128)S(1)}, f32[10,64,128]{2,1,0:T(8,128)S(1)}, u32[]{:S(2)}, u32[]{:S(2)}) collective-permute-start(f32[10,64,128]{2,1,0:T(8,128)S(1)} %get-tuple-element.51), channel_id=1, source_target_pairs={{0,4},{4,0},{8,12},{12,8},{16,20},{20,16},{24,28},{28,24},{1,5},{5... | collective-permute-start | bytes 983048 | tf_op jit(solution)/shard_map/ppermute | solution.py:82
  30.5 1.5 %fusion.9 = f32[128,20,64]{0,2,1:T(8,128)S(1)} fusion(f32[128,20,64]{0,2,1:T(8,128)S(1)} %bitcast.86, f32[128,128]{1,0:T(8,128)S(1)} %fusion.83, f32[20,128]{1,0:T(8,128)S(1)} %bitcast.99, pred[128,128]{1,0:T(8,128)(4,1)S(1)} %iota_compare_fusion.6, f32[128,20]{0,1:T(8,128)S(1)} %bitcast.104, f32[20]{0:T(128)S(1)} %copy-done.12), kind=kOutput, calls=%fused_computation.10 | convolution fusion | flops 127631360 | bytes 1413200 | tf_op jit(solution)/shard_map/jvp(hij,jhp->ihp)/dot_general | solution.py:167
  32.2 3.8 %collective-permute-done.5 = f32[10,64,128]{2,1,0:T(8,128)S(1)} collective-permute-done((f32[10,64,128]{2,1,0:T(8,128)S(1)}, f32[10,64,128]{2,1,0:T(8,128)S(1)}, u32[]{:S(2)}, u32[]{:S(2)}) %collective-permute-start.5) | collective-permute-done | bytes 327712 | tf_op jit(solution)/shard_map/ppermute | solution.py:82
  36.8 1.1 copy.24
  37.8 1.9 %multiply_reduce_fusion.7 = (f32[128]{0:T(128)S(1)}, f32[128]{0:T(128)S(1)}, f32[128,1280]{1,0:T(8,128)S(1)}) fusion(f32[128,1280]{1,0:T(8,128)} %param.10, f32[128,1280]{1,0:T(8,128)} %param.17, f32[1280]{0:T(1024)S(1)} %copy-done.11, f32[128,1280]{1,0:T(8,128)S(1)} %copy.23, f32[128,1280]{1,0:T(8,128)} %copy.24), kind=kLoop, calls=%fused_computation.32 | loop fusion | flops 1801984 | bytes 3282944 | tf_op jit(solution)/shard_map/reduce_sum | solution.py:244
  39.9 1.1 collective-permute-done.6
  41.0 1.6 %collective-permute-start.7 = (f32[2,128]{1,0:T(2,128)S(1)}, f32[2,128]{1,0:T(2,128)S(1)}, u32[]{:S(2)}, u32[]{:S(2)}) collective-permute-start(f32[2,128]{1,0:T(2,128)S(1)} %fusion.79), channel_id=1, source_target_pairs={{0,2},{1,3},{2,0},{3,1},{4,6},{5,7},{6,4},{7,5},{8,10},{9,11},{10,... | collective-permute-start | bytes 3080 | tf_op jit(solution)/shard_map/ppermute | solution.py:94
  42.6 2.0 %collective-permute-done.7 = f32[2,128]{1,0:T(2,128)S(1)} collective-permute-done((f32[2,128]{1,0:T(2,128)S(1)}, f32[2,128]{1,0:T(2,128)S(1)}, u32[]{:S(2)}, u32[]{:S(2)}) %collective-permute-start.7) | collective-permute-done | bytes 1056 | tf_op jit(solution)/shard_map/ppermute | solution.py:94
  44.7 1.3 %add_multiply_fusion = (f32[128,1280]{1,0:T(8,128)}, f32[128,1280]{1,0:T(8,128)S(1)}) fusion(f32[128,1280]{1,0:T(8,128)S(1)} %copy-done.1, f32[128,1280]{1,0:T(8,128)S(1)} %get-tuple-element.36, f32[128]{0:T(128)S(1)} %fusion.70, f32[128,1280]{1,0:T(8,128)S(1)} %copy-done.2, f32[128]{0:T(128)S(1)} %rsqrt_bitcast_fusion, f32[1280]{0:T(1024)S(1)} %copy-done.11), kind=kLoop, calls=%fused_computation.28 | loop fusion | flops 2621440 | bytes 3282944 | tf_op jit(solution)/shard_map/mul | solution.py:253
  46.7 1.6 %collective-permute-start.9 = (f32[10,64,128]{2,1,0:T(8,128)S(1)}, f32[10,64,128]{2,1,0:T(8,128)S(1)}, u32[]{:S(2)}, u32[]{:S(2)}) collective-permute-start(f32[10,64,128]{2,1,0:T(8,128)S(1)} %constant_dynamic-slice_fusion), channel_id=1, source_target_pairs={{28,24},{24,28},{20,16},{16,20},{12,8},{8,12},{4,0},{0,4},{29,25},... | collective-permute-start | bytes 983048 | tf_op jit(solution)/shard_map/ppermute | solution.py:42
  48.2 7.1 %collective-permute-done.9 = f32[10,64,128]{2,1,0:T(8,128)S(1)} collective-permute-done((f32[10,64,128]{2,1,0:T(8,128)S(1)}, f32[10,64,128]{2,1,0:T(8,128)S(1)}, u32[]{:S(2)}, u32[]{:S(2)}) %collective-permute-start.9) | collective-permute-done | bytes 327712 | tf_op jit(solution)/shard_map/ppermute | solution.py:42
  56.2 1.4 %collective-permute-start.10 = (f32[10,64,128]{2,1,0:T(8,128)}, f32[10,64,128]{2,1,0:T(8,128)}, u32[]{:S(2)}, u32[]{:S(2)}) collective-permute-start(f32[10,64,128]{2,1,0:T(8,128)} %get-tuple-element.30), channel_id=1, source_target_pairs={{28,20},{24,16},{29,21},{25,17},{30,22},{26,18},{31,23},{27,19}} | collective-permute-start | bytes 983048 | tf_op jit(solution)/shard_map/ppermute | solution.py:62
  58.4 2.8 %fusion.19 = (f32[20,128]{1,0:T(8,128)S(1)}, f32[20,128]{1,0:T(8,128)S(1)}, f32[128,128]{1,0:T(8,128)S(1)}) fusion(f32[128,128]{1,0:T(8,128)} %copy-done.9, f32[20,128]{1,0:T(8,128)S(1)} %bitcast.100, pred[128,128]{1,0:T(8,128)(4,1)S(1)} %iota_compare_fusion.6, f32[20,64,128]{2,1,0:T(8,128)S(1)} %bitcast.91, f32[128,20,64]{0,2,1:T(8,128)S(1)} %bitcast.87, ...), kind=kOutput, calls=%fused_computation.20 | convolution fusion | flops 129575936 | bytes 1499136 | tf_op jit(solution)/shard_map/transpose(jvp(hij,jhp->ihp))/dot_general | solution.py:167
  61.5 1.6 %collective-permute-start.12 = (f32[10,64,128]{2,1,0:T(8,128)S(1)}, f32[10,64,128]{2,1,0:T(8,128)S(1)}, u32[]{:S(2)}, u32[]{:S(2)}) collective-permute-start(f32[10,64,128]{2,1,0:T(8,128)S(1)} %get-tuple-element.28), channel_id=1, source_target_pairs={{12,4},{8,0},{13,5},{9,1},{14,6},{10,2},{15,7},{11,3}} | collective-permute-start | bytes 983048 | tf_op jit(solution)/shard_map/ppermute | solution.py:59
  63.9 1.8 %fusion.12 = f32[128,20,64]{0,2,1:T(8,128)} fusion(f32[20,64,128]{2,1,0:T(8,128)S(1)} %bitcast.93, f32[128,128]{1,0:T(8,128)S(1)} %copy-done.10, f32[20,128]{1,0:T(8,128)S(1)} %bitcast.101, pred[128,128]{1,0:T(8,128)(4,1)S(1)} %iota_compare_fusion.6), kind=kOutput, calls=%fused_computation.11 | convolution fusion | flops 127139840 | bytes 1402880 | tf_op jit(solution)/shard_map/transpose(jvp(hij,jhp->ihp))/dot_general | solution.py:167
  65.7 29.6 %collective-permute-done.12 = f32[10,64,128]{2,1,0:T(8,128)S(1)} collective-permute-done((f32[10,64,128]{2,1,0:T(8,128)S(1)}, f32[10,64,128]{2,1,0:T(8,128)S(1)}, u32[]{:S(2)}, u32[]{:S(2)}) %collective-permute-start.12) | collective-permute-done | bytes 327712 | tf_op jit(solution)/shard_map/ppermute | solution.py:59
  95.4 1.6 %collective-permute-start.13 = (f32[10,64,128]{2,1,0:T(8,128)S(1)}, f32[10,64,128]{2,1,0:T(8,128)S(1)}, u32[]{:S(2)}, u32[]{:S(2)}) collective-permute-start(f32[10,64,128]{2,1,0:T(8,128)S(1)} %get-tuple-element.49), channel_id=1, source_target_pairs={{28,24},{24,28},{20,16},{16,20},{12,8},{8,12},{4,0},{0,4},{29,25},... | collective-permute-start | bytes 983048 | tf_op jit(solution)/shard_map/ppermute | solution.py:82
  97.3 1.6 %collective-permute-start.17 = (f32[128,128]{1,0:T(8,128)S(1)}, f32[128,128]{1,0:T(8,128)S(1)}, u32[]{:S(2)}, u32[]{:S(2)}) collective-permute-start(f32[128,128]{1,0:T(8,128)S(1)} %add.165), channel_id=1, source_target_pairs={{0,2},{1,3},{2,0},{3,1},{4,6},{5,7},{6,4},{7,5},{8,10},{9,11},{10,... | collective-permute-start | bytes 196616 | tf_op jit(solution)/shard_map/ppermute | solution.py:94
  99.0 2.6 %collective-permute-done.17 = f32[128,128]{1,0:T(8,128)S(1)} collective-permute-done((f32[128,128]{1,0:T(8,128)S(1)}, f32[128,128]{1,0:T(8,128)S(1)}, u32[]{:S(2)}, u32[]{:S(2)}) %collective-permute-start.17) | collective-permute-done | bytes 65568 | tf_op jit(solution)/shard_map/ppermute | solution.py:94
  103.8 2.4 %multiply_reduce_fusion.2 = (f32[128,20]{0,1:T(8,128)S(1)}, f32[128,20]{0,1:T(8,128)}, f32[128,20]{0,1:T(8,128)}, f32[128,20,64]{0,2,1:T(8,128)S(1)}, f32[128,20]{0,1:T(8,128)}) fusion(f32[128,20,64]{0,2,1:T(8,128)S(1)} %bitcast.89, f32[128,20]{0,1:T(8,128)S(1)} %bitcast.107, f32[128,20]{0,1:T(8,128)S(1)} %get-tuple-element.54, f32[128,20,64]{0,2,1:T(8,128)} %fusion.12, ...), kind=kOutput, calls=%fused_computation.24 | convolution fusion | flops 128276480 | bytes 4059216 | tf_op jit(solution)/shard_map/transpose(jvp(jhp,jn->hpn))/dot_general | solution.py:186
  106.7 0.9 convolution_add_fusion.1
  107.6 1.4 %add_bitcast_fusion = f32[20,128]{1,0:T(8,128)} fusion(f32[128,20]{0,1:T(8,128)} %get-tuple-element.27, f32[128,20]{0,1:T(8,128)} %get-tuple-element.24), kind=kLoop, calls=%fused_computation.102 | loop fusion | flops 2560 | bytes 30720 | tf_op jit(solution)/shard_map/add | solution.py:276
  109.8 1.6 %collective-permute-start.15 = (f32[128,128]{1,0:T(8,128)S(1)}, f32[128,128]{1,0:T(8,128)S(1)}, u32[]{:S(2)}, u32[]{:S(2)}) collective-permute-start(f32[128,128]{1,0:T(8,128)S(1)} %add.162), channel_id=1, source_target_pairs={{0,2},{1,3},{2,0},{3,1},{4,6},{5,7},{6,4},{7,5},{8,10},{9,11},{10,... | collective-permute-start | bytes 196616 | tf_op jit(solution)/shard_map/ppermute | solution.py:94
  112.3 1.1 copy.28
  113.3 1.1 collective-permute-done.15
  (87 shorter events, 14.0 us)
Async XLA Ops:
  0.6 27.8 %copy-start = (f32[128,128]{1,0:T(8,128)S(1)}, f32[128,128]{1,0:T(8,128)}, u32[]{:S(2)}) copy-start(f32[128,128]{1,0:T(8,128)} %param.12) | copy-start | bytes 196612
  1.8 1.4 %copy-start.7 = (f32[128,128]{1,0:T(8,128)S(1)}, f32[128,128]{1,0:T(8,128)}, u32[]{:S(2)}) copy-start(f32[128,128]{1,0:T(8,128)} %param.11) | copy-start | bytes 196612
  1.8 1.4 %copy-start.8 = (f32[20,128]{1,0:T(8,128)S(1)}, f32[20,128]{1,0:T(8,128)}, u32[]{:S(2)}) copy-start(f32[20,128]{1,0:T(8,128)} %param.13) | copy-start | bytes 30724
  3.7 14.5 %collective-permute-start.1 = (f32[10,64,128]{2,1,0:T(8,128)S(1)}, f32[10,64,128]{2,1,0:T(8,128)S(1)}, u32[]{:S(2)}, u32[]{:S(2)}) collective-permute-start(f32[10,64,128]{2,1,0:T(8,128)S(1)} %constant_dynamic-slice_fusion.1), channel_id=1, source_target_pairs={{0,4},{4,0},{8,12},{12,8},{16,20},{20,16},{24,28},{28,24},{1,5},{5... | collective-permute-start | bytes 983048 | tf_op jit(solution)/shard_map/ppermute | solution.py:42
  6.8 7.7 %collective-permute-start.8 = (f32[10]{0:T(128)S(1)}, f32[10]{0:T(128)S(1)}, u32[]{:S(2)}, u32[]{:S(2)}) collective-permute-start(f32[10]{0:T(128)S(1)} %dynamic_slice.29), channel_id=1, source_target_pairs={{28,24},{24,28},{20,16},{16,20},{12,8},{8,12},{4,0},{0,4},{29,25},... | collective-permute-start | bytes 128 | tf_op jit(solution)/shard_map/ppermute | solution.py:42
  14.5 3.5 %collective-permute-start = (f32[10]{0:T(128)S(1)}, f32[10]{0:T(128)S(1)}, u32[]{:S(2)}, u32[]{:S(2)}) collective-permute-start(f32[10]{0:T(128)S(1)} %get-tuple-element.55), channel_id=1, source_target_pairs={{0,4},{4,0},{8,12},{12,8},{16,20},{20,16},{24,28},{28,24},{1,5},{5... | collective-permute-start | bytes 128 | tf_op jit(solution)/shard_map/ppermute | solution.py:42
  18.3 8.6 %collective-permute-start.2 = (f32[10,64,128]{2,1,0:T(8,128)S(1)}, f32[10,64,128]{2,1,0:T(8,128)S(1)}, u32[]{:S(2)}, u32[]{:S(2)}) collective-permute-start(f32[10,64,128]{2,1,0:T(8,128)S(1)} %get-tuple-element.39), channel_id=1, source_target_pairs={{0,8},{4,12},{1,9},{5,13},{2,10},{6,14},{3,11},{7,15}} | collective-permute-start | bytes 983048 | tf_op jit(solution)/shard_map/ppermute | solution.py:62
  27.0 0.7 collective-permute-start.3
  27.8 0.9 collective-permute-start.4
  28.7 1.8 %copy-start.9 = (f32[128,128]{1,0:T(8,128)}, f32[128,128]{1,0:T(8,128)S(1)}, u32[]{:S(2)}) copy-start(f32[128,128]{1,0:T(8,128)S(1)} %fusion.83) | copy-start | bytes 196612
  28.7 1.8 %copy-start.12 = (f32[20]{0:T(128)S(1)}, f32[20]{0:T(128)}, u32[]{:S(2)}) copy-start(f32[20]{0:T(128)} %param.15) | copy-start | bytes 244
  28.9 7.1 %collective-permute-start.5 = (f32[10,64,128]{2,1,0:T(8,128)S(1)}, f32[10,64,128]{2,1,0:T(8,128)S(1)}, u32[]{:S(2)}, u32[]{:S(2)}) collective-permute-start(f32[10,64,128]{2,1,0:T(8,128)S(1)} %get-tuple-element.51), channel_id=1, source_target_pairs={{0,4},{4,0},{8,12},{12,8},{16,20},{20,16},{24,28},{28,24},{1,5},{5... | collective-permute-start | bytes 983048 | tf_op jit(solution)/shard_map/ppermute | solution.py:82
  36.0 0.7 copy-start.5
  36.8 1.1 copy-start.11
  37.8 6.8 %copy-start.1 = (f32[128,1280]{1,0:T(8,128)S(1)}, f32[128,1280]{1,0:T(8,128)}, u32[]{:S(2)}) copy-start(f32[128,1280]{1,0:T(8,128)} %param.10) | copy-start | bytes 1966084
  37.8 6.8 %copy-start.2 = (f32[128,1280]{1,0:T(8,128)S(1)}, f32[128,1280]{1,0:T(8,128)}, u32[]{:S(2)}) copy-start(f32[128,1280]{1,0:T(8,128)} %param.17) | copy-start | bytes 1966084
  39.8 1.2 %collective-permute-start.6 = (f32[2,128]{1,0:T(2,128)S(1)}, f32[2,128]{1,0:T(2,128)S(1)}, u32[]{:S(2)}, u32[]{:S(2)}) collective-permute-start(f32[2,128]{1,0:T(2,128)S(1)} %pad_maximum_fusion), channel_id=1, source_target_pairs={{0,1},{1,0},{2,3},{3,2},{4,5},{5,4},{6,7},{7,6},{8,9},{9,8},{10,11... | collective-permute-start | bytes 3080 | tf_op jit(solution)/shard_map/ppermute | solution.py:94
  41.0 3.6 %collective-permute-start.7 = (f32[2,128]{1,0:T(2,128)S(1)}, f32[2,128]{1,0:T(2,128)S(1)}, u32[]{:S(2)}, u32[]{:S(2)}) collective-permute-start(f32[2,128]{1,0:T(2,128)S(1)} %fusion.79), channel_id=1, source_target_pairs={{0,2},{1,3},{2,0},{3,1},{4,6},{5,7},{6,4},{7,5},{8,10},{9,11},{10,... | collective-permute-start | bytes 3080 | tf_op jit(solution)/shard_map/ppermute | solution.py:94
  46.7 8.7 %collective-permute-start.9 = (f32[10,64,128]{2,1,0:T(8,128)S(1)}, f32[10,64,128]{2,1,0:T(8,128)S(1)}, u32[]{:S(2)}, u32[]{:S(2)}) collective-permute-start(f32[10,64,128]{2,1,0:T(8,128)S(1)} %constant_dynamic-slice_fusion), channel_id=1, source_target_pairs={{28,24},{24,28},{20,16},{16,20},{12,8},{8,12},{4,0},{0,4},{29,25},... | collective-permute-start | bytes 983048 | tf_op jit(solution)/shard_map/ppermute | solution.py:42
  55.3 0.8 copy-start.3
  56.2 1.4 %collective-permute-start.10 = (f32[10,64,128]{2,1,0:T(8,128)}, f32[10,64,128]{2,1,0:T(8,128)}, u32[]{:S(2)}, u32[]{:S(2)}) collective-permute-start(f32[10,64,128]{2,1,0:T(8,128)} %get-tuple-element.30), channel_id=1, source_target_pairs={{28,20},{24,16},{29,21},{25,17},{30,22},{26,18},{31,23},{27,19}} | collective-permute-start | bytes 983048 | tf_op jit(solution)/shard_map/ppermute | solution.py:62
  57.7 3.7 %collective-permute-start.11 = (f32[10,64,128]{2,1,0:T(8,128)S(1)}, f32[10,64,128]{2,1,0:T(8,128)S(1)}, u32[]{:S(2)}, u32[]{:S(2)}) collective-permute-start(f32[10,64,128]{2,1,0:T(8,128)S(1)} %multiply_add_fusion.2), channel_id=1, source_target_pairs={{20,12},{16,8},{21,13},{17,9},{22,14},{18,10},{23,15},{19,11}} | collective-permute-start | bytes 983048 | tf_op jit(solution)/shard_map/ppermute | solution.py:62
  61.3 1.8 %copy-start.6 = (f32[10,64,128]{2,1,0:T(8,128)S(1)}, f32[10,64,128]{2,1,0:T(8,128)}, u32[]{:S(2)}) copy-start(f32[10,64,128]{2,1,0:T(8,128)} %copy-done.5) | copy-start | bytes 983044
  61.5 2.4 %copy-start.10 = (f32[128,128]{1,0:T(8,128)S(1)}, f32[128,128]{1,0:T(8,128)}, u32[]{:S(2)}) copy-start(f32[128,128]{1,0:T(8,128)} %copy-done.9) | copy-start | bytes 196612
  61.5 33.8 %collective-permute-start.12 = (f32[10,64,128]{2,1,0:T(8,128)S(1)}, f32[10,64,128]{2,1,0:T(8,128)S(1)}, u32[]{:S(2)}, u32[]{:S(2)}) collective-permute-start(f32[10,64,128]{2,1,0:T(8,128)S(1)} %get-tuple-element.28), channel_id=1, source_target_pairs={{12,4},{8,0},{13,5},{9,1},{14,6},{10,2},{15,7},{11,3}} | collective-permute-start | bytes 983048 | tf_op jit(solution)/shard_map/ppermute | solution.py:59
  63.8 31.5 %copy-start.4 = (f32[10,64,128]{2,1,0:T(8,128)S(1)}, f32[10,64,128]{2,1,0:T(8,128)}, u32[]{:S(2)}) copy-start(f32[10,64,128]{2,1,0:T(8,128)} %copy-done.3) | copy-start | bytes 983044
  63.8 33.5 %collective-permute-start.16 = (f32[128,128]{1,0:T(8,128)S(1)}, f32[128,128]{1,0:T(8,128)S(1)}, u32[]{:S(2)}, u32[]{:S(2)}) collective-permute-start(f32[128,128]{1,0:T(8,128)S(1)} %fusion.16), channel_id=1, source_target_pairs={{0,1},{1,0},{2,3},{3,2},{4,5},{5,4},{6,7},{7,6},{8,9},{9,8},{10,11... | collective-permute-start | bytes 196616 | tf_op jit(solution)/shard_map/ppermute | solution.py:94
  95.4 7.1 %collective-permute-start.13 = (f32[10,64,128]{2,1,0:T(8,128)S(1)}, f32[10,64,128]{2,1,0:T(8,128)S(1)}, u32[]{:S(2)}, u32[]{:S(2)}) collective-permute-start(f32[10,64,128]{2,1,0:T(8,128)S(1)} %get-tuple-element.49), channel_id=1, source_target_pairs={{28,24},{24,28},{20,16},{16,20},{12,8},{8,12},{4,0},{0,4},{29,25},... | collective-permute-start | bytes 983048 | tf_op jit(solution)/shard_map/ppermute | solution.py:82
  97.3 4.3 %collective-permute-start.17 = (f32[128,128]{1,0:T(8,128)S(1)}, f32[128,128]{1,0:T(8,128)S(1)}, u32[]{:S(2)}, u32[]{:S(2)}) collective-permute-start(f32[128,128]{1,0:T(8,128)S(1)} %add.165), channel_id=1, source_target_pairs={{0,2},{1,3},{2,0},{3,1},{4,6},{5,7},{6,4},{7,5},{8,10},{9,11},{10,... | collective-permute-start | bytes 196616 | tf_op jit(solution)/shard_map/ppermute | solution.py:94
  103.3 5.7 %collective-permute-start.14 = (f32[128,128]{1,0:T(8,128)S(1)}, f32[128,128]{1,0:T(8,128)}, u32[]{:S(2)}, u32[]{:S(2)}) collective-permute-start(f32[128,128]{1,0:T(8,128)S(1)} %fusion.15), channel_id=1, source_target_pairs={{0,1},{1,0},{2,3},{3,2},{4,5},{5,4},{6,7},{7,6},{8,9},{9,8},{10,11... | collective-permute-start | bytes 196616 | tf_op jit(solution)/shard_map/ppermute | solution.py:94
  109.8 4.5 %collective-permute-start.15 = (f32[128,128]{1,0:T(8,128)S(1)}, f32[128,128]{1,0:T(8,128)S(1)}, u32[]{:S(2)}, u32[]{:S(2)}) collective-permute-start(f32[128,128]{1,0:T(8,128)S(1)} %add.162), channel_id=1, source_target_pairs={{0,2},{1,3},{2,0},{3,1},{4,6},{5,7},{6,4},{7,5},{8,10},{9,11},{10,... | collective-permute-start | bytes 196616 | tf_op jit(solution)/shard_map/ppermute | solution.py:94

commit v17 on v14

--- a/solution.py
+++ b/solution.py
@@ -14,7 +14,7 @@
     return (earlier[0] * later[0], later[0][:, None, None] * earlier[1] + later[1])
 
 
-def pair_scan(decay, state, axis, reverse):
+def pair_scan(decay, state, axis, reverse, split=False):
     count = lax.axis_size(axis)
     if count == 1:
         return jnp.zeros_like(state)
@@ -80,6 +80,8 @@
     send = jnp.where(first, with_lead_own, s_g)
     keep = jnp.where(first, s_g, with_lead_rcv)
     other = lax.ppermute(send, axis, swap)
+    if split:
+        return keep, other, own_start, send_start, first
     return jnp.where(
         first, jnp.concatenate([other, keep], 0), jnp.concatenate([keep, other], 0)
     )
@@ -254,21 +256,44 @@
     from_start = jnp.transpose(jnp.exp(cumul))
     weighted_grad = grad_mixed.reshape(length, head_count, head_width) * from_start[:, :, None]
     local_grad = jnp.einsum("jhp,jn->hpn", weighted_grad, read_queries, precision=highest)
-    state_grad = pair_scan(decay_total, local_grad, "seq", True)
     if single:
+        sg_keep, sg_other, own_start, send_start, first = pair_scan(
+            decay_total, local_grad, "seq", True, split=True
+        )
         gf_w, gs_w, gd_w, gw_w, gr_w = pull_w(grad_mixed)
         gd_c, gr_c = pull_c(grad_mixed)
         grad_read = butterfly_psum(gr_w + gr_c, "head")
-        _, pull_e = jax.vjp(
-            lambda f, s, d, w: end_part(f, s, d, w, state_in),
-            features, step_sizes, log_decay, write_keys,
-        )
-        gf_e, gs_e, gd_e, gw_e = pull_e(state_grad)
+        half = sg_keep.shape[0]
+
+        def end_half(start, grad_half):
+            feat_h = lax.dynamic_slice_in_dim(features, start * head_width, half * head_width, 1)
+            step_h = lax.dynamic_slice_in_dim(step_sizes, start, half, 0)
+            decay_h = lax.dynamic_slice_in_dim(log_decay, start, half, 0)
+            state_h = lax.dynamic_slice_in_dim(state_in, start, half, 0)
+            _, pull_h = jax.vjp(
+                lambda f, s, d, w: end_part(f, s, d, w, state_h),
+                feat_h, step_h, decay_h, write_keys,
+            )
+            return pull_h(grad_half)
+
+        own = end_half(own_start, sg_keep)
+        rest = end_half(send_start, sg_other)
+
+        def join(a, b, axis):
+            return jnp.where(
+                first, jnp.concatenate([b, a], axis), jnp.concatenate([a, b], axis)
+            )
+
+        gf_e = join(own[0], rest[0], 1)
+        gs_e = join(own[1], rest[1], 0)
+        gd_e = join(own[2], rest[2], 0)
+        gw_e = own[3] + rest[3]
         grad_features = gf_w + gf_e
         grad_steps = gs_w + gs_e
         grad_decay = gd_w + gd_c + gd_e
         grad_write = butterfly_psum(gw_w + gw_e, "head")
     else:
+        state_grad = pair_scan(decay_total, local_grad, "seq", True)
         grad_features, grad_steps, grad_decay, grad_write, grad_read = pullback(
             (state_grad, grad_mixed)
         )

time: 116 us -> 115 us (level)
  waiting for transfers between devices: 62.3 us -> 56.5 us
  local copies, waits for them, and re-layouts: 5.32 us -> 9.74 us
  starting transfers between devices: 23.1 us -> 19.5 us
  other arithmetic: 9.22 us -> 11.6 us
  matrix products: 14 us -> 15.8 us
    ppermute x4, waiting for transfers between devices: 16.5 us -> 11.8 us  [pair_scan(): a_rcv, s_rcv = lax.ppermute((a_snd, s_snd), axis, swap)]
    dynamic_slice x0 -> x3, local copies, waits for them, and re-layouts: none -> 3.2 us  [end_half(): lax.dynamic_slice_in_dim(features, start * head_width, half * head_width, 1)]
    ppermute x2, waiting for transfers between devices: 30.4 us -> 27.4 us  [pair_scan(): s_in = lax.ppermute(out[1], axis, pairs)]
    ppermute x2, starting transfers between devices: 3.13 us -> 1.18 us  [pair_scan(): other = lax.ppermute(send, axis, swap)]
    dot_general x5 -> x9, matrix products: 2.87 us -> 4.75 us  [prefix_sum(): return jnp.dot(decay_in, upper, precision=lax.Precision.HIGHEST)]
    dot_general x2 -> x4, matrix products: 3.33 us -> 1.68 us  [state_update(): return jnp.einsum('jhp,jn->hpn', weighted_in, writes, precision=highest)]
    reshape x0 -> x3, local copies, waits for them, and re-layouts: none -> 1.64 us  [the longest x1 1.32 us: within_part(): feat3 = feat_in.reshape(length, head_count, head_width)]
    ppermute x2, waiting for transfers between devices: 4.17 us -> 5.37 us  [pair_scan(): other = lax.ppermute(send, axis, swap)]
  transfers between devices with their start and end apart: 18 -> 18, of which waited for: 12 -> 10; matrix products, arithmetic and copies ran while one was open for 11% -> 19% of each run, Pallas kernels for 0% -> 0%
where the time goes in v17:
time: 115 us; the launch traced here: 114 us
  waiting for transfers between devices  56.5 us (49%)
  starting transfers between devices  19.5 us (17%)
  matrix products  15.8 us (14%)
  other arithmetic  11.6 us (10%)
  local copies, waits for them, and re-layouts  9.74 us (8%)
  between operations  1.25 us (1%)
    ppermute x2, waiting for transfers between devices, pair_scan(): s_in = lax.ppermute(out[1], axis, pairs)  27.4 us
    ppermute x4, waiting for transfers between devices, pair_scan(): a_rcv, s_rcv = lax.ppermute((a_snd, s_snd), axis, swap)  11.8 us
    ppermute x6, waiting for transfers between devices, butterfly_psum(): got = lax.ppermute(parts, axis, [(i, i ^ k) for i in range(count)])  6.31 us
    dot_general x3, matrix products, within_part(): within = jnp.einsum('hij,jhp->ihp', masked, scaled, precision=highest)  5.88 us
    ppermute x4, waiting for transfers between devices, pair_scan(): a_in, s_in = lax.ppermute(out, axis, pairs)  5.67 us
    ppermute x4, starting transfers between devices, pair_scan(): a_in, s_in = lax.ppermute(out, axis, pairs)  5.55 us
    ppermute x4, starting transfers between devices, pair_scan(): a_rcv, s_rcv = lax.ppermute((a_snd, s_snd), axis, swap)  5.53 us
    ppermute x2, waiting for transfers between devices, pair_scan(): other = lax.ppermute(send, axis, swap)  5.37 us
  transfers between devices with their start and end apart: 18, of which 10 were waited for; matrix products, arithmetic and copies ran while one was open for 19% of the time, Pallas kernels for 0%

profile of v17, /device:TPU:0, one launch (start us, length us, event | category | flops | bytes accessed | tf_op | source)
XLA Modules:
  0.0 114.3 jit_solution(6966199819550978126)
XLA Ops:
  0.7 0.8 fusion.68
  1.8 2.9 %collective-permute-start.8 = (f32[10]{0:T(128)S(1)}, f32[10]{0:T(128)S(1)}, u32[]{:S(2)}, u32[]{:S(2)}) collective-permute-start(f32[10]{0:T(128)S(1)} %dynamic_slice.53), channel_id=1, source_target_pairs={{28,24},{24,28},{20,16},{16,20},{12,8},{8,12},{4,0},{0,4},{29,25},... | collective-permute-start | bytes 128 | tf_op jit(solution)/shard_map/ppermute | solution.py:42
  4.8 1.3 %copy.30 = f32[128,1280]{0,1:T(8,128)S(1)} copy(f32[128,1280]{1,0:T(8,128)} %param.9) | data formatting | bytes 1310720 | tf_op args[0]
  7.4 2.0 %collective-permute-start = (f32[10]{0:T(128)S(1)}, f32[10]{0:T(128)S(1)}, u32[]{:S(2)}, u32[]{:S(2)}) collective-permute-start(f32[10]{0:T(128)S(1)} %get-tuple-element.54), channel_id=1, source_target_pairs={{0,4},{4,0},{8,12},{12,8},{16,20},{20,16},{24,28},{28,24},{1,5},{5... | collective-permute-start | bytes 128 | tf_op jit(solution)/shard_map/ppermute | solution.py:42
  9.4 6.6 %collective-permute-done = f32[10]{0:T(128)S(1)} collective-permute-done((f32[10]{0:T(128)S(1)}, f32[10]{0:T(128)S(1)}, u32[]{:S(2)}, u32[]{:S(2)}) %collective-permute-start) | collective-permute-done | bytes 72 | tf_op jit(solution)/shard_map/ppermute | solution.py:42
  16.2 3.5 %collective-permute-start.2 = (f32[10,64,128]{2,1,0:T(8,128)S(1)}, f32[10,64,128]{2,1,0:T(8,128)S(1)}, u32[]{:S(2)}, u32[]{:S(2)}) collective-permute-start(f32[10,64,128]{2,1,0:T(8,128)S(1)} %get-tuple-element.29), channel_id=1, source_target_pairs={{0,8},{4,12},{1,9},{5,13},{2,10},{6,14},{3,11},{7,15}} | collective-permute-start | bytes 983048 | tf_op jit(solution)/shard_map/ppermute | solution.py:62
  19.7 5.7 %collective-permute-done.2 = f32[10,64,128]{2,1,0:T(8,128)S(1)} collective-permute-done((f32[10,64,128]{2,1,0:T(8,128)S(1)}, f32[10,64,128]{2,1,0:T(8,128)S(1)}, u32[]{:S(2)}, u32[]{:S(2)}) %collective-permute-start.2) | collective-permute-done | bytes 327712 | tf_op jit(solution)/shard_map/ppermute | solution.py:62
  28.0 1.5 %fusion.9 = f32[128,20,64]{0,2,1:T(8,128)S(1)} fusion(f32[128,20,64]{0,2,1:T(8,128)S(1)} %bitcast.127, f32[128,128]{1,0:T(8,128)S(1)} %fusion.104, f32[20,128]{1,0:T(8,128)S(1)} %bitcast.136, pred[128,128]{1,0:T(8,128)(4,1)S(1)} %iota_compare_fusion.10, f32[128,20]{0,1:T(8,128)S(1)} %bitcast.140, f32[20]{0:T(128)S(1)} %copy-done.22), kind=kOutput, calls=%fused_computation.9 | convolution fusion | flops 127631360 | bytes 1413200 | tf_op jit(solution)/shard_map/jvp(hij,jhp->ihp)/dot_general | solution.py:169
  29.7 5.0 %collective-permute-done.5 = f32[10,64,128]{2,1,0:T(8,128)S(1)} collective-permute-done((f32[10,64,128]{2,1,0:T(8,128)S(1)}, f32[10,64,128]{2,1,0:T(8,128)S(1)}, u32[]{:S(2)}, u32[]{:S(2)}) %collective-permute-start.5) | collective-permute-done | bytes 327712 | tf_op jit(solution)/shard_map/ppermute | solution.py:82
  34.8 1.3 %broadcast_multiply_fusion = (f32[128,20,64]{0,2,1:T(8,128)S(1)}, f32[128,20,64]{0,2,1:T(8,128)}) fusion(f32[128,20]{0,1:T(8,128)S(1)} %get-tuple-element.48, f32[20,64,128]{2,1,0:T(8,128)S(1)} %maximum_select_fusion, f32[128,128]{1,0:T(8,128)S(1)} %copy-done), kind=kOutput, calls=%fused_computation.72 | convolution fusion | flops 125992960 | bytes 2041856 | tf_op jit(solution)/shard_map/jvp(in,hpn->ihp)/dot_general | solution.py:176
  36.8 1.7 %multiply_reduce_fusion.4 = (f32[128]{0:T(128)S(1)}, f32[128]{0:T(128)S(1)}, f32[128,1280]{1,0:T(8,128)S(1)}) fusion(f32[128,1280]{1,0:T(8,128)} %param.10, f32[128,1280]{1,0:T(8,128)} %param.17, f32[1280]{0:T(1024)S(1)} %copy-done.14, f32[128,1280]{1,0:T(8,128)S(1)} %copy.31, f32[128,1280]{1,0:T(8,128)S(1)} %copy.32), kind=kLoop, calls=%fused_computation.34 | loop fusion | flops 1801984 | bytes 3282944 | tf_op jit(solution)/shard_map/reduce_sum | solution.py:246
  38.6 1.1 collective-permute-done.6
  39.7 1.6 %collective-permute-start.7 = (f32[2,128]{1,0:T(2,128)S(1)}, f32[2,128]{1,0:T(2,128)S(1)}, u32[]{:S(2)}, u32[]{:S(2)}) collective-permute-start(f32[2,128]{1,0:T(2,128)S(1)} %fusion.100), channel_id=1, source_target_pairs={{0,2},{1,3},{2,0},{3,1},{4,6},{5,7},{6,4},{7,5},{8,10},{9,11},{10,... | collective-permute-start | bytes 3080 | tf_op jit(solution)/shard_map/ppermute | solution.py:96
  41.3 2.0 %collective-permute-done.7 = f32[2,128]{1,0:T(2,128)S(1)} collective-permute-done((f32[2,128]{1,0:T(2,128)S(1)}, f32[2,128]{1,0:T(2,128)S(1)}, u32[]{:S(2)}, u32[]{:S(2)}) %collective-permute-start.7) | collective-permute-done | bytes 1056 | tf_op jit(solution)/shard_map/ppermute | solution.py:96
  43.4 1.3 %add_multiply_fusion = (f32[128,1280]{1,0:T(8,128)}, f32[128,1280]{1,0:T(8,128)S(1)}) fusion(f32[128,1280]{1,0:T(8,128)S(1)} %copy-done.4, f32[128,1280]{1,0:T(8,128)S(1)} %get-tuple-element.26, f32[128]{0:T(128)S(1)} %fusion.90, f32[128,1280]{1,0:T(8,128)S(1)} %copy-done.5, f32[128]{0:T(128)S(1)} %rsqrt_bitcast_fusion, f32[1280]{0:T(1024)S(1)} %copy-done.14), kind=kLoop, calls=%fused_computation.30 | loop fusion | flops 2621440 | bytes 3282944 | tf_op jit(solution)/shard_map/mul | solution.py:255
  46.7 0.9 constant_dynamic-slice_fusion.1
  47.6 1.2 %copy.39 = f32[128,640]{0,1:T(8,128)S(1)} copy(f32[128,640]{1,0:T(8,128)} %get-tuple-element.40) | data formatting | bytes 655360 | tf_op jit(solution)/shard_map/dynamic_slice | solution.py:269
  48.7 1.1 copy.40
  49.9 5.2 %collective-permute-done.9 = f32[10,64,128]{2,1,0:T(8,128)} collective-permute-done((f32[10,64,128]{2,1,0:T(8,128)}, f32[10,64,128]{2,1,0:T(8,128)}, u32[]{:S(2)}, u32[]{:S(2)}) %collective-permute-start.9) | collective-permute-done | bytes 327712 | tf_op jit(solution)/shard_map/ppermute | solution.py:42
  55.1 1.1 broadcast_add_fusion
  59.8 2.0 %fusion.20 = (f32[20,128]{1,0:T(8,128)S(1)}, f32[20,128]{1,0:T(8,128)S(1)}, f32[128,128]{1,0:T(8,128)S(1)}) fusion(f32[128,128]{1,0:T(8,128)S(1)} %fusion.104, f32[20,128]{1,0:T(8,128)S(1)} %bitcast.137, pred[128,128]{1,0:T(8,128)(4,1)S(1)} %iota_compare_fusion.10, f32[20,64,128]{2,1,0:T(8,128)S(1)} %bitcast.118, f32[128,20,64]{0,2,1:T(8,128)S(1)} %bitcast.128, ...), kind=kOutput, calls=%fused_computation.24 | convolution fusion | flops 129575936 | bytes 1499136 | tf_op jit(solution)/shard_map/transpose(jvp(hij,jhp->ihp))/dot_general | solution.py:169
  62.1 1.6 %collective-permute-start.12 = (f32[10,64,128]{2,1,0:T(8,128)S(1)}, f32[10,64,128]{2,1,0:T(8,128)S(1)}, u32[]{:S(2)}, u32[]{:S(2)}) collective-permute-start(f32[10,64,128]{2,1,0:T(8,128)S(1)} %get-tuple-element.18), channel_id=1, source_target_pairs={{12,4},{8,0},{13,5},{9,1},{14,6},{10,2},{15,7},{11,3}} | collective-permute-start | bytes 983048 | tf_op jit(solution)/shard_map/ppermute | solution.py:59
  64.5 2.5 %multiply_reduce_fusion.1 = (f32[128,20]{0,1:T(8,128)}, f32[128,20,64]{0,2,1:T(8,128)}, f32[128,20]{0,1:T(8,128)}) fusion(f32[128,20,64]{0,2,1:T(8,128)S(1)} %copy-done.7, f32[128,20,64]{0,2,1:T(8,128)S(1)} %bitcast.120, f32[128,20]{0,1:T(8,128)S(1)} %bitcast.142, f32[20]{0:T(128)S(1)} %copy-done.23, f32[128,20,64]{0,2,1:T(8,128)S(1)} %bitcast.129, ...), kind=kOutput, calls=%fused_computation.28 | convolution fusion | flops 128281600 | bytes 3399760 | tf_op jit(solution)/shard_map/transpose(jvp(hij,jhp->ihp))/dot_general | solution.py:169
  67.0 27.4 %collective-permute-done.12 = f32[10,64,128]{2,1,0:T(8,128)S(1)} collective-permute-done((f32[10,64,128]{2,1,0:T(8,128)S(1)}, f32[10,64,128]{2,1,0:T(8,128)S(1)}, u32[]{:S(2)}, u32[]{:S(2)}) %collective-permute-start.12) | collective-permute-done | bytes 327712 | tf_op jit(solution)/shard_map/ppermute | solution.py:59
  95.3 1.6 %collective-permute-start.17 = (f32[128,128]{1,0:T(8,128)S(1)}, f32[128,128]{1,0:T(8,128)}, u32[]{:S(2)}, u32[]{:S(2)}) collective-permute-start(f32[128,128]{1,0:T(8,128)S(1)} %add.180), channel_id=1, source_target_pairs={{0,2},{1,3},{2,0},{3,1},{4,6},{5,7},{6,4},{7,5},{8,10},{9,11},{10,... | collective-permute-start | bytes 196616 | tf_op jit(solution)/shard_map/ppermute | solution.py:96
  97.7 1.3 %copy.38 = f32[128,1280]{1,0:T(8,128)S(1)} copy(f32[128,1280]{0,1:T(8,128)} %bitcast.133) | data formatting | bytes 1310720 | tf_op jit(solution)/shard_map/transpose(jvp())/reshape | solution.py:166
  99.7 1.5 %add.181 = f32[128,128]{1,0:T(8,128)} add(f32[128,128]{1,0:T(8,128)S(1)} %add.180, f32[128,128]{1,0:T(8,128)} %collective-permute-done.17) | non-fusion elementwise | flops 16384 | bytes 196608 | tf_op jit(solution)/shard_map/add | solution.py:97
  101.6 1.2 %multiply_reduce_fusion.7 = (f32[10]{0:T(128)S(1)}, f32[10]{0:T(128)S(1)}, f32[10,64,128]{2,1,0:T(8,128)S(1)}) fusion(f32[10,64,128]{2,1,0:T(8,128)S(1)} %collective-permute-done.13, f32[20,64,128]{2,1,0:T(8,128)S(1)} %maximum_select_fusion, s32[]{:T(128)S(6)} %select_n.213, s32[]{:T(128)S(6)} %select_n.209, f32[10,64,128]{2,1,0:T(8,128)} %collective-permute-done.9, ...), kind=kLoop, calls=%fused_computation.58 | loop fusion | flops 655340 | bytes 2293890 | tf_op jit(solution)/shard_map/transpose(jvp())/reduce_sum | solution.py:193
  107.3 0.9 fusion.21
  108.3 0.8 fusion.18
  109.1 1.6 %collective-permute-start.15 = (f32[128,128]{1,0:T(8,128)S(1)}, f32[128,128]{1,0:T(8,128)S(1)}, u32[]{:S(2)}, u32[]{:S(2)}) collective-permute-start(f32[128,128]{1,0:T(8,128)S(1)} %add.177), channel_id=1, source_target_pairs={{0,2},{1,3},{2,0},{3,1},{4,6},{5,7},{6,4},{7,5},{8,10},{9,11},{10,... | collective-permute-start | bytes 196616 | tf_op jit(solution)/shard_map/ppermute | solution.py:96
  111.2 2.4 %collective-permute-done.15 = f32[128,128]{1,0:T(8,128)S(1)} collective-permute-done((f32[128,128]{1,0:T(8,128)S(1)}, f32[128,128]{1,0:T(8,128)S(1)}, u32[]{:S(2)}, u32[]{:S(2)}) %collective-permute-start.15) | collective-permute-done | bytes 65568 | tf_op jit(solution)/shard_map/ppermute | solution.py:96
  (128 shorter events, 20.5 us)
Async XLA Ops:
  0.6 26.4 %copy-start = (f32[128,128]{1,0:T(8,128)S(1)}, f32[128,128]{1,0:T(8,128)}, u32[]{:S(2)}) copy-start(f32[128,128]{1,0:T(8,128)} %param.12) | copy-start | bytes 196612
  1.8 5.0 %collective-permute-start.8 = (f32[10]{0:T(128)S(1)}, f32[10]{0:T(128)S(1)}, u32[]{:S(2)}, u32[]{:S(2)}) collective-permute-start(f32[10]{0:T(128)S(1)} %dynamic_slice.53), channel_id=1, source_target_pairs={{28,24},{24,28},{20,16},{16,20},{12,8},{8,12},{4,0},{0,4},{29,25},... | collective-permute-start | bytes 128 | tf_op jit(solution)/shard_map/ppermute | solution.py:42
  6.2 53.6 %copy-start.2 = (f32[128,1280]{0,1:T(8,128)}, f32[128,1280]{0,1:T(8,128)S(1)}, u32[]{:S(2)}) copy-start(f32[128,1280]{0,1:T(8,128)S(1)} %copy.30) | copy-start | bytes 1966084
  6.7 9.4 %collective-permute-start.1 = (f32[10,64,128]{2,1,0:T(8,128)S(1)}, f32[10,64,128]{2,1,0:T(8,128)S(1)}, u32[]{:S(2)}, u32[]{:S(2)}) collective-permute-start(f32[10,64,128]{2,1,0:T(8,128)S(1)} %constant_dynamic-slice_fusion.3), channel_id=1, source_target_pairs={{0,4},{4,0},{8,12},{12,8},{16,20},{20,16},{24,28},{28,24},{1,5},{5... | collective-permute-start | bytes 983048 | tf_op jit(solution)/shard_map/ppermute | solution.py:42
  6.8 9.4 %copy-start.20 = (f32[10]{0:T(128)}, f32[10]{0:T(128)S(1)}, u32[]{:S(2)}) copy-start(f32[10]{0:T(128)S(1)} %collective-permute-done.8) | copy-start | bytes 124
  7.4 8.6 %collective-permute-start = (f32[10]{0:T(128)S(1)}, f32[10]{0:T(128)S(1)}, u32[]{:S(2)}, u32[]{:S(2)}) collective-permute-start(f32[10]{0:T(128)S(1)} %get-tuple-element.54), channel_id=1, source_target_pairs={{0,4},{4,0},{8,12},{12,8},{16,20},{20,16},{24,28},{28,24},{1,5},{5... | collective-permute-start | bytes 128 | tf_op jit(solution)/shard_map/ppermute | solution.py:42
  16.2 9.2 %collective-permute-start.2 = (f32[10,64,128]{2,1,0:T(8,128)S(1)}, f32[10,64,128]{2,1,0:T(8,128)S(1)}, u32[]{:S(2)}, u32[]{:S(2)}) collective-permute-start(f32[10,64,128]{2,1,0:T(8,128)S(1)} %get-tuple-element.29), channel_id=1, source_target_pairs={{0,8},{4,12},{1,9},{5,13},{2,10},{6,14},{3,11},{7,15}} | collective-permute-start | bytes 983048 | tf_op jit(solution)/shard_map/ppermute | solution.py:62
  25.5 0.7 collective-permute-start.3
  26.3 0.9 collective-permute-start.4
  27.4 7.3 %collective-permute-start.5 = (f32[10,64,128]{2,1,0:T(8,128)S(1)}, f32[10,64,128]{2,1,0:T(8,128)S(1)}, u32[]{:S(2)}, u32[]{:S(2)}) collective-permute-start(f32[10,64,128]{2,1,0:T(8,128)S(1)} %get-tuple-element.42), channel_id=1, source_target_pairs={{0,4},{4,0},{8,12},{12,8},{16,20},{20,16},{24,28},{28,24},{1,5},{5... | collective-permute-start | bytes 983048 | tf_op jit(solution)/shard_map/ppermute | solution.py:82
  36.8 6.6 %copy-start.4 = (f32[128,1280]{1,0:T(8,128)S(1)}, f32[128,1280]{1,0:T(8,128)}, u32[]{:S(2)}) copy-start(f32[128,1280]{1,0:T(8,128)} %param.10) | copy-start | bytes 1966084
  36.8 6.7 %copy-start.5 = (f32[128,1280]{1,0:T(8,128)S(1)}, f32[128,1280]{1,0:T(8,128)}, u32[]{:S(2)}) copy-start(f32[128,1280]{1,0:T(8,128)} %param.17) | copy-start | bytes 1966084
  38.5 1.2 %collective-permute-start.6 = (f32[2,128]{1,0:T(2,128)S(1)}, f32[2,128]{1,0:T(2,128)S(1)}, u32[]{:S(2)}, u32[]{:S(2)}) collective-permute-start(f32[2,128]{1,0:T(2,128)S(1)} %pad_maximum_fusion), channel_id=1, source_target_pairs={{0,1},{1,0},{2,3},{3,2},{4,5},{5,4},{6,7},{7,6},{8,9},{9,8},{10,11... | collective-permute-start | bytes 3080 | tf_op jit(solution)/shard_map/ppermute | solution.py:96
  39.7 3.6 %collective-permute-start.7 = (f32[2,128]{1,0:T(2,128)S(1)}, f32[2,128]{1,0:T(2,128)S(1)}, u32[]{:S(2)}, u32[]{:S(2)}) collective-permute-start(f32[2,128]{1,0:T(2,128)S(1)} %fusion.100), channel_id=1, source_target_pairs={{0,2},{1,3},{2,0},{3,1},{4,6},{5,7},{6,4},{7,5},{8,10},{9,11},{10,... | collective-permute-start | bytes 3080 | tf_op jit(solution)/shard_map/ppermute | solution.py:96
  46.1 8.9 %collective-permute-start.9 = (f32[10,64,128]{2,1,0:T(8,128)}, f32[10,64,128]{2,1,0:T(8,128)}, u32[]{:S(2)}, u32[]{:S(2)}) collective-permute-start(f32[10,64,128]{2,1,0:T(8,128)} %constant_dynamic-slice_fusion.2), channel_id=1, source_target_pairs={{28,24},{24,28},{20,16},{16,20},{12,8},{8,12},{4,0},{0,4},{29,25},... | collective-permute-start | bytes 983048 | tf_op jit(solution)/shard_map/ppermute | solution.py:42
  47.6 7.5 %copy-start.18 = (f32[10]{0:T(128)S(1)}, f32[10]{0:T(128)}, u32[]{:S(2)}) copy-start(f32[10]{0:T(128)} %get-tuple-element.22) | copy-start | bytes 124
  47.6 7.5 %copy-start.19 = (f32[10]{0:T(128)S(1)}, f32[10]{0:T(128)}, u32[]{:S(2)}) copy-start(f32[10]{0:T(128)} %get-tuple-element.24) | copy-start | bytes 124
  56.2 2.8 %collective-permute-start.10 = (f32[10,64,128]{2,1,0:T(8,128)S(1)}, f32[10,64,128]{2,1,0:T(8,128)S(1)}, u32[]{:S(2)}, u32[]{:S(2)}) collective-permute-start(f32[10,64,128]{2,1,0:T(8,128)S(1)} %get-tuple-element.20), channel_id=1, source_target_pairs={{28,20},{24,16},{29,21},{25,17},{30,22},{26,18},{31,23},{27,19}} | collective-permute-start | bytes 983048 | tf_op jit(solution)/shard_map/ppermute | solution.py:62
  59.1 2.8 %collective-permute-start.11 = (f32[10,64,128]{2,1,0:T(8,128)S(1)}, f32[10,64,128]{2,1,0:T(8,128)S(1)}, u32[]{:S(2)}, u32[]{:S(2)}) collective-permute-start(f32[10,64,128]{2,1,0:T(8,128)S(1)} %multiply_add_fusion.2), channel_id=1, source_target_pairs={{20,12},{16,8},{21,13},{17,9},{22,14},{18,10},{23,15},{19,11}} | collective-permute-start | bytes 983048 | tf_op jit(solution)/shard_map/ppermute | solution.py:62
  62.0 2.4 %copy-start.3 = (f32[128,1280]{0,1:T(8,128)S(1)}, f32[128,1280]{0,1:T(8,128)}, u32[]{:S(2)}) copy-start(f32[128,1280]{0,1:T(8,128)} %copy-done.2) | copy-start | bytes 1966084
  62.1 2.4 %copy-start.7 = (f32[128,20,64]{0,2,1:T(8,128)S(1)}, f32[128,20,64]{0,2,1:T(8,128)}, u32[]{:S(2)}) copy-start(f32[128,20,64]{0,2,1:T(8,128)} %get-tuple-element.56) | copy-start | bytes 1966084
  62.1 2.4 %copy-start.23 = (f32[20]{0:T(128)S(1)}, f32[20]{0:T(128)}, u32[]{:S(2)}) copy-start(f32[20]{0:T(128)} %param.15) | copy-start | bytes 244
  62.1 32.2 %collective-permute-start.12 = (f32[10,64,128]{2,1,0:T(8,128)S(1)}, f32[10,64,128]{2,1,0:T(8,128)S(1)}, u32[]{:S(2)}, u32[]{:S(2)}) collective-permute-start(f32[10,64,128]{2,1,0:T(8,128)S(1)} %get-tuple-element.18), channel_id=1, source_target_pairs={{12,4},{8,0},{13,5},{9,1},{14,6},{10,2},{15,7},{11,3}} | collective-permute-start | bytes 983048 | tf_op jit(solution)/shard_map/ppermute | solution.py:59
  64.4 30.9 %collective-permute-start.16 = (f32[128,128]{1,0:T(8,128)S(1)}, f32[128,128]{1,0:T(8,128)S(1)}, u32[]{:S(2)}, u32[]{:S(2)}) collective-permute-start(f32[128,128]{1,0:T(8,128)S(1)} %fusion.17), channel_id=1, source_target_pairs={{0,1},{1,0},{2,3},{3,2},{4,5},{5,4},{6,7},{7,6},{8,9},{9,8},{10,11... | collective-permute-start | bytes 196616 | tf_op jit(solution)/shard_map/ppermute | solution.py:96
  94.4 7.1 %collective-permute-start.13 = (f32[10,64,128]{2,1,0:T(8,128)S(1)}, f32[10,64,128]{2,1,0:T(8,128)S(1)}, u32[]{:S(2)}, u32[]{:S(2)}) collective-permute-start(f32[10,64,128]{2,1,0:T(8,128)S(1)} %add_select_fusion.1), channel_id=1, source_target_pairs={{28,24},{24,28},{20,16},{16,20},{12,8},{8,12},{4,0},{0,4},{29,25},... | collective-permute-start | bytes 983048 | tf_op jit(solution)/shard_map/ppermute | solution.py:82
  95.3 4.4 %collective-permute-start.17 = (f32[128,128]{1,0:T(8,128)S(1)}, f32[128,128]{1,0:T(8,128)}, u32[]{:S(2)}, u32[]{:S(2)}) collective-permute-start(f32[128,128]{1,0:T(8,128)S(1)} %add.180), channel_id=1, source_target_pairs={{0,2},{1,3},{2,0},{3,1},{4,6},{5,7},{6,4},{7,5},{8,10},{9,11},{10,... | collective-permute-start | bytes 196616 | tf_op jit(solution)/shard_map/ppermute | solution.py:96
  97.7 3.9 %copy-start.21 = (f32[10]{0:T(128)S(1)}, f32[10]{0:T(128)}, u32[]{:S(2)}) copy-start(f32[10]{0:T(128)} %copy-done.20) | copy-start | bytes 124
  101.2 2.1 %copy-start.11 = (f32[10,128]{1,0:T(8,128)S(1)}, f32[10,128]{1,0:T(8,128)}, u32[]{:S(2)}) copy-start(f32[10,128]{1,0:T(8,128)} %fusion.66) | copy-start | bytes 15364
  101.2 2.3 %copy-start.8 = (f32[128,10]{0,1:T(8,128)S(1)}, f32[128,10]{0,1:T(8,128)}, u32[]{:S(2)}) copy-start(f32[128,10]{0,1:T(8,128)} %get-tuple-element.47) | copy-start | bytes 15364
  106.8 2.3 %collective-permute-start.14 = (f32[128,128]{1,0:T(8,128)S(1)}, f32[128,128]{1,0:T(8,128)S(1)}, u32[]{:S(2)}, u32[]{:S(2)}) collective-permute-start(f32[128,128]{1,0:T(8,128)S(1)} %fusion.16), channel_id=1, source_target_pairs={{0,1},{1,0},{2,3},{3,2},{4,5},{5,4},{6,7},{7,6},{8,9},{9,8},{10,11... | collective-permute-start | bytes 196616 | tf_op jit(solution)/shard_map/ppermute | solution.py:96
  107.3 3.4 %copy-start.17 = (f32[128,20]{0,1:T(8,128)S(1)}, f32[128,20]{0,1:T(8,128)}, u32[]{:S(2)}) copy-start(f32[128,20]{0,1:T(8,128)} %get-tuple-element.39) | copy-start | bytes 30724
  109.1 4.6 %collective-permute-start.15 = (f32[128,128]{1,0:T(8,128)S(1)}, f32[128,128]{1,0:T(8,128)S(1)}, u32[]{:S(2)}, u32[]{:S(2)}) collective-permute-start(f32[128,128]{1,0:T(8,128)S(1)} %add.177), channel_id=1, source_target_pairs={{0,2},{1,3},{2,0},{3,1},{4,6},{5,7},{6,4},{7,5},{8,10},{9,11},{10,... | collective-permute-start | bytes 196616 | tf_op jit(solution)/shard_map/ppermute | solution.py:96
  (10 other events, 11.9 us)

commit v18 on v17

--- a/solution.py
+++ b/solution.py
@@ -215,19 +215,50 @@
     to_end = jnp.exp(cumul[:, -1:] - cumul)
     weighted_in = scaled * jnp.transpose(to_end)[:, :, None]
     local_state = jnp.einsum("jhp,jn->hpn", weighted_in, write_keys, precision=highest)
-    state_in = pair_scan(decay_total, local_state, "seq", False)
     single = length == BLOCK
+    sigmoid_gate = jax.nn.sigmoid(gate_pre)
+    active = gate_pre * sigmoid_gate
+    weighted = out_grad * norm_gain[None, :]
     if single:
+        keep_f, other_f, own_f, send_f, first_f = pair_scan(
+            decay_total, local_state, "seq", False, split=True
+        )
+        half_f = keep_f.shape[0]
+
+        def join_f(a, b, axis):
+            return jnp.where(
+                first_f, jnp.concatenate([b, a], axis), jnp.concatenate([a, b], axis)
+            )
+
+        def cols(x, start):
+            return lax.dynamic_slice_in_dim(x, start * head_width, half_f * head_width, 1)
+
+        state_in = join_f(keep_f, other_f, 0)
         mixed_w, pull_w = jax.vjp(
             lambda f, s, d, w, r: within_part(f, s, d, w, r, skip_scale),
             features, step_sizes, log_decay, write_keys, read_queries,
         )
-        mixed_c, pull_c = jax.vjp(
-            lambda d, r: carried_part(d, r, state_in), log_decay, read_queries
-        )
         mixed_w = lax.optimization_barrier(mixed_w)
-        mixed_out = mixed_w + mixed_c
+
+        def carried_half(start, state_h):
+            decay_h = lax.dynamic_slice_in_dim(log_decay, start, half_f, 0)
+            out_h, pull_h = jax.vjp(
+                lambda d, r: carried_part(d, r, state_h), decay_h, read_queries
+            )
+            return cols(mixed_w, start) + out_h, pull_h
+
+        mixed_own, pull_c_own = carried_half(own_f, keep_f)
+        mixed_oth, pull_c_oth = carried_half(send_f, other_f)
+        mixed_out = join_f(mixed_own, mixed_oth, 1)
+        gated_own = mixed_own * cols(active, own_f)
+        gated_oth = mixed_oth * cols(active, send_f)
+        sums = jnp.stack([
+            jnp.sum(gated_own * gated_own, axis=1) + jnp.sum(gated_oth * gated_oth, axis=1),
+            jnp.sum(cols(weighted, own_f) * gated_own, axis=1)
+            + jnp.sum(cols(weighted, send_f) * gated_oth, axis=1),
+        ])
     else:
+        state_in = pair_scan(decay_total, local_state, "seq", False)
 
         def local_mixer(feat_in, step_in, decay_factors, writes, read_in):
             return run_mixer(
@@ -238,14 +269,12 @@
             local_mixer, features, step_sizes, log_decay, write_keys, read_queries
         )
         mixed_out = primal[1]
-    sigmoid_gate = jax.nn.sigmoid(gate_pre)
-    active = gate_pre * sigmoid_gate
+        gated_full = mixed_out * active
+        sums = jnp.stack(
+            [jnp.sum(gated_full * gated_full, axis=1), jnp.sum(weighted * gated_full, axis=1)]
+        )
     gated_out = mixed_out * active
-    weighted = out_grad * norm_gain[None, :]
-    square_sum, cross_sum = butterfly_psum(
-        jnp.stack([jnp.sum(gated_out * gated_out, axis=1), jnp.sum(weighted * gated_out, axis=1)]),
-        "head",
-    )
+    square_sum, cross_sum = butterfly_psum(sums, "head")
     inverse = lax.rsqrt(square_sum / channels + eps)
     grad_gated = (
         inverse[:, None] * weighted
@@ -261,7 +290,10 @@
             decay_total, local_grad, "seq", True, split=True
         )
         gf_w, gs_w, gd_w, gw_w, gr_w = pull_w(grad_mixed)
-        gd_c, gr_c = pull_c(grad_mixed)
+        gd_own, gr_own = pull_c_own(cols(grad_mixed, own_f))
+        gd_oth, gr_oth = pull_c_oth(cols(grad_mixed, send_f))
+        gd_c = join_f(gd_own, gd_oth, 0)
+        gr_c = gr_own + gr_oth
         grad_read = butterfly_psum(gr_w + gr_c, "head")
         half = sg_keep.shape[0]
 

time: 115 us -> 125 us (1.087)
  local copies, waits for them, and re-layouts: 9.74 us -> 16 us
  waiting for transfers between devices: 56.5 us -> 52 us
  other arithmetic: 11.6 us -> 14.8 us
  matrix products: 15.8 us -> 18.7 us
  starting transfers between devices: 19.5 us -> 20.9 us
    unnamed x49 -> x97, local copies, waits for them, and re-layouts: 2.16 us -> 5.9 us
    ppermute x4, waiting for transfers between devices: 11.8 us -> 8.28 us  [pair_scan(): a_rcv, s_rcv = lax.ppermute((a_snd, s_snd), axis, swap)]
    reshape x1 -> x2, local copies, waits for them, and re-layouts: 0.23 us -> 2.77 us  [carried_part(): return carried.reshape(length, -1)]
    ppermute x2, waiting for transfers between devices: 27.4 us -> 29.7 us  [pair_scan(): s_in = lax.ppermute(out[1], axis, pairs)]
    ppermute x6, waiting for transfers between devices: 6.31 us -> 4.66 us  [butterfly_psum(): got = lax.ppermute(parts, axis, [(i, i ^ k) for i in range(count)])]
    ppermute x4, waiting for transfers between devices: 5.67 us -> 4.09 us  [pair_scan(): a_in, s_in = lax.ppermute(out, axis, pairs)]
    select_n x2, other arithmetic: 0.26 us -> 1.72 us  [pair_scan(): send = jnp.where(first, with_lead_own, s_g)]
    dot_general x3, matrix products: 5.88 us -> 7.26 us  [within_part(): within = jnp.einsum('hij,jhp->ihp', masked, scaled, precision=highest)]
  transfers between devices with their start and end apart: 18 -> 18, of which waited for: 10 -> 9; matrix products, arithmetic and copies ran while one was open for 19% -> 21% of each run, Pallas kernels for 0% -> 0%
where the time goes in v18:
time: 125 us; the launch traced here: 124 us
  waiting for transfers between devices  52 us (42%)
  starting transfers between devices  20.9 us (17%)
  matrix products  18.7 us (15%)
  local copies, waits for them, and re-layouts  16 us (13%)
  other arithmetic  14.8 us (12%)
  between operations  1.47 us (1%)
    ppermute x2, waiting for transfers between devices, pair_scan(): s_in = lax.ppermute(out[1], axis, pairs)  29.7 us
    ppermute x4, waiting for transfers between devices, pair_scan(): a_rcv, s_rcv = lax.ppermute((a_snd, s_snd), axis, swap)  8.28 us
    dot_general x3, matrix products, within_part(): within = jnp.einsum('hij,jhp->ihp', masked, scaled, precision=highest)  7.26 us
    unnamed x97, local copies, waits for them, and re-layouts  5.9 us
    ppermute x4, starting transfers between devices, pair_scan(): a_in, s_in = lax.ppermute(out, axis, pairs)  5.68 us
    ppermute x4, starting transfers between devices, pair_scan(): a_rcv, s_rcv = lax.ppermute((a_snd, s_snd), axis, swap)  5.59 us
    ppermute x2, waiting for transfers between devices, pair_scan(): other = lax.ppermute(send, axis, swap)  5.31 us
    dot_general x12, matrix products, prefix_sum(): return jnp.dot(decay_in, upper, precision=lax.Precision.HIGHEST)  5.13 us
  transfers between devices with their start and end apart: 18, of which 9 were waited for; matrix products, arithmetic and copies ran while one was open for 21% of the time, Pallas kernels for 0%

profile of v18, /device:TPU:0, one launch (start us, length us, event | category | flops | bytes accessed | tf_op | source)
XLA Modules:
  0.0 123.9 jit_solution(8493982218466751859)
XLA Ops:
  1.8 2.9 %collective-permute-start.8 = (f32[10]{0:T(128)S(1)}, f32[10]{0:T(128)S(1)}, u32[]{:S(2)}, u32[]{:S(2)}) collective-permute-start(f32[10]{0:T(128)S(1)} %dynamic_slice.91), channel_id=1, source_target_pairs={{28,24},{24,28},{20,16},{16,20},{12,8},{8,12},{4,0},{0,4},{29,25},... | collective-permute-start | bytes 128 | tf_op jit(solution)/shard_map/ppermute | solution.py:42
  4.8 1.3 %copy.34 = f32[128,1280]{0,1:T(8,128)S(1)} copy(f32[128,1280]{1,0:T(8,128)} %param.9) | data formatting | bytes 1310720 | tf_op args[0]
  8.4 1.5 %fusion.9 = f32[128,20,64]{0,2,1:T(8,128)S(1)} fusion(f32[128,20,64]{0,2,1:T(8,128)S(1)} %bitcast.144, f32[128,128]{1,0:T(8,128)S(1)} %fusion.110, f32[20,128]{1,0:T(8,128)S(1)} %bitcast.158, pred[128,128]{1,0:T(8,128)(4,1)S(1)} %iota_compare_fusion.13, f32[128,20]{0,1:T(8,128)S(1)} %bitcast.166, f32[20]{0:T(128)S(1)} %copy-done.43), kind=kOutput, calls=%fused_computation.8 | convolution fusion | flops 127631360 | bytes 1413200 | tf_op jit(solution)/shard_map/jvp(hij,jhp->ihp)/dot_general | solution.py:169
  12.4 1.5 %collective-permute-start = (f32[10]{0:T(128)S(1)}, f32[10]{0:T(128)S(1)}, u32[]{:S(2)}, u32[]{:S(2)}) collective-permute-start(f32[10]{0:T(128)S(1)} %get-tuple-element.60), channel_id=1, source_target_pairs={{0,4},{4,0},{8,12},{12,8},{16,20},{20,16},{24,28},{28,24},{1,5},{5... | collective-permute-start | bytes 128 | tf_op jit(solution)/shard_map/ppermute | solution.py:42
  13.9 2.2 %collective-permute-done = f32[10]{0:T(128)S(1)} collective-permute-done((f32[10]{0:T(128)S(1)}, f32[10]{0:T(128)S(1)}, u32[]{:S(2)}, u32[]{:S(2)}) %collective-permute-start) | collective-permute-done | bytes 72 | tf_op jit(solution)/shard_map/ppermute | solution.py:42
  16.2 3.6 %collective-permute-start.2 = (f32[10,64,128]{2,1,0:T(8,128)S(1)}, f32[10,64,128]{2,1,0:T(8,128)S(1)}, u32[]{:S(2)}, u32[]{:S(2)}) collective-permute-start(f32[10,64,128]{2,1,0:T(8,128)S(1)} %get-tuple-element.32), channel_id=1, source_target_pairs={{0,8},{4,12},{1,9},{5,13},{2,10},{6,14},{3,11},{7,15}} | collective-permute-start | bytes 983048 | tf_op jit(solution)/shard_map/ppermute | solution.py:62
  21.5 4.1 %collective-permute-done.2 = f32[10,64,128]{2,1,0:T(8,128)S(1)} collective-permute-done((f32[10,64,128]{2,1,0:T(8,128)S(1)}, f32[10,64,128]{2,1,0:T(8,128)S(1)}, u32[]{:S(2)}, u32[]{:S(2)}) %collective-permute-start.2) | collective-permute-done | bytes 327712 | tf_op jit(solution)/shard_map/ppermute | solution.py:62
  29.5 1.2 collective-permute-start.5
  30.8 1.1 broadcast_multiply_fusion.2
  32.8 4.2 %collective-permute-done.5 = f32[10,64,128]{2,1,0:T(8,128)S(1)} collective-permute-done((f32[10,64,128]{2,1,0:T(8,128)}, f32[10,64,128]{2,1,0:T(8,128)S(1)}, u32[]{:S(2)}, u32[]{:S(2)}) %collective-permute-start.5) | collective-permute-done | bytes 327712 | tf_op jit(solution)/shard_map/ppermute | solution.py:82
  37.0 1.2 broadcast_multiply_fusion.1
  38.2 1.9 %copy.38 = f32[128,640]{1,0:T(8,128)} copy(f32[128,640]{0,1:T(8,128)} %bitcast.154) | data formatting | bytes 655360 | tf_op jit(solution)/shard_map/jvp()/reshape | solution.py:178
  40.1 2.3 %multiply_reduce_fusion.10 = (f32[128]{0:T(128)S(1)}, f32[128]{0:T(128)S(1)}, f32[128]{0:T(128)S(1)}, f32[128]{0:T(128)S(1)}, f32[128,640]{1,0:T(8,128)}, /*index=5*/f32[128,640]{1,0:T(8,128)}) fusion(f32[128,1280]{1,0:T(8,128)S(1)} %broadcast_multiply_fusion, s32[]{:T(128)S(6)} %select_n.230, f32[128,1280]{1,0:T(8,128)S(1)} %copy-done.10, ...), kind=kLoop, calls=%fused_computation.77 | loop fusion | flops 982528 | bytes 3278856 | tf_op jit(solution)/shard_map/reduce_sum | solution.py:258
  43.2 1.1 copy.45
  44.6 1.6 %collective-permute-start.7 = (f32[2,128]{1,0:T(2,128)S(1)}, f32[2,128]{1,0:T(2,128)S(1)}, u32[]{:S(2)}, u32[]{:S(2)}) collective-permute-start(f32[2,128]{1,0:T(2,128)S(1)} %fusion.106), channel_id=1, source_target_pairs={{0,2},{1,3},{2,0},{3,1},{4,6},{5,7},{6,4},{7,5},{8,10},{9,11},{10,... | collective-permute-start | bytes 3080 | tf_op jit(solution)/shard_map/ppermute | solution.py:96
  47.0 1.1 collective-permute-done.7
  48.3 1.3 %add_multiply_fusion = (f32[128,1280]{1,0:T(8,128)}, f32[128,1280]{1,0:T(8,128)S(1)}) fusion(f32[128,1280]{1,0:T(8,128)S(1)} %copy-done.2, f32[128,640]{1,0:T(8,128)S(1)} %copy-done.17, f32[128,640]{1,0:T(8,128)S(1)} %copy-done.16, f32[128]{0:T(128)S(1)} %fusion.97, f32[128]{0:T(128)S(1)} %rsqrt_bitcast_fusion, pred[]{:T(512)S(6)} %eq.27, ...), kind=kLoop, calls=%fused_computation.35 | loop fusion | flops 3112960 | bytes 3282945 | tf_op jit(solution)/shard_map/mul | solution.py:284
  50.6 3.4 %fusion.21 = (f32[20,128]{1,0:T(8,128)}, f32[20,128]{1,0:T(8,128)}, f32[128,128]{1,0:T(8,128)S(1)}) fusion(f32[128,128]{1,0:T(8,128)} %copy-done.30, f32[20,128]{1,0:T(8,128)S(1)} %bitcast.159, pred[128,128]{1,0:T(8,128)(4,1)S(1)} %iota_compare_fusion.13, f32[20,64,128]{2,1,0:T(8,128)S(1)} %bitcast.147, f32[128,20,64]{0,2,1:T(8,128)S(1)} %bitcast.145, ...), kind=kOutput, calls=%fused_computation.29 | convolution fusion | flops 129575936 | bytes 1499136 | tf_op jit(solution)/shard_map/transpose(jvp(hij,jhp->ihp))/dot_general | solution.py:169
  55.2 1.1 collective-permute-start.9
  58.3 6.1 %collective-permute-done.9 = f32[10,64,128]{2,1,0:T(8,128)} collective-permute-done((f32[10,64,128]{2,1,0:T(8,128)}, f32[10,64,128]{2,1,0:T(8,128)}, u32[]{:S(2)}, u32[]{:S(2)}) %collective-permute-start.9) | collective-permute-done | bytes 327712 | tf_op jit(solution)/shard_map/ppermute | solution.py:42
  64.5 1.1 broadcast_add_fusion
  68.5 1.6 %collective-permute-start.12 = (f32[10,64,128]{2,1,0:T(8,128)S(1)}, f32[10,64,128]{2,1,0:T(8,128)S(1)}, u32[]{:S(2)}, u32[]{:S(2)}) collective-permute-start(f32[10,64,128]{2,1,0:T(8,128)S(1)} %get-tuple-element.20), channel_id=1, source_target_pairs={{12,4},{8,0},{13,5},{9,1},{14,6},{10,2},{15,7},{11,3}} | collective-permute-start | bytes 983048 | tf_op jit(solution)/shard_map/ppermute | solution.py:59
  71.0 2.4 %multiply_reduce_fusion.1 = (f32[128,20]{0,1:T(8,128)}, f32[128,20,64]{0,2,1:T(8,128)}) fusion(f32[128,20,64]{0,2,1:T(8,128)S(1)} %bitcast.146, f32[128,20]{0,1:T(8,128)S(1)} %bitcast.168, f32[128,20,64]{0,2,1:T(8,128)S(1)} %bitcast.149, f32[20]{0:T(128)S(1)} %copy-done.44, f32[20,64,128]{2,1,0:T(8,128)S(1)} %bitcast.150, f32[128,128]{1,0:T(8,128)S(1)} %copy-done.31, ...), kind=kOutput, calls=%fused_computation.34 | convolution fusion | flops 127956480 | bytes 2734160 | tf_op jit(solution)/shard_map/transpose(jvp(hij,jhp->ihp))/dot_general | solution.py:169
  73.4 29.7 %collective-permute-done.12 = f32[10,64,128]{2,1,0:T(8,128)S(1)} collective-permute-done((f32[10,64,128]{2,1,0:T(8,128)S(1)}, f32[10,64,128]{2,1,0:T(8,128)S(1)}, u32[]{:S(2)}, u32[]{:S(2)}) %collective-permute-start.12) | collective-permute-done | bytes 327712 | tf_op jit(solution)/shard_map/ppermute | solution.py:59
  103.9 1.1 collective-permute-start.13
  105.1 1.6 %collective-permute-start.17 = (f32[128,128]{1,0:T(8,128)S(1)}, f32[128,128]{1,0:T(8,128)S(1)}, u32[]{:S(2)}, u32[]{:S(2)}) collective-permute-start(f32[128,128]{1,0:T(8,128)S(1)} %add.234), channel_id=1, source_target_pairs={{0,2},{1,3},{2,0},{3,1},{4,6},{5,7},{6,4},{7,5},{8,10},{9,11},{10,... | collective-permute-start | bytes 196616 | tf_op jit(solution)/shard_map/ppermute | solution.py:96
  106.9 1.4 %copy.44 = f32[128,1280]{1,0:T(8,128)S(1)} copy(f32[128,1280]{0,1:T(8,128)} %bitcast.155) | data formatting | bytes 1310720 | tf_op jit(solution)/shard_map/transpose(jvp())/reshape | solution.py:166
  108.3 1.2 collective-permute-done.17
  110.1 1.1 collective-permute-done.13
  111.2 1.3 %multiply_reduce_fusion.4 = (f32[10]{0:T(128)S(1)}, f32[10]{0:T(128)S(1)}, f32[10,64,128]{2,1,0:T(8,128)S(1)}) fusion(f32[10,64,128]{2,1,0:T(8,128)S(1)} %collective-permute-done.13, f32[20,64,128]{2,1,0:T(8,128)S(1)} %copy-done.9, s32[]{:T(128)S(6)} %select_n.241, s32[]{:T(128)S(6)} %select_n.237, f32[10,64,128]{2,1,0:T(8,128)} %collective-permute-done.9, ...), kind=kLoop, calls=%fused_computation.61 | loop fusion | flops 655340 | bytes 2293890 | tf_op jit(solution)/shard_map/transpose(jvp())/reduce_sum | solution.py:193
  118.7 1.6 %collective-permute-start.15 = (f32[128,128]{1,0:T(8,128)S(1)}, f32[128,128]{1,0:T(8,128)S(1)}, u32[]{:S(2)}, u32[]{:S(2)}) collective-permute-start(f32[128,128]{1,0:T(8,128)S(1)} %add.230), channel_id=1, source_target_pairs={{0,2},{1,3},{2,0},{3,1},{4,6},{5,7},{6,4},{7,5},{8,10},{9,11},{10,... | collective-permute-start | bytes 196616 | tf_op jit(solution)/shard_map/ppermute | solution.py:96
  120.9 2.4 %collective-permute-done.15 = f32[128,128]{1,0:T(8,128)S(1)} collective-permute-done((f32[128,128]{1,0:T(8,128)S(1)}, f32[128,128]{1,0:T(8,128)S(1)}, u32[]{:S(2)}, u32[]{:S(2)}) %collective-permute-start.15) | collective-permute-done | bytes 65568 | tf_op jit(solution)/shard_map/ppermute | solution.py:96
  (190 shorter events, 31.5 us)
Async XLA Ops:
  0.6 7.5 %copy-start = (f32[128,128]{1,0:T(8,128)S(1)}, f32[128,128]{1,0:T(8,128)}, u32[]{:S(2)}) copy-start(f32[128,128]{1,0:T(8,128)} %param.12) | copy-start | bytes 196612
  1.8 9.9 %collective-permute-start.8 = (f32[10]{0:T(128)S(1)}, f32[10]{0:T(128)S(1)}, u32[]{:S(2)}, u32[]{:S(2)}) collective-permute-start(f32[10]{0:T(128)S(1)} %dynamic_slice.91), channel_id=1, source_target_pairs={{28,24},{24,28},{20,16},{16,20},{12,8},{8,12},{4,0},{0,4},{29,25},... | collective-permute-start | bytes 128 | tf_op jit(solution)/shard_map/ppermute | solution.py:42
  6.7 9.4 %collective-permute-start.1 = (f32[10,64,128]{2,1,0:T(8,128)S(1)}, f32[10,64,128]{2,1,0:T(8,128)S(1)}, u32[]{:S(2)}, u32[]{:S(2)}) collective-permute-start(f32[10,64,128]{2,1,0:T(8,128)S(1)} %constant_dynamic-slice_fusion.6), channel_id=1, source_target_pairs={{0,4},{4,0},{8,12},{12,8},{16,20},{20,16},{24,28},{28,24},{1,5},{5... | collective-permute-start | bytes 983048 | tf_op jit(solution)/shard_map/ppermute | solution.py:42
  6.9 42.9 %copy-start.33 = (pred[128,128]{1,0:T(8,128)(4,1)}, pred[128,128]{1,0:T(8,128)(4,1)S(1)}, u32[]{:S(2)}) copy-start(pred[128,128]{1,0:T(8,128)(4,1)S(1)} %iota_compare_fusion.13) | copy-start | bytes 49156
  12.4 3.7 %collective-permute-start = (f32[10]{0:T(128)S(1)}, f32[10]{0:T(128)S(1)}, u32[]{:S(2)}, u32[]{:S(2)}) collective-permute-start(f32[10]{0:T(128)S(1)} %get-tuple-element.60), channel_id=1, source_target_pairs={{0,4},{4,0},{8,12},{12,8},{16,20},{20,16},{24,28},{28,24},{1,5},{5... | collective-permute-start | bytes 128 | tf_op jit(solution)/shard_map/ppermute | solution.py:42
  16.1 4.5 %copy-start.3 = (f32[128,1280]{1,0:T(8,128)S(1)}, f32[128,1280]{1,0:T(8,128)}, u32[]{:S(2)}) copy-start(f32[128,1280]{1,0:T(8,128)} %param.9) | copy-start | bytes 1966084
  16.2 9.4 %collective-permute-start.2 = (f32[10,64,128]{2,1,0:T(8,128)S(1)}, f32[10,64,128]{2,1,0:T(8,128)S(1)}, u32[]{:S(2)}, u32[]{:S(2)}) collective-permute-start(f32[10,64,128]{2,1,0:T(8,128)S(1)} %get-tuple-element.32), channel_id=1, source_target_pairs={{0,8},{4,12},{1,9},{5,13},{2,10},{6,14},{3,11},{7,15}} | collective-permute-start | bytes 983048 | tf_op jit(solution)/shard_map/ppermute | solution.py:62
  20.0 46.3 %copy-start.20 = (f32[10,128]{1,0:T(8,128)}, f32[10,128]{1,0:T(8,128)S(1)}, u32[]{:S(2)}) copy-start(f32[10,128]{1,0:T(8,128)S(1)} %convolution_exponential_fusion) | copy-start | bytes 15364
  21.5 4.9 %copy-start.1 = (f32[128,1280]{1,0:T(8,128)S(1)}, f32[128,1280]{1,0:T(8,128)}, u32[]{:S(2)}) copy-start(f32[128,1280]{1,0:T(8,128)} %param.17) | copy-start | bytes 1966084
  21.5 4.9 %copy-start.32 = (f32[1280]{0:T(1024)S(1)}, f32[1280]{0:T(1024)}, u32[]{:S(2)}) copy-start(f32[1280]{0:T(1024)} %param.16) | copy-start | bytes 15364
  25.7 0.8 collective-permute-start.3
  26.6 2.0 %collective-permute-start.4 = (f32[10,64,128]{2,1,0:T(8,128)S(1)}, f32[10,64,128]{2,1,0:T(8,128)S(1)}, u32[]{:S(2)}, u32[]{:S(2)}) collective-permute-start(f32[10,64,128]{2,1,0:T(8,128)S(1)} %get-tuple-element.30), channel_id=1, source_target_pairs={{16,24},{20,28},{17,25},{21,29},{18,26},{22,30},{19,27},{23,31}} | collective-permute-start | bytes 983048 | tf_op jit(solution)/shard_map/ppermute | solution.py:59
  29.5 7.6 %collective-permute-start.5 = (f32[10,64,128]{2,1,0:T(8,128)}, f32[10,64,128]{2,1,0:T(8,128)S(1)}, u32[]{:S(2)}, u32[]{:S(2)}) collective-permute-start(f32[10,64,128]{2,1,0:T(8,128)} %get-tuple-element.46), channel_id=1, source_target_pairs={{0,4},{4,0},{8,12},{12,8},{16,20},{20,16},{24,28},{28,24},{1,5},{5... | collective-permute-start | bytes 983048 | tf_op jit(solution)/shard_map/ppermute | solution.py:82
  42.4 2.1 %collective-permute-start.6 = (f32[2,128]{1,0:T(2,128)S(1)}, f32[2,128]{1,0:T(2,128)S(1)}, u32[]{:S(2)}, u32[]{:S(2)}) collective-permute-start(f32[2,128]{1,0:T(2,128)S(1)} %pad_maximum_fusion), channel_id=1, source_target_pairs={{0,1},{1,0},{2,3},{3,2},{4,5},{5,4},{6,7},{7,6},{8,9},{9,8},{10,11... | collective-permute-start | bytes 3080 | tf_op jit(solution)/shard_map/ppermute | solution.py:96
  44.5 3.7 %copy-start.16 = (f32[128,640]{1,0:T(8,128)S(1)}, f32[128,640]{1,0:T(8,128)}, u32[]{:S(2)}) copy-start(f32[128,640]{1,0:T(8,128)} %get-tuple-element.28) | copy-start | bytes 983044
  44.6 3.6 %collective-permute-start.7 = (f32[2,128]{1,0:T(2,128)S(1)}, f32[2,128]{1,0:T(2,128)S(1)}, u32[]{:S(2)}, u32[]{:S(2)}) collective-permute-start(f32[2,128]{1,0:T(2,128)S(1)} %fusion.106), channel_id=1, source_target_pairs={{0,2},{1,3},{2,0},{3,1},{4,6},{5,7},{6,4},{7,5},{8,10},{9,11},{10,... | collective-permute-start | bytes 3080 | tf_op jit(solution)/shard_map/ppermute | solution.py:96
  49.8 4.2 %copy-start.7 = (f32[128,1280]{0,1:T(8,128)}, f32[128,1280]{0,1:T(8,128)S(1)}, u32[]{:S(2)}) copy-start(f32[128,1280]{0,1:T(8,128)S(1)} %copy.39) | copy-start | bytes 1966084
  55.2 9.3 %collective-permute-start.9 = (f32[10,64,128]{2,1,0:T(8,128)}, f32[10,64,128]{2,1,0:T(8,128)}, u32[]{:S(2)}, u32[]{:S(2)}) collective-permute-start(f32[10,64,128]{2,1,0:T(8,128)} %constant_dynamic-slice_fusion.4), channel_id=1, source_target_pairs={{28,24},{24,28},{20,16},{16,20},{12,8},{8,12},{4,0},{0,4},{29,25},... | collective-permute-start | bytes 983048 | tf_op jit(solution)/shard_map/ppermute | solution.py:42
  57.0 7.4 %copy-start.39 = (f32[10]{0:T(128)S(1)}, f32[10]{0:T(128)}, u32[]{:S(2)}) copy-start(f32[10]{0:T(128)} %get-tuple-element.24) | copy-start | bytes 124
  57.0 7.4 %copy-start.40 = (f32[10]{0:T(128)S(1)}, f32[10]{0:T(128)}, u32[]{:S(2)}) copy-start(f32[10]{0:T(128)} %get-tuple-element.26) | copy-start | bytes 124
  65.6 1.4 %collective-permute-start.10 = (f32[10,64,128]{2,1,0:T(8,128)S(1)}, f32[10,64,128]{2,1,0:T(8,128)S(1)}, u32[]{:S(2)}, u32[]{:S(2)}) collective-permute-start(f32[10,64,128]{2,1,0:T(8,128)S(1)} %get-tuple-element.22), channel_id=1, source_target_pairs={{28,20},{24,16},{29,21},{25,17},{30,22},{26,18},{31,23},{27,19}} | collective-permute-start | bytes 983048 | tf_op jit(solution)/shard_map/ppermute | solution.py:62
  67.1 1.3 %collective-permute-start.11 = (f32[10,64,128]{2,1,0:T(8,128)S(1)}, f32[10,64,128]{2,1,0:T(8,128)S(1)}, u32[]{:S(2)}, u32[]{:S(2)}) collective-permute-start(f32[10,64,128]{2,1,0:T(8,128)S(1)} %multiply_add_fusion.2), channel_id=1, source_target_pairs={{20,12},{16,8},{21,13},{17,9},{22,14},{18,10},{23,15},{19,11}} | collective-permute-start | bytes 983048 | tf_op jit(solution)/shard_map/ppermute | solution.py:62
  68.5 34.6 %collective-permute-start.12 = (f32[10,64,128]{2,1,0:T(8,128)S(1)}, f32[10,64,128]{2,1,0:T(8,128)S(1)}, u32[]{:S(2)}, u32[]{:S(2)}) collective-permute-start(f32[10,64,128]{2,1,0:T(8,128)S(1)} %get-tuple-element.20), channel_id=1, source_target_pairs={{12,4},{8,0},{13,5},{9,1},{14,6},{10,2},{15,7},{11,3}} | collective-permute-start | bytes 983048 | tf_op jit(solution)/shard_map/ppermute | solution.py:59
  70.9 32.2 %copy-start.38 = (f32[10]{0:T(128)S(1)}, f32[10]{0:T(128)}, u32[]{:S(2)}) copy-start(f32[10]{0:T(128)} %get-tuple-element.27) | copy-start | bytes 124
  70.9 34.2 %collective-permute-start.16 = (f32[128,128]{1,0:T(8,128)S(1)}, f32[128,128]{1,0:T(8,128)S(1)}, u32[]{:S(2)}, u32[]{:S(2)}) collective-permute-start(f32[128,128]{1,0:T(8,128)S(1)} %fusion.18), channel_id=1, source_target_pairs={{0,1},{1,0},{2,3},{3,2},{4,5},{5,4},{6,7},{7,6},{8,9},{9,8},{10,11... | collective-permute-start | bytes 196616 | tf_op jit(solution)/shard_map/ppermute | solution.py:96
  103.9 7.3 %collective-permute-start.13 = (f32[10,64,128]{2,1,0:T(8,128)}, f32[10,64,128]{2,1,0:T(8,128)S(1)}, u32[]{:S(2)}, u32[]{:S(2)}) collective-permute-start(f32[10,64,128]{2,1,0:T(8,128)} %add_select_fusion.1), channel_id=1, source_target_pairs={{28,24},{24,28},{20,16},{16,20},{12,8},{8,12},{4,0},{0,4},{29,25},... | collective-permute-start | bytes 983048 | tf_op jit(solution)/shard_map/ppermute | solution.py:82
  105.1 4.3 %collective-permute-start.17 = (f32[128,128]{1,0:T(8,128)S(1)}, f32[128,128]{1,0:T(8,128)S(1)}, u32[]{:S(2)}, u32[]{:S(2)}) collective-permute-start(f32[128,128]{1,0:T(8,128)S(1)} %add.234), channel_id=1, source_target_pairs={{0,2},{1,3},{2,0},{3,1},{4,6},{5,7},{6,4},{7,5},{8,10},{9,11},{10,... | collective-permute-start | bytes 196616 | tf_op jit(solution)/shard_map/ppermute | solution.py:96
  106.8 4.4 %copy-start.9 = (f32[20,64,128]{2,1,0:T(8,128)S(1)}, f32[20,64,128]{2,1,0:T(8,128)}, u32[]{:S(2)}) copy-start(f32[20,64,128]{2,1,0:T(8,128)} %maximum_select_fusion.2) | copy-start | bytes 1966084
  106.8 4.4 %copy-start.19 = (f32[10,64,128]{2,1,0:T(8,128)S(1)}, f32[10,64,128]{2,1,0:T(8,128)}, u32[]{:S(2)}) copy-start(f32[10,64,128]{2,1,0:T(8,128)} %copy-done.18) | copy-start | bytes 983044
  106.8 4.4 %copy-start.42 = (f32[10]{0:T(128)S(1)}, f32[10]{0:T(128)}, u32[]{:S(2)}) copy-start(f32[10]{0:T(128)} %copy-done.41) | copy-start | bytes 124
  116.4 2.3 %collective-permute-start.14 = (f32[128,128]{1,0:T(8,128)S(1)}, f32[128,128]{1,0:T(8,128)S(1)}, u32[]{:S(2)}, u32[]{:S(2)}) collective-permute-start(f32[128,128]{1,0:T(8,128)S(1)} %fusion.16), channel_id=1, source_target_pairs={{0,1},{1,0},{2,3},{3,2},{4,5},{5,4},{6,7},{7,6},{8,9},{9,8},{10,11... | collective-permute-start | bytes 196616 | tf_op jit(solution)/shard_map/ppermute | solution.py:96
  118.7 4.6 %collective-permute-start.15 = (f32[128,128]{1,0:T(8,128)S(1)}, f32[128,128]{1,0:T(8,128)S(1)}, u32[]{:S(2)}, u32[]{:S(2)}) collective-permute-start(f32[128,128]{1,0:T(8,128)S(1)} %add.230), channel_id=1, source_target_pairs={{0,2},{1,3},{2,0},{3,1},{4,6},{5,7},{6,4},{7,5},{8,10},{9,11},{10,... | collective-permute-start | bytes 196616 | tf_op jit(solution)/shard_map/ppermute | solution.py:96
  (33 other events, 61.9 us)

commit v19 on v17

--- a/solution.py
+++ b/solution.py
@@ -271,11 +271,21 @@
             decay_h = lax.dynamic_slice_in_dim(log_decay, start, half, 0)
             state_h = lax.dynamic_slice_in_dim(state_in, start, half, 0)
             _, pull_h = jax.vjp(
-                lambda f, s, d, w: end_part(f, s, d, w, state_h),
-                feat_h, step_h, decay_h, write_keys,
+                lambda f, s, d: end_part(f, s, d, write_keys, state_h),
+                feat_h, step_h, decay_h,
             )
             return pull_h(grad_half)
 
+        def write_half(start, grad_half):
+            wi_h = lax.dynamic_slice_in_dim(weighted_in, start, half, 1)
+            return jnp.dot(
+                wi_h.reshape(length, -1), grad_half.reshape(-1, grad_half.shape[2]),
+                precision=highest,
+            )
+
+        write_part = gw_w + (write_half(own_start, sg_keep) + write_half(send_start, sg_other))
+        grad_write = butterfly_psum(write_part, "head")
+        sg_keep, sg_other, write_part = lax.optimization_barrier((sg_keep, sg_other, write_part))
         own = end_half(own_start, sg_keep)
         rest = end_half(send_start, sg_other)
 
@@ -287,11 +297,9 @@
         gf_e = join(own[0], rest[0], 1)
         gs_e = join(own[1], rest[1], 0)
         gd_e = join(own[2], rest[2], 0)
-        gw_e = own[3] + rest[3]
         grad_features = gf_w + gf_e
         grad_steps = gs_w + gs_e
         grad_decay = gd_w + gd_c + gd_e
-        grad_write = butterfly_psum(gw_w + gw_e, "head")
     else:
         state_grad = pair_scan(decay_total, local_grad, "seq", True)
         grad_features, grad_steps, grad_decay, grad_write, grad_read = pullback(

time: 115 us -> 119 us (1.035)
  other arithmetic: 11.6 us -> 13.8 us
    select_n x2, other arithmetic: 0.26 us -> 2.71 us  [pair_scan(): send = jnp.where(first, with_lead_own, s_g)]
  transfers between devices with their start and end apart: 18 -> 18, of which waited for: 10 -> 10; matrix products, arithmetic and copies ran while one was open for 19% -> 22% of each run, Pallas kernels for 0% -> 0%
where the time goes in v19:
time: 119 us
  waiting for transfers between devices  57 us (48%)
  starting transfers between devices  20.3 us (17%)
  matrix products  15.7 us (13%)
  other arithmetic  13.8 us (12%)
  local copies, waits for them, and re-layouts  10.6 us (9%)
  between operations  1.25 us (1%)
    ppermute x2, waiting for transfers between devices, pair_scan(): s_in = lax.ppermute(out[1], axis, pairs)  27.8 us
    ppermute x4, waiting for transfers between devices, pair_scan(): a_rcv, s_rcv = lax.ppermute((a_snd, s_snd), axis, swap)  11.8 us
    ppermute x4, starting transfers between devices, pair_scan(): a_in, s_in = lax.ppermute(out, axis, pairs)  6.39 us
    ppermute x6, waiting for transfers between devices, butterfly_psum(): got = lax.ppermute(parts, axis, [(i, i ^ k) for i in range(count)])  6 us
    dot_general x3, matrix products, within_part(): within = jnp.einsum('hij,jhp->ihp', masked, scaled, precision=highest)  5.89 us
    ppermute x2, waiting for transfers between devices, pair_scan(): other = lax.ppermute(send, axis, swap)  5.74 us
    ppermute x4, waiting for transfers between devices, pair_scan(): a_in, s_in = lax.ppermute(out, axis, pairs)  5.66 us
    ppermute x4, starting transfers between devices, pair_scan(): a_rcv, s_rcv = lax.ppermute((a_snd, s_snd), axis, swap)  5.56 us
  transfers between devices with their start and end apart: 18, of which 10 were waited for; matrix products, arithmetic and copies ran while one was open for 22% of the time, Pallas kernels for 0%

profile of v19, /device:TPU:0, one launch (start us, length us, event | category | flops | bytes accessed | tf_op | source)
XLA Modules:
  0.0 118.7 jit_solution(17985836471105056725)
XLA Ops:
  1.8 2.9 %collective-permute-start.8 = (f32[10]{0:T(128)S(1)}, f32[10]{0:T(128)S(1)}, u32[]{:S(2)}, u32[]{:S(2)}) collective-permute-start(f32[10]{0:T(128)S(1)} %dynamic_slice.59), channel_id=1, source_target_pairs={{28,24},{24,28},{20,16},{16,20},{12,8},{8,12},{4,0},{0,4},{29,25},... | collective-permute-start | bytes 128 | tf_op jit(solution)/shard_map/ppermute | solution.py:42
  4.8 1.3 %copy.30 = f32[128,1280]{0,1:T(8,128)S(1)} copy(f32[128,1280]{1,0:T(8,128)} %param.9) | data formatting | bytes 1310720 | tf_op args[0]
  8.3 2.0 %collective-permute-start = (f32[10]{0:T(128)S(1)}, f32[10]{0:T(128)S(1)}, u32[]{:S(2)}, u32[]{:S(2)}) collective-permute-start(f32[10]{0:T(128)S(1)} %get-tuple-element.59), channel_id=1, source_target_pairs={{0,4},{4,0},{8,12},{12,8},{16,20},{20,16},{24,28},{28,24},{1,5},{5... | collective-permute-start | bytes 128 | tf_op jit(solution)/shard_map/ppermute | solution.py:42
  10.3 6.6 %collective-permute-done = f32[10]{0:T(128)S(1)} collective-permute-done((f32[10]{0:T(128)S(1)}, f32[10]{0:T(128)S(1)}, u32[]{:S(2)}, u32[]{:S(2)}) %collective-permute-start) | collective-permute-done | bytes 72 | tf_op jit(solution)/shard_map/ppermute | solution.py:42
  17.1 3.5 %collective-permute-start.2 = (f32[10,64,128]{2,1,0:T(8,128)S(1)}, f32[10,64,128]{2,1,0:T(8,128)S(1)}, u32[]{:S(2)}, u32[]{:S(2)}) collective-permute-start(f32[10,64,128]{2,1,0:T(8,128)S(1)} %get-tuple-element.32), channel_id=1, source_target_pairs={{0,8},{4,12},{1,9},{5,13},{2,10},{6,14},{3,11},{7,15}} | collective-permute-start | bytes 983048 | tf_op jit(solution)/shard_map/ppermute | solution.py:62
  20.6 5.7 %collective-permute-done.2 = f32[10,64,128]{2,1,0:T(8,128)S(1)} collective-permute-done((f32[10,64,128]{2,1,0:T(8,128)S(1)}, f32[10,64,128]{2,1,0:T(8,128)S(1)}, u32[]{:S(2)}, u32[]{:S(2)}) %collective-permute-start.2) | collective-permute-done | bytes 327712 | tf_op jit(solution)/shard_map/ppermute | solution.py:62
  26.4 1.4 %collective-permute-start.3 = (f32[10,64,128]{2,1,0:T(8,128)S(1)}, f32[10,64,128]{2,1,0:T(8,128)}, u32[]{:S(2)}, u32[]{:S(2)}) collective-permute-start(f32[10,64,128]{2,1,0:T(8,128)S(1)} %multiply_add_fusion.4), channel_id=1, source_target_pairs={{8,16},{12,20},{9,17},{13,21},{10,18},{14,22},{11,19},{15,23}} | collective-permute-start | bytes 983048 | tf_op jit(solution)/shard_map/ppermute | solution.py:62
  29.5 0.9 add_select_fusion.3
  31.0 1.5 %fusion.9 = f32[128,20,64]{0,2,1:T(8,128)S(1)} fusion(f32[128,20,64]{0,2,1:T(8,128)S(1)} %bitcast.124, f32[128,128]{1,0:T(8,128)S(1)} %fusion.96, f32[20,128]{1,0:T(8,128)S(1)} %bitcast.135, pred[128,128]{1,0:T(8,128)(4,1)S(1)} %iota_compare_fusion.10, f32[128,20]{0,1:T(8,128)S(1)} %bitcast.139, f32[20]{0:T(128)S(1)} %copy-done.22), kind=kOutput, calls=%fused_computation.9 | convolution fusion | flops 127631360 | bytes 1413200 | tf_op jit(solution)/shard_map/jvp(hij,jhp->ihp)/dot_general | solution.py:169
  32.7 5.2 %collective-permute-done.5 = f32[10,64,128]{2,1,0:T(8,128)S(1)} collective-permute-done((f32[10,64,128]{2,1,0:T(8,128)}, f32[10,64,128]{2,1,0:T(8,128)S(1)}, u32[]{:S(2)}, u32[]{:S(2)}) %collective-permute-start.5) | collective-permute-done | bytes 327712 | tf_op jit(solution)/shard_map/ppermute | solution.py:82
  37.9 1.3 %broadcast_multiply_fusion = (f32[128,20,64]{0,2,1:T(8,128)S(1)}, f32[128,20,64]{0,2,1:T(8,128)}) fusion(f32[128,20]{0,1:T(8,128)S(1)} %get-tuple-element.53, f32[20,64,128]{2,1,0:T(8,128)S(1)} %maximum_select_fusion, f32[128,128]{1,0:T(8,128)S(1)} %copy-done), kind=kOutput, calls=%fused_computation.70 | convolution fusion | flops 125992960 | bytes 2041856 | tf_op jit(solution)/shard_map/jvp(in,hpn->ihp)/dot_general | solution.py:176
  39.9 1.7 %multiply_reduce_fusion.4 = (f32[128]{0:T(128)S(1)}, f32[128]{0:T(128)S(1)}, f32[128,1280]{1,0:T(8,128)S(1)}) fusion(f32[128,1280]{1,0:T(8,128)} %param.10, f32[128,1280]{1,0:T(8,128)} %param.17, f32[1280]{0:T(1024)S(1)} %copy-done.12, f32[128,1280]{1,0:T(8,128)S(1)} %copy.31, f32[128,1280]{1,0:T(8,128)S(1)} %copy.32), kind=kLoop, calls=%fused_computation.34 | loop fusion | flops 1801984 | bytes 3282944 | tf_op jit(solution)/shard_map/reduce_sum | solution.py:246
  41.8 1.1 collective-permute-done.6
  42.9 1.6 %collective-permute-start.7 = (f32[2,128]{1,0:T(2,128)S(1)}, f32[2,128]{1,0:T(2,128)S(1)}, u32[]{:S(2)}, u32[]{:S(2)}) collective-permute-start(f32[2,128]{1,0:T(2,128)S(1)} %fusion.92), channel_id=1, source_target_pairs={{0,2},{1,3},{2,0},{3,1},{4,6},{5,7},{6,4},{7,5},{8,10},{9,11},{10,... | collective-permute-start | bytes 3080 | tf_op jit(solution)/shard_map/ppermute | solution.py:96
  44.5 2.0 %collective-permute-done.7 = f32[2,128]{1,0:T(2,128)S(1)} collective-permute-done((f32[2,128]{1,0:T(2,128)S(1)}, f32[2,128]{1,0:T(2,128)S(1)}, u32[]{:S(2)}, u32[]{:S(2)}) %collective-permute-start.7) | collective-permute-done | bytes 1056 | tf_op jit(solution)/shard_map/ppermute | solution.py:96
  46.6 1.3 %add_multiply_fusion = (f32[128,1280]{1,0:T(8,128)}, f32[128,1280]{1,0:T(8,128)S(1)}) fusion(f32[128,1280]{1,0:T(8,128)S(1)} %copy-done.4, f32[128,1280]{1,0:T(8,128)S(1)} %get-tuple-element.29, f32[128]{0:T(128)S(1)} %fusion.82, f32[128,1280]{1,0:T(8,128)S(1)} %copy-done.5, f32[128]{0:T(128)S(1)} %rsqrt_bitcast_fusion, f32[1280]{0:T(1024)S(1)} %copy-done.12), kind=kLoop, calls=%fused_computation.30 | loop fusion | flops 2621440 | bytes 3282944 | tf_op jit(solution)/shard_map/mul | solution.py:255
  49.8 0.9 constant_dynamic-slice_fusion.1
  50.7 1.1 copy.39
  51.9 1.1 copy.40
  53.0 5.2 %collective-permute-done.9 = f32[10,64,128]{2,1,0:T(8,128)} collective-permute-done((f32[10,64,128]{2,1,0:T(8,128)}, f32[10,64,128]{2,1,0:T(8,128)}, u32[]{:S(2)}, u32[]{:S(2)}) %collective-permute-start.9) | collective-permute-done | bytes 327712 | tf_op jit(solution)/shard_map/ppermute | solution.py:42
  58.2 1.1 broadcast_add_fusion
  63.1 2.0 %fusion.20 = (f32[20,128]{1,0:T(8,128)S(1)}, f32[20,128]{1,0:T(8,128)S(1)}, f32[128,128]{1,0:T(8,128)S(1)}) fusion(f32[128,128]{1,0:T(8,128)S(1)} %fusion.96, f32[20,128]{1,0:T(8,128)S(1)} %bitcast.136, pred[128,128]{1,0:T(8,128)(4,1)S(1)} %iota_compare_fusion.10, f32[20,64,128]{2,1,0:T(8,128)S(1)} %bitcast.119, f32[128,20,64]{0,2,1:T(8,128)S(1)} %bitcast.125, ...), kind=kOutput, calls=%fused_computation.24 | convolution fusion | flops 129575936 | bytes 1499136 | tf_op jit(solution)/shard_map/transpose(jvp(hij,jhp->ihp))/dot_general | solution.py:169
  65.4 1.6 %collective-permute-start.12 = (f32[10,64,128]{2,1,0:T(8,128)S(1)}, f32[10,64,128]{2,1,0:T(8,128)S(1)}, u32[]{:S(2)}, u32[]{:S(2)}) collective-permute-start(f32[10,64,128]{2,1,0:T(8,128)S(1)} %get-tuple-element.21), channel_id=1, source_target_pairs={{12,4},{8,0},{13,5},{9,1},{14,6},{10,2},{15,7},{11,3}} | collective-permute-start | bytes 983048 | tf_op jit(solution)/shard_map/ppermute | solution.py:59
  67.8 2.5 %multiply_reduce_fusion.1 = (f32[128,20]{0,1:T(8,128)}, f32[128,20,64]{0,2,1:T(8,128)}, f32[128,20]{0,1:T(8,128)}) fusion(f32[128,20,64]{0,2,1:T(8,128)S(1)} %copy-done.7, f32[128,20,64]{0,2,1:T(8,128)S(1)} %bitcast.121, f32[128,20]{0,1:T(8,128)S(1)} %bitcast.141, f32[20]{0:T(128)S(1)} %copy-done.23, f32[128,20,64]{0,2,1:T(8,128)S(1)} %bitcast.126, ...), kind=kOutput, calls=%fused_computation.28 | convolution fusion | flops 128281600 | bytes 3399760 | tf_op jit(solution)/shard_map/transpose(jvp(hij,jhp->ihp))/dot_general | solution.py:169
  70.3 27.8 %collective-permute-done.12 = f32[10,64,128]{2,1,0:T(8,128)S(1)} collective-permute-done((f32[10,64,128]{2,1,0:T(8,128)S(1)}, f32[10,64,128]{2,1,0:T(8,128)S(1)}, u32[]{:S(2)}, u32[]{:S(2)}) %collective-permute-start.12) | collective-permute-done | bytes 327712 | tf_op jit(solution)/shard_map/ppermute | solution.py:59
  98.1 1.8 %add_select_fusion = (f32[10,64,128]{2,1,0:T(8,128)}, f32[10,64,128]{2,1,0:T(8,128)S(1)}) fusion(f32[20,64,128]{2,1,0:T(8,128)S(1)} %fusion.34, s32[]{:T(128)S(6)} %select_n.214, f32[10]{0:T(128)S(1)} %copy-done.21, pred[]{:T(512)S(6)} %eq.31, f32[10,64,128]{2,1,0:T(8,128)S(1)} %collective-permute-done.12, f32[10,64,128]{2,1,0:T(8,128)S(1)} %get-tuple-element.22, ...), kind=kLoop, calls=%fused_computation.62 | loop fusion | flops 573440 | bytes 1966166 | tf_op jit(solution)/shard_map/jit(_where)/select_n | solution.py:80
  100.8 1.6 %collective-permute-start.17 = (f32[128,128]{1,0:T(8,128)S(1)}, f32[128,128]{1,0:T(8,128)}, u32[]{:S(2)}, u32[]{:S(2)}) collective-permute-start(f32[128,128]{1,0:T(8,128)S(1)} %add.180), channel_id=1, source_target_pairs={{0,2},{1,3},{2,0},{3,1},{4,6},{5,7},{6,4},{7,5},{8,10},{9,11},{10,... | collective-permute-start | bytes 196616 | tf_op jit(solution)/shard_map/ppermute | solution.py:96
  103.2 1.3 %copy.38 = f32[128,1280]{1,0:T(8,128)S(1)} copy(f32[128,1280]{0,1:T(8,128)} %bitcast.132) | data formatting | bytes 1310720 | tf_op jit(solution)/shard_map/transpose(jvp())/reshape | solution.py:166
  105.2 1.5 %add.181 = f32[128,128]{1,0:T(8,128)} add(f32[128,128]{1,0:T(8,128)S(1)} %add.180, f32[128,128]{1,0:T(8,128)} %collective-permute-done.17) | non-fusion elementwise | flops 16384 | bytes 196608 | tf_op jit(solution)/shard_map/add | solution.py:97
  112.0 0.9 fusion.21
  113.7 1.6 %collective-permute-start.15 = (f32[128,128]{1,0:T(8,128)S(1)}, f32[128,128]{1,0:T(8,128)S(1)}, u32[]{:S(2)}, u32[]{:S(2)}) collective-permute-start(f32[128,128]{1,0:T(8,128)S(1)} %add.177), channel_id=1, source_target_pairs={{0,2},{1,3},{2,0},{3,1},{4,6},{5,7},{6,4},{7,5},{8,10},{9,11},{10,... | collective-permute-start | bytes 196616 | tf_op jit(solution)/shard_map/ppermute | solution.py:96
  115.9 2.1 %collective-permute-done.15 = f32[128,128]{1,0:T(8,128)S(1)} collective-permute-done((f32[128,128]{1,0:T(8,128)S(1)}, f32[128,128]{1,0:T(8,128)S(1)}, u32[]{:S(2)}, u32[]{:S(2)}) %collective-permute-start.15) | collective-permute-done | bytes 65568 | tf_op jit(solution)/shard_map/ppermute | solution.py:96
  (129 shorter events, 23.3 us)
Async XLA Ops:
  0.6 28.7 %copy-start = (f32[128,128]{1,0:T(8,128)S(1)}, f32[128,128]{1,0:T(8,128)}, u32[]{:S(2)}) copy-start(f32[128,128]{1,0:T(8,128)} %param.12) | copy-start | bytes 196612
  1.8 5.9 %collective-permute-start.8 = (f32[10]{0:T(128)S(1)}, f32[10]{0:T(128)S(1)}, u32[]{:S(2)}, u32[]{:S(2)}) collective-permute-start(f32[10]{0:T(128)S(1)} %dynamic_slice.59), channel_id=1, source_target_pairs={{28,24},{24,28},{20,16},{16,20},{12,8},{8,12},{4,0},{0,4},{29,25},... | collective-permute-start | bytes 128 | tf_op jit(solution)/shard_map/ppermute | solution.py:42
  6.2 24.8 %copy-start.2 = (f32[128,1280]{0,1:T(8,128)}, f32[128,1280]{0,1:T(8,128)S(1)}, u32[]{:S(2)}) copy-start(f32[128,1280]{0,1:T(8,128)S(1)} %copy.30) | copy-start | bytes 1966084
  7.6 9.4 %collective-permute-start.1 = (f32[10,64,128]{2,1,0:T(8,128)S(1)}, f32[10,64,128]{2,1,0:T(8,128)S(1)}, u32[]{:S(2)}, u32[]{:S(2)}) collective-permute-start(f32[10,64,128]{2,1,0:T(8,128)S(1)} %constant_dynamic-slice_fusion.3), channel_id=1, source_target_pairs={{0,4},{4,0},{8,12},{12,8},{16,20},{20,16},{24,28},{28,24},{1,5},{5... | collective-permute-start | bytes 983048 | tf_op jit(solution)/shard_map/ppermute | solution.py:42
  7.7 9.4 %copy-start.19 = (f32[10]{0:T(128)}, f32[10]{0:T(128)S(1)}, u32[]{:S(2)}) copy-start(f32[10]{0:T(128)S(1)} %collective-permute-done.8) | copy-start | bytes 124
  8.3 8.6 %collective-permute-start = (f32[10]{0:T(128)S(1)}, f32[10]{0:T(128)S(1)}, u32[]{:S(2)}, u32[]{:S(2)}) collective-permute-start(f32[10]{0:T(128)S(1)} %get-tuple-element.59), channel_id=1, source_target_pairs={{0,4},{4,0},{8,12},{12,8},{16,20},{20,16},{24,28},{28,24},{1,5},{5... | collective-permute-start | bytes 128 | tf_op jit(solution)/shard_map/ppermute | solution.py:42
  17.1 9.2 %collective-permute-start.2 = (f32[10,64,128]{2,1,0:T(8,128)S(1)}, f32[10,64,128]{2,1,0:T(8,128)S(1)}, u32[]{:S(2)}, u32[]{:S(2)}) collective-permute-start(f32[10,64,128]{2,1,0:T(8,128)S(1)} %get-tuple-element.32), channel_id=1, source_target_pairs={{0,8},{4,12},{1,9},{5,13},{2,10},{6,14},{3,11},{7,15}} | collective-permute-start | bytes 983048 | tf_op jit(solution)/shard_map/ppermute | solution.py:62
  26.4 1.4 %collective-permute-start.3 = (f32[10,64,128]{2,1,0:T(8,128)S(1)}, f32[10,64,128]{2,1,0:T(8,128)}, u32[]{:S(2)}, u32[]{:S(2)}) collective-permute-start(f32[10,64,128]{2,1,0:T(8,128)S(1)} %multiply_add_fusion.4), channel_id=1, source_target_pairs={{8,16},{12,20},{9,17},{13,21},{10,18},{14,22},{11,19},{15,23}} | collective-permute-start | bytes 983048 | tf_op jit(solution)/shard_map/ppermute | solution.py:62
  28.6 0.9 collective-permute-start.4
  29.5 1.5 %copy-start.22 = (f32[20]{0:T(128)S(1)}, f32[20]{0:T(128)}, u32[]{:S(2)}) copy-start(f32[20]{0:T(128)} %param.15) | copy-start | bytes 244
  30.4 7.5 %collective-permute-start.5 = (f32[10,64,128]{2,1,0:T(8,128)}, f32[10,64,128]{2,1,0:T(8,128)S(1)}, u32[]{:S(2)}, u32[]{:S(2)}) collective-permute-start(f32[10,64,128]{2,1,0:T(8,128)} %get-tuple-element.47), channel_id=1, source_target_pairs={{0,4},{4,0},{8,12},{12,8},{16,20},{20,16},{24,28},{28,24},{1,5},{5... | collective-permute-start | bytes 983048 | tf_op jit(solution)/shard_map/ppermute | solution.py:82
  39.9 6.6 %copy-start.4 = (f32[128,1280]{1,0:T(8,128)S(1)}, f32[128,1280]{1,0:T(8,128)}, u32[]{:S(2)}) copy-start(f32[128,1280]{1,0:T(8,128)} %param.10) | copy-start | bytes 1966084
  39.9 6.7 %copy-start.5 = (f32[128,1280]{1,0:T(8,128)S(1)}, f32[128,1280]{1,0:T(8,128)}, u32[]{:S(2)}) copy-start(f32[128,1280]{1,0:T(8,128)} %param.17) | copy-start | bytes 1966084
  41.7 1.2 %collective-permute-start.6 = (f32[2,128]{1,0:T(2,128)S(1)}, f32[2,128]{1,0:T(2,128)S(1)}, u32[]{:S(2)}, u32[]{:S(2)}) collective-permute-start(f32[2,128]{1,0:T(2,128)S(1)} %pad_maximum_fusion), channel_id=1, source_target_pairs={{0,1},{1,0},{2,3},{3,2},{4,5},{5,4},{6,7},{7,6},{8,9},{9,8},{10,11... | collective-permute-start | bytes 3080 | tf_op jit(solution)/shard_map/ppermute | solution.py:96
  42.9 3.6 %collective-permute-start.7 = (f32[2,128]{1,0:T(2,128)S(1)}, f32[2,128]{1,0:T(2,128)S(1)}, u32[]{:S(2)}, u32[]{:S(2)}) collective-permute-start(f32[2,128]{1,0:T(2,128)S(1)} %fusion.92), channel_id=1, source_target_pairs={{0,2},{1,3},{2,0},{3,1},{4,6},{5,7},{6,4},{7,5},{8,10},{9,11},{10,... | collective-permute-start | bytes 3080 | tf_op jit(solution)/shard_map/ppermute | solution.py:96
  49.3 8.9 %collective-permute-start.9 = (f32[10,64,128]{2,1,0:T(8,128)}, f32[10,64,128]{2,1,0:T(8,128)}, u32[]{:S(2)}, u32[]{:S(2)}) collective-permute-start(f32[10,64,128]{2,1,0:T(8,128)} %constant_dynamic-slice_fusion.2), channel_id=1, source_target_pairs={{28,24},{24,28},{20,16},{16,20},{12,8},{8,12},{4,0},{0,4},{29,25},... | collective-permute-start | bytes 983048 | tf_op jit(solution)/shard_map/ppermute | solution.py:42
  50.7 7.5 %copy-start.18 = (f32[10]{0:T(128)S(1)}, f32[10]{0:T(128)}, u32[]{:S(2)}) copy-start(f32[10]{0:T(128)} %get-tuple-element.27) | copy-start | bytes 124
  58.2 1.9 %copy-start.16 = (f32[20,128]{1,0:T(8,128)S(1)}, f32[20,128]{1,0:T(8,128)}, u32[]{:S(2)}) copy-start(f32[20,128]{1,0:T(8,128)} %param.14) | copy-start | bytes 30724
  59.3 3.7 %copy-start.3 = (f32[128,1280]{0,1:T(8,128)S(1)}, f32[128,1280]{0,1:T(8,128)}, u32[]{:S(2)}) copy-start(f32[128,1280]{0,1:T(8,128)} %copy-done.2) | copy-start | bytes 1966084
  59.3 2.9 %collective-permute-start.10 = (f32[10,64,128]{2,1,0:T(8,128)S(1)}, f32[10,64,128]{2,1,0:T(8,128)S(1)}, u32[]{:S(2)}, u32[]{:S(2)}) collective-permute-start(f32[10,64,128]{2,1,0:T(8,128)S(1)} %get-tuple-element.23), channel_id=1, source_target_pairs={{28,20},{24,16},{29,21},{25,17},{30,22},{26,18},{31,23},{27,19}} | collective-permute-start | bytes 983048 | tf_op jit(solution)/shard_map/ppermute | solution.py:62
  62.4 2.8 %collective-permute-start.11 = (f32[10,64,128]{2,1,0:T(8,128)S(1)}, f32[10,64,128]{2,1,0:T(8,128)S(1)}, u32[]{:S(2)}, u32[]{:S(2)}) collective-permute-start(f32[10,64,128]{2,1,0:T(8,128)S(1)} %multiply_add_fusion.2), channel_id=1, source_target_pairs={{20,12},{16,8},{21,13},{17,9},{22,14},{18,10},{23,15},{19,11}} | collective-permute-start | bytes 983048 | tf_op jit(solution)/shard_map/ppermute | solution.py:62
  65.3 2.4 %copy-start.7 = (f32[128,20,64]{0,2,1:T(8,128)S(1)}, f32[128,20,64]{0,2,1:T(8,128)}, u32[]{:S(2)}) copy-start(f32[128,20,64]{0,2,1:T(8,128)} %get-tuple-element.61) | copy-start | bytes 1966084
  65.3 2.4 %copy-start.23 = (f32[20]{0:T(128)S(1)}, f32[20]{0:T(128)}, u32[]{:S(2)}) copy-start(f32[20]{0:T(128)} %param.15) | copy-start | bytes 244
  65.4 32.7 %collective-permute-start.12 = (f32[10,64,128]{2,1,0:T(8,128)S(1)}, f32[10,64,128]{2,1,0:T(8,128)S(1)}, u32[]{:S(2)}, u32[]{:S(2)}) collective-permute-start(f32[10,64,128]{2,1,0:T(8,128)S(1)} %get-tuple-element.21), channel_id=1, source_target_pairs={{12,4},{8,0},{13,5},{9,1},{14,6},{10,2},{15,7},{11,3}} | collective-permute-start | bytes 983048 | tf_op jit(solution)/shard_map/ppermute | solution.py:59
  67.7 33.1 %collective-permute-start.16 = (f32[128,128]{1,0:T(8,128)S(1)}, f32[128,128]{1,0:T(8,128)S(1)}, u32[]{:S(2)}, u32[]{:S(2)}) collective-permute-start(f32[128,128]{1,0:T(8,128)S(1)} %fusion.17), channel_id=1, source_target_pairs={{0,1},{1,0},{2,3},{3,2},{4,5},{5,4},{6,7},{7,6},{8,9},{9,8},{10,11... | collective-permute-start | bytes 196616 | tf_op jit(solution)/shard_map/ppermute | solution.py:96
  67.8 30.3 %copy-start.20 = (f32[10]{0:T(128)S(1)}, f32[10]{0:T(128)}, u32[]{:S(2)}) copy-start(f32[10]{0:T(128)} %copy-done.19) | copy-start | bytes 124
  67.8 30.3 %copy-start.21 = (f32[10]{0:T(128)S(1)}, f32[10]{0:T(128)}, u32[]{:S(2)}) copy-start(f32[10]{0:T(128)} %get-tuple-element.28) | copy-start | bytes 124
  99.9 7.3 %collective-permute-start.13 = (f32[10,64,128]{2,1,0:T(8,128)}, f32[10,64,128]{2,1,0:T(8,128)S(1)}, u32[]{:S(2)}, u32[]{:S(2)}) collective-permute-start(f32[10,64,128]{2,1,0:T(8,128)} %get-tuple-element.45), channel_id=1, source_target_pairs={{28,24},{24,28},{20,16},{16,20},{12,8},{8,12},{4,0},{0,4},{29,25},... | collective-permute-start | bytes 983048 | tf_op jit(solution)/shard_map/ppermute | solution.py:82
  100.8 4.4 %collective-permute-start.17 = (f32[128,128]{1,0:T(8,128)S(1)}, f32[128,128]{1,0:T(8,128)}, u32[]{:S(2)}, u32[]{:S(2)}) collective-permute-start(f32[128,128]{1,0:T(8,128)S(1)} %add.180), channel_id=1, source_target_pairs={{0,2},{1,3},{2,0},{3,1},{4,6},{5,7},{6,4},{7,5},{8,10},{9,11},{10,... | collective-permute-start | bytes 196616 | tf_op jit(solution)/shard_map/ppermute | solution.py:96
  108.2 5.5 %collective-permute-start.14 = (f32[128,128]{1,0:T(8,128)S(1)}, f32[128,128]{1,0:T(8,128)S(1)}, u32[]{:S(2)}, u32[]{:S(2)}) collective-permute-start(f32[128,128]{1,0:T(8,128)S(1)} %fusion.16), channel_id=1, source_target_pairs={{0,1},{1,0},{2,3},{3,2},{4,5},{5,4},{6,7},{7,6},{8,9},{9,8},{10,11... | collective-permute-start | bytes 196616 | tf_op jit(solution)/shard_map/ppermute | solution.py:96
  111.9 3.4 %copy-start.17 = (f32[128,20]{0,1:T(8,128)S(1)}, f32[128,20]{0,1:T(8,128)}, u32[]{:S(2)}) copy-start(f32[128,20]{0,1:T(8,128)} %get-tuple-element.42) | copy-start | bytes 30724
  113.7 4.3 %collective-permute-start.15 = (f32[128,128]{1,0:T(8,128)S(1)}, f32[128,128]{1,0:T(8,128)S(1)}, u32[]{:S(2)}, u32[]{:S(2)}) collective-permute-start(f32[128,128]{1,0:T(8,128)S(1)} %add.177), channel_id=1, source_target_pairs={{0,2},{1,3},{2,0},{3,1},{4,6},{5,7},{6,4},{7,5},{8,10},{9,11},{10,... | collective-permute-start | bytes 196616 | tf_op jit(solution)/shard_map/ppermute | solution.py:96
  (10 other events, 9.9 us)

commit v20 on v17

--- a/solution.py
+++ b/solution.py
@@ -50,19 +50,16 @@
         ]
 
     if groups <= 4:
-        a_g = jnp.ones_like(a_tot)
+        got = None
         s_g = jnp.zeros_like(s_tot)
         for r in range(groups - 1):
-            out = combine((a_g, s_g), (a_tot, s_tot))
+            out = (a_tot, s_tot) if got is None else combine(got, (a_tot, s_tot))
             pairs = [(phys(2 * r + x), phys(2 * (r + 1) + x)) for x in (0, 1)]
             if r == groups - 2:
-                s_in = lax.ppermute(out[1], axis, pairs)
-                a_in = a_g
+                got = (a_tot, lax.ppermute(out[1], axis, pairs))
             else:
-                a_in, s_in = lax.ppermute(out, axis, pairs)
-            dst = group == r + 1
-            a_g = jnp.where(dst, a_in, a_g)
-            s_g = jnp.where(dst, s_in, s_g)
+                got = lax.ppermute(out, axis, pairs)
+            s_g = jnp.where(group == r + 1, got[1], s_g)
     else:
         a_g, s_g = lax.ppermute((a_tot, s_tot), axis, shift_pairs(1))
         a_g = jnp.where(group == 0, 1.0, a_g)

time: 115 us -> 117 us (1.017)
  waiting for transfers between devices: 56.5 us -> 60.4 us
  matrix products: 15.8 us -> 13.3 us
    ppermute x6, waiting for transfers between devices: 33 us -> 35.4 us  [the longest x2 29.7 us: pair_scan(): got = (a_tot, lax.ppermute(out[1], axis, pairs))]
    dot_general x9, matrix products: 4.75 us -> 2.9 us  [prefix_sum(): return jnp.dot(decay_in, upper, precision=lax.Precision.HIGHEST)]
  transfers between devices with their start and end apart: 18 -> 18, of which waited for: 10 -> 10; matrix products, arithmetic and copies ran while one was open for 19% -> 16% of each run, Pallas kernels for 0% -> 0%
where the time goes in v20:
time: 117 us; the launch traced here: 116 us
  waiting for transfers between devices  60.4 us (52%)
  starting transfers between devices  19.5 us (17%)
  matrix products  13.3 us (11%)
  other arithmetic  12.6 us (11%)
  local copies, waits for them, and re-layouts  8.87 us (8%)
  between operations  1.25 us (1%)
    ppermute x2, waiting for transfers between devices, pair_scan(): got = (a_tot, lax.ppermute(out[1], axis, pairs))  29.7 us
    ppermute x4, waiting for transfers between devices, pair_scan(): a_rcv, s_rcv = lax.ppermute((a_snd, s_snd), axis, swap)  11.8 us
    ppermute x6, waiting for transfers between devices, butterfly_psum(): got = lax.ppermute(parts, axis, [(i, i ^ k) for i in range(count)])  6.72 us
    ppermute x2, waiting for transfers between devices, pair_scan(): other = lax.ppermute(send, axis, swap)  6.53 us
    ppermute x4, waiting for transfers between devices, pair_scan(): got = lax.ppermute(out, axis, pairs)  5.68 us
    ppermute x4, starting transfers between devices, pair_scan(): a_rcv, s_rcv = lax.ppermute((a_snd, s_snd), axis, swap)  5.55 us
    ppermute x4, starting transfers between devices, pair_scan(): got = lax.ppermute(out, axis, pairs)  5.54 us
    dot_general x3, matrix products, within_part(): within = jnp.einsum('hij,jhp->ihp', masked, scaled, precision=highest)  5.27 us
  transfers between devices with their start and end apart: 18, of which 10 were waited for; matrix products, arithmetic and copies ran while one was open for 16% of the time, Pallas kernels for 0%

profile of v20, /device:TPU:0, one launch (start us, length us, event | category | flops | bytes accessed | tf_op | source)
XLA Modules:
  0.0 115.9 jit_solution(8253880818414654217)
XLA Ops:
  1.8 2.9 %collective-permute-start.8 = (f32[10]{0:T(128)S(1)}, f32[10]{0:T(128)S(1)}, u32[]{:S(2)}, u32[]{:S(2)}) collective-permute-start(f32[10]{0:T(128)S(1)} %dynamic_slice.53), channel_id=1, source_target_pairs={{28,24},{24,28},{20,16},{16,20},{12,8},{8,12},{4,0},{0,4},{29,25},... | collective-permute-start | bytes 128 | tf_op jit(solution)/shard_map/ppermute | solution.py:42
  4.8 1.3 %copy.30 = f32[128,1280]{0,1:T(8,128)S(1)} copy(f32[128,1280]{1,0:T(8,128)} %param.9) | data formatting | bytes 1310720 | tf_op args[0]
  7.4 2.0 %collective-permute-start = (f32[10]{0:T(128)S(1)}, f32[10]{0:T(128)S(1)}, u32[]{:S(2)}, u32[]{:S(2)}) collective-permute-start(f32[10]{0:T(128)S(1)} %get-tuple-element.46), channel_id=1, source_target_pairs={{0,4},{4,0},{8,12},{12,8},{16,20},{20,16},{24,28},{28,24},{1,5},{5... | collective-permute-start | bytes 128 | tf_op jit(solution)/shard_map/ppermute | solution.py:42
  9.4 6.6 %collective-permute-done = f32[10]{0:T(128)S(1)} collective-permute-done((f32[10]{0:T(128)S(1)}, f32[10]{0:T(128)S(1)}, u32[]{:S(2)}, u32[]{:S(2)}) %collective-permute-start) | collective-permute-done | bytes 72 | tf_op jit(solution)/shard_map/ppermute | solution.py:42
  16.2 3.5 %collective-permute-start.2 = (f32[10,64,128]{2,1,0:T(8,128)S(1)}, f32[10,64,128]{2,1,0:T(8,128)S(1)}, u32[]{:S(2)}, u32[]{:S(2)}) collective-permute-start(f32[10,64,128]{2,1,0:T(8,128)S(1)} %select_add_fusion.1), channel_id=1, source_target_pairs={{0,8},{4,12},{1,9},{5,13},{2,10},{6,14},{3,11},{7,15}} | collective-permute-start | bytes 983048 | tf_op jit(solution)/shard_map/ppermute | solution.py:61
  19.7 5.7 %collective-permute-done.2 = f32[10,64,128]{2,1,0:T(8,128)S(1)} collective-permute-done((f32[10,64,128]{2,1,0:T(8,128)S(1)}, f32[10,64,128]{2,1,0:T(8,128)S(1)}, u32[]{:S(2)}, u32[]{:S(2)}) %collective-permute-start.2) | collective-permute-done | bytes 327712 | tf_op jit(solution)/shard_map/ppermute | solution.py:61
  28.6 1.5 %fusion.9 = f32[128,20,64]{0,2,1:T(8,128)S(1)} fusion(f32[128,20,64]{0,2,1:T(8,128)S(1)} %bitcast.127, f32[128,128]{1,0:T(8,128)S(1)} %fusion.102, f32[20,128]{1,0:T(8,128)S(1)} %bitcast.136, pred[128,128]{1,0:T(8,128)(4,1)S(1)} %iota_compare_fusion.10, f32[128,20]{0,1:T(8,128)S(1)} %bitcast.140, f32[20]{0:T(128)S(1)} %copy-done.14), kind=kOutput, calls=%fused_computation.9 | convolution fusion | flops 127631360 | bytes 1413200 | tf_op jit(solution)/shard_map/jvp(hij,jhp->ihp)/dot_general | solution.py:166
  30.4 5.2 %collective-permute-done.5 = f32[10,64,128]{2,1,0:T(8,128)} collective-permute-done((f32[10,64,128]{2,1,0:T(8,128)}, f32[10,64,128]{2,1,0:T(8,128)}, u32[]{:S(2)}, u32[]{:S(2)}) %collective-permute-start.5) | collective-permute-done | bytes 327712 | tf_op jit(solution)/shard_map/ppermute | solution.py:79
  35.7 1.1 maximum_select_fusion
  36.8 1.3 %broadcast_multiply_fusion = (f32[128,20,64]{0,2,1:T(8,128)S(1)}, f32[128,20,64]{0,2,1:T(8,128)}) fusion(f32[128,20]{0,1:T(8,128)S(1)} %get-tuple-element.40, f32[20,64,128]{2,1,0:T(8,128)S(1)} %maximum_select_fusion, f32[128,128]{1,0:T(8,128)S(1)} %copy-done), kind=kOutput, calls=%fused_computation.73 | convolution fusion | flops 125992960 | bytes 2041856 | tf_op jit(solution)/shard_map/jvp(in,hpn->ihp)/dot_general | solution.py:173
  38.8 1.7 %multiply_reduce_fusion.4 = (f32[128]{0:T(128)S(1)}, f32[128]{0:T(128)S(1)}, f32[128,1280]{1,0:T(8,128)S(1)}) fusion(f32[128,1280]{1,0:T(8,128)} %param.10, f32[128,1280]{1,0:T(8,128)} %param.17, f32[1280]{0:T(1024)S(1)} %copy-done.7, f32[128,1280]{1,0:T(8,128)S(1)} %copy.31, f32[128,1280]{1,0:T(8,128)S(1)} %copy.32), kind=kLoop, calls=%fused_computation.34 | loop fusion | flops 1801984 | bytes 3282944 | tf_op jit(solution)/shard_map/reduce_sum | solution.py:243
  40.6 1.1 collective-permute-done.6
  41.7 1.6 %collective-permute-start.7 = (f32[2,128]{1,0:T(2,128)S(1)}, f32[2,128]{1,0:T(2,128)S(1)}, u32[]{:S(2)}, u32[]{:S(2)}) collective-permute-start(f32[2,128]{1,0:T(2,128)S(1)} %fusion.100), channel_id=1, source_target_pairs={{0,2},{1,3},{2,0},{3,1},{4,6},{5,7},{6,4},{7,5},{8,10},{9,11},{10,... | collective-permute-start | bytes 3080 | tf_op jit(solution)/shard_map/ppermute | solution.py:93
  43.3 2.0 %collective-permute-done.7 = f32[2,128]{1,0:T(2,128)S(1)} collective-permute-done((f32[2,128]{1,0:T(2,128)S(1)}, f32[2,128]{1,0:T(2,128)S(1)}, u32[]{:S(2)}, u32[]{:S(2)}) %collective-permute-start.7) | collective-permute-done | bytes 1056 | tf_op jit(solution)/shard_map/ppermute | solution.py:93
  45.4 1.3 %add_multiply_fusion = (f32[128,1280]{1,0:T(8,128)}, f32[128,1280]{1,0:T(8,128)S(1)}) fusion(f32[128,1280]{1,0:T(8,128)S(1)} %copy-done.2, f32[128,1280]{1,0:T(8,128)S(1)} %get-tuple-element.23, f32[128]{0:T(128)S(1)} %fusion.90, f32[128,1280]{1,0:T(8,128)S(1)} %copy-done.3, f32[128]{0:T(128)S(1)} %rsqrt_bitcast_fusion, f32[1280]{0:T(1024)S(1)} %copy-done.7), kind=kLoop, calls=%fused_computation.30 | loop fusion | flops 2621440 | bytes 3282944 | tf_op jit(solution)/shard_map/mul | solution.py:252
  48.7 0.9 constant_dynamic-slice_fusion.1
  49.6 1.1 copy.39
  50.7 1.1 copy.40
  51.8 5.2 %collective-permute-done.9 = f32[10,64,128]{2,1,0:T(8,128)} collective-permute-done((f32[10,64,128]{2,1,0:T(8,128)}, f32[10,64,128]{2,1,0:T(8,128)}, u32[]{:S(2)}, u32[]{:S(2)}) %collective-permute-start.9) | collective-permute-done | bytes 327712 | tf_op jit(solution)/shard_map/ppermute | solution.py:42
  57.0 1.1 select_add_fusion
  60.0 2.0 %fusion.20 = (f32[20,128]{1,0:T(8,128)S(1)}, f32[20,128]{1,0:T(8,128)S(1)}, f32[128,128]{1,0:T(8,128)S(1)}) fusion(f32[128,128]{1,0:T(8,128)S(1)} %fusion.102, f32[20,128]{1,0:T(8,128)S(1)} %bitcast.137, pred[128,128]{1,0:T(8,128)(4,1)S(1)} %copy-done.9, f32[20,64,128]{2,1,0:T(8,128)S(1)} %bitcast.118, f32[128,20,64]{0,2,1:T(8,128)S(1)} %bitcast.128, ...), kind=kOutput, calls=%fused_computation.24 | convolution fusion | flops 129575936 | bytes 1499136 | tf_op jit(solution)/shard_map/transpose(jvp(hij,jhp->ihp))/dot_general | solution.py:166
  62.2 1.6 %collective-permute-start.12 = (f32[10,64,128]{2,1,0:T(8,128)S(1)}, f32[10,64,128]{2,1,0:T(8,128)S(1)}, u32[]{:S(2)}, u32[]{:S(2)}) collective-permute-start(f32[10,64,128]{2,1,0:T(8,128)S(1)} %multiply_add_fusion.1), channel_id=1, source_target_pairs={{12,4},{8,0},{13,5},{9,1},{14,6},{10,2},{15,7},{11,3}} | collective-permute-start | bytes 983048 | tf_op jit(solution)/shard_map/ppermute | solution.py:59
  64.7 1.9 %multiply_reduce_fusion.1 = (f32[128,20]{0,1:T(8,128)S(1)}, f32[128,20,64]{0,2,1:T(8,128)}, f32[128,20]{0,1:T(8,128)S(1)}) fusion(f32[128,20,64]{0,2,1:T(8,128)S(1)} %copy-done.5, f32[128,20,64]{0,2,1:T(8,128)S(1)} %bitcast.120, f32[128,20]{0,1:T(8,128)S(1)} %bitcast.142, f32[20]{0:T(128)S(1)} %copy-done.15, f32[128,20,64]{0,2,1:T(8,128)S(1)} %bitcast.129, ...), kind=kOutput, calls=%fused_computation.28 | convolution fusion | flops 128281600 | bytes 3399760 | tf_op jit(solution)/shard_map/transpose(jvp(hij,jhp->ihp))/dot_general | solution.py:166
  66.5 29.7 %collective-permute-done.12 = f32[10,64,128]{2,1,0:T(8,128)S(1)} collective-permute-done((f32[10,64,128]{2,1,0:T(8,128)S(1)}, f32[10,64,128]{2,1,0:T(8,128)S(1)}, u32[]{:S(2)}, u32[]{:S(2)}) %collective-permute-start.12) | collective-permute-done | bytes 327712 | tf_op jit(solution)/shard_map/ppermute | solution.py:59
  97.2 1.6 %collective-permute-start.17 = (f32[128,128]{1,0:T(8,128)S(1)}, f32[128,128]{1,0:T(8,128)S(1)}, u32[]{:S(2)}, u32[]{:S(2)}) collective-permute-start(f32[128,128]{1,0:T(8,128)S(1)} %add.172), channel_id=1, source_target_pairs={{0,2},{1,3},{2,0},{3,1},{4,6},{5,7},{6,4},{7,5},{8,10},{9,11},{10,... | collective-permute-start | bytes 196616 | tf_op jit(solution)/shard_map/ppermute | solution.py:93
  99.0 1.3 %copy.38 = f32[128,1280]{1,0:T(8,128)S(1)} copy(f32[128,1280]{0,1:T(8,128)} %bitcast.133) | data formatting | bytes 1310720 | tf_op jit(solution)/shard_map/transpose(jvp())/reshape | solution.py:163
  100.3 1.2 %collective-permute-done.17 = f32[128,128]{1,0:T(8,128)S(1)} collective-permute-done((f32[128,128]{1,0:T(8,128)S(1)}, f32[128,128]{1,0:T(8,128)S(1)}, u32[]{:S(2)}, u32[]{:S(2)}) %collective-permute-start.17) | collective-permute-done | bytes 65568 | tf_op jit(solution)/shard_map/ppermute | solution.py:93
  102.2 1.3 %collective-permute-done.13 = f32[10,64,128]{2,1,0:T(8,128)S(1)} collective-permute-done((f32[10,64,128]{2,1,0:T(8,128)S(1)}, f32[10,64,128]{2,1,0:T(8,128)S(1)}, u32[]{:S(2)}, u32[]{:S(2)}) %collective-permute-start.13) | collective-permute-done | bytes 327712 | tf_op jit(solution)/shard_map/ppermute | solution.py:79
  103.5 1.2 %multiply_reduce_fusion.7 = (f32[10]{0:T(128)S(1)}, f32[10]{0:T(128)S(1)}, f32[10,64,128]{2,1,0:T(8,128)S(1)}) fusion(f32[10,64,128]{2,1,0:T(8,128)S(1)} %collective-permute-done.13, f32[20,64,128]{2,1,0:T(8,128)S(1)} %maximum_select_fusion, s32[]{:T(128)S(6)} %select_n.213, s32[]{:T(128)S(6)} %select_n.209, f32[10,64,128]{2,1,0:T(8,128)S(1)} %get-tuple-element.19, ...), kind=kLoop, calls=%fused_computation.58 | loop fusion | flops 573420 | bytes 1966209 | tf_op jit(solution)/shard_map/transpose(jvp())/reduce_sum | solution.py:190
  108.9 1.0 fusion.21
  110.7 1.6 %collective-permute-start.15 = (f32[128,128]{1,0:T(8,128)S(1)}, f32[128,128]{1,0:T(8,128)S(1)}, u32[]{:S(2)}, u32[]{:S(2)}) collective-permute-start(f32[128,128]{1,0:T(8,128)S(1)} %add.169), channel_id=1, source_target_pairs={{0,2},{1,3},{2,0},{3,1},{4,6},{5,7},{6,4},{7,5},{8,10},{9,11},{10,... | collective-permute-start | bytes 196616 | tf_op jit(solution)/shard_map/ppermute | solution.py:93
  113.0 2.3 %collective-permute-done.15 = f32[128,128]{1,0:T(8,128)S(1)} collective-permute-done((f32[128,128]{1,0:T(8,128)S(1)}, f32[128,128]{1,0:T(8,128)S(1)}, u32[]{:S(2)}, u32[]{:S(2)}) %collective-permute-start.15) | collective-permute-done | bytes 65568 | tf_op jit(solution)/shard_map/ppermute | solution.py:93
  (113 shorter events, 19.6 us)
Async XLA Ops:
  0.6 26.3 %copy-start = (f32[128,128]{1,0:T(8,128)S(1)}, f32[128,128]{1,0:T(8,128)}, u32[]{:S(2)}) copy-start(f32[128,128]{1,0:T(8,128)} %param.12) | copy-start | bytes 196612
  1.8 5.0 %collective-permute-start.8 = (f32[10]{0:T(128)S(1)}, f32[10]{0:T(128)S(1)}, u32[]{:S(2)}, u32[]{:S(2)}) collective-permute-start(f32[10]{0:T(128)S(1)} %dynamic_slice.53), channel_id=1, source_target_pairs={{28,24},{24,28},{20,16},{16,20},{12,8},{8,12},{4,0},{0,4},{29,25},... | collective-permute-start | bytes 128 | tf_op jit(solution)/shard_map/ppermute | solution.py:42
  4.8 1.4 %copy-start.4 = (f32[128,128]{1,0:T(8,128)S(1)}, f32[128,128]{1,0:T(8,128)}, u32[]{:S(2)}) copy-start(f32[128,128]{1,0:T(8,128)} %param.11) | copy-start | bytes 196612
  4.8 1.4 %copy-start.6 = (f32[20,128]{1,0:T(8,128)S(1)}, f32[20,128]{1,0:T(8,128)}, u32[]{:S(2)}) copy-start(f32[20,128]{1,0:T(8,128)} %param.13) | copy-start | bytes 30724
  6.7 9.4 %collective-permute-start.1 = (f32[10,64,128]{2,1,0:T(8,128)S(1)}, f32[10,64,128]{2,1,0:T(8,128)S(1)}, u32[]{:S(2)}, u32[]{:S(2)}) collective-permute-start(f32[10,64,128]{2,1,0:T(8,128)S(1)} %constant_dynamic-slice_fusion.3), channel_id=1, source_target_pairs={{0,4},{4,0},{8,12},{12,8},{16,20},{20,16},{24,28},{28,24},{1,5},{5... | collective-permute-start | bytes 983048 | tf_op jit(solution)/shard_map/ppermute | solution.py:42
  7.4 8.6 %collective-permute-start = (f32[10]{0:T(128)S(1)}, f32[10]{0:T(128)S(1)}, u32[]{:S(2)}, u32[]{:S(2)}) collective-permute-start(f32[10]{0:T(128)S(1)} %get-tuple-element.46), channel_id=1, source_target_pairs={{0,4},{4,0},{8,12},{12,8},{16,20},{20,16},{24,28},{28,24},{1,5},{5... | collective-permute-start | bytes 128 | tf_op jit(solution)/shard_map/ppermute | solution.py:42
  16.2 9.2 %collective-permute-start.2 = (f32[10,64,128]{2,1,0:T(8,128)S(1)}, f32[10,64,128]{2,1,0:T(8,128)S(1)}, u32[]{:S(2)}, u32[]{:S(2)}) collective-permute-start(f32[10,64,128]{2,1,0:T(8,128)S(1)} %select_add_fusion.1), channel_id=1, source_target_pairs={{0,8},{4,12},{1,9},{5,13},{2,10},{6,14},{3,11},{7,15}} | collective-permute-start | bytes 983048 | tf_op jit(solution)/shard_map/ppermute | solution.py:61
  25.4 0.7 collective-permute-start.3
  26.3 1.0 collective-permute-start.4
  27.0 1.6 %copy-start.8 = (pred[128,128]{1,0:T(8,128)(4,1)}, pred[128,128]{1,0:T(8,128)(4,1)S(1)}, u32[]{:S(2)}) copy-start(pred[128,128]{1,0:T(8,128)(4,1)S(1)} %iota_compare_fusion.10) | copy-start | bytes 49156
  27.2 1.4 %copy-start.14 = (f32[20]{0:T(128)S(1)}, f32[20]{0:T(128)}, u32[]{:S(2)}) copy-start(f32[20]{0:T(128)} %param.15) | copy-start | bytes 244
  28.1 7.6 %collective-permute-start.5 = (f32[10,64,128]{2,1,0:T(8,128)}, f32[10,64,128]{2,1,0:T(8,128)}, u32[]{:S(2)}, u32[]{:S(2)}) collective-permute-start(f32[10,64,128]{2,1,0:T(8,128)} %get-tuple-element.24), channel_id=1, source_target_pairs={{0,4},{4,0},{8,12},{12,8},{16,20},{20,16},{24,28},{28,24},{1,5},{5... | collective-permute-start | bytes 983048 | tf_op jit(solution)/shard_map/ppermute | solution.py:79
  38.8 6.6 %copy-start.2 = (f32[128,1280]{1,0:T(8,128)S(1)}, f32[128,1280]{1,0:T(8,128)}, u32[]{:S(2)}) copy-start(f32[128,1280]{1,0:T(8,128)} %param.10) | copy-start | bytes 1966084
  38.8 6.7 %copy-start.3 = (f32[128,1280]{1,0:T(8,128)S(1)}, f32[128,1280]{1,0:T(8,128)}, u32[]{:S(2)}) copy-start(f32[128,1280]{1,0:T(8,128)} %param.17) | copy-start | bytes 1966084
  40.5 1.2 %collective-permute-start.6 = (f32[2,128]{1,0:T(2,128)S(1)}, f32[2,128]{1,0:T(2,128)S(1)}, u32[]{:S(2)}, u32[]{:S(2)}) collective-permute-start(f32[2,128]{1,0:T(2,128)S(1)} %pad_maximum_fusion), channel_id=1, source_target_pairs={{0,1},{1,0},{2,3},{3,2},{4,5},{5,4},{6,7},{7,6},{8,9},{9,8},{10,11... | collective-permute-start | bytes 3080 | tf_op jit(solution)/shard_map/ppermute | solution.py:93
  41.7 3.6 %collective-permute-start.7 = (f32[2,128]{1,0:T(2,128)S(1)}, f32[2,128]{1,0:T(2,128)S(1)}, u32[]{:S(2)}, u32[]{:S(2)}) collective-permute-start(f32[2,128]{1,0:T(2,128)S(1)} %fusion.100), channel_id=1, source_target_pairs={{0,2},{1,3},{2,0},{3,1},{4,6},{5,7},{6,4},{7,5},{8,10},{9,11},{10,... | collective-permute-start | bytes 3080 | tf_op jit(solution)/shard_map/ppermute | solution.py:93
  47.4 1.3 %copy-start.1 = (f32[128,1280]{1,0:T(8,128)S(1)}, f32[128,1280]{1,0:T(8,128)}, u32[]{:S(2)}) copy-start(f32[128,1280]{1,0:T(8,128)} %param.9) | copy-start | bytes 1966084
  48.1 8.9 %collective-permute-start.9 = (f32[10,64,128]{2,1,0:T(8,128)}, f32[10,64,128]{2,1,0:T(8,128)}, u32[]{:S(2)}, u32[]{:S(2)}) collective-permute-start(f32[10,64,128]{2,1,0:T(8,128)} %constant_dynamic-slice_fusion.2), channel_id=1, source_target_pairs={{28,24},{24,28},{20,16},{16,20},{12,8},{8,12},{4,0},{0,4},{29,25},... | collective-permute-start | bytes 983048 | tf_op jit(solution)/shard_map/ppermute | solution.py:42
  51.8 7.0 %copy-start.10 = (f32[20,128]{1,0:T(8,128)S(1)}, f32[20,128]{1,0:T(8,128)}, u32[]{:S(2)}) copy-start(f32[20,128]{1,0:T(8,128)} %param.14) | copy-start | bytes 30724
  58.1 1.8 %copy-start.9 = (pred[128,128]{1,0:T(8,128)(4,1)S(1)}, pred[128,128]{1,0:T(8,128)(4,1)}, u32[]{:S(2)}) copy-start(pred[128,128]{1,0:T(8,128)(4,1)} %copy-done.8) | copy-start | bytes 49156
  58.1 1.0 collective-permute-start.10
  59.3 2.8 %collective-permute-start.11 = (f32[10,64,128]{2,1,0:T(8,128)S(1)}, f32[10,64,128]{2,1,0:T(8,128)S(1)}, u32[]{:S(2)}, u32[]{:S(2)}) collective-permute-start(f32[10,64,128]{2,1,0:T(8,128)S(1)} %multiply_add_fusion.2), channel_id=1, source_target_pairs={{20,12},{16,8},{21,13},{17,9},{22,14},{18,10},{23,15},{19,11}} | collective-permute-start | bytes 983048 | tf_op jit(solution)/shard_map/ppermute | solution.py:61
  62.2 2.4 %copy-start.5 = (f32[128,20,64]{0,2,1:T(8,128)S(1)}, f32[128,20,64]{0,2,1:T(8,128)}, u32[]{:S(2)}) copy-start(f32[128,20,64]{0,2,1:T(8,128)} %get-tuple-element.48) | copy-start | bytes 1966084
  62.2 2.4 %copy-start.15 = (f32[20]{0:T(128)S(1)}, f32[20]{0:T(128)}, u32[]{:S(2)}) copy-start(f32[20]{0:T(128)} %param.15) | copy-start | bytes 244
  62.2 34.0 %collective-permute-start.12 = (f32[10,64,128]{2,1,0:T(8,128)S(1)}, f32[10,64,128]{2,1,0:T(8,128)S(1)}, u32[]{:S(2)}, u32[]{:S(2)}) collective-permute-start(f32[10,64,128]{2,1,0:T(8,128)S(1)} %multiply_add_fusion.1), channel_id=1, source_target_pairs={{12,4},{8,0},{13,5},{9,1},{14,6},{10,2},{15,7},{11,3}} | collective-permute-start | bytes 983048 | tf_op jit(solution)/shard_map/ppermute | solution.py:59
  64.5 32.6 %collective-permute-start.16 = (f32[128,128]{1,0:T(8,128)S(1)}, f32[128,128]{1,0:T(8,128)S(1)}, u32[]{:S(2)}, u32[]{:S(2)}) collective-permute-start(f32[128,128]{1,0:T(8,128)S(1)} %fusion.17), channel_id=1, source_target_pairs={{0,1},{1,0},{2,3},{3,2},{4,5},{5,4},{6,7},{7,6},{8,9},{9,8},{10,11... | collective-permute-start | bytes 196616 | tf_op jit(solution)/shard_map/ppermute | solution.py:93
  64.6 31.6 %copy-start.13 = (f32[10]{0:T(128)S(1)}, f32[10]{0:T(128)}, u32[]{:S(2)}) copy-start(f32[10]{0:T(128)} %get-tuple-element.22) | copy-start | bytes 124
  96.3 7.1 %collective-permute-start.13 = (f32[10,64,128]{2,1,0:T(8,128)S(1)}, f32[10,64,128]{2,1,0:T(8,128)S(1)}, u32[]{:S(2)}, u32[]{:S(2)}) collective-permute-start(f32[10,64,128]{2,1,0:T(8,128)S(1)} %get-tuple-element.18), channel_id=1, source_target_pairs={{28,24},{24,28},{20,16},{16,20},{12,8},{8,12},{4,0},{0,4},{29,25},... | collective-permute-start | bytes 983048 | tf_op jit(solution)/shard_map/ppermute | solution.py:79
  97.2 4.3 %collective-permute-start.17 = (f32[128,128]{1,0:T(8,128)S(1)}, f32[128,128]{1,0:T(8,128)S(1)}, u32[]{:S(2)}, u32[]{:S(2)}) collective-permute-start(f32[128,128]{1,0:T(8,128)S(1)} %add.172), channel_id=1, source_target_pairs={{0,2},{1,3},{2,0},{3,1},{4,6},{5,7},{6,4},{7,5},{8,10},{9,11},{10,... | collective-permute-start | bytes 196616 | tf_op jit(solution)/shard_map/ppermute | solution.py:93
  98.9 4.5 %copy-start.12 = (f32[10]{0:T(128)S(1)}, f32[10]{0:T(128)}, u32[]{:S(2)}) copy-start(f32[10]{0:T(128)} %copy-done.11) | copy-start | bytes 124
  108.5 2.3 %collective-permute-start.14 = (f32[128,128]{1,0:T(8,128)S(1)}, f32[128,128]{1,0:T(8,128)S(1)}, u32[]{:S(2)}, u32[]{:S(2)}) collective-permute-start(f32[128,128]{1,0:T(8,128)S(1)} %fusion.16), channel_id=1, source_target_pairs={{0,1},{1,0},{2,3},{3,2},{4,5},{5,4},{6,7},{7,6},{8,9},{9,8},{10,11... | collective-permute-start | bytes 196616 | tf_op jit(solution)/shard_map/ppermute | solution.py:93
  110.7 4.6 %collective-permute-start.15 = (f32[128,128]{1,0:T(8,128)S(1)}, f32[128,128]{1,0:T(8,128)S(1)}, u32[]{:S(2)}, u32[]{:S(2)}) collective-permute-start(f32[128,128]{1,0:T(8,128)S(1)} %add.169), channel_id=1, source_target_pairs={{0,2},{1,3},{2,0},{3,1},{4,6},{5,7},{6,4},{7,5},{8,10},{9,11},{10,... | collective-permute-start | bytes 196616 | tf_op jit(solution)/shard_map/ppermute | solution.py:93
  (2 other events, 1.3 us)

commit v21 on v17

--- a/solution.py
+++ b/solution.py
@@ -39,7 +39,9 @@
     a_own, s_own = part(decay, own_start), part(state, own_start)
     a_snd, s_snd = part(decay, send_start), part(state, send_start)
     swap = [(phys(u), phys(u ^ 1)) for u in range(count)]
-    a_rcv, s_rcv = lax.ppermute((a_snd, s_snd), axis, swap)
+    row = jnp.broadcast_to(a_snd[:, None, None], (half, 1, s_snd.shape[2]))
+    got = lax.ppermute(jnp.concatenate([s_snd, row], 1), axis, swap)
+    s_rcv, a_rcv = got[:, : s_snd.shape[1]], got[:, s_snd.shape[1], 0]
     lead = (jnp.where(first, a_own, a_rcv), jnp.where(first, s_own, s_rcv))
     trail = (jnp.where(first, a_rcv, a_own), jnp.where(first, s_rcv, s_own))
     a_tot, s_tot = combine(lead, trail)

time: 115 us -> 120 us (1.043)
  waiting for transfers between devices: 56.5 us -> 58.4 us
  starting transfers between devices: 19.5 us -> 21.3 us
    ppermute x2, starting transfers between devices: 1.18 us -> 3.12 us  [pair_scan(): other = lax.ppermute(send, axis, swap)]
    ppermute x4 -> x2, waiting for transfers between devices: 11.8 us -> 13.7 us  [pair_scan(): got = lax.ppermute(jnp.concatenate([s_snd, row], 1), axis, swap)]
    ppermute x4 -> x2, starting transfers between devices: 5.53 us -> 4.49 us  [pair_scan(): got = lax.ppermute(jnp.concatenate([s_snd, row], 1), axis, swap)]
  transfers between devices with their start and end apart: 18 -> 16, of which waited for: 10 -> 9; matrix products, arithmetic and copies ran while one was open for 19% -> 16% of each run, Pallas kernels for 0% -> 0%
where the time goes in v21:
time: 120 us; the launch traced here: 119 us
  waiting for transfers between devices  58.4 us (49%)
  starting transfers between devices  21.3 us (18%)
  matrix products  15.8 us (13%)
  other arithmetic  11.9 us (10%)
  local copies, waits for them, and re-layouts  10.2 us (8%)
  between operations  1.23 us (1%)
    ppermute x2, waiting for transfers between devices, pair_scan(): s_in = lax.ppermute(out[1], axis, pairs)  27.9 us
    ppermute x2, waiting for transfers between devices, pair_scan(): got = lax.ppermute(jnp.concatenate([s_snd, row], 1), axis, swap)  13.7 us
    ppermute x4, starting transfers between devices, pair_scan(): a_in, s_in = lax.ppermute(out, axis, pairs)  6.51 us
    ppermute x6, waiting for transfers between devices, butterfly_psum(): got = lax.ppermute(parts, axis, [(i, i ^ k) for i in range(count)])  6.31 us
    ppermute x4, waiting for transfers between devices, pair_scan(): a_in, s_in = lax.ppermute(out, axis, pairs)  6.05 us
    dot_general x3, matrix products, within_part(): within = jnp.einsum('hij,jhp->ihp', masked, scaled, precision=highest)  5.88 us
    ppermute x6, starting transfers between devices, butterfly_psum(): got = lax.ppermute(parts, axis, [(i, i ^ k) for i in range(count)])  4.94 us
    dot_general x9, matrix products, prefix_sum(): return jnp.dot(decay_in, upper, precision=lax.Precision.HIGHEST)  4.75 us
  transfers between devices with their start and end apart: 16, of which 9 were waited for; matrix products, arithmetic and copies ran while one was open for 16% of the time, Pallas kernels for 0%

profile of v21, /device:TPU:0, one launch (start us, length us, event | category | flops | bytes accessed | tf_op | source)
XLA Modules:
  0.0 118.9 jit_solution(16204974939516489128)
XLA Ops:
  1.8 1.3 %copy.30 = f32[128,1280]{0,1:T(8,128)S(1)} copy(f32[128,1280]{1,0:T(8,128)} %param.9) | data formatting | bytes 1310720 | tf_op args[0]
  3.9 3.0 %collective-permute-start = (f32[10,65,128]{2,1,0:T(8,128)S(1)}, f32[10,65,128]{2,1,0:T(8,128)S(1)}, u32[]{:S(2)}, u32[]{:S(2)}) collective-permute-start(f32[10,65,128]{2,1,0:T(8,128)S(1)} %pad_maximum_fusion), channel_id=1, source_target_pairs={{0,4},{4,0},{8,12},{12,8},{16,20},{20,16},{24,28},{28,24},{1,5},{5... | collective-permute-start | bytes 998408 | tf_op jit(solution)/shard_map/ppermute | solution.py:43
  6.9 8.6 %collective-permute-done = f32[10,65,128]{2,1,0:T(8,128)S(1)} collective-permute-done((f32[10,65,128]{2,1,0:T(8,128)S(1)}, f32[10,65,128]{2,1,0:T(8,128)S(1)}, u32[]{:S(2)}, u32[]{:S(2)}) %collective-permute-start) | collective-permute-done | bytes 332832 | tf_op jit(solution)/shard_map/ppermute | solution.py:43
  15.8 3.8 %collective-permute-start.1 = (f32[10,64,128]{2,1,0:T(8,128)S(1)}, f32[10,64,128]{2,1,0:T(8,128)S(1)}, u32[]{:S(2)}, u32[]{:S(2)}) collective-permute-start(f32[10,64,128]{2,1,0:T(8,128)S(1)} %get-tuple-element.29), channel_id=1, source_target_pairs={{0,8},{4,12},{1,9},{5,13},{2,10},{6,14},{3,11},{7,15}} | collective-permute-start | bytes 983048 | tf_op jit(solution)/shard_map/ppermute | solution.py:64
  19.6 6.0 %collective-permute-done.1 = f32[10,64,128]{2,1,0:T(8,128)S(1)} collective-permute-done((f32[10,64,128]{2,1,0:T(8,128)S(1)}, f32[10,64,128]{2,1,0:T(8,128)S(1)}, u32[]{:S(2)}, u32[]{:S(2)}) %collective-permute-start.1) | collective-permute-done | bytes 327712 | tf_op jit(solution)/shard_map/ppermute | solution.py:64
  25.8 1.4 %collective-permute-start.2 = (f32[10,64,128]{2,1,0:T(8,128)S(1)}, f32[10,64,128]{2,1,0:T(8,128)}, u32[]{:S(2)}, u32[]{:S(2)}) collective-permute-start(f32[10,64,128]{2,1,0:T(8,128)S(1)} %multiply_add_fusion.4), channel_id=1, source_target_pairs={{8,16},{12,20},{9,17},{13,21},{10,18},{14,22},{11,19},{15,23}} | collective-permute-start | bytes 983048 | tf_op jit(solution)/shard_map/ppermute | solution.py:64
  28.4 1.6 %collective-permute-start.4 = (f32[10,64,128]{2,1,0:T(8,128)S(1)}, f32[10,64,128]{2,1,0:T(8,128)S(1)}, u32[]{:S(2)}, u32[]{:S(2)}) collective-permute-start(f32[10,64,128]{2,1,0:T(8,128)S(1)} %get-tuple-element.42), channel_id=1, source_target_pairs={{0,4},{4,0},{8,12},{12,8},{16,20},{20,16},{24,28},{28,24},{1,5},{5... | collective-permute-start | bytes 983048 | tf_op jit(solution)/shard_map/ppermute | solution.py:84
  29.9 1.5 %fusion.9 = f32[128,20,64]{0,2,1:T(8,128)S(1)} fusion(f32[128,20,64]{0,2,1:T(8,128)S(1)} %bitcast.127, f32[128,128]{1,0:T(8,128)S(1)} %fusion.105, f32[20,128]{1,0:T(8,128)S(1)} %bitcast.136, pred[128,128]{1,0:T(8,128)(4,1)S(1)} %iota_compare_fusion.10, f32[128,20]{0,1:T(8,128)S(1)} %bitcast.140, f32[20]{0:T(128)S(1)} %copy-done.18), kind=kOutput, calls=%fused_computation.9 | convolution fusion | flops 127631360 | bytes 1413200 | tf_op jit(solution)/shard_map/jvp(hij,jhp->ihp)/dot_general | solution.py:171
  31.6 4.4 %collective-permute-done.4 = f32[10,64,128]{2,1,0:T(8,128)S(1)} collective-permute-done((f32[10,64,128]{2,1,0:T(8,128)S(1)}, f32[10,64,128]{2,1,0:T(8,128)S(1)}, u32[]{:S(2)}, u32[]{:S(2)}) %collective-permute-start.4) | collective-permute-done | bytes 327712 | tf_op jit(solution)/shard_map/ppermute | solution.py:84
  36.1 1.3 %broadcast_multiply_fusion = (f32[128,20,64]{0,2,1:T(8,128)S(1)}, f32[128,20,64]{0,2,1:T(8,128)}) fusion(f32[128,20]{0,1:T(8,128)S(1)} %get-tuple-element.48, f32[20,64,128]{2,1,0:T(8,128)S(1)} %maximum_select_fusion, f32[128,128]{1,0:T(8,128)S(1)} %copy-done), kind=kOutput, calls=%fused_computation.74 | convolution fusion | flops 125992960 | bytes 2041856 | tf_op jit(solution)/shard_map/jvp(in,hpn->ihp)/dot_general | solution.py:178
  38.1 1.7 %multiply_reduce_fusion.4 = (f32[128]{0:T(128)S(1)}, f32[128]{0:T(128)S(1)}, f32[128,1280]{1,0:T(8,128)S(1)}) fusion(f32[128,1280]{1,0:T(8,128)} %param.10, f32[128,1280]{1,0:T(8,128)} %param.17, f32[1280]{0:T(1024)S(1)} %copy-done.14, f32[128,1280]{1,0:T(8,128)S(1)} %copy.31, f32[128,1280]{1,0:T(8,128)S(1)} %copy.32), kind=kLoop, calls=%fused_computation.34 | loop fusion | flops 1801984 | bytes 3282944 | tf_op jit(solution)/shard_map/reduce_sum | solution.py:248
  40.0 1.1 collective-permute-done.5
  41.1 1.6 %collective-permute-start.6 = (f32[2,128]{1,0:T(2,128)S(1)}, f32[2,128]{1,0:T(2,128)S(1)}, u32[]{:S(2)}, u32[]{:S(2)}) collective-permute-start(f32[2,128]{1,0:T(2,128)S(1)} %fusion.100), channel_id=1, source_target_pairs={{0,2},{1,3},{2,0},{3,1},{4,6},{5,7},{6,4},{7,5},{8,10},{9,11},{10,... | collective-permute-start | bytes 3080 | tf_op jit(solution)/shard_map/ppermute | solution.py:98
  42.7 2.1 %collective-permute-done.6 = f32[2,128]{1,0:T(2,128)S(1)} collective-permute-done((f32[2,128]{1,0:T(2,128)S(1)}, f32[2,128]{1,0:T(2,128)S(1)}, u32[]{:S(2)}, u32[]{:S(2)}) %collective-permute-start.6) | collective-permute-done | bytes 1056 | tf_op jit(solution)/shard_map/ppermute | solution.py:98
  44.8 1.3 %add_multiply_fusion = (f32[128,1280]{1,0:T(8,128)}, f32[128,1280]{1,0:T(8,128)S(1)}) fusion(f32[128,1280]{1,0:T(8,128)S(1)} %copy-done.4, f32[128,1280]{1,0:T(8,128)S(1)} %get-tuple-element.26, f32[128]{0:T(128)S(1)} %fusion.90, f32[128,1280]{1,0:T(8,128)S(1)} %copy-done.5, f32[128]{0:T(128)S(1)} %rsqrt_bitcast_fusion, f32[1280]{0:T(1024)S(1)} %copy-done.14), kind=kLoop, calls=%fused_computation.30 | loop fusion | flops 2621440 | bytes 3282944 | tf_op jit(solution)/shard_map/mul | solution.py:257
  47.6 1.5 %collective-permute-start.7 = (f32[10,65,128]{2,1,0:T(8,128)}, f32[10,65,128]{2,1,0:T(8,128)}, u32[]{:S(2)}, u32[]{:S(2)}) collective-permute-start(f32[10,65,128]{2,1,0:T(8,128)} %pad_maximum_fusion.1), channel_id=1, source_target_pairs={{28,24},{24,28},{20,16},{16,20},{12,8},{8,12},{4,0},{0,4},{29,25},... | collective-permute-start | bytes 998408 | tf_op jit(solution)/shard_map/ppermute | solution.py:43
  50.0 1.1 copy.39
  51.2 1.1 copy.40
  52.3 5.1 %collective-permute-done.7 = f32[10,65,128]{2,1,0:T(8,128)} collective-permute-done((f32[10,65,128]{2,1,0:T(8,128)}, f32[10,65,128]{2,1,0:T(8,128)}, u32[]{:S(2)}, u32[]{:S(2)}) %collective-permute-start.7) | collective-permute-done | bytes 332832 | tf_op jit(solution)/shard_map/ppermute | solution.py:43
  57.4 0.9 slice_reduce_fusion.3
  58.4 1.1 broadcast_add_fusion
  63.2 2.0 %fusion.20 = (f32[20,128]{1,0:T(8,128)S(1)}, f32[20,128]{1,0:T(8,128)S(1)}, f32[128,128]{1,0:T(8,128)S(1)}) fusion(f32[128,128]{1,0:T(8,128)S(1)} %fusion.105, f32[20,128]{1,0:T(8,128)S(1)} %bitcast.137, pred[128,128]{1,0:T(8,128)(4,1)S(1)} %iota_compare_fusion.10, f32[20,64,128]{2,1,0:T(8,128)S(1)} %bitcast.118, f32[128,20,64]{0,2,1:T(8,128)S(1)} %bitcast.128, ...), kind=kOutput, calls=%fused_computation.24 | convolution fusion | flops 129575936 | bytes 1499136 | tf_op jit(solution)/shard_map/transpose(jvp(hij,jhp->ihp))/dot_general | solution.py:171
  65.5 1.6 %collective-permute-start.10 = (f32[10,64,128]{2,1,0:T(8,128)S(1)}, f32[10,64,128]{2,1,0:T(8,128)S(1)}, u32[]{:S(2)}, u32[]{:S(2)}) collective-permute-start(f32[10,64,128]{2,1,0:T(8,128)S(1)} %get-tuple-element.18), channel_id=1, source_target_pairs={{12,4},{8,0},{13,5},{9,1},{14,6},{10,2},{15,7},{11,3}} | collective-permute-start | bytes 983048 | tf_op jit(solution)/shard_map/ppermute | solution.py:61
  67.9 2.5 %multiply_reduce_fusion.1 = (f32[128,20]{0,1:T(8,128)}, f32[128,20,64]{0,2,1:T(8,128)}, f32[128,20]{0,1:T(8,128)}) fusion(f32[128,20,64]{0,2,1:T(8,128)S(1)} %copy-done.7, f32[128,20,64]{0,2,1:T(8,128)S(1)} %bitcast.120, f32[128,20]{0,1:T(8,128)S(1)} %bitcast.142, f32[20]{0:T(128)S(1)} %copy-done.19, f32[128,20,64]{0,2,1:T(8,128)S(1)} %bitcast.129, ...), kind=kOutput, calls=%fused_computation.28 | convolution fusion | flops 128281600 | bytes 3399760 | tf_op jit(solution)/shard_map/transpose(jvp(hij,jhp->ihp))/dot_general | solution.py:171
  70.3 27.9 %collective-permute-done.10 = f32[10,64,128]{2,1,0:T(8,128)S(1)} collective-permute-done((f32[10,64,128]{2,1,0:T(8,128)S(1)}, f32[10,64,128]{2,1,0:T(8,128)S(1)}, u32[]{:S(2)}, u32[]{:S(2)}) %collective-permute-start.10) | collective-permute-done | bytes 327712 | tf_op jit(solution)/shard_map/ppermute | solution.py:61
  98.4 1.6 %collective-permute-start.11 = (f32[10,64,128]{2,1,0:T(8,128)S(1)}, f32[10,64,128]{2,1,0:T(8,128)S(1)}, u32[]{:S(2)}, u32[]{:S(2)}) collective-permute-start(f32[10,64,128]{2,1,0:T(8,128)S(1)} %add_select_fusion.1), channel_id=1, source_target_pairs={{28,24},{24,28},{20,16},{16,20},{12,8},{8,12},{4,0},{0,4},{29,25},... | collective-permute-start | bytes 983048 | tf_op jit(solution)/shard_map/ppermute | solution.py:84
  100.2 1.6 %collective-permute-start.15 = (f32[128,128]{1,0:T(8,128)S(1)}, f32[128,128]{1,0:T(8,128)}, u32[]{:S(2)}, u32[]{:S(2)}) collective-permute-start(f32[128,128]{1,0:T(8,128)S(1)} %add.180), channel_id=1, source_target_pairs={{0,2},{1,3},{2,0},{3,1},{4,6},{5,7},{6,4},{7,5},{8,10},{9,11},{10,... | collective-permute-start | bytes 196616 | tf_op jit(solution)/shard_map/ppermute | solution.py:98
  102.6 1.3 %copy.38 = f32[128,1280]{1,0:T(8,128)S(1)} copy(f32[128,1280]{0,1:T(8,128)} %bitcast.133) | data formatting | bytes 1310720 | tf_op jit(solution)/shard_map/transpose(jvp())/reshape | solution.py:168
  104.7 1.5 %add.181 = f32[128,128]{1,0:T(8,128)} add(f32[128,128]{1,0:T(8,128)S(1)} %add.180, f32[128,128]{1,0:T(8,128)} %collective-permute-done.15) | non-fusion elementwise | flops 16384 | bytes 196608 | tf_op jit(solution)/shard_map/add | solution.py:99
  106.2 1.3 %multiply_reduce_fusion.7 = (f32[10]{0:T(128)S(1)}, f32[10]{0:T(128)S(1)}, f32[10,64,128]{2,1,0:T(8,128)S(1)}) fusion(f32[10,64,128]{2,1,0:T(8,128)S(1)} %collective-permute-done.11, f32[20,64,128]{2,1,0:T(8,128)S(1)} %maximum_select_fusion, s32[]{:T(128)S(6)} %select_n.213, s32[]{:T(128)S(6)} %select_n.209, f32[10,65,128]{2,1,0:T(8,128)} %collective-permute-done.7, ...), kind=kLoop, calls=%fused_computation.60 | loop fusion | flops 655340 | bytes 2293890 | tf_op jit(solution)/shard_map/transpose(jvp())/reduce_sum | solution.py:195
  113.7 1.6 %collective-permute-start.13 = (f32[128,128]{1,0:T(8,128)S(1)}, f32[128,128]{1,0:T(8,128)S(1)}, u32[]{:S(2)}, u32[]{:S(2)}) collective-permute-start(f32[128,128]{1,0:T(8,128)S(1)} %add.177), channel_id=1, source_target_pairs={{0,2},{1,3},{2,0},{3,1},{4,6},{5,7},{6,4},{7,5},{8,10},{9,11},{10,... | collective-permute-start | bytes 196616 | tf_op jit(solution)/shard_map/ppermute | solution.py:98
  115.9 2.4 %collective-permute-done.13 = f32[128,128]{1,0:T(8,128)S(1)} collective-permute-done((f32[128,128]{1,0:T(8,128)S(1)}, f32[128,128]{1,0:T(8,128)S(1)}, u32[]{:S(2)}, u32[]{:S(2)}) %collective-permute-start.13) | collective-permute-done | bytes 65568 | tf_op jit(solution)/shard_map/ppermute | solution.py:98
  (122 shorter events, 21.0 us)
Async XLA Ops:
  0.6 27.3 %copy-start = (f32[128,128]{1,0:T(8,128)S(1)}, f32[128,128]{1,0:T(8,128)}, u32[]{:S(2)}) copy-start(f32[128,128]{1,0:T(8,128)} %param.12) | copy-start | bytes 196612
  1.8 1.4 %copy-start.6 = (f32[128,128]{1,0:T(8,128)S(1)}, f32[128,128]{1,0:T(8,128)}, u32[]{:S(2)}) copy-start(f32[128,128]{1,0:T(8,128)} %param.11) | copy-start | bytes 196612
  1.8 1.4 %copy-start.12 = (f32[20,128]{1,0:T(8,128)S(1)}, f32[20,128]{1,0:T(8,128)}, u32[]{:S(2)}) copy-start(f32[20,128]{1,0:T(8,128)} %param.13) | copy-start | bytes 30724
  3.2 60.0 %copy-start.2 = (f32[128,1280]{0,1:T(8,128)}, f32[128,1280]{0,1:T(8,128)S(1)}, u32[]{:S(2)}) copy-start(f32[128,1280]{0,1:T(8,128)S(1)} %copy.30) | copy-start | bytes 1966084
  3.9 11.6 %collective-permute-start = (f32[10,65,128]{2,1,0:T(8,128)S(1)}, f32[10,65,128]{2,1,0:T(8,128)S(1)}, u32[]{:S(2)}, u32[]{:S(2)}) collective-permute-start(f32[10,65,128]{2,1,0:T(8,128)S(1)} %pad_maximum_fusion), channel_id=1, source_target_pairs={{0,4},{4,0},{8,12},{12,8},{16,20},{20,16},{24,28},{28,24},{1,5},{5... | collective-permute-start | bytes 998408 | tf_op jit(solution)/shard_map/ppermute | solution.py:43
  15.8 9.8 %collective-permute-start.1 = (f32[10,64,128]{2,1,0:T(8,128)S(1)}, f32[10,64,128]{2,1,0:T(8,128)S(1)}, u32[]{:S(2)}, u32[]{:S(2)}) collective-permute-start(f32[10,64,128]{2,1,0:T(8,128)S(1)} %get-tuple-element.29), channel_id=1, source_target_pairs={{0,8},{4,12},{1,9},{5,13},{2,10},{6,14},{3,11},{7,15}} | collective-permute-start | bytes 983048 | tf_op jit(solution)/shard_map/ppermute | solution.py:64
  25.8 1.4 %collective-permute-start.2 = (f32[10,64,128]{2,1,0:T(8,128)S(1)}, f32[10,64,128]{2,1,0:T(8,128)}, u32[]{:S(2)}, u32[]{:S(2)}) collective-permute-start(f32[10,64,128]{2,1,0:T(8,128)S(1)} %multiply_add_fusion.4), channel_id=1, source_target_pairs={{8,16},{12,20},{9,17},{13,21},{10,18},{14,22},{11,19},{15,23}} | collective-permute-start | bytes 983048 | tf_op jit(solution)/shard_map/ppermute | solution.py:64
  27.3 0.9 collective-permute-start.3
  28.2 1.7 %copy-start.18 = (f32[20]{0:T(128)S(1)}, f32[20]{0:T(128)}, u32[]{:S(2)}) copy-start(f32[20]{0:T(128)} %param.15) | copy-start | bytes 244
  28.4 7.7 %collective-permute-start.4 = (f32[10,64,128]{2,1,0:T(8,128)S(1)}, f32[10,64,128]{2,1,0:T(8,128)S(1)}, u32[]{:S(2)}, u32[]{:S(2)}) collective-permute-start(f32[10,64,128]{2,1,0:T(8,128)S(1)} %get-tuple-element.42), channel_id=1, source_target_pairs={{0,4},{4,0},{8,12},{12,8},{16,20},{20,16},{24,28},{28,24},{1,5},{5... | collective-permute-start | bytes 983048 | tf_op jit(solution)/shard_map/ppermute | solution.py:84
  38.1 6.6 %copy-start.4 = (f32[128,1280]{1,0:T(8,128)S(1)}, f32[128,1280]{1,0:T(8,128)}, u32[]{:S(2)}) copy-start(f32[128,1280]{1,0:T(8,128)} %param.10) | copy-start | bytes 1966084
  38.1 6.7 %copy-start.5 = (f32[128,1280]{1,0:T(8,128)S(1)}, f32[128,1280]{1,0:T(8,128)}, u32[]{:S(2)}) copy-start(f32[128,1280]{1,0:T(8,128)} %param.17) | copy-start | bytes 1966084
  39.9 1.2 %collective-permute-start.5 = (f32[2,128]{1,0:T(2,128)S(1)}, f32[2,128]{1,0:T(2,128)S(1)}, u32[]{:S(2)}, u32[]{:S(2)}) collective-permute-start(f32[2,128]{1,0:T(2,128)S(1)} %pad_maximum_fusion.2), channel_id=1, source_target_pairs={{0,1},{1,0},{2,3},{3,2},{4,5},{5,4},{6,7},{7,6},{8,9},{9,8},{10,11... | collective-permute-start | bytes 3080 | tf_op jit(solution)/shard_map/ppermute | solution.py:98
  41.1 3.6 %collective-permute-start.6 = (f32[2,128]{1,0:T(2,128)S(1)}, f32[2,128]{1,0:T(2,128)S(1)}, u32[]{:S(2)}, u32[]{:S(2)}) collective-permute-start(f32[2,128]{1,0:T(2,128)S(1)} %fusion.100), channel_id=1, source_target_pairs={{0,2},{1,3},{2,0},{3,1},{4,6},{5,7},{6,4},{7,5},{8,10},{9,11},{10,... | collective-permute-start | bytes 3080 | tf_op jit(solution)/shard_map/ppermute | solution.py:98
  46.7 2.4 %copy-start.1 = (f32[128,1280]{1,0:T(8,128)S(1)}, f32[128,1280]{1,0:T(8,128)}, u32[]{:S(2)}) copy-start(f32[128,1280]{1,0:T(8,128)} %param.9) | copy-start | bytes 1966084
  47.6 9.8 %collective-permute-start.7 = (f32[10,65,128]{2,1,0:T(8,128)}, f32[10,65,128]{2,1,0:T(8,128)}, u32[]{:S(2)}, u32[]{:S(2)}) collective-permute-start(f32[10,65,128]{2,1,0:T(8,128)} %pad_maximum_fusion.1), channel_id=1, source_target_pairs={{28,24},{24,28},{20,16},{16,20},{12,8},{8,12},{4,0},{0,4},{29,25},... | collective-permute-start | bytes 998408 | tf_op jit(solution)/shard_map/ppermute | solution.py:43
  58.4 1.8 %copy-start.16 = (f32[20,128]{1,0:T(8,128)S(1)}, f32[20,128]{1,0:T(8,128)}, u32[]{:S(2)}) copy-start(f32[20,128]{1,0:T(8,128)} %param.14) | copy-start | bytes 30724
  59.5 2.8 %collective-permute-start.8 = (f32[10,64,128]{2,1,0:T(8,128)S(1)}, f32[10,64,128]{2,1,0:T(8,128)S(1)}, u32[]{:S(2)}, u32[]{:S(2)}) collective-permute-start(f32[10,64,128]{2,1,0:T(8,128)S(1)} %get-tuple-element.20), channel_id=1, source_target_pairs={{28,20},{24,16},{29,21},{25,17},{30,22},{26,18},{31,23},{27,19}} | collective-permute-start | bytes 983048 | tf_op jit(solution)/shard_map/ppermute | solution.py:64
  62.5 2.8 %collective-permute-start.9 = (f32[10,64,128]{2,1,0:T(8,128)S(1)}, f32[10,64,128]{2,1,0:T(8,128)S(1)}, u32[]{:S(2)}, u32[]{:S(2)}) collective-permute-start(f32[10,64,128]{2,1,0:T(8,128)S(1)} %multiply_add_fusion.2), channel_id=1, source_target_pairs={{20,12},{16,8},{21,13},{17,9},{22,14},{18,10},{23,15},{19,11}} | collective-permute-start | bytes 983048 | tf_op jit(solution)/shard_map/ppermute | solution.py:64
  65.4 2.4 %copy-start.3 = (f32[128,1280]{0,1:T(8,128)S(1)}, f32[128,1280]{0,1:T(8,128)}, u32[]{:S(2)}) copy-start(f32[128,1280]{0,1:T(8,128)} %copy-done.2) | copy-start | bytes 1966084
  65.4 2.4 %copy-start.7 = (f32[128,20,64]{0,2,1:T(8,128)S(1)}, f32[128,20,64]{0,2,1:T(8,128)}, u32[]{:S(2)}) copy-start(f32[128,20,64]{0,2,1:T(8,128)} %get-tuple-element.57) | copy-start | bytes 1966084
  65.4 2.4 %copy-start.19 = (f32[20]{0:T(128)S(1)}, f32[20]{0:T(128)}, u32[]{:S(2)}) copy-start(f32[20]{0:T(128)} %param.15) | copy-start | bytes 244
  65.5 32.8 %collective-permute-start.10 = (f32[10,64,128]{2,1,0:T(8,128)S(1)}, f32[10,64,128]{2,1,0:T(8,128)S(1)}, u32[]{:S(2)}, u32[]{:S(2)}) collective-permute-start(f32[10,64,128]{2,1,0:T(8,128)S(1)} %get-tuple-element.18), channel_id=1, source_target_pairs={{12,4},{8,0},{13,5},{9,1},{14,6},{10,2},{15,7},{11,3}} | collective-permute-start | bytes 983048 | tf_op jit(solution)/shard_map/ppermute | solution.py:61
  67.8 32.4 %collective-permute-start.14 = (f32[128,128]{1,0:T(8,128)S(1)}, f32[128,128]{1,0:T(8,128)S(1)}, u32[]{:S(2)}, u32[]{:S(2)}) collective-permute-start(f32[128,128]{1,0:T(8,128)S(1)} %fusion.17), channel_id=1, source_target_pairs={{0,1},{1,0},{2,3},{3,2},{4,5},{5,4},{6,7},{7,6},{8,9},{9,8},{10,11... | collective-permute-start | bytes 196616 | tf_op jit(solution)/shard_map/ppermute | solution.py:98
  98.4 7.8 %collective-permute-start.11 = (f32[10,64,128]{2,1,0:T(8,128)S(1)}, f32[10,64,128]{2,1,0:T(8,128)S(1)}, u32[]{:S(2)}, u32[]{:S(2)}) collective-permute-start(f32[10,64,128]{2,1,0:T(8,128)S(1)} %add_select_fusion.1), channel_id=1, source_target_pairs={{28,24},{24,28},{20,16},{16,20},{12,8},{8,12},{4,0},{0,4},{29,25},... | collective-permute-start | bytes 983048 | tf_op jit(solution)/shard_map/ppermute | solution.py:84
  100.2 4.4 %collective-permute-start.15 = (f32[128,128]{1,0:T(8,128)S(1)}, f32[128,128]{1,0:T(8,128)}, u32[]{:S(2)}, u32[]{:S(2)}) collective-permute-start(f32[128,128]{1,0:T(8,128)S(1)} %add.180), channel_id=1, source_target_pairs={{0,2},{1,3},{2,0},{3,1},{4,6},{5,7},{6,4},{7,5},{8,10},{9,11},{10,... | collective-permute-start | bytes 196616 | tf_op jit(solution)/shard_map/ppermute | solution.py:98
  106.1 1.5 %copy-start.10 = (f32[10,128]{1,0:T(8,128)S(1)}, f32[10,128]{1,0:T(8,128)}, u32[]{:S(2)}) copy-start(f32[10,128]{1,0:T(8,128)} %fusion.67) | copy-start | bytes 15364
  106.2 1.7 %copy-start.11 = (f32[10,128]{1,0:T(8,128)S(1)}, f32[10,128]{1,0:T(8,128)}, u32[]{:S(2)}) copy-start(f32[10,128]{1,0:T(8,128)} %fusion.66) | copy-start | bytes 15364
  106.2 2.0 %copy-start.8 = (f32[128,10]{0,1:T(8,128)S(1)}, f32[128,10]{0,1:T(8,128)}, u32[]{:S(2)}) copy-start(f32[128,10]{0,1:T(8,128)} %get-tuple-element.47) | copy-start | bytes 15364
  111.4 2.3 %collective-permute-start.12 = (f32[128,128]{1,0:T(8,128)S(1)}, f32[128,128]{1,0:T(8,128)S(1)}, u32[]{:S(2)}, u32[]{:S(2)}) collective-permute-start(f32[128,128]{1,0:T(8,128)S(1)} %fusion.16), channel_id=1, source_target_pairs={{0,1},{1,0},{2,3},{3,2},{4,5},{5,4},{6,7},{7,6},{8,9},{9,8},{10,11... | collective-permute-start | bytes 196616 | tf_op jit(solution)/shard_map/ppermute | solution.py:98
  111.9 3.4 %copy-start.17 = (f32[128,20]{0,1:T(8,128)S(1)}, f32[128,20]{0,1:T(8,128)}, u32[]{:S(2)}) copy-start(f32[128,20]{0,1:T(8,128)} %get-tuple-element.39) | copy-start | bytes 30724
  113.7 4.6 %collective-permute-start.13 = (f32[128,128]{1,0:T(8,128)S(1)}, f32[128,128]{1,0:T(8,128)S(1)}, u32[]{:S(2)}, u32[]{:S(2)}) collective-permute-start(f32[128,128]{1,0:T(8,128)S(1)} %add.177), channel_id=1, source_target_pairs={{0,2},{1,3},{2,0},{3,1},{4,6},{5,7},{6,4},{7,5},{8,10},{9,11},{10,... | collective-permute-start | bytes 196616 | tf_op jit(solution)/shard_map/ppermute | solution.py:98
  (4 other events, 3.4 us)

commit v22 on v17

--- a/solution.py
+++ b/solution.py
@@ -279,18 +279,15 @@
         own = end_half(own_start, sg_keep)
         rest = end_half(send_start, sg_other)
 
-        def join(a, b, axis):
-            return jnp.where(
-                first, jnp.concatenate([b, a], axis), jnp.concatenate([a, b], axis)
-            )
-
-        gf_e = join(own[0], rest[0], 1)
-        gs_e = join(own[1], rest[1], 0)
-        gd_e = join(own[2], rest[2], 0)
+        def add_at(total, piece, start, axis):
+            cur = lax.dynamic_slice_in_dim(total, start, piece.shape[axis], axis)
+            return lax.dynamic_update_slice_in_dim(total, cur + piece, start, axis)
+
         gw_e = own[3] + rest[3]
-        grad_features = gf_w + gf_e
-        grad_steps = gs_w + gs_e
-        grad_decay = gd_w + gd_c + gd_e
+        grad_features = add_at(add_at(gf_w, own[0], own_start * head_width, 1), rest[0],
+                               send_start * head_width, 1)
+        grad_steps = add_at(add_at(gs_w, own[1], own_start, 0), rest[1], send_start, 0)
+        grad_decay = add_at(add_at(gd_w + gd_c, own[2], own_start, 0), rest[2], send_start, 0)
         grad_write = butterfly_psum(gw_w + gw_e, "head")
     else:
         state_grad = pair_scan(decay_total, local_grad, "seq", True)

time: 115 us -> 115 us (level)
    unnamed x49 -> x71, local copies, waits for them, and re-layouts: 2.16 us -> 3.75 us
    add x2, other arithmetic: 1.54 us -> 0.03 us  [add_at(): return lax.dynamic_update_slice_in_dim(total, cur + piece, start, axis)]
    ppermute x2, waiting for transfers between devices: 27.4 us -> 26 us  [pair_scan(): s_in = lax.ppermute(out[1], axis, pairs)]
  transfers between devices with their start and end apart: 18 -> 18, of which waited for: 10 -> 10; matrix products, arithmetic and copies ran while one was open for 19% -> 18% of each run, Pallas kernels for 0% -> 0%
where the time goes in v22:
time: 115 us
  waiting for transfers between devices  55.8 us (49%)
  starting transfers between devices  19.5 us (17%)
  matrix products  16.1 us (14%)
  other arithmetic  11.5 us (10%)
  local copies, waits for them, and re-layouts  10.4 us (9%)
  between operations  1.44 us (1%)
    ppermute x2, waiting for transfers between devices, pair_scan(): s_in = lax.ppermute(out[1], axis, pairs)  26 us
    ppermute x4, waiting for transfers between devices, pair_scan(): a_rcv, s_rcv = lax.ppermute((a_snd, s_snd), axis, swap)  12.4 us
    dot_general x3, matrix products, within_part(): within = jnp.einsum('hij,jhp->ihp', masked, scaled, precision=highest)  6.99 us
    ppermute x6, waiting for transfers between devices, butterfly_psum(): got = lax.ppermute(parts, axis, [(i, i ^ k) for i in range(count)])  6.29 us
    ppermute x4, waiting for transfers between devices, pair_scan(): a_in, s_in = lax.ppermute(out, axis, pairs)  5.67 us
    ppermute x4, starting transfers between devices, pair_scan(): a_rcv, s_rcv = lax.ppermute((a_snd, s_snd), axis, swap)  5.59 us
    ppermute x4, starting transfers between devices, pair_scan(): a_in, s_in = lax.ppermute(out, axis, pairs)  5.54 us
    ppermute x2, waiting for transfers between devices, pair_scan(): other = lax.ppermute(send, axis, swap)  5.41 us
  transfers between devices with their start and end apart: 18, of which 10 were waited for; matrix products, arithmetic and copies ran while one was open for 18% of the time, Pallas kernels for 0%

profile of v22, /device:TPU:0, one launch (start us, length us, event | category | flops | bytes accessed | tf_op | source)
XLA Modules:
  0.0 114.7 jit_solution(8233056263689705192)
XLA Ops:
  0.7 0.8 fusion.68
  1.8 2.9 %collective-permute-start.8 = (f32[10]{0:T(128)S(1)}, f32[10]{0:T(128)S(1)}, u32[]{:S(2)}, u32[]{:S(2)}) collective-permute-start(f32[10]{0:T(128)S(1)} %dynamic_slice.72), channel_id=1, source_target_pairs={{28,24},{24,28},{20,16},{16,20},{12,8},{8,12},{4,0},{0,4},{29,25},... | collective-permute-start | bytes 128 | tf_op jit(solution)/shard_map/ppermute | solution.py:42
  4.8 1.3 %copy.29 = f32[128,1280]{0,1:T(8,128)S(1)} copy(f32[128,1280]{1,0:T(8,128)} %param.9) | data formatting | bytes 1310720 | tf_op args[0]
  7.4 2.0 %collective-permute-start = (f32[10]{0:T(128)S(1)}, f32[10]{0:T(128)S(1)}, u32[]{:S(2)}, u32[]{:S(2)}) collective-permute-start(f32[10]{0:T(128)S(1)} %get-tuple-element.54), channel_id=1, source_target_pairs={{0,4},{4,0},{8,12},{12,8},{16,20},{20,16},{24,28},{28,24},{1,5},{5... | collective-permute-start | bytes 128 | tf_op jit(solution)/shard_map/ppermute | solution.py:42
  9.4 6.6 %collective-permute-done = f32[10]{0:T(128)S(1)} collective-permute-done((f32[10]{0:T(128)S(1)}, f32[10]{0:T(128)S(1)}, u32[]{:S(2)}, u32[]{:S(2)}) %collective-permute-start) | collective-permute-done | bytes 72 | tf_op jit(solution)/shard_map/ppermute | solution.py:42
  16.2 3.5 %collective-permute-start.2 = (f32[10,64,128]{2,1,0:T(8,128)S(1)}, f32[10,64,128]{2,1,0:T(8,128)S(1)}, u32[]{:S(2)}, u32[]{:S(2)}) collective-permute-start(f32[10,64,128]{2,1,0:T(8,128)S(1)} %get-tuple-element.29), channel_id=1, source_target_pairs={{0,8},{4,12},{1,9},{5,13},{2,10},{6,14},{3,11},{7,15}} | collective-permute-start | bytes 983048 | tf_op jit(solution)/shard_map/ppermute | solution.py:62
  19.7 5.7 %collective-permute-done.2 = f32[10,64,128]{2,1,0:T(8,128)S(1)} collective-permute-done((f32[10,64,128]{2,1,0:T(8,128)S(1)}, f32[10,64,128]{2,1,0:T(8,128)S(1)}, u32[]{:S(2)}, u32[]{:S(2)}) %collective-permute-start.2) | collective-permute-done | bytes 327712 | tf_op jit(solution)/shard_map/ppermute | solution.py:62
  28.0 1.5 %fusion.9 = f32[128,20,64]{0,2,1:T(8,128)S(1)} fusion(f32[128,20,64]{0,2,1:T(8,128)S(1)} %bitcast.128, f32[128,128]{1,0:T(8,128)S(1)} %fusion.103, f32[20,128]{1,0:T(8,128)S(1)} %bitcast.137, pred[128,128]{1,0:T(8,128)(4,1)S(1)} %iota_compare_fusion.10, f32[128,20]{0,1:T(8,128)S(1)} %bitcast.141, f32[20]{0:T(128)S(1)} %copy-done.33), kind=kOutput, calls=%fused_computation.9 | convolution fusion | flops 127631360 | bytes 1413200 | tf_op jit(solution)/shard_map/jvp(hij,jhp->ihp)/dot_general | solution.py:169
  29.7 5.0 %collective-permute-done.5 = f32[10,64,128]{2,1,0:T(8,128)S(1)} collective-permute-done((f32[10,64,128]{2,1,0:T(8,128)S(1)}, f32[10,64,128]{2,1,0:T(8,128)S(1)}, u32[]{:S(2)}, u32[]{:S(2)}) %collective-permute-start.5) | collective-permute-done | bytes 327712 | tf_op jit(solution)/shard_map/ppermute | solution.py:82
  34.8 1.3 %broadcast_multiply_fusion = (f32[128,20,64]{0,2,1:T(8,128)S(1)}, f32[128,20,64]{0,2,1:T(8,128)}) fusion(f32[128,20]{0,1:T(8,128)S(1)} %get-tuple-element.48, f32[20,64,128]{2,1,0:T(8,128)S(1)} %maximum_select_fusion, f32[128,128]{1,0:T(8,128)S(1)} %copy-done), kind=kOutput, calls=%fused_computation.73 | convolution fusion | flops 125992960 | bytes 2041856 | tf_op jit(solution)/shard_map/jvp(in,hpn->ihp)/dot_general | solution.py:176
  36.3 0.8 copy-done.5
  37.2 2.3 %multiply_reduce_fusion.4 = (f32[128]{0:T(128)S(1)}, f32[128]{0:T(128)S(1)}, f32[128,1280]{1,0:T(8,128)}) fusion(f32[128,1280]{1,0:T(8,128)S(1)} %copy-done.5, f32[128,1280]{1,0:T(8,128)} %param.17, f32[1280]{0:T(1024)S(1)} %copy-done.23, f32[128,1280]{1,0:T(8,128)S(1)} %copy.30, f32[128,1280]{1,0:T(8,128)S(1)} %copy.31), kind=kLoop, calls=%fused_computation.33 | loop fusion | flops 1801984 | bytes 3282944 | tf_op jit(solution)/shard_map/reduce_sum | solution.py:246
  39.5 1.1 collective-permute-done.6
  40.7 1.6 %collective-permute-start.7 = (f32[2,128]{1,0:T(2,128)S(1)}, f32[2,128]{1,0:T(2,128)S(1)}, u32[]{:S(2)}, u32[]{:S(2)}) collective-permute-start(f32[2,128]{1,0:T(2,128)S(1)} %fusion.99), channel_id=1, source_target_pairs={{0,2},{1,3},{2,0},{3,1},{4,6},{5,7},{6,4},{7,5},{8,10},{9,11},{10,... | collective-permute-start | bytes 3080 | tf_op jit(solution)/shard_map/ppermute | solution.py:96
  42.2 2.1 %collective-permute-done.7 = f32[2,128]{1,0:T(2,128)S(1)} collective-permute-done((f32[2,128]{1,0:T(2,128)S(1)}, f32[2,128]{1,0:T(2,128)S(1)}, u32[]{:S(2)}, u32[]{:S(2)}) %collective-permute-start.7) | collective-permute-done | bytes 1056 | tf_op jit(solution)/shard_map/ppermute | solution.py:96
  44.3 2.3 %add_multiply_fusion = (f32[128,1280]{1,0:T(8,128)}, f32[128,1280]{1,0:T(8,128)S(1)}) fusion(f32[128,1280]{1,0:T(8,128)S(1)} %copy-done.5, f32[128,1280]{1,0:T(8,128)} %get-tuple-element.26, f32[128]{0:T(128)S(1)} %fusion.89, f32[128,1280]{1,0:T(8,128)S(1)} %copy-done.6, f32[128]{0:T(128)S(1)} %rsqrt_bitcast_fusion, f32[1280]{0:T(1024)S(1)} %copy-done.23), kind=kLoop, calls=%fused_computation.29 | loop fusion | flops 2621440 | bytes 3282944 | tf_op jit(solution)/shard_map/mul | solution.py:255
  49.3 0.9 constant_dynamic-slice_fusion.1
  50.2 5.8 %collective-permute-done.9 = f32[10,64,128]{2,1,0:T(8,128)S(1)} collective-permute-done((f32[10,64,128]{2,1,0:T(8,128)S(1)}, f32[10,64,128]{2,1,0:T(8,128)S(1)}, u32[]{:S(2)}, u32[]{:S(2)}) %collective-permute-start.9) | collective-permute-done | bytes 327712 | tf_op jit(solution)/shard_map/ppermute | solution.py:42
  56.1 0.9 broadcast_add_fusion
  57.6 0.8 fusion.67
  58.5 1.1 copy.38
  59.7 3.1 %fusion.21 = (f32[20,128]{1,0:T(8,128)S(1)}, f32[20,128]{1,0:T(8,128)S(1)}, f32[128,128]{1,0:T(8,128)S(1)}) fusion(f32[128,128]{1,0:T(8,128)S(1)} %fusion.103, f32[20,128]{1,0:T(8,128)S(1)} %bitcast.138, pred[128,128]{1,0:T(8,128)(4,1)S(1)} %iota_compare_fusion.10, f32[20,64,128]{2,1,0:T(8,128)S(1)} %bitcast.119, f32[128,20,64]{0,2,1:T(8,128)} %bitcast.129, ...), kind=kOutput, calls=%fused_computation.25 | convolution fusion | flops 129575936 | bytes 1499136 | tf_op jit(solution)/shard_map/transpose(jvp(hij,jhp->ihp))/dot_general | solution.py:169
  64.6 1.6 %collective-permute-start.12 = (f32[10,64,128]{2,1,0:T(8,128)S(1)}, f32[10,64,128]{2,1,0:T(8,128)S(1)}, u32[]{:S(2)}, u32[]{:S(2)}) collective-permute-start(f32[10,64,128]{2,1,0:T(8,128)S(1)} %get-tuple-element.18), channel_id=1, source_target_pairs={{12,4},{8,0},{13,5},{9,1},{14,6},{10,2},{15,7},{11,3}} | collective-permute-start | bytes 983048 | tf_op jit(solution)/shard_map/ppermute | solution.py:59
  66.6 2.5 %multiply_reduce_fusion.1 = (f32[128,20]{0,1:T(8,128)S(1)}, f32[128,20,64]{0,2,1:T(8,128)}, f32[128,20]{0,1:T(8,128)}) fusion(f32[128,20,64]{0,2,1:T(8,128)S(1)} %copy-done.13, f32[128,20,64]{0,2,1:T(8,128)S(1)} %bitcast.121, f32[128,20]{0,1:T(8,128)S(1)} %bitcast.143, f32[20]{0:T(128)S(1)} %copy-done.34, f32[128,20,64]{0,2,1:T(8,128)S(1)} %bitcast.130, ...), kind=kOutput, calls=%fused_computation.27 | convolution fusion | flops 128281600 | bytes 3399760 | tf_op jit(solution)/shard_map/transpose(jvp(hij,jhp->ihp))/dot_general | solution.py:169
  69.1 26.0 %collective-permute-done.12 = f32[10,64,128]{2,1,0:T(8,128)S(1)} collective-permute-done((f32[10,64,128]{2,1,0:T(8,128)S(1)}, f32[10,64,128]{2,1,0:T(8,128)S(1)}, u32[]{:S(2)}, u32[]{:S(2)}) %collective-permute-start.12) | collective-permute-done | bytes 327712 | tf_op jit(solution)/shard_map/ppermute | solution.py:59
  96.5 1.6 %collective-permute-start.17 = (f32[128,128]{1,0:T(8,128)S(1)}, f32[128,128]{1,0:T(8,128)}, u32[]{:S(2)}, u32[]{:S(2)}) collective-permute-start(f32[128,128]{1,0:T(8,128)S(1)} %add.205), channel_id=1, source_target_pairs={{0,2},{1,3},{2,0},{3,1},{4,6},{5,7},{6,4},{7,5},{8,10},{9,11},{10,... | collective-permute-start | bytes 196616 | tf_op jit(solution)/shard_map/ppermute | solution.py:96
  98.1 0.8 convolution_add_fusion
  98.9 1.4 %copy.35 = f32[128,1280]{1,0:T(8,128)S(1)} copy(f32[128,1280]{0,1:T(8,128)} %bitcast.134) | data formatting | bytes 1310720 | tf_op jit(solution)/shard_map/transpose(jvp())/reshape | solution.py:166
  101.0 1.5 %add.206 = f32[128,128]{1,0:T(8,128)} add(f32[128,128]{1,0:T(8,128)S(1)} %add.205, f32[128,128]{1,0:T(8,128)} %collective-permute-done.17) | non-fusion elementwise | flops 16384 | bytes 196608 | tf_op jit(solution)/shard_map/add | solution.py:97
  102.9 1.2 %multiply_reduce_fusion.5 = (f32[10]{0:T(128)S(1)}, f32[10]{0:T(128)S(1)}, f32[10,64,128]{2,1,0:T(8,128)S(1)}) fusion(f32[10,64,128]{2,1,0:T(8,128)S(1)} %collective-permute-done.13, f32[20,64,128]{2,1,0:T(8,128)S(1)} %maximum_select_fusion, s32[]{:T(128)S(6)} %select_n.205, s32[]{:T(128)S(6)} %select_n.204, f32[10,64,128]{2,1,0:T(8,128)S(1)} %copy-done.11, ...), kind=kLoop, calls=%fused_computation.55 | loop fusion | flops 655340 | bytes 2293890 | tf_op jit(solution)/shard_map/transpose(jvp())/reduce_sum | solution.py:193
  109.5 1.6 %collective-permute-start.15 = (f32[128,128]{1,0:T(8,128)S(1)}, f32[128,128]{1,0:T(8,128)S(1)}, u32[]{:S(2)}, u32[]{:S(2)}) collective-permute-start(f32[128,128]{1,0:T(8,128)S(1)} %add.202), channel_id=1, source_target_pairs={{0,2},{1,3},{2,0},{3,1},{4,6},{5,7},{6,4},{7,5},{8,10},{9,11},{10,... | collective-permute-start | bytes 196616 | tf_op jit(solution)/shard_map/ppermute | solution.py:96
  111.7 2.4 %collective-permute-done.15 = f32[128,128]{1,0:T(8,128)S(1)} collective-permute-done((f32[128,128]{1,0:T(8,128)S(1)}, f32[128,128]{1,0:T(8,128)S(1)}, u32[]{:S(2)}, u32[]{:S(2)}) %collective-permute-start.15) | collective-permute-done | bytes 65568 | tf_op jit(solution)/shard_map/ppermute | solution.py:96
  (156 shorter events, 19.4 us)
Async XLA Ops:
  0.6 26.4 %copy-start = (f32[128,128]{1,0:T(8,128)S(1)}, f32[128,128]{1,0:T(8,128)}, u32[]{:S(2)}) copy-start(f32[128,128]{1,0:T(8,128)} %param.12) | copy-start | bytes 196612
  1.8 5.0 %collective-permute-start.8 = (f32[10]{0:T(128)S(1)}, f32[10]{0:T(128)S(1)}, u32[]{:S(2)}, u32[]{:S(2)}) collective-permute-start(f32[10]{0:T(128)S(1)} %dynamic_slice.72), channel_id=1, source_target_pairs={{28,24},{24,28},{20,16},{16,20},{12,8},{8,12},{4,0},{0,4},{29,25},... | collective-permute-start | bytes 128 | tf_op jit(solution)/shard_map/ppermute | solution.py:42
  6.2 21.8 %copy-start.3 = (f32[128,1280]{0,1:T(8,128)}, f32[128,1280]{0,1:T(8,128)S(1)}, u32[]{:S(2)}) copy-start(f32[128,1280]{0,1:T(8,128)S(1)} %copy.29) | copy-start | bytes 1966084
  6.7 9.4 %collective-permute-start.1 = (f32[10,64,128]{2,1,0:T(8,128)S(1)}, f32[10,64,128]{2,1,0:T(8,128)S(1)}, u32[]{:S(2)}, u32[]{:S(2)}) collective-permute-start(f32[10,64,128]{2,1,0:T(8,128)S(1)} %constant_dynamic-slice_fusion.3), channel_id=1, source_target_pairs={{0,4},{4,0},{8,12},{12,8},{16,20},{20,16},{24,28},{28,24},{1,5},{5... | collective-permute-start | bytes 983048 | tf_op jit(solution)/shard_map/ppermute | solution.py:42
  6.8 9.4 %copy-start.31 = (f32[10]{0:T(128)}, f32[10]{0:T(128)S(1)}, u32[]{:S(2)}) copy-start(f32[10]{0:T(128)S(1)} %collective-permute-done.8) | copy-start | bytes 124
  7.4 8.6 %collective-permute-start = (f32[10]{0:T(128)S(1)}, f32[10]{0:T(128)S(1)}, u32[]{:S(2)}, u32[]{:S(2)}) collective-permute-start(f32[10]{0:T(128)S(1)} %get-tuple-element.54), channel_id=1, source_target_pairs={{0,4},{4,0},{8,12},{12,8},{16,20},{20,16},{24,28},{28,24},{1,5},{5... | collective-permute-start | bytes 128 | tf_op jit(solution)/shard_map/ppermute | solution.py:42
  16.2 9.2 %collective-permute-start.2 = (f32[10,64,128]{2,1,0:T(8,128)S(1)}, f32[10,64,128]{2,1,0:T(8,128)S(1)}, u32[]{:S(2)}, u32[]{:S(2)}) collective-permute-start(f32[10,64,128]{2,1,0:T(8,128)S(1)} %get-tuple-element.29), channel_id=1, source_target_pairs={{0,8},{4,12},{1,9},{5,13},{2,10},{6,14},{3,11},{7,15}} | collective-permute-start | bytes 983048 | tf_op jit(solution)/shard_map/ppermute | solution.py:62
  25.5 0.7 collective-permute-start.3
  26.3 0.9 collective-permute-start.4
  27.2 32.5 %copy-start.21 = (f32[128,128]{1,0:T(8,128)}, f32[128,128]{1,0:T(8,128)S(1)}, u32[]{:S(2)}) copy-start(f32[128,128]{1,0:T(8,128)S(1)} %fusion.103) | copy-start | bytes 196612
  27.4 7.3 %collective-permute-start.5 = (f32[10,64,128]{2,1,0:T(8,128)S(1)}, f32[10,64,128]{2,1,0:T(8,128)S(1)}, u32[]{:S(2)}, u32[]{:S(2)}) collective-permute-start(f32[10,64,128]{2,1,0:T(8,128)S(1)} %get-tuple-element.42), channel_id=1, source_target_pairs={{0,4},{4,0},{8,12},{12,8},{16,20},{20,16},{24,28},{28,24},{1,5},{5... | collective-permute-start | bytes 983048 | tf_op jit(solution)/shard_map/ppermute | solution.py:82
  28.0 31.6 %copy-start.26 = (pred[128,128]{1,0:T(8,128)(4,1)}, pred[128,128]{1,0:T(8,128)(4,1)S(1)}, u32[]{:S(2)}) copy-start(pred[128,128]{1,0:T(8,128)(4,1)S(1)} %iota_compare_fusion.10) | copy-start | bytes 49156
  37.2 7.2 %copy-start.6 = (f32[128,1280]{1,0:T(8,128)S(1)}, f32[128,1280]{1,0:T(8,128)}, u32[]{:S(2)}) copy-start(f32[128,1280]{1,0:T(8,128)} %param.17) | copy-start | bytes 1966084
  39.4 1.2 %collective-permute-start.6 = (f32[2,128]{1,0:T(2,128)S(1)}, f32[2,128]{1,0:T(2,128)S(1)}, u32[]{:S(2)}, u32[]{:S(2)}) collective-permute-start(f32[2,128]{1,0:T(2,128)S(1)} %pad_maximum_fusion), channel_id=1, source_target_pairs={{0,1},{1,0},{2,3},{3,2},{4,5},{5,4},{6,7},{7,6},{8,9},{9,8},{10,11... | collective-permute-start | bytes 3080 | tf_op jit(solution)/shard_map/ppermute | solution.py:96
  40.7 3.6 %collective-permute-start.7 = (f32[2,128]{1,0:T(2,128)S(1)}, f32[2,128]{1,0:T(2,128)S(1)}, u32[]{:S(2)}, u32[]{:S(2)}) collective-permute-start(f32[2,128]{1,0:T(2,128)S(1)} %fusion.99), channel_id=1, source_target_pairs={{0,2},{1,3},{2,0},{3,1},{4,6},{5,7},{6,4},{7,5},{8,10},{9,11},{10,... | collective-permute-start | bytes 3080 | tf_op jit(solution)/shard_map/ppermute | solution.py:96
  47.4 8.7 %collective-permute-start.9 = (f32[10,64,128]{2,1,0:T(8,128)S(1)}, f32[10,64,128]{2,1,0:T(8,128)S(1)}, u32[]{:S(2)}, u32[]{:S(2)}) collective-permute-start(f32[10,64,128]{2,1,0:T(8,128)S(1)} %constant_dynamic-slice_fusion.2), channel_id=1, source_target_pairs={{28,24},{24,28},{20,16},{16,20},{12,8},{8,12},{4,0},{0,4},{29,25},... | collective-permute-start | bytes 983048 | tf_op jit(solution)/shard_map/ppermute | solution.py:42
  49.3 6.7 %copy-start.29 = (f32[10]{0:T(128)S(1)}, f32[10]{0:T(128)}, u32[]{:S(2)}) copy-start(f32[10]{0:T(128)} %get-tuple-element.22) | copy-start | bytes 124
  49.3 6.7 %copy-start.30 = (f32[10]{0:T(128)S(1)}, f32[10]{0:T(128)}, u32[]{:S(2)}) copy-start(f32[10]{0:T(128)} %get-tuple-element.24) | copy-start | bytes 124
  56.9 5.8 %collective-permute-start.10 = (f32[10,64,128]{2,1,0:T(8,128)}, f32[10,64,128]{2,1,0:T(8,128)S(1)}, u32[]{:S(2)}, u32[]{:S(2)}) collective-permute-start(f32[10,64,128]{2,1,0:T(8,128)} %get-tuple-element.20), channel_id=1, source_target_pairs={{28,20},{24,16},{29,21},{25,17},{30,22},{26,18},{31,23},{27,19}} | collective-permute-start | bytes 983048 | tf_op jit(solution)/shard_map/ppermute | solution.py:62
  62.9 1.6 %collective-permute-start.11 = (f32[10,64,128]{2,1,0:T(8,128)S(1)}, f32[10,64,128]{2,1,0:T(8,128)S(1)}, u32[]{:S(2)}, u32[]{:S(2)}) collective-permute-start(f32[10,64,128]{2,1,0:T(8,128)S(1)} %multiply_add_fusion.2), channel_id=1, source_target_pairs={{20,12},{16,8},{21,13},{17,9},{22,14},{18,10},{23,15},{19,11}} | collective-permute-start | bytes 983048 | tf_op jit(solution)/shard_map/ppermute | solution.py:62
  64.6 30.5 %collective-permute-start.12 = (f32[10,64,128]{2,1,0:T(8,128)S(1)}, f32[10,64,128]{2,1,0:T(8,128)S(1)}, u32[]{:S(2)}, u32[]{:S(2)}) collective-permute-start(f32[10,64,128]{2,1,0:T(8,128)S(1)} %get-tuple-element.18), channel_id=1, source_target_pairs={{12,4},{8,0},{13,5},{9,1},{14,6},{10,2},{15,7},{11,3}} | collective-permute-start | bytes 983048 | tf_op jit(solution)/shard_map/ppermute | solution.py:59
  66.5 30.0 %collective-permute-start.16 = (f32[128,128]{1,0:T(8,128)S(1)}, f32[128,128]{1,0:T(8,128)S(1)}, u32[]{:S(2)}, u32[]{:S(2)}) collective-permute-start(f32[128,128]{1,0:T(8,128)S(1)} %fusion.17), channel_id=1, source_target_pairs={{0,1},{1,0},{2,3},{3,2},{4,5},{5,4},{6,7},{7,6},{8,9},{9,8},{10,11... | collective-permute-start | bytes 196616 | tf_op jit(solution)/shard_map/ppermute | solution.py:96
  95.8 7.1 %collective-permute-start.13 = (f32[10,64,128]{2,1,0:T(8,128)S(1)}, f32[10,64,128]{2,1,0:T(8,128)S(1)}, u32[]{:S(2)}, u32[]{:S(2)}) collective-permute-start(f32[10,64,128]{2,1,0:T(8,128)S(1)} %add_select_fusion), channel_id=1, source_target_pairs={{28,24},{24,28},{20,16},{16,20},{12,8},{8,12},{4,0},{0,4},{29,25},... | collective-permute-start | bytes 983048 | tf_op jit(solution)/shard_map/ppermute | solution.py:82
  96.5 4.4 %collective-permute-start.17 = (f32[128,128]{1,0:T(8,128)S(1)}, f32[128,128]{1,0:T(8,128)}, u32[]{:S(2)}, u32[]{:S(2)}) collective-permute-start(f32[128,128]{1,0:T(8,128)S(1)} %add.205), channel_id=1, source_target_pairs={{0,2},{1,3},{2,0},{3,1},{4,6},{5,7},{6,4},{7,5},{8,10},{9,11},{10,... | collective-permute-start | bytes 196616 | tf_op jit(solution)/shard_map/ppermute | solution.py:96
  98.9 4.0 %copy-start.11 = (f32[10,64,128]{2,1,0:T(8,128)S(1)}, f32[10,64,128]{2,1,0:T(8,128)}, u32[]{:S(2)}) copy-start(f32[10,64,128]{2,1,0:T(8,128)} %copy-done.10) | copy-start | bytes 983044
  98.9 4.0 %copy-start.32 = (f32[10]{0:T(128)S(1)}, f32[10]{0:T(128)}, u32[]{:S(2)}) copy-start(f32[10]{0:T(128)} %copy-done.31) | copy-start | bytes 124
  102.5 2.4 %copy-start.14 = (f32[128,10]{0,1:T(8,128)S(1)}, f32[128,10]{0,1:T(8,128)}, u32[]{:S(2)}) copy-start(f32[128,10]{0,1:T(8,128)} %get-tuple-element.47) | copy-start | bytes 15364
  108.1 1.4 %collective-permute-start.14 = (f32[128,128]{1,0:T(8,128)S(1)}, f32[128,128]{1,0:T(8,128)S(1)}, u32[]{:S(2)}, u32[]{:S(2)}) collective-permute-start(f32[128,128]{1,0:T(8,128)S(1)} %fusion.16), channel_id=1, source_target_pairs={{0,1},{1,0},{2,3},{3,2},{4,5},{5,4},{6,7},{7,6},{8,9},{9,8},{10,11... | collective-permute-start | bytes 196616 | tf_op jit(solution)/shard_map/ppermute | solution.py:96
  108.5 6.2 %copy-start.1 = (f32[128,1280]{1,0:T(8,128)}, f32[128,1280]{1,0:T(8,128)S(1)}, u32[]{:S(2)}) copy-start(f32[128,1280]{1,0:T(8,128)S(1)} %add_dynamic-update-slice_fusion) | copy-start | bytes 1966084
  109.5 4.5 %collective-permute-start.15 = (f32[128,128]{1,0:T(8,128)S(1)}, f32[128,128]{1,0:T(8,128)S(1)}, u32[]{:S(2)}, u32[]{:S(2)}) collective-permute-start(f32[128,128]{1,0:T(8,128)S(1)} %add.202), channel_id=1, source_target_pairs={{0,2},{1,3},{2,0},{3,1},{4,6},{5,7},{6,4},{7,5},{8,10},{9,11},{10,... | collective-permute-start | bytes 196616 | tf_op jit(solution)/shard_map/ppermute | solution.py:96
  111.5 3.3 %copy-start.25 = (f32[20,128]{1,0:T(8,128)}, f32[20,128]{1,0:T(8,128)S(1)}, u32[]{:S(2)}) copy-start(f32[20,128]{1,0:T(8,128)S(1)} %dynamic_update_slice.21) | copy-start | bytes 30724
  111.7 3.1 %copy-start.20 = (f32[20,128]{1,0:T(8,128)}, f32[20,128]{1,0:T(8,128)S(1)}, u32[]{:S(2)}) copy-start(f32[20,128]{1,0:T(8,128)S(1)} %dynamic_update_slice.23) | copy-start | bytes 30724
  (21 other events, 31.5 us)

commit v23 on v17

--- a/solution.py
+++ b/solution.py
@@ -91,11 +91,11 @@
     count = lax.axis_size(axis)
     if count & (count - 1):
         return lax.psum(parts, axis)
-    k = 1
-    while k < count:
+    k = count // 2
+    while k >= 1:
         got = lax.ppermute(parts, axis, [(i, i ^ k) for i in range(count)])
         parts = jax.tree.map(jnp.add, parts, got)
-        k *= 2
+        k //= 2
     return parts
 
 

time: 115 us -> 118 us (1.026)
  waiting for transfers between devices: 56.5 us -> 59.8 us
    ppermute x2, waiting for transfers between devices: 5.37 us -> 7.59 us  [pair_scan(): other = lax.ppermute(send, axis, swap)]
    ppermute x6, waiting for transfers between devices: 6.31 us -> 4.37 us  [butterfly_psum(): got = lax.ppermute(parts, axis, [(i, i ^ k) for i in range(count)])]
    ppermute x2, waiting for transfers between devices: 27.4 us -> 29.2 us  [pair_scan(): s_in = lax.ppermute(out[1], axis, pairs)]
    ppermute x4, waiting for transfers between devices: 11.8 us -> 13 us  [pair_scan(): a_rcv, s_rcv = lax.ppermute((a_snd, s_snd), axis, swap)]
  transfers between devices with their start and end apart: 18 -> 18, of which waited for: 10 -> 10; matrix products, arithmetic and copies ran while one was open for 19% -> 18% of each run, Pallas kernels for 0% -> 0%
where the time goes in v23:
time: 118 us
  waiting for transfers between devices  59.8 us (51%)
  starting transfers between devices  19.5 us (17%)
  matrix products  15.8 us (13%)
  other arithmetic  11.6 us (10%)
  local copies, waits for them, and re-layouts  9.73 us (8%)
  between operations  1.24 us (1%)
    ppermute x2, waiting for transfers between devices, pair_scan(): s_in = lax.ppermute(out[1], axis, pairs)  29.2 us
    ppermute x4, waiting for transfers between devices, pair_scan(): a_rcv, s_rcv = lax.ppermute((a_snd, s_snd), axis, swap)  13 us
    ppermute x2, waiting for transfers between devices, pair_scan(): other = lax.ppermute(send, axis, swap)  7.59 us
    dot_general x3, matrix products, within_part(): within = jnp.einsum('hij,jhp->ihp', masked, scaled, precision=highest)  5.88 us
    ppermute x4, waiting for transfers between devices, pair_scan(): a_in, s_in = lax.ppermute(out, axis, pairs)  5.67 us
    ppermute x4, starting transfers between devices, pair_scan(): a_in, s_in = lax.ppermute(out, axis, pairs)  5.55 us
    ppermute x4, starting transfers between devices, pair_scan(): a_rcv, s_rcv = lax.ppermute((a_snd, s_snd), axis, swap)  5.53 us
    ppermute x6, starting transfers between devices, butterfly_psum(): got = lax.ppermute(parts, axis, [(i, i ^ k) for i in range(count)])  4.94 us
  transfers between devices with their start and end apart: 18, of which 10 were waited for; matrix products, arithmetic and copies ran while one was open for 18% of the time, Pallas kernels for 0%

profile of v23, /device:TPU:0, one launch (start us, length us, event | category | flops | bytes accessed | tf_op | source)
XLA Modules:
  0.0 117.6 jit_solution(12247311575630565907)
XLA Ops:
  0.7 0.8 fusion.68
  1.8 2.9 %collective-permute-start.8 = (f32[10]{0:T(128)S(1)}, f32[10]{0:T(128)S(1)}, u32[]{:S(2)}, u32[]{:S(2)}) collective-permute-start(f32[10]{0:T(128)S(1)} %dynamic_slice.53), channel_id=1, source_target_pairs={{28,24},{24,28},{20,16},{16,20},{12,8},{8,12},{4,0},{0,4},{29,25},... | collective-permute-start | bytes 128 | tf_op jit(solution)/shard_map/ppermute | solution.py:42
  4.8 1.3 %copy.30 = f32[128,1280]{0,1:T(8,128)S(1)} copy(f32[128,1280]{1,0:T(8,128)} %param.9) | data formatting | bytes 1310720 | tf_op args[0]
  7.4 2.0 %collective-permute-start = (f32[10]{0:T(128)S(1)}, f32[10]{0:T(128)S(1)}, u32[]{:S(2)}, u32[]{:S(2)}) collective-permute-start(f32[10]{0:T(128)S(1)} %get-tuple-element.54), channel_id=1, source_target_pairs={{0,4},{4,0},{8,12},{12,8},{16,20},{20,16},{24,28},{28,24},{1,5},{5... | collective-permute-start | bytes 128 | tf_op jit(solution)/shard_map/ppermute | solution.py:42
  9.4 6.6 %collective-permute-done = f32[10]{0:T(128)S(1)} collective-permute-done((f32[10]{0:T(128)S(1)}, f32[10]{0:T(128)S(1)}, u32[]{:S(2)}, u32[]{:S(2)}) %collective-permute-start) | collective-permute-done | bytes 72 | tf_op jit(solution)/shard_map/ppermute | solution.py:42
  16.2 3.5 %collective-permute-start.2 = (f32[10,64,128]{2,1,0:T(8,128)S(1)}, f32[10,64,128]{2,1,0:T(8,128)S(1)}, u32[]{:S(2)}, u32[]{:S(2)}) collective-permute-start(f32[10,64,128]{2,1,0:T(8,128)S(1)} %get-tuple-element.29), channel_id=1, source_target_pairs={{0,8},{4,12},{1,9},{5,13},{2,10},{6,14},{3,11},{7,15}} | collective-permute-start | bytes 983048 | tf_op jit(solution)/shard_map/ppermute | solution.py:62
  19.7 5.7 %collective-permute-done.2 = f32[10,64,128]{2,1,0:T(8,128)S(1)} collective-permute-done((f32[10,64,128]{2,1,0:T(8,128)S(1)}, f32[10,64,128]{2,1,0:T(8,128)S(1)}, u32[]{:S(2)}, u32[]{:S(2)}) %collective-permute-start.2) | collective-permute-done | bytes 327712 | tf_op jit(solution)/shard_map/ppermute | solution.py:62
  28.0 1.5 %fusion.9 = f32[128,20,64]{0,2,1:T(8,128)S(1)} fusion(f32[128,20,64]{0,2,1:T(8,128)S(1)} %bitcast.127, f32[128,128]{1,0:T(8,128)S(1)} %fusion.104, f32[20,128]{1,0:T(8,128)S(1)} %bitcast.136, pred[128,128]{1,0:T(8,128)(4,1)S(1)} %iota_compare_fusion.10, f32[128,20]{0,1:T(8,128)S(1)} %bitcast.140, f32[20]{0:T(128)S(1)} %copy-done.22), kind=kOutput, calls=%fused_computation.9 | convolution fusion | flops 127631360 | bytes 1413200 | tf_op jit(solution)/shard_map/jvp(hij,jhp->ihp)/dot_general | solution.py:169
  29.7 5.0 %collective-permute-done.5 = f32[10,64,128]{2,1,0:T(8,128)S(1)} collective-permute-done((f32[10,64,128]{2,1,0:T(8,128)S(1)}, f32[10,64,128]{2,1,0:T(8,128)S(1)}, u32[]{:S(2)}, u32[]{:S(2)}) %collective-permute-start.5) | collective-permute-done | bytes 327712 | tf_op jit(solution)/shard_map/ppermute | solution.py:82
  34.8 1.3 %broadcast_multiply_fusion = (f32[128,20,64]{0,2,1:T(8,128)S(1)}, f32[128,20,64]{0,2,1:T(8,128)}) fusion(f32[128,20]{0,1:T(8,128)S(1)} %get-tuple-element.48, f32[20,64,128]{2,1,0:T(8,128)S(1)} %maximum_select_fusion, f32[128,128]{1,0:T(8,128)S(1)} %copy-done), kind=kOutput, calls=%fused_computation.72 | convolution fusion | flops 125992960 | bytes 2041856 | tf_op jit(solution)/shard_map/jvp(in,hpn->ihp)/dot_general | solution.py:176
  36.8 1.7 %multiply_reduce_fusion.4 = (f32[128]{0:T(128)S(1)}, f32[128]{0:T(128)S(1)}, f32[128,1280]{1,0:T(8,128)S(1)}) fusion(f32[128,1280]{1,0:T(8,128)} %param.10, f32[128,1280]{1,0:T(8,128)} %param.17, f32[1280]{0:T(1024)S(1)} %copy-done.14, f32[128,1280]{1,0:T(8,128)S(1)} %copy.31, f32[128,1280]{1,0:T(8,128)S(1)} %copy.32), kind=kLoop, calls=%fused_computation.34 | loop fusion | flops 1801984 | bytes 3282944 | tf_op jit(solution)/shard_map/reduce_sum | solution.py:246
  38.5 1.6 %collective-permute-start.6 = (f32[2,128]{1,0:T(2,128)S(1)}, f32[2,128]{1,0:T(2,128)S(1)}, u32[]{:S(2)}, u32[]{:S(2)}) collective-permute-start(f32[2,128]{1,0:T(2,128)S(1)} %pad_maximum_fusion), channel_id=1, source_target_pairs={{0,2},{1,3},{2,0},{3,1},{4,6},{5,7},{6,4},{7,5},{8,10},{9,11},{10,... | collective-permute-start | bytes 3080 | tf_op jit(solution)/shard_map/ppermute | solution.py:96
  40.1 2.0 %collective-permute-done.6 = f32[2,128]{1,0:T(2,128)S(1)} collective-permute-done((f32[2,128]{1,0:T(2,128)S(1)}, f32[2,128]{1,0:T(2,128)S(1)}, u32[]{:S(2)}, u32[]{:S(2)}) %collective-permute-start.6) | collective-permute-done | bytes 1056 | tf_op jit(solution)/shard_map/ppermute | solution.py:96
  42.2 1.1 collective-permute-done.7
  43.4 1.3 %add_multiply_fusion = (f32[128,1280]{1,0:T(8,128)}, f32[128,1280]{1,0:T(8,128)S(1)}) fusion(f32[128,1280]{1,0:T(8,128)S(1)} %copy-done.4, f32[128,1280]{1,0:T(8,128)S(1)} %get-tuple-element.26, f32[128]{0:T(128)S(1)} %fusion.90, f32[128,1280]{1,0:T(8,128)S(1)} %copy-done.5, f32[128]{0:T(128)S(1)} %rsqrt_bitcast_fusion, f32[1280]{0:T(1024)S(1)} %copy-done.14), kind=kLoop, calls=%fused_computation.30 | loop fusion | flops 2621440 | bytes 3282944 | tf_op jit(solution)/shard_map/mul | solution.py:255
  46.7 0.9 constant_dynamic-slice_fusion.1
  47.6 1.2 copy.39
  48.7 1.1 copy.40
  49.9 6.4 %collective-permute-done.9 = f32[10,64,128]{2,1,0:T(8,128)} collective-permute-done((f32[10,64,128]{2,1,0:T(8,128)}, f32[10,64,128]{2,1,0:T(8,128)}, u32[]{:S(2)}, u32[]{:S(2)}) %collective-permute-start.9) | collective-permute-done | bytes 327712 | tf_op jit(solution)/shard_map/ppermute | solution.py:42
  56.3 1.1 broadcast_add_fusion
  61.0 2.0 %fusion.20 = (f32[20,128]{1,0:T(8,128)S(1)}, f32[20,128]{1,0:T(8,128)S(1)}, f32[128,128]{1,0:T(8,128)S(1)}) fusion(f32[128,128]{1,0:T(8,128)S(1)} %fusion.104, f32[20,128]{1,0:T(8,128)S(1)} %bitcast.137, pred[128,128]{1,0:T(8,128)(4,1)S(1)} %iota_compare_fusion.10, f32[20,64,128]{2,1,0:T(8,128)S(1)} %bitcast.118, f32[128,20,64]{0,2,1:T(8,128)S(1)} %bitcast.128, ...), kind=kOutput, calls=%fused_computation.24 | convolution fusion | flops 129575936 | bytes 1499136 | tf_op jit(solution)/shard_map/transpose(jvp(hij,jhp->ihp))/dot_general | solution.py:169
  63.3 1.6 %collective-permute-start.12 = (f32[10,64,128]{2,1,0:T(8,128)S(1)}, f32[10,64,128]{2,1,0:T(8,128)S(1)}, u32[]{:S(2)}, u32[]{:S(2)}) collective-permute-start(f32[10,64,128]{2,1,0:T(8,128)S(1)} %get-tuple-element.18), channel_id=1, source_target_pairs={{12,4},{8,0},{13,5},{9,1},{14,6},{10,2},{15,7},{11,3}} | collective-permute-start | bytes 983048 | tf_op jit(solution)/shard_map/ppermute | solution.py:59
  65.6 1.6 %collective-permute-start.16 = (f32[128,128]{1,0:T(8,128)S(1)}, f32[128,128]{1,0:T(8,128)S(1)}, u32[]{:S(2)}, u32[]{:S(2)}) collective-permute-start(f32[128,128]{1,0:T(8,128)S(1)} %fusion.17), channel_id=1, source_target_pairs={{0,2},{1,3},{2,0},{3,1},{4,6},{5,7},{6,4},{7,5},{8,10},{9,11},{10,... | collective-permute-start | bytes 196616 | tf_op jit(solution)/shard_map/ppermute | solution.py:96
  67.2 2.5 %multiply_reduce_fusion.1 = (f32[128,20]{0,1:T(8,128)}, f32[128,20,64]{0,2,1:T(8,128)}, f32[128,20]{0,1:T(8,128)}) fusion(f32[128,20,64]{0,2,1:T(8,128)S(1)} %copy-done.7, f32[128,20,64]{0,2,1:T(8,128)S(1)} %bitcast.120, f32[128,20]{0,1:T(8,128)S(1)} %bitcast.142, f32[20]{0:T(128)S(1)} %copy-done.23, f32[128,20,64]{0,2,1:T(8,128)S(1)} %bitcast.129, ...), kind=kOutput, calls=%fused_computation.28 | convolution fusion | flops 128281600 | bytes 3399760 | tf_op jit(solution)/shard_map/transpose(jvp(hij,jhp->ihp))/dot_general | solution.py:169
  69.6 29.2 %collective-permute-done.12 = f32[10,64,128]{2,1,0:T(8,128)S(1)} collective-permute-done((f32[10,64,128]{2,1,0:T(8,128)S(1)}, f32[10,64,128]{2,1,0:T(8,128)S(1)}, u32[]{:S(2)}, u32[]{:S(2)}) %collective-permute-start.12) | collective-permute-done | bytes 327712 | tf_op jit(solution)/shard_map/ppermute | solution.py:59
  100.7 1.3 %copy.38 = f32[128,1280]{1,0:T(8,128)S(1)} copy(f32[128,1280]{0,1:T(8,128)} %bitcast.133) | data formatting | bytes 1310720 | tf_op jit(solution)/shard_map/transpose(jvp())/reshape | solution.py:166
  102.0 1.5 %add.181 = f32[128,128]{1,0:T(8,128)} add(f32[128,128]{1,0:T(8,128)S(1)} %add.180, f32[128,128]{1,0:T(8,128)} %collective-permute-done.17) | non-fusion elementwise | flops 16384 | bytes 196608 | tf_op jit(solution)/shard_map/add | solution.py:97
  103.5 2.6 %collective-permute-done.13 = f32[10,64,128]{2,1,0:T(8,128)S(1)} collective-permute-done((f32[10,64,128]{2,1,0:T(8,128)S(1)}, f32[10,64,128]{2,1,0:T(8,128)S(1)}, u32[]{:S(2)}, u32[]{:S(2)}) %collective-permute-start.13) | collective-permute-done | bytes 327712 | tf_op jit(solution)/shard_map/ppermute | solution.py:82
  106.1 1.2 %multiply_reduce_fusion.7 = (f32[10]{0:T(128)S(1)}, f32[10]{0:T(128)S(1)}, f32[10,64,128]{2,1,0:T(8,128)S(1)}) fusion(f32[10,64,128]{2,1,0:T(8,128)S(1)} %collective-permute-done.13, f32[20,64,128]{2,1,0:T(8,128)S(1)} %maximum_select_fusion, s32[]{:T(128)S(6)} %select_n.213, s32[]{:T(128)S(6)} %select_n.209, f32[10,64,128]{2,1,0:T(8,128)} %collective-permute-done.9, ...), kind=kLoop, calls=%fused_computation.58 | loop fusion | flops 655340 | bytes 2293890 | tf_op jit(solution)/shard_map/transpose(jvp())/reduce_sum | solution.py:193
  111.3 1.6 %collective-permute-start.14 = (f32[128,128]{1,0:T(8,128)S(1)}, f32[128,128]{1,0:T(8,128)S(1)}, u32[]{:S(2)}, u32[]{:S(2)}) collective-permute-start(f32[128,128]{1,0:T(8,128)S(1)} %fusion.16), channel_id=1, source_target_pairs={{0,2},{1,3},{2,0},{3,1},{4,6},{5,7},{6,4},{7,5},{8,10},{9,11},{10,... | collective-permute-start | bytes 196616 | tf_op jit(solution)/shard_map/ppermute | solution.py:96
  113.3 0.9 fusion.21
  114.3 0.8 fusion.18
  (128 shorter events, 20.6 us)
Async XLA Ops:
  0.6 26.4 %copy-start = (f32[128,128]{1,0:T(8,128)S(1)}, f32[128,128]{1,0:T(8,128)}, u32[]{:S(2)}) copy-start(f32[128,128]{1,0:T(8,128)} %param.12) | copy-start | bytes 196612
  1.8 5.0 %collective-permute-start.8 = (f32[10]{0:T(128)S(1)}, f32[10]{0:T(128)S(1)}, u32[]{:S(2)}, u32[]{:S(2)}) collective-permute-start(f32[10]{0:T(128)S(1)} %dynamic_slice.53), channel_id=1, source_target_pairs={{28,24},{24,28},{20,16},{16,20},{12,8},{8,12},{4,0},{0,4},{29,25},... | collective-permute-start | bytes 128 | tf_op jit(solution)/shard_map/ppermute | solution.py:42
  6.2 54.8 %copy-start.2 = (f32[128,1280]{0,1:T(8,128)}, f32[128,1280]{0,1:T(8,128)S(1)}, u32[]{:S(2)}) copy-start(f32[128,1280]{0,1:T(8,128)S(1)} %copy.30) | copy-start | bytes 1966084
  6.7 9.4 %collective-permute-start.1 = (f32[10,64,128]{2,1,0:T(8,128)S(1)}, f32[10,64,128]{2,1,0:T(8,128)S(1)}, u32[]{:S(2)}, u32[]{:S(2)}) collective-permute-start(f32[10,64,128]{2,1,0:T(8,128)S(1)} %constant_dynamic-slice_fusion.3), channel_id=1, source_target_pairs={{0,4},{4,0},{8,12},{12,8},{16,20},{20,16},{24,28},{28,24},{1,5},{5... | collective-permute-start | bytes 983048 | tf_op jit(solution)/shard_map/ppermute | solution.py:42
  6.8 9.4 %copy-start.20 = (f32[10]{0:T(128)}, f32[10]{0:T(128)S(1)}, u32[]{:S(2)}) copy-start(f32[10]{0:T(128)S(1)} %collective-permute-done.8) | copy-start | bytes 124
  7.4 8.6 %collective-permute-start = (f32[10]{0:T(128)S(1)}, f32[10]{0:T(128)S(1)}, u32[]{:S(2)}, u32[]{:S(2)}) collective-permute-start(f32[10]{0:T(128)S(1)} %get-tuple-element.54), channel_id=1, source_target_pairs={{0,4},{4,0},{8,12},{12,8},{16,20},{20,16},{24,28},{28,24},{1,5},{5... | collective-permute-start | bytes 128 | tf_op jit(solution)/shard_map/ppermute | solution.py:42
  16.2 9.2 %collective-permute-start.2 = (f32[10,64,128]{2,1,0:T(8,128)S(1)}, f32[10,64,128]{2,1,0:T(8,128)S(1)}, u32[]{:S(2)}, u32[]{:S(2)}) collective-permute-start(f32[10,64,128]{2,1,0:T(8,128)S(1)} %get-tuple-element.29), channel_id=1, source_target_pairs={{0,8},{4,12},{1,9},{5,13},{2,10},{6,14},{3,11},{7,15}} | collective-permute-start | bytes 983048 | tf_op jit(solution)/shard_map/ppermute | solution.py:62
  25.5 0.7 collective-permute-start.3
  26.3 0.9 collective-permute-start.4
  27.4 7.3 %collective-permute-start.5 = (f32[10,64,128]{2,1,0:T(8,128)S(1)}, f32[10,64,128]{2,1,0:T(8,128)S(1)}, u32[]{:S(2)}, u32[]{:S(2)}) collective-permute-start(f32[10,64,128]{2,1,0:T(8,128)S(1)} %get-tuple-element.42), channel_id=1, source_target_pairs={{0,4},{4,0},{8,12},{12,8},{16,20},{20,16},{24,28},{28,24},{1,5},{5... | collective-permute-start | bytes 983048 | tf_op jit(solution)/shard_map/ppermute | solution.py:82
  36.8 6.6 %copy-start.4 = (f32[128,1280]{1,0:T(8,128)S(1)}, f32[128,1280]{1,0:T(8,128)}, u32[]{:S(2)}) copy-start(f32[128,1280]{1,0:T(8,128)} %param.10) | copy-start | bytes 1966084
  36.8 6.7 %copy-start.5 = (f32[128,1280]{1,0:T(8,128)S(1)}, f32[128,1280]{1,0:T(8,128)}, u32[]{:S(2)}) copy-start(f32[128,1280]{1,0:T(8,128)} %param.17) | copy-start | bytes 1966084
  38.5 3.6 %collective-permute-start.6 = (f32[2,128]{1,0:T(2,128)S(1)}, f32[2,128]{1,0:T(2,128)S(1)}, u32[]{:S(2)}, u32[]{:S(2)}) collective-permute-start(f32[2,128]{1,0:T(2,128)S(1)} %pad_maximum_fusion), channel_id=1, source_target_pairs={{0,2},{1,3},{2,0},{3,1},{4,6},{5,7},{6,4},{7,5},{8,10},{9,11},{10,... | collective-permute-start | bytes 3080 | tf_op jit(solution)/shard_map/ppermute | solution.py:96
  42.2 1.2 %collective-permute-start.7 = (f32[2,128]{1,0:T(2,128)S(1)}, f32[2,128]{1,0:T(2,128)S(1)}, u32[]{:S(2)}, u32[]{:S(2)}) collective-permute-start(f32[2,128]{1,0:T(2,128)S(1)} %fusion.100), channel_id=1, source_target_pairs={{0,1},{1,0},{2,3},{3,2},{4,5},{5,4},{6,7},{7,6},{8,9},{9,8},{10,11... | collective-permute-start | bytes 3080 | tf_op jit(solution)/shard_map/ppermute | solution.py:96
  46.1 10.1 %collective-permute-start.9 = (f32[10,64,128]{2,1,0:T(8,128)}, f32[10,64,128]{2,1,0:T(8,128)}, u32[]{:S(2)}, u32[]{:S(2)}) collective-permute-start(f32[10,64,128]{2,1,0:T(8,128)} %constant_dynamic-slice_fusion.2), channel_id=1, source_target_pairs={{28,24},{24,28},{20,16},{16,20},{12,8},{8,12},{4,0},{0,4},{29,25},... | collective-permute-start | bytes 983048 | tf_op jit(solution)/shard_map/ppermute | solution.py:42
  47.6 8.7 %copy-start.18 = (f32[10]{0:T(128)S(1)}, f32[10]{0:T(128)}, u32[]{:S(2)}) copy-start(f32[10]{0:T(128)} %get-tuple-element.22) | copy-start | bytes 124
  47.6 8.7 %copy-start.19 = (f32[10]{0:T(128)S(1)}, f32[10]{0:T(128)}, u32[]{:S(2)}) copy-start(f32[10]{0:T(128)} %get-tuple-element.24) | copy-start | bytes 124
  57.4 2.8 %collective-permute-start.10 = (f32[10,64,128]{2,1,0:T(8,128)S(1)}, f32[10,64,128]{2,1,0:T(8,128)S(1)}, u32[]{:S(2)}, u32[]{:S(2)}) collective-permute-start(f32[10,64,128]{2,1,0:T(8,128)S(1)} %get-tuple-element.20), channel_id=1, source_target_pairs={{28,20},{24,16},{29,21},{25,17},{30,22},{26,18},{31,23},{27,19}} | collective-permute-start | bytes 983048 | tf_op jit(solution)/shard_map/ppermute | solution.py:62
  60.3 2.8 %collective-permute-start.11 = (f32[10,64,128]{2,1,0:T(8,128)S(1)}, f32[10,64,128]{2,1,0:T(8,128)S(1)}, u32[]{:S(2)}, u32[]{:S(2)}) collective-permute-start(f32[10,64,128]{2,1,0:T(8,128)S(1)} %multiply_add_fusion.2), channel_id=1, source_target_pairs={{20,12},{16,8},{21,13},{17,9},{22,14},{18,10},{23,15},{19,11}} | collective-permute-start | bytes 983048 | tf_op jit(solution)/shard_map/ppermute | solution.py:62
  63.2 3.9 %copy-start.3 = (f32[128,1280]{0,1:T(8,128)S(1)}, f32[128,1280]{0,1:T(8,128)}, u32[]{:S(2)}) copy-start(f32[128,1280]{0,1:T(8,128)} %copy-done.2) | copy-start | bytes 1966084
  63.3 3.9 %copy-start.7 = (f32[128,20,64]{0,2,1:T(8,128)S(1)}, f32[128,20,64]{0,2,1:T(8,128)}, u32[]{:S(2)}) copy-start(f32[128,20,64]{0,2,1:T(8,128)} %get-tuple-element.56) | copy-start | bytes 1966084
  63.3 3.9 %copy-start.23 = (f32[20]{0:T(128)S(1)}, f32[20]{0:T(128)}, u32[]{:S(2)}) copy-start(f32[20]{0:T(128)} %param.15) | copy-start | bytes 244
  63.3 35.6 %collective-permute-start.12 = (f32[10,64,128]{2,1,0:T(8,128)S(1)}, f32[10,64,128]{2,1,0:T(8,128)S(1)}, u32[]{:S(2)}, u32[]{:S(2)}) collective-permute-start(f32[10,64,128]{2,1,0:T(8,128)S(1)} %get-tuple-element.18), channel_id=1, source_target_pairs={{12,4},{8,0},{13,5},{9,1},{14,6},{10,2},{15,7},{11,3}} | collective-permute-start | bytes 983048 | tf_op jit(solution)/shard_map/ppermute | solution.py:59
  65.6 34.2 %collective-permute-start.16 = (f32[128,128]{1,0:T(8,128)S(1)}, f32[128,128]{1,0:T(8,128)S(1)}, u32[]{:S(2)}, u32[]{:S(2)}) collective-permute-start(f32[128,128]{1,0:T(8,128)S(1)} %fusion.17), channel_id=1, source_target_pairs={{0,2},{1,3},{2,0},{3,1},{4,6},{5,7},{6,4},{7,5},{8,10},{9,11},{10,... | collective-permute-start | bytes 196616 | tf_op jit(solution)/shard_map/ppermute | solution.py:96
  99.0 7.1 %collective-permute-start.13 = (f32[10,64,128]{2,1,0:T(8,128)S(1)}, f32[10,64,128]{2,1,0:T(8,128)S(1)}, u32[]{:S(2)}, u32[]{:S(2)}) collective-permute-start(f32[10,64,128]{2,1,0:T(8,128)S(1)} %add_select_fusion.1), channel_id=1, source_target_pairs={{28,24},{24,28},{20,16},{16,20},{12,8},{8,12},{4,0},{0,4},{29,25},... | collective-permute-start | bytes 983048 | tf_op jit(solution)/shard_map/ppermute | solution.py:82
  99.8 2.2 %collective-permute-start.17 = (f32[128,128]{1,0:T(8,128)S(1)}, f32[128,128]{1,0:T(8,128)}, u32[]{:S(2)}, u32[]{:S(2)}) collective-permute-start(f32[128,128]{1,0:T(8,128)S(1)} %add.180), channel_id=1, source_target_pairs={{0,1},{1,0},{2,3},{3,2},{4,5},{5,4},{6,7},{7,6},{8,9},{9,8},{10,11... | collective-permute-start | bytes 196616 | tf_op jit(solution)/shard_map/ppermute | solution.py:96
  100.7 5.4 %copy-start.21 = (f32[10]{0:T(128)S(1)}, f32[10]{0:T(128)}, u32[]{:S(2)}) copy-start(f32[10]{0:T(128)} %copy-done.20) | copy-start | bytes 124
  103.5 4.0 %copy-start.10 = (f32[10,128]{1,0:T(8,128)S(1)}, f32[10,128]{1,0:T(8,128)}, u32[]{:S(2)}) copy-start(f32[10,128]{1,0:T(8,128)} %fusion.67) | copy-start | bytes 15364
  103.5 4.3 %copy-start.11 = (f32[10,128]{1,0:T(8,128)S(1)}, f32[10,128]{1,0:T(8,128)}, u32[]{:S(2)}) copy-start(f32[10,128]{1,0:T(8,128)} %fusion.66) | copy-start | bytes 15364
  103.5 4.5 %copy-start.8 = (f32[128,10]{0,1:T(8,128)S(1)}, f32[128,10]{0,1:T(8,128)}, u32[]{:S(2)}) copy-start(f32[128,10]{0,1:T(8,128)} %get-tuple-element.47) | copy-start | bytes 15364
  111.3 4.3 %collective-permute-start.14 = (f32[128,128]{1,0:T(8,128)S(1)}, f32[128,128]{1,0:T(8,128)S(1)}, u32[]{:S(2)}, u32[]{:S(2)}) collective-permute-start(f32[128,128]{1,0:T(8,128)S(1)} %fusion.16), channel_id=1, source_target_pairs={{0,2},{1,3},{2,0},{3,1},{4,6},{5,7},{6,4},{7,5},{8,10},{9,11},{10,... | collective-permute-start | bytes 196616 | tf_op jit(solution)/shard_map/ppermute | solution.py:96
  115.6 1.3 %collective-permute-start.15 = (f32[128,128]{1,0:T(8,128)S(1)}, f32[128,128]{1,0:T(8,128)S(1)}, u32[]{:S(2)}, u32[]{:S(2)}) collective-permute-start(f32[128,128]{1,0:T(8,128)S(1)} %add.177), channel_id=1, source_target_pairs={{0,1},{1,0},{2,3},{3,2},{4,5},{5,4},{6,7},{7,6},{8,9},{9,8},{10,11... | collective-permute-start | bytes 196616 | tf_op jit(solution)/shard_map/ppermute | solution.py:96
  (10 other events, 12.5 us)
